TPU v7x, 32 devices: a whole 2x2x4 slice. The times are simulated.
32 devices in a mesh: ex: 8 (over z, y), ey: 4 (over x, core).
Axes of the slice: x: 2, y: 2, z: 4, core: 2. Of those that a mesh axis runs over, the one named last changes fastest.
Arguments:
- source: float32 [8, 4, 8, 8, 8, 128], P('ex', 'ey'), may hold values from -8 to 8
- metric: float32 [4, 8, 4, 128], P(None, 'ex', 'ey'), may hold values from 0.5 to 2
- fac_point: int32 [8, 16384], P('ex', 'ey'), may hold values from 0 to 65535
- fac_strip: int32 [8, 16384, 1], P('ex', 'ey'), may hold values from 0 to 3; in each aligned block of 4096 rows (0 to 4095, 4096 to 8191, ..., all dimensions but the last counted through in order) at most 4096 rows name the same one
- fac_shell: int32 [8, 16384], P('ex', 'ey'), may hold values from 0 to 16383
- fac_area: float32 [8, 16384], P('ex', 'ey'), may hold values from 0.5 to 2
Outputs:
- pressure: float32 [8, 4, 8, 8, 8, 128], P('ex', 'ey')
- resid: float32 [8, 4, 8, 8, 8, 128], P('ex', 'ey')
- shell_load: float32 [65536], P('ey')
Inputs may be any that keep to these rules, and one draw needn't show every extreme that they name: `fac_strip`: among the facade points of one device at most 4096 go to one strip, and in every draw some device sends exactly 4096 to some strip.
All inputs are finite; a program needn't handle non-finite values.
Results may differ from a plain program's by a relative error of at most 0.00021.
Values sent between devices are 32-bit elements; how exact they have to be, the bound alone decides.
No kernel may reach another device: no remote copies, remote signals or barrier semaphores. Data moves between devices by JAX's collectives and lax.ppermute only.
A program may use at most 64 MiB of HBM per device.

v0:
```python
import jax
import jax.numpy as jnp
import numpy as np
from jax import lax
from jax.sharding import PartitionSpec as P

SWEEPS = 4
SHELL_STRIP = 16384


def padded_2(block, sides, width):
    for axis, dim in sides:
        count = lax.axis_size(axis)
        forward = [(i, i + 1) for i in range(count - 1)]
        backward = [(target, source) for source, target in forward]
        low = lax.ppermute(
            lax.slice_in_dim(block, block.shape[dim] - width, None, axis=dim), axis, forward
        )
        high = lax.ppermute(lax.slice_in_dim(block, 0, width, axis=dim), axis, backward)
        block = jnp.concatenate([low, block, high], axis=dim)
    return block


def gll_tables():
    degree = 7
    points = np.array(
        [
            -1.0,
            -0.8717401485096066,
            -0.5917001814331423,
            -0.2092992179024789,
            0.2092992179024789,
            0.5917001814331423,
            0.8717401485096066,
            1.0,
        ]
    )
    previous = points * 0.0 + 1.0
    current = points * 1.0
    for order in range(1, degree):
        following = ((2 * order + 1) * points * current - order * previous) / (order + 1)
        previous = current
        current = following
    weights = 2.0 / (degree * (degree + 1) * current**2)
    count = degree + 1
    same = np.array([[1.0 if row == col else 0.0 for col in range(count)] for row in range(count)])
    between = points[:, None] - points[None, :] + same
    deriv = current[:, None] / current[None, :] / between * (1.0 - same)
    deriv[0, 0] = -degree * (degree + 1) / 4.0
    deriv[-1, -1] = degree * (degree + 1) / 4.0
    stiff = deriv.T @ (weights[:, None] * deriv)
    return (jnp.asarray(weights, jnp.float32), jnp.asarray(stiff, jnp.float32))


def spread(metric, which):
    return metric[which][:, :, None, None, None, :]


def element_apply(values_in, metric, weights, stiff):
    top = lax.Precision.HIGHEST
    weight_i = weights[None, None, :, None, None, None]
    weight_j = weights[None, None, None, :, None, None]
    weight_k = weights[None, None, None, None, :, None]
    along_x = jnp.einsum("im,abmjkc->abijkc", stiff, values_in, precision=top)
    along_y = jnp.einsum("jm,abimkc->abijkc", stiff, values_in, precision=top)
    along_z = jnp.einsum("km,abijmc->abijkc", stiff, values_in, precision=top)
    return (
        spread(metric, 0) * weight_j * weight_k * along_x
        + spread(metric, 1) * weight_i * weight_k * along_y
        + spread(metric, 2) * weight_i * weight_j * along_z
        + spread(metric, 3) * weight_i * weight_j * weight_k * values_in
    )


def local_diagonal(metric, weights, stiff):
    stiff_diag = jnp.diagonal(stiff)
    weight_i = weights[None, None, :, None, None, None]
    weight_j = weights[None, None, None, :, None, None]
    weight_k = weights[None, None, None, None, :, None]
    diag_i = stiff_diag[None, None, :, None, None, None]
    diag_j = stiff_diag[None, None, None, :, None, None]
    diag_k = stiff_diag[None, None, None, None, :, None]
    return (
        spread(metric, 0) * diag_i * weight_j * weight_k
        + spread(metric, 1) * weight_i * diag_j * weight_k
        + spread(metric, 2) * weight_i * weight_j * diag_k
        + spread(metric, 3) * weight_i * weight_j * weight_k
    )


def faces(values_in, face_dim):
    last = values_in.shape[face_dim] - 1
    lower = lax.index_in_dim(values_in, 0, face_dim, keepdims=False)
    upper = lax.index_in_dim(values_in, last, face_dim, keepdims=False)
    return (lower, upper)


def combine(values_in, face_dim, elem_dim, lower, upper, before, after):
    total = lower.shape[elem_dim]
    upper_prev = jnp.concatenate(
        [before, lax.slice_in_dim(upper, 0, total - 1, axis=elem_dim)], elem_dim
    )
    lower_next = jnp.concatenate(
        [lax.slice_in_dim(lower, 1, total, axis=elem_dim), after], elem_dim
    )
    middle = lax.slice_in_dim(values_in, 1, values_in.shape[face_dim] - 1, axis=face_dim)
    return jnp.concatenate(
        [
            jnp.expand_dims(lower + upper_prev, face_dim),
            middle,
            jnp.expand_dims(upper + lower_next, face_dim),
        ],
        face_dim,
    )


def assemble(values_in):
    lower, upper = faces(values_in, 2)
    rim_faces = jnp.concatenate([lower, upper], 0)
    padded = padded_2(rim_faces, (("ex", 0),), 1)
    values_in = combine(values_in, 2, 0, lower, upper, padded[:1], padded[3:])
    lower, upper = faces(values_in, 3)
    rim_faces = jnp.concatenate([lower, upper], 1)
    padded = padded_2(rim_faces, (("ey", 1),), 1)
    values_in = combine(values_in, 3, 1, lower, upper, padded[:, :1], padded[:, 3:])
    lower, upper = faces(values_in, 4)
    empty = jnp.zeros_like(upper[..., :1])
    return combine(values_in, 4, 4, lower, upper, empty, empty)


def on_device(source, metric, fac_point, fac_strip, fac_shell, fac_area):
    weights, stiff = gll_tables()
    high, low = (2.0, 0.2)
    theta = (high + low) / 2.0
    delta = (high - low) / 2.0
    sigma = theta / delta
    rho_now = 1.0 / sigma
    rhs = assemble(source)
    pinv = 1.0 / assemble(local_diagonal(metric, weights, stiff))
    pressure = jnp.zeros_like(source)
    resid = rhs
    update = pinv * resid / theta
    for step in range(SWEEPS):
        pressure = pressure + update
        resid = resid - assemble(element_apply(update, metric, weights, stiff))
        if step + 1 < SWEEPS:
            rho_new = 1.0 / (2.0 * sigma - rho_now)
            update = rho_new * rho_now * update + 2.0 * rho_new / delta * pinv * resid
            rho_now = rho_new
    picks = fac_point[0]
    samples = pressure.reshape(-1)[picks]
    areas = fac_area[0]
    weighted = areas * samples
    strip_of = fac_strip[0, :, 0]
    shell_of = fac_shell[0]
    strips = lax.axis_size("ey")
    global_ids = strip_of * SHELL_STRIP + shell_of
    full_numer = jax.ops.segment_sum(weighted, global_ids, strips * SHELL_STRIP)
    full_denom = jax.ops.segment_sum(areas, global_ids, strips * SHELL_STRIP)
    strip_numer, strip_denom = (
        lax.psum_scatter(full_numer, "ey", scatter_dimension=0, tiled=True),
        lax.psum_scatter(full_denom, "ey", scatter_dimension=0, tiled=True),
    )
    total_numer, total_denom = lax.psum((strip_numer, strip_denom), "ex")
    shell_load = total_numer / jnp.maximum(total_denom, 1.0)
    return (pressure, resid, shell_load)


def solution(mesh):
    placed = (
        P("ex", "ey", None, None, None, None),
        P(None, "ex", "ey", None),
        P("ex", "ey"),
        P("ex", "ey", None),
        P("ex", "ey"),
        P("ex", "ey"),
    )
    return jax.shard_map(
        on_device,
        mesh=mesh,
        in_specs=placed,
        out_specs=(
            P("ex", "ey", None, None, None, None),
            P("ex", "ey", None, None, None, None),
            P("ey"),
        ),
        check_vma=False,
    )
```

profile of v0, /device:TPU:2, one launch (start us, length us, event | category | flops | bytes accessed | tf_op | source)
XLA Modules:
  0.0 305.0 jit_solution(6339015300999951671)
XLA Ops:
  8.0 3.6 %collective-permute-start.4 = (f32[1,1,8,8,128]{4,3,2,1,0:T(8,128)S(1)}, f32[1,1,8,8,128]{4,3,2,1,0:T(8,128)S(1)}, u32[]{:S(2)}, u32[]{:S(2)}) collective-permute-start(f32[1,1,8,8,128]{4,3,2,1,0:T(8,128)S(1)} %get-tuple-element.74), channel_id=1, source_target_pairs={{0,4},{4,8},{8,12},{12,16},{16,20},{20,24},{24,28},{1,5},{5,9},{9,... | collective-permute-start | bytes 98312 | tf_op jit(solution)/shard_map/ppermute | solution.py:16
  11.6 1.3 collective-permute-start.5
  14.5 4.5 %collective-permute-start = (f32[1,1,8,8,128]{4,3,2,1,0:T(8,128)S(1)}, f32[1,1,8,8,128]{4,3,2,1,0:T(8,128)S(1)}, u32[]{:S(2)}, u32[]{:S(2)}) collective-permute-start(f32[1,1,8,8,128]{4,3,2,1,0:T(8,128)S(1)} %get-tuple-element.70), channel_id=1, source_target_pairs={{0,4},{4,8},{8,12},{12,16},{16,20},{20,24},{24,28},{1,5},{5,9},{9,... | collective-permute-start | bytes 98312 | tf_op jit(solution)/shard_map/ppermute | solution.py:16
  19.1 1.3 collective-permute-start.1
  20.4 0.9 slice-done
  22.4 1.9 collective-permute-start.6
  24.3 1.0 collective-permute-done.1
  25.3 1.9 collective-permute-start.2
  27.6 3.3 %collective-permute-start.7 = (f32[1,1,8,8,128]{4,2,3,1,0:T(8,128)S(1)}, f32[1,1,8,8,128]{4,2,3,1,0:T(8,128)S(1)}, u32[]{:S(2)}, u32[]{:S(2)}) collective-permute-start(f32[1,1,8,8,128]{4,2,3,1,0:T(8,128)S(1)} %get-tuple-element.31), channel_id=1, source_target_pairs={{1,0},{2,1},{3,2},{5,4},{6,5},{7,6},{9,8},{10,9},{11,10},{13,12},{... | collective-permute-start | bytes 98312 | tf_op jit(solution)/shard_map/ppermute | solution.py:19
  30.9 1.9 collective-permute-start.3
  33.2 1.2 collective-permute-done.3
  37.6 1.3 collective-permute-start.9
  38.9 5.4 %collective-permute-start.8 = (f32[1,1,8,8,128]{4,3,2,1,0:T(8,128)S(1)}, f32[1,1,8,8,128]{4,3,2,1,0:T(8,128)S(1)}, u32[]{:S(2)}, u32[]{:S(2)}) collective-permute-start(f32[1,1,8,8,128]{4,3,2,1,0:T(8,128)S(1)} %bitcast.500), channel_id=1, source_target_pairs={{0,4},{4,8},{8,12},{12,16},{16,20},{20,24},{24,28},{1,5},{5,9},{9,... | collective-permute-start | bytes 98312 | tf_op jit(solution)/shard_map/ppermute | solution.py:16
  44.4 1.5 collective-permute-done.8
  46.0 1.9 collective-permute-start.10
  47.9 3.3 %collective-permute-done.10 = f32[1,1,8,8,128]{4,2,3,1,0:T(8,128)S(1)} collective-permute-done((f32[1,1,8,8,128]{4,2,3,1,0:T(8,128)S(1)}, f32[1,1,8,8,128]{4,2,3,1,0:T(8,128)S(1)}, u32[]{:S(2)}, u32[]{:S(2)}) %collective-permute-start.10) | collective-permute-done | bytes 32800 | tf_op jit(solution)/shard_map/ppermute | solution.py:16
  51.2 1.9 collective-permute-start.11
  53.1 1.6 collective-permute-done.11
  56.9 4.8 %collective-permute-start.12 = (f32[1,1,8,8,128]{4,3,2,1,0:T(8,128)S(1)}, f32[1,1,8,8,128]{4,3,2,1,0:T(8,128)S(1)}, u32[]{:S(2)}, u32[]{:S(2)}) collective-permute-start(f32[1,1,8,8,128]{4,3,2,1,0:T(8,128)S(1)} %get-tuple-element.54), channel_id=1, source_target_pairs={{0,4},{4,8},{8,12},{12,16},{16,20},{20,24},{24,28},{1,5},{5,9},{9,... | collective-permute-start | bytes 98312 | tf_op jit(solution)/shard_map/ppermute | solution.py:16
  61.7 1.3 collective-permute-start.13
  63.3 5.4 %collective-permute-done.13 = f32[1,1,8,8,128]{4,3,2,1,0:T(8,128)S(1)} collective-permute-done((f32[1,1,8,8,128]{4,3,2,1,0:T(8,128)S(1)}, f32[1,1,8,8,128]{4,3,2,1,0:T(8,128)S(1)}, u32[]{:S(2)}, u32[]{:S(2)}) %collective-permute-start.13) | collective-permute-done | bytes 32800 | tf_op jit(solution)/shard_map/ppermute | solution.py:19
  68.8 1.9 collective-permute-start.14
  70.7 3.3 %collective-permute-done.14 = f32[1,1,8,8,128]{4,3,2,1,0:T(8,128)S(1)} collective-permute-done((f32[1,1,8,8,128]{4,3,2,1,0:T(8,128)S(1)}, f32[1,1,8,8,128]{4,3,2,1,0:T(8,128)S(1)}, u32[]{:S(2)}, u32[]{:S(2)}) %collective-permute-start.14) | collective-permute-done | bytes 32800 | tf_op jit(solution)/shard_map/ppermute | solution.py:16
  74.0 1.9 collective-permute-start.15
  76.0 1.6 collective-permute-done.15
  79.4 1.0 fusion.14
  80.4 4.8 %collective-permute-start.16 = (f32[1,1,8,8,128]{4,3,2,1,0:T(8,128)S(1)}, f32[1,1,8,8,128]{4,3,2,1,0:T(8,128)S(1)}, u32[]{:S(2)}, u32[]{:S(2)}) collective-permute-start(f32[1,1,8,8,128]{4,3,2,1,0:T(8,128)S(1)} %get-tuple-element.46), channel_id=1, source_target_pairs={{0,4},{4,8},{8,12},{12,16},{16,20},{20,24},{24,28},{1,5},{5,9},{9,... | collective-permute-start | bytes 98312 | tf_op jit(solution)/shard_map/ppermute | solution.py:16
  85.2 1.3 collective-permute-start.17
  86.8 4.2 %collective-permute-done.17 = f32[1,1,8,8,128]{4,3,2,1,0:T(8,128)S(1)} collective-permute-done((f32[1,1,8,8,128]{4,3,2,1,0:T(8,128)S(1)}, f32[1,1,8,8,128]{4,3,2,1,0:T(8,128)S(1)}, u32[]{:S(2)}, u32[]{:S(2)}) %collective-permute-start.17) | collective-permute-done | bytes 32800 | tf_op jit(solution)/shard_map/ppermute | solution.py:19
  91.1 1.9 collective-permute-start.18
  93.0 3.3 %collective-permute-done.18 = f32[1,1,8,8,128]{4,3,2,1,0:T(8,128)S(1)} collective-permute-done((f32[1,1,8,8,128]{4,3,2,1,0:T(8,128)S(1)}, f32[1,1,8,8,128]{4,3,2,1,0:T(8,128)S(1)}, u32[]{:S(2)}, u32[]{:S(2)}) %collective-permute-start.18) | collective-permute-done | bytes 32800 | tf_op jit(solution)/shard_map/ppermute | solution.py:16
  96.3 2.1 collective-permute-start.19
  98.5 1.3 collective-permute-done.19
  101.9 1.2 fusion.18
  103.1 2.9 collective-permute-start.20
  106.0 1.3 collective-permute-start.21
  107.6 4.2 %collective-permute-done.21 = f32[1,1,8,8,128]{4,3,2,1,0:T(8,128)S(1)} collective-permute-done((f32[1,1,8,8,128]{4,3,2,1,0:T(8,128)S(1)}, f32[1,1,8,8,128]{4,3,2,1,0:T(8,128)S(1)}, u32[]{:S(2)}, u32[]{:S(2)}) %collective-permute-start.21) | collective-permute-done | bytes 32800 | tf_op jit(solution)/shard_map/ppermute | solution.py:19
  111.9 1.9 collective-permute-start.22
  115.7 22.6 %scatter_custom_fusion.1 = f32[65536]{0:T(1024)} fusion(s32[4096]{0:T(1024)S(1)} %bitcast.506, f32[4096]{0:T(1024)S(1)} %bitcast.504, f32[]{:T(128)} %constant.15.clone.1), kind=kCustom, calls=%fused_computation.122 | custom fusion | flops 4096 | bytes 262148 | tf_op jit(solution)/shard_map/scatter-add | solution.py:159
  138.3 3.6 %collective-permute-start.23 = (f32[1,1,8,8,128]{4,2,3,1,0:T(8,128)S(1)}, f32[1,1,8,8,128]{4,2,3,1,0:T(8,128)S(1)}, u32[]{:S(2)}, u32[]{:S(2)}) collective-permute-start(f32[1,1,8,8,128]{4,2,3,1,0:T(8,128)S(1)} %get-tuple-element.19), channel_id=1, source_target_pairs={{1,0},{2,1},{3,2},{5,4},{6,5},{7,6},{9,8},{10,9},{11,10},{13,12},{... | collective-permute-start | bytes 98312 | tf_op jit(solution)/shard_map/ppermute | solution.py:19
  142.8 23.0 %gather_fusion.1 = f32[4096]{0:T(1024)S(1)} fusion(f32[65536]{0:T(1024)S(1)} %bitcast.434, s32[4096]{0:T(1024)S(1)} %broadcast_clamp_fusion), kind=kCustom, calls=%fused_computation.1 | custom fusion | bytes 49152 | tf_op jit(solution)/shard_map/gather | solution.py:151
  165.9 22.6 %scatter_custom_fusion = f32[65536]{0:T(1024)} fusion(s32[4096]{0:T(1024)S(1)} %bitcast.507, f32[4096]{0:T(1024)S(1)} %mul.1170, f32[]{:T(128)} %constant.15.clone.1), kind=kCustom, calls=%fused_computation.124 | custom fusion | flops 4096 | bytes 262148 | tf_op jit(solution)/shard_map/scatter-add | solution.py:158
  188.7 32.5 %all-reduce.21.cloned.1.call-done = (f32[65536]{0:T(1024)}, f32[65536]{0:T(1024)}) async-done(((f32[65536]{0:T(1024)}, f32[65536]{0:T(1024)}), (f32[65536]{0:T(1024)}, f32[65536]{0:T(1024)})) %all-reduce.21.cloned.1.call-update) | async-done | bytes 524304
  221.2 1.5 dynamic-slice.1
  222.7 1.5 dynamic-slice.3
  224.3 0.9 copy.223
  225.1 71.5 %all-reduce.19.cloned.1.call-done = (f32[16384]{0:T(1024)}, f32[16384]{0:T(1024)}) async-done(((f32[16384]{0:T(1024)}, f32[16384]{0:T(1024)}), (f32[16384]{0:T(1024)}, f32[16384]{0:T(1024)})) %all-reduce.19.cloned.1.call-update) | async-done | bytes 131088 | tf_op jit(solution)/shard_map/psum | solution.py:164
  296.7 1.5 maximum_divide_fusion.1
  (149 shorter events, 16.5 us)
Async XLA Ops:
  7.2 214.1 %all-reduce.21.cloned.1.call-start = ((), (), s32[]{:S(2)}) async-start(), calls=%async_computation.1 | async-start | bytes 1048576
  8.0 4.9 %copy-start.9 = (f32[4,1,1,128]{3,2,1,0:T(1,128)S(1)}, f32[4,1,1,128]{3,2,1,0:T(1,128)}, u32[]{:S(2)}) copy-start(f32[4,1,1,128]{3,2,1,0:T(1,128)} %param.9) | copy-start | bytes 6148
  8.0 4.9 %copy-start.1 = (f32[8,8]{1,0:T(8,128)S(1)}, f32[8,8]{1,0:T(8,128)}, u32[]{:S(2)}) copy-start(f32[8,8]{1,0:T(8,128)} %constant.38.clone) | copy-start | bytes 772
  8.0 13.4 %collective-permute-start.4 = (f32[1,1,8,8,128]{4,3,2,1,0:T(8,128)S(1)}, f32[1,1,8,8,128]{4,3,2,1,0:T(8,128)S(1)}, u32[]{:S(2)}, u32[]{:S(2)}) collective-permute-start(f32[1,1,8,8,128]{4,3,2,1,0:T(8,128)S(1)} %get-tuple-element.74), channel_id=1, source_target_pairs={{0,4},{4,8},{8,12},{12,16},{16,20},{20,24},{24,28},{1,5},{5,9},{9,... | collective-permute-start | bytes 98312 | tf_op jit(solution)/shard_map/ppermute | solution.py:16
  11.6 9.9 %collective-permute-start.5 = (f32[1,1,8,8,128]{4,3,2,1,0:T(8,128)S(1)}, f32[1,1,8,8,128]{4,3,2,1,0:T(8,128)S(1)}, u32[]{:S(2)}, u32[]{:S(2)}) collective-permute-start(f32[1,1,8,8,128]{4,3,2,1,0:T(8,128)S(1)} %get-tuple-element.75), channel_id=1, source_target_pairs={{4,0},{8,4},{12,8},{16,12},{20,16},{24,20},{28,24},{5,1},{9,5},{13... | collective-permute-start | bytes 98312 | tf_op jit(solution)/shard_map/ppermute | solution.py:19
  13.5 0.7 copy-start.8
  14.5 9.8 %collective-permute-start = (f32[1,1,8,8,128]{4,3,2,1,0:T(8,128)S(1)}, f32[1,1,8,8,128]{4,3,2,1,0:T(8,128)S(1)}, u32[]{:S(2)}, u32[]{:S(2)}) collective-permute-start(f32[1,1,8,8,128]{4,3,2,1,0:T(8,128)S(1)} %get-tuple-element.70), channel_id=1, source_target_pairs={{0,4},{4,8},{8,12},{12,16},{16,20},{20,24},{24,28},{1,5},{5,9},{9,... | collective-permute-start | bytes 98312 | tf_op jit(solution)/shard_map/ppermute | solution.py:16
  19.1 6.2 %collective-permute-start.1 = (f32[1,1,8,8,128]{4,3,2,1,0:T(8,128)S(1)}, f32[1,1,8,8,128]{4,3,2,1,0:T(8,128)S(1)}, u32[]{:S(2)}, u32[]{:S(2)}) collective-permute-start(f32[1,1,8,8,128]{4,3,2,1,0:T(8,128)S(1)} %get-tuple-element.71), channel_id=1, source_target_pairs={{4,0},{8,4},{12,8},{16,12},{20,16},{24,20},{28,24},{5,1},{9,5},{13... | collective-permute-start | bytes 98312 | tf_op jit(solution)/shard_map/ppermute | solution.py:19
  20.4 0.9 slice-start
  21.3 0.9 copy-start.2
  22.4 5.2 %collective-permute-start.6 = (f32[1,1,8,8,128]{4,2,3,1,0:T(8,128)S(1)}, f32[1,1,8,8,128]{4,2,3,1,0:T(8,128)S(1)}, u32[]{:S(2)}, u32[]{:S(2)}) collective-permute-start(f32[1,1,8,8,128]{4,2,3,1,0:T(8,128)S(1)} %maximum_bitcast_fusion.12), channel_id=1, source_target_pairs={{0,1},{1,2},{2,3},{4,5},{5,6},{6,7},{8,9},{9,10},{10,11},{12,13},{... | collective-permute-start | bytes 98312 | tf_op jit(solution)/shard_map/ppermute | solution.py:16
  25.3 5.6 %collective-permute-start.2 = (f32[1,1,8,8,128]{4,3,2,1,0:T(8,128)S(1)}, f32[1,1,8,8,128]{4,3,2,1,0:T(8,128)S(1)}, u32[]{:S(2)}, u32[]{:S(2)}) collective-permute-start(f32[1,1,8,8,128]{4,3,2,1,0:T(8,128)S(1)} %maximum_bitcast_fusion.14), channel_id=1, source_target_pairs={{0,1},{1,2},{2,3},{4,5},{5,6},{6,7},{8,9},{9,10},{10,11},{12,13},{... | collective-permute-start | bytes 98312 | tf_op jit(solution)/shard_map/ppermute | solution.py:16
  27.6 5.3 %collective-permute-start.7 = (f32[1,1,8,8,128]{4,2,3,1,0:T(8,128)S(1)}, f32[1,1,8,8,128]{4,2,3,1,0:T(8,128)S(1)}, u32[]{:S(2)}, u32[]{:S(2)}) collective-permute-start(f32[1,1,8,8,128]{4,2,3,1,0:T(8,128)S(1)} %get-tuple-element.31), channel_id=1, source_target_pairs={{1,0},{2,1},{3,2},{5,4},{6,5},{7,6},{9,8},{10,9},{11,10},{13,12},{... | collective-permute-start | bytes 98312 | tf_op jit(solution)/shard_map/ppermute | solution.py:19
  30.9 3.5 %collective-permute-start.3 = (f32[1,1,8,8,128]{4,3,2,1,0:T(8,128)S(1)}, f32[1,1,8,8,128]{4,3,2,1,0:T(8,128)S(1)}, u32[]{:S(2)}, u32[]{:S(2)}) collective-permute-start(f32[1,1,8,8,128]{4,3,2,1,0:T(8,128)S(1)} %get-tuple-element.27), channel_id=1, source_target_pairs={{1,0},{2,1},{3,2},{5,4},{6,5},{7,6},{9,8},{10,9},{11,10},{13,12},{... | collective-permute-start | bytes 98312 | tf_op jit(solution)/shard_map/ppermute | solution.py:19
  34.9 0.7 copy-start.3
  37.6 6.8 %collective-permute-start.9 = (f32[1,1,8,8,128]{4,3,2,1,0:T(8,128)S(1)}, f32[1,1,8,8,128]{4,3,2,1,0:T(8,128)S(1)}, u32[]{:S(2)}, u32[]{:S(2)}) collective-permute-start(f32[1,1,8,8,128]{4,3,2,1,0:T(8,128)S(1)} %bitcast.498), channel_id=1, source_target_pairs={{4,0},{8,4},{12,8},{16,12},{20,16},{24,20},{28,24},{5,1},{9,5},{13... | collective-permute-start | bytes 98312 | tf_op jit(solution)/shard_map/ppermute | solution.py:19
  38.9 7.0 %collective-permute-start.8 = (f32[1,1,8,8,128]{4,3,2,1,0:T(8,128)S(1)}, f32[1,1,8,8,128]{4,3,2,1,0:T(8,128)S(1)}, u32[]{:S(2)}, u32[]{:S(2)}) collective-permute-start(f32[1,1,8,8,128]{4,3,2,1,0:T(8,128)S(1)} %bitcast.500), channel_id=1, source_target_pairs={{0,4},{4,8},{8,12},{12,16},{16,20},{20,24},{24,28},{1,5},{5,9},{9,... | collective-permute-start | bytes 98312 | tf_op jit(solution)/shard_map/ppermute | solution.py:16
  46.0 5.2 %collective-permute-start.10 = (f32[1,1,8,8,128]{4,2,3,1,0:T(8,128)S(1)}, f32[1,1,8,8,128]{4,2,3,1,0:T(8,128)S(1)}, u32[]{:S(2)}, u32[]{:S(2)}) collective-permute-start(f32[1,1,8,8,128]{4,2,3,1,0:T(8,128)S(1)} %maximum_bitcast_fusion.8), channel_id=1, source_target_pairs={{0,1},{1,2},{2,3},{4,5},{5,6},{6,7},{8,9},{9,10},{10,11},{12,13},{... | collective-permute-start | bytes 98312 | tf_op jit(solution)/shard_map/ppermute | solution.py:16
  51.2 3.5 %collective-permute-start.11 = (f32[1,1,8,8,128]{4,2,3,1,0:T(8,128)S(1)}, f32[1,1,8,8,128]{4,2,3,1,0:T(8,128)S(1)}, u32[]{:S(2)}, u32[]{:S(2)}) collective-permute-start(f32[1,1,8,8,128]{4,2,3,1,0:T(8,128)S(1)} %get-tuple-element.25), channel_id=1, source_target_pairs={{1,0},{2,1},{3,2},{5,4},{6,5},{7,6},{9,8},{10,9},{11,10},{13,12},{... | collective-permute-start | bytes 98312 | tf_op jit(solution)/shard_map/ppermute | solution.py:19
  56.9 6.4 %collective-permute-start.12 = (f32[1,1,8,8,128]{4,3,2,1,0:T(8,128)S(1)}, f32[1,1,8,8,128]{4,3,2,1,0:T(8,128)S(1)}, u32[]{:S(2)}, u32[]{:S(2)}) collective-permute-start(f32[1,1,8,8,128]{4,3,2,1,0:T(8,128)S(1)} %get-tuple-element.54), channel_id=1, source_target_pairs={{0,4},{4,8},{8,12},{12,16},{16,20},{20,24},{24,28},{1,5},{5,9},{9,... | collective-permute-start | bytes 98312 | tf_op jit(solution)/shard_map/ppermute | solution.py:16
  61.7 7.0 %collective-permute-start.13 = (f32[1,1,8,8,128]{4,3,2,1,0:T(8,128)S(1)}, f32[1,1,8,8,128]{4,3,2,1,0:T(8,128)S(1)}, u32[]{:S(2)}, u32[]{:S(2)}) collective-permute-start(f32[1,1,8,8,128]{4,3,2,1,0:T(8,128)S(1)} %get-tuple-element.55), channel_id=1, source_target_pairs={{4,0},{8,4},{12,8},{16,12},{20,16},{24,20},{28,24},{5,1},{9,5},{13... | collective-permute-start | bytes 98312 | tf_op jit(solution)/shard_map/ppermute | solution.py:19
  68.8 5.2 %collective-permute-start.14 = (f32[1,1,8,8,128]{4,3,2,1,0:T(8,128)S(1)}, f32[1,1,8,8,128]{4,3,2,1,0:T(8,128)S(1)}, u32[]{:S(2)}, u32[]{:S(2)}) collective-permute-start(f32[1,1,8,8,128]{4,3,2,1,0:T(8,128)S(1)} %maximum_bitcast_fusion.6), channel_id=1, source_target_pairs={{0,1},{1,2},{2,3},{4,5},{5,6},{6,7},{8,9},{9,10},{10,11},{12,13},{... | collective-permute-start | bytes 98312 | tf_op jit(solution)/shard_map/ppermute | solution.py:16
  74.0 3.5 %collective-permute-start.15 = (f32[1,1,8,8,128]{4,3,2,1,0:T(8,128)S(1)}, f32[1,1,8,8,128]{4,3,2,1,0:T(8,128)S(1)}, u32[]{:S(2)}, u32[]{:S(2)}) collective-permute-start(f32[1,1,8,8,128]{4,3,2,1,0:T(8,128)S(1)} %get-tuple-element.23), channel_id=1, source_target_pairs={{1,0},{2,1},{3,2},{5,4},{6,5},{7,6},{9,8},{10,9},{11,10},{13,12},{... | collective-permute-start | bytes 98312 | tf_op jit(solution)/shard_map/ppermute | solution.py:19
  80.4 6.4 %collective-permute-start.16 = (f32[1,1,8,8,128]{4,3,2,1,0:T(8,128)S(1)}, f32[1,1,8,8,128]{4,3,2,1,0:T(8,128)S(1)}, u32[]{:S(2)}, u32[]{:S(2)}) collective-permute-start(f32[1,1,8,8,128]{4,3,2,1,0:T(8,128)S(1)} %get-tuple-element.46), channel_id=1, source_target_pairs={{0,4},{4,8},{8,12},{12,16},{16,20},{20,24},{24,28},{1,5},{5,9},{9,... | collective-permute-start | bytes 98312 | tf_op jit(solution)/shard_map/ppermute | solution.py:16
  85.2 5.8 %collective-permute-start.17 = (f32[1,1,8,8,128]{4,3,2,1,0:T(8,128)S(1)}, f32[1,1,8,8,128]{4,3,2,1,0:T(8,128)S(1)}, u32[]{:S(2)}, u32[]{:S(2)}) collective-permute-start(f32[1,1,8,8,128]{4,3,2,1,0:T(8,128)S(1)} %get-tuple-element.47), channel_id=1, source_target_pairs={{4,0},{8,4},{12,8},{16,12},{20,16},{24,20},{28,24},{5,1},{9,5},{13... | collective-permute-start | bytes 98312 | tf_op jit(solution)/shard_map/ppermute | solution.py:19
  91.1 7.4 %copy-start.4 = (s32[1,4096]{1,0:T(1,128)S(1)}, s32[1,4096]{1,0:T(1,128)}, u32[]{:S(2)}) copy-start(s32[1,4096]{1,0:T(1,128)} %param.12) | copy-start | bytes 49156
  91.1 7.4 %copy-start.5 = (s32[1,4096,1]{1,2,0:T(1,128)S(1)}, s32[1,4096,1]{1,2,0:T(1,128)}, u32[]{:S(2)}) copy-start(s32[1,4096,1]{1,2,0:T(1,128)} %param.11) | copy-start | bytes 49156
  91.1 5.2 %collective-permute-start.18 = (f32[1,1,8,8,128]{4,3,2,1,0:T(8,128)S(1)}, f32[1,1,8,8,128]{4,3,2,1,0:T(8,128)S(1)}, u32[]{:S(2)}, u32[]{:S(2)}) collective-permute-start(f32[1,1,8,8,128]{4,3,2,1,0:T(8,128)S(1)} %maximum_bitcast_fusion.4), channel_id=1, source_target_pairs={{0,1},{1,2},{2,3},{4,5},{5,6},{6,7},{8,9},{9,10},{10,11},{12,13},{... | collective-permute-start | bytes 98312 | tf_op jit(solution)/shard_map/ppermute | solution.py:16
  96.3 3.5 %collective-permute-start.19 = (f32[1,1,8,8,128]{4,3,2,1,0:T(8,128)S(1)}, f32[1,1,8,8,128]{4,3,2,1,0:T(8,128)S(1)}, u32[]{:S(2)}, u32[]{:S(2)}) collective-permute-start(f32[1,1,8,8,128]{4,3,2,1,0:T(8,128)S(1)} %get-tuple-element.21), channel_id=1, source_target_pairs={{1,0},{2,1},{3,2},{5,4},{6,5},{7,6},{9,8},{10,9},{11,10},{13,12},{... | collective-permute-start | bytes 98312 | tf_op jit(solution)/shard_map/ppermute | solution.py:19
  103.1 4.3 %copy-start.7 = (s32[1,4096]{1,0:T(1,128)S(1)}, s32[1,4096]{1,0:T(1,128)}, u32[]{:S(2)}) copy-start(s32[1,4096]{1,0:T(1,128)} %param.10) | copy-start | bytes 49156
  103.1 4.5 %collective-permute-start.20 = (f32[1,1,8,8,128]{4,3,2,1,0:T(8,128)S(1)}, f32[1,1,8,8,128]{4,3,2,1,0:T(8,128)S(1)}, u32[]{:S(2)}, u32[]{:S(2)}) collective-permute-start(f32[1,1,8,8,128]{4,3,2,1,0:T(8,128)S(1)} %get-tuple-element.38), channel_id=1, source_target_pairs={{0,4},{4,8},{8,12},{12,16},{16,20},{20,24},{24,28},{1,5},{5,9},{9,... | collective-permute-start | bytes 98312 | tf_op jit(solution)/shard_map/ppermute | solution.py:16
  106.0 5.8 %collective-permute-start.21 = (f32[1,1,8,8,128]{4,3,2,1,0:T(8,128)S(1)}, f32[1,1,8,8,128]{4,3,2,1,0:T(8,128)S(1)}, u32[]{:S(2)}, u32[]{:S(2)}) collective-permute-start(f32[1,1,8,8,128]{4,3,2,1,0:T(8,128)S(1)} %get-tuple-element.39), channel_id=1, source_target_pairs={{4,0},{8,4},{12,8},{16,12},{20,16},{24,20},{28,24},{5,1},{9,5},{13... | collective-permute-start | bytes 98312 | tf_op jit(solution)/shard_map/ppermute | solution.py:19
  111.9 26.4 %collective-permute-start.22 = (f32[1,1,8,8,128]{4,2,3,1,0:T(8,128)S(1)}, f32[1,1,8,8,128]{4,2,3,1,0:T(8,128)S(1)}, u32[]{:S(2)}, u32[]{:S(2)}) collective-permute-start(f32[1,1,8,8,128]{4,2,3,1,0:T(8,128)S(1)} %maximum_bitcast_fusion.2), channel_id=1, source_target_pairs={{0,1},{1,2},{2,3},{4,5},{5,6},{6,7},{8,9},{9,10},{10,11},{12,13},{... | collective-permute-start | bytes 98312 | tf_op jit(solution)/shard_map/ppermute | solution.py:16
  113.8 1.9 copy-start.6
  113.8 0.7 copy-start.10
  138.3 50.2 %collective-permute-start.23 = (f32[1,1,8,8,128]{4,2,3,1,0:T(8,128)S(1)}, f32[1,1,8,8,128]{4,2,3,1,0:T(8,128)S(1)}, u32[]{:S(2)}, u32[]{:S(2)}) collective-permute-start(f32[1,1,8,8,128]{4,2,3,1,0:T(8,128)S(1)} %get-tuple-element.19), channel_id=1, source_target_pairs={{1,0},{2,1},{3,2},{5,4},{6,5},{7,6},{9,8},{10,9},{11,10},{13,12},{... | collective-permute-start | bytes 98312 | tf_op jit(solution)/shard_map/ppermute | solution.py:19
  142.8 23.1 %copy-start = (f32[1,1,8,8,8,128]{5,4,3,2,1,0:T(8,128)}, f32[1,1,8,8,8,128]{5,4,3,2,1,0:T(8,128)S(1)}, u32[]{:S(2)}) copy-start(f32[1,1,8,8,8,128]{5,4,3,2,1,0:T(8,128)S(1)} %add_add_fusion) | copy-start | bytes 786436
  188.5 108.2 %all-reduce.19.cloned.1.call-start = ((), (), s32[]{:S(2)}) async-start(), calls=%async_computation | async-start | bytes 262144 | tf_op jit(solution)/shard_map/psum | solution.py:164
Sparse Core Ops, SparseCore 0:
  188.6 32.5 all-reduce.20
  225.3 71.3 all-reduce.18
where the time goes:
time: 308 us; the launch traced here: 305 us
  waiting for transfers between devices  137 us (44%)
  starting transfers between devices  60.3 us (20%)
  other arithmetic  51.4 us (17%)
  local copies, waits for them, and re-layouts  33.5 us (11%)
  between operations  15.7 us (5%)
  matrix products  7.11 us (2%)
    psum x1, waiting for transfers between devices, on_device(): total_numer, total_denom = lax.psum((strip_numer, strip_denom), 'ex')  71.5 us
    ppermute x12, starting transfers between devices, padded_2(): lax.ppermute(lax.slice_in_dim(block, block.shape[dim] - width, None, axis...  37.6 us
    unnamed x3, waiting for transfers between devices  32.5 us
    gather x1, local copies, waits for them, and re-layouts, on_device(): samples = pressure.reshape(-1)[picks]  23 us
    scatter-add x1, other arithmetic, on_device(): full_denom = jax.ops.segment_sum(areas, global_ids, strips * SHELL_STRIP)  22.6 us
    scatter-add x1, other arithmetic, on_device(): full_numer = jax.ops.segment_sum(weighted, global_ids, strips * SHELL_STRIP)  22.6 us
    ppermute x12, starting transfers between devices, padded_2(): lax.ppermute(lax.slice_in_dim(block, 0, width, axis=dim), axis, backward)  22.6 us
    ppermute x12, waiting for transfers between devices, padded_2(): lax.ppermute(lax.slice_in_dim(block, 0, width, axis=dim), axis, backward)  20.6 us
  transfers between devices with their start and end apart: 26, of which 18 were waited for; matrix products, arithmetic and copies ran while one was open for 24% of the time, Pallas kernels for 0%

commit v1 on v0

--- a/solution.py
+++ b/solution.py
@@ -115,17 +115,69 @@
 
 
 def assemble(values_in):
-    lower, upper = faces(values_in, 2)
-    rim_faces = jnp.concatenate([lower, upper], 0)
-    padded = padded_2(rim_faces, (("ex", 0),), 1)
-    values_in = combine(values_in, 2, 0, lower, upper, padded[:1], padded[3:])
     lower, upper = faces(values_in, 3)
     rim_faces = jnp.concatenate([lower, upper], 1)
-    padded = padded_2(rim_faces, (("ey", 1),), 1)
+    padded = padded_2(rim_faces, (("ex", 1),), 1)
     values_in = combine(values_in, 3, 1, lower, upper, padded[:, :1], padded[:, 3:])
     lower, upper = faces(values_in, 4)
+    rim_faces = jnp.concatenate([lower, upper], 2)
+    padded = padded_2(rim_faces, (("ey", 2),), 1)
+    values_in = combine(values_in, 4, 2, lower, upper, padded[:, :, :1], padded[:, :, 3:])
+    lower, upper = faces(values_in, 5)
     empty = jnp.zeros_like(upper[..., :1])
-    return combine(values_in, 4, 4, lower, upper, empty, empty)
+    return combine(values_in, 5, 5, lower, upper, empty, empty)
+
+
+def split3(values):
+    first = lax.reduce_precision(values, exponent_bits=8, mantissa_bits=7)
+    rest = values - first
+    second = lax.reduce_precision(rest, exponent_bits=8, mantissa_bits=7)
+    third = rest - second
+    return [part.astype(jnp.bfloat16) for part in (first, second, third)]
+
+
+def one_hot(index, count):
+    return (index[:, None] == lax.broadcasted_iota(jnp.int32, (1, count), 1)).astype(jnp.bfloat16)
+
+
+def gather_flat(values, picks, lanes):
+    rows = values.shape[0] // lanes
+    table = values.reshape(rows, lanes)
+    parts = jnp.concatenate(split3(table), axis=1)
+    hit_row = one_hot(picks // lanes, rows)
+    picked = jnp.dot(hit_row, parts, preferred_element_type=jnp.float32)
+    picked = picked[:, :lanes] + picked[:, lanes : 2 * lanes] + picked[:, 2 * lanes :]
+    hit_lane = (picks % lanes)[:, None] == lax.broadcasted_iota(jnp.int32, (1, lanes), 1)
+    return jnp.sum(jnp.where(hit_lane, picked, 0.0), axis=1)
+
+
+def segment_pair(first, second, ids, bins, lanes):
+    rows = bins // lanes
+    hit_lane = one_hot(ids % lanes, lanes)
+    spread_parts = [hit_lane * part[:, None] for part in split3(first) + split3(second)]
+    rhs = jnp.concatenate(spread_parts, axis=1)
+    hit_row = one_hot(ids // lanes, rows)
+    sums = lax.dot_general(
+        hit_row, rhs, (((0,), (0,)), ((), ())), preferred_element_type=jnp.float32
+    )
+    sums = sums.reshape(rows, 6, lanes)
+    numer = sums[:, 0] + sums[:, 1] + sums[:, 2]
+    denom = sums[:, 3] + sums[:, 4] + sums[:, 5]
+    return jnp.stack([numer.reshape(-1), denom.reshape(-1)])
+
+
+def strip_totals(partial, strips, strip_size):
+    n_ex = lax.axis_size("ex")
+    piece = -(-strip_size // n_ex)
+    chunks = partial.reshape(2, strips, strip_size)
+    if piece * n_ex != strip_size:
+        chunks = jnp.pad(chunks, ((0, 0), (0, 0), (0, piece * n_ex - strip_size)))
+    chunks = chunks.reshape(2, strips, n_ex, piece).transpose(2, 1, 0, 3)
+    chunks = chunks.reshape(n_ex * strips, 2, piece)
+    mine = lax.all_to_all(chunks, ("ex", "ey"), 0, 0, tiled=True).sum(0)
+    spread_out = jnp.broadcast_to(mine[None], (n_ex, 2, piece))
+    whole = lax.all_to_all(spread_out, "ex", 0, 0, tiled=True)
+    return whole.transpose(1, 0, 2).reshape(2, n_ex * piece)[:, :strip_size]
 
 
 def on_device(source, metric, fac_point, fac_strip, fac_shell, fac_area):
@@ -135,34 +187,30 @@
     delta = (high - low) / 2.0
     sigma = theta / delta
     rho_now = 1.0 / sigma
-    rhs = assemble(source)
-    pinv = 1.0 / assemble(local_diagonal(metric, weights, stiff))
+    both = assemble(jnp.stack([source, local_diagonal(metric, weights, stiff)]))
+    rhs = both[0]
+    pinv = 1.0 / both[1]
     pressure = jnp.zeros_like(source)
     resid = rhs
     update = pinv * resid / theta
     for step in range(SWEEPS):
         pressure = pressure + update
-        resid = resid - assemble(element_apply(update, metric, weights, stiff))
+        resid = resid - assemble(element_apply(update, metric, weights, stiff)[None])[0]
         if step + 1 < SWEEPS:
             rho_new = 1.0 / (2.0 * sigma - rho_now)
             update = rho_new * rho_now * update + 2.0 * rho_new / delta * pinv * resid
             rho_now = rho_new
     picks = fac_point[0]
-    samples = pressure.reshape(-1)[picks]
+    samples = gather_flat(pressure.reshape(-1), picks, 256)
     areas = fac_area[0]
     weighted = areas * samples
     strip_of = fac_strip[0, :, 0]
     shell_of = fac_shell[0]
     strips = lax.axis_size("ey")
     global_ids = strip_of * SHELL_STRIP + shell_of
-    full_numer = jax.ops.segment_sum(weighted, global_ids, strips * SHELL_STRIP)
-    full_denom = jax.ops.segment_sum(areas, global_ids, strips * SHELL_STRIP)
-    strip_numer, strip_denom = (
-        lax.psum_scatter(full_numer, "ey", scatter_dimension=0, tiled=True),
-        lax.psum_scatter(full_denom, "ey", scatter_dimension=0, tiled=True),
-    )
-    total_numer, total_denom = lax.psum((strip_numer, strip_denom), "ex")
-    shell_load = total_numer / jnp.maximum(total_denom, 1.0)
+    partial = segment_pair(weighted, areas, global_ids, strips * SHELL_STRIP, 256)
+    total = strip_totals(partial, strips, SHELL_STRIP)
+    shell_load = total[0] / jnp.maximum(total[1], 1.0)
     return (pressure, resid, shell_load)
 
 

time: 308 us -> 156 us (0.51)
  waiting for transfers between devices: 137 us -> 57 us
  other arithmetic: 51.4 us -> 18.3 us
  local copies, waits for them, and re-layouts: 33.5 us -> 6.95 us
  between operations: 15.7 us -> 1.53 us
  matrix products: 7.11 us -> 14.5 us
  starting transfers between devices: 60.3 us -> 55.4 us
    psum x1 -> x0, waiting for transfers between devices: 71.5 us -> none  [on_device(): total_numer, total_denom = lax.psum((strip_numer, strip_denom), 'ex')]
    scatter-add x2 -> x0, other arithmetic: 45.2 us -> none  [the longest x1 22.6 us: on_device(): full_denom = jax.ops.segment_sum(areas, global_ids, strips * SHELL_STRIP)]
    unnamed x3 -> x0, waiting for transfers between devices: 32.5 us -> none
    gather x1 -> x0, local copies, waits for them, and re-layouts: 23 us -> none  [on_device(): samples = pressure.reshape(-1)[picks]]
    all_to_all x0 -> x2, waiting for transfers between devices: none -> 17.5 us  [the longest x1 10.8 us: strip_totals(): mine = lax.all_to_all(chunks, ('ex', 'ey'), 0, 0, tiled=True).sum(0)]
    all_to_all x0 -> x2, starting transfers between devices: none -> 9.13 us  [the longest x1 5.5 us: strip_totals(): mine = lax.all_to_all(chunks, ('ex', 'ey'), 0, 0, tiled=True).sum(0)]
    dot_general x0 -> x2, matrix products: none -> 8.45 us  [the longest x1 6.44 us: segment_pair(): lax.dot_general(hit_row, rhs, (((0,), (0,)), ((), ())), preferred_element...]
    ppermute x12 -> x10, starting transfers between devices: 37.6 us -> 29.9 us  [padded_2(): lax.ppermute(lax.slice_in_dim(block, block.shape[dim] - width, None, axis...]
  transfers between devices with their start and end apart: 26 -> 22, of which waited for: 18 -> 19; matrix products, arithmetic and copies ran while one was open for 24% -> 15% of each run, Pallas kernels for 0% -> 0%
where the time goes in v1:
time: 156 us; the launch traced here: 154 us
  waiting for transfers between devices  57 us (37%)
  starting transfers between devices  55.4 us (36%)
  other arithmetic  18.3 us (12%)
  matrix products  14.5 us (9%)
  local copies, waits for them, and re-layouts  6.95 us (4%)
    ppermute x10, starting transfers between devices, padded_2(): lax.ppermute(lax.slice_in_dim(block, block.shape[dim] - width, None, axis...  29.9 us
    ppermute x10, waiting for transfers between devices, padded_2(): lax.ppermute(lax.slice_in_dim(block, 0, width, axis=dim), axis, backward)  23.5 us
    ppermute x10, starting transfers between devices, padded_2(): lax.ppermute(lax.slice_in_dim(block, 0, width, axis=dim), axis, backward)  16.3 us
    ppermute x10, waiting for transfers between devices, padded_2(): lax.ppermute(lax.slice_in_dim(block, block.shape[dim] - width, None, axis...  16.1 us
    all_to_all x1, waiting for transfers between devices, strip_totals(): mine = lax.all_to_all(chunks, ('ex', 'ey'), 0, 0, tiled=True).sum(0)  10.8 us
    unnamed x5, other arithmetic  6.96 us
    all_to_all x1, waiting for transfers between devices, strip_totals(): whole = lax.all_to_all(spread_out, 'ex', 0, 0, tiled=True)  6.71 us
    dot_general x1, matrix products, segment_pair(): lax.dot_general(hit_row, rhs, (((0,), (0,)), ((), ())), preferred_element...  6.44 us
  transfers between devices with their start and end apart: 22, of which 19 were waited for; matrix products, arithmetic and copies ran while one was open for 15% of the time, Pallas kernels for 0%

profile of v1, /device:TPU:2, one launch (start us, length us, event | category | flops | bytes accessed | tf_op | source)
XLA Modules:
  0.0 153.7 jit_solution(6572687039784867753)
XLA Ops:
  1.4 1.3 gather_fusion
  6.2 3.4 %collective-permute-start = (f32[2,1,1,8,8,128]{5,0,4,3,2,1:T(2,128)S(1)}, f32[2,1,1,8,8,128]{5,0,4,3,2,1:T(2,128)S(1)}, u32[]{:S(2)}, u32[]{:S(2)}) collective-permute-start(f32[2,1,1,8,8,128]{5,0,4,3,2,1:T(2,128)S(1)} %maximum_bitcast_fusion.5), channel_id=1, source_target_pairs={{0,4},{4,8},{8,12},{12,16},{16,20},{20,24},{24,28},{1,5},{5,9},{9,... | collective-permute-start | bytes 196616 | tf_op jit(solution)/shard_map/ppermute | solution.py:16
  9.6 1.9 %collective-permute-done = f32[2,1,1,8,8,128]{5,0,4,3,2,1:T(2,128)S(1)} collective-permute-done((f32[2,1,1,8,8,128]{5,0,4,3,2,1:T(2,128)S(1)}, f32[2,1,1,8,8,128]{5,0,4,3,2,1:T(2,128)S(1)}, u32[]{:S(2)}, u32[]{:S(2)}) %collective-permute-start) | collective-permute-done | bytes 65568 | tf_op jit(solution)/shard_map/ppermute | solution.py:16
  12.4 1.3 collective-permute-start.1
  13.7 1.3 pad_maximum_fusion.5
  15.2 3.6 %collective-permute-done.1 = f32[2,1,1,8,8,128]{5,0,4,3,2,1:T(2,128)S(1)} collective-permute-done((f32[2,1,1,8,8,128]{5,0,4,3,2,1:T(2,128)S(1)}, f32[2,1,1,8,8,128]{5,0,4,3,2,1:T(2,128)S(1)}, u32[]{:S(2)}, u32[]{:S(2)}) %collective-permute-start.1) | collective-permute-done | bytes 65568 | tf_op jit(solution)/shard_map/ppermute | solution.py:19
  18.9 1.9 %collective-permute-start.2 = (f32[2,1,1,8,8,128]{5,3,0,4,2,1:T(8,128)S(1)}, f32[2,1,1,8,8,128]{5,3,0,4,2,1:T(8,128)S(1)}, u32[]{:S(2)}, u32[]{:S(2)}) collective-permute-start(f32[2,1,1,8,8,128]{5,3,0,4,2,1:T(8,128)S(1)} %maximum_bitcast_fusion.3), channel_id=1, source_target_pairs={{0,1},{1,2},{2,3},{4,5},{5,6},{6,7},{8,9},{9,10},{10,11},{12,13},{... | collective-permute-start | bytes 196616 | tf_op jit(solution)/shard_map/ppermute | solution.py:16
  20.9 3.6 %collective-permute-done.2 = f32[2,1,1,8,8,128]{5,3,0,4,2,1:T(8,128)S(1)} collective-permute-done((f32[2,1,1,8,8,128]{5,3,0,4,2,1:T(8,128)S(1)}, f32[2,1,1,8,8,128]{5,3,0,4,2,1:T(8,128)S(1)}, u32[]{:S(2)}, u32[]{:S(2)}) %collective-permute-start.2) | collective-permute-done | bytes 65568 | tf_op jit(solution)/shard_map/ppermute | solution.py:16
  24.6 1.9 %collective-permute-start.3 = (f32[2,1,1,8,8,128]{5,3,0,4,2,1:T(8,128)S(1)}, f32[2,1,1,8,8,128]{5,3,0,4,2,1:T(8,128)S(1)}, u32[]{:S(2)}, u32[]{:S(2)}) collective-permute-start(f32[2,1,1,8,8,128]{5,3,0,4,2,1:T(8,128)S(1)} %get-tuple-element.28), channel_id=1, source_target_pairs={{1,0},{2,1},{3,2},{5,4},{6,5},{7,6},{9,8},{10,9},{11,10},{13,12},{... | collective-permute-start | bytes 196616 | tf_op jit(solution)/shard_map/ppermute | solution.py:19
  26.6 1.7 %collective-permute-done.3 = f32[2,1,1,8,8,128]{5,3,0,4,2,1:T(8,128)S(1)} collective-permute-done((f32[2,1,1,8,8,128]{5,3,0,4,2,1:T(8,128)S(1)}, f32[2,1,1,8,8,128]{5,3,0,4,2,1:T(8,128)S(1)}, u32[]{:S(2)}, u32[]{:S(2)}) %collective-permute-start.3) | collective-permute-done | bytes 65568 | tf_op jit(solution)/shard_map/ppermute | solution.py:19
  30.3 4.8 %collective-permute-start.4 = (f32[1,1,1,8,8,128]{5,4,3,2,1,0:T(8,128)S(1)}, f32[1,1,1,8,8,128]{5,4,3,2,1,0:T(8,128)S(1)}, u32[]{:S(2)}, u32[]{:S(2)}) collective-permute-start(f32[1,1,1,8,8,128]{5,4,3,2,1,0:T(8,128)S(1)} %bitcast.487), channel_id=1, source_target_pairs={{0,4},{4,8},{8,12},{12,16},{16,20},{20,24},{24,28},{1,5},{5,9},{9,... | collective-permute-start | bytes 98312 | tf_op jit(solution)/shard_map/ppermute | solution.py:16
  35.1 1.3 collective-permute-start.5
  36.7 4.2 %collective-permute-done.5 = f32[1,1,1,8,8,128]{5,4,3,2,1,0:T(8,128)S(1)} collective-permute-done((f32[1,1,1,8,8,128]{5,4,3,2,1,0:T(8,128)S(1)}, f32[1,1,1,8,8,128]{5,4,3,2,1,0:T(8,128)S(1)}, u32[]{:S(2)}, u32[]{:S(2)}) %collective-permute-start.5) | collective-permute-done | bytes 32800 | tf_op jit(solution)/shard_map/ppermute | solution.py:19
  41.0 1.9 %collective-permute-start.6 = (f32[1,1,1,8,8,128]{5,3,4,2,1,0:T(8,128)S(1)}, f32[1,1,1,8,8,128]{5,3,4,2,1,0:T(8,128)S(1)}, u32[]{:S(2)}, u32[]{:S(2)}) collective-permute-start(f32[1,1,1,8,8,128]{5,3,4,2,1,0:T(8,128)S(1)} %maximum_bitcast_fusion.13), channel_id=1, source_target_pairs={{0,1},{1,2},{2,3},{4,5},{5,6},{6,7},{8,9},{9,10},{10,11},{12,13},{... | collective-permute-start | bytes 98312 | tf_op jit(solution)/shard_map/ppermute | solution.py:16
  42.9 3.3 %collective-permute-done.6 = f32[1,1,1,8,8,128]{5,3,4,2,1,0:T(8,128)S(1)} collective-permute-done((f32[1,1,1,8,8,128]{5,3,4,2,1,0:T(8,128)S(1)}, f32[1,1,1,8,8,128]{5,3,4,2,1,0:T(8,128)S(1)}, u32[]{:S(2)}, u32[]{:S(2)}) %collective-permute-start.6) | collective-permute-done | bytes 32800 | tf_op jit(solution)/shard_map/ppermute | solution.py:16
  46.2 1.9 %collective-permute-start.7 = (f32[1,1,1,8,8,128]{5,3,4,2,1,0:T(8,128)S(1)}, f32[1,1,1,8,8,128]{5,3,4,2,1,0:T(8,128)S(1)}, u32[]{:S(2)}, u32[]{:S(2)}) collective-permute-start(f32[1,1,1,8,8,128]{5,3,4,2,1,0:T(8,128)S(1)} %get-tuple-element.24), channel_id=1, source_target_pairs={{1,0},{2,1},{3,2},{5,4},{6,5},{7,6},{9,8},{10,9},{11,10},{13,12},{... | collective-permute-start | bytes 98312 | tf_op jit(solution)/shard_map/ppermute | solution.py:19
  48.2 1.6 %collective-permute-done.7 = f32[1,1,1,8,8,128]{5,3,4,2,1,0:T(8,128)S(1)} collective-permute-done((f32[1,1,1,8,8,128]{5,3,4,2,1,0:T(8,128)S(1)}, f32[1,1,1,8,8,128]{5,3,4,2,1,0:T(8,128)S(1)}, u32[]{:S(2)}, u32[]{:S(2)}) %collective-permute-start.7) | collective-permute-done | bytes 32800 | tf_op jit(solution)/shard_map/ppermute | solution.py:19
  51.7 4.3 %collective-permute-start.8 = (f32[1,1,1,8,8,128]{5,4,3,2,1,0:T(8,128)S(1)}, f32[1,1,1,8,8,128]{5,4,3,2,1,0:T(8,128)S(1)}, u32[]{:S(2)}, u32[]{:S(2)}) collective-permute-start(f32[1,1,1,8,8,128]{5,4,3,2,1,0:T(8,128)S(1)} %bitcast.489), channel_id=1, source_target_pairs={{0,4},{4,8},{8,12},{12,16},{16,20},{20,24},{24,28},{1,5},{5,9},{9,... | collective-permute-start | bytes 98312 | tf_op jit(solution)/shard_map/ppermute | solution.py:16
  56.0 1.3 collective-permute-start.9
  57.6 4.2 %collective-permute-done.9 = f32[1,1,1,8,8,128]{5,4,3,2,1,0:T(8,128)S(1)} collective-permute-done((f32[1,1,1,8,8,128]{5,4,3,2,1,0:T(8,128)S(1)}, f32[1,1,1,8,8,128]{5,4,3,2,1,0:T(8,128)S(1)}, u32[]{:S(2)}, u32[]{:S(2)}) %collective-permute-start.9) | collective-permute-done | bytes 32800 | tf_op jit(solution)/shard_map/ppermute | solution.py:19
  61.9 1.9 %collective-permute-start.10 = (f32[1,1,1,8,8,128]{5,3,4,2,1,0:T(8,128)S(1)}, f32[1,1,1,8,8,128]{5,3,4,2,1,0:T(8,128)S(1)}, u32[]{:S(2)}, u32[]{:S(2)}) collective-permute-start(f32[1,1,1,8,8,128]{5,3,4,2,1,0:T(8,128)S(1)} %maximum_bitcast_fusion.11), channel_id=1, source_target_pairs={{0,1},{1,2},{2,3},{4,5},{5,6},{6,7},{8,9},{9,10},{10,11},{12,13},{... | collective-permute-start | bytes 98312 | tf_op jit(solution)/shard_map/ppermute | solution.py:16
  63.8 3.3 %collective-permute-done.10 = f32[1,1,1,8,8,128]{5,3,4,2,1,0:T(8,128)S(1)} collective-permute-done((f32[1,1,1,8,8,128]{5,3,4,2,1,0:T(8,128)S(1)}, f32[1,1,1,8,8,128]{5,3,4,2,1,0:T(8,128)S(1)}, u32[]{:S(2)}, u32[]{:S(2)}) %collective-permute-start.10) | collective-permute-done | bytes 32800 | tf_op jit(solution)/shard_map/ppermute | solution.py:16
  67.1 1.9 %collective-permute-start.11 = (f32[1,1,1,8,8,128]{5,3,4,2,1,0:T(8,128)S(1)}, f32[1,1,1,8,8,128]{5,3,4,2,1,0:T(8,128)S(1)}, u32[]{:S(2)}, u32[]{:S(2)}) collective-permute-start(f32[1,1,1,8,8,128]{5,3,4,2,1,0:T(8,128)S(1)} %get-tuple-element.22), channel_id=1, source_target_pairs={{1,0},{2,1},{3,2},{5,4},{6,5},{7,6},{9,8},{10,9},{11,10},{13,12},{... | collective-permute-start | bytes 98312 | tf_op jit(solution)/shard_map/ppermute | solution.py:19
  69.1 1.6 %collective-permute-done.11 = f32[1,1,1,8,8,128]{5,3,4,2,1,0:T(8,128)S(1)} collective-permute-done((f32[1,1,1,8,8,128]{5,3,4,2,1,0:T(8,128)S(1)}, f32[1,1,1,8,8,128]{5,3,4,2,1,0:T(8,128)S(1)}, u32[]{:S(2)}, u32[]{:S(2)}) %collective-permute-start.11) | collective-permute-done | bytes 32800 | tf_op jit(solution)/shard_map/ppermute | solution.py:19
  72.6 3.4 %collective-permute-start.12 = (f32[1,1,1,8,8,128]{5,4,3,2,1,0:T(8,128)S(1)}, f32[1,1,1,8,8,128]{5,4,3,2,1,0:T(8,128)S(1)}, u32[]{:S(2)}, u32[]{:S(2)}) collective-permute-start(f32[1,1,1,8,8,128]{5,4,3,2,1,0:T(8,128)S(1)} %bitcast.485), channel_id=1, source_target_pairs={{0,4},{4,8},{8,12},{12,16},{16,20},{20,24},{24,28},{1,5},{5,9},{9,... | collective-permute-start | bytes 98312 | tf_op jit(solution)/shard_map/ppermute | solution.py:16
  76.0 1.3 collective-permute-start.13
  77.6 4.2 %collective-permute-done.13 = f32[1,1,1,8,8,128]{5,4,3,2,1,0:T(8,128)S(1)} collective-permute-done((f32[1,1,1,8,8,128]{5,4,3,2,1,0:T(8,128)S(1)}, f32[1,1,1,8,8,128]{5,4,3,2,1,0:T(8,128)S(1)}, u32[]{:S(2)}, u32[]{:S(2)}) %collective-permute-start.13) | collective-permute-done | bytes 32800 | tf_op jit(solution)/shard_map/ppermute | solution.py:19
  81.9 1.9 %collective-permute-start.14 = (f32[1,1,1,8,8,128]{5,3,4,2,1,0:T(8,128)S(1)}, f32[1,1,1,8,8,128]{5,3,4,2,1,0:T(8,128)S(1)}, u32[]{:S(2)}, u32[]{:S(2)}) collective-permute-start(f32[1,1,1,8,8,128]{5,3,4,2,1,0:T(8,128)S(1)} %maximum_bitcast_fusion.9), channel_id=1, source_target_pairs={{0,1},{1,2},{2,3},{4,5},{5,6},{6,7},{8,9},{9,10},{10,11},{12,13},{... | collective-permute-start | bytes 98312 | tf_op jit(solution)/shard_map/ppermute | solution.py:16
  83.8 3.3 %collective-permute-done.14 = f32[1,1,1,8,8,128]{5,3,4,2,1,0:T(8,128)S(1)} collective-permute-done((f32[1,1,1,8,8,128]{5,3,4,2,1,0:T(8,128)S(1)}, f32[1,1,1,8,8,128]{5,3,4,2,1,0:T(8,128)S(1)}, u32[]{:S(2)}, u32[]{:S(2)}) %collective-permute-start.14) | collective-permute-done | bytes 32800 | tf_op jit(solution)/shard_map/ppermute | solution.py:16
  87.1 1.9 %collective-permute-start.15 = (f32[1,1,1,8,8,128]{5,3,4,2,1,0:T(8,128)S(1)}, f32[1,1,1,8,8,128]{5,3,4,2,1,0:T(8,128)S(1)}, u32[]{:S(2)}, u32[]{:S(2)}) collective-permute-start(f32[1,1,1,8,8,128]{5,3,4,2,1,0:T(8,128)S(1)} %get-tuple-element.17), channel_id=1, source_target_pairs={{1,0},{2,1},{3,2},{5,4},{6,5},{7,6},{9,8},{10,9},{11,10},{13,12},{... | collective-permute-start | bytes 98312 | tf_op jit(solution)/shard_map/ppermute | solution.py:19
  89.1 1.5 %collective-permute-done.15 = f32[1,1,1,8,8,128]{5,3,4,2,1,0:T(8,128)S(1)} collective-permute-done((f32[1,1,1,8,8,128]{5,3,4,2,1,0:T(8,128)S(1)}, f32[1,1,1,8,8,128]{5,3,4,2,1,0:T(8,128)S(1)}, u32[]{:S(2)}, u32[]{:S(2)}) %collective-permute-start.15) | collective-permute-done | bytes 32800 | tf_op jit(solution)/shard_map/ppermute | solution.py:19
  92.9 4.3 %collective-permute-start.16 = (f32[1,1,1,8,8,128]{5,4,3,2,1,0:T(8,128)S(1)}, f32[1,1,1,8,8,128]{5,4,3,2,1,0:T(8,128)S(1)}, u32[]{:S(2)}, u32[]{:S(2)}) collective-permute-start(f32[1,1,1,8,8,128]{5,4,3,2,1,0:T(8,128)S(1)} %bitcast.481), channel_id=1, source_target_pairs={{0,4},{4,8},{8,12},{12,16},{16,20},{20,24},{24,28},{1,5},{5,9},{9,... | collective-permute-start | bytes 98312 | tf_op jit(solution)/shard_map/ppermute | solution.py:16
  97.3 1.5 collective-permute-start.17
  98.7 2.0 %fusion.9 = f32[4096,768]{0,1:T(8,128)S(1)} fusion(s32[4096]{0:T(1024)S(1)} %get-tuple-element.69, bf16[256,256]{1,0:T(8,128)(2,1)S(1)} %get-tuple-element.34, bf16[256,256]{1,0:T(8,128)(2,1)S(1)} %get-tuple-element.35, bf16[256,256]{1,0:T(8,128)(2,1)S(1)} %get-tuple-element.33), kind=kOutput, calls=%fused_computation.16 | convolution fusion | flops 1612840960 | bytes 12992512 | tf_op jit(solution)/shard_map/dot_general | solution.py:148
  100.8 1.4 fusion.1
  102.2 1.4 fusion.10
  103.6 1.4 fusion.11
  105.0 1.4 fusion.12
  106.4 1.4 fusion.13
  107.8 1.4 fusion.14
  109.2 1.4 fusion.15
  110.6 6.4 %fusion.8 = f32[256,1536]{0,1:T(8,128)S(1)} fusion(bf16[4096,1536]{1,0:T(8,128)(2,1)S(1)} %fusion.15, s32[4096]{0:T(1024)S(1)} %get-tuple-element.60), kind=kOutput, calls=%fused_computation.15 | convolution fusion | flops 3222274048 | bytes 14172160 | tf_op jit(solution)/shard_map/dot_general | solution.py:160
  117.6 1.9 %collective-permute-start.18 = (f32[1,1,1,8,8,128]{5,3,4,2,1,0:T(8,128)S(1)}, f32[1,1,1,8,8,128]{5,3,4,2,1,0:T(8,128)S(1)}, u32[]{:S(2)}, u32[]{:S(2)}) collective-permute-start(f32[1,1,1,8,8,128]{5,3,4,2,1,0:T(8,128)S(1)} %maximum_bitcast_fusion.7), channel_id=1, source_target_pairs={{0,1},{1,2},{2,3},{4,5},{5,6},{6,7},{8,9},{9,10},{10,11},{12,13},{... | collective-permute-start | bytes 98312 | tf_op jit(solution)/shard_map/ppermute | solution.py:16
  120.8 5.5 %all-to-all-start = ((f32[32,2,2048]{2,1,0:T(2,128)}), f32[32,2,2048]{2,1,0:T(2,128)S(1)}, u32[]{:S(2)}, u32[]{:S(2)}) async-start(f32[32,2,2048]{2,1,0:T(2,128)} %bitcast.123), calls=%async_computation | async-start | bytes 1048576 | tf_op jit(solution)/shard_map/all_to_all | solution.py:177
  126.3 2.0 %collective-permute-start.19 = (f32[1,1,1,8,8,128]{5,3,4,2,1,0:T(8,128)S(1)}, f32[1,1,1,8,8,128]{5,3,4,2,1,0:T(8,128)S(1)}, u32[]{:S(2)}, u32[]{:S(2)}) collective-permute-start(f32[1,1,1,8,8,128]{5,3,4,2,1,0:T(8,128)S(1)} %get-tuple-element.15), channel_id=1, source_target_pairs={{1,0},{2,1},{3,2},{5,4},{6,5},{7,6},{9,8},{10,9},{11,10},{13,12},{... | collective-permute-start | bytes 98312 | tf_op jit(solution)/shard_map/ppermute | solution.py:19
  130.2 10.8 %all-to-all-done = f32[32,2,2048]{2,1,0:T(2,128)S(1)} async-done(((f32[32,2,2048]{2,1,0:T(2,128)}), f32[32,2,2048]{2,1,0:T(2,128)S(1)}, u32[]{:S(2)}, u32[]{:S(2)}) %all-to-all-start) | async-done | bytes 524320 | tf_op jit(solution)/shard_map/all_to_all | solution.py:177
  141.8 3.6 %all-to-all-start.1 = ((f32[8,2,2048]{2,1,0:T(2,128)}), f32[8,2,2048]{2,1,0:T(2,128)S(1)}, u32[]{:S(2)}, u32[]{:S(2)}) async-start(f32[8,2,2048]{2,1,0:T(2,128)} %broadcast_in_dim.180), calls=%async_computation.1 | async-start | bytes 262144 | tf_op jit(solution)/shard_map/all_to_all | solution.py:179
  146.3 6.7 %all-to-all-done.1 = f32[8,2,2048]{2,1,0:T(2,128)S(1)} async-done(((f32[8,2,2048]{2,1,0:T(2,128)}), f32[8,2,2048]{2,1,0:T(2,128)S(1)}, u32[]{:S(2)}, u32[]{:S(2)}) %all-to-all-start.1) | async-done | bytes 131104 | tf_op jit(solution)/shard_map/all_to_all | solution.py:179
  (127 shorter events, 20.4 us)
Async XLA Ops:
  6.2 5.3 %collective-permute-start = (f32[2,1,1,8,8,128]{5,0,4,3,2,1:T(2,128)S(1)}, f32[2,1,1,8,8,128]{5,0,4,3,2,1:T(2,128)S(1)}, u32[]{:S(2)}, u32[]{:S(2)}) collective-permute-start(f32[2,1,1,8,8,128]{5,0,4,3,2,1:T(2,128)S(1)} %maximum_bitcast_fusion.5), channel_id=1, source_target_pairs={{0,4},{4,8},{8,12},{12,16},{16,20},{20,24},{24,28},{1,5},{5,9},{9,... | collective-permute-start | bytes 196616 | tf_op jit(solution)/shard_map/ppermute | solution.py:16
  12.4 6.5 %collective-permute-start.1 = (f32[2,1,1,8,8,128]{5,0,4,3,2,1:T(2,128)S(1)}, f32[2,1,1,8,8,128]{5,0,4,3,2,1:T(2,128)S(1)}, u32[]{:S(2)}, u32[]{:S(2)}) collective-permute-start(f32[2,1,1,8,8,128]{5,0,4,3,2,1:T(2,128)S(1)} %get-tuple-element.30), channel_id=1, source_target_pairs={{4,0},{8,4},{12,8},{16,12},{20,16},{24,20},{28,24},{5,1},{9,5},{13... | collective-permute-start | bytes 196616 | tf_op jit(solution)/shard_map/ppermute | solution.py:19
  15.0 13.8 %copy-start = (f32[8,8,1,1]{1,0,3,2:T(8,128)S(1)}, f32[8,8,1,1]{1,0,3,2:T(8,128)}, u32[]{:S(2)}) copy-start(f32[8,8,1,1]{1,0,3,2:T(8,128)} %constant.122) | copy-start | bytes 772
  15.2 14.4 %copy-start.1 = (f32[8]{0:T(128)S(1)}, f32[8]{0:T(128)}, u32[]{:S(2)}) copy-start(f32[8]{0:T(128)} %constant.81.clone) | copy-start | bytes 100
  18.9 5.6 %collective-permute-start.2 = (f32[2,1,1,8,8,128]{5,3,0,4,2,1:T(8,128)S(1)}, f32[2,1,1,8,8,128]{5,3,0,4,2,1:T(8,128)S(1)}, u32[]{:S(2)}, u32[]{:S(2)}) collective-permute-start(f32[2,1,1,8,8,128]{5,3,0,4,2,1:T(8,128)S(1)} %maximum_bitcast_fusion.3), channel_id=1, source_target_pairs={{0,1},{1,2},{2,3},{4,5},{5,6},{6,7},{8,9},{9,10},{10,11},{12,13},{... | collective-permute-start | bytes 196616 | tf_op jit(solution)/shard_map/ppermute | solution.py:16
  24.6 3.8 %collective-permute-start.3 = (f32[2,1,1,8,8,128]{5,3,0,4,2,1:T(8,128)S(1)}, f32[2,1,1,8,8,128]{5,3,0,4,2,1:T(8,128)S(1)}, u32[]{:S(2)}, u32[]{:S(2)}) collective-permute-start(f32[2,1,1,8,8,128]{5,3,0,4,2,1:T(8,128)S(1)} %get-tuple-element.28), channel_id=1, source_target_pairs={{1,0},{2,1},{3,2},{5,4},{6,5},{7,6},{9,8},{10,9},{11,10},{13,12},{... | collective-permute-start | bytes 196616 | tf_op jit(solution)/shard_map/ppermute | solution.py:19
  30.3 6.4 %collective-permute-start.4 = (f32[1,1,1,8,8,128]{5,4,3,2,1,0:T(8,128)S(1)}, f32[1,1,1,8,8,128]{5,4,3,2,1,0:T(8,128)S(1)}, u32[]{:S(2)}, u32[]{:S(2)}) collective-permute-start(f32[1,1,1,8,8,128]{5,4,3,2,1,0:T(8,128)S(1)} %bitcast.487), channel_id=1, source_target_pairs={{0,4},{4,8},{8,12},{12,16},{16,20},{20,24},{24,28},{1,5},{5,9},{9,... | collective-permute-start | bytes 98312 | tf_op jit(solution)/shard_map/ppermute | solution.py:16
  35.1 5.8 %collective-permute-start.5 = (f32[1,1,1,8,8,128]{5,4,3,2,1,0:T(8,128)S(1)}, f32[1,1,1,8,8,128]{5,4,3,2,1,0:T(8,128)S(1)}, u32[]{:S(2)}, u32[]{:S(2)}) collective-permute-start(f32[1,1,1,8,8,128]{5,4,3,2,1,0:T(8,128)S(1)} %bitcast.493), channel_id=1, source_target_pairs={{4,0},{8,4},{12,8},{16,12},{20,16},{24,20},{28,24},{5,1},{9,5},{13... | collective-permute-start | bytes 98312 | tf_op jit(solution)/shard_map/ppermute | solution.py:19
  41.0 5.2 %collective-permute-start.6 = (f32[1,1,1,8,8,128]{5,3,4,2,1,0:T(8,128)S(1)}, f32[1,1,1,8,8,128]{5,3,4,2,1,0:T(8,128)S(1)}, u32[]{:S(2)}, u32[]{:S(2)}) collective-permute-start(f32[1,1,1,8,8,128]{5,3,4,2,1,0:T(8,128)S(1)} %maximum_bitcast_fusion.13), channel_id=1, source_target_pairs={{0,1},{1,2},{2,3},{4,5},{5,6},{6,7},{8,9},{9,10},{10,11},{12,13},{... | collective-permute-start | bytes 98312 | tf_op jit(solution)/shard_map/ppermute | solution.py:16
  46.2 3.5 %collective-permute-start.7 = (f32[1,1,1,8,8,128]{5,3,4,2,1,0:T(8,128)S(1)}, f32[1,1,1,8,8,128]{5,3,4,2,1,0:T(8,128)S(1)}, u32[]{:S(2)}, u32[]{:S(2)}) collective-permute-start(f32[1,1,1,8,8,128]{5,3,4,2,1,0:T(8,128)S(1)} %get-tuple-element.24), channel_id=1, source_target_pairs={{1,0},{2,1},{3,2},{5,4},{6,5},{7,6},{9,8},{10,9},{11,10},{13,12},{... | collective-permute-start | bytes 98312 | tf_op jit(solution)/shard_map/ppermute | solution.py:19
  51.6 25.7 %copy-start.4 = (s32[1,4096,1]{1,2,0:T(1,128)S(1)}, s32[1,4096,1]{1,2,0:T(1,128)}, u32[]{:S(2)}) copy-start(s32[1,4096,1]{1,2,0:T(1,128)} %param.11) | copy-start | bytes 49156
  51.7 5.9 %collective-permute-start.8 = (f32[1,1,1,8,8,128]{5,4,3,2,1,0:T(8,128)S(1)}, f32[1,1,1,8,8,128]{5,4,3,2,1,0:T(8,128)S(1)}, u32[]{:S(2)}, u32[]{:S(2)}) collective-permute-start(f32[1,1,1,8,8,128]{5,4,3,2,1,0:T(8,128)S(1)} %bitcast.489), channel_id=1, source_target_pairs={{0,4},{4,8},{8,12},{12,16},{16,20},{20,24},{24,28},{1,5},{5,9},{9,... | collective-permute-start | bytes 98312 | tf_op jit(solution)/shard_map/ppermute | solution.py:16
  56.0 5.8 %collective-permute-start.9 = (f32[1,1,1,8,8,128]{5,4,3,2,1,0:T(8,128)S(1)}, f32[1,1,1,8,8,128]{5,4,3,2,1,0:T(8,128)S(1)}, u32[]{:S(2)}, u32[]{:S(2)}) collective-permute-start(f32[1,1,1,8,8,128]{5,4,3,2,1,0:T(8,128)S(1)} %bitcast.495), channel_id=1, source_target_pairs={{4,0},{8,4},{12,8},{16,12},{20,16},{24,20},{28,24},{5,1},{9,5},{13... | collective-permute-start | bytes 98312 | tf_op jit(solution)/shard_map/ppermute | solution.py:19
  57.4 26.4 %copy-start.5 = (s32[1,4096]{1,0:T(1,128)S(1)}, s32[1,4096]{1,0:T(1,128)}, u32[]{:S(2)}) copy-start(s32[1,4096]{1,0:T(1,128)} %param.12) | copy-start | bytes 49156
  61.9 27.2 %copy-start.2 = (s32[1,4096]{1,0:T(1,128)S(1)}, s32[1,4096]{1,0:T(1,128)}, u32[]{:S(2)}) copy-start(s32[1,4096]{1,0:T(1,128)} %param.10) | copy-start | bytes 49156
  61.9 5.2 %collective-permute-start.10 = (f32[1,1,1,8,8,128]{5,3,4,2,1,0:T(8,128)S(1)}, f32[1,1,1,8,8,128]{5,3,4,2,1,0:T(8,128)S(1)}, u32[]{:S(2)}, u32[]{:S(2)}) collective-permute-start(f32[1,1,1,8,8,128]{5,3,4,2,1,0:T(8,128)S(1)} %maximum_bitcast_fusion.11), channel_id=1, source_target_pairs={{0,1},{1,2},{2,3},{4,5},{5,6},{6,7},{8,9},{9,10},{10,11},{12,13},{... | collective-permute-start | bytes 98312 | tf_op jit(solution)/shard_map/ppermute | solution.py:16
  67.1 3.5 %collective-permute-start.11 = (f32[1,1,1,8,8,128]{5,3,4,2,1,0:T(8,128)S(1)}, f32[1,1,1,8,8,128]{5,3,4,2,1,0:T(8,128)S(1)}, u32[]{:S(2)}, u32[]{:S(2)}) collective-permute-start(f32[1,1,1,8,8,128]{5,3,4,2,1,0:T(8,128)S(1)} %get-tuple-element.22), channel_id=1, source_target_pairs={{1,0},{2,1},{3,2},{5,4},{6,5},{7,6},{9,8},{10,9},{11,10},{13,12},{... | collective-permute-start | bytes 98312 | tf_op jit(solution)/shard_map/ppermute | solution.py:19
  72.6 5.0 %collective-permute-start.12 = (f32[1,1,1,8,8,128]{5,4,3,2,1,0:T(8,128)S(1)}, f32[1,1,1,8,8,128]{5,4,3,2,1,0:T(8,128)S(1)}, u32[]{:S(2)}, u32[]{:S(2)}) collective-permute-start(f32[1,1,1,8,8,128]{5,4,3,2,1,0:T(8,128)S(1)} %bitcast.485), channel_id=1, source_target_pairs={{0,4},{4,8},{8,12},{12,16},{16,20},{20,24},{24,28},{1,5},{5,9},{9,... | collective-permute-start | bytes 98312 | tf_op jit(solution)/shard_map/ppermute | solution.py:16
  76.0 5.8 %collective-permute-start.13 = (f32[1,1,1,8,8,128]{5,4,3,2,1,0:T(8,128)S(1)}, f32[1,1,1,8,8,128]{5,4,3,2,1,0:T(8,128)S(1)}, u32[]{:S(2)}, u32[]{:S(2)}) collective-permute-start(f32[1,1,1,8,8,128]{5,4,3,2,1,0:T(8,128)S(1)} %bitcast.491), channel_id=1, source_target_pairs={{4,0},{8,4},{12,8},{16,12},{20,16},{24,20},{28,24},{5,1},{9,5},{13... | collective-permute-start | bytes 98312 | tf_op jit(solution)/shard_map/ppermute | solution.py:19
  81.9 5.2 %collective-permute-start.14 = (f32[1,1,1,8,8,128]{5,3,4,2,1,0:T(8,128)S(1)}, f32[1,1,1,8,8,128]{5,3,4,2,1,0:T(8,128)S(1)}, u32[]{:S(2)}, u32[]{:S(2)}) collective-permute-start(f32[1,1,1,8,8,128]{5,3,4,2,1,0:T(8,128)S(1)} %maximum_bitcast_fusion.9), channel_id=1, source_target_pairs={{0,1},{1,2},{2,3},{4,5},{5,6},{6,7},{8,9},{9,10},{10,11},{12,13},{... | collective-permute-start | bytes 98312 | tf_op jit(solution)/shard_map/ppermute | solution.py:16
  87.1 3.5 %collective-permute-start.15 = (f32[1,1,1,8,8,128]{5,3,4,2,1,0:T(8,128)S(1)}, f32[1,1,1,8,8,128]{5,3,4,2,1,0:T(8,128)S(1)}, u32[]{:S(2)}, u32[]{:S(2)}) collective-permute-start(f32[1,1,1,8,8,128]{5,3,4,2,1,0:T(8,128)S(1)} %get-tuple-element.17), channel_id=1, source_target_pairs={{1,0},{2,1},{3,2},{5,4},{6,5},{7,6},{9,8},{10,9},{11,10},{13,12},{... | collective-permute-start | bytes 98312 | tf_op jit(solution)/shard_map/ppermute | solution.py:19
  92.9 24.6 %collective-permute-start.16 = (f32[1,1,1,8,8,128]{5,4,3,2,1,0:T(8,128)S(1)}, f32[1,1,1,8,8,128]{5,4,3,2,1,0:T(8,128)S(1)}, u32[]{:S(2)}, u32[]{:S(2)}) collective-permute-start(f32[1,1,1,8,8,128]{5,4,3,2,1,0:T(8,128)S(1)} %bitcast.481), channel_id=1, source_target_pairs={{0,4},{4,8},{8,12},{12,16},{16,20},{20,24},{24,28},{1,5},{5,9},{9,... | collective-permute-start | bytes 98312 | tf_op jit(solution)/shard_map/ppermute | solution.py:16
  97.3 20.3 %collective-permute-start.17 = (f32[1,1,1,8,8,128]{5,4,3,2,1,0:T(8,128)S(1)}, f32[1,1,1,8,8,128]{5,4,3,2,1,0:T(8,128)S(1)}, u32[]{:S(2)}, u32[]{:S(2)}) collective-permute-start(f32[1,1,1,8,8,128]{5,4,3,2,1,0:T(8,128)S(1)} %bitcast.483), channel_id=1, source_target_pairs={{4,0},{8,4},{12,8},{16,12},{20,16},{24,20},{28,24},{5,1},{9,5},{13... | collective-permute-start | bytes 98312 | tf_op jit(solution)/shard_map/ppermute | solution.py:19
  100.8 1.4 copy-start.3
  117.6 8.7 %collective-permute-start.18 = (f32[1,1,1,8,8,128]{5,3,4,2,1,0:T(8,128)S(1)}, f32[1,1,1,8,8,128]{5,3,4,2,1,0:T(8,128)S(1)}, u32[]{:S(2)}, u32[]{:S(2)}) collective-permute-start(f32[1,1,1,8,8,128]{5,3,4,2,1,0:T(8,128)S(1)} %maximum_bitcast_fusion.7), channel_id=1, source_target_pairs={{0,1},{1,2},{2,3},{4,5},{5,6},{6,7},{8,9},{9,10},{10,11},{12,13},{... | collective-permute-start | bytes 98312 | tf_op jit(solution)/shard_map/ppermute | solution.py:16
  120.8 20.2 %all-to-all-start = ((f32[32,2,2048]{2,1,0:T(2,128)}), f32[32,2,2048]{2,1,0:T(2,128)S(1)}, u32[]{:S(2)}, u32[]{:S(2)}) async-start(f32[32,2,2048]{2,1,0:T(2,128)} %bitcast.123), calls=%async_computation | async-start | bytes 1048576 | tf_op jit(solution)/shard_map/all_to_all | solution.py:177
  126.3 3.6 %collective-permute-start.19 = (f32[1,1,1,8,8,128]{5,3,4,2,1,0:T(8,128)S(1)}, f32[1,1,1,8,8,128]{5,3,4,2,1,0:T(8,128)S(1)}, u32[]{:S(2)}, u32[]{:S(2)}) collective-permute-start(f32[1,1,1,8,8,128]{5,3,4,2,1,0:T(8,128)S(1)} %get-tuple-element.15), channel_id=1, source_target_pairs={{1,0},{2,1},{3,2},{5,4},{6,5},{7,6},{9,8},{10,9},{11,10},{13,12},{... | collective-permute-start | bytes 98312 | tf_op jit(solution)/shard_map/ppermute | solution.py:19
  141.8 11.1 %all-to-all-start.1 = ((f32[8,2,2048]{2,1,0:T(2,128)}), f32[8,2,2048]{2,1,0:T(2,128)S(1)}, u32[]{:S(2)}, u32[]{:S(2)}) async-start(f32[8,2,2048]{2,1,0:T(2,128)} %broadcast_in_dim.180), calls=%async_computation.1 | async-start | bytes 262144 | tf_op jit(solution)/shard_map/all_to_all | solution.py:179

commit v2 on v1

--- a/solution.py
+++ b/solution.py
@@ -1,3 +1,5 @@
+import itertools
+
 import jax
 import jax.numpy as jnp
 import numpy as np
@@ -6,19 +8,6 @@
 
 SWEEPS = 4
 SHELL_STRIP = 16384
-
-
-def padded_2(block, sides, width):
-    for axis, dim in sides:
-        count = lax.axis_size(axis)
-        forward = [(i, i + 1) for i in range(count - 1)]
-        backward = [(target, source) for source, target in forward]
-        low = lax.ppermute(
-            lax.slice_in_dim(block, block.shape[dim] - width, None, axis=dim), axis, forward
-        )
-        high = lax.ppermute(lax.slice_in_dim(block, 0, width, axis=dim), axis, backward)
-        block = jnp.concatenate([low, block, high], axis=dim)
-    return block
 
 
 def gll_tables():
@@ -114,15 +103,51 @@
     )
 
 
+def shifted(block, axes, step, sizes):
+    pairs = []
+    for source in itertools.product(*[range(size) for size in sizes]):
+        target = [s + d for s, d in zip(source, step)]
+        if all(0 <= t < size for t, size in zip(target, sizes)):
+            pairs.append((linear(source, sizes), linear(target, sizes)))
+    name = axes[0] if len(axes) == 1 else axes
+    return lax.ppermute(block, name, pairs)
+
+
+def linear(place, sizes):
+    index = 0
+    for p, size in zip(place, sizes):
+        index = index * size + p
+    return index
+
+
 def assemble(values_in):
-    lower, upper = faces(values_in, 3)
-    rim_faces = jnp.concatenate([lower, upper], 1)
-    padded = padded_2(rim_faces, (("ex", 1),), 1)
-    values_in = combine(values_in, 3, 1, lower, upper, padded[:, :1], padded[:, 3:])
-    lower, upper = faces(values_in, 4)
-    rim_faces = jnp.concatenate([lower, upper], 2)
-    padded = padded_2(rim_faces, (("ey", 2),), 1)
-    values_in = combine(values_in, 4, 2, lower, upper, padded[:, :, :1], padded[:, :, 3:])
+    n_ex = lax.axis_size("ex")
+    n_ey = lax.axis_size("ey")
+    u = values_in[:, 0, 0]
+    last = u.shape[1] - 1
+    x_lo, x_hi = u[:, 0], u[:, last]
+    y_lo, y_hi = u[:, :, 0], u[:, :, last]
+    from_xm = shifted(x_hi, ("ex",), (1,), (n_ex,))
+    from_xp = shifted(x_lo, ("ex",), (-1,), (n_ex,))
+    from_ym = shifted(y_hi, ("ey",), (1,), (n_ey,))
+    from_yp = shifted(y_lo, ("ey",), (-1,), (n_ey,))
+    both = ("ex", "ey")
+    sizes = (n_ex, n_ey)
+    diag_mm = shifted(u[:, last, last], both, (1, 1), sizes)
+    diag_mp = shifted(u[:, last, 0], both, (1, -1), sizes)
+    diag_pm = shifted(u[:, 0, last], both, (-1, 1), sizes)
+    diag_pp = shifted(u[:, 0, 0], both, (-1, -1), sizes)
+    middle = u[:, 1:last]
+    u1 = jnp.concatenate([(x_lo + from_xm)[:, None], middle, (x_hi + from_xp)[:, None]], 1)
+    ym1 = jnp.concatenate(
+        [(from_ym[:, 0] + diag_mm)[:, None], from_ym[:, 1:last], (from_ym[:, last] + diag_pm)[:, None]], 1
+    )
+    yp1 = jnp.concatenate(
+        [(from_yp[:, 0] + diag_mp)[:, None], from_yp[:, 1:last], (from_yp[:, last] + diag_pp)[:, None]], 1
+    )
+    lo1, hi1 = u1[:, :, 0], u1[:, :, last]
+    u2 = jnp.concatenate([(lo1 + ym1)[:, :, None], u1[:, :, 1:last], (hi1 + yp1)[:, :, None]], 2)
+    values_in = u2[:, None, None]
     lower, upper = faces(values_in, 5)
     empty = jnp.zeros_like(upper[..., :1])
     return combine(values_in, 5, 5, lower, upper, empty, empty)

time: 156 us -> 207 us (1.33)
  starting transfers between devices: 55.4 us -> 119 us
  waiting for transfers between devices: 57 us -> 43.4 us
    ppermute x20 -> x40, starting transfers between devices: 46.3 us -> 107 us  [shifted(): return lax.ppermute(block, name, pairs)]
    all_to_all x1, waiting for transfers between devices: 10.8 us -> 1.47 us  [strip_totals(): mine = lax.all_to_all(chunks, ('ex', 'ey'), 0, 0, tiled=True).sum(0)]
    ppermute x20 -> x40, waiting for transfers between devices: 39.6 us -> 35.5 us  [shifted(): return lax.ppermute(block, name, pairs)]
  transfers between devices with their start and end apart: 22 -> 42, of which waited for: 19 -> 17; matrix products, arithmetic and copies ran while one was open for 15% -> 12% of each run, Pallas kernels for 0% -> 0%
where the time goes in v2:
time: 207 us; the launch traced here: 205 us
  starting transfers between devices  119 us (57%)
  waiting for transfers between devices  43.4 us (21%)
  other arithmetic  19.5 us (9%)
  matrix products  13.7 us (7%)
  local copies, waits for them, and re-layouts  7.37 us (4%)
  between operations  2.21 us (1%)
    ppermute x40, starting transfers between devices, shifted(): return lax.ppermute(block, name, pairs)  107 us
    ppermute x40, waiting for transfers between devices, shifted(): return lax.ppermute(block, name, pairs)  35.5 us
    unnamed x5, other arithmetic  6.96 us
    all_to_all x1, waiting for transfers between devices, strip_totals(): whole = lax.all_to_all(spread_out, 'ex', 0, 0, tiled=True)  6.44 us
    dot_general x1, matrix products, segment_pair(): lax.dot_general(hit_row, rhs, (((0,), (0,)), ((), ())), preferred_element...  6.44 us
    all_to_all x1, starting transfers between devices, strip_totals(): mine = lax.all_to_all(chunks, ('ex', 'ey'), 0, 0, tiled=True).sum(0)  6.27 us
    all_to_all x1, starting transfers between devices, strip_totals(): whole = lax.all_to_all(spread_out, 'ex', 0, 0, tiled=True)  5.22 us
  transfers between devices with their start and end apart: 42, of which 17 were waited for; matrix products, arithmetic and copies ran while one was open for 12% of the time, Pallas kernels for 0%

profile of v2, /device:TPU:2, one launch (start us, length us, event | category | flops | bytes accessed | tf_op | source)
XLA Modules:
  0.0 205.1 jit_solution(14306907096798205962)
XLA Ops:
  5.4 1.4 maximum_bitcast_fusion
  6.8 2.9 %collective-permute-start.3 = (f32[2,8,128]{2,0,1:T(2,128)S(1)}, f32[2,8,128]{2,0,1:T(2,128)S(1)}, u32[]{:S(2)}, u32[]{:S(2)}) collective-permute-start(f32[2,8,128]{2,0,1:T(2,128)S(1)} %get-tuple-element.27), channel_id=1, source_target_pairs={{0,5},{1,6},{2,7},{4,9},{5,10},{6,11},{8,13},{9,14},{10,15},{12,17... | collective-permute-start | bytes 24584 | tf_op jit(solution)/shard_map/ppermute | solution.py:113
  9.7 4.6 %collective-permute-start.6 = (f32[2,8,128]{2,0,1:T(2,128)S(1)}, f32[2,8,128]{2,0,1:T(2,128)S(1)}, u32[]{:S(2)}, u32[]{:S(2)}) collective-permute-start(f32[2,8,128]{2,0,1:T(2,128)S(1)} %get-tuple-element.28), channel_id=1, source_target_pairs={{1,4},{2,5},{3,6},{5,8},{6,9},{7,10},{9,12},{10,13},{11,14},{13,16... | collective-permute-start | bytes 24584 | tf_op jit(solution)/shard_map/ppermute | solution.py:113
  15.6 4.1 %collective-permute-start = (f32[2,8,8,128]{3,0,2,1:T(2,128)S(1)}, f32[2,8,8,128]{3,0,2,1:T(2,128)S(1)}, u32[]{:S(2)}, u32[]{:S(2)}) collective-permute-start(f32[2,8,8,128]{3,0,2,1:T(2,128)S(1)} %get-tuple-element.35), channel_id=1, source_target_pairs={{0,4},{4,8},{8,12},{12,16},{16,20},{20,24},{24,28},{1,5},{5,9},{9,... | collective-permute-start | bytes 196616 | tf_op jit(solution)/shard_map/ppermute | solution.py:113
  25.8 1.9 collective-permute-start.2
  28.1 3.3 %collective-permute-done.2 = f32[2,8,8,128]{3,0,2,1:T(2,128)S(1)} collective-permute-done((f32[2,8,8,128]{3,0,2,1:T(2,128)S(1)}, f32[2,8,8,128]{3,0,2,1:T(2,128)S(1)}, u32[]{:S(2)}, u32[]{:S(2)}) %collective-permute-start.2) | collective-permute-done | bytes 65568 | tf_op jit(solution)/shard_map/ppermute | solution.py:113
  31.4 1.9 collective-permute-start.5
  33.5 1.7 collective-permute-done.5
  37.9 4.3 %collective-permute-start.8 = (f32[1,8,8,128]{3,2,1,0:T(8,128)S(1)}, f32[1,8,8,128]{3,2,1,0:T(8,128)S(1)}, u32[]{:S(2)}, u32[]{:S(2)}) collective-permute-start(f32[1,8,8,128]{3,2,1,0:T(8,128)S(1)} %bitcast.717), channel_id=1, source_target_pairs={{0,4},{4,8},{8,12},{12,16},{16,20},{20,24},{24,28},{1,5},{5,9},{9,... | collective-permute-start | bytes 98312 | tf_op jit(solution)/shard_map/ppermute | solution.py:113
  43.5 4.5 %collective-permute-start.11 = (f32[1,8,128]{2,1,0:T(8,128)S(1)}, f32[1,8,128]{2,1,0:T(8,128)S(1)}, u32[]{:S(2)}, u32[]{:S(2)}) collective-permute-start(f32[1,8,128]{2,1,0:T(8,128)S(1)} %bitcast.730), channel_id=1, source_target_pairs={{0,5},{1,6},{2,7},{4,9},{5,10},{6,11},{8,13},{9,14},{10,15},{12,17... | collective-permute-start | bytes 12296 | tf_op jit(solution)/shard_map/ppermute | solution.py:113
  48.0 6.1 %collective-permute-start.14 = (f32[1,8,128]{2,1,0:T(8,128)S(1)}, f32[1,8,128]{2,1,0:T(8,128)S(1)}, u32[]{:S(2)}, u32[]{:S(2)}) collective-permute-start(f32[1,8,128]{2,1,0:T(8,128)S(1)} %bitcast.733), channel_id=1, source_target_pairs={{1,4},{2,5},{3,6},{5,8},{6,9},{7,10},{9,12},{10,13},{11,14},{13,16... | collective-permute-start | bytes 12296 | tf_op jit(solution)/shard_map/ppermute | solution.py:113
  56.8 6.0 %collective-permute-done.9 = f32[1,8,8,128]{3,2,1,0:T(8,128)S(1)} collective-permute-done((f32[1,8,8,128]{3,2,1,0:T(8,128)S(1)}, f32[1,8,8,128]{3,2,1,0:T(8,128)S(1)}, u32[]{:S(2)}, u32[]{:S(2)}) %collective-permute-start.9) | collective-permute-done | bytes 32800 | tf_op jit(solution)/shard_map/ppermute | solution.py:113
  62.8 1.9 collective-permute-start.13
  64.8 1.6 collective-permute-done.13
  66.3 1.9 collective-permute-start.10
  68.2 3.3 %collective-permute-done.10 = f32[1,8,8,128]{3,2,1,0:T(8,128)S(1)} collective-permute-done((f32[1,8,8,128]{3,2,1,0:T(8,128)S(1)}, f32[1,8,8,128]{3,2,1,0:T(8,128)S(1)}, u32[]{:S(2)}, u32[]{:S(2)}) %collective-permute-start.10) | collective-permute-done | bytes 32800 | tf_op jit(solution)/shard_map/ppermute | solution.py:113
  73.5 1.9 collective-permute-start.18
  75.4 1.7 collective-permute-start.19
  79.7 8.0 %collective-permute-start.22 = (f32[1,8,128]{2,1,0:T(8,128)S(1)}, f32[1,8,128]{2,1,0:T(8,128)S(1)}, u32[]{:S(2)}, u32[]{:S(2)}) collective-permute-start(f32[1,8,128]{2,1,0:T(8,128)S(1)} %get-tuple-element.75), channel_id=1, source_target_pairs={{1,4},{2,5},{3,6},{5,8},{6,9},{7,10},{9,12},{10,13},{11,14},{13,16... | collective-permute-start | bytes 12296 | tf_op jit(solution)/shard_map/ppermute | solution.py:113
  87.7 2.5 %collective-permute-start.21 = (f32[1,8,8,128]{3,2,1,0:T(8,128)S(1)}, f32[1,8,8,128]{3,2,1,0:T(8,128)S(1)}, u32[]{:S(2)}, u32[]{:S(2)}) collective-permute-start(f32[1,8,8,128]{3,2,1,0:T(8,128)S(1)} %get-tuple-element.77), channel_id=1, source_target_pairs={{1,0},{2,1},{3,2},{5,4},{6,5},{7,6},{9,8},{10,9},{11,10},{13,12},{... | collective-permute-start | bytes 98312 | tf_op jit(solution)/shard_map/ppermute | solution.py:113
  90.2 1.6 collective-permute-done.21
  91.8 4.9 %collective-permute-start.16 = (f32[1,8,8,128]{3,2,1,0:T(8,128)S(1)}, f32[1,8,8,128]{3,2,1,0:T(8,128)S(1)}, u32[]{:S(2)}, u32[]{:S(2)}) collective-permute-start(f32[1,8,8,128]{3,2,1,0:T(8,128)S(1)} %get-tuple-element.80), channel_id=1, source_target_pairs={{0,4},{4,8},{8,12},{12,16},{16,20},{20,24},{24,28},{1,5},{5,9},{9,... | collective-permute-start | bytes 98312 | tf_op jit(solution)/shard_map/ppermute | solution.py:113
  98.3 4.3 %collective-permute-done.17 = f32[1,8,8,128]{3,2,1,0:T(8,128)S(1)} collective-permute-done((f32[1,8,8,128]{3,2,1,0:T(8,128)S(1)}, f32[1,8,8,128]{3,2,1,0:T(8,128)S(1)}, u32[]{:S(2)}, u32[]{:S(2)}) %collective-permute-start.17) | collective-permute-done | bytes 32800 | tf_op jit(solution)/shard_map/ppermute | solution.py:113
  104.5 1.9 collective-permute-start.26
  110.4 7.4 %collective-permute-start.30 = (f32[1,8,128]{2,1,0:T(8,128)S(1)}, f32[1,8,128]{2,1,0:T(8,128)S(1)}, u32[]{:S(2)}, u32[]{:S(2)}) collective-permute-start(f32[1,8,128]{2,1,0:T(8,128)S(1)} %get-tuple-element.61), channel_id=1, source_target_pairs={{1,4},{2,5},{3,6},{5,8},{6,9},{7,10},{9,12},{10,13},{11,14},{13,16... | collective-permute-start | bytes 12296 | tf_op jit(solution)/shard_map/ppermute | solution.py:113
  117.9 2.3 %collective-permute-start.29 = (f32[1,8,8,128]{3,2,1,0:T(8,128)S(1)}, f32[1,8,8,128]{3,2,1,0:T(8,128)S(1)}, u32[]{:S(2)}, u32[]{:S(2)}) collective-permute-start(f32[1,8,8,128]{3,2,1,0:T(8,128)S(1)} %get-tuple-element.63), channel_id=1, source_target_pairs={{1,0},{2,1},{3,2},{5,4},{6,5},{7,6},{9,8},{10,9},{11,10},{13,12},{... | collective-permute-start | bytes 98312 | tf_op jit(solution)/shard_map/ppermute | solution.py:113
  120.1 1.6 collective-permute-done.29
  121.7 4.9 %collective-permute-start.24 = (f32[1,8,8,128]{3,2,1,0:T(8,128)S(1)}, f32[1,8,8,128]{3,2,1,0:T(8,128)S(1)}, u32[]{:S(2)}, u32[]{:S(2)}) collective-permute-start(f32[1,8,8,128]{3,2,1,0:T(8,128)S(1)} %get-tuple-element.66), channel_id=1, source_target_pairs={{0,4},{4,8},{8,12},{12,16},{16,20},{20,24},{24,28},{1,5},{5,9},{9,... | collective-permute-start | bytes 98312 | tf_op jit(solution)/shard_map/ppermute | solution.py:113
  128.2 4.3 %collective-permute-done.25 = f32[1,8,8,128]{3,2,1,0:T(8,128)S(1)} collective-permute-done((f32[1,8,8,128]{3,2,1,0:T(8,128)S(1)}, f32[1,8,8,128]{3,2,1,0:T(8,128)S(1)}, u32[]{:S(2)}, u32[]{:S(2)}) %collective-permute-start.25) | collective-permute-done | bytes 32800 | tf_op jit(solution)/shard_map/ppermute | solution.py:113
  135.5 2.0 collective-permute-start.35
  138.8 1.5 collective-permute-start.39
  140.3 6.7 %collective-permute-start.38 = (f32[1,8,128]{2,1,0:T(8,128)S(1)}, f32[1,8,128]{2,1,0:T(8,128)S(1)}, u32[]{:S(2)}, u32[]{:S(2)}) collective-permute-start(f32[1,8,128]{2,1,0:T(8,128)S(1)} %get-tuple-element.47), channel_id=1, source_target_pairs={{1,4},{2,5},{3,6},{5,8},{6,9},{7,10},{9,12},{10,13},{11,14},{13,16... | collective-permute-start | bytes 12296 | tf_op jit(solution)/shard_map/ppermute | solution.py:113
  147.0 2.6 %collective-permute-start.34 = (f32[1,8,8,128]{3,2,1,0:T(8,128)S(1)}, f32[1,8,8,128]{3,2,1,0:T(8,128)S(1)}, u32[]{:S(2)}, u32[]{:S(2)}) collective-permute-start(f32[1,8,8,128]{3,2,1,0:T(8,128)S(1)} %get-tuple-element.48), channel_id=1, source_target_pairs={{0,1},{1,2},{2,3},{4,5},{5,6},{6,7},{8,9},{9,10},{10,11},{12,13},{... | collective-permute-start | bytes 98312 | tf_op jit(solution)/shard_map/ppermute | solution.py:113
  149.6 2.0 fusion.9
  153.0 1.4 fusion.10
  154.4 1.4 fusion.11
  157.2 1.4 fusion.13
  158.6 1.4 fusion.14
  160.0 1.4 fusion.15
  161.4 6.4 %fusion.8 = f32[256,1536]{0,1:T(8,128)S(1)} fusion(bf16[4096,1536]{1,0:T(8,128)(2,1)S(1)} %fusion.15, s32[4096]{0:T(1024)S(1)} %get-tuple-element.98), kind=kOutput, calls=%fused_computation.15 | convolution fusion | flops 3222274048 | bytes 14172160 | tf_op jit(solution)/shard_map/dot_general | solution.py:185
  169.6 6.3 %all-to-all-start = ((f32[32,2,2048]{2,1,0:T(2,128)}), f32[32,2,2048]{2,1,0:T(2,128)S(1)}, u32[]{:S(2)}, u32[]{:S(2)}) async-start(f32[32,2,2048]{2,1,0:T(2,128)} %bitcast.198), calls=%async_computation | async-start | bytes 1048576 | tf_op jit(solution)/shard_map/all_to_all | solution.py:202
  175.9 2.0 collective-permute-start.37
  177.9 1.6 collective-permute-done.37
  179.5 3.6 %collective-permute-start.32 = (f32[1,8,8,128]{3,2,1,0:T(8,128)S(1)}, f32[1,8,8,128]{3,2,1,0:T(8,128)S(1)}, u32[]{:S(2)}, u32[]{:S(2)}) collective-permute-start(f32[1,8,8,128]{3,2,1,0:T(8,128)S(1)} %get-tuple-element.52), channel_id=1, source_target_pairs={{0,4},{4,8},{8,12},{12,16},{16,20},{20,24},{24,28},{1,5},{5,9},{9,... | collective-permute-start | bytes 98312 | tf_op jit(solution)/shard_map/ppermute | solution.py:113
  184.7 4.3 %collective-permute-done.33 = f32[1,8,8,128]{3,2,1,0:T(8,128)S(1)} collective-permute-done((f32[1,8,8,128]{3,2,1,0:T(8,128)S(1)}, f32[1,8,8,128]{3,2,1,0:T(8,128)S(1)}, u32[]{:S(2)}, u32[]{:S(2)}) %collective-permute-start.33) | collective-permute-done | bytes 32800 | tf_op jit(solution)/shard_map/ppermute | solution.py:113
  189.5 1.5 all-to-all-done
  191.8 5.2 %all-to-all-start.1 = ((f32[8,2,2048]{2,1,0:T(2,128)}), f32[8,2,2048]{2,1,0:T(2,128)S(1)}, u32[]{:S(2)}, u32[]{:S(2)}) async-start(f32[8,2,2048]{2,1,0:T(2,128)} %broadcast_in_dim.86), calls=%async_computation.1 | async-start | bytes 262144 | tf_op jit(solution)/shard_map/all_to_all | solution.py:204
  197.9 6.4 %all-to-all-done.1 = f32[8,2,2048]{2,1,0:T(2,128)S(1)} async-done(((f32[8,2,2048]{2,1,0:T(2,128)}), f32[8,2,2048]{2,1,0:T(2,128)S(1)}, u32[]{:S(2)}, u32[]{:S(2)}) %all-to-all-start.1) | async-done | bytes 131104 | tf_op jit(solution)/shard_map/all_to_all | solution.py:204
  (202 shorter events, 45.1 us)
Async XLA Ops:
  6.8 26.5 %collective-permute-start.3 = (f32[2,8,128]{2,0,1:T(2,128)S(1)}, f32[2,8,128]{2,0,1:T(2,128)S(1)}, u32[]{:S(2)}, u32[]{:S(2)}) collective-permute-start(f32[2,8,128]{2,0,1:T(2,128)S(1)} %get-tuple-element.27), channel_id=1, source_target_pairs={{0,5},{1,6},{2,7},{4,9},{5,10},{6,11},{8,13},{9,14},{10,15},{12,17... | collective-permute-start | bytes 24584 | tf_op jit(solution)/shard_map/ppermute | solution.py:113
  9.7 25.8 %collective-permute-start.6 = (f32[2,8,128]{2,0,1:T(2,128)S(1)}, f32[2,8,128]{2,0,1:T(2,128)S(1)}, u32[]{:S(2)}, u32[]{:S(2)}) collective-permute-start(f32[2,8,128]{2,0,1:T(2,128)S(1)} %get-tuple-element.28), channel_id=1, source_target_pairs={{1,4},{2,5},{3,6},{5,8},{6,9},{7,10},{9,12},{10,13},{11,14},{13,16... | collective-permute-start | bytes 24584 | tf_op jit(solution)/shard_map/ppermute | solution.py:113
  14.3 19.1 %collective-permute-start.4 = (f32[2,8,128]{2,0,1:T(2,128)S(1)}, f32[2,8,128]{2,0,1:T(2,128)S(1)}, u32[]{:S(2)}, u32[]{:S(2)}) collective-permute-start(f32[2,8,128]{2,0,1:T(2,128)S(1)} %get-tuple-element.29), channel_id=1, source_target_pairs={{4,1},{5,2},{6,3},{8,5},{9,6},{10,7},{12,9},{13,10},{14,11},{16,13... | collective-permute-start | bytes 24584 | tf_op jit(solution)/shard_map/ppermute | solution.py:113
  15.6 7.6 %collective-permute-start = (f32[2,8,8,128]{3,0,2,1:T(2,128)S(1)}, f32[2,8,8,128]{3,0,2,1:T(2,128)S(1)}, u32[]{:S(2)}, u32[]{:S(2)}) collective-permute-start(f32[2,8,8,128]{3,0,2,1:T(2,128)S(1)} %get-tuple-element.35), channel_id=1, source_target_pairs={{0,4},{4,8},{8,12},{12,16},{16,20},{20,24},{24,28},{1,5},{5,9},{9,... | collective-permute-start | bytes 196616 | tf_op jit(solution)/shard_map/ppermute | solution.py:113
  19.7 6.2 %collective-permute-start.1 = (f32[2,8,8,128]{3,0,2,1:T(2,128)S(1)}, f32[2,8,8,128]{3,0,2,1:T(2,128)S(1)}, u32[]{:S(2)}, u32[]{:S(2)}) collective-permute-start(f32[2,8,8,128]{3,0,2,1:T(2,128)S(1)} %get-tuple-element.36), channel_id=1, source_target_pairs={{4,0},{8,4},{12,8},{16,12},{20,16},{24,20},{28,24},{5,1},{9,5},{13... | collective-permute-start | bytes 196616 | tf_op jit(solution)/shard_map/ppermute | solution.py:113
  23.3 12.2 %collective-permute-start.7 = (f32[2,8,128]{2,0,1:T(2,128)S(1)}, f32[2,8,128]{2,0,1:T(2,128)S(1)}, u32[]{:S(2)}, u32[]{:S(2)}) collective-permute-start(f32[2,8,128]{2,0,1:T(2,128)S(1)} %get-tuple-element.30), channel_id=1, source_target_pairs={{5,0},{6,1},{7,2},{9,4},{10,5},{11,6},{13,8},{14,9},{15,10},{17,12... | collective-permute-start | bytes 24584 | tf_op jit(solution)/shard_map/ppermute | solution.py:113
  25.8 5.6 %collective-permute-start.2 = (f32[2,8,8,128]{3,0,2,1:T(2,128)S(1)}, f32[2,8,8,128]{3,0,2,1:T(2,128)S(1)}, u32[]{:S(2)}, u32[]{:S(2)}) collective-permute-start(f32[2,8,8,128]{3,0,2,1:T(2,128)S(1)} %get-tuple-element.31), channel_id=1, source_target_pairs={{0,1},{1,2},{2,3},{4,5},{5,6},{6,7},{8,9},{9,10},{10,11},{12,13},{... | collective-permute-start | bytes 196616 | tf_op jit(solution)/shard_map/ppermute | solution.py:113
  27.8 8.4 %copy-start.2 = (f32[8]{0:T(128)S(1)}, f32[8]{0:T(128)}, u32[]{:S(2)}) copy-start(f32[8]{0:T(128)} %constant.81.clone) | copy-start | bytes 100
  31.4 3.8 %collective-permute-start.5 = (f32[2,8,8,128]{3,0,2,1:T(2,128)S(1)}, f32[2,8,8,128]{3,0,2,1:T(2,128)S(1)}, u32[]{:S(2)}, u32[]{:S(2)}) collective-permute-start(f32[2,8,8,128]{3,0,2,1:T(2,128)S(1)} %get-tuple-element.32), channel_id=1, source_target_pairs={{1,0},{2,1},{3,2},{5,4},{6,5},{7,6},{9,8},{10,9},{11,10},{13,12},{... | collective-permute-start | bytes 196616 | tf_op jit(solution)/shard_map/ppermute | solution.py:113
  33.4 3.0 %copy-start.1 = (f32[8,8,1,1]{1,0,2,3:T(8,128)S(1)}, f32[8,8,1,1]{1,0,2,3:T(8,128)}, u32[]{:S(2)}) copy-start(f32[8,8,1,1]{1,0,2,3:T(8,128)} %constant.123) | copy-start | bytes 772
  35.2 1.5 copy-start
  37.9 17.6 %collective-permute-start.8 = (f32[1,8,8,128]{3,2,1,0:T(8,128)S(1)}, f32[1,8,8,128]{3,2,1,0:T(8,128)S(1)}, u32[]{:S(2)}, u32[]{:S(2)}) collective-permute-start(f32[1,8,8,128]{3,2,1,0:T(8,128)S(1)} %bitcast.717), channel_id=1, source_target_pairs={{0,4},{4,8},{8,12},{12,16},{16,20},{20,24},{24,28},{1,5},{5,9},{9,... | collective-permute-start | bytes 98312 | tf_op jit(solution)/shard_map/ppermute | solution.py:113
  42.2 29.4 %collective-permute-start.12 = (f32[1,8,128]{2,1,0:T(8,128)S(1)}, f32[1,8,128]{2,1,0:T(8,128)S(1)}, u32[]{:S(2)}, u32[]{:S(2)}) collective-permute-start(f32[1,8,128]{2,1,0:T(8,128)S(1)} %bitcast.731), channel_id=1, source_target_pairs={{4,1},{5,2},{6,3},{8,5},{9,6},{10,7},{12,9},{13,10},{14,11},{16,13... | collective-permute-start | bytes 12296 | tf_op jit(solution)/shard_map/ppermute | solution.py:113
  43.5 28.1 %collective-permute-start.11 = (f32[1,8,128]{2,1,0:T(8,128)S(1)}, f32[1,8,128]{2,1,0:T(8,128)S(1)}, u32[]{:S(2)}, u32[]{:S(2)}) collective-permute-start(f32[1,8,128]{2,1,0:T(8,128)S(1)} %bitcast.730), channel_id=1, source_target_pairs={{0,5},{1,6},{2,7},{4,9},{5,10},{6,11},{8,13},{9,14},{10,15},{12,17... | collective-permute-start | bytes 12296 | tf_op jit(solution)/shard_map/ppermute | solution.py:113
  48.0 23.5 %collective-permute-start.14 = (f32[1,8,128]{2,1,0:T(8,128)S(1)}, f32[1,8,128]{2,1,0:T(8,128)S(1)}, u32[]{:S(2)}, u32[]{:S(2)}) collective-permute-start(f32[1,8,128]{2,1,0:T(8,128)S(1)} %bitcast.733), channel_id=1, source_target_pairs={{1,4},{2,5},{3,6},{5,8},{6,9},{7,10},{9,12},{10,13},{11,14},{13,16... | collective-permute-start | bytes 12296 | tf_op jit(solution)/shard_map/ppermute | solution.py:113
  54.1 17.5 %collective-permute-start.15 = (f32[1,8,128]{2,1,0:T(8,128)S(1)}, f32[1,8,128]{2,1,0:T(8,128)S(1)}, u32[]{:S(2)}, u32[]{:S(2)}) collective-permute-start(f32[1,8,128]{2,1,0:T(8,128)S(1)} %bitcast.732), channel_id=1, source_target_pairs={{5,0},{6,1},{7,2},{9,4},{10,5},{11,6},{13,8},{14,9},{15,10},{17,12... | collective-permute-start | bytes 12296 | tf_op jit(solution)/shard_map/ppermute | solution.py:113
  55.5 7.3 %collective-permute-start.9 = (f32[1,8,8,128]{3,2,1,0:T(8,128)S(1)}, f32[1,8,8,128]{3,2,1,0:T(8,128)S(1)}, u32[]{:S(2)}, u32[]{:S(2)}) collective-permute-start(f32[1,8,8,128]{3,2,1,0:T(8,128)S(1)} %bitcast.719), channel_id=1, source_target_pairs={{4,0},{8,4},{12,8},{16,12},{20,16},{24,20},{28,24},{5,1},{9,5},{13... | collective-permute-start | bytes 98312 | tf_op jit(solution)/shard_map/ppermute | solution.py:113
  62.8 3.5 %collective-permute-start.13 = (f32[1,8,8,128]{3,2,1,0:T(8,128)S(1)}, f32[1,8,8,128]{3,2,1,0:T(8,128)S(1)}, u32[]{:S(2)}, u32[]{:S(2)}) collective-permute-start(f32[1,8,8,128]{3,2,1,0:T(8,128)S(1)} %bitcast.724), channel_id=1, source_target_pairs={{1,0},{2,1},{3,2},{5,4},{6,5},{7,6},{9,8},{10,9},{11,10},{13,12},{... | collective-permute-start | bytes 98312 | tf_op jit(solution)/shard_map/ppermute | solution.py:113
  66.3 5.2 %collective-permute-start.10 = (f32[1,8,8,128]{3,2,1,0:T(8,128)S(1)}, f32[1,8,8,128]{3,2,1,0:T(8,128)S(1)}, u32[]{:S(2)}, u32[]{:S(2)}) collective-permute-start(f32[1,8,8,128]{3,2,1,0:T(8,128)S(1)} %bitcast.723), channel_id=1, source_target_pairs={{0,1},{1,2},{2,3},{4,5},{5,6},{6,7},{8,9},{9,10},{10,11},{12,13},{... | collective-permute-start | bytes 98312 | tf_op jit(solution)/shard_map/ppermute | solution.py:113
  73.5 14.2 %collective-permute-start.18 = (f32[1,8,8,128]{3,2,1,0:T(8,128)S(1)}, f32[1,8,8,128]{3,2,1,0:T(8,128)S(1)}, u32[]{:S(2)}, u32[]{:S(2)}) collective-permute-start(f32[1,8,8,128]{3,2,1,0:T(8,128)S(1)} %get-tuple-element.76), channel_id=1, source_target_pairs={{0,1},{1,2},{2,3},{4,5},{5,6},{6,7},{8,9},{9,10},{10,11},{12,13},{... | collective-permute-start | bytes 98312 | tf_op jit(solution)/shard_map/ppermute | solution.py:113
  75.4 21.3 %collective-permute-start.19 = (f32[1,8,128]{2,1,0:T(8,128)S(1)}, f32[1,8,128]{2,1,0:T(8,128)S(1)}, u32[]{:S(2)}, u32[]{:S(2)}) collective-permute-start(f32[1,8,128]{2,1,0:T(8,128)S(1)} %get-tuple-element.72), channel_id=1, source_target_pairs={{0,5},{1,6},{2,7},{4,9},{5,10},{6,11},{8,13},{9,14},{10,15},{12,17... | collective-permute-start | bytes 12296 | tf_op jit(solution)/shard_map/ppermute | solution.py:113
  77.1 20.9 %collective-permute-start.20 = (f32[1,8,128]{2,1,0:T(8,128)S(1)}, f32[1,8,128]{2,1,0:T(8,128)S(1)}, u32[]{:S(2)}, u32[]{:S(2)}) collective-permute-start(f32[1,8,128]{2,1,0:T(8,128)S(1)} %get-tuple-element.73), channel_id=1, source_target_pairs={{4,1},{5,2},{6,3},{8,5},{9,6},{10,7},{12,9},{13,10},{14,11},{16,13... | collective-permute-start | bytes 12296 | tf_op jit(solution)/shard_map/ppermute | solution.py:113
  78.4 24.2 %collective-permute-start.23 = (f32[1,8,128]{2,1,0:T(8,128)S(1)}, f32[1,8,128]{2,1,0:T(8,128)S(1)}, u32[]{:S(2)}, u32[]{:S(2)}) collective-permute-start(f32[1,8,128]{2,1,0:T(8,128)S(1)} %get-tuple-element.74), channel_id=1, source_target_pairs={{5,0},{6,1},{7,2},{9,4},{10,5},{11,6},{13,8},{14,9},{15,10},{17,12... | collective-permute-start | bytes 12296 | tf_op jit(solution)/shard_map/ppermute | solution.py:113
  79.7 22.9 %collective-permute-start.22 = (f32[1,8,128]{2,1,0:T(8,128)S(1)}, f32[1,8,128]{2,1,0:T(8,128)S(1)}, u32[]{:S(2)}, u32[]{:S(2)}) collective-permute-start(f32[1,8,128]{2,1,0:T(8,128)S(1)} %get-tuple-element.75), channel_id=1, source_target_pairs={{1,4},{2,5},{3,6},{5,8},{6,9},{7,10},{9,12},{10,13},{11,14},{13,16... | collective-permute-start | bytes 12296 | tf_op jit(solution)/shard_map/ppermute | solution.py:113
  87.7 4.1 %collective-permute-start.21 = (f32[1,8,8,128]{3,2,1,0:T(8,128)S(1)}, f32[1,8,8,128]{3,2,1,0:T(8,128)S(1)}, u32[]{:S(2)}, u32[]{:S(2)}) collective-permute-start(f32[1,8,8,128]{3,2,1,0:T(8,128)S(1)} %get-tuple-element.77), channel_id=1, source_target_pairs={{1,0},{2,1},{3,2},{5,4},{6,5},{7,6},{9,8},{10,9},{11,10},{13,12},{... | collective-permute-start | bytes 98312 | tf_op jit(solution)/shard_map/ppermute | solution.py:113
  91.8 6.5 %collective-permute-start.16 = (f32[1,8,8,128]{3,2,1,0:T(8,128)S(1)}, f32[1,8,8,128]{3,2,1,0:T(8,128)S(1)}, u32[]{:S(2)}, u32[]{:S(2)}) collective-permute-start(f32[1,8,8,128]{3,2,1,0:T(8,128)S(1)} %get-tuple-element.80), channel_id=1, source_target_pairs={{0,4},{4,8},{8,12},{12,16},{16,20},{20,24},{24,28},{1,5},{5,9},{9,... | collective-permute-start | bytes 98312 | tf_op jit(solution)/shard_map/ppermute | solution.py:113
  96.7 5.8 %collective-permute-start.17 = (f32[1,8,8,128]{3,2,1,0:T(8,128)S(1)}, f32[1,8,8,128]{3,2,1,0:T(8,128)S(1)}, u32[]{:S(2)}, u32[]{:S(2)}) collective-permute-start(f32[1,8,8,128]{3,2,1,0:T(8,128)S(1)} %get-tuple-element.81), channel_id=1, source_target_pairs={{4,0},{8,4},{12,8},{16,12},{20,16},{24,20},{28,24},{5,1},{9,5},{13... | collective-permute-start | bytes 98312 | tf_op jit(solution)/shard_map/ppermute | solution.py:113
  104.5 13.3 %collective-permute-start.26 = (f32[1,8,8,128]{3,2,1,0:T(8,128)S(1)}, f32[1,8,8,128]{3,2,1,0:T(8,128)S(1)}, u32[]{:S(2)}, u32[]{:S(2)}) collective-permute-start(f32[1,8,8,128]{3,2,1,0:T(8,128)S(1)} %get-tuple-element.62), channel_id=1, source_target_pairs={{0,1},{1,2},{2,3},{4,5},{5,6},{6,7},{8,9},{9,10},{10,11},{12,13},{... | collective-permute-start | bytes 98312 | tf_op jit(solution)/shard_map/ppermute | solution.py:113
  106.5 20.1 %collective-permute-start.27 = (f32[1,8,128]{2,1,0:T(8,128)S(1)}, f32[1,8,128]{2,1,0:T(8,128)S(1)}, u32[]{:S(2)}, u32[]{:S(2)}) collective-permute-start(f32[1,8,128]{2,1,0:T(8,128)S(1)} %get-tuple-element.58), channel_id=1, source_target_pairs={{0,5},{1,6},{2,7},{4,9},{5,10},{6,11},{8,13},{9,14},{10,15},{12,17... | collective-permute-start | bytes 12296 | tf_op jit(solution)/shard_map/ppermute | solution.py:113
  107.8 20.1 %collective-permute-start.28 = (f32[1,8,128]{2,1,0:T(8,128)S(1)}, f32[1,8,128]{2,1,0:T(8,128)S(1)}, u32[]{:S(2)}, u32[]{:S(2)}) collective-permute-start(f32[1,8,128]{2,1,0:T(8,128)S(1)} %get-tuple-element.59), channel_id=1, source_target_pairs={{4,1},{5,2},{6,3},{8,5},{9,6},{10,7},{12,9},{13,10},{14,11},{16,13... | collective-permute-start | bytes 12296 | tf_op jit(solution)/shard_map/ppermute | solution.py:113
  109.1 23.4 %collective-permute-start.31 = (f32[1,8,128]{2,1,0:T(8,128)S(1)}, f32[1,8,128]{2,1,0:T(8,128)S(1)}, u32[]{:S(2)}, u32[]{:S(2)}) collective-permute-start(f32[1,8,128]{2,1,0:T(8,128)S(1)} %get-tuple-element.60), channel_id=1, source_target_pairs={{5,0},{6,1},{7,2},{9,4},{10,5},{11,6},{13,8},{14,9},{15,10},{17,12... | collective-permute-start | bytes 12296 | tf_op jit(solution)/shard_map/ppermute | solution.py:113
  110.4 22.1 %collective-permute-start.30 = (f32[1,8,128]{2,1,0:T(8,128)S(1)}, f32[1,8,128]{2,1,0:T(8,128)S(1)}, u32[]{:S(2)}, u32[]{:S(2)}) collective-permute-start(f32[1,8,128]{2,1,0:T(8,128)S(1)} %get-tuple-element.61), channel_id=1, source_target_pairs={{1,4},{2,5},{3,6},{5,8},{6,9},{7,10},{9,12},{10,13},{11,14},{13,16... | collective-permute-start | bytes 12296 | tf_op jit(solution)/shard_map/ppermute | solution.py:113
  117.9 3.9 %collective-permute-start.29 = (f32[1,8,8,128]{3,2,1,0:T(8,128)S(1)}, f32[1,8,8,128]{3,2,1,0:T(8,128)S(1)}, u32[]{:S(2)}, u32[]{:S(2)}) collective-permute-start(f32[1,8,8,128]{3,2,1,0:T(8,128)S(1)} %get-tuple-element.63), channel_id=1, source_target_pairs={{1,0},{2,1},{3,2},{5,4},{6,5},{7,6},{9,8},{10,9},{11,10},{13,12},{... | collective-permute-start | bytes 98312 | tf_op jit(solution)/shard_map/ppermute | solution.py:113
  121.7 6.5 %collective-permute-start.24 = (f32[1,8,8,128]{3,2,1,0:T(8,128)S(1)}, f32[1,8,8,128]{3,2,1,0:T(8,128)S(1)}, u32[]{:S(2)}, u32[]{:S(2)}) collective-permute-start(f32[1,8,8,128]{3,2,1,0:T(8,128)S(1)} %get-tuple-element.66), channel_id=1, source_target_pairs={{0,4},{4,8},{8,12},{12,16},{16,20},{20,24},{24,28},{1,5},{5,9},{9,... | collective-permute-start | bytes 98312 | tf_op jit(solution)/shard_map/ppermute | solution.py:113
  126.6 5.8 %collective-permute-start.25 = (f32[1,8,8,128]{3,2,1,0:T(8,128)S(1)}, f32[1,8,8,128]{3,2,1,0:T(8,128)S(1)}, u32[]{:S(2)}, u32[]{:S(2)}) collective-permute-start(f32[1,8,8,128]{3,2,1,0:T(8,128)S(1)} %get-tuple-element.67), channel_id=1, source_target_pairs={{4,0},{8,4},{12,8},{16,12},{20,16},{24,20},{28,24},{5,1},{9,5},{13... | collective-permute-start | bytes 98312 | tf_op jit(solution)/shard_map/ppermute | solution.py:113
  135.5 47.7 %collective-permute-start.35 = (f32[1,8,128]{2,1,0:T(8,128)S(1)}, f32[1,8,128]{2,1,0:T(8,128)S(1)}, u32[]{:S(2)}, u32[]{:S(2)}) collective-permute-start(f32[1,8,128]{2,1,0:T(8,128)S(1)} %get-tuple-element.44), channel_id=1, source_target_pairs={{0,5},{1,6},{2,7},{4,9},{5,10},{6,11},{8,13},{9,14},{10,15},{12,17... | collective-permute-start | bytes 12296 | tf_op jit(solution)/shard_map/ppermute | solution.py:113
  137.5 47.0 %collective-permute-start.36 = (f32[1,8,128]{2,1,0:T(8,128)S(1)}, f32[1,8,128]{2,1,0:T(8,128)S(1)}, u32[]{:S(2)}, u32[]{:S(2)}) collective-permute-start(f32[1,8,128]{2,1,0:T(8,128)S(1)} %get-tuple-element.45), channel_id=1, source_target_pairs={{4,1},{5,2},{6,3},{8,5},{9,6},{10,7},{12,9},{13,10},{14,11},{16,13... | collective-permute-start | bytes 12296 | tf_op jit(solution)/shard_map/ppermute | solution.py:113
  138.8 45.7 %collective-permute-start.39 = (f32[1,8,128]{2,1,0:T(8,128)S(1)}, f32[1,8,128]{2,1,0:T(8,128)S(1)}, u32[]{:S(2)}, u32[]{:S(2)}) collective-permute-start(f32[1,8,128]{2,1,0:T(8,128)S(1)} %get-tuple-element.46), channel_id=1, source_target_pairs={{5,0},{6,1},{7,2},{9,4},{10,5},{11,6},{13,8},{14,9},{15,10},{17,12... | collective-permute-start | bytes 12296 | tf_op jit(solution)/shard_map/ppermute | solution.py:113
  140.3 44.2 %collective-permute-start.38 = (f32[1,8,128]{2,1,0:T(8,128)S(1)}, f32[1,8,128]{2,1,0:T(8,128)S(1)}, u32[]{:S(2)}, u32[]{:S(2)}) collective-permute-start(f32[1,8,128]{2,1,0:T(8,128)S(1)} %get-tuple-element.47), channel_id=1, source_target_pairs={{1,4},{2,5},{3,6},{5,8},{6,9},{7,10},{9,12},{10,13},{11,14},{13,16... | collective-permute-start | bytes 12296 | tf_op jit(solution)/shard_map/ppermute | solution.py:113
  147.0 28.9 %collective-permute-start.34 = (f32[1,8,8,128]{3,2,1,0:T(8,128)S(1)}, f32[1,8,8,128]{3,2,1,0:T(8,128)S(1)}, u32[]{:S(2)}, u32[]{:S(2)}) collective-permute-start(f32[1,8,8,128]{3,2,1,0:T(8,128)S(1)} %get-tuple-element.48), channel_id=1, source_target_pairs={{0,1},{1,2},{2,3},{4,5},{5,6},{6,7},{8,9},{9,10},{10,11},{12,13},{... | collective-permute-start | bytes 98312 | tf_op jit(solution)/shard_map/ppermute | solution.py:113
  151.6 1.4 copy-start.3
  169.6 21.3 %all-to-all-start = ((f32[32,2,2048]{2,1,0:T(2,128)}), f32[32,2,2048]{2,1,0:T(2,128)S(1)}, u32[]{:S(2)}, u32[]{:S(2)}) async-start(f32[32,2,2048]{2,1,0:T(2,128)} %bitcast.198), calls=%async_computation | async-start | bytes 1048576 | tf_op jit(solution)/shard_map/all_to_all | solution.py:202
  175.9 3.6 %collective-permute-start.37 = (f32[1,8,8,128]{3,2,1,0:T(8,128)S(1)}, f32[1,8,8,128]{3,2,1,0:T(8,128)S(1)}, u32[]{:S(2)}, u32[]{:S(2)}) collective-permute-start(f32[1,8,8,128]{3,2,1,0:T(8,128)S(1)} %get-tuple-element.49), channel_id=1, source_target_pairs={{1,0},{2,1},{3,2},{5,4},{6,5},{7,6},{9,8},{10,9},{11,10},{13,12},{... | collective-permute-start | bytes 98312 | tf_op jit(solution)/shard_map/ppermute | solution.py:113
  179.5 5.2 %collective-permute-start.32 = (f32[1,8,8,128]{3,2,1,0:T(8,128)S(1)}, f32[1,8,8,128]{3,2,1,0:T(8,128)S(1)}, u32[]{:S(2)}, u32[]{:S(2)}) collective-permute-start(f32[1,8,8,128]{3,2,1,0:T(8,128)S(1)} %get-tuple-element.52), channel_id=1, source_target_pairs={{0,4},{4,8},{8,12},{12,16},{16,20},{20,24},{24,28},{1,5},{5,9},{9,... | collective-permute-start | bytes 98312 | tf_op jit(solution)/shard_map/ppermute | solution.py:113
  183.2 5.9 %collective-permute-start.33 = (f32[1,8,8,128]{3,2,1,0:T(8,128)S(1)}, f32[1,8,8,128]{3,2,1,0:T(8,128)S(1)}, u32[]{:S(2)}, u32[]{:S(2)}) collective-permute-start(f32[1,8,8,128]{3,2,1,0:T(8,128)S(1)} %get-tuple-element.53), channel_id=1, source_target_pairs={{4,0},{8,4},{12,8},{16,12},{20,16},{24,20},{28,24},{5,1},{9,5},{13... | collective-permute-start | bytes 98312 | tf_op jit(solution)/shard_map/ppermute | solution.py:113
  191.8 12.6 %all-to-all-start.1 = ((f32[8,2,2048]{2,1,0:T(2,128)}), f32[8,2,2048]{2,1,0:T(2,128)S(1)}, u32[]{:S(2)}, u32[]{:S(2)}) async-start(f32[8,2,2048]{2,1,0:T(2,128)} %broadcast_in_dim.86), calls=%async_computation.1 | async-start | bytes 262144 | tf_op jit(solution)/shard_map/all_to_all | solution.py:204

commit v3 on v1

--- a/solution.py
+++ b/solution.py
@@ -151,19 +151,15 @@
     return jnp.sum(jnp.where(hit_lane, picked, 0.0), axis=1)
 
 
-def segment_pair(first, second, ids, bins, lanes):
+def segment_sum(values, ids, bins, lanes):
     rows = bins // lanes
     hit_lane = one_hot(ids % lanes, lanes)
-    spread_parts = [hit_lane * part[:, None] for part in split3(first) + split3(second)]
-    rhs = jnp.concatenate(spread_parts, axis=1)
+    rhs = jnp.concatenate([hit_lane * part[:, None] for part in split3(values)], axis=1)
     hit_row = one_hot(ids // lanes, rows)
     sums = lax.dot_general(
         hit_row, rhs, (((0,), (0,)), ((), ())), preferred_element_type=jnp.float32
     )
-    sums = sums.reshape(rows, 6, lanes)
-    numer = sums[:, 0] + sums[:, 1] + sums[:, 2]
-    denom = sums[:, 3] + sums[:, 4] + sums[:, 5]
-    return jnp.stack([numer.reshape(-1), denom.reshape(-1)])
+    return (sums[:, :lanes] + sums[:, lanes : 2 * lanes] + sums[:, 2 * lanes :]).reshape(-1)
 
 
 def strip_totals(partial, strips, strip_size):
@@ -193,22 +189,24 @@
     pressure = jnp.zeros_like(source)
     resid = rhs
     update = pinv * resid / theta
+    picks = fac_point[0]
+    areas = fac_area[0]
+    strips = lax.axis_size("ey")
+    global_ids = fac_strip[0, :, 0] * SHELL_STRIP + fac_shell[0]
+    denom = segment_sum(areas, global_ids, strips * SHELL_STRIP, 256)
     for step in range(SWEEPS):
+        if step + 1 == SWEEPS:
+            early = gather_flat(pressure.reshape(-1), picks, 256)
+            samples = early + gather_flat(update.reshape(-1), picks, 256)
         pressure = pressure + update
         resid = resid - assemble(element_apply(update, metric, weights, stiff)[None])[0]
         if step + 1 < SWEEPS:
             rho_new = 1.0 / (2.0 * sigma - rho_now)
             update = rho_new * rho_now * update + 2.0 * rho_new / delta * pinv * resid
             rho_now = rho_new
-    picks = fac_point[0]
-    samples = gather_flat(pressure.reshape(-1), picks, 256)
-    areas = fac_area[0]
     weighted = areas * samples
-    strip_of = fac_strip[0, :, 0]
-    shell_of = fac_shell[0]
-    strips = lax.axis_size("ey")
-    global_ids = strip_of * SHELL_STRIP + shell_of
-    partial = segment_pair(weighted, areas, global_ids, strips * SHELL_STRIP, 256)
+    numer = segment_sum(weighted, global_ids, strips * SHELL_STRIP, 256)
+    partial = jnp.stack([numer, denom])
     total = strip_totals(partial, strips, SHELL_STRIP)
     shell_load = total[0] / jnp.maximum(total[1], 1.0)
     return (pressure, resid, shell_load)

time: 156 us -> 159 us (1.019)
  matrix products: 14.5 us -> 18.9 us
  other arithmetic: 18.3 us -> 16.3 us
  local copies, waits for them, and re-layouts: 6.95 us -> 8.71 us
  waiting for transfers between devices: 57 us -> 55.3 us
    unnamed x5 -> x0, other arithmetic: 6.96 us -> none
    dot_general x1 -> x2, matrix products: 2.01 us -> 7.73 us  [gather_flat(): picked = jnp.dot(hit_row, parts, preferred_element_type=jnp.float32)]
    mul x1 -> x2, other arithmetic: 0.02 us -> 4.6 us  [the longest x1 4.58 us: segment_sum(): hit_lane * part[:, None]]
    unnamed x14 -> x16, local copies, waits for them, and re-layouts: 1.54 us -> 4.09 us
    dot_general x1 -> x2, matrix products: 6.44 us -> 5.17 us  [segment_sum(): lax.dot_general(hit_row, rhs, (((0,), (0,)), ((), ())), preferred_element...]
  transfers between devices with their start and end apart: 22 -> 22, of which waited for: 19 -> 18; matrix products, arithmetic and copies ran while one was open for 15% -> 16% of each run, Pallas kernels for 0% -> 0%
where the time goes in v3:
time: 159 us; the launch traced here: 156 us
  starting transfers between devices  55.4 us (35%)
  waiting for transfers between devices  55.3 us (35%)
  matrix products  18.9 us (12%)
  other arithmetic  16.3 us (10%)
  local copies, waits for them, and re-layouts  8.71 us (5%)
    ppermute x10, starting transfers between devices, padded_2(): lax.ppermute(lax.slice_in_dim(block, block.shape[dim] - width, None, axis...  30.1 us
    ppermute x10, waiting for transfers between devices, padded_2(): lax.ppermute(lax.slice_in_dim(block, 0, width, axis=dim), axis, backward)  21.9 us
    ppermute x10, starting transfers between devices, padded_2(): lax.ppermute(lax.slice_in_dim(block, 0, width, axis=dim), axis, backward)  16.3 us
    ppermute x10, waiting for transfers between devices, padded_2(): lax.ppermute(lax.slice_in_dim(block, block.shape[dim] - width, None, axis...  15.9 us
    all_to_all x1, waiting for transfers between devices, strip_totals(): mine = lax.all_to_all(chunks, ('ex', 'ey'), 0, 0, tiled=True).sum(0)  10.8 us
    dot_general x2, matrix products, gather_flat(): picked = jnp.dot(hit_row, parts, preferred_element_type=jnp.float32)  7.73 us
    all_to_all x1, waiting for transfers between devices, strip_totals(): whole = lax.all_to_all(spread_out, 'ex', 0, 0, tiled=True)  6.71 us
    all_to_all x1, starting transfers between devices, strip_totals(): mine = lax.all_to_all(chunks, ('ex', 'ey'), 0, 0, tiled=True).sum(0)  5.3 us
  transfers between devices with their start and end apart: 22, of which 18 were waited for; matrix products, arithmetic and copies ran while one was open for 16% of the time, Pallas kernels for 0%

profile of v3, /device:TPU:2, one launch (start us, length us, event | category | flops | bytes accessed | tf_op | source)
XLA Modules:
  0.0 156.2 jit_solution(10524264506517109983)
XLA Ops:
  1.4 1.3 gather_fusion
  4.2 1.1 fusion.91
  6.2 3.4 %collective-permute-start = (f32[2,1,1,8,8,128]{5,0,4,3,2,1:T(2,128)S(1)}, f32[2,1,1,8,8,128]{5,0,4,3,2,1:T(2,128)S(1)}, u32[]{:S(2)}, u32[]{:S(2)}) collective-permute-start(f32[2,1,1,8,8,128]{5,0,4,3,2,1:T(2,128)S(1)} %maximum_bitcast_fusion.4), channel_id=1, source_target_pairs={{0,4},{4,8},{8,12},{12,16},{16,20},{20,24},{24,28},{1,5},{5,9},{9,... | collective-permute-start | bytes 196616 | tf_op jit(solution)/shard_map/ppermute | solution.py:16
  9.6 1.9 %collective-permute-done = f32[2,1,1,8,8,128]{5,0,4,3,2,1:T(2,128)S(1)} collective-permute-done((f32[2,1,1,8,8,128]{5,0,4,3,2,1:T(2,128)S(1)}, f32[2,1,1,8,8,128]{5,0,4,3,2,1:T(2,128)S(1)}, u32[]{:S(2)}, u32[]{:S(2)}) %collective-permute-start) | collective-permute-done | bytes 65568 | tf_op jit(solution)/shard_map/ppermute | solution.py:16
  11.5 0.8 fusion.109
  12.4 1.3 collective-permute-start.1
  13.7 1.3 pad_maximum_fusion.6
  15.2 3.6 %collective-permute-done.1 = f32[2,1,1,8,8,128]{5,0,4,3,2,1:T(2,128)S(1)} collective-permute-done((f32[2,1,1,8,8,128]{5,0,4,3,2,1:T(2,128)S(1)}, f32[2,1,1,8,8,128]{5,0,4,3,2,1:T(2,128)S(1)}, u32[]{:S(2)}, u32[]{:S(2)}) %collective-permute-start.1) | collective-permute-done | bytes 65568 | tf_op jit(solution)/shard_map/ppermute | solution.py:19
  18.9 1.9 %collective-permute-start.2 = (f32[2,1,1,8,8,128]{5,3,0,4,2,1:T(8,128)S(1)}, f32[2,1,1,8,8,128]{5,3,0,4,2,1:T(8,128)S(1)}, u32[]{:S(2)}, u32[]{:S(2)}) collective-permute-start(f32[2,1,1,8,8,128]{5,3,0,4,2,1:T(8,128)S(1)} %maximum_bitcast_fusion.2), channel_id=1, source_target_pairs={{0,1},{1,2},{2,3},{4,5},{5,6},{6,7},{8,9},{9,10},{10,11},{12,13},{... | collective-permute-start | bytes 196616 | tf_op jit(solution)/shard_map/ppermute | solution.py:16
  20.9 3.6 %collective-permute-done.2 = f32[2,1,1,8,8,128]{5,3,0,4,2,1:T(8,128)S(1)} collective-permute-done((f32[2,1,1,8,8,128]{5,3,0,4,2,1:T(8,128)S(1)}, f32[2,1,1,8,8,128]{5,3,0,4,2,1:T(8,128)S(1)}, u32[]{:S(2)}, u32[]{:S(2)}) %collective-permute-start.2) | collective-permute-done | bytes 65568 | tf_op jit(solution)/shard_map/ppermute | solution.py:16
  24.6 1.9 %collective-permute-start.3 = (f32[2,1,1,8,8,128]{5,3,0,4,2,1:T(8,128)S(1)}, f32[2,1,1,8,8,128]{5,3,0,4,2,1:T(8,128)S(1)}, u32[]{:S(2)}, u32[]{:S(2)}) collective-permute-start(f32[2,1,1,8,8,128]{5,3,0,4,2,1:T(8,128)S(1)} %get-tuple-element.29), channel_id=1, source_target_pairs={{1,0},{2,1},{3,2},{5,4},{6,5},{7,6},{9,8},{10,9},{11,10},{13,12},{... | collective-permute-start | bytes 196616 | tf_op jit(solution)/shard_map/ppermute | solution.py:19
  26.6 1.7 %collective-permute-done.3 = f32[2,1,1,8,8,128]{5,3,0,4,2,1:T(8,128)S(1)} collective-permute-done((f32[2,1,1,8,8,128]{5,3,0,4,2,1:T(8,128)S(1)}, f32[2,1,1,8,8,128]{5,3,0,4,2,1:T(8,128)S(1)}, u32[]{:S(2)}, u32[]{:S(2)}) %collective-permute-start.3) | collective-permute-done | bytes 65568 | tf_op jit(solution)/shard_map/ppermute | solution.py:19
  30.3 4.8 %collective-permute-start.4 = (f32[1,1,1,8,8,128]{5,4,3,2,1,0:T(8,128)S(1)}, f32[1,1,1,8,8,128]{5,4,3,2,1,0:T(8,128)S(1)}, u32[]{:S(2)}, u32[]{:S(2)}) collective-permute-start(f32[1,1,1,8,8,128]{5,4,3,2,1,0:T(8,128)S(1)} %bitcast.484), channel_id=1, source_target_pairs={{0,4},{4,8},{8,12},{12,16},{16,20},{20,24},{24,28},{1,5},{5,9},{9,... | collective-permute-start | bytes 98312 | tf_op jit(solution)/shard_map/ppermute | solution.py:16
  35.2 1.3 collective-permute-start.5
  36.8 4.2 %collective-permute-done.5 = f32[1,1,1,8,8,128]{5,4,3,2,1,0:T(8,128)S(1)} collective-permute-done((f32[1,1,1,8,8,128]{5,4,3,2,1,0:T(8,128)S(1)}, f32[1,1,1,8,8,128]{5,4,3,2,1,0:T(8,128)S(1)}, u32[]{:S(2)}, u32[]{:S(2)}) %collective-permute-start.5) | collective-permute-done | bytes 32800 | tf_op jit(solution)/shard_map/ppermute | solution.py:19
  41.0 1.9 %collective-permute-start.6 = (f32[1,1,1,8,8,128]{5,3,4,2,1,0:T(8,128)S(1)}, f32[1,1,1,8,8,128]{5,3,4,2,1,0:T(8,128)S(1)}, u32[]{:S(2)}, u32[]{:S(2)}) collective-permute-start(f32[1,1,1,8,8,128]{5,3,4,2,1,0:T(8,128)S(1)} %maximum_bitcast_fusion.12), channel_id=1, source_target_pairs={{0,1},{1,2},{2,3},{4,5},{5,6},{6,7},{8,9},{9,10},{10,11},{12,13},{... | collective-permute-start | bytes 98312 | tf_op jit(solution)/shard_map/ppermute | solution.py:16
  42.9 3.3 %collective-permute-done.6 = f32[1,1,1,8,8,128]{5,3,4,2,1,0:T(8,128)S(1)} collective-permute-done((f32[1,1,1,8,8,128]{5,3,4,2,1,0:T(8,128)S(1)}, f32[1,1,1,8,8,128]{5,3,4,2,1,0:T(8,128)S(1)}, u32[]{:S(2)}, u32[]{:S(2)}) %collective-permute-start.6) | collective-permute-done | bytes 32800 | tf_op jit(solution)/shard_map/ppermute | solution.py:16
  46.3 1.9 %collective-permute-start.7 = (f32[1,1,1,8,8,128]{5,3,4,2,1,0:T(8,128)S(1)}, f32[1,1,1,8,8,128]{5,3,4,2,1,0:T(8,128)S(1)}, u32[]{:S(2)}, u32[]{:S(2)}) collective-permute-start(f32[1,1,1,8,8,128]{5,3,4,2,1,0:T(8,128)S(1)} %get-tuple-element.25), channel_id=1, source_target_pairs={{1,0},{2,1},{3,2},{5,4},{6,5},{7,6},{9,8},{10,9},{11,10},{13,12},{... | collective-permute-start | bytes 98312 | tf_op jit(solution)/shard_map/ppermute | solution.py:19
  48.2 1.6 %collective-permute-done.7 = f32[1,1,1,8,8,128]{5,3,4,2,1,0:T(8,128)S(1)} collective-permute-done((f32[1,1,1,8,8,128]{5,3,4,2,1,0:T(8,128)S(1)}, f32[1,1,1,8,8,128]{5,3,4,2,1,0:T(8,128)S(1)}, u32[]{:S(2)}, u32[]{:S(2)}) %collective-permute-start.7) | collective-permute-done | bytes 32800 | tf_op jit(solution)/shard_map/ppermute | solution.py:19
  51.7 4.3 %collective-permute-start.8 = (f32[1,1,1,8,8,128]{5,4,3,2,1,0:T(8,128)S(1)}, f32[1,1,1,8,8,128]{5,4,3,2,1,0:T(8,128)S(1)}, u32[]{:S(2)}, u32[]{:S(2)}) collective-permute-start(f32[1,1,1,8,8,128]{5,4,3,2,1,0:T(8,128)S(1)} %bitcast.486), channel_id=1, source_target_pairs={{0,4},{4,8},{8,12},{12,16},{16,20},{20,24},{24,28},{1,5},{5,9},{9,... | collective-permute-start | bytes 98312 | tf_op jit(solution)/shard_map/ppermute | solution.py:16
  56.0 1.3 collective-permute-start.9
  57.6 4.2 %collective-permute-done.9 = f32[1,1,1,8,8,128]{5,4,3,2,1,0:T(8,128)S(1)} collective-permute-done((f32[1,1,1,8,8,128]{5,4,3,2,1,0:T(8,128)S(1)}, f32[1,1,1,8,8,128]{5,4,3,2,1,0:T(8,128)S(1)}, u32[]{:S(2)}, u32[]{:S(2)}) %collective-permute-start.9) | collective-permute-done | bytes 32800 | tf_op jit(solution)/shard_map/ppermute | solution.py:19
  61.9 1.9 %collective-permute-start.10 = (f32[1,1,1,8,8,128]{5,3,4,2,1,0:T(8,128)S(1)}, f32[1,1,1,8,8,128]{5,3,4,2,1,0:T(8,128)S(1)}, u32[]{:S(2)}, u32[]{:S(2)}) collective-permute-start(f32[1,1,1,8,8,128]{5,3,4,2,1,0:T(8,128)S(1)} %maximum_bitcast_fusion.10), channel_id=1, source_target_pairs={{0,1},{1,2},{2,3},{4,5},{5,6},{6,7},{8,9},{9,10},{10,11},{12,13},{... | collective-permute-start | bytes 98312 | tf_op jit(solution)/shard_map/ppermute | solution.py:16
  63.8 3.3 %collective-permute-done.10 = f32[1,1,1,8,8,128]{5,3,4,2,1,0:T(8,128)S(1)} collective-permute-done((f32[1,1,1,8,8,128]{5,3,4,2,1,0:T(8,128)S(1)}, f32[1,1,1,8,8,128]{5,3,4,2,1,0:T(8,128)S(1)}, u32[]{:S(2)}, u32[]{:S(2)}) %collective-permute-start.10) | collective-permute-done | bytes 32800 | tf_op jit(solution)/shard_map/ppermute | solution.py:16
  67.1 1.9 %collective-permute-start.11 = (f32[1,1,1,8,8,128]{5,3,4,2,1,0:T(8,128)S(1)}, f32[1,1,1,8,8,128]{5,3,4,2,1,0:T(8,128)S(1)}, u32[]{:S(2)}, u32[]{:S(2)}) collective-permute-start(f32[1,1,1,8,8,128]{5,3,4,2,1,0:T(8,128)S(1)} %get-tuple-element.23), channel_id=1, source_target_pairs={{1,0},{2,1},{3,2},{5,4},{6,5},{7,6},{9,8},{10,9},{11,10},{13,12},{... | collective-permute-start | bytes 98312 | tf_op jit(solution)/shard_map/ppermute | solution.py:19
  69.1 1.5 collective-permute-done.11
  72.6 3.4 %collective-permute-start.12 = (f32[1,1,1,8,8,128]{5,4,3,2,1,0:T(8,128)S(1)}, f32[1,1,1,8,8,128]{5,4,3,2,1,0:T(8,128)S(1)}, u32[]{:S(2)}, u32[]{:S(2)}) collective-permute-start(f32[1,1,1,8,8,128]{5,4,3,2,1,0:T(8,128)S(1)} %bitcast.480), channel_id=1, source_target_pairs={{0,4},{4,8},{8,12},{12,16},{16,20},{20,24},{24,28},{1,5},{5,9},{9,... | collective-permute-start | bytes 98312 | tf_op jit(solution)/shard_map/ppermute | solution.py:16
  76.1 1.3 collective-permute-start.13
  77.7 4.2 %collective-permute-done.13 = f32[1,1,1,8,8,128]{5,4,3,2,1,0:T(8,128)S(1)} collective-permute-done((f32[1,1,1,8,8,128]{5,4,3,2,1,0:T(8,128)S(1)}, f32[1,1,1,8,8,128]{5,4,3,2,1,0:T(8,128)S(1)}, u32[]{:S(2)}, u32[]{:S(2)}) %collective-permute-start.13) | collective-permute-done | bytes 32800 | tf_op jit(solution)/shard_map/ppermute | solution.py:19
  81.9 1.9 %collective-permute-start.14 = (f32[1,1,1,8,8,128]{5,3,4,2,1,0:T(8,128)S(1)}, f32[1,1,1,8,8,128]{5,3,4,2,1,0:T(8,128)S(1)}, u32[]{:S(2)}, u32[]{:S(2)}) collective-permute-start(f32[1,1,1,8,8,128]{5,3,4,2,1,0:T(8,128)S(1)} %maximum_bitcast_fusion.8), channel_id=1, source_target_pairs={{0,1},{1,2},{2,3},{4,5},{5,6},{6,7},{8,9},{9,10},{10,11},{12,13},{... | collective-permute-start | bytes 98312 | tf_op jit(solution)/shard_map/ppermute | solution.py:16
  83.9 3.2 %collective-permute-done.14 = f32[1,1,1,8,8,128]{5,3,4,2,1,0:T(8,128)S(1)} collective-permute-done((f32[1,1,1,8,8,128]{5,3,4,2,1,0:T(8,128)S(1)}, f32[1,1,1,8,8,128]{5,3,4,2,1,0:T(8,128)S(1)}, u32[]{:S(2)}, u32[]{:S(2)}) %collective-permute-start.14) | collective-permute-done | bytes 32800 | tf_op jit(solution)/shard_map/ppermute | solution.py:16
  87.2 1.9 %collective-permute-start.15 = (f32[1,1,1,8,8,128]{5,3,4,2,1,0:T(8,128)S(1)}, f32[1,1,1,8,8,128]{5,3,4,2,1,0:T(8,128)S(1)}, u32[]{:S(2)}, u32[]{:S(2)}) collective-permute-start(f32[1,1,1,8,8,128]{5,3,4,2,1,0:T(8,128)S(1)} %get-tuple-element.21), channel_id=1, source_target_pairs={{1,0},{2,1},{3,2},{5,4},{6,5},{7,6},{9,8},{10,9},{11,10},{13,12},{... | collective-permute-start | bytes 98312 | tf_op jit(solution)/shard_map/ppermute | solution.py:19
  89.1 5.7 %fusion.17 = f32[4096,768]{0,1:T(8,128)} fusion(s32[4096]{0:T(1024)S(1)} %get-tuple-element.76, bf16[256,256]{1,0:T(8,128)(2,1)S(1)} %get-tuple-element.33, bf16[256,256]{1,0:T(8,128)(2,1)S(1)} %get-tuple-element.34, bf16[256,256]{1,0:T(8,128)(2,1)S(1)} %get-tuple-element.32), kind=kOutput, calls=%fused_computation.23 | convolution fusion | flops 1612840960 | bytes 12992512 | tf_op jit(solution)/shard_map/dot_general | solution.py:148
  97.1 4.3 %collective-permute-start.16 = (f32[1,1,1,8,8,128]{5,4,3,2,1,0:T(8,128)S(1)}, f32[1,1,1,8,8,128]{5,4,3,2,1,0:T(8,128)S(1)}, u32[]{:S(2)}, u32[]{:S(2)}) collective-permute-start(f32[1,1,1,8,8,128]{5,4,3,2,1,0:T(8,128)S(1)} %bitcast.476), channel_id=1, source_target_pairs={{0,4},{4,8},{8,12},{12,16},{16,20},{20,24},{24,28},{1,5},{5,9},{9,... | collective-permute-start | bytes 98312 | tf_op jit(solution)/shard_map/ppermute | solution.py:16
  101.4 1.5 collective-permute-start.17
  102.9 2.0 %fusion.16 = f32[4096,768]{0,1:T(8,128)S(1)} fusion(s32[4096]{0:T(1024)S(1)} %get-tuple-element.76, bf16[256,256]{1,0:T(8,128)(2,1)S(1)} %get-tuple-element.36, bf16[256,256]{1,0:T(8,128)(2,1)S(1)} %get-tuple-element.37, bf16[256,256]{1,0:T(8,128)(2,1)S(1)} %get-tuple-element.35), kind=kOutput, calls=%fused_computation.22 | convolution fusion | flops 1612840960 | bytes 12992512 | tf_op jit(solution)/shard_map/dot_general | solution.py:148
  104.9 2.5 %copy-done = f32[4096,768]{0,1:T(8,128)S(1)} copy-done((f32[4096,768]{0,1:T(8,128)S(1)}, f32[4096,768]{0,1:T(8,128)}, u32[]{:S(2)}) %copy-start) | copy-done | bytes 12582936
  107.5 1.9 %fusion.13 = (f32[4096]{0:T(1024)S(1)}, f32[4096]{0:T(1024)S(1)}) fusion(f32[4096,768]{0,1:T(8,128)S(1)} %fusion.16, s32[4096]{0:T(1024)S(1)} %get-tuple-element.75, f32[4096,768]{0,1:T(8,128)S(1)} %copy-done), kind=kLoop, calls=%fused_computation.15 | loop fusion | flops 9428992 | bytes 25214976 | tf_op jit(solution)/shard_map/reduce_sum | solution.py:151
  109.4 4.6 %fusion.23 = (bf16[4096,256]{1,0:T(8,128)(2,1)S(1)}, bf16[4096,256]{1,0:T(8,128)(2,1)S(1)}, bf16[4096,256]{1,0:T(8,128)(2,1)S(1)}, bf16[4096,256]{1,0:T(8,128)(2...) fusion(s32[4096]{0:T(1024)S(1)} %get-tuple-element.63, bf16[4096]{0:T(1024)(128)(2,1)S(1)} %get-tuple-element.11, ...), kind=kLoop, calls=%fused_computation.31 | loop fusion | flops 7340032 | bytes 12648448 | tf_op jit(solution)/shard_map/mul | solution.py:157
  114.0 2.6 %fusion.6 = f32[256,768]{1,0:T(8,128)S(1)} fusion(bf16[4096,256]{1,0:T(8,128)(2,1)S(1)} %get-tuple-element.65, bf16[4096,256]{1,0:T(8,128)(2,1)S(1)} %get-tuple-element.66, bf16[4096,256]{1,0:T(8,128)(2,1)S(1)} %get-tuple-element.67, s32[4096]{0:T(1024)S(1)} %get-tuple-element.62), kind=kOutput, calls=%fused_computation.7 | convolution fusion | flops 1630535680 | bytes 7094272 | tf_op jit(solution)/shard_map/dot_general | solution.py:159
  116.6 2.6 %fusion = f32[256,768]{1,0:T(8,128)S(1)} fusion(bf16[4096,256]{1,0:T(8,128)(2,1)S(1)} %get-tuple-element.68, bf16[4096,256]{1,0:T(8,128)(2,1)S(1)} %get-tuple-element.69, bf16[4096,256]{1,0:T(8,128)(2,1)S(1)} %get-tuple-element.64, s32[4096]{0:T(1024)S(1)} %get-tuple-element.62), kind=kOutput, calls=%fused_computation.1 | convolution fusion | flops 1630535680 | bytes 7094272 | tf_op jit(solution)/shard_map/dot_general | solution.py:159
  120.1 2.1 %collective-permute-start.18 = (f32[1,1,1,8,8,128]{5,3,4,2,1,0:T(8,128)S(1)}, f32[1,1,1,8,8,128]{5,3,4,2,1,0:T(8,128)S(1)}, u32[]{:S(2)}, u32[]{:S(2)}) collective-permute-start(f32[1,1,1,8,8,128]{5,3,4,2,1,0:T(8,128)S(1)} %maximum_bitcast_fusion.6), channel_id=1, source_target_pairs={{0,1},{1,2},{2,3},{4,5},{5,6},{6,7},{8,9},{9,10},{10,11},{12,13},{... | collective-permute-start | bytes 98312 | tf_op jit(solution)/shard_map/ppermute | solution.py:16
  122.2 1.3 pad_maximum_fusion.1
  123.5 5.3 %all-to-all-start = ((f32[32,2,2048]{2,1,0:T(2,128)}), f32[32,2,2048]{2,1,0:T(2,128)S(1)}, u32[]{:S(2)}, u32[]{:S(2)}) async-start(f32[32,2,2048]{2,1,0:T(2,128)} %bitcast.122), calls=%async_computation | async-start | bytes 1048576 | tf_op jit(solution)/shard_map/all_to_all | solution.py:173
  128.8 2.0 %collective-permute-start.19 = (f32[1,1,1,8,8,128]{5,3,4,2,1,0:T(8,128)S(1)}, f32[1,1,1,8,8,128]{5,3,4,2,1,0:T(8,128)S(1)}, u32[]{:S(2)}, u32[]{:S(2)}) collective-permute-start(f32[1,1,1,8,8,128]{5,3,4,2,1,0:T(8,128)S(1)} %get-tuple-element.19), channel_id=1, source_target_pairs={{1,0},{2,1},{3,2},{5,4},{6,5},{7,6},{9,8},{10,9},{11,10},{13,12},{... | collective-permute-start | bytes 98312 | tf_op jit(solution)/shard_map/ppermute | solution.py:19
  132.7 10.8 %all-to-all-done = f32[32,2,2048]{2,1,0:T(2,128)S(1)} async-done(((f32[32,2,2048]{2,1,0:T(2,128)}), f32[32,2,2048]{2,1,0:T(2,128)S(1)}, u32[]{:S(2)}, u32[]{:S(2)}) %all-to-all-start) | async-done | bytes 524320 | tf_op jit(solution)/shard_map/all_to_all | solution.py:173
  144.3 3.6 %all-to-all-start.1 = ((f32[8,2,2048]{2,1,0:T(2,128)}), f32[8,2,2048]{2,1,0:T(2,128)S(1)}, u32[]{:S(2)}, u32[]{:S(2)}) async-start(f32[8,2,2048]{2,1,0:T(2,128)} %broadcast_in_dim.185), calls=%async_computation.1 | async-start | bytes 262144 | tf_op jit(solution)/shard_map/all_to_all | solution.py:175
  148.8 6.7 %all-to-all-done.1 = f32[8,2,2048]{2,1,0:T(2,128)S(1)} async-done(((f32[8,2,2048]{2,1,0:T(2,128)}), f32[8,2,2048]{2,1,0:T(2,128)S(1)}, u32[]{:S(2)}, u32[]{:S(2)}) %all-to-all-start.1) | async-done | bytes 131104 | tf_op jit(solution)/shard_map/all_to_all | solution.py:175
  (131 shorter events, 17.5 us)
Async XLA Ops:
  6.2 5.3 %collective-permute-start = (f32[2,1,1,8,8,128]{5,0,4,3,2,1:T(2,128)S(1)}, f32[2,1,1,8,8,128]{5,0,4,3,2,1:T(2,128)S(1)}, u32[]{:S(2)}, u32[]{:S(2)}) collective-permute-start(f32[2,1,1,8,8,128]{5,0,4,3,2,1:T(2,128)S(1)} %maximum_bitcast_fusion.4), channel_id=1, source_target_pairs={{0,4},{4,8},{8,12},{12,16},{16,20},{20,24},{24,28},{1,5},{5,9},{9,... | collective-permute-start | bytes 196616 | tf_op jit(solution)/shard_map/ppermute | solution.py:16
  12.4 6.5 %collective-permute-start.1 = (f32[2,1,1,8,8,128]{5,0,4,3,2,1:T(2,128)S(1)}, f32[2,1,1,8,8,128]{5,0,4,3,2,1:T(2,128)S(1)}, u32[]{:S(2)}, u32[]{:S(2)}) collective-permute-start(f32[2,1,1,8,8,128]{5,0,4,3,2,1:T(2,128)S(1)} %get-tuple-element.31), channel_id=1, source_target_pairs={{4,0},{8,4},{12,8},{16,12},{20,16},{24,20},{28,24},{5,1},{9,5},{13... | collective-permute-start | bytes 196616 | tf_op jit(solution)/shard_map/ppermute | solution.py:19
  15.0 13.8 %copy-start.1 = (f32[8,8,1,1]{1,0,3,2:T(8,128)S(1)}, f32[8,8,1,1]{1,0,3,2:T(8,128)}, u32[]{:S(2)}) copy-start(f32[8,8,1,1]{1,0,3,2:T(8,128)} %constant.132) | copy-start | bytes 772
  15.2 14.4 %copy-start.2 = (f32[8]{0:T(128)S(1)}, f32[8]{0:T(128)}, u32[]{:S(2)}) copy-start(f32[8]{0:T(128)} %constant.91.clone) | copy-start | bytes 100
  18.9 5.6 %collective-permute-start.2 = (f32[2,1,1,8,8,128]{5,3,0,4,2,1:T(8,128)S(1)}, f32[2,1,1,8,8,128]{5,3,0,4,2,1:T(8,128)S(1)}, u32[]{:S(2)}, u32[]{:S(2)}) collective-permute-start(f32[2,1,1,8,8,128]{5,3,0,4,2,1:T(8,128)S(1)} %maximum_bitcast_fusion.2), channel_id=1, source_target_pairs={{0,1},{1,2},{2,3},{4,5},{5,6},{6,7},{8,9},{9,10},{10,11},{12,13},{... | collective-permute-start | bytes 196616 | tf_op jit(solution)/shard_map/ppermute | solution.py:16
  24.6 3.8 %collective-permute-start.3 = (f32[2,1,1,8,8,128]{5,3,0,4,2,1:T(8,128)S(1)}, f32[2,1,1,8,8,128]{5,3,0,4,2,1:T(8,128)S(1)}, u32[]{:S(2)}, u32[]{:S(2)}) collective-permute-start(f32[2,1,1,8,8,128]{5,3,0,4,2,1:T(8,128)S(1)} %get-tuple-element.29), channel_id=1, source_target_pairs={{1,0},{2,1},{3,2},{5,4},{6,5},{7,6},{9,8},{10,9},{11,10},{13,12},{... | collective-permute-start | bytes 196616 | tf_op jit(solution)/shard_map/ppermute | solution.py:19
  30.3 33.5 %copy-start.4 = (s32[1,4096,1]{1,2,0:T(1,128)S(1)}, s32[1,4096,1]{1,2,0:T(1,128)}, u32[]{:S(2)}) copy-start(s32[1,4096,1]{1,2,0:T(1,128)} %param.11) | copy-start | bytes 49156
  30.3 38.8 %copy-start.5 = (s32[1,4096]{1,0:T(1,128)S(1)}, s32[1,4096]{1,0:T(1,128)}, u32[]{:S(2)}) copy-start(s32[1,4096]{1,0:T(1,128)} %param.12) | copy-start | bytes 49156
  30.3 6.4 %collective-permute-start.4 = (f32[1,1,1,8,8,128]{5,4,3,2,1,0:T(8,128)S(1)}, f32[1,1,1,8,8,128]{5,4,3,2,1,0:T(8,128)S(1)}, u32[]{:S(2)}, u32[]{:S(2)}) collective-permute-start(f32[1,1,1,8,8,128]{5,4,3,2,1,0:T(8,128)S(1)} %bitcast.484), channel_id=1, source_target_pairs={{0,4},{4,8},{8,12},{12,16},{16,20},{20,24},{24,28},{1,5},{5,9},{9,... | collective-permute-start | bytes 98312 | tf_op jit(solution)/shard_map/ppermute | solution.py:16
  35.2 5.8 %collective-permute-start.5 = (f32[1,1,1,8,8,128]{5,4,3,2,1,0:T(8,128)S(1)}, f32[1,1,1,8,8,128]{5,4,3,2,1,0:T(8,128)S(1)}, u32[]{:S(2)}, u32[]{:S(2)}) collective-permute-start(f32[1,1,1,8,8,128]{5,4,3,2,1,0:T(8,128)S(1)} %bitcast.488), channel_id=1, source_target_pairs={{4,0},{8,4},{12,8},{16,12},{20,16},{24,20},{28,24},{5,1},{9,5},{13... | collective-permute-start | bytes 98312 | tf_op jit(solution)/shard_map/ppermute | solution.py:19
  41.0 5.2 %collective-permute-start.6 = (f32[1,1,1,8,8,128]{5,3,4,2,1,0:T(8,128)S(1)}, f32[1,1,1,8,8,128]{5,3,4,2,1,0:T(8,128)S(1)}, u32[]{:S(2)}, u32[]{:S(2)}) collective-permute-start(f32[1,1,1,8,8,128]{5,3,4,2,1,0:T(8,128)S(1)} %maximum_bitcast_fusion.12), channel_id=1, source_target_pairs={{0,1},{1,2},{2,3},{4,5},{5,6},{6,7},{8,9},{9,10},{10,11},{12,13},{... | collective-permute-start | bytes 98312 | tf_op jit(solution)/shard_map/ppermute | solution.py:16
  46.3 3.5 %collective-permute-start.7 = (f32[1,1,1,8,8,128]{5,3,4,2,1,0:T(8,128)S(1)}, f32[1,1,1,8,8,128]{5,3,4,2,1,0:T(8,128)S(1)}, u32[]{:S(2)}, u32[]{:S(2)}) collective-permute-start(f32[1,1,1,8,8,128]{5,3,4,2,1,0:T(8,128)S(1)} %get-tuple-element.25), channel_id=1, source_target_pairs={{1,0},{2,1},{3,2},{5,4},{6,5},{7,6},{9,8},{10,9},{11,10},{13,12},{... | collective-permute-start | bytes 98312 | tf_op jit(solution)/shard_map/ppermute | solution.py:19
  51.7 5.9 %collective-permute-start.8 = (f32[1,1,1,8,8,128]{5,4,3,2,1,0:T(8,128)S(1)}, f32[1,1,1,8,8,128]{5,4,3,2,1,0:T(8,128)S(1)}, u32[]{:S(2)}, u32[]{:S(2)}) collective-permute-start(f32[1,1,1,8,8,128]{5,4,3,2,1,0:T(8,128)S(1)} %bitcast.486), channel_id=1, source_target_pairs={{0,4},{4,8},{8,12},{12,16},{16,20},{20,24},{24,28},{1,5},{5,9},{9,... | collective-permute-start | bytes 98312 | tf_op jit(solution)/shard_map/ppermute | solution.py:16
  56.0 5.8 %collective-permute-start.9 = (f32[1,1,1,8,8,128]{5,4,3,2,1,0:T(8,128)S(1)}, f32[1,1,1,8,8,128]{5,4,3,2,1,0:T(8,128)S(1)}, u32[]{:S(2)}, u32[]{:S(2)}) collective-permute-start(f32[1,1,1,8,8,128]{5,4,3,2,1,0:T(8,128)S(1)} %bitcast.490), channel_id=1, source_target_pairs={{4,0},{8,4},{12,8},{16,12},{20,16},{24,20},{28,24},{5,1},{9,5},{13... | collective-permute-start | bytes 98312 | tf_op jit(solution)/shard_map/ppermute | solution.py:19
  57.4 20.0 %copy-start.3 = (s32[1,4096]{1,0:T(1,128)S(1)}, s32[1,4096]{1,0:T(1,128)}, u32[]{:S(2)}) copy-start(s32[1,4096]{1,0:T(1,128)} %param.10) | copy-start | bytes 49156
  61.9 5.2 %collective-permute-start.10 = (f32[1,1,1,8,8,128]{5,3,4,2,1,0:T(8,128)S(1)}, f32[1,1,1,8,8,128]{5,3,4,2,1,0:T(8,128)S(1)}, u32[]{:S(2)}, u32[]{:S(2)}) collective-permute-start(f32[1,1,1,8,8,128]{5,3,4,2,1,0:T(8,128)S(1)} %maximum_bitcast_fusion.10), channel_id=1, source_target_pairs={{0,1},{1,2},{2,3},{4,5},{5,6},{6,7},{8,9},{9,10},{10,11},{12,13},{... | collective-permute-start | bytes 98312 | tf_op jit(solution)/shard_map/ppermute | solution.py:16
  67.1 3.5 %collective-permute-start.11 = (f32[1,1,1,8,8,128]{5,3,4,2,1,0:T(8,128)S(1)}, f32[1,1,1,8,8,128]{5,3,4,2,1,0:T(8,128)S(1)}, u32[]{:S(2)}, u32[]{:S(2)}) collective-permute-start(f32[1,1,1,8,8,128]{5,3,4,2,1,0:T(8,128)S(1)} %get-tuple-element.23), channel_id=1, source_target_pairs={{1,0},{2,1},{3,2},{5,4},{6,5},{7,6},{9,8},{10,9},{11,10},{13,12},{... | collective-permute-start | bytes 98312 | tf_op jit(solution)/shard_map/ppermute | solution.py:19
  72.6 5.0 %collective-permute-start.12 = (f32[1,1,1,8,8,128]{5,4,3,2,1,0:T(8,128)S(1)}, f32[1,1,1,8,8,128]{5,4,3,2,1,0:T(8,128)S(1)}, u32[]{:S(2)}, u32[]{:S(2)}) collective-permute-start(f32[1,1,1,8,8,128]{5,4,3,2,1,0:T(8,128)S(1)} %bitcast.480), channel_id=1, source_target_pairs={{0,4},{4,8},{8,12},{12,16},{16,20},{20,24},{24,28},{1,5},{5,9},{9,... | collective-permute-start | bytes 98312 | tf_op jit(solution)/shard_map/ppermute | solution.py:16
  76.1 5.8 %collective-permute-start.13 = (f32[1,1,1,8,8,128]{5,4,3,2,1,0:T(8,128)S(1)}, f32[1,1,1,8,8,128]{5,4,3,2,1,0:T(8,128)S(1)}, u32[]{:S(2)}, u32[]{:S(2)}) collective-permute-start(f32[1,1,1,8,8,128]{5,4,3,2,1,0:T(8,128)S(1)} %bitcast.482), channel_id=1, source_target_pairs={{4,0},{8,4},{12,8},{16,12},{20,16},{24,20},{28,24},{5,1},{9,5},{13... | collective-permute-start | bytes 98312 | tf_op jit(solution)/shard_map/ppermute | solution.py:19
  81.9 5.2 %collective-permute-start.14 = (f32[1,1,1,8,8,128]{5,3,4,2,1,0:T(8,128)S(1)}, f32[1,1,1,8,8,128]{5,3,4,2,1,0:T(8,128)S(1)}, u32[]{:S(2)}, u32[]{:S(2)}) collective-permute-start(f32[1,1,1,8,8,128]{5,3,4,2,1,0:T(8,128)S(1)} %maximum_bitcast_fusion.8), channel_id=1, source_target_pairs={{0,1},{1,2},{2,3},{4,5},{5,6},{6,7},{8,9},{9,10},{10,11},{12,13},{... | collective-permute-start | bytes 98312 | tf_op jit(solution)/shard_map/ppermute | solution.py:16
  87.2 7.7 %collective-permute-start.15 = (f32[1,1,1,8,8,128]{5,3,4,2,1,0:T(8,128)S(1)}, f32[1,1,1,8,8,128]{5,3,4,2,1,0:T(8,128)S(1)}, u32[]{:S(2)}, u32[]{:S(2)}) collective-permute-start(f32[1,1,1,8,8,128]{5,3,4,2,1,0:T(8,128)S(1)} %get-tuple-element.21), channel_id=1, source_target_pairs={{1,0},{2,1},{3,2},{5,4},{6,5},{7,6},{9,8},{10,9},{11,10},{13,12},{... | collective-permute-start | bytes 98312 | tf_op jit(solution)/shard_map/ppermute | solution.py:19
  97.1 22.9 %collective-permute-start.16 = (f32[1,1,1,8,8,128]{5,4,3,2,1,0:T(8,128)S(1)}, f32[1,1,1,8,8,128]{5,4,3,2,1,0:T(8,128)S(1)}, u32[]{:S(2)}, u32[]{:S(2)}) collective-permute-start(f32[1,1,1,8,8,128]{5,4,3,2,1,0:T(8,128)S(1)} %bitcast.476), channel_id=1, source_target_pairs={{0,4},{4,8},{8,12},{12,16},{16,20},{20,24},{24,28},{1,5},{5,9},{9,... | collective-permute-start | bytes 98312 | tf_op jit(solution)/shard_map/ppermute | solution.py:16
  101.4 18.6 %collective-permute-start.17 = (f32[1,1,1,8,8,128]{5,4,3,2,1,0:T(8,128)S(1)}, f32[1,1,1,8,8,128]{5,4,3,2,1,0:T(8,128)S(1)}, u32[]{:S(2)}, u32[]{:S(2)}) collective-permute-start(f32[1,1,1,8,8,128]{5,4,3,2,1,0:T(8,128)S(1)} %bitcast.478), channel_id=1, source_target_pairs={{4,0},{8,4},{12,8},{16,12},{20,16},{24,20},{28,24},{5,1},{9,5},{13... | collective-permute-start | bytes 98312 | tf_op jit(solution)/shard_map/ppermute | solution.py:19
  102.9 4.6 %copy-start = (f32[4096,768]{0,1:T(8,128)S(1)}, f32[4096,768]{0,1:T(8,128)}, u32[]{:S(2)}) copy-start(f32[4096,768]{0,1:T(8,128)} %fusion.17) | copy-start | bytes 37748740
  107.5 1.9 %copy-start.6 = (f32[1,4096]{1,0:T(1,128)S(1)}, f32[1,4096]{1,0:T(1,128)}, u32[]{:S(2)}) copy-start(f32[1,4096]{1,0:T(1,128)} %param.13) | copy-start | bytes 49156
  120.1 8.7 %collective-permute-start.18 = (f32[1,1,1,8,8,128]{5,3,4,2,1,0:T(8,128)S(1)}, f32[1,1,1,8,8,128]{5,3,4,2,1,0:T(8,128)S(1)}, u32[]{:S(2)}, u32[]{:S(2)}) collective-permute-start(f32[1,1,1,8,8,128]{5,3,4,2,1,0:T(8,128)S(1)} %maximum_bitcast_fusion.6), channel_id=1, source_target_pairs={{0,1},{1,2},{2,3},{4,5},{5,6},{6,7},{8,9},{9,10},{10,11},{12,13},{... | collective-permute-start | bytes 98312 | tf_op jit(solution)/shard_map/ppermute | solution.py:16
  123.5 20.0 %all-to-all-start = ((f32[32,2,2048]{2,1,0:T(2,128)}), f32[32,2,2048]{2,1,0:T(2,128)S(1)}, u32[]{:S(2)}, u32[]{:S(2)}) async-start(f32[32,2,2048]{2,1,0:T(2,128)} %bitcast.122), calls=%async_computation | async-start | bytes 1048576 | tf_op jit(solution)/shard_map/all_to_all | solution.py:173
  128.8 3.6 %collective-permute-start.19 = (f32[1,1,1,8,8,128]{5,3,4,2,1,0:T(8,128)S(1)}, f32[1,1,1,8,8,128]{5,3,4,2,1,0:T(8,128)S(1)}, u32[]{:S(2)}, u32[]{:S(2)}) collective-permute-start(f32[1,1,1,8,8,128]{5,3,4,2,1,0:T(8,128)S(1)} %get-tuple-element.19), channel_id=1, source_target_pairs={{1,0},{2,1},{3,2},{5,4},{6,5},{7,6},{9,8},{10,9},{11,10},{13,12},{... | collective-permute-start | bytes 98312 | tf_op jit(solution)/shard_map/ppermute | solution.py:19
  144.3 11.1 %all-to-all-start.1 = ((f32[8,2,2048]{2,1,0:T(2,128)}), f32[8,2,2048]{2,1,0:T(2,128)S(1)}, u32[]{:S(2)}, u32[]{:S(2)}) async-start(f32[8,2,2048]{2,1,0:T(2,128)} %broadcast_in_dim.185), calls=%async_computation.1 | async-start | bytes 262144 | tf_op jit(solution)/shard_map/all_to_all | solution.py:175

commit v4 on v3

--- a/solution.py
+++ b/solution.py
@@ -195,18 +195,23 @@
     global_ids = fac_strip[0, :, 0] * SHELL_STRIP + fac_shell[0]
     denom = segment_sum(areas, global_ids, strips * SHELL_STRIP, 256)
     for step in range(SWEEPS):
+        pressure = pressure + update
+        if step + 2 == SWEEPS:
+            early = gather_flat(pressure.reshape(-1), picks, 256)
+        applied = element_apply(update, metric, weights, stiff)
         if step + 1 == SWEEPS:
-            early = gather_flat(pressure.reshape(-1), picks, 256)
             samples = early + gather_flat(update.reshape(-1), picks, 256)
-        pressure = pressure + update
-        resid = resid - assemble(element_apply(update, metric, weights, stiff)[None])[0]
+            numer = segment_sum(areas * samples, global_ids, strips * SHELL_STRIP, 256)
+            partial = jnp.stack([numer, denom])
+            applied, partial = lax.optimization_barrier((applied, partial))
+        assembled = assemble(applied[None])[0]
+        if step + 2 == SWEEPS:
+            assembled, early = lax.optimization_barrier((assembled, early))
+        resid = resid - assembled
         if step + 1 < SWEEPS:
             rho_new = 1.0 / (2.0 * sigma - rho_now)
             update = rho_new * rho_now * update + 2.0 * rho_new / delta * pinv * resid
             rho_now = rho_new
-    weighted = areas * samples
-    numer = segment_sum(weighted, global_ids, strips * SHELL_STRIP, 256)
-    partial = jnp.stack([numer, denom])
     total = strip_totals(partial, strips, SHELL_STRIP)
     shell_load = total[0] / jnp.maximum(total[1], 1.0)
     return (pressure, resid, shell_load)

time: 159 us -> 156 us (0.981)
  starting transfers between devices: 55.4 us -> 66.2 us
  waiting for transfers between devices: 55.3 us -> 46.1 us
  matrix products: 18.9 us -> 15.2 us
    ppermute x10, waiting for transfers between devices: 21.9 us -> 9.4 us  [padded_2(): lax.ppermute(lax.slice_in_dim(block, 0, width, axis=dim), axis, backward)]
    ppermute x10, starting transfers between devices: 30.1 us -> 35.4 us  [padded_2(): lax.ppermute(lax.slice_in_dim(block, block.shape[dim] - width, None, axis...]
    all_to_all x1, starting transfers between devices: 5.3 us -> 10.4 us  [strip_totals(): mine = lax.all_to_all(chunks, ('ex', 'ey'), 0, 0, tiled=True).sum(0)]
    dot_general x2, matrix products: 7.73 us -> 4.02 us  [gather_flat(): picked = jnp.dot(hit_row, parts, preferred_element_type=jnp.float32)]
    ppermute x10, waiting for transfers between devices: 15.9 us -> 19.2 us  [padded_2(): lax.ppermute(lax.slice_in_dim(block, block.shape[dim] - width, None, axis...]
    unnamed x16 -> x17, local copies, waits for them, and re-layouts: 4.09 us -> 2.39 us
  transfers between devices with their start and end apart: 22 -> 22, of which waited for: 18 -> 16; matrix products, arithmetic and copies ran while one was open for 16% -> 6% of each run, Pallas kernels for 0% -> 0%
where the time goes in v4:
time: 156 us; the launch traced here: 153 us
  starting transfers between devices  66.2 us (42%)
  waiting for transfers between devices  46.1 us (30%)
  other arithmetic  16.5 us (11%)
  matrix products  15.2 us (10%)
  local copies, waits for them, and re-layouts  7.58 us (5%)
  between operations  1.57 us (1%)
    ppermute x10, starting transfers between devices, padded_2(): lax.ppermute(lax.slice_in_dim(block, block.shape[dim] - width, None, axis...  35.4 us
    ppermute x10, waiting for transfers between devices, padded_2(): lax.ppermute(lax.slice_in_dim(block, block.shape[dim] - width, None, axis...  19.2 us
    ppermute x10, starting transfers between devices, padded_2(): lax.ppermute(lax.slice_in_dim(block, 0, width, axis=dim), axis, backward)  16.8 us
    all_to_all x1, waiting for transfers between devices, strip_totals(): mine = lax.all_to_all(chunks, ('ex', 'ey'), 0, 0, tiled=True).sum(0)  10.8 us
    all_to_all x1, starting transfers between devices, strip_totals(): mine = lax.all_to_all(chunks, ('ex', 'ey'), 0, 0, tiled=True).sum(0)  10.4 us
    ppermute x10, waiting for transfers between devices, padded_2(): lax.ppermute(lax.slice_in_dim(block, 0, width, axis=dim), axis, backward)  9.4 us
    all_to_all x1, waiting for transfers between devices, strip_totals(): whole = lax.all_to_all(spread_out, 'ex', 0, 0, tiled=True)  6.71 us
    dot_general x2, matrix products, segment_sum(): lax.dot_general(hit_row, rhs, (((0,), (0,)), ((), ())), preferred_element...  5.17 us
  transfers between devices with their start and end apart: 22, of which 16 were waited for; matrix products, arithmetic and copies ran while one was open for 6% of the time, Pallas kernels for 0%

profile of v4, /device:TPU:2, one launch (start us, length us, event | category | flops | bytes accessed | tf_op | source)
XLA Modules:
  0.0 153.2 jit_solution(2115724542475724903)
XLA Ops:
  1.4 1.3 gather_fusion
  4.2 1.1 fusion.94
  6.2 3.4 %collective-permute-start = (f32[2,1,1,8,8,128]{5,0,4,3,2,1:T(2,128)S(1)}, f32[2,1,1,8,8,128]{5,0,4,3,2,1:T(2,128)S(1)}, u32[]{:S(2)}, u32[]{:S(2)}) collective-permute-start(f32[2,1,1,8,8,128]{5,0,4,3,2,1:T(2,128)S(1)} %maximum_bitcast_fusion.6), channel_id=1, source_target_pairs={{0,4},{4,8},{8,12},{12,16},{16,20},{20,24},{24,28},{1,5},{5,9},{9,... | collective-permute-start | bytes 196616 | tf_op jit(solution)/shard_map/ppermute | solution.py:16
  9.6 1.9 %collective-permute-done = f32[2,1,1,8,8,128]{5,0,4,3,2,1:T(2,128)S(1)} collective-permute-done((f32[2,1,1,8,8,128]{5,0,4,3,2,1:T(2,128)S(1)}, f32[2,1,1,8,8,128]{5,0,4,3,2,1:T(2,128)S(1)}, u32[]{:S(2)}, u32[]{:S(2)}) %collective-permute-start) | collective-permute-done | bytes 65568 | tf_op jit(solution)/shard_map/ppermute | solution.py:16
  12.4 1.3 collective-permute-start.1
  13.7 1.3 pad_maximum_fusion.6
  15.2 3.6 %collective-permute-done.1 = f32[2,1,1,8,8,128]{5,0,4,3,2,1:T(2,128)S(1)} collective-permute-done((f32[2,1,1,8,8,128]{5,0,4,3,2,1:T(2,128)S(1)}, f32[2,1,1,8,8,128]{5,0,4,3,2,1:T(2,128)S(1)}, u32[]{:S(2)}, u32[]{:S(2)}) %collective-permute-start.1) | collective-permute-done | bytes 65568 | tf_op jit(solution)/shard_map/ppermute | solution.py:19
  18.9 1.9 %collective-permute-start.2 = (f32[2,1,1,8,8,128]{5,3,0,4,2,1:T(8,128)S(1)}, f32[2,1,1,8,8,128]{5,3,0,4,2,1:T(8,128)S(1)}, u32[]{:S(2)}, u32[]{:S(2)}) collective-permute-start(f32[2,1,1,8,8,128]{5,3,0,4,2,1:T(8,128)S(1)} %maximum_bitcast_fusion.4), channel_id=1, source_target_pairs={{0,1},{1,2},{2,3},{4,5},{5,6},{6,7},{8,9},{9,10},{10,11},{12,13},{... | collective-permute-start | bytes 196616 | tf_op jit(solution)/shard_map/ppermute | solution.py:16
  20.9 3.6 %collective-permute-done.2 = f32[2,1,1,8,8,128]{5,3,0,4,2,1:T(8,128)S(1)} collective-permute-done((f32[2,1,1,8,8,128]{5,3,0,4,2,1:T(8,128)S(1)}, f32[2,1,1,8,8,128]{5,3,0,4,2,1:T(8,128)S(1)}, u32[]{:S(2)}, u32[]{:S(2)}) %collective-permute-start.2) | collective-permute-done | bytes 65568 | tf_op jit(solution)/shard_map/ppermute | solution.py:16
  24.6 1.9 %collective-permute-start.3 = (f32[2,1,1,8,8,128]{5,3,0,4,2,1:T(8,128)S(1)}, f32[2,1,1,8,8,128]{5,3,0,4,2,1:T(8,128)S(1)}, u32[]{:S(2)}, u32[]{:S(2)}) collective-permute-start(f32[2,1,1,8,8,128]{5,3,0,4,2,1:T(8,128)S(1)} %get-tuple-element.37), channel_id=1, source_target_pairs={{1,0},{2,1},{3,2},{5,4},{6,5},{7,6},{9,8},{10,9},{11,10},{13,12},{... | collective-permute-start | bytes 196616 | tf_op jit(solution)/shard_map/ppermute | solution.py:19
  26.6 1.7 %collective-permute-done.3 = f32[2,1,1,8,8,128]{5,3,0,4,2,1:T(8,128)S(1)} collective-permute-done((f32[2,1,1,8,8,128]{5,3,0,4,2,1:T(8,128)S(1)}, f32[2,1,1,8,8,128]{5,3,0,4,2,1:T(8,128)S(1)}, u32[]{:S(2)}, u32[]{:S(2)}) %collective-permute-start.3) | collective-permute-done | bytes 65568 | tf_op jit(solution)/shard_map/ppermute | solution.py:19
  30.4 1.3 collective-permute-start.5
  31.7 5.4 %collective-permute-start.4 = (f32[1,1,1,8,8,128]{5,4,3,2,1,0:T(8,128)S(1)}, f32[1,1,1,8,8,128]{5,4,3,2,1,0:T(8,128)S(1)}, u32[]{:S(2)}, u32[]{:S(2)}) collective-permute-start(f32[1,1,1,8,8,128]{5,4,3,2,1,0:T(8,128)S(1)} %bitcast.516), channel_id=1, source_target_pairs={{0,4},{4,8},{8,12},{12,16},{16,20},{20,24},{24,28},{1,5},{5,9},{9,... | collective-permute-start | bytes 98312 | tf_op jit(solution)/shard_map/ppermute | solution.py:16
  37.2 1.5 collective-permute-done.4
  38.7 1.9 %collective-permute-start.6 = (f32[1,1,1,8,8,128]{5,3,4,2,1,0:T(8,128)S(1)}, f32[1,1,1,8,8,128]{5,3,4,2,1,0:T(8,128)S(1)}, u32[]{:S(2)}, u32[]{:S(2)}) collective-permute-start(f32[1,1,1,8,8,128]{5,3,4,2,1,0:T(8,128)S(1)} %maximum_bitcast_fusion.14), channel_id=1, source_target_pairs={{0,1},{1,2},{2,3},{4,5},{5,6},{6,7},{8,9},{9,10},{10,11},{12,13},{... | collective-permute-start | bytes 98312 | tf_op jit(solution)/shard_map/ppermute | solution.py:16
  40.7 3.3 %collective-permute-done.6 = f32[1,1,1,8,8,128]{5,3,4,2,1,0:T(8,128)S(1)} collective-permute-done((f32[1,1,1,8,8,128]{5,3,4,2,1,0:T(8,128)S(1)}, f32[1,1,1,8,8,128]{5,3,4,2,1,0:T(8,128)S(1)}, u32[]{:S(2)}, u32[]{:S(2)}) %collective-permute-start.6) | collective-permute-done | bytes 32800 | tf_op jit(solution)/shard_map/ppermute | solution.py:16
  44.0 1.9 %collective-permute-start.7 = (f32[1,1,1,8,8,128]{5,3,4,2,1,0:T(8,128)S(1)}, f32[1,1,1,8,8,128]{5,3,4,2,1,0:T(8,128)S(1)}, u32[]{:S(2)}, u32[]{:S(2)}) collective-permute-start(f32[1,1,1,8,8,128]{5,3,4,2,1,0:T(8,128)S(1)} %get-tuple-element.33), channel_id=1, source_target_pairs={{1,0},{2,1},{3,2},{5,4},{6,5},{7,6},{9,8},{10,9},{11,10},{13,12},{... | collective-permute-start | bytes 98312 | tf_op jit(solution)/shard_map/ppermute | solution.py:19
  45.9 1.6 %collective-permute-done.7 = f32[1,1,1,8,8,128]{5,3,4,2,1,0:T(8,128)S(1)} collective-permute-done((f32[1,1,1,8,8,128]{5,3,4,2,1,0:T(8,128)S(1)}, f32[1,1,1,8,8,128]{5,3,4,2,1,0:T(8,128)S(1)}, u32[]{:S(2)}, u32[]{:S(2)}) %collective-permute-start.7) | collective-permute-done | bytes 32800 | tf_op jit(solution)/shard_map/ppermute | solution.py:19
  49.4 1.3 collective-permute-start.9
  50.7 5.4 %collective-permute-start.8 = (f32[1,1,1,8,8,128]{5,4,3,2,1,0:T(8,128)S(1)}, f32[1,1,1,8,8,128]{5,4,3,2,1,0:T(8,128)S(1)}, u32[]{:S(2)}, u32[]{:S(2)}) collective-permute-start(f32[1,1,1,8,8,128]{5,4,3,2,1,0:T(8,128)S(1)} %bitcast.514), channel_id=1, source_target_pairs={{0,4},{4,8},{8,12},{12,16},{16,20},{20,24},{24,28},{1,5},{5,9},{9,... | collective-permute-start | bytes 98312 | tf_op jit(solution)/shard_map/ppermute | solution.py:16
  56.3 1.5 collective-permute-done.8
  57.8 1.9 %collective-permute-start.10 = (f32[1,1,1,8,8,128]{5,3,4,2,1,0:T(8,128)S(1)}, f32[1,1,1,8,8,128]{5,3,4,2,1,0:T(8,128)S(1)}, u32[]{:S(2)}, u32[]{:S(2)}) collective-permute-start(f32[1,1,1,8,8,128]{5,3,4,2,1,0:T(8,128)S(1)} %maximum_bitcast_fusion.12), channel_id=1, source_target_pairs={{0,1},{1,2},{2,3},{4,5},{5,6},{6,7},{8,9},{9,10},{10,11},{12,13},{... | collective-permute-start | bytes 98312 | tf_op jit(solution)/shard_map/ppermute | solution.py:16
  59.8 3.3 %collective-permute-done.10 = f32[1,1,1,8,8,128]{5,3,4,2,1,0:T(8,128)S(1)} collective-permute-done((f32[1,1,1,8,8,128]{5,3,4,2,1,0:T(8,128)S(1)}, f32[1,1,1,8,8,128]{5,3,4,2,1,0:T(8,128)S(1)}, u32[]{:S(2)}, u32[]{:S(2)}) %collective-permute-start.10) | collective-permute-done | bytes 32800 | tf_op jit(solution)/shard_map/ppermute | solution.py:16
  63.0 1.9 %collective-permute-start.11 = (f32[1,1,1,8,8,128]{5,3,4,2,1,0:T(8,128)S(1)}, f32[1,1,1,8,8,128]{5,3,4,2,1,0:T(8,128)S(1)}, u32[]{:S(2)}, u32[]{:S(2)}) collective-permute-start(f32[1,1,1,8,8,128]{5,3,4,2,1,0:T(8,128)S(1)} %get-tuple-element.31), channel_id=1, source_target_pairs={{1,0},{2,1},{3,2},{5,4},{6,5},{7,6},{9,8},{10,9},{11,10},{13,12},{... | collective-permute-start | bytes 98312 | tf_op jit(solution)/shard_map/ppermute | solution.py:19
  65.0 1.5 %collective-permute-done.11 = f32[1,1,1,8,8,128]{5,3,4,2,1,0:T(8,128)S(1)} collective-permute-done((f32[1,1,1,8,8,128]{5,3,4,2,1,0:T(8,128)S(1)}, f32[1,1,1,8,8,128]{5,3,4,2,1,0:T(8,128)S(1)}, u32[]{:S(2)}, u32[]{:S(2)}) %collective-permute-start.11) | collective-permute-done | bytes 32800 | tf_op jit(solution)/shard_map/ppermute | solution.py:19
  68.6 1.3 collective-permute-start.13
  69.9 5.7 %collective-permute-start.12 = (f32[1,1,1,8,8,128]{5,4,3,2,1,0:T(8,128)S(1)}, f32[1,1,1,8,8,128]{5,4,3,2,1,0:T(8,128)S(1)}, u32[]{:S(2)}, u32[]{:S(2)}) collective-permute-start(f32[1,1,1,8,8,128]{5,4,3,2,1,0:T(8,128)S(1)} %bitcast.506), channel_id=1, source_target_pairs={{0,4},{4,8},{8,12},{12,16},{16,20},{20,24},{24,28},{1,5},{5,9},{9,... | collective-permute-start | bytes 98312 | tf_op jit(solution)/shard_map/ppermute | solution.py:16
  75.9 1.3 collective-permute-done.12
  77.3 1.9 %collective-permute-start.14 = (f32[1,1,1,8,8,128]{5,3,4,2,1,0:T(8,128)S(1)}, f32[1,1,1,8,8,128]{5,3,4,2,1,0:T(8,128)S(1)}, u32[]{:S(2)}, u32[]{:S(2)}) collective-permute-start(f32[1,1,1,8,8,128]{5,3,4,2,1,0:T(8,128)S(1)} %maximum_bitcast_fusion.10), channel_id=1, source_target_pairs={{0,1},{1,2},{2,3},{4,5},{5,6},{6,7},{8,9},{9,10},{10,11},{12,13},{... | collective-permute-start | bytes 98312 | tf_op jit(solution)/shard_map/ppermute | solution.py:16
  79.2 2.0 %fusion.23 = f32[4096,768]{0,1:T(8,128)S(1)} fusion(s32[4096]{0:T(1024)S(1)} %get-tuple-element.84, bf16[256,256]{1,0:T(8,128)(2,1)S(1)} %get-tuple-element.50, bf16[256,256]{1,0:T(8,128)(2,1)S(1)} %get-tuple-element.51, bf16[256,256]{1,0:T(8,128)(2,1)S(1)} %get-tuple-element.49), kind=kOutput, calls=%fused_computation.31 | convolution fusion | flops 1612840960 | bytes 12992512 | tf_op jit(solution)/shard_map/dot_general | solution.py:148
  81.2 1.3 collective-permute-done.14
  82.5 2.6 %collective-permute-start.15 = (f32[1,1,1,8,8,128]{5,3,4,2,1,0:T(8,128)S(1)}, f32[1,1,1,8,8,128]{5,3,4,2,1,0:T(8,128)S(1)}, u32[]{:S(2)}, u32[]{:S(2)}) collective-permute-start(f32[1,1,1,8,8,128]{5,3,4,2,1,0:T(8,128)S(1)} %get-tuple-element.29), channel_id=1, source_target_pairs={{1,0},{2,1},{3,2},{5,4},{6,5},{7,6},{9,8},{10,9},{11,10},{13,12},{... | collective-permute-start | bytes 98312 | tf_op jit(solution)/shard_map/ppermute | solution.py:19
  85.1 1.4 fusion.15
  88.1 2.0 %fusion.22 = f32[4096,768]{0,1:T(8,128)S(1)} fusion(s32[4096]{0:T(1024)S(1)} %get-tuple-element.84, bf16[256,256]{1,0:T(8,128)(2,1)S(1)} %get-tuple-element.47, bf16[256,256]{1,0:T(8,128)(2,1)S(1)} %get-tuple-element.48, bf16[256,256]{1,0:T(8,128)(2,1)S(1)} %get-tuple-element.46), kind=kOutput, calls=%fused_computation.30 | convolution fusion | flops 1612840960 | bytes 12992512 | tf_op jit(solution)/shard_map/dot_general | solution.py:148
  90.1 1.4 fusion.13
  91.5 4.8 %fusion.21 = (bf16[4096,256]{1,0:T(8,128)(2,1)S(1)}, bf16[4096,256]{1,0:T(8,128)(2,1)S(1)}, bf16[4096,256]{1,0:T(8,128)(2,1)S(1)}, bf16[4096,256]{1,0:T(8,128)(2...) fusion(s32[4096]{0:T(1024)S(1)} %get-tuple-element.71, bf16[4096]{0:T(1024)(128)(2,1)S(1)} %get-tuple-element.22, ...), kind=kLoop, calls=%fused_computation.27 | loop fusion | flops 7340032 | bytes 12648448 | tf_op jit(solution)/shard_map/mul | solution.py:157
  96.3 2.6 %fusion.6 = f32[256,768]{1,0:T(8,128)S(1)} fusion(bf16[4096,256]{1,0:T(8,128)(2,1)S(1)} %get-tuple-element.73, bf16[4096,256]{1,0:T(8,128)(2,1)S(1)} %get-tuple-element.74, bf16[4096,256]{1,0:T(8,128)(2,1)S(1)} %get-tuple-element.75, s32[4096]{0:T(1024)S(1)} %get-tuple-element.70), kind=kOutput, calls=%fused_computation.7 | convolution fusion | flops 1630535680 | bytes 7094272 | tf_op jit(solution)/shard_map/dot_general | solution.py:159
  99.2 2.6 %fusion = f32[256,768]{1,0:T(8,128)S(1)} fusion(bf16[4096,256]{1,0:T(8,128)(2,1)S(1)} %get-tuple-element.76, bf16[4096,256]{1,0:T(8,128)(2,1)S(1)} %get-tuple-element.77, bf16[4096,256]{1,0:T(8,128)(2,1)S(1)} %get-tuple-element.72, s32[4096]{0:T(1024)S(1)} %get-tuple-element.70), kind=kOutput, calls=%fused_computation.1 | convolution fusion | flops 1630535680 | bytes 7094272 | tf_op jit(solution)/shard_map/dot_general | solution.py:159
  103.3 1.3 collective-permute-start.17
  104.6 5.7 %collective-permute-start.16 = (f32[1,1,1,8,8,128]{5,4,3,2,1,0:T(8,128)S(1)}, f32[1,1,1,8,8,128]{5,4,3,2,1,0:T(8,128)S(1)}, u32[]{:S(2)}, u32[]{:S(2)}) collective-permute-start(f32[1,1,1,8,8,128]{5,4,3,2,1,0:T(8,128)S(1)} %bitcast.518), channel_id=1, source_target_pairs={{0,4},{4,8},{8,12},{12,16},{16,20},{20,24},{24,28},{1,5},{5,9},{9,... | collective-permute-start | bytes 98312 | tf_op jit(solution)/shard_map/ppermute | solution.py:16
  110.4 1.5 collective-permute-done.16
  112.0 1.9 %collective-permute-start.18 = (f32[1,1,1,8,8,128]{5,3,4,2,1,0:T(8,128)S(1)}, f32[1,1,1,8,8,128]{5,3,4,2,1,0:T(8,128)S(1)}, u32[]{:S(2)}, u32[]{:S(2)}) collective-permute-start(f32[1,1,1,8,8,128]{5,3,4,2,1,0:T(8,128)S(1)} %maximum_bitcast_fusion.8), channel_id=1, source_target_pairs={{0,1},{1,2},{2,3},{4,5},{5,6},{6,7},{8,9},{9,10},{10,11},{12,13},{... | collective-permute-start | bytes 98312 | tf_op jit(solution)/shard_map/ppermute | solution.py:16
  114.2 1.2 copy.169
  115.4 10.4 %all-to-all-start = ((f32[32,2,2048]{2,1,0:T(2,128)}), f32[32,2,2048]{2,1,0:T(2,128)S(1)}, u32[]{:S(2)}, u32[]{:S(2)}) async-start(f32[32,2,2048]{2,1,0:T(2,128)} %bitcast.124), calls=%async_computation | async-start | bytes 1048576 | tf_op jit(solution)/shard_map/all_to_all | solution.py:173
  125.8 2.0 %collective-permute-start.19 = (f32[1,1,1,8,8,128]{5,3,4,2,1,0:T(8,128)S(1)}, f32[1,1,1,8,8,128]{5,3,4,2,1,0:T(8,128)S(1)}, u32[]{:S(2)}, u32[]{:S(2)}) collective-permute-start(f32[1,1,1,8,8,128]{5,3,4,2,1,0:T(8,128)S(1)} %get-tuple-element.21), channel_id=1, source_target_pairs={{1,0},{2,1},{3,2},{5,4},{6,5},{7,6},{9,8},{10,9},{11,10},{13,12},{... | collective-permute-start | bytes 98312 | tf_op jit(solution)/shard_map/ppermute | solution.py:19
  129.8 10.8 %all-to-all-done = f32[32,2,2048]{2,1,0:T(2,128)S(1)} async-done(((f32[32,2,2048]{2,1,0:T(2,128)}), f32[32,2,2048]{2,1,0:T(2,128)S(1)}, u32[]{:S(2)}, u32[]{:S(2)}) %all-to-all-start) | async-done | bytes 524320 | tf_op jit(solution)/shard_map/all_to_all | solution.py:173
  141.4 3.6 %all-to-all-start.1 = ((f32[8,2,2048]{2,1,0:T(2,128)}), f32[8,2,2048]{2,1,0:T(2,128)S(1)}, u32[]{:S(2)}, u32[]{:S(2)}) async-start(f32[8,2,2048]{2,1,0:T(2,128)} %broadcast_in_dim.185), calls=%async_computation.1 | async-start | bytes 262144 | tf_op jit(solution)/shard_map/all_to_all | solution.py:175
  145.8 6.7 %all-to-all-done.1 = f32[8,2,2048]{2,1,0:T(2,128)S(1)} async-done(((f32[8,2,2048]{2,1,0:T(2,128)}), f32[8,2,2048]{2,1,0:T(2,128)S(1)}, u32[]{:S(2)}, u32[]{:S(2)}) %all-to-all-start.1) | async-done | bytes 131104 | tf_op jit(solution)/shard_map/all_to_all | solution.py:175
  (129 shorter events, 18.6 us)
Async XLA Ops:
  6.2 5.3 %collective-permute-start = (f32[2,1,1,8,8,128]{5,0,4,3,2,1:T(2,128)S(1)}, f32[2,1,1,8,8,128]{5,0,4,3,2,1:T(2,128)S(1)}, u32[]{:S(2)}, u32[]{:S(2)}) collective-permute-start(f32[2,1,1,8,8,128]{5,0,4,3,2,1:T(2,128)S(1)} %maximum_bitcast_fusion.6), channel_id=1, source_target_pairs={{0,4},{4,8},{8,12},{12,16},{16,20},{20,24},{24,28},{1,5},{5,9},{9,... | collective-permute-start | bytes 196616 | tf_op jit(solution)/shard_map/ppermute | solution.py:16
  12.4 6.5 %collective-permute-start.1 = (f32[2,1,1,8,8,128]{5,0,4,3,2,1:T(2,128)S(1)}, f32[2,1,1,8,8,128]{5,0,4,3,2,1:T(2,128)S(1)}, u32[]{:S(2)}, u32[]{:S(2)}) collective-permute-start(f32[2,1,1,8,8,128]{5,0,4,3,2,1:T(2,128)S(1)} %get-tuple-element.39), channel_id=1, source_target_pairs={{4,0},{8,4},{12,8},{16,12},{20,16},{24,20},{28,24},{5,1},{9,5},{13... | collective-permute-start | bytes 196616 | tf_op jit(solution)/shard_map/ppermute | solution.py:19
  15.0 13.8 %copy-start = (f32[8,8,1,1]{1,0,3,2:T(8,128)S(1)}, f32[8,8,1,1]{1,0,3,2:T(8,128)}, u32[]{:S(2)}) copy-start(f32[8,8,1,1]{1,0,3,2:T(8,128)} %constant.132) | copy-start | bytes 772
  15.2 14.4 %copy-start.5 = (f32[8]{0:T(128)S(1)}, f32[8]{0:T(128)}, u32[]{:S(2)}) copy-start(f32[8]{0:T(128)} %constant.91.clone) | copy-start | bytes 100
  18.9 5.6 %collective-permute-start.2 = (f32[2,1,1,8,8,128]{5,3,0,4,2,1:T(8,128)S(1)}, f32[2,1,1,8,8,128]{5,3,0,4,2,1:T(8,128)S(1)}, u32[]{:S(2)}, u32[]{:S(2)}) collective-permute-start(f32[2,1,1,8,8,128]{5,3,0,4,2,1:T(8,128)S(1)} %maximum_bitcast_fusion.4), channel_id=1, source_target_pairs={{0,1},{1,2},{2,3},{4,5},{5,6},{6,7},{8,9},{9,10},{10,11},{12,13},{... | collective-permute-start | bytes 196616 | tf_op jit(solution)/shard_map/ppermute | solution.py:16
  24.6 3.8 %collective-permute-start.3 = (f32[2,1,1,8,8,128]{5,3,0,4,2,1:T(8,128)S(1)}, f32[2,1,1,8,8,128]{5,3,0,4,2,1:T(8,128)S(1)}, u32[]{:S(2)}, u32[]{:S(2)}) collective-permute-start(f32[2,1,1,8,8,128]{5,3,0,4,2,1:T(8,128)S(1)} %get-tuple-element.37), channel_id=1, source_target_pairs={{1,0},{2,1},{3,2},{5,4},{6,5},{7,6},{9,8},{10,9},{11,10},{13,12},{... | collective-permute-start | bytes 196616 | tf_op jit(solution)/shard_map/ppermute | solution.py:19
  29.6 26.6 %copy-start.2 = (s32[1,4096,1]{1,2,0:T(1,128)S(1)}, s32[1,4096,1]{1,2,0:T(1,128)}, u32[]{:S(2)}) copy-start(s32[1,4096,1]{1,2,0:T(1,128)} %param.11) | copy-start | bytes 49156
  30.3 29.4 %copy-start.3 = (s32[1,4096]{1,0:T(1,128)S(1)}, s32[1,4096]{1,0:T(1,128)}, u32[]{:S(2)}) copy-start(s32[1,4096]{1,0:T(1,128)} %param.12) | copy-start | bytes 49156
  30.3 34.7 %copy-start.1 = (s32[1,4096]{1,0:T(1,128)S(1)}, s32[1,4096]{1,0:T(1,128)}, u32[]{:S(2)}) copy-start(s32[1,4096]{1,0:T(1,128)} %param.10) | copy-start | bytes 49156
  30.4 6.8 %collective-permute-start.5 = (f32[1,1,1,8,8,128]{5,4,3,2,1,0:T(8,128)S(1)}, f32[1,1,1,8,8,128]{5,4,3,2,1,0:T(8,128)S(1)}, u32[]{:S(2)}, u32[]{:S(2)}) collective-permute-start(f32[1,1,1,8,8,128]{5,4,3,2,1,0:T(8,128)S(1)} %bitcast.510), channel_id=1, source_target_pairs={{4,0},{8,4},{12,8},{16,12},{20,16},{24,20},{28,24},{5,1},{9,5},{13... | collective-permute-start | bytes 98312 | tf_op jit(solution)/shard_map/ppermute | solution.py:19
  31.7 7.0 %collective-permute-start.4 = (f32[1,1,1,8,8,128]{5,4,3,2,1,0:T(8,128)S(1)}, f32[1,1,1,8,8,128]{5,4,3,2,1,0:T(8,128)S(1)}, u32[]{:S(2)}, u32[]{:S(2)}) collective-permute-start(f32[1,1,1,8,8,128]{5,4,3,2,1,0:T(8,128)S(1)} %bitcast.516), channel_id=1, source_target_pairs={{0,4},{4,8},{8,12},{12,16},{16,20},{20,24},{24,28},{1,5},{5,9},{9,... | collective-permute-start | bytes 98312 | tf_op jit(solution)/shard_map/ppermute | solution.py:16
  38.7 5.2 %collective-permute-start.6 = (f32[1,1,1,8,8,128]{5,3,4,2,1,0:T(8,128)S(1)}, f32[1,1,1,8,8,128]{5,3,4,2,1,0:T(8,128)S(1)}, u32[]{:S(2)}, u32[]{:S(2)}) collective-permute-start(f32[1,1,1,8,8,128]{5,3,4,2,1,0:T(8,128)S(1)} %maximum_bitcast_fusion.14), channel_id=1, source_target_pairs={{0,1},{1,2},{2,3},{4,5},{5,6},{6,7},{8,9},{9,10},{10,11},{12,13},{... | collective-permute-start | bytes 98312 | tf_op jit(solution)/shard_map/ppermute | solution.py:16
  44.0 3.5 %collective-permute-start.7 = (f32[1,1,1,8,8,128]{5,3,4,2,1,0:T(8,128)S(1)}, f32[1,1,1,8,8,128]{5,3,4,2,1,0:T(8,128)S(1)}, u32[]{:S(2)}, u32[]{:S(2)}) collective-permute-start(f32[1,1,1,8,8,128]{5,3,4,2,1,0:T(8,128)S(1)} %get-tuple-element.33), channel_id=1, source_target_pairs={{1,0},{2,1},{3,2},{5,4},{6,5},{7,6},{9,8},{10,9},{11,10},{13,12},{... | collective-permute-start | bytes 98312 | tf_op jit(solution)/shard_map/ppermute | solution.py:19
  49.4 6.8 %collective-permute-start.9 = (f32[1,1,1,8,8,128]{5,4,3,2,1,0:T(8,128)S(1)}, f32[1,1,1,8,8,128]{5,4,3,2,1,0:T(8,128)S(1)}, u32[]{:S(2)}, u32[]{:S(2)}) collective-permute-start(f32[1,1,1,8,8,128]{5,4,3,2,1,0:T(8,128)S(1)} %bitcast.508), channel_id=1, source_target_pairs={{4,0},{8,4},{12,8},{16,12},{20,16},{24,20},{28,24},{5,1},{9,5},{13... | collective-permute-start | bytes 98312 | tf_op jit(solution)/shard_map/ppermute | solution.py:19
  50.7 7.0 %collective-permute-start.8 = (f32[1,1,1,8,8,128]{5,4,3,2,1,0:T(8,128)S(1)}, f32[1,1,1,8,8,128]{5,4,3,2,1,0:T(8,128)S(1)}, u32[]{:S(2)}, u32[]{:S(2)}) collective-permute-start(f32[1,1,1,8,8,128]{5,4,3,2,1,0:T(8,128)S(1)} %bitcast.514), channel_id=1, source_target_pairs={{0,4},{4,8},{8,12},{12,16},{16,20},{20,24},{24,28},{1,5},{5,9},{9,... | collective-permute-start | bytes 98312 | tf_op jit(solution)/shard_map/ppermute | solution.py:16
  57.8 5.2 %collective-permute-start.10 = (f32[1,1,1,8,8,128]{5,3,4,2,1,0:T(8,128)S(1)}, f32[1,1,1,8,8,128]{5,3,4,2,1,0:T(8,128)S(1)}, u32[]{:S(2)}, u32[]{:S(2)}) collective-permute-start(f32[1,1,1,8,8,128]{5,3,4,2,1,0:T(8,128)S(1)} %maximum_bitcast_fusion.12), channel_id=1, source_target_pairs={{0,1},{1,2},{2,3},{4,5},{5,6},{6,7},{8,9},{9,10},{10,11},{12,13},{... | collective-permute-start | bytes 98312 | tf_op jit(solution)/shard_map/ppermute | solution.py:16
  63.0 3.5 %collective-permute-start.11 = (f32[1,1,1,8,8,128]{5,3,4,2,1,0:T(8,128)S(1)}, f32[1,1,1,8,8,128]{5,3,4,2,1,0:T(8,128)S(1)}, u32[]{:S(2)}, u32[]{:S(2)}) collective-permute-start(f32[1,1,1,8,8,128]{5,3,4,2,1,0:T(8,128)S(1)} %get-tuple-element.31), channel_id=1, source_target_pairs={{1,0},{2,1},{3,2},{5,4},{6,5},{7,6},{9,8},{10,9},{11,10},{13,12},{... | collective-permute-start | bytes 98312 | tf_op jit(solution)/shard_map/ppermute | solution.py:19
  68.6 7.3 %collective-permute-start.13 = (f32[1,1,1,8,8,128]{5,4,3,2,1,0:T(8,128)S(1)}, f32[1,1,1,8,8,128]{5,4,3,2,1,0:T(8,128)S(1)}, u32[]{:S(2)}, u32[]{:S(2)}) collective-permute-start(f32[1,1,1,8,8,128]{5,4,3,2,1,0:T(8,128)S(1)} %bitcast.504), channel_id=1, source_target_pairs={{4,0},{8,4},{12,8},{16,12},{20,16},{24,20},{28,24},{5,1},{9,5},{13... | collective-permute-start | bytes 98312 | tf_op jit(solution)/shard_map/ppermute | solution.py:19
  69.9 7.3 %collective-permute-start.12 = (f32[1,1,1,8,8,128]{5,4,3,2,1,0:T(8,128)S(1)}, f32[1,1,1,8,8,128]{5,4,3,2,1,0:T(8,128)S(1)}, u32[]{:S(2)}, u32[]{:S(2)}) collective-permute-start(f32[1,1,1,8,8,128]{5,4,3,2,1,0:T(8,128)S(1)} %bitcast.506), channel_id=1, source_target_pairs={{0,4},{4,8},{8,12},{12,16},{16,20},{20,24},{24,28},{1,5},{5,9},{9,... | collective-permute-start | bytes 98312 | tf_op jit(solution)/shard_map/ppermute | solution.py:16
  77.3 5.2 %collective-permute-start.14 = (f32[1,1,1,8,8,128]{5,3,4,2,1,0:T(8,128)S(1)}, f32[1,1,1,8,8,128]{5,3,4,2,1,0:T(8,128)S(1)}, u32[]{:S(2)}, u32[]{:S(2)}) collective-permute-start(f32[1,1,1,8,8,128]{5,3,4,2,1,0:T(8,128)S(1)} %maximum_bitcast_fusion.10), channel_id=1, source_target_pairs={{0,1},{1,2},{2,3},{4,5},{5,6},{6,7},{8,9},{9,10},{10,11},{12,13},{... | collective-permute-start | bytes 98312 | tf_op jit(solution)/shard_map/ppermute | solution.py:16
  82.5 4.0 %collective-permute-start.15 = (f32[1,1,1,8,8,128]{5,3,4,2,1,0:T(8,128)S(1)}, f32[1,1,1,8,8,128]{5,3,4,2,1,0:T(8,128)S(1)}, u32[]{:S(2)}, u32[]{:S(2)}) collective-permute-start(f32[1,1,1,8,8,128]{5,3,4,2,1,0:T(8,128)S(1)} %get-tuple-element.29), channel_id=1, source_target_pairs={{1,0},{2,1},{3,2},{5,4},{6,5},{7,6},{9,8},{10,9},{11,10},{13,12},{... | collective-permute-start | bytes 98312 | tf_op jit(solution)/shard_map/ppermute | solution.py:19
  90.1 1.4 copy-start.4
  103.3 7.1 %collective-permute-start.17 = (f32[1,1,1,8,8,128]{5,4,3,2,1,0:T(8,128)S(1)}, f32[1,1,1,8,8,128]{5,4,3,2,1,0:T(8,128)S(1)}, u32[]{:S(2)}, u32[]{:S(2)}) collective-permute-start(f32[1,1,1,8,8,128]{5,4,3,2,1,0:T(8,128)S(1)} %bitcast.512), channel_id=1, source_target_pairs={{4,0},{8,4},{12,8},{16,12},{20,16},{24,20},{28,24},{5,1},{9,5},{13... | collective-permute-start | bytes 98312 | tf_op jit(solution)/shard_map/ppermute | solution.py:19
  104.6 7.3 %collective-permute-start.16 = (f32[1,1,1,8,8,128]{5,4,3,2,1,0:T(8,128)S(1)}, f32[1,1,1,8,8,128]{5,4,3,2,1,0:T(8,128)S(1)}, u32[]{:S(2)}, u32[]{:S(2)}) collective-permute-start(f32[1,1,1,8,8,128]{5,4,3,2,1,0:T(8,128)S(1)} %bitcast.518), channel_id=1, source_target_pairs={{0,4},{4,8},{8,12},{12,16},{16,20},{20,24},{24,28},{1,5},{5,9},{9,... | collective-permute-start | bytes 98312 | tf_op jit(solution)/shard_map/ppermute | solution.py:16
  112.0 13.8 %collective-permute-start.18 = (f32[1,1,1,8,8,128]{5,3,4,2,1,0:T(8,128)S(1)}, f32[1,1,1,8,8,128]{5,3,4,2,1,0:T(8,128)S(1)}, u32[]{:S(2)}, u32[]{:S(2)}) collective-permute-start(f32[1,1,1,8,8,128]{5,3,4,2,1,0:T(8,128)S(1)} %maximum_bitcast_fusion.8), channel_id=1, source_target_pairs={{0,1},{1,2},{2,3},{4,5},{5,6},{6,7},{8,9},{9,10},{10,11},{12,13},{... | collective-permute-start | bytes 98312 | tf_op jit(solution)/shard_map/ppermute | solution.py:16
  115.4 25.1 %all-to-all-start = ((f32[32,2,2048]{2,1,0:T(2,128)}), f32[32,2,2048]{2,1,0:T(2,128)S(1)}, u32[]{:S(2)}, u32[]{:S(2)}) async-start(f32[32,2,2048]{2,1,0:T(2,128)} %bitcast.124), calls=%async_computation | async-start | bytes 1048576 | tf_op jit(solution)/shard_map/all_to_all | solution.py:173
  125.8 3.6 %collective-permute-start.19 = (f32[1,1,1,8,8,128]{5,3,4,2,1,0:T(8,128)S(1)}, f32[1,1,1,8,8,128]{5,3,4,2,1,0:T(8,128)S(1)}, u32[]{:S(2)}, u32[]{:S(2)}) collective-permute-start(f32[1,1,1,8,8,128]{5,3,4,2,1,0:T(8,128)S(1)} %get-tuple-element.21), channel_id=1, source_target_pairs={{1,0},{2,1},{3,2},{5,4},{6,5},{7,6},{9,8},{10,9},{11,10},{13,12},{... | collective-permute-start | bytes 98312 | tf_op jit(solution)/shard_map/ppermute | solution.py:19
  141.4 11.1 %all-to-all-start.1 = ((f32[8,2,2048]{2,1,0:T(2,128)}), f32[8,2,2048]{2,1,0:T(2,128)S(1)}, u32[]{:S(2)}, u32[]{:S(2)}) async-start(f32[8,2,2048]{2,1,0:T(2,128)} %broadcast_in_dim.185), calls=%async_computation.1 | async-start | bytes 262144 | tf_op jit(solution)/shard_map/all_to_all | solution.py:175

commit v5 on v4

--- a/solution.py
+++ b/solution.py
@@ -203,10 +203,11 @@
             samples = early + gather_flat(update.reshape(-1), picks, 256)
             numer = segment_sum(areas * samples, global_ids, strips * SHELL_STRIP, 256)
             partial = jnp.stack([numer, denom])
-            applied, partial = lax.optimization_barrier((applied, partial))
         assembled = assemble(applied[None])[0]
         if step + 2 == SWEEPS:
             assembled, early = lax.optimization_barrier((assembled, early))
+        if step == 0:
+            assembled, denom = lax.optimization_barrier((assembled, denom))
         resid = resid - assembled
         if step + 1 < SWEEPS:
             rho_new = 1.0 / (2.0 * sigma - rho_now)

time: 156 us -> 152 us (0.974)
  starting transfers between devices: 66.2 us -> 58.4 us
  other arithmetic: 16.5 us -> 21.5 us
    ppermute x10, waiting for transfers between devices: 19.2 us -> 9.79 us  [padded_2(): lax.ppermute(lax.slice_in_dim(block, block.shape[dim] - width, None, axis...]
    ppermute x10, waiting for transfers between devices: 9.4 us -> 18.8 us  [padded_2(): lax.ppermute(lax.slice_in_dim(block, 0, width, axis=dim), axis, backward)]
    ppermute x10, starting transfers between devices: 35.4 us -> 29.9 us  [padded_2(): lax.ppermute(lax.slice_in_dim(block, block.shape[dim] - width, None, axis...]
    all_to_all x1, starting transfers between devices: 10.4 us -> 6.8 us  [strip_totals(): mine = lax.all_to_all(chunks, ('ex', 'ey'), 0, 0, tiled=True).sum(0)]
    mul x1 -> x2, other arithmetic: 4.8 us -> 7.28 us  [segment_sum(): hit_lane * part[:, None]]
  transfers between devices with their start and end apart: 22 -> 22, of which waited for: 16 -> 18; matrix products, arithmetic and copies ran while one was open for 6% -> 15% of each run, Pallas kernels for 0% -> 0%
where the time goes in v5:
time: 152 us; the launch traced here: 149 us
  starting transfers between devices  58.4 us (38%)
  waiting for transfers between devices  46.2 us (30%)
  other arithmetic  21.5 us (14%)
  matrix products  14.7 us (10%)
  local copies, waits for them, and re-layouts  6.58 us (4%)
  between operations  1.57 us (1%)
    ppermute x10, starting transfers between devices, padded_2(): lax.ppermute(lax.slice_in_dim(block, block.shape[dim] - width, None, axis...  29.9 us
    ppermute x10, waiting for transfers between devices, padded_2(): lax.ppermute(lax.slice_in_dim(block, 0, width, axis=dim), axis, backward)  18.8 us
    ppermute x10, starting transfers between devices, padded_2(): lax.ppermute(lax.slice_in_dim(block, 0, width, axis=dim), axis, backward)  18 us
    all_to_all x1, waiting for transfers between devices, strip_totals(): mine = lax.all_to_all(chunks, ('ex', 'ey'), 0, 0, tiled=True).sum(0)  10.8 us
    ppermute x10, waiting for transfers between devices, padded_2(): lax.ppermute(lax.slice_in_dim(block, block.shape[dim] - width, None, axis...  9.79 us
    mul x2, other arithmetic, segment_sum(): hit_lane * part[:, None]  7.28 us
    all_to_all x1, starting transfers between devices, strip_totals(): mine = lax.all_to_all(chunks, ('ex', 'ey'), 0, 0, tiled=True).sum(0)  6.8 us
    all_to_all x1, waiting for transfers between devices, strip_totals(): whole = lax.all_to_all(spread_out, 'ex', 0, 0, tiled=True)  6.72 us
  transfers between devices with their start and end apart: 22, of which 18 were waited for; matrix products, arithmetic and copies ran while one was open for 15% of the time, Pallas kernels for 0%

profile of v5, /device:TPU:2, one launch (start us, length us, event | category | flops | bytes accessed | tf_op | source)
XLA Modules:
  0.0 148.9 jit_solution(927745201880002431)
XLA Ops:
  1.4 1.3 gather_fusion
  4.2 1.1 fusion.93
  6.1 3.4 %collective-permute-start = (f32[2,1,1,8,8,128]{5,0,4,3,2,1:T(2,128)S(1)}, f32[2,1,1,8,8,128]{5,0,4,3,2,1:T(2,128)S(1)}, u32[]{:S(2)}, u32[]{:S(2)}) collective-permute-start(f32[2,1,1,8,8,128]{5,0,4,3,2,1:T(2,128)S(1)} %maximum_bitcast_fusion.9), channel_id=1, source_target_pairs={{0,4},{4,8},{8,12},{12,16},{16,20},{20,24},{24,28},{1,5},{5,9},{9,... | collective-permute-start | bytes 196616 | tf_op jit(solution)/shard_map/ppermute | solution.py:16
  11.5 0.8 fusion.116
  12.3 1.3 collective-permute-start.1
  13.6 1.3 pad_maximum_fusion.5
  15.2 3.7 %collective-permute-done.1 = f32[2,1,1,8,8,128]{5,0,4,3,2,1:T(2,128)S(1)} collective-permute-done((f32[2,1,1,8,8,128]{5,0,4,3,2,1:T(2,128)S(1)}, f32[2,1,1,8,8,128]{5,0,4,3,2,1:T(2,128)S(1)}, u32[]{:S(2)}, u32[]{:S(2)}) %collective-permute-start.1) | collective-permute-done | bytes 65568 | tf_op jit(solution)/shard_map/ppermute | solution.py:19
  18.9 1.9 %collective-permute-start.2 = (f32[2,1,1,8,8,128]{5,3,0,4,2,1:T(8,128)S(1)}, f32[2,1,1,8,8,128]{5,3,0,4,2,1:T(8,128)S(1)}, u32[]{:S(2)}, u32[]{:S(2)}) collective-permute-start(f32[2,1,1,8,8,128]{5,3,0,4,2,1:T(8,128)S(1)} %maximum_bitcast_fusion.7), channel_id=1, source_target_pairs={{0,1},{1,2},{2,3},{4,5},{5,6},{6,7},{8,9},{9,10},{10,11},{12,13},{... | collective-permute-start | bytes 196616 | tf_op jit(solution)/shard_map/ppermute | solution.py:16
  20.9 3.6 %collective-permute-done.2 = f32[2,1,1,8,8,128]{5,3,0,4,2,1:T(8,128)S(1)} collective-permute-done((f32[2,1,1,8,8,128]{5,3,0,4,2,1:T(8,128)S(1)}, f32[2,1,1,8,8,128]{5,3,0,4,2,1:T(8,128)S(1)}, u32[]{:S(2)}, u32[]{:S(2)}) %collective-permute-start.2) | collective-permute-done | bytes 65568 | tf_op jit(solution)/shard_map/ppermute | solution.py:16
  24.5 1.9 %collective-permute-start.3 = (f32[2,1,1,8,8,128]{5,3,0,4,2,1:T(8,128)S(1)}, f32[2,1,1,8,8,128]{5,3,0,4,2,1:T(8,128)S(1)}, u32[]{:S(2)}, u32[]{:S(2)}) collective-permute-start(f32[2,1,1,8,8,128]{5,3,0,4,2,1:T(8,128)S(1)} %get-tuple-element.39), channel_id=1, source_target_pairs={{1,0},{2,1},{3,2},{5,4},{6,5},{7,6},{9,8},{10,9},{11,10},{13,12},{... | collective-permute-start | bytes 196616 | tf_op jit(solution)/shard_map/ppermute | solution.py:19
  26.9 1.5 collective-permute-done.3
  30.1 0.9 fusion.33
  31.1 4.8 %collective-permute-start.4 = (f32[1,1,1,8,8,128]{5,4,3,2,1,0:T(8,128)S(1)}, f32[1,1,1,8,8,128]{5,4,3,2,1,0:T(8,128)S(1)}, u32[]{:S(2)}, u32[]{:S(2)}) collective-permute-start(f32[1,1,1,8,8,128]{5,4,3,2,1,0:T(8,128)S(1)} %bitcast.477), channel_id=1, source_target_pairs={{0,4},{4,8},{8,12},{12,16},{16,20},{20,24},{24,28},{1,5},{5,9},{9,... | collective-permute-start | bytes 98312 | tf_op jit(solution)/shard_map/ppermute | solution.py:16
  35.9 1.3 collective-permute-start.5
  37.2 3.6 %fusion.23 = (bf16[4096,256]{1,0:T(8,128)(2,1)S(1)}, bf16[4096,256]{1,0:T(8,128)(2,1)S(1)}, bf16[4096,256]{1,0:T(8,128)(2,1)S(1)}) fusion(s32[4096]{0:T(1024)S(1)} %get-tuple-element.73, bf16[4096]{0:T(1024)(128)(2,1)S(1)} %get-tuple-element.84, bf16[4096]{0:T(1024)(128)(2,1)S(1)} %get-tuple-element.85, bf16[4096]{0:T(1024)(128)(2,1)S(1)} %get-tuple-element.86), kind=kLoop, calls=%fused_computation.31 | loop fusion | flops 4194304 | bytes 6332416 | tf_op jit(solution)/shard_map/mul | solution.py:157
  41.7 1.9 %collective-permute-start.6 = (f32[1,1,1,8,8,128]{5,3,4,2,1,0:T(8,128)S(1)}, f32[1,1,1,8,8,128]{5,3,4,2,1,0:T(8,128)S(1)}, u32[]{:S(2)}, u32[]{:S(2)}) collective-permute-start(f32[1,1,1,8,8,128]{5,3,4,2,1,0:T(8,128)S(1)} %maximum_bitcast_fusion.19), channel_id=1, source_target_pairs={{0,1},{1,2},{2,3},{4,5},{5,6},{6,7},{8,9},{9,10},{10,11},{12,13},{... | collective-permute-start | bytes 98312 | tf_op jit(solution)/shard_map/ppermute | solution.py:16
  43.6 2.6 %fusion = f32[256,768]{1,0:T(8,128)S(1)} fusion(bf16[4096,256]{1,0:T(8,128)(2,1)S(1)} %get-tuple-element.82, bf16[4096,256]{1,0:T(8,128)(2,1)S(1)} %get-tuple-element.83, bf16[4096,256]{1,0:T(8,128)(2,1)S(1)} %get-tuple-element.81, s32[4096]{0:T(1024)S(1)} %get-tuple-element.72), kind=kOutput, calls=%fused_computation.1 | convolution fusion | flops 1630535680 | bytes 7094272 | tf_op jit(solution)/shard_map/dot_general | solution.py:159
  47.0 2.9 %collective-permute-start.7 = (f32[1,1,1,8,8,128]{5,3,4,2,1,0:T(8,128)S(1)}, f32[1,1,1,8,8,128]{5,3,4,2,1,0:T(8,128)S(1)}, u32[]{:S(2)}, u32[]{:S(2)}) collective-permute-start(f32[1,1,1,8,8,128]{5,3,4,2,1,0:T(8,128)S(1)} %get-tuple-element.35), channel_id=1, source_target_pairs={{1,0},{2,1},{3,2},{5,4},{6,5},{7,6},{9,8},{10,9},{11,10},{13,12},{... | collective-permute-start | bytes 98312 | tf_op jit(solution)/shard_map/ppermute | solution.py:19
  50.1 1.4 collective-permute-done.7
  53.4 4.3 %collective-permute-start.8 = (f32[1,1,1,8,8,128]{5,4,3,2,1,0:T(8,128)S(1)}, f32[1,1,1,8,8,128]{5,4,3,2,1,0:T(8,128)S(1)}, u32[]{:S(2)}, u32[]{:S(2)}) collective-permute-start(f32[1,1,1,8,8,128]{5,4,3,2,1,0:T(8,128)S(1)} %get-tuple-element.64), channel_id=1, source_target_pairs={{0,4},{4,8},{8,12},{12,16},{16,20},{20,24},{24,28},{1,5},{5,9},{9,... | collective-permute-start | bytes 98312 | tf_op jit(solution)/shard_map/ppermute | solution.py:16
  57.7 1.3 collective-permute-start.9
  59.3 4.2 %collective-permute-done.9 = f32[1,1,1,8,8,128]{5,4,3,2,1,0:T(8,128)S(1)} collective-permute-done((f32[1,1,1,8,8,128]{5,4,3,2,1,0:T(8,128)S(1)}, f32[1,1,1,8,8,128]{5,4,3,2,1,0:T(8,128)S(1)}, u32[]{:S(2)}, u32[]{:S(2)}) %collective-permute-start.9) | collective-permute-done | bytes 32800 | tf_op jit(solution)/shard_map/ppermute | solution.py:19
  63.6 1.9 %collective-permute-start.10 = (f32[1,1,1,8,8,128]{5,4,3,2,1,0:T(8,128)S(1)}, f32[1,1,1,8,8,128]{5,4,3,2,1,0:T(8,128)S(1)}, u32[]{:S(2)}, u32[]{:S(2)}) collective-permute-start(f32[1,1,1,8,8,128]{5,4,3,2,1,0:T(8,128)S(1)} %maximum_bitcast_fusion.17), channel_id=1, source_target_pairs={{0,1},{1,2},{2,3},{4,5},{5,6},{6,7},{8,9},{9,10},{10,11},{12,13},{... | collective-permute-start | bytes 98312 | tf_op jit(solution)/shard_map/ppermute | solution.py:16
  65.5 3.3 %collective-permute-done.10 = f32[1,1,1,8,8,128]{5,4,3,2,1,0:T(8,128)S(1)} collective-permute-done((f32[1,1,1,8,8,128]{5,4,3,2,1,0:T(8,128)S(1)}, f32[1,1,1,8,8,128]{5,4,3,2,1,0:T(8,128)S(1)}, u32[]{:S(2)}, u32[]{:S(2)}) %collective-permute-start.10) | collective-permute-done | bytes 32800 | tf_op jit(solution)/shard_map/ppermute | solution.py:16
  68.8 2.1 %collective-permute-start.11 = (f32[1,1,1,8,8,128]{5,4,3,2,1,0:T(8,128)S(1)}, f32[1,1,1,8,8,128]{5,4,3,2,1,0:T(8,128)S(1)}, u32[]{:S(2)}, u32[]{:S(2)}) collective-permute-start(f32[1,1,1,8,8,128]{5,4,3,2,1,0:T(8,128)S(1)} %get-tuple-element.33), channel_id=1, source_target_pairs={{1,0},{2,1},{3,2},{5,4},{6,5},{7,6},{9,8},{10,9},{11,10},{13,12},{... | collective-permute-start | bytes 98312 | tf_op jit(solution)/shard_map/ppermute | solution.py:19
  71.0 1.3 collective-permute-done.11
  74.4 4.7 %collective-permute-start.12 = (f32[1,1,1,8,8,128]{5,4,3,2,1,0:T(8,128)S(1)}, f32[1,1,1,8,8,128]{5,4,3,2,1,0:T(8,128)S(1)}, u32[]{:S(2)}, u32[]{:S(2)}) collective-permute-start(f32[1,1,1,8,8,128]{5,4,3,2,1,0:T(8,128)S(1)} %get-tuple-element.58), channel_id=1, source_target_pairs={{0,4},{4,8},{8,12},{12,16},{16,20},{20,24},{24,28},{1,5},{5,9},{9,... | collective-permute-start | bytes 98312 | tf_op jit(solution)/shard_map/ppermute | solution.py:16
  79.1 1.3 collective-permute-start.13
  80.7 4.2 %collective-permute-done.13 = f32[1,1,1,8,8,128]{5,4,3,2,1,0:T(8,128)S(1)} collective-permute-done((f32[1,1,1,8,8,128]{5,4,3,2,1,0:T(8,128)S(1)}, f32[1,1,1,8,8,128]{5,4,3,2,1,0:T(8,128)S(1)}, u32[]{:S(2)}, u32[]{:S(2)}) %collective-permute-start.13) | collective-permute-done | bytes 32800 | tf_op jit(solution)/shard_map/ppermute | solution.py:19
  84.9 1.9 %collective-permute-start.14 = (f32[1,1,1,8,8,128]{5,4,3,2,1,0:T(8,128)S(1)}, f32[1,1,1,8,8,128]{5,4,3,2,1,0:T(8,128)S(1)}, u32[]{:S(2)}, u32[]{:S(2)}) collective-permute-start(f32[1,1,1,8,8,128]{5,4,3,2,1,0:T(8,128)S(1)} %maximum_bitcast_fusion.15), channel_id=1, source_target_pairs={{0,1},{1,2},{2,3},{4,5},{5,6},{6,7},{8,9},{9,10},{10,11},{12,13},{... | collective-permute-start | bytes 98312 | tf_op jit(solution)/shard_map/ppermute | solution.py:16
  86.9 2.0 %fusion.17 = f32[4096,768]{0,1:T(8,128)S(1)} fusion(s32[4096]{0:T(1024)S(1)} %get-tuple-element.80, bf16[256,256]{1,0:T(8,128)(2,1)S(1)} %get-tuple-element.52, bf16[256,256]{1,0:T(8,128)(2,1)S(1)} %get-tuple-element.53, bf16[256,256]{1,0:T(8,128)(2,1)S(1)} %get-tuple-element.51), kind=kOutput, calls=%fused_computation.23 | convolution fusion | flops 1612840960 | bytes 12992512 | tf_op jit(solution)/shard_map/dot_general | solution.py:148
  88.9 1.3 collective-permute-done.14
  90.2 2.4 %collective-permute-start.15 = (f32[1,1,1,8,8,128]{5,4,3,2,1,0:T(8,128)S(1)}, f32[1,1,1,8,8,128]{5,4,3,2,1,0:T(8,128)S(1)}, u32[]{:S(2)}, u32[]{:S(2)}) collective-permute-start(f32[1,1,1,8,8,128]{5,4,3,2,1,0:T(8,128)S(1)} %get-tuple-element.29), channel_id=1, source_target_pairs={{1,0},{2,1},{3,2},{5,4},{6,5},{7,6},{9,8},{10,9},{11,10},{13,12},{... | collective-permute-start | bytes 98312 | tf_op jit(solution)/shard_map/ppermute | solution.py:19
  92.5 1.4 fusion.15
  96.5 2.0 %fusion.16 = f32[4096,768]{0,1:T(8,128)S(1)} fusion(s32[4096]{0:T(1024)S(1)} %get-tuple-element.80, bf16[256,256]{1,0:T(8,128)(2,1)S(1)} %get-tuple-element.45, bf16[256,256]{1,0:T(8,128)(2,1)S(1)} %get-tuple-element.46, bf16[256,256]{1,0:T(8,128)(2,1)S(1)} %get-tuple-element.44), kind=kOutput, calls=%fused_computation.22 | convolution fusion | flops 1612840960 | bytes 12992512 | tf_op jit(solution)/shard_map/dot_general | solution.py:148
  98.5 1.4 fusion.13
  100.4 3.1 %collective-permute-start.16 = (f32[1,1,1,8,8,128]{5,4,3,2,1,0:T(8,128)S(1)}, f32[1,1,1,8,8,128]{5,4,3,2,1,0:T(8,128)S(1)}, u32[]{:S(2)}, u32[]{:S(2)}) collective-permute-start(f32[1,1,1,8,8,128]{5,4,3,2,1,0:T(8,128)S(1)} %get-tuple-element.49), channel_id=1, source_target_pairs={{0,4},{4,8},{8,12},{12,16},{16,20},{20,24},{24,28},{1,5},{5,9},{9,... | collective-permute-start | bytes 98312 | tf_op jit(solution)/shard_map/ppermute | solution.py:16
  103.4 1.5 %collective-permute-start.17 = (f32[1,1,1,8,8,128]{5,4,3,2,1,0:T(8,128)S(1)}, f32[1,1,1,8,8,128]{5,4,3,2,1,0:T(8,128)S(1)}, u32[]{:S(2)}, u32[]{:S(2)}) collective-permute-start(f32[1,1,1,8,8,128]{5,4,3,2,1,0:T(8,128)S(1)} %get-tuple-element.50), channel_id=1, source_target_pairs={{4,0},{8,4},{12,8},{16,12},{20,16},{24,20},{28,24},{5,1},{9,5},{13... | collective-permute-start | bytes 98312 | tf_op jit(solution)/shard_map/ppermute | solution.py:19
  105.0 3.6 %fusion.20 = (bf16[4096,256]{1,0:T(8,128)(2,1)S(1)}, bf16[4096,256]{1,0:T(8,128)(2,1)S(1)}, bf16[4096,256]{1,0:T(8,128)(2,1)S(1)}) fusion(s32[4096]{0:T(1024)S(1)} %get-tuple-element.73, bf16[4096]{0:T(1024)(128)(2,1)S(1)} %get-tuple-element.20, bf16[4096]{0:T(1024)(128)(2,1)S(1)} %get-tuple-element.78, bf16[4096]{0:T(1024)(128)(2,1)S(1)} %get-tuple-element.77), kind=kLoop, calls=%fused_computation.28 | loop fusion | flops 4194304 | bytes 6332416 | tf_op jit(solution)/shard_map/mul | solution.py:157
  108.6 2.6 %fusion.6 = f32[256,768]{1,0:T(8,128)S(1)} fusion(bf16[4096,256]{1,0:T(8,128)(2,1)S(1)} %get-tuple-element.75, bf16[4096,256]{1,0:T(8,128)(2,1)S(1)} %get-tuple-element.76, bf16[4096,256]{1,0:T(8,128)(2,1)S(1)} %get-tuple-element.74, s32[4096]{0:T(1024)S(1)} %get-tuple-element.72), kind=kOutput, calls=%fused_computation.7 | convolution fusion | flops 1630535680 | bytes 7094272 | tf_op jit(solution)/shard_map/dot_general | solution.py:159
  111.5 1.9 %collective-permute-start.18 = (f32[1,1,1,8,8,128]{5,3,4,2,1,0:T(8,128)S(1)}, f32[1,1,1,8,8,128]{5,3,4,2,1,0:T(8,128)S(1)}, u32[]{:S(2)}, u32[]{:S(2)}) collective-permute-start(f32[1,1,1,8,8,128]{5,3,4,2,1,0:T(8,128)S(1)} %maximum_bitcast_fusion.13), channel_id=1, source_target_pairs={{0,1},{1,2},{2,3},{4,5},{5,6},{6,7},{8,9},{9,10},{10,11},{12,13},{... | collective-permute-start | bytes 98312 | tf_op jit(solution)/shard_map/ppermute | solution.py:16
  113.5 1.2 copy.179
  114.7 6.8 %all-to-all-start = ((f32[32,2,2048]{2,1,0:T(2,128)}), f32[32,2,2048]{2,1,0:T(2,128)S(1)}, u32[]{:S(2)}, u32[]{:S(2)}) async-start(f32[32,2,2048]{2,1,0:T(2,128)} %bitcast.124), calls=%async_computation | async-start | bytes 1048576 | tf_op jit(solution)/shard_map/all_to_all | solution.py:173
  121.5 2.0 %collective-permute-start.19 = (f32[1,1,1,8,8,128]{5,3,4,2,1,0:T(8,128)S(1)}, f32[1,1,1,8,8,128]{5,3,4,2,1,0:T(8,128)S(1)}, u32[]{:S(2)}, u32[]{:S(2)}) collective-permute-start(f32[1,1,1,8,8,128]{5,3,4,2,1,0:T(8,128)S(1)} %get-tuple-element.25), channel_id=1, source_target_pairs={{1,0},{2,1},{3,2},{5,4},{6,5},{7,6},{9,8},{10,9},{11,10},{13,12},{... | collective-permute-start | bytes 98312 | tf_op jit(solution)/shard_map/ppermute | solution.py:19
  123.6 1.5 %collective-permute-done.19 = f32[1,1,1,8,8,128]{5,3,4,2,1,0:T(8,128)S(1)} collective-permute-done((f32[1,1,1,8,8,128]{5,3,4,2,1,0:T(8,128)S(1)}, f32[1,1,1,8,8,128]{5,3,4,2,1,0:T(8,128)S(1)}, u32[]{:S(2)}, u32[]{:S(2)}) %collective-permute-start.19) | collective-permute-done | bytes 32800 | tf_op jit(solution)/shard_map/ppermute | solution.py:19
  125.4 10.8 %all-to-all-done = f32[32,2,2048]{2,1,0:T(2,128)S(1)} async-done(((f32[32,2,2048]{2,1,0:T(2,128)}), f32[32,2,2048]{2,1,0:T(2,128)S(1)}, u32[]{:S(2)}, u32[]{:S(2)}) %all-to-all-start) | async-done | bytes 524320 | tf_op jit(solution)/shard_map/all_to_all | solution.py:173
  137.1 3.6 %all-to-all-start.1 = ((f32[8,2,2048]{2,1,0:T(2,128)}), f32[8,2,2048]{2,1,0:T(2,128)S(1)}, u32[]{:S(2)}, u32[]{:S(2)}) async-start(f32[8,2,2048]{2,1,0:T(2,128)} %broadcast_in_dim.185), calls=%async_computation.1 | async-start | bytes 262144 | tf_op jit(solution)/shard_map/all_to_all | solution.py:175
  141.5 6.7 %all-to-all-done.1 = f32[8,2,2048]{2,1,0:T(2,128)S(1)} async-done(((f32[8,2,2048]{2,1,0:T(2,128)}), f32[8,2,2048]{2,1,0:T(2,128)S(1)}, u32[]{:S(2)}, u32[]{:S(2)}) %all-to-all-start.1) | async-done | bytes 131104 | tf_op jit(solution)/shard_map/all_to_all | solution.py:175
  (129 shorter events, 19.5 us)
Async XLA Ops:
  0.6 20.2 %copy-start.1 = (f32[1,4096]{1,0:T(1,128)S(1)}, f32[1,4096]{1,0:T(1,128)}, u32[]{:S(2)}) copy-start(f32[1,4096]{1,0:T(1,128)} %param.13) | copy-start | bytes 49156
  6.1 5.3 %collective-permute-start = (f32[2,1,1,8,8,128]{5,0,4,3,2,1:T(2,128)S(1)}, f32[2,1,1,8,8,128]{5,0,4,3,2,1:T(2,128)S(1)}, u32[]{:S(2)}, u32[]{:S(2)}) collective-permute-start(f32[2,1,1,8,8,128]{5,0,4,3,2,1:T(2,128)S(1)} %maximum_bitcast_fusion.9), channel_id=1, source_target_pairs={{0,4},{4,8},{8,12},{12,16},{16,20},{20,24},{24,28},{1,5},{5,9},{9,... | collective-permute-start | bytes 196616 | tf_op jit(solution)/shard_map/ppermute | solution.py:16
  12.3 6.5 %collective-permute-start.1 = (f32[2,1,1,8,8,128]{5,0,4,3,2,1:T(2,128)S(1)}, f32[2,1,1,8,8,128]{5,0,4,3,2,1:T(2,128)S(1)}, u32[]{:S(2)}, u32[]{:S(2)}) collective-permute-start(f32[2,1,1,8,8,128]{5,0,4,3,2,1:T(2,128)S(1)} %get-tuple-element.41), channel_id=1, source_target_pairs={{4,0},{8,4},{12,8},{16,12},{20,16},{24,20},{28,24},{5,1},{9,5},{13... | collective-permute-start | bytes 196616 | tf_op jit(solution)/shard_map/ppermute | solution.py:19
  18.9 5.6 %collective-permute-start.2 = (f32[2,1,1,8,8,128]{5,3,0,4,2,1:T(8,128)S(1)}, f32[2,1,1,8,8,128]{5,3,0,4,2,1:T(8,128)S(1)}, u32[]{:S(2)}, u32[]{:S(2)}) collective-permute-start(f32[2,1,1,8,8,128]{5,3,0,4,2,1:T(8,128)S(1)} %maximum_bitcast_fusion.7), channel_id=1, source_target_pairs={{0,1},{1,2},{2,3},{4,5},{5,6},{6,7},{8,9},{9,10},{10,11},{12,13},{... | collective-permute-start | bytes 196616 | tf_op jit(solution)/shard_map/ppermute | solution.py:16
  24.5 4.7 %copy-start = (f32[8,8,1,1]{1,0,3,2:T(8,128)S(1)}, f32[8,8,1,1]{1,0,3,2:T(8,128)}, u32[]{:S(2)}) copy-start(f32[8,8,1,1]{1,0,3,2:T(8,128)} %constant.132) | copy-start | bytes 772
  24.5 3.8 %collective-permute-start.3 = (f32[2,1,1,8,8,128]{5,3,0,4,2,1:T(8,128)S(1)}, f32[2,1,1,8,8,128]{5,3,0,4,2,1:T(8,128)S(1)}, u32[]{:S(2)}, u32[]{:S(2)}) collective-permute-start(f32[2,1,1,8,8,128]{5,3,0,4,2,1:T(8,128)S(1)} %get-tuple-element.39), channel_id=1, source_target_pairs={{1,0},{2,1},{3,2},{5,4},{6,5},{7,6},{9,8},{10,9},{11,10},{13,12},{... | collective-permute-start | bytes 196616 | tf_op jit(solution)/shard_map/ppermute | solution.py:19
  26.6 3.3 %copy-start.2 = (f32[8]{0:T(128)S(1)}, f32[8]{0:T(128)}, u32[]{:S(2)}) copy-start(f32[8]{0:T(128)} %constant.91.clone) | copy-start | bytes 100
  31.1 9.8 %collective-permute-start.4 = (f32[1,1,1,8,8,128]{5,4,3,2,1,0:T(8,128)S(1)}, f32[1,1,1,8,8,128]{5,4,3,2,1,0:T(8,128)S(1)}, u32[]{:S(2)}, u32[]{:S(2)}) collective-permute-start(f32[1,1,1,8,8,128]{5,4,3,2,1,0:T(8,128)S(1)} %bitcast.477), channel_id=1, source_target_pairs={{0,4},{4,8},{8,12},{12,16},{16,20},{20,24},{24,28},{1,5},{5,9},{9,... | collective-permute-start | bytes 98312 | tf_op jit(solution)/shard_map/ppermute | solution.py:16
  35.9 5.8 %collective-permute-start.5 = (f32[1,1,1,8,8,128]{5,4,3,2,1,0:T(8,128)S(1)}, f32[1,1,1,8,8,128]{5,4,3,2,1,0:T(8,128)S(1)}, u32[]{:S(2)}, u32[]{:S(2)}) collective-permute-start(f32[1,1,1,8,8,128]{5,4,3,2,1,0:T(8,128)S(1)} %bitcast.479), channel_id=1, source_target_pairs={{4,0},{8,4},{12,8},{16,12},{20,16},{24,20},{28,24},{5,1},{9,5},{13... | collective-permute-start | bytes 98312 | tf_op jit(solution)/shard_map/ppermute | solution.py:19
  41.7 5.2 %collective-permute-start.6 = (f32[1,1,1,8,8,128]{5,3,4,2,1,0:T(8,128)S(1)}, f32[1,1,1,8,8,128]{5,3,4,2,1,0:T(8,128)S(1)}, u32[]{:S(2)}, u32[]{:S(2)}) collective-permute-start(f32[1,1,1,8,8,128]{5,3,4,2,1,0:T(8,128)S(1)} %maximum_bitcast_fusion.19), channel_id=1, source_target_pairs={{0,1},{1,2},{2,3},{4,5},{5,6},{6,7},{8,9},{9,10},{10,11},{12,13},{... | collective-permute-start | bytes 98312 | tf_op jit(solution)/shard_map/ppermute | solution.py:16
  47.0 4.5 %collective-permute-start.7 = (f32[1,1,1,8,8,128]{5,3,4,2,1,0:T(8,128)S(1)}, f32[1,1,1,8,8,128]{5,3,4,2,1,0:T(8,128)S(1)}, u32[]{:S(2)}, u32[]{:S(2)}) collective-permute-start(f32[1,1,1,8,8,128]{5,3,4,2,1,0:T(8,128)S(1)} %get-tuple-element.35), channel_id=1, source_target_pairs={{1,0},{2,1},{3,2},{5,4},{6,5},{7,6},{9,8},{10,9},{11,10},{13,12},{... | collective-permute-start | bytes 98312 | tf_op jit(solution)/shard_map/ppermute | solution.py:19
  50.0 20.9 %copy-start.3 = (s32[1,4096]{1,0:T(1,128)S(1)}, s32[1,4096]{1,0:T(1,128)}, u32[]{:S(2)}) copy-start(s32[1,4096]{1,0:T(1,128)} %param.10) | copy-start | bytes 49156
  53.4 5.9 %collective-permute-start.8 = (f32[1,1,1,8,8,128]{5,4,3,2,1,0:T(8,128)S(1)}, f32[1,1,1,8,8,128]{5,4,3,2,1,0:T(8,128)S(1)}, u32[]{:S(2)}, u32[]{:S(2)}) collective-permute-start(f32[1,1,1,8,8,128]{5,4,3,2,1,0:T(8,128)S(1)} %get-tuple-element.64), channel_id=1, source_target_pairs={{0,4},{4,8},{8,12},{12,16},{16,20},{20,24},{24,28},{1,5},{5,9},{9,... | collective-permute-start | bytes 98312 | tf_op jit(solution)/shard_map/ppermute | solution.py:16
  57.7 5.8 %collective-permute-start.9 = (f32[1,1,1,8,8,128]{5,4,3,2,1,0:T(8,128)S(1)}, f32[1,1,1,8,8,128]{5,4,3,2,1,0:T(8,128)S(1)}, u32[]{:S(2)}, u32[]{:S(2)}) collective-permute-start(f32[1,1,1,8,8,128]{5,4,3,2,1,0:T(8,128)S(1)} %get-tuple-element.65), channel_id=1, source_target_pairs={{4,0},{8,4},{12,8},{16,12},{20,16},{24,20},{28,24},{5,1},{9,5},{13... | collective-permute-start | bytes 98312 | tf_op jit(solution)/shard_map/ppermute | solution.py:19
  63.6 5.2 %collective-permute-start.10 = (f32[1,1,1,8,8,128]{5,4,3,2,1,0:T(8,128)S(1)}, f32[1,1,1,8,8,128]{5,4,3,2,1,0:T(8,128)S(1)}, u32[]{:S(2)}, u32[]{:S(2)}) collective-permute-start(f32[1,1,1,8,8,128]{5,4,3,2,1,0:T(8,128)S(1)} %maximum_bitcast_fusion.17), channel_id=1, source_target_pairs={{0,1},{1,2},{2,3},{4,5},{5,6},{6,7},{8,9},{9,10},{10,11},{12,13},{... | collective-permute-start | bytes 98312 | tf_op jit(solution)/shard_map/ppermute | solution.py:16
  68.8 3.5 %collective-permute-start.11 = (f32[1,1,1,8,8,128]{5,4,3,2,1,0:T(8,128)S(1)}, f32[1,1,1,8,8,128]{5,4,3,2,1,0:T(8,128)S(1)}, u32[]{:S(2)}, u32[]{:S(2)}) collective-permute-start(f32[1,1,1,8,8,128]{5,4,3,2,1,0:T(8,128)S(1)} %get-tuple-element.33), channel_id=1, source_target_pairs={{1,0},{2,1},{3,2},{5,4},{6,5},{7,6},{9,8},{10,9},{11,10},{13,12},{... | collective-permute-start | bytes 98312 | tf_op jit(solution)/shard_map/ppermute | solution.py:19
  74.4 6.3 %collective-permute-start.12 = (f32[1,1,1,8,8,128]{5,4,3,2,1,0:T(8,128)S(1)}, f32[1,1,1,8,8,128]{5,4,3,2,1,0:T(8,128)S(1)}, u32[]{:S(2)}, u32[]{:S(2)}) collective-permute-start(f32[1,1,1,8,8,128]{5,4,3,2,1,0:T(8,128)S(1)} %get-tuple-element.58), channel_id=1, source_target_pairs={{0,4},{4,8},{8,12},{12,16},{16,20},{20,24},{24,28},{1,5},{5,9},{9,... | collective-permute-start | bytes 98312 | tf_op jit(solution)/shard_map/ppermute | solution.py:16
  79.1 5.8 %collective-permute-start.13 = (f32[1,1,1,8,8,128]{5,4,3,2,1,0:T(8,128)S(1)}, f32[1,1,1,8,8,128]{5,4,3,2,1,0:T(8,128)S(1)}, u32[]{:S(2)}, u32[]{:S(2)}) collective-permute-start(f32[1,1,1,8,8,128]{5,4,3,2,1,0:T(8,128)S(1)} %get-tuple-element.59), channel_id=1, source_target_pairs={{4,0},{8,4},{12,8},{16,12},{20,16},{24,20},{28,24},{5,1},{9,5},{13... | collective-permute-start | bytes 98312 | tf_op jit(solution)/shard_map/ppermute | solution.py:19
  84.9 5.2 %collective-permute-start.14 = (f32[1,1,1,8,8,128]{5,4,3,2,1,0:T(8,128)S(1)}, f32[1,1,1,8,8,128]{5,4,3,2,1,0:T(8,128)S(1)}, u32[]{:S(2)}, u32[]{:S(2)}) collective-permute-start(f32[1,1,1,8,8,128]{5,4,3,2,1,0:T(8,128)S(1)} %maximum_bitcast_fusion.15), channel_id=1, source_target_pairs={{0,1},{1,2},{2,3},{4,5},{5,6},{6,7},{8,9},{9,10},{10,11},{12,13},{... | collective-permute-start | bytes 98312 | tf_op jit(solution)/shard_map/ppermute | solution.py:16
  90.2 4.0 %collective-permute-start.15 = (f32[1,1,1,8,8,128]{5,4,3,2,1,0:T(8,128)S(1)}, f32[1,1,1,8,8,128]{5,4,3,2,1,0:T(8,128)S(1)}, u32[]{:S(2)}, u32[]{:S(2)}) collective-permute-start(f32[1,1,1,8,8,128]{5,4,3,2,1,0:T(8,128)S(1)} %get-tuple-element.29), channel_id=1, source_target_pairs={{1,0},{2,1},{3,2},{5,4},{6,5},{7,6},{9,8},{10,9},{11,10},{13,12},{... | collective-permute-start | bytes 98312 | tf_op jit(solution)/shard_map/ppermute | solution.py:19
  100.4 11.1 %collective-permute-start.16 = (f32[1,1,1,8,8,128]{5,4,3,2,1,0:T(8,128)S(1)}, f32[1,1,1,8,8,128]{5,4,3,2,1,0:T(8,128)S(1)}, u32[]{:S(2)}, u32[]{:S(2)}) collective-permute-start(f32[1,1,1,8,8,128]{5,4,3,2,1,0:T(8,128)S(1)} %get-tuple-element.49), channel_id=1, source_target_pairs={{0,4},{4,8},{8,12},{12,16},{16,20},{20,24},{24,28},{1,5},{5,9},{9,... | collective-permute-start | bytes 98312 | tf_op jit(solution)/shard_map/ppermute | solution.py:16
  103.4 8.0 %collective-permute-start.17 = (f32[1,1,1,8,8,128]{5,4,3,2,1,0:T(8,128)S(1)}, f32[1,1,1,8,8,128]{5,4,3,2,1,0:T(8,128)S(1)}, u32[]{:S(2)}, u32[]{:S(2)}) collective-permute-start(f32[1,1,1,8,8,128]{5,4,3,2,1,0:T(8,128)S(1)} %get-tuple-element.50), channel_id=1, source_target_pairs={{4,0},{8,4},{12,8},{16,12},{20,16},{24,20},{28,24},{5,1},{9,5},{13... | collective-permute-start | bytes 98312 | tf_op jit(solution)/shard_map/ppermute | solution.py:19
  111.5 10.0 %collective-permute-start.18 = (f32[1,1,1,8,8,128]{5,3,4,2,1,0:T(8,128)S(1)}, f32[1,1,1,8,8,128]{5,3,4,2,1,0:T(8,128)S(1)}, u32[]{:S(2)}, u32[]{:S(2)}) collective-permute-start(f32[1,1,1,8,8,128]{5,3,4,2,1,0:T(8,128)S(1)} %maximum_bitcast_fusion.13), channel_id=1, source_target_pairs={{0,1},{1,2},{2,3},{4,5},{5,6},{6,7},{8,9},{9,10},{10,11},{12,13},{... | collective-permute-start | bytes 98312 | tf_op jit(solution)/shard_map/ppermute | solution.py:16
  114.7 21.5 %all-to-all-start = ((f32[32,2,2048]{2,1,0:T(2,128)}), f32[32,2,2048]{2,1,0:T(2,128)S(1)}, u32[]{:S(2)}, u32[]{:S(2)}) async-start(f32[32,2,2048]{2,1,0:T(2,128)} %bitcast.124), calls=%async_computation | async-start | bytes 1048576 | tf_op jit(solution)/shard_map/all_to_all | solution.py:173
  121.5 3.6 %collective-permute-start.19 = (f32[1,1,1,8,8,128]{5,3,4,2,1,0:T(8,128)S(1)}, f32[1,1,1,8,8,128]{5,3,4,2,1,0:T(8,128)S(1)}, u32[]{:S(2)}, u32[]{:S(2)}) collective-permute-start(f32[1,1,1,8,8,128]{5,3,4,2,1,0:T(8,128)S(1)} %get-tuple-element.25), channel_id=1, source_target_pairs={{1,0},{2,1},{3,2},{5,4},{6,5},{7,6},{9,8},{10,9},{11,10},{13,12},{... | collective-permute-start | bytes 98312 | tf_op jit(solution)/shard_map/ppermute | solution.py:19
  137.1 11.1 %all-to-all-start.1 = ((f32[8,2,2048]{2,1,0:T(2,128)}), f32[8,2,2048]{2,1,0:T(2,128)S(1)}, u32[]{:S(2)}, u32[]{:S(2)}) async-start(f32[8,2,2048]{2,1,0:T(2,128)} %broadcast_in_dim.185), calls=%async_computation.1 | async-start | bytes 262144 | tf_op jit(solution)/shard_map/all_to_all | solution.py:175

commit v6 on v5

--- a/solution.py
+++ b/solution.py
@@ -165,15 +165,16 @@
 def strip_totals(partial, strips, strip_size):
     n_ex = lax.axis_size("ex")
     piece = -(-strip_size // n_ex)
-    chunks = partial.reshape(2, strips, strip_size)
+    count = partial.shape[0]
+    chunks = partial.reshape(count, strips, strip_size)
     if piece * n_ex != strip_size:
         chunks = jnp.pad(chunks, ((0, 0), (0, 0), (0, piece * n_ex - strip_size)))
-    chunks = chunks.reshape(2, strips, n_ex, piece).transpose(2, 1, 0, 3)
-    chunks = chunks.reshape(n_ex * strips, 2, piece)
+    chunks = chunks.reshape(count, strips, n_ex, piece).transpose(2, 1, 0, 3)
+    chunks = chunks.reshape(n_ex * strips, count, piece)
     mine = lax.all_to_all(chunks, ("ex", "ey"), 0, 0, tiled=True).sum(0)
-    spread_out = jnp.broadcast_to(mine[None], (n_ex, 2, piece))
+    spread_out = jnp.broadcast_to(mine[None], (n_ex, count, piece))
     whole = lax.all_to_all(spread_out, "ex", 0, 0, tiled=True)
-    return whole.transpose(1, 0, 2).reshape(2, n_ex * piece)[:, :strip_size]
+    return whole.transpose(1, 0, 2).reshape(count, n_ex * piece)[:, :strip_size]
 
 
 def on_device(source, metric, fac_point, fac_strip, fac_shell, fac_area):
@@ -202,19 +203,19 @@
         if step + 1 == SWEEPS:
             samples = early + gather_flat(update.reshape(-1), picks, 256)
             numer = segment_sum(areas * samples, global_ids, strips * SHELL_STRIP, 256)
-            partial = jnp.stack([numer, denom])
         assembled = assemble(applied[None])[0]
         if step + 2 == SWEEPS:
             assembled, early = lax.optimization_barrier((assembled, early))
         if step == 0:
             assembled, denom = lax.optimization_barrier((assembled, denom))
+            denom_total = strip_totals(denom[None], strips, SHELL_STRIP)[0]
         resid = resid - assembled
         if step + 1 < SWEEPS:
             rho_new = 1.0 / (2.0 * sigma - rho_now)
             update = rho_new * rho_now * update + 2.0 * rho_new / delta * pinv * resid
             rho_now = rho_new
-    total = strip_totals(partial, strips, SHELL_STRIP)
-    shell_load = total[0] / jnp.maximum(total[1], 1.0)
+    numer_total = strip_totals(numer[None], strips, SHELL_STRIP)[0]
+    shell_load = numer_total / jnp.maximum(denom_total, 1.0)
     return (pressure, resid, shell_load)
 
 

time: 152 us -> 166 us (1.092)
  the two profiles are of different devices: /device:TPU:2 before, /device:TPU:0 now
where the time goes in v6:
time: 166 us; the launch traced here: 165 us
  starting transfers between devices  72.8 us (44%)
  waiting for transfers between devices  46.2 us (28%)
  other arithmetic  21.7 us (13%)
  matrix products  14.7 us (9%)
  local copies, waits for them, and re-layouts  7.97 us (5%)
    ppermute x10, starting transfers between devices, padded_2(): lax.ppermute(lax.slice_in_dim(block, block.shape[dim] - width, None, axis...  36.3 us
    ppermute x10, waiting for transfers between devices, padded_2(): lax.ppermute(lax.slice_in_dim(block, 0, width, axis=dim), axis, backward)  20.8 us
    all_to_all x2, starting transfers between devices, strip_totals(): mine = lax.all_to_all(chunks, ('ex', 'ey'), 0, 0, tiled=True).sum(0)  16.7 us
    ppermute x10, starting transfers between devices, padded_2(): lax.ppermute(lax.slice_in_dim(block, 0, width, axis=dim), axis, backward)  13.1 us
    all_to_all x2, waiting for transfers between devices, strip_totals(): whole = lax.all_to_all(spread_out, 'ex', 0, 0, tiled=True)  12.7 us
    all_to_all x2, waiting for transfers between devices, strip_totals(): mine = lax.all_to_all(chunks, ('ex', 'ey'), 0, 0, tiled=True).sum(0)  10.2 us
    mul x2, other arithmetic, segment_sum(): hit_lane * part[:, None]  7.28 us
    all_to_all x2, starting transfers between devices, strip_totals(): whole = lax.all_to_all(spread_out, 'ex', 0, 0, tiled=True)  6.7 us
  transfers between devices with their start and end apart: 24, of which 15 were waited for; matrix products, arithmetic and copies ran while one was open for 19% of the time, Pallas kernels for 0%

profile of v6, /device:TPU:0, one launch (start us, length us, event | category | flops | bytes accessed | tf_op | source)
XLA Modules:
  0.0 164.9 jit_solution(14827737539627890240)
XLA Ops:
  1.4 1.3 gather_fusion
  4.2 1.1 fusion.93
  6.1 4.9 %collective-permute-start = (f32[2,1,1,8,8,128]{5,0,4,3,2,1:T(2,128)S(1)}, f32[2,1,1,8,8,128]{5,0,4,3,2,1:T(2,128)S(1)}, u32[]{:S(2)}, u32[]{:S(2)}) collective-permute-start(f32[2,1,1,8,8,128]{5,0,4,3,2,1:T(2,128)S(1)} %maximum_bitcast_fusion.8), channel_id=1, source_target_pairs={{0,4},{4,8},{8,12},{12,16},{16,20},{20,24},{24,28},{1,5},{5,9},{9,... | collective-permute-start | bytes 196616 | tf_op jit(solution)/shard_map/ppermute | solution.py:16
  13.8 1.3 collective-permute-start.1
  15.1 1.3 pad_maximum_fusion.5
  16.6 3.7 %collective-permute-done.1 = f32[2,1,1,8,8,128]{5,0,4,3,2,1:T(2,128)S(1)} collective-permute-done((f32[2,1,1,8,8,128]{5,0,4,3,2,1:T(2,128)S(1)}, f32[2,1,1,8,8,128]{5,0,4,3,2,1:T(2,128)S(1)}, u32[]{:S(2)}, u32[]{:S(2)}) %collective-permute-start.1) | collective-permute-done | bytes 65568 | tf_op jit(solution)/shard_map/ppermute | solution.py:19
  20.3 1.3 collective-permute-start.2
  21.7 0.9 collective-permute-done.2
  22.6 1.3 collective-permute-start.3
  24.3 3.6 %collective-permute-done.3 = f32[2,1,1,8,8,128]{5,3,0,4,2,1:T(8,128)S(1)} collective-permute-done((f32[2,1,1,8,8,128]{5,3,0,4,2,1:T(8,128)S(1)}, f32[2,1,1,8,8,128]{5,3,0,4,2,1:T(8,128)S(1)}, u32[]{:S(2)}, u32[]{:S(2)}) %collective-permute-start.3) | collective-permute-done | bytes 65568 | tf_op jit(solution)/shard_map/ppermute | solution.py:19
  29.6 0.9 fusion.33
  30.6 4.8 %collective-permute-start.4 = (f32[1,1,1,8,8,128]{5,4,3,2,1,0:T(8,128)S(1)}, f32[1,1,1,8,8,128]{5,4,3,2,1,0:T(8,128)S(1)}, u32[]{:S(2)}, u32[]{:S(2)}) collective-permute-start(f32[1,1,1,8,8,128]{5,4,3,2,1,0:T(8,128)S(1)} %bitcast.478), channel_id=1, source_target_pairs={{0,4},{4,8},{8,12},{12,16},{16,20},{20,24},{24,28},{1,5},{5,9},{9,... | collective-permute-start | bytes 98312 | tf_op jit(solution)/shard_map/ppermute | solution.py:16
  35.4 1.3 collective-permute-start.5
  36.7 3.6 %fusion.23 = (bf16[4096,256]{1,0:T(8,128)(2,1)S(1)}, bf16[4096,256]{1,0:T(8,128)(2,1)S(1)}, bf16[4096,256]{1,0:T(8,128)(2,1)S(1)}) fusion(s32[4096]{0:T(1024)S(1)} %get-tuple-element.73, bf16[4096]{0:T(1024)(128)(2,1)S(1)} %get-tuple-element.84, bf16[4096]{0:T(1024)(128)(2,1)S(1)} %get-tuple-element.85, bf16[4096]{0:T(1024)(128)(2,1)S(1)} %get-tuple-element.86), kind=kLoop, calls=%fused_computation.31 | loop fusion | flops 4194304 | bytes 6332416 | tf_op jit(solution)/shard_map/mul | solution.py:157
  41.3 4.4 %collective-permute-start.6 = (f32[1,1,1,8,8,128]{5,3,4,2,1,0:T(8,128)S(1)}, f32[1,1,1,8,8,128]{5,3,4,2,1,0:T(8,128)S(1)}, u32[]{:S(2)}, u32[]{:S(2)}) collective-permute-start(f32[1,1,1,8,8,128]{5,3,4,2,1,0:T(8,128)S(1)} %maximum_bitcast_fusion.18), channel_id=1, source_target_pairs={{0,1},{1,2},{2,3},{4,5},{5,6},{6,7},{8,9},{9,10},{10,11},{12,13},{... | collective-permute-start | bytes 98312 | tf_op jit(solution)/shard_map/ppermute | solution.py:16
  45.7 2.6 %fusion = f32[256,768]{1,0:T(8,128)S(1)} fusion(bf16[4096,256]{1,0:T(8,128)(2,1)S(1)} %get-tuple-element.82, bf16[4096,256]{1,0:T(8,128)(2,1)S(1)} %get-tuple-element.83, bf16[4096,256]{1,0:T(8,128)(2,1)S(1)} %get-tuple-element.81, s32[4096]{0:T(1024)S(1)} %get-tuple-element.72), kind=kOutput, calls=%fused_computation.1 | convolution fusion | flops 1630535680 | bytes 7094272 | tf_op jit(solution)/shard_map/dot_general | solution.py:159
  48.3 1.3 collective-permute-start.7
  49.8 2.1 %collective-permute-done.7 = f32[1,1,1,8,8,128]{5,3,4,2,1,0:T(8,128)S(1)} collective-permute-done((f32[1,1,1,8,8,128]{5,3,4,2,1,0:T(8,128)S(1)}, f32[1,1,1,8,8,128]{5,3,4,2,1,0:T(8,128)S(1)}, u32[]{:S(2)}, u32[]{:S(2)}) %collective-permute-start.7) | collective-permute-done | bytes 32800 | tf_op jit(solution)/shard_map/ppermute | solution.py:19
  53.8 4.3 %collective-permute-start.8 = (f32[1,1,1,8,8,128]{5,4,3,2,1,0:T(8,128)S(1)}, f32[1,1,1,8,8,128]{5,4,3,2,1,0:T(8,128)S(1)}, u32[]{:S(2)}, u32[]{:S(2)}) collective-permute-start(f32[1,1,1,8,8,128]{5,4,3,2,1,0:T(8,128)S(1)} %get-tuple-element.64), channel_id=1, source_target_pairs={{0,4},{4,8},{8,12},{12,16},{16,20},{20,24},{24,28},{1,5},{5,9},{9,... | collective-permute-start | bytes 98312 | tf_op jit(solution)/shard_map/ppermute | solution.py:16
  58.2 1.3 collective-permute-start.9
  59.7 4.2 %collective-permute-done.9 = f32[1,1,1,8,8,128]{5,4,3,2,1,0:T(8,128)S(1)} collective-permute-done((f32[1,1,1,8,8,128]{5,4,3,2,1,0:T(8,128)S(1)}, f32[1,1,1,8,8,128]{5,4,3,2,1,0:T(8,128)S(1)}, u32[]{:S(2)}, u32[]{:S(2)}) %collective-permute-start.9) | collective-permute-done | bytes 32800 | tf_op jit(solution)/shard_map/ppermute | solution.py:19
  64.0 3.2 %collective-permute-start.10 = (f32[1,1,1,8,8,128]{5,4,3,2,1,0:T(8,128)S(1)}, f32[1,1,1,8,8,128]{5,4,3,2,1,0:T(8,128)S(1)}, u32[]{:S(2)}, u32[]{:S(2)}) collective-permute-start(f32[1,1,1,8,8,128]{5,4,3,2,1,0:T(8,128)S(1)} %maximum_bitcast_fusion.16), channel_id=1, source_target_pairs={{0,1},{1,2},{2,3},{4,5},{5,6},{6,7},{8,9},{9,10},{10,11},{12,13},{... | collective-permute-start | bytes 98312 | tf_op jit(solution)/shard_map/ppermute | solution.py:16
  68.1 1.3 collective-permute-start.11
  69.5 1.0 copy.180
  70.4 9.2 %all-to-all-start.2 = ((f32[32,1,2048]{2,1,0:T(1,128)}), f32[32,1,2048]{2,1,0:T(1,128)S(1)}, u32[]{:S(2)}, u32[]{:S(2)}) async-start(f32[32,1,2048]{2,1,0:T(1,128)} %bitcast.126), calls=%async_computation.2 | async-start | bytes 524288 | tf_op jit(solution)/shard_map/all_to_all | solution.py:174
  81.7 3.5 %collective-permute-start.12 = (f32[1,1,1,8,8,128]{5,4,3,2,1,0:T(8,128)S(1)}, f32[1,1,1,8,8,128]{5,4,3,2,1,0:T(8,128)S(1)}, u32[]{:S(2)}, u32[]{:S(2)}) collective-permute-start(f32[1,1,1,8,8,128]{5,4,3,2,1,0:T(8,128)S(1)} %get-tuple-element.58), channel_id=1, source_target_pairs={{0,4},{4,8},{8,12},{12,16},{16,20},{20,24},{24,28},{1,5},{5,9},{9,... | collective-permute-start | bytes 98312 | tf_op jit(solution)/shard_map/ppermute | solution.py:16
  85.2 1.3 collective-permute-start.13
  86.8 4.2 %collective-permute-done.13 = f32[1,1,1,8,8,128]{5,4,3,2,1,0:T(8,128)S(1)} collective-permute-done((f32[1,1,1,8,8,128]{5,4,3,2,1,0:T(8,128)S(1)}, f32[1,1,1,8,8,128]{5,4,3,2,1,0:T(8,128)S(1)}, u32[]{:S(2)}, u32[]{:S(2)}) %collective-permute-start.13) | collective-permute-done | bytes 32800 | tf_op jit(solution)/shard_map/ppermute | solution.py:19
  91.1 1.3 collective-permute-start.14
  92.4 2.0 %fusion.17 = f32[4096,768]{0,1:T(8,128)S(1)} fusion(s32[4096]{0:T(1024)S(1)} %get-tuple-element.80, bf16[256,256]{1,0:T(8,128)(2,1)S(1)} %get-tuple-element.52, bf16[256,256]{1,0:T(8,128)(2,1)S(1)} %get-tuple-element.53, bf16[256,256]{1,0:T(8,128)(2,1)S(1)} %get-tuple-element.51), kind=kOutput, calls=%fused_computation.23 | convolution fusion | flops 1612840960 | bytes 12992512 | tf_op jit(solution)/shard_map/dot_general | solution.py:148
  94.4 1.3 collective-permute-start.15
  95.7 1.4 fusion.15
  97.1 2.1 %collective-permute-done.15 = f32[1,1,1,8,8,128]{5,4,3,2,1,0:T(8,128)S(1)} collective-permute-done((f32[1,1,1,8,8,128]{5,4,3,2,1,0:T(8,128)S(1)}, f32[1,1,1,8,8,128]{5,4,3,2,1,0:T(8,128)S(1)}, u32[]{:S(2)}, u32[]{:S(2)}) %collective-permute-start.15) | collective-permute-done | bytes 32800 | tf_op jit(solution)/shard_map/ppermute | solution.py:19
  101.6 2.0 %fusion.16 = f32[4096,768]{0,1:T(8,128)S(1)} fusion(s32[4096]{0:T(1024)S(1)} %get-tuple-element.80, bf16[256,256]{1,0:T(8,128)(2,1)S(1)} %get-tuple-element.45, bf16[256,256]{1,0:T(8,128)(2,1)S(1)} %get-tuple-element.46, bf16[256,256]{1,0:T(8,128)(2,1)S(1)} %get-tuple-element.44), kind=kOutput, calls=%fused_computation.22 | convolution fusion | flops 1612840960 | bytes 12992512 | tf_op jit(solution)/shard_map/dot_general | solution.py:148
  103.6 1.4 fusion.13
  105.4 4.3 %collective-permute-start.16 = (f32[1,1,1,8,8,128]{5,4,3,2,1,0:T(8,128)S(1)}, f32[1,1,1,8,8,128]{5,4,3,2,1,0:T(8,128)S(1)}, u32[]{:S(2)}, u32[]{:S(2)}) collective-permute-start(f32[1,1,1,8,8,128]{5,4,3,2,1,0:T(8,128)S(1)} %get-tuple-element.49), channel_id=1, source_target_pairs={{0,4},{4,8},{8,12},{12,16},{16,20},{20,24},{24,28},{1,5},{5,9},{9,... | collective-permute-start | bytes 98312 | tf_op jit(solution)/shard_map/ppermute | solution.py:16
  109.7 1.5 collective-permute-start.17
  111.3 3.6 %fusion.20 = (bf16[4096,256]{1,0:T(8,128)(2,1)S(1)}, bf16[4096,256]{1,0:T(8,128)(2,1)S(1)}, bf16[4096,256]{1,0:T(8,128)(2,1)S(1)}) fusion(s32[4096]{0:T(1024)S(1)} %get-tuple-element.73, bf16[4096]{0:T(1024)(128)(2,1)S(1)} %get-tuple-element.20, bf16[4096]{0:T(1024)(128)(2,1)S(1)} %get-tuple-element.78, bf16[4096]{0:T(1024)(128)(2,1)S(1)} %get-tuple-element.77), kind=kLoop, calls=%fused_computation.28 | loop fusion | flops 4194304 | bytes 6332416 | tf_op jit(solution)/shard_map/mul | solution.py:157
  114.9 2.6 %fusion.6 = f32[256,768]{1,0:T(8,128)S(1)} fusion(bf16[4096,256]{1,0:T(8,128)(2,1)S(1)} %get-tuple-element.75, bf16[4096,256]{1,0:T(8,128)(2,1)S(1)} %get-tuple-element.76, bf16[4096,256]{1,0:T(8,128)(2,1)S(1)} %get-tuple-element.74, s32[4096]{0:T(1024)S(1)} %get-tuple-element.72), kind=kOutput, calls=%fused_computation.7 | convolution fusion | flops 1630535680 | bytes 7094272 | tf_op jit(solution)/shard_map/dot_general | solution.py:159
  117.7 4.3 %collective-permute-start.18 = (f32[1,1,1,8,8,128]{5,3,4,2,1,0:T(8,128)S(1)}, f32[1,1,1,8,8,128]{5,3,4,2,1,0:T(8,128)S(1)}, u32[]{:S(2)}, u32[]{:S(2)}) collective-permute-start(f32[1,1,1,8,8,128]{5,3,4,2,1,0:T(8,128)S(1)} %maximum_bitcast_fusion.12), channel_id=1, source_target_pairs={{0,1},{1,2},{2,3},{4,5},{5,6},{6,7},{8,9},{9,10},{10,11},{12,13},{... | collective-permute-start | bytes 98312 | tf_op jit(solution)/shard_map/ppermute | solution.py:16
  122.1 1.0 copy.179
  123.1 1.3 collective-permute-start.19
  124.4 7.5 %all-to-all-start = ((f32[32,1,2048]{2,1,0:T(1,128)}), f32[32,1,2048]{2,1,0:T(1,128)S(1)}, u32[]{:S(2)}, u32[]{:S(2)}) async-start(f32[32,1,2048]{2,1,0:T(1,128)} %bitcast.124), calls=%async_computation | async-start | bytes 524288 | tf_op jit(solution)/shard_map/all_to_all | solution.py:174
  132.3 10.2 %all-to-all-done = f32[32,1,2048]{2,1,0:T(1,128)S(1)} async-done(((f32[32,1,2048]{2,1,0:T(1,128)}), f32[32,1,2048]{2,1,0:T(1,128)S(1)}, u32[]{:S(2)}, u32[]{:S(2)}) %all-to-all-start) | async-done | bytes 262176 | tf_op jit(solution)/shard_map/all_to_all | solution.py:174
  143.1 3.4 %all-to-all-start.3 = ((f32[8,1,2048]{2,1,0:T(1,128)}), f32[8,1,2048]{2,1,0:T(1,128)S(1)}, u32[]{:S(2)}, u32[]{:S(2)}) async-start(f32[8,1,2048]{2,1,0:T(1,128)} %broadcast_in_dim.192), calls=%async_computation.3 | async-start | bytes 131072 | tf_op jit(solution)/shard_map/all_to_all | solution.py:176
  146.7 6.7 %all-to-all-done.3 = f32[8,1,2048]{2,1,0:T(1,128)S(1)} async-done(((f32[8,1,2048]{2,1,0:T(1,128)}), f32[8,1,2048]{2,1,0:T(1,128)S(1)}, u32[]{:S(2)}, u32[]{:S(2)}) %all-to-all-start.3) | async-done | bytes 65568 | tf_op jit(solution)/shard_map/all_to_all | solution.py:176
  154.0 3.4 %all-to-all-start.1 = ((f32[8,1,2048]{2,1,0:T(1,128)}), f32[8,1,2048]{2,1,0:T(1,128)S(1)}, u32[]{:S(2)}, u32[]{:S(2)}) async-start(f32[8,1,2048]{2,1,0:T(1,128)} %broadcast_in_dim.191), calls=%async_computation.1 | async-start | bytes 131072 | tf_op jit(solution)/shard_map/all_to_all | solution.py:176
  158.2 6.1 %all-to-all-done.1 = f32[8,1,2048]{2,1,0:T(1,128)S(1)} async-done(((f32[8,1,2048]{2,1,0:T(1,128)}), f32[8,1,2048]{2,1,0:T(1,128)S(1)}, u32[]{:S(2)}, u32[]{:S(2)}) %all-to-all-start.1) | async-done | bytes 65568 | tf_op jit(solution)/shard_map/all_to_all | solution.py:176
  (135 shorter events, 21.0 us)
Async XLA Ops:
  0.6 21.0 %copy-start.1 = (f32[1,4096]{1,0:T(1,128)S(1)}, f32[1,4096]{1,0:T(1,128)}, u32[]{:S(2)}) copy-start(f32[1,4096]{1,0:T(1,128)} %param.13) | copy-start | bytes 49156
  6.1 6.8 %collective-permute-start = (f32[2,1,1,8,8,128]{5,0,4,3,2,1:T(2,128)S(1)}, f32[2,1,1,8,8,128]{5,0,4,3,2,1:T(2,128)S(1)}, u32[]{:S(2)}, u32[]{:S(2)}) collective-permute-start(f32[2,1,1,8,8,128]{5,0,4,3,2,1:T(2,128)S(1)} %maximum_bitcast_fusion.8), channel_id=1, source_target_pairs={{0,4},{4,8},{8,12},{12,16},{16,20},{20,24},{24,28},{1,5},{5,9},{9,... | collective-permute-start | bytes 196616 | tf_op jit(solution)/shard_map/ppermute | solution.py:16
  13.8 6.5 %collective-permute-start.1 = (f32[2,1,1,8,8,128]{5,0,4,3,2,1:T(2,128)S(1)}, f32[2,1,1,8,8,128]{5,0,4,3,2,1:T(2,128)S(1)}, u32[]{:S(2)}, u32[]{:S(2)}) collective-permute-start(f32[2,1,1,8,8,128]{5,0,4,3,2,1:T(2,128)S(1)} %get-tuple-element.41), channel_id=1, source_target_pairs={{4,0},{8,4},{12,8},{16,12},{20,16},{24,20},{28,24},{5,1},{9,5},{13... | collective-permute-start | bytes 196616 | tf_op jit(solution)/shard_map/ppermute | solution.py:19
  20.3 2.2 %collective-permute-start.2 = (f32[2,1,1,8,8,128]{5,3,0,4,2,1:T(8,128)S(1)}, f32[2,1,1,8,8,128]{5,3,0,4,2,1:T(8,128)S(1)}, u32[]{:S(2)}, u32[]{:S(2)}) collective-permute-start(f32[2,1,1,8,8,128]{5,3,0,4,2,1:T(8,128)S(1)} %maximum_bitcast_fusion.6), channel_id=1, source_target_pairs={{0,1},{1,2},{2,3},{4,5},{5,6},{6,7},{8,9},{9,10},{10,11},{12,13},{... | collective-permute-start | bytes 196616 | tf_op jit(solution)/shard_map/ppermute | solution.py:16
  22.6 6.2 %copy-start = (f32[8,8,1,1]{1,0,3,2:T(8,128)S(1)}, f32[8,8,1,1]{1,0,3,2:T(8,128)}, u32[]{:S(2)}) copy-start(f32[8,8,1,1]{1,0,3,2:T(8,128)} %constant.132) | copy-start | bytes 772
  22.6 5.3 %collective-permute-start.3 = (f32[2,1,1,8,8,128]{5,3,0,4,2,1:T(8,128)S(1)}, f32[2,1,1,8,8,128]{5,3,0,4,2,1:T(8,128)S(1)}, u32[]{:S(2)}, u32[]{:S(2)}) collective-permute-start(f32[2,1,1,8,8,128]{5,3,0,4,2,1:T(8,128)S(1)} %get-tuple-element.39), channel_id=1, source_target_pairs={{1,0},{2,1},{3,2},{5,4},{6,5},{7,6},{9,8},{10,9},{11,10},{13,12},{... | collective-permute-start | bytes 196616 | tf_op jit(solution)/shard_map/ppermute | solution.py:19
  24.0 5.5 %copy-start.2 = (f32[8]{0:T(128)S(1)}, f32[8]{0:T(128)}, u32[]{:S(2)}) copy-start(f32[8]{0:T(128)} %constant.91.clone) | copy-start | bytes 100
  30.6 9.8 %collective-permute-start.4 = (f32[1,1,1,8,8,128]{5,4,3,2,1,0:T(8,128)S(1)}, f32[1,1,1,8,8,128]{5,4,3,2,1,0:T(8,128)S(1)}, u32[]{:S(2)}, u32[]{:S(2)}) collective-permute-start(f32[1,1,1,8,8,128]{5,4,3,2,1,0:T(8,128)S(1)} %bitcast.478), channel_id=1, source_target_pairs={{0,4},{4,8},{8,12},{12,16},{16,20},{20,24},{24,28},{1,5},{5,9},{9,... | collective-permute-start | bytes 98312 | tf_op jit(solution)/shard_map/ppermute | solution.py:16
  35.4 5.8 %collective-permute-start.5 = (f32[1,1,1,8,8,128]{5,4,3,2,1,0:T(8,128)S(1)}, f32[1,1,1,8,8,128]{5,4,3,2,1,0:T(8,128)S(1)}, u32[]{:S(2)}, u32[]{:S(2)}) collective-permute-start(f32[1,1,1,8,8,128]{5,4,3,2,1,0:T(8,128)S(1)} %bitcast.480), channel_id=1, source_target_pairs={{4,0},{8,4},{12,8},{16,12},{20,16},{24,20},{28,24},{5,1},{9,5},{13... | collective-permute-start | bytes 98312 | tf_op jit(solution)/shard_map/ppermute | solution.py:19
  41.3 7.0 %collective-permute-start.6 = (f32[1,1,1,8,8,128]{5,3,4,2,1,0:T(8,128)S(1)}, f32[1,1,1,8,8,128]{5,3,4,2,1,0:T(8,128)S(1)}, u32[]{:S(2)}, u32[]{:S(2)}) collective-permute-start(f32[1,1,1,8,8,128]{5,3,4,2,1,0:T(8,128)S(1)} %maximum_bitcast_fusion.18), channel_id=1, source_target_pairs={{0,1},{1,2},{2,3},{4,5},{5,6},{6,7},{8,9},{9,10},{10,11},{12,13},{... | collective-permute-start | bytes 98312 | tf_op jit(solution)/shard_map/ppermute | solution.py:16
  48.3 3.6 %collective-permute-start.7 = (f32[1,1,1,8,8,128]{5,3,4,2,1,0:T(8,128)S(1)}, f32[1,1,1,8,8,128]{5,3,4,2,1,0:T(8,128)S(1)}, u32[]{:S(2)}, u32[]{:S(2)}) collective-permute-start(f32[1,1,1,8,8,128]{5,3,4,2,1,0:T(8,128)S(1)} %get-tuple-element.35), channel_id=1, source_target_pairs={{1,0},{2,1},{3,2},{5,4},{6,5},{7,6},{9,8},{10,9},{11,10},{13,12},{... | collective-permute-start | bytes 98312 | tf_op jit(solution)/shard_map/ppermute | solution.py:19
  49.7 19.7 %copy-start.3 = (s32[1,4096]{1,0:T(1,128)S(1)}, s32[1,4096]{1,0:T(1,128)}, u32[]{:S(2)}) copy-start(s32[1,4096]{1,0:T(1,128)} %param.10) | copy-start | bytes 49156
  53.8 5.9 %collective-permute-start.8 = (f32[1,1,1,8,8,128]{5,4,3,2,1,0:T(8,128)S(1)}, f32[1,1,1,8,8,128]{5,4,3,2,1,0:T(8,128)S(1)}, u32[]{:S(2)}, u32[]{:S(2)}) collective-permute-start(f32[1,1,1,8,8,128]{5,4,3,2,1,0:T(8,128)S(1)} %get-tuple-element.64), channel_id=1, source_target_pairs={{0,4},{4,8},{8,12},{12,16},{16,20},{20,24},{24,28},{1,5},{5,9},{9,... | collective-permute-start | bytes 98312 | tf_op jit(solution)/shard_map/ppermute | solution.py:16
  58.2 5.8 %collective-permute-start.9 = (f32[1,1,1,8,8,128]{5,4,3,2,1,0:T(8,128)S(1)}, f32[1,1,1,8,8,128]{5,4,3,2,1,0:T(8,128)S(1)}, u32[]{:S(2)}, u32[]{:S(2)}) collective-permute-start(f32[1,1,1,8,8,128]{5,4,3,2,1,0:T(8,128)S(1)} %get-tuple-element.65), channel_id=1, source_target_pairs={{4,0},{8,4},{12,8},{16,12},{20,16},{24,20},{28,24},{5,1},{9,5},{13... | collective-permute-start | bytes 98312 | tf_op jit(solution)/shard_map/ppermute | solution.py:19
  64.0 4.1 %collective-permute-start.10 = (f32[1,1,1,8,8,128]{5,4,3,2,1,0:T(8,128)S(1)}, f32[1,1,1,8,8,128]{5,4,3,2,1,0:T(8,128)S(1)}, u32[]{:S(2)}, u32[]{:S(2)}) collective-permute-start(f32[1,1,1,8,8,128]{5,4,3,2,1,0:T(8,128)S(1)} %maximum_bitcast_fusion.16), channel_id=1, source_target_pairs={{0,1},{1,2},{2,3},{4,5},{5,6},{6,7},{8,9},{9,10},{10,11},{12,13},{... | collective-permute-start | bytes 98312 | tf_op jit(solution)/shard_map/ppermute | solution.py:16
  68.1 11.5 %collective-permute-start.11 = (f32[1,1,1,8,8,128]{5,4,3,2,1,0:T(8,128)S(1)}, f32[1,1,1,8,8,128]{5,4,3,2,1,0:T(8,128)S(1)}, u32[]{:S(2)}, u32[]{:S(2)}) collective-permute-start(f32[1,1,1,8,8,128]{5,4,3,2,1,0:T(8,128)S(1)} %get-tuple-element.33), channel_id=1, source_target_pairs={{1,0},{2,1},{3,2},{5,4},{6,5},{7,6},{9,8},{10,9},{11,10},{13,12},{... | collective-permute-start | bytes 98312 | tf_op jit(solution)/shard_map/ppermute | solution.py:19
  70.4 54.0 %all-to-all-start.2 = ((f32[32,1,2048]{2,1,0:T(1,128)}), f32[32,1,2048]{2,1,0:T(1,128)S(1)}, u32[]{:S(2)}, u32[]{:S(2)}) async-start(f32[32,1,2048]{2,1,0:T(1,128)} %bitcast.126), calls=%async_computation.2 | async-start | bytes 524288 | tf_op jit(solution)/shard_map/all_to_all | solution.py:174
  81.7 5.1 %collective-permute-start.12 = (f32[1,1,1,8,8,128]{5,4,3,2,1,0:T(8,128)S(1)}, f32[1,1,1,8,8,128]{5,4,3,2,1,0:T(8,128)S(1)}, u32[]{:S(2)}, u32[]{:S(2)}) collective-permute-start(f32[1,1,1,8,8,128]{5,4,3,2,1,0:T(8,128)S(1)} %get-tuple-element.58), channel_id=1, source_target_pairs={{0,4},{4,8},{8,12},{12,16},{16,20},{20,24},{24,28},{1,5},{5,9},{9,... | collective-permute-start | bytes 98312 | tf_op jit(solution)/shard_map/ppermute | solution.py:16
  85.2 5.8 %collective-permute-start.13 = (f32[1,1,1,8,8,128]{5,4,3,2,1,0:T(8,128)S(1)}, f32[1,1,1,8,8,128]{5,4,3,2,1,0:T(8,128)S(1)}, u32[]{:S(2)}, u32[]{:S(2)}) collective-permute-start(f32[1,1,1,8,8,128]{5,4,3,2,1,0:T(8,128)S(1)} %get-tuple-element.59), channel_id=1, source_target_pairs={{4,0},{8,4},{12,8},{16,12},{20,16},{24,20},{28,24},{5,1},{9,5},{13... | collective-permute-start | bytes 98312 | tf_op jit(solution)/shard_map/ppermute | solution.py:19
  91.1 3.3 %collective-permute-start.14 = (f32[1,1,1,8,8,128]{5,4,3,2,1,0:T(8,128)S(1)}, f32[1,1,1,8,8,128]{5,4,3,2,1,0:T(8,128)S(1)}, u32[]{:S(2)}, u32[]{:S(2)}) collective-permute-start(f32[1,1,1,8,8,128]{5,4,3,2,1,0:T(8,128)S(1)} %maximum_bitcast_fusion.14), channel_id=1, source_target_pairs={{0,1},{1,2},{2,3},{4,5},{5,6},{6,7},{8,9},{9,10},{10,11},{12,13},{... | collective-permute-start | bytes 98312 | tf_op jit(solution)/shard_map/ppermute | solution.py:16
  94.4 4.8 %collective-permute-start.15 = (f32[1,1,1,8,8,128]{5,4,3,2,1,0:T(8,128)S(1)}, f32[1,1,1,8,8,128]{5,4,3,2,1,0:T(8,128)S(1)}, u32[]{:S(2)}, u32[]{:S(2)}) collective-permute-start(f32[1,1,1,8,8,128]{5,4,3,2,1,0:T(8,128)S(1)} %get-tuple-element.29), channel_id=1, source_target_pairs={{1,0},{2,1},{3,2},{5,4},{6,5},{7,6},{9,8},{10,9},{11,10},{13,12},{... | collective-permute-start | bytes 98312 | tf_op jit(solution)/shard_map/ppermute | solution.py:19
  105.4 12.2 %collective-permute-start.16 = (f32[1,1,1,8,8,128]{5,4,3,2,1,0:T(8,128)S(1)}, f32[1,1,1,8,8,128]{5,4,3,2,1,0:T(8,128)S(1)}, u32[]{:S(2)}, u32[]{:S(2)}) collective-permute-start(f32[1,1,1,8,8,128]{5,4,3,2,1,0:T(8,128)S(1)} %get-tuple-element.49), channel_id=1, source_target_pairs={{0,4},{4,8},{8,12},{12,16},{16,20},{20,24},{24,28},{1,5},{5,9},{9,... | collective-permute-start | bytes 98312 | tf_op jit(solution)/shard_map/ppermute | solution.py:16
  109.7 7.9 %collective-permute-start.17 = (f32[1,1,1,8,8,128]{5,4,3,2,1,0:T(8,128)S(1)}, f32[1,1,1,8,8,128]{5,4,3,2,1,0:T(8,128)S(1)}, u32[]{:S(2)}, u32[]{:S(2)}) collective-permute-start(f32[1,1,1,8,8,128]{5,4,3,2,1,0:T(8,128)S(1)} %get-tuple-element.50), channel_id=1, source_target_pairs={{4,0},{8,4},{12,8},{16,12},{20,16},{24,20},{28,24},{5,1},{9,5},{13... | collective-permute-start | bytes 98312 | tf_op jit(solution)/shard_map/ppermute | solution.py:19
  117.7 5.4 %collective-permute-start.18 = (f32[1,1,1,8,8,128]{5,3,4,2,1,0:T(8,128)S(1)}, f32[1,1,1,8,8,128]{5,3,4,2,1,0:T(8,128)S(1)}, u32[]{:S(2)}, u32[]{:S(2)}) collective-permute-start(f32[1,1,1,8,8,128]{5,3,4,2,1,0:T(8,128)S(1)} %maximum_bitcast_fusion.12), channel_id=1, source_target_pairs={{0,1},{1,2},{2,3},{4,5},{5,6},{6,7},{8,9},{9,10},{10,11},{12,13},{... | collective-permute-start | bytes 98312 | tf_op jit(solution)/shard_map/ppermute | solution.py:16
  123.1 8.9 %collective-permute-start.19 = (f32[1,1,1,8,8,128]{5,3,4,2,1,0:T(8,128)S(1)}, f32[1,1,1,8,8,128]{5,3,4,2,1,0:T(8,128)S(1)}, u32[]{:S(2)}, u32[]{:S(2)}) collective-permute-start(f32[1,1,1,8,8,128]{5,3,4,2,1,0:T(8,128)S(1)} %get-tuple-element.25), channel_id=1, source_target_pairs={{1,0},{2,1},{3,2},{5,4},{6,5},{7,6},{9,8},{10,9},{11,10},{13,12},{... | collective-permute-start | bytes 98312 | tf_op jit(solution)/shard_map/ppermute | solution.py:19
  124.4 18.1 %all-to-all-start = ((f32[32,1,2048]{2,1,0:T(1,128)}), f32[32,1,2048]{2,1,0:T(1,128)S(1)}, u32[]{:S(2)}, u32[]{:S(2)}) async-start(f32[32,1,2048]{2,1,0:T(1,128)} %bitcast.124), calls=%async_computation | async-start | bytes 524288 | tf_op jit(solution)/shard_map/all_to_all | solution.py:174
  143.1 10.2 %all-to-all-start.3 = ((f32[8,1,2048]{2,1,0:T(1,128)}), f32[8,1,2048]{2,1,0:T(1,128)S(1)}, u32[]{:S(2)}, u32[]{:S(2)}) async-start(f32[8,1,2048]{2,1,0:T(1,128)} %broadcast_in_dim.192), calls=%async_computation.3 | async-start | bytes 131072 | tf_op jit(solution)/shard_map/all_to_all | solution.py:176
  154.0 10.2 %all-to-all-start.1 = ((f32[8,1,2048]{2,1,0:T(1,128)}), f32[8,1,2048]{2,1,0:T(1,128)S(1)}, u32[]{:S(2)}, u32[]{:S(2)}) async-start(f32[8,1,2048]{2,1,0:T(1,128)} %broadcast_in_dim.191), calls=%async_computation.1 | async-start | bytes 131072 | tf_op jit(solution)/shard_map/all_to_all | solution.py:176

commit v7 on v5

--- a/solution.py
+++ b/solution.py
@@ -49,7 +49,7 @@
     deriv[0, 0] = -degree * (degree + 1) / 4.0
     deriv[-1, -1] = degree * (degree + 1) / 4.0
     stiff = deriv.T @ (weights[:, None] * deriv)
-    return (jnp.asarray(weights, jnp.float32), jnp.asarray(stiff, jnp.float32))
+    return (np.asarray(weights, np.float32), np.asarray(stiff, np.float32))
 
 
 def spread(metric, which):
@@ -73,7 +73,7 @@
 
 
 def local_diagonal(metric, weights, stiff):
-    stiff_diag = jnp.diagonal(stiff)
+    stiff_diag = np.diagonal(stiff)
     weight_i = weights[None, None, :, None, None, None]
     weight_j = weights[None, None, None, :, None, None]
     weight_k = weights[None, None, None, None, :, None]
@@ -114,10 +114,12 @@
     )
 
 
-def assemble(values_in):
+def assemble(values_in, ride=None):
     lower, upper = faces(values_in, 3)
     rim_faces = jnp.concatenate([lower, upper], 1)
     padded = padded_2(rim_faces, (("ex", 1),), 1)
+    if ride is not None:
+        padded, ride = lax.optimization_barrier((padded, ride))
     values_in = combine(values_in, 3, 1, lower, upper, padded[:, :1], padded[:, 3:])
     lower, upper = faces(values_in, 4)
     rim_faces = jnp.concatenate([lower, upper], 2)
@@ -125,7 +127,7 @@
     values_in = combine(values_in, 4, 2, lower, upper, padded[:, :, :1], padded[:, :, 3:])
     lower, upper = faces(values_in, 5)
     empty = jnp.zeros_like(upper[..., :1])
-    return combine(values_in, 5, 5, lower, upper, empty, empty)
+    return combine(values_in, 5, 5, lower, upper, empty, empty), ride
 
 
 def split3(values):
@@ -162,7 +164,7 @@
     return (sums[:, :lanes] + sums[:, lanes : 2 * lanes] + sums[:, 2 * lanes :]).reshape(-1)
 
 
-def strip_totals(partial, strips, strip_size):
+def strip_reduce(partial, strips, strip_size):
     n_ex = lax.axis_size("ex")
     piece = -(-strip_size // n_ex)
     chunks = partial.reshape(2, strips, strip_size)
@@ -170,7 +172,12 @@
         chunks = jnp.pad(chunks, ((0, 0), (0, 0), (0, piece * n_ex - strip_size)))
     chunks = chunks.reshape(2, strips, n_ex, piece).transpose(2, 1, 0, 3)
     chunks = chunks.reshape(n_ex * strips, 2, piece)
-    mine = lax.all_to_all(chunks, ("ex", "ey"), 0, 0, tiled=True).sum(0)
+    return lax.all_to_all(chunks, ("ex", "ey"), 0, 0, tiled=True).sum(0)
+
+
+def strip_gather(mine, strip_size):
+    n_ex = lax.axis_size("ex")
+    count, piece = mine.shape
     spread_out = jnp.broadcast_to(mine[None], (n_ex, 2, piece))
     whole = lax.all_to_all(spread_out, "ex", 0, 0, tiled=True)
     return whole.transpose(1, 0, 2).reshape(2, n_ex * piece)[:, :strip_size]
@@ -183,7 +190,7 @@
     delta = (high - low) / 2.0
     sigma = theta / delta
     rho_now = 1.0 / sigma
-    both = assemble(jnp.stack([source, local_diagonal(metric, weights, stiff)]))
+    both, _ = assemble(jnp.stack([source, local_diagonal(metric, weights, stiff)]))
     rhs = both[0]
     pinv = 1.0 / both[1]
     pressure = jnp.zeros_like(source)
@@ -203,7 +210,10 @@
             samples = early + gather_flat(update.reshape(-1), picks, 256)
             numer = segment_sum(areas * samples, global_ids, strips * SHELL_STRIP, 256)
             partial = jnp.stack([numer, denom])
-        assembled = assemble(applied[None])[0]
+            assembled, mine = assemble(applied[None], strip_reduce(partial, strips, SHELL_STRIP))
+        else:
+            assembled, _ = assemble(applied[None])
+        assembled = assembled[0]
         if step + 2 == SWEEPS:
             assembled, early = lax.optimization_barrier((assembled, early))
         if step == 0:
@@ -213,7 +223,7 @@
             rho_new = 1.0 / (2.0 * sigma - rho_now)
             update = rho_new * rho_now * update + 2.0 * rho_new / delta * pinv * resid
             rho_now = rho_new
-    total = strip_totals(partial, strips, SHELL_STRIP)
+    total = strip_gather(mine, SHELL_STRIP)
     shell_load = total[0] / jnp.maximum(total[1], 1.0)
     return (pressure, resid, shell_load)
 

time: 152 us -> 146 us (0.961); the launches traced: 149 us -> 145 us
  starting transfers between devices: 58.4 us -> 56.2 us
    all_to_all x2, waiting for transfers between devices: 17.6 us -> 10.9 us  [the longest x1 6.78 us: strip_gather(): whole = lax.all_to_all(spread_out, 'ex', 0, 0, tiled=True)]
    ppermute x10, waiting for transfers between devices: 9.79 us -> 13.3 us  [padded_2(): lax.ppermute(lax.slice_in_dim(block, block.shape[dim] - width, None, axis...]
    ppermute x10, waiting for transfers between devices: 18.8 us -> 21.8 us  [padded_2(): lax.ppermute(lax.slice_in_dim(block, 0, width, axis=dim), axis, backward)]
    all_to_all x2, starting transfers between devices: 10.4 us -> 8.24 us  [the longest x1 4.79 us: strip_reduce(): return lax.all_to_all(chunks, ('ex', 'ey'), 0, 0, tiled=True).sum(0)]
  transfers between devices with their start and end apart: 22 -> 22, of which waited for: 18 -> 20; matrix products, arithmetic and copies ran while one was open for 15% -> 11% of each run, Pallas kernels for 0% -> 0%
where the time goes in v7:
time: 146 us; the launch traced here: 145 us
  starting transfers between devices  56.2 us (38%)
  waiting for transfers between devices  46 us (32%)
  other arithmetic  21.6 us (15%)
  matrix products  14.7 us (10%)
  local copies, waits for them, and re-layouts  5.25 us (4%)
  between operations  1.55 us (1%)
    ppermute x10, starting transfers between devices, padded_2(): lax.ppermute(lax.slice_in_dim(block, block.shape[dim] - width, None, axis...  30.2 us
    ppermute x10, waiting for transfers between devices, padded_2(): lax.ppermute(lax.slice_in_dim(block, 0, width, axis=dim), axis, backward)  21.8 us
    ppermute x10, starting transfers between devices, padded_2(): lax.ppermute(lax.slice_in_dim(block, 0, width, axis=dim), axis, backward)  17.7 us
    ppermute x10, waiting for transfers between devices, padded_2(): lax.ppermute(lax.slice_in_dim(block, block.shape[dim] - width, None, axis...  13.3 us
    mul x2, other arithmetic, segment_sum(): hit_lane * part[:, None]  7.28 us
    all_to_all x1, waiting for transfers between devices, strip_gather(): whole = lax.all_to_all(spread_out, 'ex', 0, 0, tiled=True)  6.78 us
    dot_general x2, matrix products, segment_sum(): lax.dot_general(hit_row, rhs, (((0,), (0,)), ((), ())), preferred_element...  5.17 us
    all_to_all x1, starting transfers between devices, strip_reduce(): return lax.all_to_all(chunks, ('ex', 'ey'), 0, 0, tiled=True).sum(0)  4.79 us
  transfers between devices with their start and end apart: 22, of which 20 were waited for; matrix products, arithmetic and copies ran while one was open for 11% of the time, Pallas kernels for 0%

profile of v7, /device:TPU:2, one launch (start us, length us, event | category | flops | bytes accessed | tf_op | source)
XLA Modules:
  0.0 145.3 jit_solution(15870916007871566410)
XLA Ops:
  2.9 1.2 fusion.93
  4.8 3.4 %collective-permute-start = (f32[2,1,1,8,8,128]{5,0,4,3,2,1:T(2,128)S(1)}, f32[2,1,1,8,8,128]{5,0,4,3,2,1:T(2,128)S(1)}, u32[]{:S(2)}, u32[]{:S(2)}) collective-permute-start(f32[2,1,1,8,8,128]{5,0,4,3,2,1:T(2,128)S(1)} %maximum_bitcast_fusion.9), channel_id=1, source_target_pairs={{0,4},{4,8},{8,12},{12,16},{16,20},{20,24},{24,28},{1,5},{5,9},{9,... | collective-permute-start | bytes 196616 | tf_op jit(solution)/shard_map/ppermute | solution.py:16
  10.2 0.8 fusion.114
  11.0 1.3 collective-permute-start.1
  12.3 1.3 pad_maximum_fusion.5
  13.9 3.7 %collective-permute-done.1 = f32[2,1,1,8,8,128]{5,0,4,3,2,1:T(2,128)S(1)} collective-permute-done((f32[2,1,1,8,8,128]{5,0,4,3,2,1:T(2,128)S(1)}, f32[2,1,1,8,8,128]{5,0,4,3,2,1:T(2,128)S(1)}, u32[]{:S(2)}, u32[]{:S(2)}) %collective-permute-start.1) | collective-permute-done | bytes 65568 | tf_op jit(solution)/shard_map/ppermute | solution.py:19
  17.6 1.9 %collective-permute-start.2 = (f32[2,1,1,8,8,128]{5,3,0,4,2,1:T(8,128)S(1)}, f32[2,1,1,8,8,128]{5,3,0,4,2,1:T(8,128)S(1)}, u32[]{:S(2)}, u32[]{:S(2)}) collective-permute-start(f32[2,1,1,8,8,128]{5,3,0,4,2,1:T(8,128)S(1)} %maximum_bitcast_fusion.7), channel_id=1, source_target_pairs={{0,1},{1,2},{2,3},{4,5},{5,6},{6,7},{8,9},{9,10},{10,11},{12,13},{... | collective-permute-start | bytes 196616 | tf_op jit(solution)/shard_map/ppermute | solution.py:16
  19.5 3.6 %collective-permute-done.2 = f32[2,1,1,8,8,128]{5,3,0,4,2,1:T(8,128)S(1)} collective-permute-done((f32[2,1,1,8,8,128]{5,3,0,4,2,1:T(8,128)S(1)}, f32[2,1,1,8,8,128]{5,3,0,4,2,1:T(8,128)S(1)}, u32[]{:S(2)}, u32[]{:S(2)}) %collective-permute-start.2) | collective-permute-done | bytes 65568 | tf_op jit(solution)/shard_map/ppermute | solution.py:16
  23.2 1.9 %collective-permute-start.3 = (f32[2,1,1,8,8,128]{5,3,0,4,2,1:T(8,128)S(1)}, f32[2,1,1,8,8,128]{5,3,0,4,2,1:T(8,128)S(1)}, u32[]{:S(2)}, u32[]{:S(2)}) collective-permute-start(f32[2,1,1,8,8,128]{5,3,0,4,2,1:T(8,128)S(1)} %get-tuple-element.43), channel_id=1, source_target_pairs={{1,0},{2,1},{3,2},{5,4},{6,5},{7,6},{9,8},{10,9},{11,10},{13,12},{... | collective-permute-start | bytes 196616 | tf_op jit(solution)/shard_map/ppermute | solution.py:19
  25.6 1.5 %collective-permute-done.3 = f32[2,1,1,8,8,128]{5,3,0,4,2,1:T(8,128)S(1)} collective-permute-done((f32[2,1,1,8,8,128]{5,3,0,4,2,1:T(8,128)S(1)}, f32[2,1,1,8,8,128]{5,3,0,4,2,1:T(8,128)S(1)}, u32[]{:S(2)}, u32[]{:S(2)}) %collective-permute-start.3) | collective-permute-done | bytes 65568 | tf_op jit(solution)/shard_map/ppermute | solution.py:19
  28.8 0.9 fusion.33
  29.8 4.8 %collective-permute-start.4 = (f32[1,1,1,8,8,128]{5,4,3,2,1,0:T(8,128)S(1)}, f32[1,1,1,8,8,128]{5,4,3,2,1,0:T(8,128)S(1)}, u32[]{:S(2)}, u32[]{:S(2)}) collective-permute-start(f32[1,1,1,8,8,128]{5,4,3,2,1,0:T(8,128)S(1)} %bitcast.475), channel_id=1, source_target_pairs={{0,4},{4,8},{8,12},{12,16},{16,20},{20,24},{24,28},{1,5},{5,9},{9,... | collective-permute-start | bytes 98312 | tf_op jit(solution)/shard_map/ppermute | solution.py:16
  34.6 1.3 collective-permute-start.5
  35.9 3.6 %fusion.23 = (bf16[4096,256]{1,0:T(8,128)(2,1)S(1)}, bf16[4096,256]{1,0:T(8,128)(2,1)S(1)}, bf16[4096,256]{1,0:T(8,128)(2,1)S(1)}) fusion(s32[4096]{0:T(1024)S(1)} %get-tuple-element.77, bf16[4096]{0:T(1024)(128)(2,1)S(1)} %get-tuple-element.88, bf16[4096]{0:T(1024)(128)(2,1)S(1)} %get-tuple-element.89, bf16[4096]{0:T(1024)(128)(2,1)S(1)} %get-tuple-element.90), kind=kLoop, calls=%fused_computation.30 | loop fusion | flops 4194304 | bytes 6332416 | tf_op jit(solution)/shard_map/mul | solution.py:159
  40.4 1.9 %collective-permute-start.6 = (f32[1,1,1,8,8,128]{5,3,4,2,1,0:T(8,128)S(1)}, f32[1,1,1,8,8,128]{5,3,4,2,1,0:T(8,128)S(1)}, u32[]{:S(2)}, u32[]{:S(2)}) collective-permute-start(f32[1,1,1,8,8,128]{5,3,4,2,1,0:T(8,128)S(1)} %maximum_bitcast_fusion.19), channel_id=1, source_target_pairs={{0,1},{1,2},{2,3},{4,5},{5,6},{6,7},{8,9},{9,10},{10,11},{12,13},{... | collective-permute-start | bytes 98312 | tf_op jit(solution)/shard_map/ppermute | solution.py:16
  42.3 2.6 %fusion = f32[256,768]{1,0:T(8,128)S(1)} fusion(bf16[4096,256]{1,0:T(8,128)(2,1)S(1)} %get-tuple-element.86, bf16[4096,256]{1,0:T(8,128)(2,1)S(1)} %get-tuple-element.87, bf16[4096,256]{1,0:T(8,128)(2,1)S(1)} %get-tuple-element.85, s32[4096]{0:T(1024)S(1)} %get-tuple-element.76), kind=kOutput, calls=%fused_computation | convolution fusion | flops 1630535680 | bytes 7094272 | tf_op jit(solution)/shard_map/dot_general | solution.py:161
  45.7 2.9 %collective-permute-start.7 = (f32[1,1,1,8,8,128]{5,3,4,2,1,0:T(8,128)S(1)}, f32[1,1,1,8,8,128]{5,3,4,2,1,0:T(8,128)S(1)}, u32[]{:S(2)}, u32[]{:S(2)}) collective-permute-start(f32[1,1,1,8,8,128]{5,3,4,2,1,0:T(8,128)S(1)} %get-tuple-element.39), channel_id=1, source_target_pairs={{1,0},{2,1},{3,2},{5,4},{6,5},{7,6},{9,8},{10,9},{11,10},{13,12},{... | collective-permute-start | bytes 98312 | tf_op jit(solution)/shard_map/ppermute | solution.py:19
  48.8 1.4 collective-permute-done.7
  52.1 4.3 %collective-permute-start.8 = (f32[1,1,1,8,8,128]{5,4,3,2,1,0:T(8,128)S(1)}, f32[1,1,1,8,8,128]{5,4,3,2,1,0:T(8,128)S(1)}, u32[]{:S(2)}, u32[]{:S(2)}) collective-permute-start(f32[1,1,1,8,8,128]{5,4,3,2,1,0:T(8,128)S(1)} %get-tuple-element.68), channel_id=1, source_target_pairs={{0,4},{4,8},{8,12},{12,16},{16,20},{20,24},{24,28},{1,5},{5,9},{9,... | collective-permute-start | bytes 98312 | tf_op jit(solution)/shard_map/ppermute | solution.py:16
  56.4 1.3 collective-permute-start.9
  58.0 4.2 %collective-permute-done.9 = f32[1,1,1,8,8,128]{5,4,3,2,1,0:T(8,128)S(1)} collective-permute-done((f32[1,1,1,8,8,128]{5,4,3,2,1,0:T(8,128)S(1)}, f32[1,1,1,8,8,128]{5,4,3,2,1,0:T(8,128)S(1)}, u32[]{:S(2)}, u32[]{:S(2)}) %collective-permute-start.9) | collective-permute-done | bytes 32800 | tf_op jit(solution)/shard_map/ppermute | solution.py:19
  62.3 1.9 %collective-permute-start.10 = (f32[1,1,1,8,8,128]{5,4,3,2,1,0:T(8,128)S(1)}, f32[1,1,1,8,8,128]{5,4,3,2,1,0:T(8,128)S(1)}, u32[]{:S(2)}, u32[]{:S(2)}) collective-permute-start(f32[1,1,1,8,8,128]{5,4,3,2,1,0:T(8,128)S(1)} %maximum_bitcast_fusion.17), channel_id=1, source_target_pairs={{0,1},{1,2},{2,3},{4,5},{5,6},{6,7},{8,9},{9,10},{10,11},{12,13},{... | collective-permute-start | bytes 98312 | tf_op jit(solution)/shard_map/ppermute | solution.py:16
  64.2 3.3 %collective-permute-done.10 = f32[1,1,1,8,8,128]{5,4,3,2,1,0:T(8,128)S(1)} collective-permute-done((f32[1,1,1,8,8,128]{5,4,3,2,1,0:T(8,128)S(1)}, f32[1,1,1,8,8,128]{5,4,3,2,1,0:T(8,128)S(1)}, u32[]{:S(2)}, u32[]{:S(2)}) %collective-permute-start.10) | collective-permute-done | bytes 32800 | tf_op jit(solution)/shard_map/ppermute | solution.py:16
  67.5 2.1 %collective-permute-start.11 = (f32[1,1,1,8,8,128]{5,4,3,2,1,0:T(8,128)S(1)}, f32[1,1,1,8,8,128]{5,4,3,2,1,0:T(8,128)S(1)}, u32[]{:S(2)}, u32[]{:S(2)}) collective-permute-start(f32[1,1,1,8,8,128]{5,4,3,2,1,0:T(8,128)S(1)} %get-tuple-element.37), channel_id=1, source_target_pairs={{1,0},{2,1},{3,2},{5,4},{6,5},{7,6},{9,8},{10,9},{11,10},{13,12},{... | collective-permute-start | bytes 98312 | tf_op jit(solution)/shard_map/ppermute | solution.py:19
  69.7 1.3 collective-permute-done.11
  73.1 4.7 %collective-permute-start.12 = (f32[1,1,1,8,8,128]{5,4,3,2,1,0:T(8,128)S(1)}, f32[1,1,1,8,8,128]{5,4,3,2,1,0:T(8,128)S(1)}, u32[]{:S(2)}, u32[]{:S(2)}) collective-permute-start(f32[1,1,1,8,8,128]{5,4,3,2,1,0:T(8,128)S(1)} %get-tuple-element.62), channel_id=1, source_target_pairs={{0,4},{4,8},{8,12},{12,16},{16,20},{20,24},{24,28},{1,5},{5,9},{9,... | collective-permute-start | bytes 98312 | tf_op jit(solution)/shard_map/ppermute | solution.py:16
  77.8 1.3 collective-permute-start.13
  79.4 4.2 %collective-permute-done.13 = f32[1,1,1,8,8,128]{5,4,3,2,1,0:T(8,128)S(1)} collective-permute-done((f32[1,1,1,8,8,128]{5,4,3,2,1,0:T(8,128)S(1)}, f32[1,1,1,8,8,128]{5,4,3,2,1,0:T(8,128)S(1)}, u32[]{:S(2)}, u32[]{:S(2)}) %collective-permute-start.13) | collective-permute-done | bytes 32800 | tf_op jit(solution)/shard_map/ppermute | solution.py:19
  83.6 1.9 %collective-permute-start.14 = (f32[1,1,1,8,8,128]{5,4,3,2,1,0:T(8,128)S(1)}, f32[1,1,1,8,8,128]{5,4,3,2,1,0:T(8,128)S(1)}, u32[]{:S(2)}, u32[]{:S(2)}) collective-permute-start(f32[1,1,1,8,8,128]{5,4,3,2,1,0:T(8,128)S(1)} %maximum_bitcast_fusion.15), channel_id=1, source_target_pairs={{0,1},{1,2},{2,3},{4,5},{5,6},{6,7},{8,9},{9,10},{10,11},{12,13},{... | collective-permute-start | bytes 98312 | tf_op jit(solution)/shard_map/ppermute | solution.py:16
  85.5 2.0 %fusion.17 = f32[4096,768]{0,1:T(8,128)S(1)} fusion(s32[4096]{0:T(1024)S(1)} %get-tuple-element.84, bf16[256,256]{1,0:T(8,128)(2,1)S(1)} %get-tuple-element.56, bf16[256,256]{1,0:T(8,128)(2,1)S(1)} %get-tuple-element.57, bf16[256,256]{1,0:T(8,128)(2,1)S(1)} %get-tuple-element.55), kind=kOutput, calls=%fused_computation.22 | convolution fusion | flops 1612840960 | bytes 12992512 | tf_op jit(solution)/shard_map/dot_general | solution.py:150
  87.6 1.3 collective-permute-done.14
  88.9 2.4 %collective-permute-start.15 = (f32[1,1,1,8,8,128]{5,4,3,2,1,0:T(8,128)S(1)}, f32[1,1,1,8,8,128]{5,4,3,2,1,0:T(8,128)S(1)}, u32[]{:S(2)}, u32[]{:S(2)}) collective-permute-start(f32[1,1,1,8,8,128]{5,4,3,2,1,0:T(8,128)S(1)} %get-tuple-element.33), channel_id=1, source_target_pairs={{1,0},{2,1},{3,2},{5,4},{6,5},{7,6},{9,8},{10,9},{11,10},{13,12},{... | collective-permute-start | bytes 98312 | tf_op jit(solution)/shard_map/ppermute | solution.py:19
  91.2 1.4 fusion.15
  94.3 2.0 %fusion.16 = f32[4096,768]{0,1:T(8,128)S(1)} fusion(s32[4096]{0:T(1024)S(1)} %get-tuple-element.84, bf16[256,256]{1,0:T(8,128)(2,1)S(1)} %get-tuple-element.51, bf16[256,256]{1,0:T(8,128)(2,1)S(1)} %get-tuple-element.52, bf16[256,256]{1,0:T(8,128)(2,1)S(1)} %get-tuple-element.50), kind=kOutput, calls=%fused_computation.21 | convolution fusion | flops 1612840960 | bytes 12992512 | tf_op jit(solution)/shard_map/dot_general | solution.py:150
  96.3 1.4 fusion.13
  97.7 3.6 %fusion.20 = (bf16[4096,256]{1,0:T(8,128)(2,1)S(1)}, bf16[4096,256]{1,0:T(8,128)(2,1)S(1)}, bf16[4096,256]{1,0:T(8,128)(2,1)S(1)}) fusion(s32[4096]{0:T(1024)S(1)} %get-tuple-element.77, bf16[4096]{0:T(1024)(128)(2,1)S(1)} %get-tuple-element.28, bf16[4096]{0:T(1024)(128)(2,1)S(1)} %get-tuple-element.82, bf16[4096]{0:T(1024)(128)(2,1)S(1)} %get-tuple-element.81), kind=kLoop, calls=%fused_computation.27 | loop fusion | flops 4194304 | bytes 6332416 | tf_op jit(solution)/shard_map/mul | solution.py:159
  101.4 2.6 %fusion.6 = f32[256,768]{1,0:T(8,128)S(1)} fusion(bf16[4096,256]{1,0:T(8,128)(2,1)S(1)} %get-tuple-element.79, bf16[4096,256]{1,0:T(8,128)(2,1)S(1)} %get-tuple-element.80, bf16[4096,256]{1,0:T(8,128)(2,1)S(1)} %get-tuple-element.78, s32[4096]{0:T(1024)S(1)} %get-tuple-element.76), kind=kOutput, calls=%fused_computation.6 | convolution fusion | flops 1630535680 | bytes 7094272 | tf_op jit(solution)/shard_map/dot_general | solution.py:161
  104.1 1.2 copy.201
  105.3 4.8 %all-to-all-start = ((f32[32,2,2048]{2,1,0:T(2,128)}), f32[32,2,2048]{2,1,0:T(2,128)S(1)}, u32[]{:S(2)}, u32[]{:S(2)}) async-start(f32[32,2,2048]{2,1,0:T(2,128)} %bitcast.109), calls=%async_computation | async-start | bytes 1048576 | tf_op jit(solution)/shard_map/all_to_all | solution.py:175
  111.4 3.4 %collective-permute-start.16 = (f32[1,1,1,8,8,128]{5,4,3,2,1,0:T(8,128)S(1)}, f32[1,1,1,8,8,128]{5,4,3,2,1,0:T(8,128)S(1)}, u32[]{:S(2)}, u32[]{:S(2)}) collective-permute-start(f32[1,1,1,8,8,128]{5,4,3,2,1,0:T(8,128)S(1)} %get-tuple-element.53), channel_id=1, source_target_pairs={{0,4},{4,8},{8,12},{12,16},{16,20},{20,24},{24,28},{1,5},{5,9},{9,... | collective-permute-start | bytes 98312 | tf_op jit(solution)/shard_map/ppermute | solution.py:16
  114.8 1.3 collective-permute-start.17
  116.6 4.5 %collective-permute-done.17 = f32[1,1,1,8,8,128]{5,4,3,2,1,0:T(8,128)S(1)} collective-permute-done((f32[1,1,1,8,8,128]{5,4,3,2,1,0:T(8,128)S(1)}, f32[1,1,1,8,8,128]{5,4,3,2,1,0:T(8,128)S(1)}, u32[]{:S(2)}, u32[]{:S(2)}) %collective-permute-start.17) | collective-permute-done | bytes 32800 | tf_op jit(solution)/shard_map/ppermute | solution.py:19
  121.1 4.1 %all-to-all-done = f32[32,2,2048]{2,1,0:T(2,128)S(1)} async-done(((f32[32,2,2048]{2,1,0:T(2,128)}), f32[32,2,2048]{2,1,0:T(2,128)S(1)}, u32[]{:S(2)}, u32[]{:S(2)}) %all-to-all-start) | async-done | bytes 524320 | tf_op jit(solution)/shard_map/all_to_all | solution.py:175
  125.4 2.0 %collective-permute-start.18 = (f32[1,1,1,8,8,128]{5,3,4,2,1,0:T(8,128)S(1)}, f32[1,1,1,8,8,128]{5,3,4,2,1,0:T(8,128)S(1)}, u32[]{:S(2)}, u32[]{:S(2)}) collective-permute-start(f32[1,1,1,8,8,128]{5,3,4,2,1,0:T(8,128)S(1)} %maximum_bitcast_fusion.13), channel_id=1, source_target_pairs={{0,1},{1,2},{2,3},{4,5},{5,6},{6,7},{8,9},{9,10},{10,11},{12,13},{... | collective-permute-start | bytes 98312 | tf_op jit(solution)/shard_map/ppermute | solution.py:16
  127.3 3.3 %collective-permute-done.18 = f32[1,1,1,8,8,128]{5,3,4,2,1,0:T(8,128)S(1)} collective-permute-done((f32[1,1,1,8,8,128]{5,3,4,2,1,0:T(8,128)S(1)}, f32[1,1,1,8,8,128]{5,3,4,2,1,0:T(8,128)S(1)}, u32[]{:S(2)}, u32[]{:S(2)}) %collective-permute-start.18) | collective-permute-done | bytes 32800 | tf_op jit(solution)/shard_map/ppermute | solution.py:16
  130.6 1.9 %collective-permute-start.19 = (f32[1,1,1,8,8,128]{5,3,4,2,1,0:T(8,128)S(1)}, f32[1,1,1,8,8,128]{5,3,4,2,1,0:T(8,128)S(1)}, u32[]{:S(2)}, u32[]{:S(2)}) collective-permute-start(f32[1,1,1,8,8,128]{5,3,4,2,1,0:T(8,128)S(1)} %get-tuple-element.27), channel_id=1, source_target_pairs={{1,0},{2,1},{3,2},{5,4},{6,5},{7,6},{9,8},{10,9},{11,10},{13,12},{... | collective-permute-start | bytes 98312 | tf_op jit(solution)/shard_map/ppermute | solution.py:19
  133.3 3.4 %all-to-all-start.1 = ((f32[8,2,2048]{2,1,0:T(2,128)}), f32[8,2,2048]{2,1,0:T(2,128)S(1)}, u32[]{:S(2)}, u32[]{:S(2)}) async-start(f32[8,2,2048]{2,1,0:T(2,128)} %broadcast_in_dim.163), calls=%async_computation.1 | async-start | bytes 262144 | tf_op jit(solution)/shard_map/all_to_all | solution.py:182
  137.8 6.8 %all-to-all-done.1 = f32[8,2,2048]{2,1,0:T(2,128)S(1)} async-done(((f32[8,2,2048]{2,1,0:T(2,128)}), f32[8,2,2048]{2,1,0:T(2,128)S(1)}, u32[]{:S(2)}, u32[]{:S(2)}) %all-to-all-start.1) | async-done | bytes 131104 | tf_op jit(solution)/shard_map/all_to_all | solution.py:182
  (128 shorter events, 19.8 us)
Async XLA Ops:
  0.6 18.9 %copy-start.1 = (f32[1,4096]{1,0:T(1,128)S(1)}, f32[1,4096]{1,0:T(1,128)}, u32[]{:S(2)}) copy-start(f32[1,4096]{1,0:T(1,128)} %param.41) | copy-start | bytes 49156
  4.8 5.3 %collective-permute-start = (f32[2,1,1,8,8,128]{5,0,4,3,2,1:T(2,128)S(1)}, f32[2,1,1,8,8,128]{5,0,4,3,2,1:T(2,128)S(1)}, u32[]{:S(2)}, u32[]{:S(2)}) collective-permute-start(f32[2,1,1,8,8,128]{5,0,4,3,2,1:T(2,128)S(1)} %maximum_bitcast_fusion.9), channel_id=1, source_target_pairs={{0,4},{4,8},{8,12},{12,16},{16,20},{20,24},{24,28},{1,5},{5,9},{9,... | collective-permute-start | bytes 196616 | tf_op jit(solution)/shard_map/ppermute | solution.py:16
  11.0 6.5 %collective-permute-start.1 = (f32[2,1,1,8,8,128]{5,0,4,3,2,1:T(2,128)S(1)}, f32[2,1,1,8,8,128]{5,0,4,3,2,1:T(2,128)S(1)}, u32[]{:S(2)}, u32[]{:S(2)}) collective-permute-start(f32[2,1,1,8,8,128]{5,0,4,3,2,1:T(2,128)S(1)} %get-tuple-element.45), channel_id=1, source_target_pairs={{4,0},{8,4},{12,8},{16,12},{20,16},{24,20},{28,24},{5,1},{9,5},{13... | collective-permute-start | bytes 196616 | tf_op jit(solution)/shard_map/ppermute | solution.py:19
  17.6 5.6 %collective-permute-start.2 = (f32[2,1,1,8,8,128]{5,3,0,4,2,1:T(8,128)S(1)}, f32[2,1,1,8,8,128]{5,3,0,4,2,1:T(8,128)S(1)}, u32[]{:S(2)}, u32[]{:S(2)}) collective-permute-start(f32[2,1,1,8,8,128]{5,3,0,4,2,1:T(8,128)S(1)} %maximum_bitcast_fusion.7), channel_id=1, source_target_pairs={{0,1},{1,2},{2,3},{4,5},{5,6},{6,7},{8,9},{9,10},{10,11},{12,13},{... | collective-permute-start | bytes 196616 | tf_op jit(solution)/shard_map/ppermute | solution.py:16
  23.2 4.7 %copy-start = (f32[8,8,1,1]{1,0,3,2:T(8,128)S(1)}, f32[8,8,1,1]{1,0,3,2:T(8,128)}, u32[]{:S(2)}) copy-start(f32[8,8,1,1]{1,0,3,2:T(8,128)} %constant.135) | copy-start | bytes 772
  23.2 3.8 %collective-permute-start.3 = (f32[2,1,1,8,8,128]{5,3,0,4,2,1:T(8,128)S(1)}, f32[2,1,1,8,8,128]{5,3,0,4,2,1:T(8,128)S(1)}, u32[]{:S(2)}, u32[]{:S(2)}) collective-permute-start(f32[2,1,1,8,8,128]{5,3,0,4,2,1:T(8,128)S(1)} %get-tuple-element.43), channel_id=1, source_target_pairs={{1,0},{2,1},{3,2},{5,4},{6,5},{7,6},{9,8},{10,9},{11,10},{13,12},{... | collective-permute-start | bytes 196616 | tf_op jit(solution)/shard_map/ppermute | solution.py:19
  25.3 3.3 %copy-start.2 = (f32[8]{0:T(128)S(1)}, f32[8]{0:T(128)}, u32[]{:S(2)}) copy-start(f32[8]{0:T(128)} %constant.130) | copy-start | bytes 100
  29.8 9.8 %collective-permute-start.4 = (f32[1,1,1,8,8,128]{5,4,3,2,1,0:T(8,128)S(1)}, f32[1,1,1,8,8,128]{5,4,3,2,1,0:T(8,128)S(1)}, u32[]{:S(2)}, u32[]{:S(2)}) collective-permute-start(f32[1,1,1,8,8,128]{5,4,3,2,1,0:T(8,128)S(1)} %bitcast.475), channel_id=1, source_target_pairs={{0,4},{4,8},{8,12},{12,16},{16,20},{20,24},{24,28},{1,5},{5,9},{9,... | collective-permute-start | bytes 98312 | tf_op jit(solution)/shard_map/ppermute | solution.py:16
  34.6 5.8 %collective-permute-start.5 = (f32[1,1,1,8,8,128]{5,4,3,2,1,0:T(8,128)S(1)}, f32[1,1,1,8,8,128]{5,4,3,2,1,0:T(8,128)S(1)}, u32[]{:S(2)}, u32[]{:S(2)}) collective-permute-start(f32[1,1,1,8,8,128]{5,4,3,2,1,0:T(8,128)S(1)} %bitcast.477), channel_id=1, source_target_pairs={{4,0},{8,4},{12,8},{16,12},{20,16},{24,20},{28,24},{5,1},{9,5},{13... | collective-permute-start | bytes 98312 | tf_op jit(solution)/shard_map/ppermute | solution.py:19
  40.4 5.2 %collective-permute-start.6 = (f32[1,1,1,8,8,128]{5,3,4,2,1,0:T(8,128)S(1)}, f32[1,1,1,8,8,128]{5,3,4,2,1,0:T(8,128)S(1)}, u32[]{:S(2)}, u32[]{:S(2)}) collective-permute-start(f32[1,1,1,8,8,128]{5,3,4,2,1,0:T(8,128)S(1)} %maximum_bitcast_fusion.19), channel_id=1, source_target_pairs={{0,1},{1,2},{2,3},{4,5},{5,6},{6,7},{8,9},{9,10},{10,11},{12,13},{... | collective-permute-start | bytes 98312 | tf_op jit(solution)/shard_map/ppermute | solution.py:16
  45.7 4.5 %collective-permute-start.7 = (f32[1,1,1,8,8,128]{5,3,4,2,1,0:T(8,128)S(1)}, f32[1,1,1,8,8,128]{5,3,4,2,1,0:T(8,128)S(1)}, u32[]{:S(2)}, u32[]{:S(2)}) collective-permute-start(f32[1,1,1,8,8,128]{5,3,4,2,1,0:T(8,128)S(1)} %get-tuple-element.39), channel_id=1, source_target_pairs={{1,0},{2,1},{3,2},{5,4},{6,5},{7,6},{9,8},{10,9},{11,10},{13,12},{... | collective-permute-start | bytes 98312 | tf_op jit(solution)/shard_map/ppermute | solution.py:19
  48.7 20.9 %copy-start.3 = (s32[1,4096]{1,0:T(1,128)S(1)}, s32[1,4096]{1,0:T(1,128)}, u32[]{:S(2)}) copy-start(s32[1,4096]{1,0:T(1,128)} %param.38) | copy-start | bytes 49156
  52.1 5.9 %collective-permute-start.8 = (f32[1,1,1,8,8,128]{5,4,3,2,1,0:T(8,128)S(1)}, f32[1,1,1,8,8,128]{5,4,3,2,1,0:T(8,128)S(1)}, u32[]{:S(2)}, u32[]{:S(2)}) collective-permute-start(f32[1,1,1,8,8,128]{5,4,3,2,1,0:T(8,128)S(1)} %get-tuple-element.68), channel_id=1, source_target_pairs={{0,4},{4,8},{8,12},{12,16},{16,20},{20,24},{24,28},{1,5},{5,9},{9,... | collective-permute-start | bytes 98312 | tf_op jit(solution)/shard_map/ppermute | solution.py:16
  56.4 5.8 %collective-permute-start.9 = (f32[1,1,1,8,8,128]{5,4,3,2,1,0:T(8,128)S(1)}, f32[1,1,1,8,8,128]{5,4,3,2,1,0:T(8,128)S(1)}, u32[]{:S(2)}, u32[]{:S(2)}) collective-permute-start(f32[1,1,1,8,8,128]{5,4,3,2,1,0:T(8,128)S(1)} %get-tuple-element.69), channel_id=1, source_target_pairs={{4,0},{8,4},{12,8},{16,12},{20,16},{24,20},{28,24},{5,1},{9,5},{13... | collective-permute-start | bytes 98312 | tf_op jit(solution)/shard_map/ppermute | solution.py:19
  62.3 5.2 %collective-permute-start.10 = (f32[1,1,1,8,8,128]{5,4,3,2,1,0:T(8,128)S(1)}, f32[1,1,1,8,8,128]{5,4,3,2,1,0:T(8,128)S(1)}, u32[]{:S(2)}, u32[]{:S(2)}) collective-permute-start(f32[1,1,1,8,8,128]{5,4,3,2,1,0:T(8,128)S(1)} %maximum_bitcast_fusion.17), channel_id=1, source_target_pairs={{0,1},{1,2},{2,3},{4,5},{5,6},{6,7},{8,9},{9,10},{10,11},{12,13},{... | collective-permute-start | bytes 98312 | tf_op jit(solution)/shard_map/ppermute | solution.py:16
  67.5 3.5 %collective-permute-start.11 = (f32[1,1,1,8,8,128]{5,4,3,2,1,0:T(8,128)S(1)}, f32[1,1,1,8,8,128]{5,4,3,2,1,0:T(8,128)S(1)}, u32[]{:S(2)}, u32[]{:S(2)}) collective-permute-start(f32[1,1,1,8,8,128]{5,4,3,2,1,0:T(8,128)S(1)} %get-tuple-element.37), channel_id=1, source_target_pairs={{1,0},{2,1},{3,2},{5,4},{6,5},{7,6},{9,8},{10,9},{11,10},{13,12},{... | collective-permute-start | bytes 98312 | tf_op jit(solution)/shard_map/ppermute | solution.py:19
  73.1 6.3 %collective-permute-start.12 = (f32[1,1,1,8,8,128]{5,4,3,2,1,0:T(8,128)S(1)}, f32[1,1,1,8,8,128]{5,4,3,2,1,0:T(8,128)S(1)}, u32[]{:S(2)}, u32[]{:S(2)}) collective-permute-start(f32[1,1,1,8,8,128]{5,4,3,2,1,0:T(8,128)S(1)} %get-tuple-element.62), channel_id=1, source_target_pairs={{0,4},{4,8},{8,12},{12,16},{16,20},{20,24},{24,28},{1,5},{5,9},{9,... | collective-permute-start | bytes 98312 | tf_op jit(solution)/shard_map/ppermute | solution.py:16
  77.8 5.8 %collective-permute-start.13 = (f32[1,1,1,8,8,128]{5,4,3,2,1,0:T(8,128)S(1)}, f32[1,1,1,8,8,128]{5,4,3,2,1,0:T(8,128)S(1)}, u32[]{:S(2)}, u32[]{:S(2)}) collective-permute-start(f32[1,1,1,8,8,128]{5,4,3,2,1,0:T(8,128)S(1)} %get-tuple-element.63), channel_id=1, source_target_pairs={{4,0},{8,4},{12,8},{16,12},{20,16},{24,20},{28,24},{5,1},{9,5},{13... | collective-permute-start | bytes 98312 | tf_op jit(solution)/shard_map/ppermute | solution.py:19
  83.6 5.2 %collective-permute-start.14 = (f32[1,1,1,8,8,128]{5,4,3,2,1,0:T(8,128)S(1)}, f32[1,1,1,8,8,128]{5,4,3,2,1,0:T(8,128)S(1)}, u32[]{:S(2)}, u32[]{:S(2)}) collective-permute-start(f32[1,1,1,8,8,128]{5,4,3,2,1,0:T(8,128)S(1)} %maximum_bitcast_fusion.15), channel_id=1, source_target_pairs={{0,1},{1,2},{2,3},{4,5},{5,6},{6,7},{8,9},{9,10},{10,11},{12,13},{... | collective-permute-start | bytes 98312 | tf_op jit(solution)/shard_map/ppermute | solution.py:16
  88.9 4.0 %collective-permute-start.15 = (f32[1,1,1,8,8,128]{5,4,3,2,1,0:T(8,128)S(1)}, f32[1,1,1,8,8,128]{5,4,3,2,1,0:T(8,128)S(1)}, u32[]{:S(2)}, u32[]{:S(2)}) collective-permute-start(f32[1,1,1,8,8,128]{5,4,3,2,1,0:T(8,128)S(1)} %get-tuple-element.33), channel_id=1, source_target_pairs={{1,0},{2,1},{3,2},{5,4},{6,5},{7,6},{9,8},{10,9},{11,10},{13,12},{... | collective-permute-start | bytes 98312 | tf_op jit(solution)/shard_map/ppermute | solution.py:19
  105.3 19.8 %all-to-all-start = ((f32[32,2,2048]{2,1,0:T(2,128)}), f32[32,2,2048]{2,1,0:T(2,128)S(1)}, u32[]{:S(2)}, u32[]{:S(2)}) async-start(f32[32,2,2048]{2,1,0:T(2,128)} %bitcast.109), calls=%async_computation | async-start | bytes 1048576 | tf_op jit(solution)/shard_map/all_to_all | solution.py:175
  111.4 5.1 %collective-permute-start.16 = (f32[1,1,1,8,8,128]{5,4,3,2,1,0:T(8,128)S(1)}, f32[1,1,1,8,8,128]{5,4,3,2,1,0:T(8,128)S(1)}, u32[]{:S(2)}, u32[]{:S(2)}) collective-permute-start(f32[1,1,1,8,8,128]{5,4,3,2,1,0:T(8,128)S(1)} %get-tuple-element.53), channel_id=1, source_target_pairs={{0,4},{4,8},{8,12},{12,16},{16,20},{20,24},{24,28},{1,5},{5,9},{9,... | collective-permute-start | bytes 98312 | tf_op jit(solution)/shard_map/ppermute | solution.py:16
  114.8 6.2 %collective-permute-start.17 = (f32[1,1,1,8,8,128]{5,4,3,2,1,0:T(8,128)S(1)}, f32[1,1,1,8,8,128]{5,4,3,2,1,0:T(8,128)S(1)}, u32[]{:S(2)}, u32[]{:S(2)}) collective-permute-start(f32[1,1,1,8,8,128]{5,4,3,2,1,0:T(8,128)S(1)} %get-tuple-element.54), channel_id=1, source_target_pairs={{4,0},{8,4},{12,8},{16,12},{20,16},{24,20},{28,24},{5,1},{9,5},{13... | collective-permute-start | bytes 98312 | tf_op jit(solution)/shard_map/ppermute | solution.py:19
  125.4 5.2 %collective-permute-start.18 = (f32[1,1,1,8,8,128]{5,3,4,2,1,0:T(8,128)S(1)}, f32[1,1,1,8,8,128]{5,3,4,2,1,0:T(8,128)S(1)}, u32[]{:S(2)}, u32[]{:S(2)}) collective-permute-start(f32[1,1,1,8,8,128]{5,3,4,2,1,0:T(8,128)S(1)} %maximum_bitcast_fusion.13), channel_id=1, source_target_pairs={{0,1},{1,2},{2,3},{4,5},{5,6},{6,7},{8,9},{9,10},{10,11},{12,13},{... | collective-permute-start | bytes 98312 | tf_op jit(solution)/shard_map/ppermute | solution.py:16
  130.6 6.1 %collective-permute-start.19 = (f32[1,1,1,8,8,128]{5,3,4,2,1,0:T(8,128)S(1)}, f32[1,1,1,8,8,128]{5,3,4,2,1,0:T(8,128)S(1)}, u32[]{:S(2)}, u32[]{:S(2)}) collective-permute-start(f32[1,1,1,8,8,128]{5,3,4,2,1,0:T(8,128)S(1)} %get-tuple-element.27), channel_id=1, source_target_pairs={{1,0},{2,1},{3,2},{5,4},{6,5},{7,6},{9,8},{10,9},{11,10},{13,12},{... | collective-permute-start | bytes 98312 | tf_op jit(solution)/shard_map/ppermute | solution.py:19
  133.3 11.2 %all-to-all-start.1 = ((f32[8,2,2048]{2,1,0:T(2,128)}), f32[8,2,2048]{2,1,0:T(2,128)S(1)}, u32[]{:S(2)}, u32[]{:S(2)}) async-start(f32[8,2,2048]{2,1,0:T(2,128)} %broadcast_in_dim.163), calls=%async_computation.1 | async-start | bytes 262144 | tf_op jit(solution)/shard_map/all_to_all | solution.py:182

commit v8 on v7

--- a/solution.py
+++ b/solution.py
@@ -19,6 +19,20 @@
         high = lax.ppermute(lax.slice_in_dim(block, 0, width, axis=dim), axis, backward)
         block = jnp.concatenate([low, block, high], axis=dim)
     return block
+
+
+def padded_swap(block, axis, dim):
+    count = lax.axis_size(axis)
+    here = lax.axis_index(axis)
+    lower = lax.slice_in_dim(block, 0, 1, axis=dim)
+    upper = lax.slice_in_dim(block, block.shape[dim] - 1, None, axis=dim)
+    slots = lax.broadcasted_iota(jnp.int32, (count,) + (1,) * lower.ndim, 0)
+    zero = jnp.zeros_like(upper)
+    outgoing = jnp.where(slots == here + 1, upper[None], jnp.where(slots == here - 1, lower[None], zero[None]))
+    incoming = lax.all_to_all(outgoing, axis, 0, 0, tiled=True)
+    low = jnp.sum(jnp.where(slots == here - 1, incoming, 0.0), axis=0)
+    high = jnp.sum(jnp.where(slots == here + 1, incoming, 0.0), axis=0)
+    return jnp.concatenate([low, block, high], axis=dim)
 
 
 def gll_tables():
@@ -123,7 +137,7 @@
     values_in = combine(values_in, 3, 1, lower, upper, padded[:, :1], padded[:, 3:])
     lower, upper = faces(values_in, 4)
     rim_faces = jnp.concatenate([lower, upper], 2)
-    padded = padded_2(rim_faces, (("ey", 2),), 1)
+    padded = padded_swap(rim_faces, "ey", 2)
     values_in = combine(values_in, 4, 2, lower, upper, padded[:, :, :1], padded[:, :, 3:])
     lower, upper = faces(values_in, 5)
     empty = jnp.zeros_like(upper[..., :1])

time: 146 us -> 152 us (1.041)
  the two profiles are of different devices: /device:TPU:2 before, /device:TPU:0 now
where the time goes in v8:
time: 152 us; the launch traced here: 151 us
  starting transfers between devices  55.4 us (36%)
  waiting for transfers between devices  37.5 us (25%)
  other arithmetic  30.6 us (20%)
  matrix products  19.5 us (13%)
  local copies, waits for them, and re-layouts  6.41 us (4%)
  between operations  1.65 us (1%)
    ppermute x5, starting transfers between devices, padded_2(): lax.ppermute(lax.slice_in_dim(block, block.shape[dim] - width, None, axis...  22 us
    all_to_all x5, starting transfers between devices, padded_swap(): incoming = lax.all_to_all(outgoing, axis, 0, 0, tiled=True)  16.7 us
    ppermute x5, waiting for transfers between devices, padded_2(): lax.ppermute(lax.slice_in_dim(block, 0, width, axis=dim), axis, backward)  14.3 us
    all_to_all x5, waiting for transfers between devices, padded_swap(): incoming = lax.all_to_all(outgoing, axis, 0, 0, tiled=True)  12.1 us
    mul x2, other arithmetic, segment_sum(): hit_lane * part[:, None]  9.16 us
    dot_general x2, matrix products, gather_flat(): picked = jnp.dot(hit_row, parts, preferred_element_type=jnp.float32)  7.75 us
    reduce_sum x2, other arithmetic, gather_flat(): return jnp.sum(jnp.where(hit_lane, picked, 0.0), axis=1)  7.38 us
    all_to_all x1, starting transfers between devices, strip_reduce(): return lax.all_to_all(chunks, ('ex', 'ey'), 0, 0, tiled=True).sum(0)  6.68 us
  transfers between devices with their start and end apart: 17, of which 12 were waited for; matrix products, arithmetic and copies ran while one was open for 18% of the time, Pallas kernels for 0%

profile of v8, /device:TPU:0, one launch (start us, length us, event | category | flops | bytes accessed | tf_op | source)
XLA Modules:
  0.0 151.0 jit_solution(3983514868222541588)
XLA Ops:
  1.3 1.0 copy.332
  2.3 0.7 broadcast_multiply_fusion.7
  3.1 0.8 broadcast_multiply_fusion
  3.8 0.8 fusion.101
  4.7 4.9 %collective-permute-start = (f32[2,1,1,8,8,128]{5,3,0,4,2,1:T(8,128)S(1)}, f32[2,1,1,8,8,128]{5,3,0,4,2,1:T(8,128)S(1)}, u32[]{:S(2)}, u32[]{:S(2)}) collective-permute-start(f32[2,1,1,8,8,128]{5,3,0,4,2,1:T(8,128)S(1)} %maximum_bitcast_fusion.5), channel_id=1, source_target_pairs={{0,4},{4,8},{8,12},{12,16},{16,20},{20,24},{24,28},{1,5},{5,9},{9,... | collective-permute-start | bytes 196616 | tf_op jit(solution)/shard_map/ppermute | solution.py:16
  10.3 0.7 add_select_fusion.3
  11.8 1.3 collective-permute-start.1
  13.1 4.9 %collective-permute-done.1 = f32[2,1,1,8,8,128]{5,3,0,4,2,1:T(8,128)S(1)} collective-permute-done((f32[2,1,1,8,8,128]{5,3,0,4,2,1:T(8,128)S(1)}, f32[2,1,1,8,8,128]{5,3,0,4,2,1:T(8,128)S(1)}, u32[]{:S(2)}, u32[]{:S(2)}) %collective-permute-start.1) | collective-permute-done | bytes 65568 | tf_op jit(solution)/shard_map/ppermute | solution.py:19
  18.1 0.8 select_select_fusion
  18.9 3.4 %all-to-all-start = ((f32[4,2,1,1,8,8,128]{6,5,4,3,2,1,0:T(8,128)}), f32[4,2,1,1,8,8,128]{6,5,4,3,2,1,0:T(8,128)S(1)}, u32[]{:S(2)}, u32[]{:S(2)}) async-start(f32[4,2,1,1,8,8,128]{6,5,4,3,2,1,0:T(8,128)} %select_select_fusion), calls=%async_computation | async-start | bytes 524288 | tf_op jit(solution)/shard_map/all_to_all | solution.py:32
  22.3 5.5 %fusion.23 = (bf16[4096,256]{1,0:T(8,128)(2,1)S(1)}, bf16[4096,256]{1,0:T(8,128)(2,1)}, bf16[4096,256]{1,0:T(8,128)(2,1)}) fusion(s32[4096]{0:T(1024)S(1)} %get-tuple-element.98, bf16[4096]{0:T(1024)(128)(2,1)S(1)} %get-tuple-element.109, bf16[4096]{0:T(1024)(128)(2,1)S(1)} %get-tuple-element.110, bf16[4096]{0:T(1024)(128)(2,1)S(1)} %get-tuple-element.111), kind=kLoop, calls=%fused_computation.30 | loop fusion | flops 4194304 | bytes 6332416 | tf_op jit(solution)/shard_map/mul | solution.py:173
  30.0 0.9 fusion.33
  31.0 4.8 %collective-permute-start.2 = (f32[1,1,1,8,8,128]{5,4,3,2,1,0:T(8,128)S(1)}, f32[1,1,1,8,8,128]{5,4,3,2,1,0:T(8,128)S(1)}, u32[]{:S(2)}, u32[]{:S(2)}) collective-permute-start(f32[1,1,1,8,8,128]{5,4,3,2,1,0:T(8,128)S(1)} %bitcast.452), channel_id=1, source_target_pairs={{0,4},{4,8},{8,12},{12,16},{16,20},{20,24},{24,28},{1,5},{5,9},{9,... | collective-permute-start | bytes 98312 | tf_op jit(solution)/shard_map/ppermute | solution.py:16
  35.8 1.3 collective-permute-start.3
  37.1 3.4 %fusion = f32[256,768]{1,0:T(8,128)} fusion(bf16[4096,256]{1,0:T(8,128)(2,1)S(1)} %copy-done, bf16[4096,256]{1,0:T(8,128)(2,1)S(1)} %copy-done.1, bf16[4096,256]{1,0:T(8,128)(2,1)S(1)} %get-tuple-element.106, s32[4096]{0:T(1024)S(1)} %get-tuple-element.97), kind=kOutput, calls=%fused_computation | convolution fusion | flops 1630535680 | bytes 7094272 | tf_op jit(solution)/shard_map/dot_general | solution.py:175
  40.6 1.0 collective-permute-done.3
  42.4 3.3 %all-to-all-start.1 = ((f32[4,1,1,1,8,8,128]{6,5,4,3,2,1,0:T(8,128)}), f32[4,1,1,1,8,8,128]{6,5,4,3,2,1,0:T(8,128)S(1)}, u32[]{:S(2)}, u32[]{:S(2)}) async-start(f32[4,1,1,1,8,8,128]{6,5,4,3,2,1,0:T(8,128)} %select_select_fusion.4), calls=%async_computation.1 | async-start | bytes 262144 | tf_op jit(solution)/shard_map/all_to_all | solution.py:32
  45.8 1.2 fusion.75
  47.1 3.3 %all-to-all-done.1 = f32[4,1,1,1,8,8,128]{6,5,4,3,2,1,0:T(8,128)S(1)} async-done(((f32[4,1,1,1,8,8,128]{6,5,4,3,2,1,0:T(8,128)}), f32[4,1,1,1,8,8,128]{6,5,4,3,2,1,0:T(8,128)S(1)}, u32[]{:S(2)}, u32[]{:S(2)}) %all-to-all-start.1) | async-done | bytes 131104 | tf_op jit(solution)/shard_map/all_to_all | solution.py:32
  52.6 4.3 %collective-permute-start.4 = (f32[1,1,1,8,8,128]{5,3,4,2,1,0:T(8,128)S(1)}, f32[1,1,1,8,8,128]{5,3,4,2,1,0:T(8,128)S(1)}, u32[]{:S(2)}, u32[]{:S(2)}) collective-permute-start(f32[1,1,1,8,8,128]{5,3,4,2,1,0:T(8,128)S(1)} %get-tuple-element.89), channel_id=1, source_target_pairs={{0,4},{4,8},{8,12},{12,16},{16,20},{20,24},{24,28},{1,5},{5,9},{9,... | collective-permute-start | bytes 98312 | tf_op jit(solution)/shard_map/ppermute | solution.py:16
  56.9 1.3 collective-permute-start.5
  58.5 4.2 %collective-permute-done.5 = f32[1,1,1,8,8,128]{5,3,4,2,1,0:T(8,128)S(1)} collective-permute-done((f32[1,1,1,8,8,128]{5,3,4,2,1,0:T(8,128)S(1)}, f32[1,1,1,8,8,128]{5,3,4,2,1,0:T(8,128)S(1)}, u32[]{:S(2)}, u32[]{:S(2)}) %collective-permute-start.5) | collective-permute-done | bytes 32800 | tf_op jit(solution)/shard_map/ppermute | solution.py:19
  62.8 0.7 select_select_fusion.3
  63.5 3.3 %all-to-all-start.2 = ((f32[4,1,1,1,8,8,128]{6,5,4,3,2,1,0:T(8,128)}), f32[4,1,1,1,8,8,128]{6,5,4,3,2,1,0:T(8,128)S(1)}, u32[]{:S(2)}, u32[]{:S(2)}) async-start(f32[4,1,1,1,8,8,128]{6,5,4,3,2,1,0:T(8,128)} %select_select_fusion.3), calls=%async_computation.2 | async-start | bytes 262144 | tf_op jit(solution)/shard_map/all_to_all | solution.py:32
  67.0 4.5 %all-to-all-done.2 = f32[4,1,1,1,8,8,128]{6,5,4,3,2,1,0:T(8,128)S(1)} async-done(((f32[4,1,1,1,8,8,128]{6,5,4,3,2,1,0:T(8,128)}), f32[4,1,1,1,8,8,128]{6,5,4,3,2,1,0:T(8,128)S(1)}, u32[]{:S(2)}, u32[]{:S(2)}) %all-to-all-start.2) | async-done | bytes 131104 | tf_op jit(solution)/shard_map/all_to_all | solution.py:32
  74.0 4.5 %collective-permute-start.6 = (f32[1,1,1,8,8,128]{5,3,4,2,1,0:T(8,128)S(1)}, f32[1,1,1,8,8,128]{5,3,4,2,1,0:T(8,128)S(1)}, u32[]{:S(2)}, u32[]{:S(2)}) collective-permute-start(f32[1,1,1,8,8,128]{5,3,4,2,1,0:T(8,128)S(1)} %get-tuple-element.79), channel_id=1, source_target_pairs={{0,4},{4,8},{8,12},{12,16},{16,20},{20,24},{24,28},{1,5},{5,9},{9,... | collective-permute-start | bytes 98312 | tf_op jit(solution)/shard_map/ppermute | solution.py:16
  78.5 1.5 collective-permute-start.7
  80.0 5.7 %fusion.17 = f32[4096,768]{0,1:T(8,128)} fusion(s32[4096]{0:T(1024)S(1)} %get-tuple-element.105, bf16[256,256]{1,0:T(8,128)(2,1)S(1)} %get-tuple-element.69, bf16[256,256]{1,0:T(8,128)(2,1)S(1)} %get-tuple-element.70, bf16[256,256]{1,0:T(8,128)(2,1)S(1)} %get-tuple-element.68), kind=kOutput, calls=%fused_computation.22 | convolution fusion | flops 1612840960 | bytes 12992512 | tf_op jit(solution)/shard_map/dot_general | solution.py:164
  85.8 0.7 select_select_fusion.2
  86.5 3.3 %all-to-all-start.3 = ((f32[4,1,1,1,8,8,128]{6,5,4,3,2,1,0:T(8,128)}), f32[4,1,1,1,8,8,128]{6,5,4,3,2,1,0:T(8,128)S(1)}, u32[]{:S(2)}, u32[]{:S(2)}) async-start(f32[4,1,1,1,8,8,128]{6,5,4,3,2,1,0:T(8,128)} %select_select_fusion.2), calls=%async_computation.3 | async-start | bytes 262144 | tf_op jit(solution)/shard_map/all_to_all | solution.py:32
  89.9 6.0 %fusion.15 = f32[4096]{0:T(1024)S(1)} fusion(f32[4096,768]{0,1:T(8,128)} %fusion.17, s32[4096]{0:T(1024)S(1)} %get-tuple-element.104), kind=kLoop, calls=%fused_computation.18 | loop fusion | flops 5238784 | bytes 12615680 | tf_op jit(solution)/shard_map/reduce_sum | solution.py:167
  97.0 2.0 %fusion.16 = f32[4096,768]{0,1:T(8,128)S(1)} fusion(s32[4096]{0:T(1024)S(1)} %get-tuple-element.105, bf16[256,256]{1,0:T(8,128)(2,1)S(1)} %get-tuple-element.64, bf16[256,256]{1,0:T(8,128)(2,1)S(1)} %get-tuple-element.65, bf16[256,256]{1,0:T(8,128)(2,1)S(1)} %get-tuple-element.63), kind=kOutput, calls=%fused_computation.21 | convolution fusion | flops 1612840960 | bytes 12992512 | tf_op jit(solution)/shard_map/dot_general | solution.py:164
  99.0 1.4 fusion.13
  100.5 3.6 %fusion.20 = (bf16[4096,256]{1,0:T(8,128)(2,1)S(1)}, bf16[4096,256]{1,0:T(8,128)(2,1)S(1)}, bf16[4096,256]{1,0:T(8,128)(2,1)S(1)}) fusion(s32[4096]{0:T(1024)S(1)} %get-tuple-element.98, bf16[4096]{0:T(1024)(128)(2,1)S(1)} %get-tuple-element.37, bf16[4096]{0:T(1024)(128)(2,1)S(1)} %get-tuple-element.103, bf16[4096]{0:T(1024)(128)(2,1)S(1)} %get-tuple-element.102), kind=kLoop, calls=%fused_computation.27 | loop fusion | flops 4194304 | bytes 6332416 | tf_op jit(solution)/shard_map/mul | solution.py:173
  104.1 2.6 %fusion.6 = f32[256,768]{1,0:T(8,128)S(1)} fusion(bf16[4096,256]{1,0:T(8,128)(2,1)S(1)} %get-tuple-element.100, bf16[4096,256]{1,0:T(8,128)(2,1)S(1)} %get-tuple-element.101, bf16[4096,256]{1,0:T(8,128)(2,1)S(1)} %get-tuple-element.99, s32[4096]{0:T(1024)S(1)} %get-tuple-element.97), kind=kOutput, calls=%fused_computation.6 | convolution fusion | flops 1630535680 | bytes 7094272 | tf_op jit(solution)/shard_map/dot_general | solution.py:175
  106.8 1.2 copy.263
  108.0 6.7 %all-to-all-start.4 = ((f32[32,2,2048]{2,1,0:T(2,128)}), f32[32,2,2048]{2,1,0:T(2,128)S(1)}, u32[]{:S(2)}, u32[]{:S(2)}) async-start(f32[32,2,2048]{2,1,0:T(2,128)} %bitcast.106), calls=%async_computation.4 | async-start | bytes 1048576 | tf_op jit(solution)/shard_map/all_to_all | solution.py:189
  116.2 3.5 %collective-permute-start.8 = (f32[1,1,1,8,8,128]{5,3,4,2,1,0:T(8,128)S(1)}, f32[1,1,1,8,8,128]{5,3,4,2,1,0:T(8,128)S(1)}, u32[]{:S(2)}, u32[]{:S(2)}) collective-permute-start(f32[1,1,1,8,8,128]{5,3,4,2,1,0:T(8,128)S(1)} %get-tuple-element.66), channel_id=1, source_target_pairs={{0,4},{4,8},{8,12},{12,16},{16,20},{20,24},{24,28},{1,5},{5,9},{9,... | collective-permute-start | bytes 98312 | tf_op jit(solution)/shard_map/ppermute | solution.py:16
  119.6 1.3 collective-permute-start.9
  121.5 4.3 %collective-permute-done.9 = f32[1,1,1,8,8,128]{5,3,4,2,1,0:T(8,128)S(1)} collective-permute-done((f32[1,1,1,8,8,128]{5,3,4,2,1,0:T(8,128)S(1)}, f32[1,1,1,8,8,128]{5,3,4,2,1,0:T(8,128)S(1)}, u32[]{:S(2)}, u32[]{:S(2)}) %collective-permute-start.9) | collective-permute-done | bytes 32800 | tf_op jit(solution)/shard_map/ppermute | solution.py:19
  125.8 4.3 %all-to-all-done.4 = f32[32,2,2048]{2,1,0:T(2,128)S(1)} async-done(((f32[32,2,2048]{2,1,0:T(2,128)}), f32[32,2,2048]{2,1,0:T(2,128)S(1)}, u32[]{:S(2)}, u32[]{:S(2)}) %all-to-all-start.4) | async-done | bytes 524320 | tf_op jit(solution)/shard_map/all_to_all | solution.py:189
  130.3 0.7 select_select_fusion.1
  131.0 3.3 %all-to-all-start.5 = ((f32[4,1,1,1,8,8,128]{6,5,4,3,2,1,0:T(8,128)}), f32[4,1,1,1,8,8,128]{6,5,4,3,2,1,0:T(8,128)S(1)}, u32[]{:S(2)}, u32[]{:S(2)}) async-start(f32[4,1,1,1,8,8,128]{6,5,4,3,2,1,0:T(8,128)} %select_select_fusion.1), calls=%async_computation.5 | async-start | bytes 262144 | tf_op jit(solution)/shard_map/all_to_all | solution.py:32
  134.4 0.8 copy.272
  135.1 3.8 %all-to-all-done.5 = f32[4,1,1,1,8,8,128]{6,5,4,3,2,1,0:T(8,128)S(1)} async-done(((f32[4,1,1,1,8,8,128]{6,5,4,3,2,1,0:T(8,128)}), f32[4,1,1,1,8,8,128]{6,5,4,3,2,1,0:T(8,128)S(1)}, u32[]{:S(2)}, u32[]{:S(2)}) %all-to-all-start.5) | async-done | bytes 131104 | tf_op jit(solution)/shard_map/all_to_all | solution.py:32
  139.6 3.4 %all-to-all-start.6 = ((f32[8,2,2048]{2,1,0:T(2,128)}), f32[8,2,2048]{2,1,0:T(2,128)S(1)}, u32[]{:S(2)}, u32[]{:S(2)}) async-start(f32[8,2,2048]{2,1,0:T(2,128)} %broadcast_in_dim.364), calls=%async_computation.6 | async-start | bytes 262144 | tf_op jit(solution)/shard_map/all_to_all | solution.py:196
  143.4 0.8 copy.273
  144.2 6.1 %all-to-all-done.6 = f32[8,2,2048]{2,1,0:T(2,128)S(1)} async-done(((f32[8,2,2048]{2,1,0:T(2,128)}), f32[8,2,2048]{2,1,0:T(2,128)S(1)}, u32[]{:S(2)}, u32[]{:S(2)}) %all-to-all-start.6) | async-done | bytes 131104 | tf_op jit(solution)/shard_map/all_to_all | solution.py:196
  (137 shorter events, 15.5 us)
Async XLA Ops:
  4.7 7.1 %collective-permute-start = (f32[2,1,1,8,8,128]{5,3,0,4,2,1:T(8,128)S(1)}, f32[2,1,1,8,8,128]{5,3,0,4,2,1:T(8,128)S(1)}, u32[]{:S(2)}, u32[]{:S(2)}) collective-permute-start(f32[2,1,1,8,8,128]{5,3,0,4,2,1:T(8,128)S(1)} %maximum_bitcast_fusion.5), channel_id=1, source_target_pairs={{0,4},{4,8},{8,12},{12,16},{16,20},{20,24},{24,28},{1,5},{5,9},{9,... | collective-permute-start | bytes 196616 | tf_op jit(solution)/shard_map/ppermute | solution.py:16
  11.8 6.2 %collective-permute-start.1 = (f32[2,1,1,8,8,128]{5,3,0,4,2,1:T(8,128)S(1)}, f32[2,1,1,8,8,128]{5,3,0,4,2,1:T(8,128)S(1)}, u32[]{:S(2)}, u32[]{:S(2)}) collective-permute-start(f32[2,1,1,8,8,128]{5,3,0,4,2,1:T(8,128)S(1)} %get-tuple-element.44), channel_id=1, source_target_pairs={{4,0},{8,4},{12,8},{16,12},{20,16},{24,20},{28,24},{5,1},{9,5},{13... | collective-permute-start | bytes 196616 | tf_op jit(solution)/shard_map/ppermute | solution.py:19
  18.9 9.4 %all-to-all-start = ((f32[4,2,1,1,8,8,128]{6,5,4,3,2,1,0:T(8,128)}), f32[4,2,1,1,8,8,128]{6,5,4,3,2,1,0:T(8,128)S(1)}, u32[]{:S(2)}, u32[]{:S(2)}) async-start(f32[4,2,1,1,8,8,128]{6,5,4,3,2,1,0:T(8,128)} %select_select_fusion), calls=%async_computation | async-start | bytes 524288 | tf_op jit(solution)/shard_map/all_to_all | solution.py:32
  27.8 1.3 copy-start.4
  27.8 1.4 copy-start.2
  28.6 8.6 %copy-start = (bf16[4096,256]{1,0:T(8,128)(2,1)S(1)}, bf16[4096,256]{1,0:T(8,128)(2,1)}, u32[]{:S(2)}) copy-start(bf16[4096,256]{1,0:T(8,128)(2,1)} %get-tuple-element.107) | copy-start | bytes 6291460
  28.6 8.6 %copy-start.1 = (bf16[4096,256]{1,0:T(8,128)(2,1)S(1)}, bf16[4096,256]{1,0:T(8,128)(2,1)}, u32[]{:S(2)}) copy-start(bf16[4096,256]{1,0:T(8,128)(2,1)} %get-tuple-element.108) | copy-start | bytes 6291460
  31.0 9.6 %collective-permute-start.2 = (f32[1,1,1,8,8,128]{5,4,3,2,1,0:T(8,128)S(1)}, f32[1,1,1,8,8,128]{5,4,3,2,1,0:T(8,128)S(1)}, u32[]{:S(2)}, u32[]{:S(2)}) collective-permute-start(f32[1,1,1,8,8,128]{5,4,3,2,1,0:T(8,128)S(1)} %bitcast.452), channel_id=1, source_target_pairs={{0,4},{4,8},{8,12},{12,16},{16,20},{20,24},{24,28},{1,5},{5,9},{9,... | collective-permute-start | bytes 98312 | tf_op jit(solution)/shard_map/ppermute | solution.py:16
  35.8 5.8 %collective-permute-start.3 = (f32[1,1,1,8,8,128]{5,4,3,2,1,0:T(8,128)S(1)}, f32[1,1,1,8,8,128]{5,4,3,2,1,0:T(8,128)S(1)}, u32[]{:S(2)}, u32[]{:S(2)}) collective-permute-start(f32[1,1,1,8,8,128]{5,4,3,2,1,0:T(8,128)S(1)} %bitcast.454), channel_id=1, source_target_pairs={{4,0},{8,4},{12,8},{16,12},{20,16},{24,20},{28,24},{5,1},{9,5},{13... | collective-permute-start | bytes 98312 | tf_op jit(solution)/shard_map/ppermute | solution.py:19
  42.4 7.9 %all-to-all-start.1 = ((f32[4,1,1,1,8,8,128]{6,5,4,3,2,1,0:T(8,128)}), f32[4,1,1,1,8,8,128]{6,5,4,3,2,1,0:T(8,128)S(1)}, u32[]{:S(2)}, u32[]{:S(2)}) async-start(f32[4,1,1,1,8,8,128]{6,5,4,3,2,1,0:T(8,128)} %select_select_fusion.4), calls=%async_computation.1 | async-start | bytes 262144 | tf_op jit(solution)/shard_map/all_to_all | solution.py:32
  46.9 19.9 %copy-start.5 = (s32[1,4096]{1,0:T(1,128)S(1)}, s32[1,4096]{1,0:T(1,128)}, u32[]{:S(2)}) copy-start(s32[1,4096]{1,0:T(1,128)} %param.38) | copy-start | bytes 49156
  52.6 5.9 %collective-permute-start.4 = (f32[1,1,1,8,8,128]{5,3,4,2,1,0:T(8,128)S(1)}, f32[1,1,1,8,8,128]{5,3,4,2,1,0:T(8,128)S(1)}, u32[]{:S(2)}, u32[]{:S(2)}) collective-permute-start(f32[1,1,1,8,8,128]{5,3,4,2,1,0:T(8,128)S(1)} %get-tuple-element.89), channel_id=1, source_target_pairs={{0,4},{4,8},{8,12},{12,16},{16,20},{20,24},{24,28},{1,5},{5,9},{9,... | collective-permute-start | bytes 98312 | tf_op jit(solution)/shard_map/ppermute | solution.py:16
  56.9 5.8 %collective-permute-start.5 = (f32[1,1,1,8,8,128]{5,3,4,2,1,0:T(8,128)S(1)}, f32[1,1,1,8,8,128]{5,3,4,2,1,0:T(8,128)S(1)}, u32[]{:S(2)}, u32[]{:S(2)}) collective-permute-start(f32[1,1,1,8,8,128]{5,3,4,2,1,0:T(8,128)S(1)} %get-tuple-element.90), channel_id=1, source_target_pairs={{4,0},{8,4},{12,8},{16,12},{20,16},{24,20},{28,24},{5,1},{9,5},{13... | collective-permute-start | bytes 98312 | tf_op jit(solution)/shard_map/ppermute | solution.py:19
  63.5 7.9 %all-to-all-start.2 = ((f32[4,1,1,1,8,8,128]{6,5,4,3,2,1,0:T(8,128)}), f32[4,1,1,1,8,8,128]{6,5,4,3,2,1,0:T(8,128)S(1)}, u32[]{:S(2)}, u32[]{:S(2)}) async-start(f32[4,1,1,1,8,8,128]{6,5,4,3,2,1,0:T(8,128)} %select_select_fusion.3), calls=%async_computation.2 | async-start | bytes 262144 | tf_op jit(solution)/shard_map/all_to_all | solution.py:32
  74.0 11.7 %collective-permute-start.6 = (f32[1,1,1,8,8,128]{5,3,4,2,1,0:T(8,128)S(1)}, f32[1,1,1,8,8,128]{5,3,4,2,1,0:T(8,128)S(1)}, u32[]{:S(2)}, u32[]{:S(2)}) collective-permute-start(f32[1,1,1,8,8,128]{5,3,4,2,1,0:T(8,128)S(1)} %get-tuple-element.79), channel_id=1, source_target_pairs={{0,4},{4,8},{8,12},{12,16},{16,20},{20,24},{24,28},{1,5},{5,9},{9,... | collective-permute-start | bytes 98312 | tf_op jit(solution)/shard_map/ppermute | solution.py:16
  78.5 7.3 %collective-permute-start.7 = (f32[1,1,1,8,8,128]{5,3,4,2,1,0:T(8,128)S(1)}, f32[1,1,1,8,8,128]{5,3,4,2,1,0:T(8,128)S(1)}, u32[]{:S(2)}, u32[]{:S(2)}) collective-permute-start(f32[1,1,1,8,8,128]{5,3,4,2,1,0:T(8,128)S(1)} %get-tuple-element.80), channel_id=1, source_target_pairs={{4,0},{8,4},{12,8},{16,12},{20,16},{24,20},{28,24},{5,1},{9,5},{13... | collective-permute-start | bytes 98312 | tf_op jit(solution)/shard_map/ppermute | solution.py:19
  86.5 9.4 %all-to-all-start.3 = ((f32[4,1,1,1,8,8,128]{6,5,4,3,2,1,0:T(8,128)}), f32[4,1,1,1,8,8,128]{6,5,4,3,2,1,0:T(8,128)S(1)}, u32[]{:S(2)}, u32[]{:S(2)}) async-start(f32[4,1,1,1,8,8,128]{6,5,4,3,2,1,0:T(8,128)} %select_select_fusion.2), calls=%async_computation.3 | async-start | bytes 262144 | tf_op jit(solution)/shard_map/all_to_all | solution.py:32
  99.0 1.4 copy-start.3
  108.0 22.0 %all-to-all-start.4 = ((f32[32,2,2048]{2,1,0:T(2,128)}), f32[32,2,2048]{2,1,0:T(2,128)S(1)}, u32[]{:S(2)}, u32[]{:S(2)}) async-start(f32[32,2,2048]{2,1,0:T(2,128)} %bitcast.106), calls=%async_computation.4 | async-start | bytes 1048576 | tf_op jit(solution)/shard_map/all_to_all | solution.py:189
  116.2 5.3 %collective-permute-start.8 = (f32[1,1,1,8,8,128]{5,3,4,2,1,0:T(8,128)S(1)}, f32[1,1,1,8,8,128]{5,3,4,2,1,0:T(8,128)S(1)}, u32[]{:S(2)}, u32[]{:S(2)}) collective-permute-start(f32[1,1,1,8,8,128]{5,3,4,2,1,0:T(8,128)S(1)} %get-tuple-element.66), channel_id=1, source_target_pairs={{0,4},{4,8},{8,12},{12,16},{16,20},{20,24},{24,28},{1,5},{5,9},{9,... | collective-permute-start | bytes 98312 | tf_op jit(solution)/shard_map/ppermute | solution.py:16
  119.6 6.1 %collective-permute-start.9 = (f32[1,1,1,8,8,128]{5,3,4,2,1,0:T(8,128)S(1)}, f32[1,1,1,8,8,128]{5,3,4,2,1,0:T(8,128)S(1)}, u32[]{:S(2)}, u32[]{:S(2)}) collective-permute-start(f32[1,1,1,8,8,128]{5,3,4,2,1,0:T(8,128)S(1)} %get-tuple-element.67), channel_id=1, source_target_pairs={{4,0},{8,4},{12,8},{16,12},{20,16},{24,20},{28,24},{5,1},{9,5},{13... | collective-permute-start | bytes 98312 | tf_op jit(solution)/shard_map/ppermute | solution.py:19
  131.0 7.9 %all-to-all-start.5 = ((f32[4,1,1,1,8,8,128]{6,5,4,3,2,1,0:T(8,128)}), f32[4,1,1,1,8,8,128]{6,5,4,3,2,1,0:T(8,128)S(1)}, u32[]{:S(2)}, u32[]{:S(2)}) async-start(f32[4,1,1,1,8,8,128]{6,5,4,3,2,1,0:T(8,128)} %select_select_fusion.1), calls=%async_computation.5 | async-start | bytes 262144 | tf_op jit(solution)/shard_map/all_to_all | solution.py:32
  139.6 10.7 %all-to-all-start.6 = ((f32[8,2,2048]{2,1,0:T(2,128)}), f32[8,2,2048]{2,1,0:T(2,128)S(1)}, u32[]{:S(2)}, u32[]{:S(2)}) async-start(f32[8,2,2048]{2,1,0:T(2,128)} %broadcast_in_dim.364), calls=%async_computation.6 | async-start | bytes 262144 | tf_op jit(solution)/shard_map/all_to_all | solution.py:196

commit v9 on v7

--- a/solution.py
+++ b/solution.py
@@ -130,38 +130,47 @@
     return combine(values_in, 5, 5, lower, upper, empty, empty), ride
 
 
-def split3(values):
-    first = lax.reduce_precision(values, exponent_bits=8, mantissa_bits=7)
-    rest = values - first
-    second = lax.reduce_precision(rest, exponent_bits=8, mantissa_bits=7)
-    third = rest - second
-    return [part.astype(jnp.bfloat16) for part in (first, second, third)]
+def split_parts(values, count):
+    parts = []
+    rest = values
+    for _ in range(count - 1):
+        part = lax.reduce_precision(rest, exponent_bits=8, mantissa_bits=7)
+        parts.append(part)
+        rest = rest - part
+    parts.append(lax.reduce_precision(rest, exponent_bits=8, mantissa_bits=7))
+    return [part.astype(jnp.bfloat16) for part in parts]
 
 
 def one_hot(index, count):
     return (index[:, None] == lax.broadcasted_iota(jnp.int32, (1, count), 1)).astype(jnp.bfloat16)
 
 
-def gather_flat(values, picks, lanes):
+def gather_flat(values, picks, lanes, count=3):
     rows = values.shape[0] // lanes
     table = values.reshape(rows, lanes)
-    parts = jnp.concatenate(split3(table), axis=1)
+    parts = jnp.concatenate(split_parts(table, count), axis=1)
     hit_row = one_hot(picks // lanes, rows)
     picked = jnp.dot(hit_row, parts, preferred_element_type=jnp.float32)
-    picked = picked[:, :lanes] + picked[:, lanes : 2 * lanes] + picked[:, 2 * lanes :]
+    pieces = [picked[:, n * lanes : (n + 1) * lanes] for n in range(count)]
+    picked = pieces[0]
+    for piece in pieces[1:]:
+        picked = picked + piece
     hit_lane = (picks % lanes)[:, None] == lax.broadcasted_iota(jnp.int32, (1, lanes), 1)
     return jnp.sum(jnp.where(hit_lane, picked, 0.0), axis=1)
 
 
-def segment_sum(values, ids, bins, lanes):
+def segment_sum(values, ids, bins, lanes, count=3):
     rows = bins // lanes
     hit_lane = one_hot(ids % lanes, lanes)
-    rhs = jnp.concatenate([hit_lane * part[:, None] for part in split3(values)], axis=1)
+    rhs = jnp.concatenate([hit_lane * part[:, None] for part in split_parts(values, count)], axis=1)
     hit_row = one_hot(ids // lanes, rows)
     sums = lax.dot_general(
         hit_row, rhs, (((0,), (0,)), ((), ())), preferred_element_type=jnp.float32
     )
-    return (sums[:, :lanes] + sums[:, lanes : 2 * lanes] + sums[:, 2 * lanes :]).reshape(-1)
+    total = sums[:, :lanes]
+    for n in range(1, count):
+        total = total + sums[:, n * lanes : (n + 1) * lanes]
+    return total.reshape(-1)
 
 
 def strip_reduce(partial, strips, strip_size):
@@ -207,8 +216,8 @@
             early = gather_flat(pressure.reshape(-1), picks, 256)
         applied = element_apply(update, metric, weights, stiff)
         if step + 1 == SWEEPS:
-            samples = early + gather_flat(update.reshape(-1), picks, 256)
-            numer = segment_sum(areas * samples, global_ids, strips * SHELL_STRIP, 256)
+            samples = early + gather_flat(update.reshape(-1), picks, 256, 2)
+            numer = segment_sum(areas * samples, global_ids, strips * SHELL_STRIP, 256, 2)
             partial = jnp.stack([numer, denom])
             assembled, mine = assemble(applied[None], strip_reduce(partial, strips, SHELL_STRIP))
         else:

time: 146 us -> 144 us (0.986)
  transfers between devices with their start and end apart: 22 -> 22, of which waited for: 20 -> 20; matrix products, arithmetic and copies ran while one was open for 11% -> 12% of each run, Pallas kernels for 0% -> 0%
where the time goes in v9:
time: 144 us; the launch traced here: 143 us
  starting transfers between devices  56.2 us (39%)
  waiting for transfers between devices  46 us (32%)
  other arithmetic  20.7 us (14%)
  matrix products  13.4 us (9%)
  local copies, waits for them, and re-layouts  5.26 us (4%)
  between operations  1.55 us (1%)
    ppermute x10, starting transfers between devices, padded_2(): lax.ppermute(lax.slice_in_dim(block, block.shape[dim] - width, None, axis...  30.2 us
    ppermute x10, waiting for transfers between devices, padded_2(): lax.ppermute(lax.slice_in_dim(block, 0, width, axis=dim), axis, backward)  21.8 us
    ppermute x10, starting transfers between devices, padded_2(): lax.ppermute(lax.slice_in_dim(block, 0, width, axis=dim), axis, backward)  17.7 us
    ppermute x10, waiting for transfers between devices, padded_2(): lax.ppermute(lax.slice_in_dim(block, block.shape[dim] - width, None, axis...  13.3 us
    mul x2, other arithmetic, segment_sum(): hit_lane * part[:, None]  6.85 us
    all_to_all x1, waiting for transfers between devices, strip_gather(): whole = lax.all_to_all(spread_out, 'ex', 0, 0, tiled=True)  6.78 us
    all_to_all x1, starting transfers between devices, strip_reduce(): return lax.all_to_all(chunks, ('ex', 'ey'), 0, 0, tiled=True).sum(0)  4.79 us
    dot_general x2, matrix products, segment_sum(): lax.dot_general(hit_row, rhs, (((0,), (0,)), ((), ())), preferred_element...  4.5 us
  transfers between devices with their start and end apart: 22, of which 20 were waited for; matrix products, arithmetic and copies ran while one was open for 12% of the time, Pallas kernels for 0%

profile of v9, /device:TPU:2, one launch (start us, length us, event | category | flops | bytes accessed | tf_op | source)
XLA Modules:
  0.0 143.1 jit_solution(10597926222721807331)
XLA Ops:
  2.9 1.2 fusion.90
  4.8 3.4 %collective-permute-start = (f32[2,1,1,8,8,128]{5,0,4,3,2,1:T(2,128)S(1)}, f32[2,1,1,8,8,128]{5,0,4,3,2,1:T(2,128)S(1)}, u32[]{:S(2)}, u32[]{:S(2)}) collective-permute-start(f32[2,1,1,8,8,128]{5,0,4,3,2,1:T(2,128)S(1)} %maximum_bitcast_fusion.9), channel_id=1, source_target_pairs={{0,4},{4,8},{8,12},{12,16},{16,20},{20,24},{24,28},{1,5},{5,9},{9,... | collective-permute-start | bytes 196616 | tf_op jit(solution)/shard_map/ppermute | solution.py:16
  10.2 0.8 fusion.113
  11.0 1.3 collective-permute-start.1
  12.3 1.3 pad_maximum_fusion.5
  13.9 3.7 %collective-permute-done.1 = f32[2,1,1,8,8,128]{5,0,4,3,2,1:T(2,128)S(1)} collective-permute-done((f32[2,1,1,8,8,128]{5,0,4,3,2,1:T(2,128)S(1)}, f32[2,1,1,8,8,128]{5,0,4,3,2,1:T(2,128)S(1)}, u32[]{:S(2)}, u32[]{:S(2)}) %collective-permute-start.1) | collective-permute-done | bytes 65568 | tf_op jit(solution)/shard_map/ppermute | solution.py:19
  17.6 1.9 %collective-permute-start.2 = (f32[2,1,1,8,8,128]{5,3,0,4,2,1:T(8,128)S(1)}, f32[2,1,1,8,8,128]{5,3,0,4,2,1:T(8,128)S(1)}, u32[]{:S(2)}, u32[]{:S(2)}) collective-permute-start(f32[2,1,1,8,8,128]{5,3,0,4,2,1:T(8,128)S(1)} %maximum_bitcast_fusion.7), channel_id=1, source_target_pairs={{0,1},{1,2},{2,3},{4,5},{5,6},{6,7},{8,9},{9,10},{10,11},{12,13},{... | collective-permute-start | bytes 196616 | tf_op jit(solution)/shard_map/ppermute | solution.py:16
  19.5 3.6 %collective-permute-done.2 = f32[2,1,1,8,8,128]{5,3,0,4,2,1:T(8,128)S(1)} collective-permute-done((f32[2,1,1,8,8,128]{5,3,0,4,2,1:T(8,128)S(1)}, f32[2,1,1,8,8,128]{5,3,0,4,2,1:T(8,128)S(1)}, u32[]{:S(2)}, u32[]{:S(2)}) %collective-permute-start.2) | collective-permute-done | bytes 65568 | tf_op jit(solution)/shard_map/ppermute | solution.py:16
  23.2 1.9 %collective-permute-start.3 = (f32[2,1,1,8,8,128]{5,3,0,4,2,1:T(8,128)S(1)}, f32[2,1,1,8,8,128]{5,3,0,4,2,1:T(8,128)S(1)}, u32[]{:S(2)}, u32[]{:S(2)}) collective-permute-start(f32[2,1,1,8,8,128]{5,3,0,4,2,1:T(8,128)S(1)} %get-tuple-element.41), channel_id=1, source_target_pairs={{1,0},{2,1},{3,2},{5,4},{6,5},{7,6},{9,8},{10,9},{11,10},{13,12},{... | collective-permute-start | bytes 196616 | tf_op jit(solution)/shard_map/ppermute | solution.py:19
  25.6 1.5 %collective-permute-done.3 = f32[2,1,1,8,8,128]{5,3,0,4,2,1:T(8,128)S(1)} collective-permute-done((f32[2,1,1,8,8,128]{5,3,0,4,2,1:T(8,128)S(1)}, f32[2,1,1,8,8,128]{5,3,0,4,2,1:T(8,128)S(1)}, u32[]{:S(2)}, u32[]{:S(2)}) %collective-permute-start.3) | collective-permute-done | bytes 65568 | tf_op jit(solution)/shard_map/ppermute | solution.py:19
  28.8 0.9 fusion.30
  29.8 4.8 %collective-permute-start.4 = (f32[1,1,1,8,8,128]{5,4,3,2,1,0:T(8,128)S(1)}, f32[1,1,1,8,8,128]{5,4,3,2,1,0:T(8,128)S(1)}, u32[]{:S(2)}, u32[]{:S(2)}) collective-permute-start(f32[1,1,1,8,8,128]{5,4,3,2,1,0:T(8,128)S(1)} %bitcast.475), channel_id=1, source_target_pairs={{0,4},{4,8},{8,12},{12,16},{16,20},{20,24},{24,28},{1,5},{5,9},{9,... | collective-permute-start | bytes 98312 | tf_op jit(solution)/shard_map/ppermute | solution.py:16
  34.6 1.3 collective-permute-start.5
  35.9 3.6 %fusion.20 = (bf16[4096,256]{1,0:T(8,128)(2,1)S(1)}, bf16[4096,256]{1,0:T(8,128)(2,1)S(1)}, bf16[4096,256]{1,0:T(8,128)(2,1)S(1)}) fusion(s32[4096]{0:T(1024)S(1)} %get-tuple-element.76, bf16[4096]{0:T(1024)(128)(2,1)S(1)} %get-tuple-element.84, bf16[4096]{0:T(1024)(128)(2,1)S(1)} %get-tuple-element.85, bf16[4096]{0:T(1024)(128)(2,1)S(1)} %get-tuple-element.86), kind=kLoop, calls=%fused_computation.26 | loop fusion | flops 4194304 | bytes 6332416 | tf_op jit(solution)/shard_map/mul | solution.py:165
  40.4 1.9 %collective-permute-start.6 = (f32[1,1,1,8,8,128]{5,3,4,2,1,0:T(8,128)S(1)}, f32[1,1,1,8,8,128]{5,3,4,2,1,0:T(8,128)S(1)}, u32[]{:S(2)}, u32[]{:S(2)}) collective-permute-start(f32[1,1,1,8,8,128]{5,3,4,2,1,0:T(8,128)S(1)} %maximum_bitcast_fusion.19), channel_id=1, source_target_pairs={{0,1},{1,2},{2,3},{4,5},{5,6},{6,7},{8,9},{9,10},{10,11},{12,13},{... | collective-permute-start | bytes 98312 | tf_op jit(solution)/shard_map/ppermute | solution.py:16
  42.3 2.6 %fusion = f32[256,768]{1,0:T(8,128)S(1)} fusion(bf16[4096,256]{1,0:T(8,128)(2,1)S(1)} %get-tuple-element.82, bf16[4096,256]{1,0:T(8,128)(2,1)S(1)} %get-tuple-element.83, bf16[4096,256]{1,0:T(8,128)(2,1)S(1)} %get-tuple-element.81, s32[4096]{0:T(1024)S(1)} %get-tuple-element.75), kind=kOutput, calls=%fused_computation | convolution fusion | flops 1630535680 | bytes 7094272 | tf_op jit(solution)/shard_map/dot_general | solution.py:167
  45.7 2.9 %collective-permute-start.7 = (f32[1,1,1,8,8,128]{5,3,4,2,1,0:T(8,128)S(1)}, f32[1,1,1,8,8,128]{5,3,4,2,1,0:T(8,128)S(1)}, u32[]{:S(2)}, u32[]{:S(2)}) collective-permute-start(f32[1,1,1,8,8,128]{5,3,4,2,1,0:T(8,128)S(1)} %get-tuple-element.37), channel_id=1, source_target_pairs={{1,0},{2,1},{3,2},{5,4},{6,5},{7,6},{9,8},{10,9},{11,10},{13,12},{... | collective-permute-start | bytes 98312 | tf_op jit(solution)/shard_map/ppermute | solution.py:19
  48.8 1.4 collective-permute-done.7
  52.1 4.3 %collective-permute-start.8 = (f32[1,1,1,8,8,128]{5,4,3,2,1,0:T(8,128)S(1)}, f32[1,1,1,8,8,128]{5,4,3,2,1,0:T(8,128)S(1)}, u32[]{:S(2)}, u32[]{:S(2)}) collective-permute-start(f32[1,1,1,8,8,128]{5,4,3,2,1,0:T(8,128)S(1)} %get-tuple-element.65), channel_id=1, source_target_pairs={{0,4},{4,8},{8,12},{12,16},{16,20},{20,24},{24,28},{1,5},{5,9},{9,... | collective-permute-start | bytes 98312 | tf_op jit(solution)/shard_map/ppermute | solution.py:16
  56.4 1.3 collective-permute-start.9
  58.0 4.2 %collective-permute-done.9 = f32[1,1,1,8,8,128]{5,4,3,2,1,0:T(8,128)S(1)} collective-permute-done((f32[1,1,1,8,8,128]{5,4,3,2,1,0:T(8,128)S(1)}, f32[1,1,1,8,8,128]{5,4,3,2,1,0:T(8,128)S(1)}, u32[]{:S(2)}, u32[]{:S(2)}) %collective-permute-start.9) | collective-permute-done | bytes 32800 | tf_op jit(solution)/shard_map/ppermute | solution.py:19
  62.3 1.9 %collective-permute-start.10 = (f32[1,1,1,8,8,128]{5,4,3,2,1,0:T(8,128)S(1)}, f32[1,1,1,8,8,128]{5,4,3,2,1,0:T(8,128)S(1)}, u32[]{:S(2)}, u32[]{:S(2)}) collective-permute-start(f32[1,1,1,8,8,128]{5,4,3,2,1,0:T(8,128)S(1)} %maximum_bitcast_fusion.17), channel_id=1, source_target_pairs={{0,1},{1,2},{2,3},{4,5},{5,6},{6,7},{8,9},{9,10},{10,11},{12,13},{... | collective-permute-start | bytes 98312 | tf_op jit(solution)/shard_map/ppermute | solution.py:16
  64.2 3.3 %collective-permute-done.10 = f32[1,1,1,8,8,128]{5,4,3,2,1,0:T(8,128)S(1)} collective-permute-done((f32[1,1,1,8,8,128]{5,4,3,2,1,0:T(8,128)S(1)}, f32[1,1,1,8,8,128]{5,4,3,2,1,0:T(8,128)S(1)}, u32[]{:S(2)}, u32[]{:S(2)}) %collective-permute-start.10) | collective-permute-done | bytes 32800 | tf_op jit(solution)/shard_map/ppermute | solution.py:16
  67.5 2.1 %collective-permute-start.11 = (f32[1,1,1,8,8,128]{5,4,3,2,1,0:T(8,128)S(1)}, f32[1,1,1,8,8,128]{5,4,3,2,1,0:T(8,128)S(1)}, u32[]{:S(2)}, u32[]{:S(2)}) collective-permute-start(f32[1,1,1,8,8,128]{5,4,3,2,1,0:T(8,128)S(1)} %get-tuple-element.35), channel_id=1, source_target_pairs={{1,0},{2,1},{3,2},{5,4},{6,5},{7,6},{9,8},{10,9},{11,10},{13,12},{... | collective-permute-start | bytes 98312 | tf_op jit(solution)/shard_map/ppermute | solution.py:19
  69.7 1.3 collective-permute-done.11
  73.1 4.7 %collective-permute-start.12 = (f32[1,1,1,8,8,128]{5,4,3,2,1,0:T(8,128)S(1)}, f32[1,1,1,8,8,128]{5,4,3,2,1,0:T(8,128)S(1)}, u32[]{:S(2)}, u32[]{:S(2)}) collective-permute-start(f32[1,1,1,8,8,128]{5,4,3,2,1,0:T(8,128)S(1)} %get-tuple-element.59), channel_id=1, source_target_pairs={{0,4},{4,8},{8,12},{12,16},{16,20},{20,24},{24,28},{1,5},{5,9},{9,... | collective-permute-start | bytes 98312 | tf_op jit(solution)/shard_map/ppermute | solution.py:16
  77.8 1.3 collective-permute-start.13
  79.4 4.2 %collective-permute-done.13 = f32[1,1,1,8,8,128]{5,4,3,2,1,0:T(8,128)S(1)} collective-permute-done((f32[1,1,1,8,8,128]{5,4,3,2,1,0:T(8,128)S(1)}, f32[1,1,1,8,8,128]{5,4,3,2,1,0:T(8,128)S(1)}, u32[]{:S(2)}, u32[]{:S(2)}) %collective-permute-start.13) | collective-permute-done | bytes 32800 | tf_op jit(solution)/shard_map/ppermute | solution.py:19
  83.6 1.9 %collective-permute-start.14 = (f32[1,1,1,8,8,128]{5,4,3,2,1,0:T(8,128)S(1)}, f32[1,1,1,8,8,128]{5,4,3,2,1,0:T(8,128)S(1)}, u32[]{:S(2)}, u32[]{:S(2)}) collective-permute-start(f32[1,1,1,8,8,128]{5,4,3,2,1,0:T(8,128)S(1)} %maximum_bitcast_fusion.15), channel_id=1, source_target_pairs={{0,1},{1,2},{2,3},{4,5},{5,6},{6,7},{8,9},{9,10},{10,11},{12,13},{... | collective-permute-start | bytes 98312 | tf_op jit(solution)/shard_map/ppermute | solution.py:16
  85.5 2.0 %fusion.15 = f32[4096,768]{0,1:T(8,128)S(1)} fusion(s32[4096]{0:T(1024)S(1)} %get-tuple-element.80, bf16[256,256]{1,0:T(8,128)(2,1)S(1)} %get-tuple-element.53, bf16[256,256]{1,0:T(8,128)(2,1)S(1)} %get-tuple-element.54, bf16[256,256]{1,0:T(8,128)(2,1)S(1)} %get-tuple-element.52), kind=kOutput, calls=%fused_computation.19 | convolution fusion | flops 1612840960 | bytes 12992512 | tf_op jit(solution)/shard_map/dot_general | solution.py:153
  87.6 1.3 collective-permute-done.14
  88.9 2.4 %collective-permute-start.15 = (f32[1,1,1,8,8,128]{5,4,3,2,1,0:T(8,128)S(1)}, f32[1,1,1,8,8,128]{5,4,3,2,1,0:T(8,128)S(1)}, u32[]{:S(2)}, u32[]{:S(2)}) collective-permute-start(f32[1,1,1,8,8,128]{5,4,3,2,1,0:T(8,128)S(1)} %get-tuple-element.31), channel_id=1, source_target_pairs={{1,0},{2,1},{3,2},{5,4},{6,5},{7,6},{9,8},{10,9},{11,10},{13,12},{... | collective-permute-start | bytes 98312 | tf_op jit(solution)/shard_map/ppermute | solution.py:19
  91.2 1.4 fusion.9
  94.3 1.4 fusion.14
  95.7 0.9 fusion.7
  96.6 3.2 %fusion.17 = (bf16[4096,256]{1,0:T(8,128)(2,1)S(1)}, bf16[4096,256]{1,0:T(8,128)(2,1)S(1)}) fusion(s32[4096]{0:T(1024)S(1)} %get-tuple-element.76, bf16[4096]{0:T(1024)(128)(2,1)S(1)} %get-tuple-element.73, bf16[4096]{0:T(1024)(128)(2,1)S(1)} %get-tuple-element.74), kind=kLoop, calls=%fused_computation.23 | loop fusion | flops 3145728 | bytes 4227072 | tf_op jit(solution)/shard_map/mul | solution.py:165
  99.9 1.9 %fusion.10 = f32[256,512]{1,0:T(8,128)S(1)} fusion(bf16[4096,256]{1,0:T(8,128)(2,1)S(1)} %get-tuple-element.78, bf16[4096,256]{1,0:T(8,128)(2,1)S(1)} %get-tuple-element.77, s32[4096]{0:T(1024)S(1)} %get-tuple-element.75), kind=kOutput, calls=%fused_computation.13 | convolution fusion | flops 1083179008 | bytes 4734976 | tf_op jit(solution)/shard_map/dot_general | solution.py:167
  101.9 1.2 copy.201
  103.1 4.8 %all-to-all-start = ((f32[32,2,2048]{2,1,0:T(2,128)}), f32[32,2,2048]{2,1,0:T(2,128)S(1)}, u32[]{:S(2)}, u32[]{:S(2)}) async-start(f32[32,2,2048]{2,1,0:T(2,128)} %bitcast.109), calls=%async_computation | async-start | bytes 1048576 | tf_op jit(solution)/shard_map/all_to_all | solution.py:184
  109.2 3.4 %collective-permute-start.16 = (f32[1,1,1,8,8,128]{5,4,3,2,1,0:T(8,128)S(1)}, f32[1,1,1,8,8,128]{5,4,3,2,1,0:T(8,128)S(1)}, u32[]{:S(2)}, u32[]{:S(2)}) collective-permute-start(f32[1,1,1,8,8,128]{5,4,3,2,1,0:T(8,128)S(1)} %get-tuple-element.50), channel_id=1, source_target_pairs={{0,4},{4,8},{8,12},{12,16},{16,20},{20,24},{24,28},{1,5},{5,9},{9,... | collective-permute-start | bytes 98312 | tf_op jit(solution)/shard_map/ppermute | solution.py:16
  112.6 1.3 collective-permute-start.17
  114.4 4.5 %collective-permute-done.17 = f32[1,1,1,8,8,128]{5,4,3,2,1,0:T(8,128)S(1)} collective-permute-done((f32[1,1,1,8,8,128]{5,4,3,2,1,0:T(8,128)S(1)}, f32[1,1,1,8,8,128]{5,4,3,2,1,0:T(8,128)S(1)}, u32[]{:S(2)}, u32[]{:S(2)}) %collective-permute-start.17) | collective-permute-done | bytes 32800 | tf_op jit(solution)/shard_map/ppermute | solution.py:19
  118.9 4.1 %all-to-all-done = f32[32,2,2048]{2,1,0:T(2,128)S(1)} async-done(((f32[32,2,2048]{2,1,0:T(2,128)}), f32[32,2,2048]{2,1,0:T(2,128)S(1)}, u32[]{:S(2)}, u32[]{:S(2)}) %all-to-all-start) | async-done | bytes 524320 | tf_op jit(solution)/shard_map/all_to_all | solution.py:184
  123.2 2.0 %collective-permute-start.18 = (f32[1,1,1,8,8,128]{5,3,4,2,1,0:T(8,128)S(1)}, f32[1,1,1,8,8,128]{5,3,4,2,1,0:T(8,128)S(1)}, u32[]{:S(2)}, u32[]{:S(2)}) collective-permute-start(f32[1,1,1,8,8,128]{5,3,4,2,1,0:T(8,128)S(1)} %maximum_bitcast_fusion.13), channel_id=1, source_target_pairs={{0,1},{1,2},{2,3},{4,5},{5,6},{6,7},{8,9},{9,10},{10,11},{12,13},{... | collective-permute-start | bytes 98312 | tf_op jit(solution)/shard_map/ppermute | solution.py:16
  125.1 3.3 %collective-permute-done.18 = f32[1,1,1,8,8,128]{5,3,4,2,1,0:T(8,128)S(1)} collective-permute-done((f32[1,1,1,8,8,128]{5,3,4,2,1,0:T(8,128)S(1)}, f32[1,1,1,8,8,128]{5,3,4,2,1,0:T(8,128)S(1)}, u32[]{:S(2)}, u32[]{:S(2)}) %collective-permute-start.18) | collective-permute-done | bytes 32800 | tf_op jit(solution)/shard_map/ppermute | solution.py:16
  128.4 1.9 %collective-permute-start.19 = (f32[1,1,1,8,8,128]{5,3,4,2,1,0:T(8,128)S(1)}, f32[1,1,1,8,8,128]{5,3,4,2,1,0:T(8,128)S(1)}, u32[]{:S(2)}, u32[]{:S(2)}) collective-permute-start(f32[1,1,1,8,8,128]{5,3,4,2,1,0:T(8,128)S(1)} %get-tuple-element.27), channel_id=1, source_target_pairs={{1,0},{2,1},{3,2},{5,4},{6,5},{7,6},{9,8},{10,9},{11,10},{13,12},{... | collective-permute-start | bytes 98312 | tf_op jit(solution)/shard_map/ppermute | solution.py:19
  131.1 3.4 %all-to-all-start.1 = ((f32[8,2,2048]{2,1,0:T(2,128)}), f32[8,2,2048]{2,1,0:T(2,128)S(1)}, u32[]{:S(2)}, u32[]{:S(2)}) async-start(f32[8,2,2048]{2,1,0:T(2,128)} %broadcast_in_dim.162), calls=%async_computation.1 | async-start | bytes 262144 | tf_op jit(solution)/shard_map/all_to_all | solution.py:191
  135.6 6.8 %all-to-all-done.1 = f32[8,2,2048]{2,1,0:T(2,128)S(1)} async-done(((f32[8,2,2048]{2,1,0:T(2,128)}), f32[8,2,2048]{2,1,0:T(2,128)S(1)}, u32[]{:S(2)}, u32[]{:S(2)}) %all-to-all-start.1) | async-done | bytes 131104 | tf_op jit(solution)/shard_map/all_to_all | solution.py:191
  (127 shorter events, 19.7 us)
Async XLA Ops:
  0.6 18.9 %copy-start.1 = (f32[1,4096]{1,0:T(1,128)S(1)}, f32[1,4096]{1,0:T(1,128)}, u32[]{:S(2)}) copy-start(f32[1,4096]{1,0:T(1,128)} %param.41) | copy-start | bytes 49156
  4.8 5.3 %collective-permute-start = (f32[2,1,1,8,8,128]{5,0,4,3,2,1:T(2,128)S(1)}, f32[2,1,1,8,8,128]{5,0,4,3,2,1:T(2,128)S(1)}, u32[]{:S(2)}, u32[]{:S(2)}) collective-permute-start(f32[2,1,1,8,8,128]{5,0,4,3,2,1:T(2,128)S(1)} %maximum_bitcast_fusion.9), channel_id=1, source_target_pairs={{0,4},{4,8},{8,12},{12,16},{16,20},{20,24},{24,28},{1,5},{5,9},{9,... | collective-permute-start | bytes 196616 | tf_op jit(solution)/shard_map/ppermute | solution.py:16
  11.0 6.5 %collective-permute-start.1 = (f32[2,1,1,8,8,128]{5,0,4,3,2,1:T(2,128)S(1)}, f32[2,1,1,8,8,128]{5,0,4,3,2,1:T(2,128)S(1)}, u32[]{:S(2)}, u32[]{:S(2)}) collective-permute-start(f32[2,1,1,8,8,128]{5,0,4,3,2,1:T(2,128)S(1)} %get-tuple-element.43), channel_id=1, source_target_pairs={{4,0},{8,4},{12,8},{16,12},{20,16},{24,20},{28,24},{5,1},{9,5},{13... | collective-permute-start | bytes 196616 | tf_op jit(solution)/shard_map/ppermute | solution.py:19
  17.6 5.6 %collective-permute-start.2 = (f32[2,1,1,8,8,128]{5,3,0,4,2,1:T(8,128)S(1)}, f32[2,1,1,8,8,128]{5,3,0,4,2,1:T(8,128)S(1)}, u32[]{:S(2)}, u32[]{:S(2)}) collective-permute-start(f32[2,1,1,8,8,128]{5,3,0,4,2,1:T(8,128)S(1)} %maximum_bitcast_fusion.7), channel_id=1, source_target_pairs={{0,1},{1,2},{2,3},{4,5},{5,6},{6,7},{8,9},{9,10},{10,11},{12,13},{... | collective-permute-start | bytes 196616 | tf_op jit(solution)/shard_map/ppermute | solution.py:16
  23.2 4.7 %copy-start = (f32[8,8,1,1]{1,0,3,2:T(8,128)S(1)}, f32[8,8,1,1]{1,0,3,2:T(8,128)}, u32[]{:S(2)}) copy-start(f32[8,8,1,1]{1,0,3,2:T(8,128)} %constant.134) | copy-start | bytes 772
  23.2 3.8 %collective-permute-start.3 = (f32[2,1,1,8,8,128]{5,3,0,4,2,1:T(8,128)S(1)}, f32[2,1,1,8,8,128]{5,3,0,4,2,1:T(8,128)S(1)}, u32[]{:S(2)}, u32[]{:S(2)}) collective-permute-start(f32[2,1,1,8,8,128]{5,3,0,4,2,1:T(8,128)S(1)} %get-tuple-element.41), channel_id=1, source_target_pairs={{1,0},{2,1},{3,2},{5,4},{6,5},{7,6},{9,8},{10,9},{11,10},{13,12},{... | collective-permute-start | bytes 196616 | tf_op jit(solution)/shard_map/ppermute | solution.py:19
  25.3 3.3 %copy-start.2 = (f32[8]{0:T(128)S(1)}, f32[8]{0:T(128)}, u32[]{:S(2)}) copy-start(f32[8]{0:T(128)} %constant.129) | copy-start | bytes 100
  29.8 9.8 %collective-permute-start.4 = (f32[1,1,1,8,8,128]{5,4,3,2,1,0:T(8,128)S(1)}, f32[1,1,1,8,8,128]{5,4,3,2,1,0:T(8,128)S(1)}, u32[]{:S(2)}, u32[]{:S(2)}) collective-permute-start(f32[1,1,1,8,8,128]{5,4,3,2,1,0:T(8,128)S(1)} %bitcast.475), channel_id=1, source_target_pairs={{0,4},{4,8},{8,12},{12,16},{16,20},{20,24},{24,28},{1,5},{5,9},{9,... | collective-permute-start | bytes 98312 | tf_op jit(solution)/shard_map/ppermute | solution.py:16
  34.6 5.8 %collective-permute-start.5 = (f32[1,1,1,8,8,128]{5,4,3,2,1,0:T(8,128)S(1)}, f32[1,1,1,8,8,128]{5,4,3,2,1,0:T(8,128)S(1)}, u32[]{:S(2)}, u32[]{:S(2)}) collective-permute-start(f32[1,1,1,8,8,128]{5,4,3,2,1,0:T(8,128)S(1)} %bitcast.477), channel_id=1, source_target_pairs={{4,0},{8,4},{12,8},{16,12},{20,16},{24,20},{28,24},{5,1},{9,5},{13... | collective-permute-start | bytes 98312 | tf_op jit(solution)/shard_map/ppermute | solution.py:19
  40.4 5.2 %collective-permute-start.6 = (f32[1,1,1,8,8,128]{5,3,4,2,1,0:T(8,128)S(1)}, f32[1,1,1,8,8,128]{5,3,4,2,1,0:T(8,128)S(1)}, u32[]{:S(2)}, u32[]{:S(2)}) collective-permute-start(f32[1,1,1,8,8,128]{5,3,4,2,1,0:T(8,128)S(1)} %maximum_bitcast_fusion.19), channel_id=1, source_target_pairs={{0,1},{1,2},{2,3},{4,5},{5,6},{6,7},{8,9},{9,10},{10,11},{12,13},{... | collective-permute-start | bytes 98312 | tf_op jit(solution)/shard_map/ppermute | solution.py:16
  45.7 4.5 %collective-permute-start.7 = (f32[1,1,1,8,8,128]{5,3,4,2,1,0:T(8,128)S(1)}, f32[1,1,1,8,8,128]{5,3,4,2,1,0:T(8,128)S(1)}, u32[]{:S(2)}, u32[]{:S(2)}) collective-permute-start(f32[1,1,1,8,8,128]{5,3,4,2,1,0:T(8,128)S(1)} %get-tuple-element.37), channel_id=1, source_target_pairs={{1,0},{2,1},{3,2},{5,4},{6,5},{7,6},{9,8},{10,9},{11,10},{13,12},{... | collective-permute-start | bytes 98312 | tf_op jit(solution)/shard_map/ppermute | solution.py:19
  48.7 20.9 %copy-start.3 = (s32[1,4096]{1,0:T(1,128)S(1)}, s32[1,4096]{1,0:T(1,128)}, u32[]{:S(2)}) copy-start(s32[1,4096]{1,0:T(1,128)} %param.38) | copy-start | bytes 49156
  52.1 5.9 %collective-permute-start.8 = (f32[1,1,1,8,8,128]{5,4,3,2,1,0:T(8,128)S(1)}, f32[1,1,1,8,8,128]{5,4,3,2,1,0:T(8,128)S(1)}, u32[]{:S(2)}, u32[]{:S(2)}) collective-permute-start(f32[1,1,1,8,8,128]{5,4,3,2,1,0:T(8,128)S(1)} %get-tuple-element.65), channel_id=1, source_target_pairs={{0,4},{4,8},{8,12},{12,16},{16,20},{20,24},{24,28},{1,5},{5,9},{9,... | collective-permute-start | bytes 98312 | tf_op jit(solution)/shard_map/ppermute | solution.py:16
  56.4 5.8 %collective-permute-start.9 = (f32[1,1,1,8,8,128]{5,4,3,2,1,0:T(8,128)S(1)}, f32[1,1,1,8,8,128]{5,4,3,2,1,0:T(8,128)S(1)}, u32[]{:S(2)}, u32[]{:S(2)}) collective-permute-start(f32[1,1,1,8,8,128]{5,4,3,2,1,0:T(8,128)S(1)} %get-tuple-element.66), channel_id=1, source_target_pairs={{4,0},{8,4},{12,8},{16,12},{20,16},{24,20},{28,24},{5,1},{9,5},{13... | collective-permute-start | bytes 98312 | tf_op jit(solution)/shard_map/ppermute | solution.py:19
  62.3 5.2 %collective-permute-start.10 = (f32[1,1,1,8,8,128]{5,4,3,2,1,0:T(8,128)S(1)}, f32[1,1,1,8,8,128]{5,4,3,2,1,0:T(8,128)S(1)}, u32[]{:S(2)}, u32[]{:S(2)}) collective-permute-start(f32[1,1,1,8,8,128]{5,4,3,2,1,0:T(8,128)S(1)} %maximum_bitcast_fusion.17), channel_id=1, source_target_pairs={{0,1},{1,2},{2,3},{4,5},{5,6},{6,7},{8,9},{9,10},{10,11},{12,13},{... | collective-permute-start | bytes 98312 | tf_op jit(solution)/shard_map/ppermute | solution.py:16
  67.5 3.5 %collective-permute-start.11 = (f32[1,1,1,8,8,128]{5,4,3,2,1,0:T(8,128)S(1)}, f32[1,1,1,8,8,128]{5,4,3,2,1,0:T(8,128)S(1)}, u32[]{:S(2)}, u32[]{:S(2)}) collective-permute-start(f32[1,1,1,8,8,128]{5,4,3,2,1,0:T(8,128)S(1)} %get-tuple-element.35), channel_id=1, source_target_pairs={{1,0},{2,1},{3,2},{5,4},{6,5},{7,6},{9,8},{10,9},{11,10},{13,12},{... | collective-permute-start | bytes 98312 | tf_op jit(solution)/shard_map/ppermute | solution.py:19
  73.1 6.3 %collective-permute-start.12 = (f32[1,1,1,8,8,128]{5,4,3,2,1,0:T(8,128)S(1)}, f32[1,1,1,8,8,128]{5,4,3,2,1,0:T(8,128)S(1)}, u32[]{:S(2)}, u32[]{:S(2)}) collective-permute-start(f32[1,1,1,8,8,128]{5,4,3,2,1,0:T(8,128)S(1)} %get-tuple-element.59), channel_id=1, source_target_pairs={{0,4},{4,8},{8,12},{12,16},{16,20},{20,24},{24,28},{1,5},{5,9},{9,... | collective-permute-start | bytes 98312 | tf_op jit(solution)/shard_map/ppermute | solution.py:16
  77.8 5.8 %collective-permute-start.13 = (f32[1,1,1,8,8,128]{5,4,3,2,1,0:T(8,128)S(1)}, f32[1,1,1,8,8,128]{5,4,3,2,1,0:T(8,128)S(1)}, u32[]{:S(2)}, u32[]{:S(2)}) collective-permute-start(f32[1,1,1,8,8,128]{5,4,3,2,1,0:T(8,128)S(1)} %get-tuple-element.60), channel_id=1, source_target_pairs={{4,0},{8,4},{12,8},{16,12},{20,16},{24,20},{28,24},{5,1},{9,5},{13... | collective-permute-start | bytes 98312 | tf_op jit(solution)/shard_map/ppermute | solution.py:19
  83.6 5.2 %collective-permute-start.14 = (f32[1,1,1,8,8,128]{5,4,3,2,1,0:T(8,128)S(1)}, f32[1,1,1,8,8,128]{5,4,3,2,1,0:T(8,128)S(1)}, u32[]{:S(2)}, u32[]{:S(2)}) collective-permute-start(f32[1,1,1,8,8,128]{5,4,3,2,1,0:T(8,128)S(1)} %maximum_bitcast_fusion.15), channel_id=1, source_target_pairs={{0,1},{1,2},{2,3},{4,5},{5,6},{6,7},{8,9},{9,10},{10,11},{12,13},{... | collective-permute-start | bytes 98312 | tf_op jit(solution)/shard_map/ppermute | solution.py:16
  88.9 4.0 %collective-permute-start.15 = (f32[1,1,1,8,8,128]{5,4,3,2,1,0:T(8,128)S(1)}, f32[1,1,1,8,8,128]{5,4,3,2,1,0:T(8,128)S(1)}, u32[]{:S(2)}, u32[]{:S(2)}) collective-permute-start(f32[1,1,1,8,8,128]{5,4,3,2,1,0:T(8,128)S(1)} %get-tuple-element.31), channel_id=1, source_target_pairs={{1,0},{2,1},{3,2},{5,4},{6,5},{7,6},{9,8},{10,9},{11,10},{13,12},{... | collective-permute-start | bytes 98312 | tf_op jit(solution)/shard_map/ppermute | solution.py:19
  103.1 19.8 %all-to-all-start = ((f32[32,2,2048]{2,1,0:T(2,128)}), f32[32,2,2048]{2,1,0:T(2,128)S(1)}, u32[]{:S(2)}, u32[]{:S(2)}) async-start(f32[32,2,2048]{2,1,0:T(2,128)} %bitcast.109), calls=%async_computation | async-start | bytes 1048576 | tf_op jit(solution)/shard_map/all_to_all | solution.py:184
  109.2 5.1 %collective-permute-start.16 = (f32[1,1,1,8,8,128]{5,4,3,2,1,0:T(8,128)S(1)}, f32[1,1,1,8,8,128]{5,4,3,2,1,0:T(8,128)S(1)}, u32[]{:S(2)}, u32[]{:S(2)}) collective-permute-start(f32[1,1,1,8,8,128]{5,4,3,2,1,0:T(8,128)S(1)} %get-tuple-element.50), channel_id=1, source_target_pairs={{0,4},{4,8},{8,12},{12,16},{16,20},{20,24},{24,28},{1,5},{5,9},{9,... | collective-permute-start | bytes 98312 | tf_op jit(solution)/shard_map/ppermute | solution.py:16
  112.6 6.2 %collective-permute-start.17 = (f32[1,1,1,8,8,128]{5,4,3,2,1,0:T(8,128)S(1)}, f32[1,1,1,8,8,128]{5,4,3,2,1,0:T(8,128)S(1)}, u32[]{:S(2)}, u32[]{:S(2)}) collective-permute-start(f32[1,1,1,8,8,128]{5,4,3,2,1,0:T(8,128)S(1)} %get-tuple-element.51), channel_id=1, source_target_pairs={{4,0},{8,4},{12,8},{16,12},{20,16},{24,20},{28,24},{5,1},{9,5},{13... | collective-permute-start | bytes 98312 | tf_op jit(solution)/shard_map/ppermute | solution.py:19
  123.2 5.2 %collective-permute-start.18 = (f32[1,1,1,8,8,128]{5,3,4,2,1,0:T(8,128)S(1)}, f32[1,1,1,8,8,128]{5,3,4,2,1,0:T(8,128)S(1)}, u32[]{:S(2)}, u32[]{:S(2)}) collective-permute-start(f32[1,1,1,8,8,128]{5,3,4,2,1,0:T(8,128)S(1)} %maximum_bitcast_fusion.13), channel_id=1, source_target_pairs={{0,1},{1,2},{2,3},{4,5},{5,6},{6,7},{8,9},{9,10},{10,11},{12,13},{... | collective-permute-start | bytes 98312 | tf_op jit(solution)/shard_map/ppermute | solution.py:16
  128.4 6.1 %collective-permute-start.19 = (f32[1,1,1,8,8,128]{5,3,4,2,1,0:T(8,128)S(1)}, f32[1,1,1,8,8,128]{5,3,4,2,1,0:T(8,128)S(1)}, u32[]{:S(2)}, u32[]{:S(2)}) collective-permute-start(f32[1,1,1,8,8,128]{5,3,4,2,1,0:T(8,128)S(1)} %get-tuple-element.27), channel_id=1, source_target_pairs={{1,0},{2,1},{3,2},{5,4},{6,5},{7,6},{9,8},{10,9},{11,10},{13,12},{... | collective-permute-start | bytes 98312 | tf_op jit(solution)/shard_map/ppermute | solution.py:19
  131.1 11.2 %all-to-all-start.1 = ((f32[8,2,2048]{2,1,0:T(2,128)}), f32[8,2,2048]{2,1,0:T(2,128)S(1)}, u32[]{:S(2)}, u32[]{:S(2)}) async-start(f32[8,2,2048]{2,1,0:T(2,128)} %broadcast_in_dim.162), calls=%async_computation.1 | async-start | bytes 262144 | tf_op jit(solution)/shard_map/all_to_all | solution.py:191

commit v10 on v9

--- a/solution.py
+++ b/solution.py
@@ -163,10 +163,8 @@
     rows = bins // lanes
     hit_lane = one_hot(ids % lanes, lanes)
     rhs = jnp.concatenate([hit_lane * part[:, None] for part in split_parts(values, count)], axis=1)
-    hit_row = one_hot(ids // lanes, rows)
-    sums = lax.dot_general(
-        hit_row, rhs, (((0,), (0,)), ((), ())), preferred_element_type=jnp.float32
-    )
+    hit_row_t = (lax.broadcasted_iota(jnp.int32, (rows, 1), 0) == (ids // lanes)[None, :]).astype(jnp.bfloat16)
+    sums = jnp.dot(hit_row_t, rhs, preferred_element_type=jnp.float32)
     total = sums[:, :lanes]
     for n in range(1, count):
         total = total + sums[:, n * lanes : (n + 1) * lanes]

time: 144 us -> 144 us (level)
    ppermute x10, waiting for transfers between devices: 13.3 us -> 9.89 us  [padded_2(): lax.ppermute(lax.slice_in_dim(block, block.shape[dim] - width, None, axis...]
    ppermute x10, waiting for transfers between devices: 21.8 us -> 25.1 us  [padded_2(): lax.ppermute(lax.slice_in_dim(block, 0, width, axis=dim), axis, backward)]
  transfers between devices with their start and end apart: 22 -> 22, of which waited for: 20 -> 18; matrix products, arithmetic and copies ran while one was open for 12% -> 12% of each run, Pallas kernels for 0% -> 0%
where the time goes in v10:
time: 144 us; the launch traced here: 143 us
  starting transfers between devices  56.6 us (39%)
  waiting for transfers between devices  45.8 us (32%)
  other arithmetic  21.4 us (15%)
  matrix products  12.1 us (8%)
  local copies, waits for them, and re-layouts  5.26 us (4%)
  between operations  1.58 us (1%)
    ppermute x10, starting transfers between devices, padded_2(): lax.ppermute(lax.slice_in_dim(block, block.shape[dim] - width, None, axis...  29 us
    ppermute x10, waiting for transfers between devices, padded_2(): lax.ppermute(lax.slice_in_dim(block, 0, width, axis=dim), axis, backward)  25.1 us
    ppermute x10, starting transfers between devices, padded_2(): lax.ppermute(lax.slice_in_dim(block, 0, width, axis=dim), axis, backward)  18.8 us
    ppermute x10, waiting for transfers between devices, padded_2(): lax.ppermute(lax.slice_in_dim(block, block.shape[dim] - width, None, axis...  9.89 us
    mul x2, other arithmetic, segment_sum(): hit_lane * part[:, None]  6.85 us
    all_to_all x1, waiting for transfers between devices, strip_gather(): whole = lax.all_to_all(spread_out, 'ex', 0, 0, tiled=True)  6.78 us
    all_to_all x1, starting transfers between devices, strip_reduce(): return lax.all_to_all(chunks, ('ex', 'ey'), 0, 0, tiled=True).sum(0)  5.29 us
    all_to_all x1, waiting for transfers between devices, strip_reduce(): return lax.all_to_all(chunks, ('ex', 'ey'), 0, 0, tiled=True).sum(0)  4.09 us
  transfers between devices with their start and end apart: 22, of which 18 were waited for; matrix products, arithmetic and copies ran while one was open for 12% of the time, Pallas kernels for 0%

profile of v10, /device:TPU:2, one launch (start us, length us, event | category | flops | bytes accessed | tf_op | source)
XLA Modules:
  0.0 142.8 jit_solution(1671977156973767307)
XLA Ops:
  2.8 1.2 fusion.90
  4.8 3.4 %collective-permute-start = (f32[2,1,1,8,8,128]{5,0,4,3,2,1:T(2,128)S(1)}, f32[2,1,1,8,8,128]{5,0,4,3,2,1:T(2,128)S(1)}, u32[]{:S(2)}, u32[]{:S(2)}) collective-permute-start(f32[2,1,1,8,8,128]{5,0,4,3,2,1:T(2,128)S(1)} %maximum_bitcast_fusion.9), channel_id=1, source_target_pairs={{0,4},{4,8},{8,12},{12,16},{16,20},{20,24},{24,28},{1,5},{5,9},{9,... | collective-permute-start | bytes 196616 | tf_op jit(solution)/shard_map/ppermute | solution.py:16
  11.3 1.3 collective-permute-start.1
  12.6 1.3 pad_maximum_fusion.5
  14.2 3.3 %collective-permute-done.1 = f32[2,1,1,8,8,128]{5,0,4,3,2,1:T(2,128)S(1)} collective-permute-done((f32[2,1,1,8,8,128]{5,0,4,3,2,1:T(2,128)S(1)}, f32[2,1,1,8,8,128]{5,0,4,3,2,1:T(2,128)S(1)}, u32[]{:S(2)}, u32[]{:S(2)}) %collective-permute-start.1) | collective-permute-done | bytes 65568 | tf_op jit(solution)/shard_map/ppermute | solution.py:19
  17.6 1.9 %collective-permute-start.2 = (f32[2,1,1,8,8,128]{5,3,0,4,2,1:T(8,128)S(1)}, f32[2,1,1,8,8,128]{5,3,0,4,2,1:T(8,128)S(1)}, u32[]{:S(2)}, u32[]{:S(2)}) collective-permute-start(f32[2,1,1,8,8,128]{5,3,0,4,2,1:T(8,128)S(1)} %maximum_bitcast_fusion.7), channel_id=1, source_target_pairs={{0,1},{1,2},{2,3},{4,5},{5,6},{6,7},{8,9},{9,10},{10,11},{12,13},{... | collective-permute-start | bytes 196616 | tf_op jit(solution)/shard_map/ppermute | solution.py:16
  19.5 3.6 %fusion.20 = (bf16[4096,256]{1,0:T(8,128)(2,1)S(1)}, bf16[4096,256]{1,0:T(8,128)(2,1)S(1)}, bf16[4096,256]{1,0:T(8,128)(2,1)S(1)}) fusion(s32[4096]{0:T(1024)S(1)} %add_select_fusion.2, bf16[4096]{0:T(1024)(128)(2,1)S(1)} %get-tuple-element.82, bf16[4096]{0:T(1024)(128)(2,1)S(1)} %get-tuple-element.83, bf16[4096]{0:T(1024)(128)(2,1)S(1)} %get-tuple-element.84), kind=kLoop, calls=%fused_computation.26 | loop fusion | flops 4194304 | bytes 6332416 | tf_op jit(solution)/shard_map/mul | solution.py:165
  23.2 3.6 %collective-permute-start.3 = (f32[2,1,1,8,8,128]{5,3,0,4,2,1:T(8,128)S(1)}, f32[2,1,1,8,8,128]{5,3,0,4,2,1:T(8,128)S(1)}, u32[]{:S(2)}, u32[]{:S(2)}) collective-permute-start(f32[2,1,1,8,8,128]{5,3,0,4,2,1:T(8,128)S(1)} %get-tuple-element.41), channel_id=1, source_target_pairs={{1,0},{2,1},{3,2},{5,4},{6,5},{7,6},{9,8},{10,9},{11,10},{13,12},{... | collective-permute-start | bytes 196616 | tf_op jit(solution)/shard_map/ppermute | solution.py:19
  27.3 1.5 %collective-permute-done.3 = f32[2,1,1,8,8,128]{5,3,0,4,2,1:T(8,128)S(1)} collective-permute-done((f32[2,1,1,8,8,128]{5,3,0,4,2,1:T(8,128)S(1)}, f32[2,1,1,8,8,128]{5,3,0,4,2,1:T(8,128)S(1)}, u32[]{:S(2)}, u32[]{:S(2)}) %collective-permute-start.3) | collective-permute-done | bytes 65568 | tf_op jit(solution)/shard_map/ppermute | solution.py:19
  30.5 0.9 fusion.30
  31.5 4.8 %collective-permute-start.4 = (f32[1,1,1,8,8,128]{5,4,3,2,1,0:T(8,128)S(1)}, f32[1,1,1,8,8,128]{5,4,3,2,1,0:T(8,128)S(1)}, u32[]{:S(2)}, u32[]{:S(2)}) collective-permute-start(f32[1,1,1,8,8,128]{5,4,3,2,1,0:T(8,128)S(1)} %bitcast.480), channel_id=1, source_target_pairs={{0,4},{4,8},{8,12},{12,16},{16,20},{20,24},{24,28},{1,5},{5,9},{9,... | collective-permute-start | bytes 98312 | tf_op jit(solution)/shard_map/ppermute | solution.py:16
  36.3 1.3 collective-permute-start.5
  37.9 4.2 %collective-permute-done.5 = f32[1,1,1,8,8,128]{5,4,3,2,1,0:T(8,128)S(1)} collective-permute-done((f32[1,1,1,8,8,128]{5,4,3,2,1,0:T(8,128)S(1)}, f32[1,1,1,8,8,128]{5,4,3,2,1,0:T(8,128)S(1)}, u32[]{:S(2)}, u32[]{:S(2)}) %collective-permute-start.5) | collective-permute-done | bytes 32800 | tf_op jit(solution)/shard_map/ppermute | solution.py:19
  42.2 1.9 %collective-permute-start.6 = (f32[1,1,1,8,8,128]{5,3,4,2,1,0:T(8,128)S(1)}, f32[1,1,1,8,8,128]{5,3,4,2,1,0:T(8,128)S(1)}, u32[]{:S(2)}, u32[]{:S(2)}) collective-permute-start(f32[1,1,1,8,8,128]{5,3,4,2,1,0:T(8,128)S(1)} %maximum_bitcast_fusion.19), channel_id=1, source_target_pairs={{0,1},{1,2},{2,3},{4,5},{5,6},{6,7},{8,9},{9,10},{10,11},{12,13},{... | collective-permute-start | bytes 98312 | tf_op jit(solution)/shard_map/ppermute | solution.py:16
  44.1 2.0 %fusion = f32[256,768]{1,0:T(8,128)S(1)} fusion(bf16[4096,256]{1,0:T(8,128)(2,1)S(1)} %get-tuple-element.80, bf16[4096,256]{1,0:T(8,128)(2,1)S(1)} %get-tuple-element.81, bf16[4096,256]{1,0:T(8,128)(2,1)S(1)} %get-tuple-element.79, s32[4096]{0:T(1024)S(1)} %bitcast.491), kind=kOutput, calls=%fused_computation | convolution fusion | flops 1630535680 | bytes 7094272 | tf_op jit(solution)/shard_map/dot_general | solution.py:167
  46.1 1.3 collective-permute-done.6
  47.4 2.3 %collective-permute-start.7 = (f32[1,1,1,8,8,128]{5,3,4,2,1,0:T(8,128)S(1)}, f32[1,1,1,8,8,128]{5,3,4,2,1,0:T(8,128)S(1)}, u32[]{:S(2)}, u32[]{:S(2)}) collective-permute-start(f32[1,1,1,8,8,128]{5,3,4,2,1,0:T(8,128)S(1)} %get-tuple-element.37), channel_id=1, source_target_pairs={{1,0},{2,1},{3,2},{5,4},{6,5},{7,6},{9,8},{10,9},{11,10},{13,12},{... | collective-permute-start | bytes 98312 | tf_op jit(solution)/shard_map/ppermute | solution.py:19
  50.0 1.4 collective-permute-done.7
  53.2 4.3 %collective-permute-start.8 = (f32[1,1,1,8,8,128]{5,4,3,2,1,0:T(8,128)S(1)}, f32[1,1,1,8,8,128]{5,4,3,2,1,0:T(8,128)S(1)}, u32[]{:S(2)}, u32[]{:S(2)}) collective-permute-start(f32[1,1,1,8,8,128]{5,4,3,2,1,0:T(8,128)S(1)} %get-tuple-element.65), channel_id=1, source_target_pairs={{0,4},{4,8},{8,12},{12,16},{16,20},{20,24},{24,28},{1,5},{5,9},{9,... | collective-permute-start | bytes 98312 | tf_op jit(solution)/shard_map/ppermute | solution.py:16
  57.5 1.3 collective-permute-start.9
  59.1 4.2 %collective-permute-done.9 = f32[1,1,1,8,8,128]{5,4,3,2,1,0:T(8,128)S(1)} collective-permute-done((f32[1,1,1,8,8,128]{5,4,3,2,1,0:T(8,128)S(1)}, f32[1,1,1,8,8,128]{5,4,3,2,1,0:T(8,128)S(1)}, u32[]{:S(2)}, u32[]{:S(2)}) %collective-permute-start.9) | collective-permute-done | bytes 32800 | tf_op jit(solution)/shard_map/ppermute | solution.py:19
  63.4 1.9 %collective-permute-start.10 = (f32[1,1,1,8,8,128]{5,4,3,2,1,0:T(8,128)S(1)}, f32[1,1,1,8,8,128]{5,4,3,2,1,0:T(8,128)S(1)}, u32[]{:S(2)}, u32[]{:S(2)}) collective-permute-start(f32[1,1,1,8,8,128]{5,4,3,2,1,0:T(8,128)S(1)} %maximum_bitcast_fusion.17), channel_id=1, source_target_pairs={{0,1},{1,2},{2,3},{4,5},{5,6},{6,7},{8,9},{9,10},{10,11},{12,13},{... | collective-permute-start | bytes 98312 | tf_op jit(solution)/shard_map/ppermute | solution.py:16
  65.3 3.3 %collective-permute-done.10 = f32[1,1,1,8,8,128]{5,4,3,2,1,0:T(8,128)S(1)} collective-permute-done((f32[1,1,1,8,8,128]{5,4,3,2,1,0:T(8,128)S(1)}, f32[1,1,1,8,8,128]{5,4,3,2,1,0:T(8,128)S(1)}, u32[]{:S(2)}, u32[]{:S(2)}) %collective-permute-start.10) | collective-permute-done | bytes 32800 | tf_op jit(solution)/shard_map/ppermute | solution.py:16
  68.6 1.9 %collective-permute-start.11 = (f32[1,1,1,8,8,128]{5,4,3,2,1,0:T(8,128)S(1)}, f32[1,1,1,8,8,128]{5,4,3,2,1,0:T(8,128)S(1)}, u32[]{:S(2)}, u32[]{:S(2)}) collective-permute-start(f32[1,1,1,8,8,128]{5,4,3,2,1,0:T(8,128)S(1)} %get-tuple-element.35), channel_id=1, source_target_pairs={{1,0},{2,1},{3,2},{5,4},{6,5},{7,6},{9,8},{10,9},{11,10},{13,12},{... | collective-permute-start | bytes 98312 | tf_op jit(solution)/shard_map/ppermute | solution.py:19
  70.6 1.5 %collective-permute-done.11 = f32[1,1,1,8,8,128]{5,4,3,2,1,0:T(8,128)S(1)} collective-permute-done((f32[1,1,1,8,8,128]{5,4,3,2,1,0:T(8,128)S(1)}, f32[1,1,1,8,8,128]{5,4,3,2,1,0:T(8,128)S(1)}, u32[]{:S(2)}, u32[]{:S(2)}) %collective-permute-start.11) | collective-permute-done | bytes 32800 | tf_op jit(solution)/shard_map/ppermute | solution.py:19
  74.2 3.4 %collective-permute-start.12 = (f32[1,1,1,8,8,128]{5,4,3,2,1,0:T(8,128)S(1)}, f32[1,1,1,8,8,128]{5,4,3,2,1,0:T(8,128)S(1)}, u32[]{:S(2)}, u32[]{:S(2)}) collective-permute-start(f32[1,1,1,8,8,128]{5,4,3,2,1,0:T(8,128)S(1)} %get-tuple-element.59), channel_id=1, source_target_pairs={{0,4},{4,8},{8,12},{12,16},{16,20},{20,24},{24,28},{1,5},{5,9},{9,... | collective-permute-start | bytes 98312 | tf_op jit(solution)/shard_map/ppermute | solution.py:16
  77.6 1.5 %collective-permute-start.13 = (f32[1,1,1,8,8,128]{5,4,3,2,1,0:T(8,128)S(1)}, f32[1,1,1,8,8,128]{5,4,3,2,1,0:T(8,128)S(1)}, u32[]{:S(2)}, u32[]{:S(2)}) collective-permute-start(f32[1,1,1,8,8,128]{5,4,3,2,1,0:T(8,128)S(1)} %get-tuple-element.60), channel_id=1, source_target_pairs={{4,0},{8,4},{12,8},{16,12},{20,16},{24,20},{28,24},{5,1},{9,5},{13... | collective-permute-start | bytes 98312 | tf_op jit(solution)/shard_map/ppermute | solution.py:19
  79.2 4.2 %collective-permute-done.13 = f32[1,1,1,8,8,128]{5,4,3,2,1,0:T(8,128)S(1)} collective-permute-done((f32[1,1,1,8,8,128]{5,4,3,2,1,0:T(8,128)S(1)}, f32[1,1,1,8,8,128]{5,4,3,2,1,0:T(8,128)S(1)}, u32[]{:S(2)}, u32[]{:S(2)}) %collective-permute-start.13) | collective-permute-done | bytes 32800 | tf_op jit(solution)/shard_map/ppermute | solution.py:19
  83.5 1.9 %collective-permute-start.14 = (f32[1,1,1,8,8,128]{5,4,3,2,1,0:T(8,128)S(1)}, f32[1,1,1,8,8,128]{5,4,3,2,1,0:T(8,128)S(1)}, u32[]{:S(2)}, u32[]{:S(2)}) collective-permute-start(f32[1,1,1,8,8,128]{5,4,3,2,1,0:T(8,128)S(1)} %maximum_bitcast_fusion.15), channel_id=1, source_target_pairs={{0,1},{1,2},{2,3},{4,5},{5,6},{6,7},{8,9},{9,10},{10,11},{12,13},{... | collective-permute-start | bytes 98312 | tf_op jit(solution)/shard_map/ppermute | solution.py:16
  85.4 2.0 %fusion.15 = f32[4096,768]{0,1:T(8,128)S(1)} fusion(s32[4096]{0:T(1024)S(1)} %get-tuple-element.78, bf16[256,256]{1,0:T(8,128)(2,1)S(1)} %get-tuple-element.53, bf16[256,256]{1,0:T(8,128)(2,1)S(1)} %get-tuple-element.54, bf16[256,256]{1,0:T(8,128)(2,1)S(1)} %get-tuple-element.52), kind=kOutput, calls=%fused_computation.19 | convolution fusion | flops 1612840960 | bytes 12992512 | tf_op jit(solution)/shard_map/dot_general | solution.py:153
  87.4 1.3 collective-permute-done.14
  88.7 2.4 %collective-permute-start.15 = (f32[1,1,1,8,8,128]{5,4,3,2,1,0:T(8,128)S(1)}, f32[1,1,1,8,8,128]{5,4,3,2,1,0:T(8,128)S(1)}, u32[]{:S(2)}, u32[]{:S(2)}) collective-permute-start(f32[1,1,1,8,8,128]{5,4,3,2,1,0:T(8,128)S(1)} %get-tuple-element.31), channel_id=1, source_target_pairs={{1,0},{2,1},{3,2},{5,4},{6,5},{7,6},{9,8},{10,9},{11,10},{13,12},{... | collective-permute-start | bytes 98312 | tf_op jit(solution)/shard_map/ppermute | solution.py:19
  91.1 1.4 fusion.9
  94.2 1.4 fusion.14
  95.6 0.9 fusion.7
  96.5 3.2 %fusion.17 = (bf16[4096,256]{1,0:T(8,128)(2,1)S(1)}, bf16[4096,256]{1,0:T(8,128)(2,1)S(1)}) fusion(s32[4096]{0:T(1024)S(1)} %add_select_fusion.2, bf16[4096]{0:T(1024)(128)(2,1)S(1)} %get-tuple-element.73, bf16[4096]{0:T(1024)(128)(2,1)S(1)} %get-tuple-element.74), kind=kLoop, calls=%fused_computation.23 | loop fusion | flops 3145728 | bytes 4227072 | tf_op jit(solution)/shard_map/mul | solution.py:165
  99.7 1.3 fusion.10
  101.1 1.2 copy.201
  102.3 5.3 %all-to-all-start = ((f32[32,2,2048]{2,1,0:T(2,128)}), f32[32,2,2048]{2,1,0:T(2,128)S(1)}, u32[]{:S(2)}, u32[]{:S(2)}) async-start(f32[32,2,2048]{2,1,0:T(2,128)} %bitcast.111), calls=%async_computation | async-start | bytes 1048576 | tf_op jit(solution)/shard_map/all_to_all | solution.py:182
  109.0 3.4 %collective-permute-start.16 = (f32[1,1,1,8,8,128]{5,4,3,2,1,0:T(8,128)S(1)}, f32[1,1,1,8,8,128]{5,4,3,2,1,0:T(8,128)S(1)}, u32[]{:S(2)}, u32[]{:S(2)}) collective-permute-start(f32[1,1,1,8,8,128]{5,4,3,2,1,0:T(8,128)S(1)} %get-tuple-element.50), channel_id=1, source_target_pairs={{0,4},{4,8},{8,12},{12,16},{16,20},{20,24},{24,28},{1,5},{5,9},{9,... | collective-permute-start | bytes 98312 | tf_op jit(solution)/shard_map/ppermute | solution.py:16
  112.3 1.3 collective-permute-start.17
  114.1 4.5 %collective-permute-done.17 = f32[1,1,1,8,8,128]{5,4,3,2,1,0:T(8,128)S(1)} collective-permute-done((f32[1,1,1,8,8,128]{5,4,3,2,1,0:T(8,128)S(1)}, f32[1,1,1,8,8,128]{5,4,3,2,1,0:T(8,128)S(1)}, u32[]{:S(2)}, u32[]{:S(2)}) %collective-permute-start.17) | collective-permute-done | bytes 32800 | tf_op jit(solution)/shard_map/ppermute | solution.py:19
  118.6 4.1 %all-to-all-done = f32[32,2,2048]{2,1,0:T(2,128)S(1)} async-done(((f32[32,2,2048]{2,1,0:T(2,128)}), f32[32,2,2048]{2,1,0:T(2,128)S(1)}, u32[]{:S(2)}, u32[]{:S(2)}) %all-to-all-start) | async-done | bytes 524320 | tf_op jit(solution)/shard_map/all_to_all | solution.py:182
  122.9 2.0 %collective-permute-start.18 = (f32[1,1,1,8,8,128]{5,3,4,2,1,0:T(8,128)S(1)}, f32[1,1,1,8,8,128]{5,3,4,2,1,0:T(8,128)S(1)}, u32[]{:S(2)}, u32[]{:S(2)}) collective-permute-start(f32[1,1,1,8,8,128]{5,3,4,2,1,0:T(8,128)S(1)} %maximum_bitcast_fusion.13), channel_id=1, source_target_pairs={{0,1},{1,2},{2,3},{4,5},{5,6},{6,7},{8,9},{9,10},{10,11},{12,13},{... | collective-permute-start | bytes 98312 | tf_op jit(solution)/shard_map/ppermute | solution.py:16
  124.8 3.3 %collective-permute-done.18 = f32[1,1,1,8,8,128]{5,3,4,2,1,0:T(8,128)S(1)} collective-permute-done((f32[1,1,1,8,8,128]{5,3,4,2,1,0:T(8,128)S(1)}, f32[1,1,1,8,8,128]{5,3,4,2,1,0:T(8,128)S(1)}, u32[]{:S(2)}, u32[]{:S(2)}) %collective-permute-start.18) | collective-permute-done | bytes 32800 | tf_op jit(solution)/shard_map/ppermute | solution.py:16
  128.1 1.9 %collective-permute-start.19 = (f32[1,1,1,8,8,128]{5,3,4,2,1,0:T(8,128)S(1)}, f32[1,1,1,8,8,128]{5,3,4,2,1,0:T(8,128)S(1)}, u32[]{:S(2)}, u32[]{:S(2)}) collective-permute-start(f32[1,1,1,8,8,128]{5,3,4,2,1,0:T(8,128)S(1)} %get-tuple-element.27), channel_id=1, source_target_pairs={{1,0},{2,1},{3,2},{5,4},{6,5},{7,6},{9,8},{10,9},{11,10},{13,12},{... | collective-permute-start | bytes 98312 | tf_op jit(solution)/shard_map/ppermute | solution.py:19
  130.8 3.4 %all-to-all-start.1 = ((f32[8,2,2048]{2,1,0:T(2,128)}), f32[8,2,2048]{2,1,0:T(2,128)S(1)}, u32[]{:S(2)}, u32[]{:S(2)}) async-start(f32[8,2,2048]{2,1,0:T(2,128)} %broadcast_in_dim.162), calls=%async_computation.1 | async-start | bytes 262144 | tf_op jit(solution)/shard_map/all_to_all | solution.py:189
  135.3 6.8 %all-to-all-done.1 = f32[8,2,2048]{2,1,0:T(2,128)S(1)} async-done(((f32[8,2,2048]{2,1,0:T(2,128)}), f32[8,2,2048]{2,1,0:T(2,128)S(1)}, u32[]{:S(2)}, u32[]{:S(2)}) %all-to-all-start.1) | async-done | bytes 131104 | tf_op jit(solution)/shard_map/all_to_all | solution.py:189
  (132 shorter events, 19.4 us)
Async XLA Ops:
  4.8 5.6 %collective-permute-start = (f32[2,1,1,8,8,128]{5,0,4,3,2,1:T(2,128)S(1)}, f32[2,1,1,8,8,128]{5,0,4,3,2,1:T(2,128)S(1)}, u32[]{:S(2)}, u32[]{:S(2)}) collective-permute-start(f32[2,1,1,8,8,128]{5,0,4,3,2,1:T(2,128)S(1)} %maximum_bitcast_fusion.9), channel_id=1, source_target_pairs={{0,4},{4,8},{8,12},{12,16},{16,20},{20,24},{24,28},{1,5},{5,9},{9,... | collective-permute-start | bytes 196616 | tf_op jit(solution)/shard_map/ppermute | solution.py:16
  11.3 6.2 %collective-permute-start.1 = (f32[2,1,1,8,8,128]{5,0,4,3,2,1:T(2,128)S(1)}, f32[2,1,1,8,8,128]{5,0,4,3,2,1:T(2,128)S(1)}, u32[]{:S(2)}, u32[]{:S(2)}) collective-permute-start(f32[2,1,1,8,8,128]{5,0,4,3,2,1:T(2,128)S(1)} %get-tuple-element.43), channel_id=1, source_target_pairs={{4,0},{8,4},{12,8},{16,12},{20,16},{24,20},{28,24},{5,1},{9,5},{13... | collective-permute-start | bytes 196616 | tf_op jit(solution)/shard_map/ppermute | solution.py:19
  17.6 5.6 %collective-permute-start.2 = (f32[2,1,1,8,8,128]{5,3,0,4,2,1:T(8,128)S(1)}, f32[2,1,1,8,8,128]{5,3,0,4,2,1:T(8,128)S(1)}, u32[]{:S(2)}, u32[]{:S(2)}) collective-permute-start(f32[2,1,1,8,8,128]{5,3,0,4,2,1:T(8,128)S(1)} %maximum_bitcast_fusion.7), channel_id=1, source_target_pairs={{0,1},{1,2},{2,3},{4,5},{5,6},{6,7},{8,9},{9,10},{10,11},{12,13},{... | collective-permute-start | bytes 196616 | tf_op jit(solution)/shard_map/ppermute | solution.py:16
  23.2 6.4 %copy-start = (f32[8,8,1,1]{1,0,3,2:T(8,128)S(1)}, f32[8,8,1,1]{1,0,3,2:T(8,128)}, u32[]{:S(2)}) copy-start(f32[8,8,1,1]{1,0,3,2:T(8,128)} %constant.134) | copy-start | bytes 772
  23.2 5.5 %collective-permute-start.3 = (f32[2,1,1,8,8,128]{5,3,0,4,2,1:T(8,128)S(1)}, f32[2,1,1,8,8,128]{5,3,0,4,2,1:T(8,128)S(1)}, u32[]{:S(2)}, u32[]{:S(2)}) collective-permute-start(f32[2,1,1,8,8,128]{5,3,0,4,2,1:T(8,128)S(1)} %get-tuple-element.41), channel_id=1, source_target_pairs={{1,0},{2,1},{3,2},{5,4},{6,5},{7,6},{9,8},{10,9},{11,10},{13,12},{... | collective-permute-start | bytes 196616 | tf_op jit(solution)/shard_map/ppermute | solution.py:19
  27.0 3.4 %copy-start.4 = (f32[8]{0:T(128)S(1)}, f32[8]{0:T(128)}, u32[]{:S(2)}) copy-start(f32[8]{0:T(128)} %constant.129) | copy-start | bytes 100
  28.9 8.7 %copy-start.1 = (s32[1,4096]{1,0:T(1,128)S(1)}, s32[1,4096]{1,0:T(1,128)}, u32[]{:S(2)}) copy-start(s32[1,4096]{1,0:T(1,128)} %param.40) | copy-start | bytes 49156
  28.9 8.7 %copy-start.2 = (s32[1,4096,1]{1,2,0:T(1,128)S(1)}, s32[1,4096,1]{1,2,0:T(1,128)}, u32[]{:S(2)}) copy-start(s32[1,4096,1]{1,2,0:T(1,128)} %param.39) | copy-start | bytes 49156
  31.5 6.4 %collective-permute-start.4 = (f32[1,1,1,8,8,128]{5,4,3,2,1,0:T(8,128)S(1)}, f32[1,1,1,8,8,128]{5,4,3,2,1,0:T(8,128)S(1)}, u32[]{:S(2)}, u32[]{:S(2)}) collective-permute-start(f32[1,1,1,8,8,128]{5,4,3,2,1,0:T(8,128)S(1)} %bitcast.480), channel_id=1, source_target_pairs={{0,4},{4,8},{8,12},{12,16},{16,20},{20,24},{24,28},{1,5},{5,9},{9,... | collective-permute-start | bytes 98312 | tf_op jit(solution)/shard_map/ppermute | solution.py:16
  36.3 5.8 %collective-permute-start.5 = (f32[1,1,1,8,8,128]{5,4,3,2,1,0:T(8,128)S(1)}, f32[1,1,1,8,8,128]{5,4,3,2,1,0:T(8,128)S(1)}, u32[]{:S(2)}, u32[]{:S(2)}) collective-permute-start(f32[1,1,1,8,8,128]{5,4,3,2,1,0:T(8,128)S(1)} %bitcast.482), channel_id=1, source_target_pairs={{4,0},{8,4},{12,8},{16,12},{20,16},{24,20},{28,24},{5,1},{9,5},{13... | collective-permute-start | bytes 98312 | tf_op jit(solution)/shard_map/ppermute | solution.py:19
  42.2 5.2 %collective-permute-start.6 = (f32[1,1,1,8,8,128]{5,3,4,2,1,0:T(8,128)S(1)}, f32[1,1,1,8,8,128]{5,3,4,2,1,0:T(8,128)S(1)}, u32[]{:S(2)}, u32[]{:S(2)}) collective-permute-start(f32[1,1,1,8,8,128]{5,3,4,2,1,0:T(8,128)S(1)} %maximum_bitcast_fusion.19), channel_id=1, source_target_pairs={{0,1},{1,2},{2,3},{4,5},{5,6},{6,7},{8,9},{9,10},{10,11},{12,13},{... | collective-permute-start | bytes 98312 | tf_op jit(solution)/shard_map/ppermute | solution.py:16
  47.4 3.9 %collective-permute-start.7 = (f32[1,1,1,8,8,128]{5,3,4,2,1,0:T(8,128)S(1)}, f32[1,1,1,8,8,128]{5,3,4,2,1,0:T(8,128)S(1)}, u32[]{:S(2)}, u32[]{:S(2)}) collective-permute-start(f32[1,1,1,8,8,128]{5,3,4,2,1,0:T(8,128)S(1)} %get-tuple-element.37), channel_id=1, source_target_pairs={{1,0},{2,1},{3,2},{5,4},{6,5},{7,6},{9,8},{10,9},{11,10},{13,12},{... | collective-permute-start | bytes 98312 | tf_op jit(solution)/shard_map/ppermute | solution.py:19
  49.8 20.8 %copy-start.5 = (s32[1,4096]{1,0:T(1,128)S(1)}, s32[1,4096]{1,0:T(1,128)}, u32[]{:S(2)}) copy-start(s32[1,4096]{1,0:T(1,128)} %param.38) | copy-start | bytes 49156
  53.2 5.9 %collective-permute-start.8 = (f32[1,1,1,8,8,128]{5,4,3,2,1,0:T(8,128)S(1)}, f32[1,1,1,8,8,128]{5,4,3,2,1,0:T(8,128)S(1)}, u32[]{:S(2)}, u32[]{:S(2)}) collective-permute-start(f32[1,1,1,8,8,128]{5,4,3,2,1,0:T(8,128)S(1)} %get-tuple-element.65), channel_id=1, source_target_pairs={{0,4},{4,8},{8,12},{12,16},{16,20},{20,24},{24,28},{1,5},{5,9},{9,... | collective-permute-start | bytes 98312 | tf_op jit(solution)/shard_map/ppermute | solution.py:16
  57.5 5.8 %collective-permute-start.9 = (f32[1,1,1,8,8,128]{5,4,3,2,1,0:T(8,128)S(1)}, f32[1,1,1,8,8,128]{5,4,3,2,1,0:T(8,128)S(1)}, u32[]{:S(2)}, u32[]{:S(2)}) collective-permute-start(f32[1,1,1,8,8,128]{5,4,3,2,1,0:T(8,128)S(1)} %get-tuple-element.66), channel_id=1, source_target_pairs={{4,0},{8,4},{12,8},{16,12},{20,16},{24,20},{28,24},{5,1},{9,5},{13... | collective-permute-start | bytes 98312 | tf_op jit(solution)/shard_map/ppermute | solution.py:19
  63.4 5.2 %collective-permute-start.10 = (f32[1,1,1,8,8,128]{5,4,3,2,1,0:T(8,128)S(1)}, f32[1,1,1,8,8,128]{5,4,3,2,1,0:T(8,128)S(1)}, u32[]{:S(2)}, u32[]{:S(2)}) collective-permute-start(f32[1,1,1,8,8,128]{5,4,3,2,1,0:T(8,128)S(1)} %maximum_bitcast_fusion.17), channel_id=1, source_target_pairs={{0,1},{1,2},{2,3},{4,5},{5,6},{6,7},{8,9},{9,10},{10,11},{12,13},{... | collective-permute-start | bytes 98312 | tf_op jit(solution)/shard_map/ppermute | solution.py:16
  68.6 3.5 %collective-permute-start.11 = (f32[1,1,1,8,8,128]{5,4,3,2,1,0:T(8,128)S(1)}, f32[1,1,1,8,8,128]{5,4,3,2,1,0:T(8,128)S(1)}, u32[]{:S(2)}, u32[]{:S(2)}) collective-permute-start(f32[1,1,1,8,8,128]{5,4,3,2,1,0:T(8,128)S(1)} %get-tuple-element.35), channel_id=1, source_target_pairs={{1,0},{2,1},{3,2},{5,4},{6,5},{7,6},{9,8},{10,9},{11,10},{13,12},{... | collective-permute-start | bytes 98312 | tf_op jit(solution)/shard_map/ppermute | solution.py:19
  74.2 5.0 %collective-permute-start.12 = (f32[1,1,1,8,8,128]{5,4,3,2,1,0:T(8,128)S(1)}, f32[1,1,1,8,8,128]{5,4,3,2,1,0:T(8,128)S(1)}, u32[]{:S(2)}, u32[]{:S(2)}) collective-permute-start(f32[1,1,1,8,8,128]{5,4,3,2,1,0:T(8,128)S(1)} %get-tuple-element.59), channel_id=1, source_target_pairs={{0,4},{4,8},{8,12},{12,16},{16,20},{20,24},{24,28},{1,5},{5,9},{9,... | collective-permute-start | bytes 98312 | tf_op jit(solution)/shard_map/ppermute | solution.py:16
  77.6 5.8 %collective-permute-start.13 = (f32[1,1,1,8,8,128]{5,4,3,2,1,0:T(8,128)S(1)}, f32[1,1,1,8,8,128]{5,4,3,2,1,0:T(8,128)S(1)}, u32[]{:S(2)}, u32[]{:S(2)}) collective-permute-start(f32[1,1,1,8,8,128]{5,4,3,2,1,0:T(8,128)S(1)} %get-tuple-element.60), channel_id=1, source_target_pairs={{4,0},{8,4},{12,8},{16,12},{20,16},{24,20},{28,24},{5,1},{9,5},{13... | collective-permute-start | bytes 98312 | tf_op jit(solution)/shard_map/ppermute | solution.py:19
  83.5 5.2 %collective-permute-start.14 = (f32[1,1,1,8,8,128]{5,4,3,2,1,0:T(8,128)S(1)}, f32[1,1,1,8,8,128]{5,4,3,2,1,0:T(8,128)S(1)}, u32[]{:S(2)}, u32[]{:S(2)}) collective-permute-start(f32[1,1,1,8,8,128]{5,4,3,2,1,0:T(8,128)S(1)} %maximum_bitcast_fusion.15), channel_id=1, source_target_pairs={{0,1},{1,2},{2,3},{4,5},{5,6},{6,7},{8,9},{9,10},{10,11},{12,13},{... | collective-permute-start | bytes 98312 | tf_op jit(solution)/shard_map/ppermute | solution.py:16
  88.7 4.0 %collective-permute-start.15 = (f32[1,1,1,8,8,128]{5,4,3,2,1,0:T(8,128)S(1)}, f32[1,1,1,8,8,128]{5,4,3,2,1,0:T(8,128)S(1)}, u32[]{:S(2)}, u32[]{:S(2)}) collective-permute-start(f32[1,1,1,8,8,128]{5,4,3,2,1,0:T(8,128)S(1)} %get-tuple-element.31), channel_id=1, source_target_pairs={{1,0},{2,1},{3,2},{5,4},{6,5},{7,6},{9,8},{10,9},{11,10},{13,12},{... | collective-permute-start | bytes 98312 | tf_op jit(solution)/shard_map/ppermute | solution.py:19
  95.6 0.9 copy-start.3
  102.3 20.3 %all-to-all-start = ((f32[32,2,2048]{2,1,0:T(2,128)}), f32[32,2,2048]{2,1,0:T(2,128)S(1)}, u32[]{:S(2)}, u32[]{:S(2)}) async-start(f32[32,2,2048]{2,1,0:T(2,128)} %bitcast.111), calls=%async_computation | async-start | bytes 1048576 | tf_op jit(solution)/shard_map/all_to_all | solution.py:182
  109.0 5.1 %collective-permute-start.16 = (f32[1,1,1,8,8,128]{5,4,3,2,1,0:T(8,128)S(1)}, f32[1,1,1,8,8,128]{5,4,3,2,1,0:T(8,128)S(1)}, u32[]{:S(2)}, u32[]{:S(2)}) collective-permute-start(f32[1,1,1,8,8,128]{5,4,3,2,1,0:T(8,128)S(1)} %get-tuple-element.50), channel_id=1, source_target_pairs={{0,4},{4,8},{8,12},{12,16},{16,20},{20,24},{24,28},{1,5},{5,9},{9,... | collective-permute-start | bytes 98312 | tf_op jit(solution)/shard_map/ppermute | solution.py:16
  112.3 6.2 %collective-permute-start.17 = (f32[1,1,1,8,8,128]{5,4,3,2,1,0:T(8,128)S(1)}, f32[1,1,1,8,8,128]{5,4,3,2,1,0:T(8,128)S(1)}, u32[]{:S(2)}, u32[]{:S(2)}) collective-permute-start(f32[1,1,1,8,8,128]{5,4,3,2,1,0:T(8,128)S(1)} %get-tuple-element.51), channel_id=1, source_target_pairs={{4,0},{8,4},{12,8},{16,12},{20,16},{24,20},{28,24},{5,1},{9,5},{13... | collective-permute-start | bytes 98312 | tf_op jit(solution)/shard_map/ppermute | solution.py:19
  122.9 5.2 %collective-permute-start.18 = (f32[1,1,1,8,8,128]{5,3,4,2,1,0:T(8,128)S(1)}, f32[1,1,1,8,8,128]{5,3,4,2,1,0:T(8,128)S(1)}, u32[]{:S(2)}, u32[]{:S(2)}) collective-permute-start(f32[1,1,1,8,8,128]{5,3,4,2,1,0:T(8,128)S(1)} %maximum_bitcast_fusion.13), channel_id=1, source_target_pairs={{0,1},{1,2},{2,3},{4,5},{5,6},{6,7},{8,9},{9,10},{10,11},{12,13},{... | collective-permute-start | bytes 98312 | tf_op jit(solution)/shard_map/ppermute | solution.py:16
  128.1 6.1 %collective-permute-start.19 = (f32[1,1,1,8,8,128]{5,3,4,2,1,0:T(8,128)S(1)}, f32[1,1,1,8,8,128]{5,3,4,2,1,0:T(8,128)S(1)}, u32[]{:S(2)}, u32[]{:S(2)}) collective-permute-start(f32[1,1,1,8,8,128]{5,3,4,2,1,0:T(8,128)S(1)} %get-tuple-element.27), channel_id=1, source_target_pairs={{1,0},{2,1},{3,2},{5,4},{6,5},{7,6},{9,8},{10,9},{11,10},{13,12},{... | collective-permute-start | bytes 98312 | tf_op jit(solution)/shard_map/ppermute | solution.py:19
  130.8 11.2 %all-to-all-start.1 = ((f32[8,2,2048]{2,1,0:T(2,128)}), f32[8,2,2048]{2,1,0:T(2,128)S(1)}, u32[]{:S(2)}, u32[]{:S(2)}) async-start(f32[8,2,2048]{2,1,0:T(2,128)} %broadcast_in_dim.162), calls=%async_computation.1 | async-start | bytes 262144 | tf_op jit(solution)/shard_map/all_to_all | solution.py:189

commit v11 on v10

--- a/solution.py
+++ b/solution.py
@@ -161,13 +161,14 @@
 
 def segment_sum(values, ids, bins, lanes, count=3):
     rows = bins // lanes
-    hit_lane = one_hot(ids % lanes, lanes)
-    rhs = jnp.concatenate([hit_lane * part[:, None] for part in split_parts(values, count)], axis=1)
-    hit_row_t = (lax.broadcasted_iota(jnp.int32, (rows, 1), 0) == (ids // lanes)[None, :]).astype(jnp.bfloat16)
-    sums = jnp.dot(hit_row_t, rhs, preferred_element_type=jnp.float32)
-    total = sums[:, :lanes]
+    hit_row_t = lax.broadcasted_iota(jnp.int32, (rows, 1), 0) == (ids // lanes)[None, :]
+    lhs = jnp.concatenate(
+        [jnp.where(hit_row_t, part[None, :], jnp.bfloat16(0)) for part in split_parts(values, count)], axis=0
+    )
+    sums = jnp.dot(lhs, one_hot(ids % lanes, lanes), preferred_element_type=jnp.float32)
+    total = sums[:rows]
     for n in range(1, count):
-        total = total + sums[:, n * lanes : (n + 1) * lanes]
+        total = total + sums[n * rows : (n + 1) * rows]
     return total.reshape(-1)
 
 

time: 144 us -> 139 us (0.965)
  other arithmetic: 21.4 us -> 14.4 us
  waiting for transfers between devices: 45.8 us -> 50.5 us
  starting transfers between devices: 56.6 us -> 54.1 us
    mul x2 -> x0, other arithmetic: 6.85 us -> none  [segment_sum(): hit_lane * part[:, None]]
    ppermute x10, waiting for transfers between devices: 9.89 us -> 13.8 us  [padded_2(): lax.ppermute(lax.slice_in_dim(block, block.shape[dim] - width, None, axis...]
    ppermute x10, starting transfers between devices: 18.8 us -> 17.1 us  [padded_2(): lax.ppermute(lax.slice_in_dim(block, 0, width, axis=dim), axis, backward)]
  transfers between devices with their start and end apart: 22 -> 22, of which waited for: 18 -> 20; matrix products, arithmetic and copies ran while one was open for 12% -> 9% of each run, Pallas kernels for 0% -> 0%
where the time goes in v11:
time: 139 us; the launch traced here: 138 us
  starting transfers between devices  54.1 us (39%)
  waiting for transfers between devices  50.5 us (36%)
  other arithmetic  14.4 us (10%)
  matrix products  12.3 us (9%)
  local copies, waits for them, and re-layouts  5.3 us (4%)
  between operations  1.6 us (1%)
    ppermute x10, starting transfers between devices, padded_2(): lax.ppermute(lax.slice_in_dim(block, block.shape[dim] - width, None, axis...  28.5 us
    ppermute x10, waiting for transfers between devices, padded_2(): lax.ppermute(lax.slice_in_dim(block, 0, width, axis=dim), axis, backward)  25.8 us
    ppermute x10, starting transfers between devices, padded_2(): lax.ppermute(lax.slice_in_dim(block, 0, width, axis=dim), axis, backward)  17.1 us
    ppermute x10, waiting for transfers between devices, padded_2(): lax.ppermute(lax.slice_in_dim(block, block.shape[dim] - width, None, axis...  13.8 us
    all_to_all x1, waiting for transfers between devices, strip_gather(): whole = lax.all_to_all(spread_out, 'ex', 0, 0, tiled=True)  6.78 us
    all_to_all x1, starting transfers between devices, strip_reduce(): return lax.all_to_all(chunks, ('ex', 'ey'), 0, 0, tiled=True).sum(0)  5.08 us
    all_to_all x1, waiting for transfers between devices, strip_reduce(): return lax.all_to_all(chunks, ('ex', 'ey'), 0, 0, tiled=True).sum(0)  4.09 us
    all_to_all x1, starting transfers between devices, strip_gather(): whole = lax.all_to_all(spread_out, 'ex', 0, 0, tiled=True)  3.45 us
  transfers between devices with their start and end apart: 22, of which 20 were waited for; matrix products, arithmetic and copies ran while one was open for 9% of the time, Pallas kernels for 0%

profile of v11, /device:TPU:2, one launch (start us, length us, event | category | flops | bytes accessed | tf_op | source)
XLA Modules:
  0.0 138.2 jit_solution(380697150070759667)
XLA Ops:
  2.9 1.2 fusion.90
  4.9 3.4 %collective-permute-start = (f32[2,1,1,8,8,128]{5,0,4,3,2,1:T(2,128)S(1)}, f32[2,1,1,8,8,128]{5,0,4,3,2,1:T(2,128)S(1)}, u32[]{:S(2)}, u32[]{:S(2)}) collective-permute-start(f32[2,1,1,8,8,128]{5,0,4,3,2,1:T(2,128)S(1)} %maximum_bitcast_fusion.9), channel_id=1, source_target_pairs={{0,4},{4,8},{8,12},{12,16},{16,20},{20,24},{24,28},{1,5},{5,9},{9,... | collective-permute-start | bytes 196616 | tf_op jit(solution)/shard_map/ppermute | solution.py:16
  10.0 1.2 fusion.20
  11.3 1.3 collective-permute-start.1
  13.3 4.3 %collective-permute-done.1 = f32[2,1,1,8,8,128]{5,0,4,3,2,1:T(2,128)S(1)} collective-permute-done((f32[2,1,1,8,8,128]{5,0,4,3,2,1:T(2,128)S(1)}, f32[2,1,1,8,8,128]{5,0,4,3,2,1:T(2,128)S(1)}, u32[]{:S(2)}, u32[]{:S(2)}) %collective-permute-start.1) | collective-permute-done | bytes 65568 | tf_op jit(solution)/shard_map/ppermute | solution.py:19
  17.6 1.9 %collective-permute-start.2 = (f32[2,1,1,8,8,128]{5,3,0,4,2,1:T(8,128)S(1)}, f32[2,1,1,8,8,128]{5,3,0,4,2,1:T(8,128)S(1)}, u32[]{:S(2)}, u32[]{:S(2)}) collective-permute-start(f32[2,1,1,8,8,128]{5,3,0,4,2,1:T(8,128)S(1)} %maximum_bitcast_fusion.7), channel_id=1, source_target_pairs={{0,1},{1,2},{2,3},{4,5},{5,6},{6,7},{8,9},{9,10},{10,11},{12,13},{... | collective-permute-start | bytes 196616 | tf_op jit(solution)/shard_map/ppermute | solution.py:16
  19.5 3.6 %collective-permute-done.2 = f32[2,1,1,8,8,128]{5,3,0,4,2,1:T(8,128)S(1)} collective-permute-done((f32[2,1,1,8,8,128]{5,3,0,4,2,1:T(8,128)S(1)}, f32[2,1,1,8,8,128]{5,3,0,4,2,1:T(8,128)S(1)}, u32[]{:S(2)}, u32[]{:S(2)}) %collective-permute-start.2) | collective-permute-done | bytes 65568 | tf_op jit(solution)/shard_map/ppermute | solution.py:16
  23.2 1.9 %collective-permute-start.3 = (f32[2,1,1,8,8,128]{5,3,0,4,2,1:T(8,128)S(1)}, f32[2,1,1,8,8,128]{5,3,0,4,2,1:T(8,128)S(1)}, u32[]{:S(2)}, u32[]{:S(2)}) collective-permute-start(f32[2,1,1,8,8,128]{5,3,0,4,2,1:T(8,128)S(1)} %get-tuple-element.44), channel_id=1, source_target_pairs={{1,0},{2,1},{3,2},{5,4},{6,5},{7,6},{9,8},{10,9},{11,10},{13,12},{... | collective-permute-start | bytes 196616 | tf_op jit(solution)/shard_map/ppermute | solution.py:19
  25.5 1.5 %collective-permute-done.3 = f32[2,1,1,8,8,128]{5,3,0,4,2,1:T(8,128)S(1)} collective-permute-done((f32[2,1,1,8,8,128]{5,3,0,4,2,1:T(8,128)S(1)}, f32[2,1,1,8,8,128]{5,3,0,4,2,1:T(8,128)S(1)}, u32[]{:S(2)}, u32[]{:S(2)}) %collective-permute-start.3) | collective-permute-done | bytes 65568 | tf_op jit(solution)/shard_map/ppermute | solution.py:19
  28.8 0.9 fusion.30
  29.8 4.3 %collective-permute-start.4 = (f32[1,1,1,8,8,128]{5,4,3,2,1,0:T(8,128)S(1)}, f32[1,1,1,8,8,128]{5,4,3,2,1,0:T(8,128)S(1)}, u32[]{:S(2)}, u32[]{:S(2)}) collective-permute-start(f32[1,1,1,8,8,128]{5,4,3,2,1,0:T(8,128)S(1)} %bitcast.482), channel_id=1, source_target_pairs={{0,4},{4,8},{8,12},{12,16},{16,20},{20,24},{24,28},{1,5},{5,9},{9,... | collective-permute-start | bytes 98312 | tf_op jit(solution)/shard_map/ppermute | solution.py:16
  34.1 1.3 collective-permute-start.5
  35.7 4.2 %collective-permute-done.5 = f32[1,1,1,8,8,128]{5,4,3,2,1,0:T(8,128)S(1)} collective-permute-done((f32[1,1,1,8,8,128]{5,4,3,2,1,0:T(8,128)S(1)}, f32[1,1,1,8,8,128]{5,4,3,2,1,0:T(8,128)S(1)}, u32[]{:S(2)}, u32[]{:S(2)}) %collective-permute-start.5) | collective-permute-done | bytes 32800 | tf_op jit(solution)/shard_map/ppermute | solution.py:19
  39.9 1.9 %collective-permute-start.6 = (f32[1,1,1,8,8,128]{5,3,4,2,1,0:T(8,128)S(1)}, f32[1,1,1,8,8,128]{5,3,4,2,1,0:T(8,128)S(1)}, u32[]{:S(2)}, u32[]{:S(2)}) collective-permute-start(f32[1,1,1,8,8,128]{5,3,4,2,1,0:T(8,128)S(1)} %maximum_bitcast_fusion.19), channel_id=1, source_target_pairs={{0,1},{1,2},{2,3},{4,5},{5,6},{6,7},{8,9},{9,10},{10,11},{12,13},{... | collective-permute-start | bytes 98312 | tf_op jit(solution)/shard_map/ppermute | solution.py:16
  41.9 1.9 %fusion = f32[768,256]{1,0:T(8,128)S(1)} fusion(bf16[256,4096]{1,0:T(8,128)(2,1)S(1)} %get-tuple-element.83, bf16[256,4096]{1,0:T(8,128)(2,1)S(1)} %get-tuple-element.84, bf16[256,4096]{1,0:T(8,128)(2,1)S(1)} %get-tuple-element.82, s32[4096]{0:T(1024)S(1)} %add_select_fusion.2), kind=kOutput, calls=%fused_computation | convolution fusion | flops 1630535680 | bytes 7094272 | tf_op jit(solution)/shard_map/dot_general | solution.py:168
  43.8 1.4 collective-permute-done.6
  45.2 2.3 %collective-permute-start.7 = (f32[1,1,1,8,8,128]{5,3,4,2,1,0:T(8,128)S(1)}, f32[1,1,1,8,8,128]{5,3,4,2,1,0:T(8,128)S(1)}, u32[]{:S(2)}, u32[]{:S(2)}) collective-permute-start(f32[1,1,1,8,8,128]{5,3,4,2,1,0:T(8,128)S(1)} %get-tuple-element.40), channel_id=1, source_target_pairs={{1,0},{2,1},{3,2},{5,4},{6,5},{7,6},{9,8},{10,9},{11,10},{13,12},{... | collective-permute-start | bytes 98312 | tf_op jit(solution)/shard_map/ppermute | solution.py:19
  47.7 1.4 collective-permute-done.7
  51.0 4.1 %collective-permute-start.8 = (f32[1,1,1,8,8,128]{5,4,3,2,1,0:T(8,128)S(1)}, f32[1,1,1,8,8,128]{5,4,3,2,1,0:T(8,128)S(1)}, u32[]{:S(2)}, u32[]{:S(2)}) collective-permute-start(f32[1,1,1,8,8,128]{5,4,3,2,1,0:T(8,128)S(1)} %get-tuple-element.68), channel_id=1, source_target_pairs={{0,4},{4,8},{8,12},{12,16},{16,20},{20,24},{24,28},{1,5},{5,9},{9,... | collective-permute-start | bytes 98312 | tf_op jit(solution)/shard_map/ppermute | solution.py:16
  55.1 1.3 collective-permute-start.9
  56.7 4.2 %collective-permute-done.9 = f32[1,1,1,8,8,128]{5,4,3,2,1,0:T(8,128)S(1)} collective-permute-done((f32[1,1,1,8,8,128]{5,4,3,2,1,0:T(8,128)S(1)}, f32[1,1,1,8,8,128]{5,4,3,2,1,0:T(8,128)S(1)}, u32[]{:S(2)}, u32[]{:S(2)}) %collective-permute-start.9) | collective-permute-done | bytes 32800 | tf_op jit(solution)/shard_map/ppermute | solution.py:19
  60.9 1.9 %collective-permute-start.10 = (f32[1,1,1,8,8,128]{5,4,3,2,1,0:T(8,128)S(1)}, f32[1,1,1,8,8,128]{5,4,3,2,1,0:T(8,128)S(1)}, u32[]{:S(2)}, u32[]{:S(2)}) collective-permute-start(f32[1,1,1,8,8,128]{5,4,3,2,1,0:T(8,128)S(1)} %maximum_bitcast_fusion.17), channel_id=1, source_target_pairs={{0,1},{1,2},{2,3},{4,5},{5,6},{6,7},{8,9},{9,10},{10,11},{12,13},{... | collective-permute-start | bytes 98312 | tf_op jit(solution)/shard_map/ppermute | solution.py:16
  62.8 3.3 %collective-permute-done.10 = f32[1,1,1,8,8,128]{5,4,3,2,1,0:T(8,128)S(1)} collective-permute-done((f32[1,1,1,8,8,128]{5,4,3,2,1,0:T(8,128)S(1)}, f32[1,1,1,8,8,128]{5,4,3,2,1,0:T(8,128)S(1)}, u32[]{:S(2)}, u32[]{:S(2)}) %collective-permute-start.10) | collective-permute-done | bytes 32800 | tf_op jit(solution)/shard_map/ppermute | solution.py:16
  66.2 2.1 %collective-permute-start.11 = (f32[1,1,1,8,8,128]{5,4,3,2,1,0:T(8,128)S(1)}, f32[1,1,1,8,8,128]{5,4,3,2,1,0:T(8,128)S(1)}, u32[]{:S(2)}, u32[]{:S(2)}) collective-permute-start(f32[1,1,1,8,8,128]{5,4,3,2,1,0:T(8,128)S(1)} %get-tuple-element.38), channel_id=1, source_target_pairs={{1,0},{2,1},{3,2},{5,4},{6,5},{7,6},{9,8},{10,9},{11,10},{13,12},{... | collective-permute-start | bytes 98312 | tf_op jit(solution)/shard_map/ppermute | solution.py:19
  68.4 1.3 collective-permute-done.11
  71.7 3.6 %collective-permute-start.12 = (f32[1,1,1,8,8,128]{5,4,3,2,1,0:T(8,128)S(1)}, f32[1,1,1,8,8,128]{5,4,3,2,1,0:T(8,128)S(1)}, u32[]{:S(2)}, u32[]{:S(2)}) collective-permute-start(f32[1,1,1,8,8,128]{5,4,3,2,1,0:T(8,128)S(1)} %get-tuple-element.62), channel_id=1, source_target_pairs={{0,4},{4,8},{8,12},{12,16},{16,20},{20,24},{24,28},{1,5},{5,9},{9,... | collective-permute-start | bytes 98312 | tf_op jit(solution)/shard_map/ppermute | solution.py:16
  75.4 1.3 collective-permute-start.13
  77.0 4.2 %collective-permute-done.13 = f32[1,1,1,8,8,128]{5,4,3,2,1,0:T(8,128)S(1)} collective-permute-done((f32[1,1,1,8,8,128]{5,4,3,2,1,0:T(8,128)S(1)}, f32[1,1,1,8,8,128]{5,4,3,2,1,0:T(8,128)S(1)}, u32[]{:S(2)}, u32[]{:S(2)}) %collective-permute-start.13) | collective-permute-done | bytes 32800 | tf_op jit(solution)/shard_map/ppermute | solution.py:19
  81.2 1.9 %collective-permute-start.14 = (f32[1,1,1,8,8,128]{5,4,3,2,1,0:T(8,128)S(1)}, f32[1,1,1,8,8,128]{5,4,3,2,1,0:T(8,128)S(1)}, u32[]{:S(2)}, u32[]{:S(2)}) collective-permute-start(f32[1,1,1,8,8,128]{5,4,3,2,1,0:T(8,128)S(1)} %maximum_bitcast_fusion.15), channel_id=1, source_target_pairs={{0,1},{1,2},{2,3},{4,5},{5,6},{6,7},{8,9},{9,10},{10,11},{12,13},{... | collective-permute-start | bytes 98312 | tf_op jit(solution)/shard_map/ppermute | solution.py:16
  83.2 2.0 %fusion.15 = f32[4096,768]{0,1:T(8,128)S(1)} fusion(s32[4096]{0:T(1024)S(1)} %get-tuple-element.81, bf16[256,256]{1,0:T(8,128)(2,1)S(1)} %get-tuple-element.56, bf16[256,256]{1,0:T(8,128)(2,1)S(1)} %get-tuple-element.57, bf16[256,256]{1,0:T(8,128)(2,1)S(1)} %get-tuple-element.55), kind=kOutput, calls=%fused_computation.19 | convolution fusion | flops 1612840960 | bytes 12992512 | tf_op jit(solution)/shard_map/dot_general | solution.py:153
  85.2 1.3 collective-permute-done.14
  86.5 2.4 %collective-permute-start.15 = (f32[1,1,1,8,8,128]{5,4,3,2,1,0:T(8,128)S(1)}, f32[1,1,1,8,8,128]{5,4,3,2,1,0:T(8,128)S(1)}, u32[]{:S(2)}, u32[]{:S(2)}) collective-permute-start(f32[1,1,1,8,8,128]{5,4,3,2,1,0:T(8,128)S(1)} %get-tuple-element.34), channel_id=1, source_target_pairs={{1,0},{2,1},{3,2},{5,4},{6,5},{7,6},{9,8},{10,9},{11,10},{13,12},{... | collective-permute-start | bytes 98312 | tf_op jit(solution)/shard_map/ppermute | solution.py:19
  88.8 1.4 fusion.9
  91.9 1.4 %fusion.14 = f32[4096,512]{0,1:T(8,128)S(1)} fusion(s32[4096]{0:T(1024)S(1)} %get-tuple-element.81, bf16[256,256]{1,0:T(8,128)(2,1)S(1)} %get-tuple-element.52, bf16[256,256]{1,0:T(8,128)(2,1)S(1)} %get-tuple-element.51), kind=kOutput, calls=%fused_computation.18 | convolution fusion | flops 1075314688 | bytes 8667136 | tf_op jit(solution)/shard_map/dot_general | solution.py:153
  93.3 0.9 fusion.7
  94.3 0.9 fusion.17
  95.1 1.4 %fusion.10 = f32[512,256]{1,0:T(8,128)S(1)} fusion(bf16[256,4096]{1,0:T(8,128)(2,1)S(1)} %get-tuple-element.79, bf16[256,4096]{1,0:T(8,128)(2,1)S(1)} %get-tuple-element.78, s32[4096]{0:T(1024)S(1)} %add_select_fusion.2), kind=kOutput, calls=%fused_computation.13 | convolution fusion | flops 1083179008 | bytes 4734976 | tf_op jit(solution)/shard_map/dot_general | solution.py:168
  96.7 1.2 copy.201
  97.9 5.1 %all-to-all-start = ((f32[32,2,2048]{2,1,0:T(2,128)}), f32[32,2,2048]{2,1,0:T(2,128)S(1)}, u32[]{:S(2)}, u32[]{:S(2)}) async-start(f32[32,2,2048]{2,1,0:T(2,128)} %bitcast.111), calls=%async_computation | async-start | bytes 1048576 | tf_op jit(solution)/shard_map/all_to_all | solution.py:183
  104.3 3.4 %collective-permute-start.16 = (f32[1,1,1,8,8,128]{5,4,3,2,1,0:T(8,128)S(1)}, f32[1,1,1,8,8,128]{5,4,3,2,1,0:T(8,128)S(1)}, u32[]{:S(2)}, u32[]{:S(2)}) collective-permute-start(f32[1,1,1,8,8,128]{5,4,3,2,1,0:T(8,128)S(1)} %get-tuple-element.53), channel_id=1, source_target_pairs={{0,4},{4,8},{8,12},{12,16},{16,20},{20,24},{24,28},{1,5},{5,9},{9,... | collective-permute-start | bytes 98312 | tf_op jit(solution)/shard_map/ppermute | solution.py:16
  107.7 1.3 collective-permute-start.17
  109.4 4.5 %collective-permute-done.17 = f32[1,1,1,8,8,128]{5,4,3,2,1,0:T(8,128)S(1)} collective-permute-done((f32[1,1,1,8,8,128]{5,4,3,2,1,0:T(8,128)S(1)}, f32[1,1,1,8,8,128]{5,4,3,2,1,0:T(8,128)S(1)}, u32[]{:S(2)}, u32[]{:S(2)}) %collective-permute-start.17) | collective-permute-done | bytes 32800 | tf_op jit(solution)/shard_map/ppermute | solution.py:19
  114.0 4.1 %all-to-all-done = f32[32,2,2048]{2,1,0:T(2,128)S(1)} async-done(((f32[32,2,2048]{2,1,0:T(2,128)}), f32[32,2,2048]{2,1,0:T(2,128)S(1)}, u32[]{:S(2)}, u32[]{:S(2)}) %all-to-all-start) | async-done | bytes 524320 | tf_op jit(solution)/shard_map/all_to_all | solution.py:183
  118.3 2.0 %collective-permute-start.18 = (f32[1,1,1,8,8,128]{5,3,4,2,1,0:T(8,128)S(1)}, f32[1,1,1,8,8,128]{5,3,4,2,1,0:T(8,128)S(1)}, u32[]{:S(2)}, u32[]{:S(2)}) collective-permute-start(f32[1,1,1,8,8,128]{5,3,4,2,1,0:T(8,128)S(1)} %maximum_bitcast_fusion.13), channel_id=1, source_target_pairs={{0,1},{1,2},{2,3},{4,5},{5,6},{6,7},{8,9},{9,10},{10,11},{12,13},{... | collective-permute-start | bytes 98312 | tf_op jit(solution)/shard_map/ppermute | solution.py:16
  120.2 3.3 %collective-permute-done.18 = f32[1,1,1,8,8,128]{5,3,4,2,1,0:T(8,128)S(1)} collective-permute-done((f32[1,1,1,8,8,128]{5,3,4,2,1,0:T(8,128)S(1)}, f32[1,1,1,8,8,128]{5,3,4,2,1,0:T(8,128)S(1)}, u32[]{:S(2)}, u32[]{:S(2)}) %collective-permute-start.18) | collective-permute-done | bytes 32800 | tf_op jit(solution)/shard_map/ppermute | solution.py:16
  123.5 1.9 %collective-permute-start.19 = (f32[1,1,1,8,8,128]{5,3,4,2,1,0:T(8,128)S(1)}, f32[1,1,1,8,8,128]{5,3,4,2,1,0:T(8,128)S(1)}, u32[]{:S(2)}, u32[]{:S(2)}) collective-permute-start(f32[1,1,1,8,8,128]{5,3,4,2,1,0:T(8,128)S(1)} %get-tuple-element.30), channel_id=1, source_target_pairs={{1,0},{2,1},{3,2},{5,4},{6,5},{7,6},{9,8},{10,9},{11,10},{13,12},{... | collective-permute-start | bytes 98312 | tf_op jit(solution)/shard_map/ppermute | solution.py:19
  126.2 3.4 %all-to-all-start.1 = ((f32[8,2,2048]{2,1,0:T(2,128)}), f32[8,2,2048]{2,1,0:T(2,128)S(1)}, u32[]{:S(2)}, u32[]{:S(2)}) async-start(f32[8,2,2048]{2,1,0:T(2,128)} %broadcast_in_dim.213), calls=%async_computation.1 | async-start | bytes 262144 | tf_op jit(solution)/shard_map/all_to_all | solution.py:190
  130.6 6.8 %all-to-all-done.1 = f32[8,2,2048]{2,1,0:T(2,128)S(1)} async-done(((f32[8,2,2048]{2,1,0:T(2,128)}), f32[8,2,2048]{2,1,0:T(2,128)S(1)}, u32[]{:S(2)}, u32[]{:S(2)}) %all-to-all-start.1) | async-done | bytes 131104 | tf_op jit(solution)/shard_map/all_to_all | solution.py:190
  (134 shorter events, 18.7 us)
Async XLA Ops:
  0.6 10.6 %copy-start = (f32[1,1,8,8,8,128]{5,4,3,2,1,0:T(8,128)S(1)}, f32[1,1,8,8,8,128]{5,4,3,2,1,0:T(8,128)}, u32[]{:S(2)}) copy-start(f32[1,1,8,8,8,128]{5,4,3,2,1,0:T(8,128)} %param.36) | copy-start | bytes 786436
  4.9 6.3 %collective-permute-start = (f32[2,1,1,8,8,128]{5,0,4,3,2,1:T(2,128)S(1)}, f32[2,1,1,8,8,128]{5,0,4,3,2,1:T(2,128)S(1)}, u32[]{:S(2)}, u32[]{:S(2)}) collective-permute-start(f32[2,1,1,8,8,128]{5,0,4,3,2,1:T(2,128)S(1)} %maximum_bitcast_fusion.9), channel_id=1, source_target_pairs={{0,4},{4,8},{8,12},{12,16},{16,20},{20,24},{24,28},{1,5},{5,9},{9,... | collective-permute-start | bytes 196616 | tf_op jit(solution)/shard_map/ppermute | solution.py:16
  10.0 9.5 %copy-start.3 = (s32[1,4096,1]{1,2,0:T(1,128)S(1)}, s32[1,4096,1]{1,2,0:T(1,128)}, u32[]{:S(2)}) copy-start(s32[1,4096,1]{1,2,0:T(1,128)} %param.39) | copy-start | bytes 49156
  11.3 6.2 %collective-permute-start.1 = (f32[2,1,1,8,8,128]{5,0,4,3,2,1:T(2,128)S(1)}, f32[2,1,1,8,8,128]{5,0,4,3,2,1:T(2,128)S(1)}, u32[]{:S(2)}, u32[]{:S(2)}) collective-permute-start(f32[2,1,1,8,8,128]{5,0,4,3,2,1:T(2,128)S(1)} %get-tuple-element.46), channel_id=1, source_target_pairs={{4,0},{8,4},{12,8},{16,12},{20,16},{24,20},{28,24},{5,1},{9,5},{13... | collective-permute-start | bytes 196616 | tf_op jit(solution)/shard_map/ppermute | solution.py:19
  17.6 5.6 %collective-permute-start.2 = (f32[2,1,1,8,8,128]{5,3,0,4,2,1:T(8,128)S(1)}, f32[2,1,1,8,8,128]{5,3,0,4,2,1:T(8,128)S(1)}, u32[]{:S(2)}, u32[]{:S(2)}) collective-permute-start(f32[2,1,1,8,8,128]{5,3,0,4,2,1:T(8,128)S(1)} %maximum_bitcast_fusion.7), channel_id=1, source_target_pairs={{0,1},{1,2},{2,3},{4,5},{5,6},{6,7},{8,9},{9,10},{10,11},{12,13},{... | collective-permute-start | bytes 196616 | tf_op jit(solution)/shard_map/ppermute | solution.py:16
  23.2 4.7 %copy-start.1 = (f32[8,8,1,1]{1,0,3,2:T(8,128)S(1)}, f32[8,8,1,1]{1,0,3,2:T(8,128)}, u32[]{:S(2)}) copy-start(f32[8,8,1,1]{1,0,3,2:T(8,128)} %constant.130) | copy-start | bytes 772
  23.2 3.8 %collective-permute-start.3 = (f32[2,1,1,8,8,128]{5,3,0,4,2,1:T(8,128)S(1)}, f32[2,1,1,8,8,128]{5,3,0,4,2,1:T(8,128)S(1)}, u32[]{:S(2)}, u32[]{:S(2)}) collective-permute-start(f32[2,1,1,8,8,128]{5,3,0,4,2,1:T(8,128)S(1)} %get-tuple-element.44), channel_id=1, source_target_pairs={{1,0},{2,1},{3,2},{5,4},{6,5},{7,6},{9,8},{10,9},{11,10},{13,12},{... | collective-permute-start | bytes 196616 | tf_op jit(solution)/shard_map/ppermute | solution.py:19
  25.3 3.4 %copy-start.5 = (f32[8]{0:T(128)S(1)}, f32[8]{0:T(128)}, u32[]{:S(2)}) copy-start(f32[8]{0:T(128)} %constant.125) | copy-start | bytes 100
  27.2 8.2 %copy-start.2 = (s32[1,4096]{1,0:T(1,128)S(1)}, s32[1,4096]{1,0:T(1,128)}, u32[]{:S(2)}) copy-start(s32[1,4096]{1,0:T(1,128)} %param.40) | copy-start | bytes 49156
  29.8 5.9 %collective-permute-start.4 = (f32[1,1,1,8,8,128]{5,4,3,2,1,0:T(8,128)S(1)}, f32[1,1,1,8,8,128]{5,4,3,2,1,0:T(8,128)S(1)}, u32[]{:S(2)}, u32[]{:S(2)}) collective-permute-start(f32[1,1,1,8,8,128]{5,4,3,2,1,0:T(8,128)S(1)} %bitcast.482), channel_id=1, source_target_pairs={{0,4},{4,8},{8,12},{12,16},{16,20},{20,24},{24,28},{1,5},{5,9},{9,... | collective-permute-start | bytes 98312 | tf_op jit(solution)/shard_map/ppermute | solution.py:16
  34.1 5.8 %collective-permute-start.5 = (f32[1,1,1,8,8,128]{5,4,3,2,1,0:T(8,128)S(1)}, f32[1,1,1,8,8,128]{5,4,3,2,1,0:T(8,128)S(1)}, u32[]{:S(2)}, u32[]{:S(2)}) collective-permute-start(f32[1,1,1,8,8,128]{5,4,3,2,1,0:T(8,128)S(1)} %bitcast.484), channel_id=1, source_target_pairs={{4,0},{8,4},{12,8},{16,12},{20,16},{24,20},{28,24},{5,1},{9,5},{13... | collective-permute-start | bytes 98312 | tf_op jit(solution)/shard_map/ppermute | solution.py:19
  39.9 5.2 %collective-permute-start.6 = (f32[1,1,1,8,8,128]{5,3,4,2,1,0:T(8,128)S(1)}, f32[1,1,1,8,8,128]{5,3,4,2,1,0:T(8,128)S(1)}, u32[]{:S(2)}, u32[]{:S(2)}) collective-permute-start(f32[1,1,1,8,8,128]{5,3,4,2,1,0:T(8,128)S(1)} %maximum_bitcast_fusion.19), channel_id=1, source_target_pairs={{0,1},{1,2},{2,3},{4,5},{5,6},{6,7},{8,9},{9,10},{10,11},{12,13},{... | collective-permute-start | bytes 98312 | tf_op jit(solution)/shard_map/ppermute | solution.py:16
  45.2 3.9 %collective-permute-start.7 = (f32[1,1,1,8,8,128]{5,3,4,2,1,0:T(8,128)S(1)}, f32[1,1,1,8,8,128]{5,3,4,2,1,0:T(8,128)S(1)}, u32[]{:S(2)}, u32[]{:S(2)}) collective-permute-start(f32[1,1,1,8,8,128]{5,3,4,2,1,0:T(8,128)S(1)} %get-tuple-element.40), channel_id=1, source_target_pairs={{1,0},{2,1},{3,2},{5,4},{6,5},{7,6},{9,8},{10,9},{11,10},{13,12},{... | collective-permute-start | bytes 98312 | tf_op jit(solution)/shard_map/ppermute | solution.py:19
  47.5 20.7 %copy-start.6 = (s32[1,4096]{1,0:T(1,128)S(1)}, s32[1,4096]{1,0:T(1,128)}, u32[]{:S(2)}) copy-start(s32[1,4096]{1,0:T(1,128)} %param.38) | copy-start | bytes 49156
  51.0 5.7 %collective-permute-start.8 = (f32[1,1,1,8,8,128]{5,4,3,2,1,0:T(8,128)S(1)}, f32[1,1,1,8,8,128]{5,4,3,2,1,0:T(8,128)S(1)}, u32[]{:S(2)}, u32[]{:S(2)}) collective-permute-start(f32[1,1,1,8,8,128]{5,4,3,2,1,0:T(8,128)S(1)} %get-tuple-element.68), channel_id=1, source_target_pairs={{0,4},{4,8},{8,12},{12,16},{16,20},{20,24},{24,28},{1,5},{5,9},{9,... | collective-permute-start | bytes 98312 | tf_op jit(solution)/shard_map/ppermute | solution.py:16
  55.1 5.8 %collective-permute-start.9 = (f32[1,1,1,8,8,128]{5,4,3,2,1,0:T(8,128)S(1)}, f32[1,1,1,8,8,128]{5,4,3,2,1,0:T(8,128)S(1)}, u32[]{:S(2)}, u32[]{:S(2)}) collective-permute-start(f32[1,1,1,8,8,128]{5,4,3,2,1,0:T(8,128)S(1)} %get-tuple-element.69), channel_id=1, source_target_pairs={{4,0},{8,4},{12,8},{16,12},{20,16},{24,20},{28,24},{5,1},{9,5},{13... | collective-permute-start | bytes 98312 | tf_op jit(solution)/shard_map/ppermute | solution.py:19
  60.9 5.2 %collective-permute-start.10 = (f32[1,1,1,8,8,128]{5,4,3,2,1,0:T(8,128)S(1)}, f32[1,1,1,8,8,128]{5,4,3,2,1,0:T(8,128)S(1)}, u32[]{:S(2)}, u32[]{:S(2)}) collective-permute-start(f32[1,1,1,8,8,128]{5,4,3,2,1,0:T(8,128)S(1)} %maximum_bitcast_fusion.17), channel_id=1, source_target_pairs={{0,1},{1,2},{2,3},{4,5},{5,6},{6,7},{8,9},{9,10},{10,11},{12,13},{... | collective-permute-start | bytes 98312 | tf_op jit(solution)/shard_map/ppermute | solution.py:16
  66.2 3.5 %collective-permute-start.11 = (f32[1,1,1,8,8,128]{5,4,3,2,1,0:T(8,128)S(1)}, f32[1,1,1,8,8,128]{5,4,3,2,1,0:T(8,128)S(1)}, u32[]{:S(2)}, u32[]{:S(2)}) collective-permute-start(f32[1,1,1,8,8,128]{5,4,3,2,1,0:T(8,128)S(1)} %get-tuple-element.38), channel_id=1, source_target_pairs={{1,0},{2,1},{3,2},{5,4},{6,5},{7,6},{9,8},{10,9},{11,10},{13,12},{... | collective-permute-start | bytes 98312 | tf_op jit(solution)/shard_map/ppermute | solution.py:19
  71.7 5.2 %collective-permute-start.12 = (f32[1,1,1,8,8,128]{5,4,3,2,1,0:T(8,128)S(1)}, f32[1,1,1,8,8,128]{5,4,3,2,1,0:T(8,128)S(1)}, u32[]{:S(2)}, u32[]{:S(2)}) collective-permute-start(f32[1,1,1,8,8,128]{5,4,3,2,1,0:T(8,128)S(1)} %get-tuple-element.62), channel_id=1, source_target_pairs={{0,4},{4,8},{8,12},{12,16},{16,20},{20,24},{24,28},{1,5},{5,9},{9,... | collective-permute-start | bytes 98312 | tf_op jit(solution)/shard_map/ppermute | solution.py:16
  75.4 5.8 %collective-permute-start.13 = (f32[1,1,1,8,8,128]{5,4,3,2,1,0:T(8,128)S(1)}, f32[1,1,1,8,8,128]{5,4,3,2,1,0:T(8,128)S(1)}, u32[]{:S(2)}, u32[]{:S(2)}) collective-permute-start(f32[1,1,1,8,8,128]{5,4,3,2,1,0:T(8,128)S(1)} %get-tuple-element.63), channel_id=1, source_target_pairs={{4,0},{8,4},{12,8},{16,12},{20,16},{24,20},{28,24},{5,1},{9,5},{13... | collective-permute-start | bytes 98312 | tf_op jit(solution)/shard_map/ppermute | solution.py:19
  81.2 5.2 %collective-permute-start.14 = (f32[1,1,1,8,8,128]{5,4,3,2,1,0:T(8,128)S(1)}, f32[1,1,1,8,8,128]{5,4,3,2,1,0:T(8,128)S(1)}, u32[]{:S(2)}, u32[]{:S(2)}) collective-permute-start(f32[1,1,1,8,8,128]{5,4,3,2,1,0:T(8,128)S(1)} %maximum_bitcast_fusion.15), channel_id=1, source_target_pairs={{0,1},{1,2},{2,3},{4,5},{5,6},{6,7},{8,9},{9,10},{10,11},{12,13},{... | collective-permute-start | bytes 98312 | tf_op jit(solution)/shard_map/ppermute | solution.py:16
  86.5 4.0 %collective-permute-start.15 = (f32[1,1,1,8,8,128]{5,4,3,2,1,0:T(8,128)S(1)}, f32[1,1,1,8,8,128]{5,4,3,2,1,0:T(8,128)S(1)}, u32[]{:S(2)}, u32[]{:S(2)}) collective-permute-start(f32[1,1,1,8,8,128]{5,4,3,2,1,0:T(8,128)S(1)} %get-tuple-element.34), channel_id=1, source_target_pairs={{1,0},{2,1},{3,2},{5,4},{6,5},{7,6},{9,8},{10,9},{11,10},{13,12},{... | collective-permute-start | bytes 98312 | tf_op jit(solution)/shard_map/ppermute | solution.py:19
  93.3 0.9 copy-start.4
  97.9 20.1 %all-to-all-start = ((f32[32,2,2048]{2,1,0:T(2,128)}), f32[32,2,2048]{2,1,0:T(2,128)S(1)}, u32[]{:S(2)}, u32[]{:S(2)}) async-start(f32[32,2,2048]{2,1,0:T(2,128)} %bitcast.111), calls=%async_computation | async-start | bytes 1048576 | tf_op jit(solution)/shard_map/all_to_all | solution.py:183
  104.3 5.1 %collective-permute-start.16 = (f32[1,1,1,8,8,128]{5,4,3,2,1,0:T(8,128)S(1)}, f32[1,1,1,8,8,128]{5,4,3,2,1,0:T(8,128)S(1)}, u32[]{:S(2)}, u32[]{:S(2)}) collective-permute-start(f32[1,1,1,8,8,128]{5,4,3,2,1,0:T(8,128)S(1)} %get-tuple-element.53), channel_id=1, source_target_pairs={{0,4},{4,8},{8,12},{12,16},{16,20},{20,24},{24,28},{1,5},{5,9},{9,... | collective-permute-start | bytes 98312 | tf_op jit(solution)/shard_map/ppermute | solution.py:16
  107.7 6.2 %collective-permute-start.17 = (f32[1,1,1,8,8,128]{5,4,3,2,1,0:T(8,128)S(1)}, f32[1,1,1,8,8,128]{5,4,3,2,1,0:T(8,128)S(1)}, u32[]{:S(2)}, u32[]{:S(2)}) collective-permute-start(f32[1,1,1,8,8,128]{5,4,3,2,1,0:T(8,128)S(1)} %get-tuple-element.54), channel_id=1, source_target_pairs={{4,0},{8,4},{12,8},{16,12},{20,16},{24,20},{28,24},{5,1},{9,5},{13... | collective-permute-start | bytes 98312 | tf_op jit(solution)/shard_map/ppermute | solution.py:19
  118.3 5.2 %collective-permute-start.18 = (f32[1,1,1,8,8,128]{5,3,4,2,1,0:T(8,128)S(1)}, f32[1,1,1,8,8,128]{5,3,4,2,1,0:T(8,128)S(1)}, u32[]{:S(2)}, u32[]{:S(2)}) collective-permute-start(f32[1,1,1,8,8,128]{5,3,4,2,1,0:T(8,128)S(1)} %maximum_bitcast_fusion.13), channel_id=1, source_target_pairs={{0,1},{1,2},{2,3},{4,5},{5,6},{6,7},{8,9},{9,10},{10,11},{12,13},{... | collective-permute-start | bytes 98312 | tf_op jit(solution)/shard_map/ppermute | solution.py:16
  123.5 6.1 %collective-permute-start.19 = (f32[1,1,1,8,8,128]{5,3,4,2,1,0:T(8,128)S(1)}, f32[1,1,1,8,8,128]{5,3,4,2,1,0:T(8,128)S(1)}, u32[]{:S(2)}, u32[]{:S(2)}) collective-permute-start(f32[1,1,1,8,8,128]{5,3,4,2,1,0:T(8,128)S(1)} %get-tuple-element.30), channel_id=1, source_target_pairs={{1,0},{2,1},{3,2},{5,4},{6,5},{7,6},{9,8},{10,9},{11,10},{13,12},{... | collective-permute-start | bytes 98312 | tf_op jit(solution)/shard_map/ppermute | solution.py:19
  126.2 11.2 %all-to-all-start.1 = ((f32[8,2,2048]{2,1,0:T(2,128)}), f32[8,2,2048]{2,1,0:T(2,128)S(1)}, u32[]{:S(2)}, u32[]{:S(2)}) async-start(f32[8,2,2048]{2,1,0:T(2,128)} %broadcast_in_dim.213), calls=%async_computation.1 | async-start | bytes 262144 | tf_op jit(solution)/shard_map/all_to_all | solution.py:190

commit v12 on v11

--- a/solution.py
+++ b/solution.py
@@ -149,14 +149,13 @@
     rows = values.shape[0] // lanes
     table = values.reshape(rows, lanes)
     parts = jnp.concatenate(split_parts(table, count), axis=1)
-    hit_row = one_hot(picks // lanes, rows)
-    picked = jnp.dot(hit_row, parts, preferred_element_type=jnp.float32)
-    pieces = [picked[:, n * lanes : (n + 1) * lanes] for n in range(count)]
-    picked = pieces[0]
-    for piece in pieces[1:]:
-        picked = picked + piece
-    hit_lane = (picks % lanes)[:, None] == lax.broadcasted_iota(jnp.int32, (1, lanes), 1)
-    return jnp.sum(jnp.where(hit_lane, picked, 0.0), axis=1)
+    hit_row_t = (lax.broadcasted_iota(jnp.int32, (rows, 1), 0) == (picks // lanes)[None, :]).astype(jnp.bfloat16)
+    picked = lax.dot_general(parts, hit_row_t, (((0,), (0,)), ((), ())), preferred_element_type=jnp.float32)
+    total = picked[:lanes]
+    for n in range(1, count):
+        total = total + picked[n * lanes : (n + 1) * lanes]
+    hit_lane_t = lax.broadcasted_iota(jnp.int32, (lanes, 1), 0) == (picks % lanes)[None, :]
+    return jnp.sum(jnp.where(hit_lane_t, total, 0.0), axis=0)
 
 
 def segment_sum(values, ids, bins, lanes, count=3):

time: 139 us -> 139 us (level)
  no operation moved by 1% of the time
where the time goes in v12:
time: 139 us; the launch traced here: 138 us
  starting transfers between devices  54 us (39%)
  waiting for transfers between devices  50.5 us (36%)
  other arithmetic  14.5 us (10%)
  matrix products  12 us (9%)
  local copies, waits for them, and re-layouts  5.3 us (4%)
  between operations  1.61 us (1%)
    ppermute x10, starting transfers between devices, padded_2(): lax.ppermute(lax.slice_in_dim(block, block.shape[dim] - width, None, axis...  28.5 us
    ppermute x10, waiting for transfers between devices, padded_2(): lax.ppermute(lax.slice_in_dim(block, 0, width, axis=dim), axis, backward)  25.8 us
    ppermute x10, starting transfers between devices, padded_2(): lax.ppermute(lax.slice_in_dim(block, 0, width, axis=dim), axis, backward)  16.9 us
    ppermute x10, waiting for transfers between devices, padded_2(): lax.ppermute(lax.slice_in_dim(block, block.shape[dim] - width, None, axis...  13.9 us
    all_to_all x1, waiting for transfers between devices, strip_gather(): whole = lax.all_to_all(spread_out, 'ex', 0, 0, tiled=True)  6.78 us
    all_to_all x1, starting transfers between devices, strip_reduce(): return lax.all_to_all(chunks, ('ex', 'ey'), 0, 0, tiled=True).sum(0)  5.08 us
    all_to_all x1, waiting for transfers between devices, strip_reduce(): return lax.all_to_all(chunks, ('ex', 'ey'), 0, 0, tiled=True).sum(0)  4.09 us
    all_to_all x1, starting transfers between devices, strip_gather(): whole = lax.all_to_all(spread_out, 'ex', 0, 0, tiled=True)  3.45 us
  transfers between devices with their start and end apart: 22, of which 20 were waited for; matrix products, arithmetic and copies ran while one was open for 9% of the time, Pallas kernels for 0%

profile of v12, /device:TPU:2, one launch (start us, length us, event | category | flops | bytes accessed | tf_op | source)
XLA Modules:
  0.0 137.9 jit_solution(7676602246461981320)
XLA Ops:
  2.9 1.2 fusion.90
  4.9 3.4 %collective-permute-start = (f32[2,1,1,8,8,128]{5,0,4,3,2,1:T(2,128)S(1)}, f32[2,1,1,8,8,128]{5,0,4,3,2,1:T(2,128)S(1)}, u32[]{:S(2)}, u32[]{:S(2)}) collective-permute-start(f32[2,1,1,8,8,128]{5,0,4,3,2,1:T(2,128)S(1)} %maximum_bitcast_fusion.9), channel_id=1, source_target_pairs={{0,4},{4,8},{8,12},{12,16},{16,20},{20,24},{24,28},{1,5},{5,9},{9,... | collective-permute-start | bytes 196616 | tf_op jit(solution)/shard_map/ppermute | solution.py:16
  10.0 1.2 fusion.20
  11.3 1.3 collective-permute-start.1
  13.3 4.3 %collective-permute-done.1 = f32[2,1,1,8,8,128]{5,0,4,3,2,1:T(2,128)S(1)} collective-permute-done((f32[2,1,1,8,8,128]{5,0,4,3,2,1:T(2,128)S(1)}, f32[2,1,1,8,8,128]{5,0,4,3,2,1:T(2,128)S(1)}, u32[]{:S(2)}, u32[]{:S(2)}) %collective-permute-start.1) | collective-permute-done | bytes 65568 | tf_op jit(solution)/shard_map/ppermute | solution.py:19
  17.6 1.9 %collective-permute-start.2 = (f32[2,1,1,8,8,128]{5,3,0,4,2,1:T(8,128)S(1)}, f32[2,1,1,8,8,128]{5,3,0,4,2,1:T(8,128)S(1)}, u32[]{:S(2)}, u32[]{:S(2)}) collective-permute-start(f32[2,1,1,8,8,128]{5,3,0,4,2,1:T(8,128)S(1)} %maximum_bitcast_fusion.7), channel_id=1, source_target_pairs={{0,1},{1,2},{2,3},{4,5},{5,6},{6,7},{8,9},{9,10},{10,11},{12,13},{... | collective-permute-start | bytes 196616 | tf_op jit(solution)/shard_map/ppermute | solution.py:16
  19.5 3.6 %collective-permute-done.2 = f32[2,1,1,8,8,128]{5,3,0,4,2,1:T(8,128)S(1)} collective-permute-done((f32[2,1,1,8,8,128]{5,3,0,4,2,1:T(8,128)S(1)}, f32[2,1,1,8,8,128]{5,3,0,4,2,1:T(8,128)S(1)}, u32[]{:S(2)}, u32[]{:S(2)}) %collective-permute-start.2) | collective-permute-done | bytes 65568 | tf_op jit(solution)/shard_map/ppermute | solution.py:16
  23.2 1.9 %collective-permute-start.3 = (f32[2,1,1,8,8,128]{5,3,0,4,2,1:T(8,128)S(1)}, f32[2,1,1,8,8,128]{5,3,0,4,2,1:T(8,128)S(1)}, u32[]{:S(2)}, u32[]{:S(2)}) collective-permute-start(f32[2,1,1,8,8,128]{5,3,0,4,2,1:T(8,128)S(1)} %get-tuple-element.46), channel_id=1, source_target_pairs={{1,0},{2,1},{3,2},{5,4},{6,5},{7,6},{9,8},{10,9},{11,10},{13,12},{... | collective-permute-start | bytes 196616 | tf_op jit(solution)/shard_map/ppermute | solution.py:19
  25.5 1.5 %collective-permute-done.3 = f32[2,1,1,8,8,128]{5,3,0,4,2,1:T(8,128)S(1)} collective-permute-done((f32[2,1,1,8,8,128]{5,3,0,4,2,1:T(8,128)S(1)}, f32[2,1,1,8,8,128]{5,3,0,4,2,1:T(8,128)S(1)}, u32[]{:S(2)}, u32[]{:S(2)}) %collective-permute-start.3) | collective-permute-done | bytes 65568 | tf_op jit(solution)/shard_map/ppermute | solution.py:19
  28.8 0.9 fusion.30
  29.8 4.3 %collective-permute-start.4 = (f32[1,1,1,8,8,128]{5,4,3,2,1,0:T(8,128)S(1)}, f32[1,1,1,8,8,128]{5,4,3,2,1,0:T(8,128)S(1)}, u32[]{:S(2)}, u32[]{:S(2)}) collective-permute-start(f32[1,1,1,8,8,128]{5,4,3,2,1,0:T(8,128)S(1)} %bitcast.487), channel_id=1, source_target_pairs={{0,4},{4,8},{8,12},{12,16},{16,20},{20,24},{24,28},{1,5},{5,9},{9,... | collective-permute-start | bytes 98312 | tf_op jit(solution)/shard_map/ppermute | solution.py:16
  34.1 1.3 collective-permute-start.5
  35.7 4.2 %collective-permute-done.5 = f32[1,1,1,8,8,128]{5,4,3,2,1,0:T(8,128)S(1)} collective-permute-done((f32[1,1,1,8,8,128]{5,4,3,2,1,0:T(8,128)S(1)}, f32[1,1,1,8,8,128]{5,4,3,2,1,0:T(8,128)S(1)}, u32[]{:S(2)}, u32[]{:S(2)}) %collective-permute-start.5) | collective-permute-done | bytes 32800 | tf_op jit(solution)/shard_map/ppermute | solution.py:19
  39.9 1.9 %collective-permute-start.6 = (f32[1,1,1,8,8,128]{5,3,4,2,1,0:T(8,128)S(1)}, f32[1,1,1,8,8,128]{5,3,4,2,1,0:T(8,128)S(1)}, u32[]{:S(2)}, u32[]{:S(2)}) collective-permute-start(f32[1,1,1,8,8,128]{5,3,4,2,1,0:T(8,128)S(1)} %maximum_bitcast_fusion.19), channel_id=1, source_target_pairs={{0,1},{1,2},{2,3},{4,5},{5,6},{6,7},{8,9},{9,10},{10,11},{12,13},{... | collective-permute-start | bytes 98312 | tf_op jit(solution)/shard_map/ppermute | solution.py:16
  41.9 1.9 %fusion = f32[768,256]{1,0:T(8,128)S(1)} fusion(bf16[256,4096]{1,0:T(8,128)(2,1)S(1)} %get-tuple-element.83, bf16[256,4096]{1,0:T(8,128)(2,1)S(1)} %get-tuple-element.84, bf16[256,4096]{1,0:T(8,128)(2,1)S(1)} %get-tuple-element.82, s32[4096]{0:T(1024)S(1)} %add_select_fusion), kind=kOutput, calls=%fused_computation | convolution fusion | flops 1630535680 | bytes 7094272 | tf_op jit(solution)/shard_map/dot_general | solution.py:167
  43.8 1.4 collective-permute-done.6
  45.2 2.3 %collective-permute-start.7 = (f32[1,1,1,8,8,128]{5,3,4,2,1,0:T(8,128)S(1)}, f32[1,1,1,8,8,128]{5,3,4,2,1,0:T(8,128)S(1)}, u32[]{:S(2)}, u32[]{:S(2)}) collective-permute-start(f32[1,1,1,8,8,128]{5,3,4,2,1,0:T(8,128)S(1)} %get-tuple-element.42), channel_id=1, source_target_pairs={{1,0},{2,1},{3,2},{5,4},{6,5},{7,6},{9,8},{10,9},{11,10},{13,12},{... | collective-permute-start | bytes 98312 | tf_op jit(solution)/shard_map/ppermute | solution.py:19
  47.7 1.4 collective-permute-done.7
  51.0 4.1 %collective-permute-start.8 = (f32[1,1,1,8,8,128]{5,4,3,2,1,0:T(8,128)S(1)}, f32[1,1,1,8,8,128]{5,4,3,2,1,0:T(8,128)S(1)}, u32[]{:S(2)}, u32[]{:S(2)}) collective-permute-start(f32[1,1,1,8,8,128]{5,4,3,2,1,0:T(8,128)S(1)} %get-tuple-element.70), channel_id=1, source_target_pairs={{0,4},{4,8},{8,12},{12,16},{16,20},{20,24},{24,28},{1,5},{5,9},{9,... | collective-permute-start | bytes 98312 | tf_op jit(solution)/shard_map/ppermute | solution.py:16
  55.1 1.3 collective-permute-start.9
  56.7 4.2 %collective-permute-done.9 = f32[1,1,1,8,8,128]{5,4,3,2,1,0:T(8,128)S(1)} collective-permute-done((f32[1,1,1,8,8,128]{5,4,3,2,1,0:T(8,128)S(1)}, f32[1,1,1,8,8,128]{5,4,3,2,1,0:T(8,128)S(1)}, u32[]{:S(2)}, u32[]{:S(2)}) %collective-permute-start.9) | collective-permute-done | bytes 32800 | tf_op jit(solution)/shard_map/ppermute | solution.py:19
  60.9 1.9 %collective-permute-start.10 = (f32[1,1,1,8,8,128]{5,4,3,2,1,0:T(8,128)S(1)}, f32[1,1,1,8,8,128]{5,4,3,2,1,0:T(8,128)S(1)}, u32[]{:S(2)}, u32[]{:S(2)}) collective-permute-start(f32[1,1,1,8,8,128]{5,4,3,2,1,0:T(8,128)S(1)} %maximum_bitcast_fusion.17), channel_id=1, source_target_pairs={{0,1},{1,2},{2,3},{4,5},{5,6},{6,7},{8,9},{9,10},{10,11},{12,13},{... | collective-permute-start | bytes 98312 | tf_op jit(solution)/shard_map/ppermute | solution.py:16
  62.9 3.2 %collective-permute-done.10 = f32[1,1,1,8,8,128]{5,4,3,2,1,0:T(8,128)S(1)} collective-permute-done((f32[1,1,1,8,8,128]{5,4,3,2,1,0:T(8,128)S(1)}, f32[1,1,1,8,8,128]{5,4,3,2,1,0:T(8,128)S(1)}, u32[]{:S(2)}, u32[]{:S(2)}) %collective-permute-start.10) | collective-permute-done | bytes 32800 | tf_op jit(solution)/shard_map/ppermute | solution.py:16
  66.2 2.1 %collective-permute-start.11 = (f32[1,1,1,8,8,128]{5,4,3,2,1,0:T(8,128)S(1)}, f32[1,1,1,8,8,128]{5,4,3,2,1,0:T(8,128)S(1)}, u32[]{:S(2)}, u32[]{:S(2)}) collective-permute-start(f32[1,1,1,8,8,128]{5,4,3,2,1,0:T(8,128)S(1)} %get-tuple-element.40), channel_id=1, source_target_pairs={{1,0},{2,1},{3,2},{5,4},{6,5},{7,6},{9,8},{10,9},{11,10},{13,12},{... | collective-permute-start | bytes 98312 | tf_op jit(solution)/shard_map/ppermute | solution.py:19
  68.4 1.3 collective-permute-done.11
  71.8 3.6 %collective-permute-start.12 = (f32[1,1,1,8,8,128]{5,4,3,2,1,0:T(8,128)S(1)}, f32[1,1,1,8,8,128]{5,4,3,2,1,0:T(8,128)S(1)}, u32[]{:S(2)}, u32[]{:S(2)}) collective-permute-start(f32[1,1,1,8,8,128]{5,4,3,2,1,0:T(8,128)S(1)} %get-tuple-element.64), channel_id=1, source_target_pairs={{0,4},{4,8},{8,12},{12,16},{16,20},{20,24},{24,28},{1,5},{5,9},{9,... | collective-permute-start | bytes 98312 | tf_op jit(solution)/shard_map/ppermute | solution.py:16
  75.4 1.3 collective-permute-start.13
  77.0 4.2 %collective-permute-done.13 = f32[1,1,1,8,8,128]{5,4,3,2,1,0:T(8,128)S(1)} collective-permute-done((f32[1,1,1,8,8,128]{5,4,3,2,1,0:T(8,128)S(1)}, f32[1,1,1,8,8,128]{5,4,3,2,1,0:T(8,128)S(1)}, u32[]{:S(2)}, u32[]{:S(2)}) %collective-permute-start.13) | collective-permute-done | bytes 32800 | tf_op jit(solution)/shard_map/ppermute | solution.py:19
  81.2 1.9 %collective-permute-start.14 = (f32[1,1,1,8,8,128]{5,4,3,2,1,0:T(8,128)S(1)}, f32[1,1,1,8,8,128]{5,4,3,2,1,0:T(8,128)S(1)}, u32[]{:S(2)}, u32[]{:S(2)}) collective-permute-start(f32[1,1,1,8,8,128]{5,4,3,2,1,0:T(8,128)S(1)} %maximum_bitcast_fusion.15), channel_id=1, source_target_pairs={{0,1},{1,2},{2,3},{4,5},{5,6},{6,7},{8,9},{9,10},{10,11},{12,13},{... | collective-permute-start | bytes 98312 | tf_op jit(solution)/shard_map/ppermute | solution.py:16
  83.2 1.9 %fusion.15 = f32[768,4096]{1,0:T(8,128)S(1)} fusion(s32[4096]{0:T(1024)S(1)} %bitcast.481, bf16[256,256]{1,0:T(8,128)(2,1)S(1)} %get-tuple-element.58, bf16[256,256]{1,0:T(8,128)(2,1)S(1)} %get-tuple-element.59, bf16[256,256]{1,0:T(8,128)(2,1)S(1)} %get-tuple-element.57), kind=kOutput, calls=%fused_computation.19 | convolution fusion | flops 1612840960 | bytes 12992512 | tf_op jit(solution)/shard_map/dot_general | solution.py:153
  85.1 1.4 %collective-permute-done.14 = f32[1,1,1,8,8,128]{5,4,3,2,1,0:T(8,128)S(1)} collective-permute-done((f32[1,1,1,8,8,128]{5,4,3,2,1,0:T(8,128)S(1)}, f32[1,1,1,8,8,128]{5,4,3,2,1,0:T(8,128)S(1)}, u32[]{:S(2)}, u32[]{:S(2)}) %collective-permute-start.14) | collective-permute-done | bytes 32800 | tf_op jit(solution)/shard_map/ppermute | solution.py:16
  86.5 2.2 %collective-permute-start.15 = (f32[1,1,1,8,8,128]{5,4,3,2,1,0:T(8,128)S(1)}, f32[1,1,1,8,8,128]{5,4,3,2,1,0:T(8,128)S(1)}, u32[]{:S(2)}, u32[]{:S(2)}) collective-permute-start(f32[1,1,1,8,8,128]{5,4,3,2,1,0:T(8,128)S(1)} %get-tuple-element.36), channel_id=1, source_target_pairs={{1,0},{2,1},{3,2},{5,4},{6,5},{7,6},{9,8},{10,9},{11,10},{13,12},{... | collective-permute-start | bytes 98312 | tf_op jit(solution)/shard_map/ppermute | solution.py:19
  88.7 1.4 fusion.9
  91.8 1.3 fusion.14
  93.1 0.9 fusion.7
  94.1 0.9 fusion.17
  94.9 1.4 %fusion.10 = f32[512,256]{1,0:T(8,128)S(1)} fusion(bf16[256,4096]{1,0:T(8,128)(2,1)S(1)} %get-tuple-element.81, bf16[256,4096]{1,0:T(8,128)(2,1)S(1)} %get-tuple-element.80, s32[4096]{0:T(1024)S(1)} %add_select_fusion), kind=kOutput, calls=%fused_computation.13 | convolution fusion | flops 1083179008 | bytes 4734976 | tf_op jit(solution)/shard_map/dot_general | solution.py:167
  96.5 1.2 copy.201
  97.7 5.1 %all-to-all-start = ((f32[32,2,2048]{2,1,0:T(2,128)}), f32[32,2,2048]{2,1,0:T(2,128)S(1)}, u32[]{:S(2)}, u32[]{:S(2)}) async-start(f32[32,2,2048]{2,1,0:T(2,128)} %bitcast.112), calls=%async_computation | async-start | bytes 1048576 | tf_op jit(solution)/shard_map/all_to_all | solution.py:182
  104.1 3.4 %collective-permute-start.16 = (f32[1,1,1,8,8,128]{5,4,3,2,1,0:T(8,128)S(1)}, f32[1,1,1,8,8,128]{5,4,3,2,1,0:T(8,128)S(1)}, u32[]{:S(2)}, u32[]{:S(2)}) collective-permute-start(f32[1,1,1,8,8,128]{5,4,3,2,1,0:T(8,128)S(1)} %get-tuple-element.55), channel_id=1, source_target_pairs={{0,4},{4,8},{8,12},{12,16},{16,20},{20,24},{24,28},{1,5},{5,9},{9,... | collective-permute-start | bytes 98312 | tf_op jit(solution)/shard_map/ppermute | solution.py:16
  107.5 1.3 collective-permute-start.17
  109.2 4.5 %collective-permute-done.17 = f32[1,1,1,8,8,128]{5,4,3,2,1,0:T(8,128)S(1)} collective-permute-done((f32[1,1,1,8,8,128]{5,4,3,2,1,0:T(8,128)S(1)}, f32[1,1,1,8,8,128]{5,4,3,2,1,0:T(8,128)S(1)}, u32[]{:S(2)}, u32[]{:S(2)}) %collective-permute-start.17) | collective-permute-done | bytes 32800 | tf_op jit(solution)/shard_map/ppermute | solution.py:19
  113.8 4.1 %all-to-all-done = f32[32,2,2048]{2,1,0:T(2,128)S(1)} async-done(((f32[32,2,2048]{2,1,0:T(2,128)}), f32[32,2,2048]{2,1,0:T(2,128)S(1)}, u32[]{:S(2)}, u32[]{:S(2)}) %all-to-all-start) | async-done | bytes 524320 | tf_op jit(solution)/shard_map/all_to_all | solution.py:182
  118.0 2.0 %collective-permute-start.18 = (f32[1,1,1,8,8,128]{5,3,4,2,1,0:T(8,128)S(1)}, f32[1,1,1,8,8,128]{5,3,4,2,1,0:T(8,128)S(1)}, u32[]{:S(2)}, u32[]{:S(2)}) collective-permute-start(f32[1,1,1,8,8,128]{5,3,4,2,1,0:T(8,128)S(1)} %maximum_bitcast_fusion.13), channel_id=1, source_target_pairs={{0,1},{1,2},{2,3},{4,5},{5,6},{6,7},{8,9},{9,10},{10,11},{12,13},{... | collective-permute-start | bytes 98312 | tf_op jit(solution)/shard_map/ppermute | solution.py:16
  120.0 3.3 %collective-permute-done.18 = f32[1,1,1,8,8,128]{5,3,4,2,1,0:T(8,128)S(1)} collective-permute-done((f32[1,1,1,8,8,128]{5,3,4,2,1,0:T(8,128)S(1)}, f32[1,1,1,8,8,128]{5,3,4,2,1,0:T(8,128)S(1)}, u32[]{:S(2)}, u32[]{:S(2)}) %collective-permute-start.18) | collective-permute-done | bytes 32800 | tf_op jit(solution)/shard_map/ppermute | solution.py:16
  123.3 1.9 %collective-permute-start.19 = (f32[1,1,1,8,8,128]{5,3,4,2,1,0:T(8,128)S(1)}, f32[1,1,1,8,8,128]{5,3,4,2,1,0:T(8,128)S(1)}, u32[]{:S(2)}, u32[]{:S(2)}) collective-permute-start(f32[1,1,1,8,8,128]{5,3,4,2,1,0:T(8,128)S(1)} %get-tuple-element.30), channel_id=1, source_target_pairs={{1,0},{2,1},{3,2},{5,4},{6,5},{7,6},{9,8},{10,9},{11,10},{13,12},{... | collective-permute-start | bytes 98312 | tf_op jit(solution)/shard_map/ppermute | solution.py:19
  126.0 3.4 %all-to-all-start.1 = ((f32[8,2,2048]{2,1,0:T(2,128)}), f32[8,2,2048]{2,1,0:T(2,128)S(1)}, u32[]{:S(2)}, u32[]{:S(2)}) async-start(f32[8,2,2048]{2,1,0:T(2,128)} %broadcast_in_dim.213), calls=%async_computation.1 | async-start | bytes 262144 | tf_op jit(solution)/shard_map/all_to_all | solution.py:189
  130.4 6.8 %all-to-all-done.1 = f32[8,2,2048]{2,1,0:T(2,128)S(1)} async-done(((f32[8,2,2048]{2,1,0:T(2,128)}), f32[8,2,2048]{2,1,0:T(2,128)S(1)}, u32[]{:S(2)}, u32[]{:S(2)}) %all-to-all-start.1) | async-done | bytes 131104 | tf_op jit(solution)/shard_map/all_to_all | solution.py:189
  (135 shorter events, 18.8 us)
Async XLA Ops:
  0.6 10.6 %copy-start = (f32[1,1,8,8,8,128]{5,4,3,2,1,0:T(8,128)S(1)}, f32[1,1,8,8,8,128]{5,4,3,2,1,0:T(8,128)}, u32[]{:S(2)}) copy-start(f32[1,1,8,8,8,128]{5,4,3,2,1,0:T(8,128)} %param.36) | copy-start | bytes 786436
  4.9 6.3 %collective-permute-start = (f32[2,1,1,8,8,128]{5,0,4,3,2,1:T(2,128)S(1)}, f32[2,1,1,8,8,128]{5,0,4,3,2,1:T(2,128)S(1)}, u32[]{:S(2)}, u32[]{:S(2)}) collective-permute-start(f32[2,1,1,8,8,128]{5,0,4,3,2,1:T(2,128)S(1)} %maximum_bitcast_fusion.9), channel_id=1, source_target_pairs={{0,4},{4,8},{8,12},{12,16},{16,20},{20,24},{24,28},{1,5},{5,9},{9,... | collective-permute-start | bytes 196616 | tf_op jit(solution)/shard_map/ppermute | solution.py:16
  10.0 9.5 %copy-start.4 = (s32[1,4096,1]{1,2,0:T(1,128)S(1)}, s32[1,4096,1]{1,2,0:T(1,128)}, u32[]{:S(2)}) copy-start(s32[1,4096,1]{1,2,0:T(1,128)} %param.39) | copy-start | bytes 49156
  11.3 6.2 %collective-permute-start.1 = (f32[2,1,1,8,8,128]{5,0,4,3,2,1:T(2,128)S(1)}, f32[2,1,1,8,8,128]{5,0,4,3,2,1:T(2,128)S(1)}, u32[]{:S(2)}, u32[]{:S(2)}) collective-permute-start(f32[2,1,1,8,8,128]{5,0,4,3,2,1:T(2,128)S(1)} %get-tuple-element.48), channel_id=1, source_target_pairs={{4,0},{8,4},{12,8},{16,12},{20,16},{24,20},{28,24},{5,1},{9,5},{13... | collective-permute-start | bytes 196616 | tf_op jit(solution)/shard_map/ppermute | solution.py:19
  17.6 5.6 %collective-permute-start.2 = (f32[2,1,1,8,8,128]{5,3,0,4,2,1:T(8,128)S(1)}, f32[2,1,1,8,8,128]{5,3,0,4,2,1:T(8,128)S(1)}, u32[]{:S(2)}, u32[]{:S(2)}) collective-permute-start(f32[2,1,1,8,8,128]{5,3,0,4,2,1:T(8,128)S(1)} %maximum_bitcast_fusion.7), channel_id=1, source_target_pairs={{0,1},{1,2},{2,3},{4,5},{5,6},{6,7},{8,9},{9,10},{10,11},{12,13},{... | collective-permute-start | bytes 196616 | tf_op jit(solution)/shard_map/ppermute | solution.py:16
  23.2 4.7 %copy-start.1 = (f32[8,8,1,1]{1,0,3,2:T(8,128)S(1)}, f32[8,8,1,1]{1,0,3,2:T(8,128)}, u32[]{:S(2)}) copy-start(f32[8,8,1,1]{1,0,3,2:T(8,128)} %constant.130) | copy-start | bytes 772
  23.2 3.8 %collective-permute-start.3 = (f32[2,1,1,8,8,128]{5,3,0,4,2,1:T(8,128)S(1)}, f32[2,1,1,8,8,128]{5,3,0,4,2,1:T(8,128)S(1)}, u32[]{:S(2)}, u32[]{:S(2)}) collective-permute-start(f32[2,1,1,8,8,128]{5,3,0,4,2,1:T(8,128)S(1)} %get-tuple-element.46), channel_id=1, source_target_pairs={{1,0},{2,1},{3,2},{5,4},{6,5},{7,6},{9,8},{10,9},{11,10},{13,12},{... | collective-permute-start | bytes 196616 | tf_op jit(solution)/shard_map/ppermute | solution.py:19
  25.3 3.4 %copy-start.6 = (f32[8]{0:T(128)S(1)}, f32[8]{0:T(128)}, u32[]{:S(2)}) copy-start(f32[8]{0:T(128)} %constant.125) | copy-start | bytes 100
  27.2 8.2 %copy-start.2 = (s32[1,4096]{1,0:T(1,128)S(1)}, s32[1,4096]{1,0:T(1,128)}, u32[]{:S(2)}) copy-start(s32[1,4096]{1,0:T(1,128)} %param.40) | copy-start | bytes 49156
  29.8 5.9 %collective-permute-start.4 = (f32[1,1,1,8,8,128]{5,4,3,2,1,0:T(8,128)S(1)}, f32[1,1,1,8,8,128]{5,4,3,2,1,0:T(8,128)S(1)}, u32[]{:S(2)}, u32[]{:S(2)}) collective-permute-start(f32[1,1,1,8,8,128]{5,4,3,2,1,0:T(8,128)S(1)} %bitcast.487), channel_id=1, source_target_pairs={{0,4},{4,8},{8,12},{12,16},{16,20},{20,24},{24,28},{1,5},{5,9},{9,... | collective-permute-start | bytes 98312 | tf_op jit(solution)/shard_map/ppermute | solution.py:16
  34.1 5.8 %collective-permute-start.5 = (f32[1,1,1,8,8,128]{5,4,3,2,1,0:T(8,128)S(1)}, f32[1,1,1,8,8,128]{5,4,3,2,1,0:T(8,128)S(1)}, u32[]{:S(2)}, u32[]{:S(2)}) collective-permute-start(f32[1,1,1,8,8,128]{5,4,3,2,1,0:T(8,128)S(1)} %bitcast.489), channel_id=1, source_target_pairs={{4,0},{8,4},{12,8},{16,12},{20,16},{24,20},{28,24},{5,1},{9,5},{13... | collective-permute-start | bytes 98312 | tf_op jit(solution)/shard_map/ppermute | solution.py:19
  39.9 5.2 %collective-permute-start.6 = (f32[1,1,1,8,8,128]{5,3,4,2,1,0:T(8,128)S(1)}, f32[1,1,1,8,8,128]{5,3,4,2,1,0:T(8,128)S(1)}, u32[]{:S(2)}, u32[]{:S(2)}) collective-permute-start(f32[1,1,1,8,8,128]{5,3,4,2,1,0:T(8,128)S(1)} %maximum_bitcast_fusion.19), channel_id=1, source_target_pairs={{0,1},{1,2},{2,3},{4,5},{5,6},{6,7},{8,9},{9,10},{10,11},{12,13},{... | collective-permute-start | bytes 98312 | tf_op jit(solution)/shard_map/ppermute | solution.py:16
  45.2 17.7 %copy-start.3 = (s32[1,4096]{1,0:T(1,128)S(1)}, s32[1,4096]{1,0:T(1,128)}, u32[]{:S(2)}) copy-start(s32[1,4096]{1,0:T(1,128)} %param.38) | copy-start | bytes 49156
  45.2 3.9 %collective-permute-start.7 = (f32[1,1,1,8,8,128]{5,3,4,2,1,0:T(8,128)S(1)}, f32[1,1,1,8,8,128]{5,3,4,2,1,0:T(8,128)S(1)}, u32[]{:S(2)}, u32[]{:S(2)}) collective-permute-start(f32[1,1,1,8,8,128]{5,3,4,2,1,0:T(8,128)S(1)} %get-tuple-element.42), channel_id=1, source_target_pairs={{1,0},{2,1},{3,2},{5,4},{6,5},{7,6},{9,8},{10,9},{11,10},{13,12},{... | collective-permute-start | bytes 98312 | tf_op jit(solution)/shard_map/ppermute | solution.py:19
  51.0 5.7 %collective-permute-start.8 = (f32[1,1,1,8,8,128]{5,4,3,2,1,0:T(8,128)S(1)}, f32[1,1,1,8,8,128]{5,4,3,2,1,0:T(8,128)S(1)}, u32[]{:S(2)}, u32[]{:S(2)}) collective-permute-start(f32[1,1,1,8,8,128]{5,4,3,2,1,0:T(8,128)S(1)} %get-tuple-element.70), channel_id=1, source_target_pairs={{0,4},{4,8},{8,12},{12,16},{16,20},{20,24},{24,28},{1,5},{5,9},{9,... | collective-permute-start | bytes 98312 | tf_op jit(solution)/shard_map/ppermute | solution.py:16
  55.1 5.8 %collective-permute-start.9 = (f32[1,1,1,8,8,128]{5,4,3,2,1,0:T(8,128)S(1)}, f32[1,1,1,8,8,128]{5,4,3,2,1,0:T(8,128)S(1)}, u32[]{:S(2)}, u32[]{:S(2)}) collective-permute-start(f32[1,1,1,8,8,128]{5,4,3,2,1,0:T(8,128)S(1)} %get-tuple-element.71), channel_id=1, source_target_pairs={{4,0},{8,4},{12,8},{16,12},{20,16},{24,20},{28,24},{5,1},{9,5},{13... | collective-permute-start | bytes 98312 | tf_op jit(solution)/shard_map/ppermute | solution.py:19
  60.9 5.2 %collective-permute-start.10 = (f32[1,1,1,8,8,128]{5,4,3,2,1,0:T(8,128)S(1)}, f32[1,1,1,8,8,128]{5,4,3,2,1,0:T(8,128)S(1)}, u32[]{:S(2)}, u32[]{:S(2)}) collective-permute-start(f32[1,1,1,8,8,128]{5,4,3,2,1,0:T(8,128)S(1)} %maximum_bitcast_fusion.17), channel_id=1, source_target_pairs={{0,1},{1,2},{2,3},{4,5},{5,6},{6,7},{8,9},{9,10},{10,11},{12,13},{... | collective-permute-start | bytes 98312 | tf_op jit(solution)/shard_map/ppermute | solution.py:16
  66.2 3.5 %collective-permute-start.11 = (f32[1,1,1,8,8,128]{5,4,3,2,1,0:T(8,128)S(1)}, f32[1,1,1,8,8,128]{5,4,3,2,1,0:T(8,128)S(1)}, u32[]{:S(2)}, u32[]{:S(2)}) collective-permute-start(f32[1,1,1,8,8,128]{5,4,3,2,1,0:T(8,128)S(1)} %get-tuple-element.40), channel_id=1, source_target_pairs={{1,0},{2,1},{3,2},{5,4},{6,5},{7,6},{9,8},{10,9},{11,10},{13,12},{... | collective-permute-start | bytes 98312 | tf_op jit(solution)/shard_map/ppermute | solution.py:19
  71.8 5.2 %collective-permute-start.12 = (f32[1,1,1,8,8,128]{5,4,3,2,1,0:T(8,128)S(1)}, f32[1,1,1,8,8,128]{5,4,3,2,1,0:T(8,128)S(1)}, u32[]{:S(2)}, u32[]{:S(2)}) collective-permute-start(f32[1,1,1,8,8,128]{5,4,3,2,1,0:T(8,128)S(1)} %get-tuple-element.64), channel_id=1, source_target_pairs={{0,4},{4,8},{8,12},{12,16},{16,20},{20,24},{24,28},{1,5},{5,9},{9,... | collective-permute-start | bytes 98312 | tf_op jit(solution)/shard_map/ppermute | solution.py:16
  75.4 5.8 %collective-permute-start.13 = (f32[1,1,1,8,8,128]{5,4,3,2,1,0:T(8,128)S(1)}, f32[1,1,1,8,8,128]{5,4,3,2,1,0:T(8,128)S(1)}, u32[]{:S(2)}, u32[]{:S(2)}) collective-permute-start(f32[1,1,1,8,8,128]{5,4,3,2,1,0:T(8,128)S(1)} %get-tuple-element.65), channel_id=1, source_target_pairs={{4,0},{8,4},{12,8},{16,12},{20,16},{24,20},{28,24},{5,1},{9,5},{13... | collective-permute-start | bytes 98312 | tf_op jit(solution)/shard_map/ppermute | solution.py:19
  81.2 5.2 %collective-permute-start.14 = (f32[1,1,1,8,8,128]{5,4,3,2,1,0:T(8,128)S(1)}, f32[1,1,1,8,8,128]{5,4,3,2,1,0:T(8,128)S(1)}, u32[]{:S(2)}, u32[]{:S(2)}) collective-permute-start(f32[1,1,1,8,8,128]{5,4,3,2,1,0:T(8,128)S(1)} %maximum_bitcast_fusion.15), channel_id=1, source_target_pairs={{0,1},{1,2},{2,3},{4,5},{5,6},{6,7},{8,9},{9,10},{10,11},{12,13},{... | collective-permute-start | bytes 98312 | tf_op jit(solution)/shard_map/ppermute | solution.py:16
  86.5 3.8 %collective-permute-start.15 = (f32[1,1,1,8,8,128]{5,4,3,2,1,0:T(8,128)S(1)}, f32[1,1,1,8,8,128]{5,4,3,2,1,0:T(8,128)S(1)}, u32[]{:S(2)}, u32[]{:S(2)}) collective-permute-start(f32[1,1,1,8,8,128]{5,4,3,2,1,0:T(8,128)S(1)} %get-tuple-element.36), channel_id=1, source_target_pairs={{1,0},{2,1},{3,2},{5,4},{6,5},{7,6},{9,8},{10,9},{11,10},{13,12},{... | collective-permute-start | bytes 98312 | tf_op jit(solution)/shard_map/ppermute | solution.py:19
  93.1 0.9 copy-start.5
  97.7 20.1 %all-to-all-start = ((f32[32,2,2048]{2,1,0:T(2,128)}), f32[32,2,2048]{2,1,0:T(2,128)S(1)}, u32[]{:S(2)}, u32[]{:S(2)}) async-start(f32[32,2,2048]{2,1,0:T(2,128)} %bitcast.112), calls=%async_computation | async-start | bytes 1048576 | tf_op jit(solution)/shard_map/all_to_all | solution.py:182
  104.1 5.1 %collective-permute-start.16 = (f32[1,1,1,8,8,128]{5,4,3,2,1,0:T(8,128)S(1)}, f32[1,1,1,8,8,128]{5,4,3,2,1,0:T(8,128)S(1)}, u32[]{:S(2)}, u32[]{:S(2)}) collective-permute-start(f32[1,1,1,8,8,128]{5,4,3,2,1,0:T(8,128)S(1)} %get-tuple-element.55), channel_id=1, source_target_pairs={{0,4},{4,8},{8,12},{12,16},{16,20},{20,24},{24,28},{1,5},{5,9},{9,... | collective-permute-start | bytes 98312 | tf_op jit(solution)/shard_map/ppermute | solution.py:16
  107.5 6.2 %collective-permute-start.17 = (f32[1,1,1,8,8,128]{5,4,3,2,1,0:T(8,128)S(1)}, f32[1,1,1,8,8,128]{5,4,3,2,1,0:T(8,128)S(1)}, u32[]{:S(2)}, u32[]{:S(2)}) collective-permute-start(f32[1,1,1,8,8,128]{5,4,3,2,1,0:T(8,128)S(1)} %get-tuple-element.56), channel_id=1, source_target_pairs={{4,0},{8,4},{12,8},{16,12},{20,16},{24,20},{28,24},{5,1},{9,5},{13... | collective-permute-start | bytes 98312 | tf_op jit(solution)/shard_map/ppermute | solution.py:19
  118.0 5.2 %collective-permute-start.18 = (f32[1,1,1,8,8,128]{5,3,4,2,1,0:T(8,128)S(1)}, f32[1,1,1,8,8,128]{5,3,4,2,1,0:T(8,128)S(1)}, u32[]{:S(2)}, u32[]{:S(2)}) collective-permute-start(f32[1,1,1,8,8,128]{5,3,4,2,1,0:T(8,128)S(1)} %maximum_bitcast_fusion.13), channel_id=1, source_target_pairs={{0,1},{1,2},{2,3},{4,5},{5,6},{6,7},{8,9},{9,10},{10,11},{12,13},{... | collective-permute-start | bytes 98312 | tf_op jit(solution)/shard_map/ppermute | solution.py:16
  123.3 6.1 %collective-permute-start.19 = (f32[1,1,1,8,8,128]{5,3,4,2,1,0:T(8,128)S(1)}, f32[1,1,1,8,8,128]{5,3,4,2,1,0:T(8,128)S(1)}, u32[]{:S(2)}, u32[]{:S(2)}) collective-permute-start(f32[1,1,1,8,8,128]{5,3,4,2,1,0:T(8,128)S(1)} %get-tuple-element.30), channel_id=1, source_target_pairs={{1,0},{2,1},{3,2},{5,4},{6,5},{7,6},{9,8},{10,9},{11,10},{13,12},{... | collective-permute-start | bytes 98312 | tf_op jit(solution)/shard_map/ppermute | solution.py:19
  126.0 11.2 %all-to-all-start.1 = ((f32[8,2,2048]{2,1,0:T(2,128)}), f32[8,2,2048]{2,1,0:T(2,128)S(1)}, u32[]{:S(2)}, u32[]{:S(2)}) async-start(f32[8,2,2048]{2,1,0:T(2,128)} %broadcast_in_dim.213), calls=%async_computation.1 | async-start | bytes 262144 | tf_op jit(solution)/shard_map/all_to_all | solution.py:189

commit v13 on v12

--- a/solution.py
+++ b/solution.py
@@ -118,12 +118,12 @@
     lower, upper = faces(values_in, 3)
     rim_faces = jnp.concatenate([lower, upper], 1)
     padded = padded_2(rim_faces, (("ex", 1),), 1)
-    if ride is not None:
-        padded, ride = lax.optimization_barrier((padded, ride))
     values_in = combine(values_in, 3, 1, lower, upper, padded[:, :1], padded[:, 3:])
     lower, upper = faces(values_in, 4)
     rim_faces = jnp.concatenate([lower, upper], 2)
     padded = padded_2(rim_faces, (("ey", 2),), 1)
+    if ride is not None:
+        padded, ride = lax.optimization_barrier((padded, ride))
     values_in = combine(values_in, 4, 2, lower, upper, padded[:, :, :1], padded[:, :, 3:])
     lower, upper = faces(values_in, 5)
     empty = jnp.zeros_like(upper[..., :1])

time: 139 us -> 140 us (level)
  waiting for transfers between devices: 50.5 us -> 44 us
  starting transfers between devices: 54 us -> 60.2 us
    all_to_all x1, starting transfers between devices: 3.45 us -> 7.95 us  [strip_gather(): whole = lax.all_to_all(spread_out, 'ex', 0, 0, tiled=True)]
    all_to_all x1, waiting for transfers between devices: 4.09 us -> 0.01 us  [strip_reduce(): return lax.all_to_all(chunks, ('ex', 'ey'), 0, 0, tiled=True).sum(0)]
    ppermute x10, waiting for transfers between devices: 13.9 us -> 10.8 us  [padded_2(): lax.ppermute(lax.slice_in_dim(block, block.shape[dim] - width, None, axis...]
    ppermute x10, starting transfers between devices: 16.9 us -> 18.6 us  [padded_2(): lax.ppermute(lax.slice_in_dim(block, 0, width, axis=dim), axis, backward)]
  transfers between devices with their start and end apart: 22 -> 22, of which waited for: 20 -> 19; matrix products, arithmetic and copies ran while one was open for 9% -> 8% of each run, Pallas kernels for 0% -> 0%
where the time goes in v13:
time: 140 us; the launch traced here: 138 us
  starting transfers between devices  60.2 us (43%)
  waiting for transfers between devices  44 us (31%)
  other arithmetic  14.5 us (10%)
  matrix products  12 us (9%)
  local copies, waits for them, and re-layouts  5.32 us (4%)
  between operations  1.61 us (1%)
    ppermute x10, starting transfers between devices, padded_2(): lax.ppermute(lax.slice_in_dim(block, block.shape[dim] - width, None, axis...  28.5 us
    ppermute x10, waiting for transfers between devices, padded_2(): lax.ppermute(lax.slice_in_dim(block, 0, width, axis=dim), axis, backward)  26.6 us
    ppermute x10, starting transfers between devices, padded_2(): lax.ppermute(lax.slice_in_dim(block, 0, width, axis=dim), axis, backward)  18.6 us
    ppermute x10, waiting for transfers between devices, padded_2(): lax.ppermute(lax.slice_in_dim(block, block.shape[dim] - width, None, axis...  10.8 us
    all_to_all x1, starting transfers between devices, strip_gather(): whole = lax.all_to_all(spread_out, 'ex', 0, 0, tiled=True)  7.95 us
    all_to_all x1, waiting for transfers between devices, strip_gather(): whole = lax.all_to_all(spread_out, 'ex', 0, 0, tiled=True)  6.56 us
    all_to_all x1, starting transfers between devices, strip_reduce(): return lax.all_to_all(chunks, ('ex', 'ey'), 0, 0, tiled=True).sum(0)  5.07 us
    dot_general x2, matrix products, segment_sum(): jnp.dot(lhs, one_hot(ids % lanes, lanes), preferred_element_type=jnp.floa...  3.36 us
  transfers between devices with their start and end apart: 22, of which 19 were waited for; matrix products, arithmetic and copies ran while one was open for 8% of the time, Pallas kernels for 0%

profile of v13, /device:TPU:2, one launch (start us, length us, event | category | flops | bytes accessed | tf_op | source)
XLA Modules:
  0.0 137.7 jit_solution(10692423735676860409)
XLA Ops:
  2.9 1.2 fusion.90
  4.9 3.4 %collective-permute-start = (f32[2,1,1,8,8,128]{5,0,4,3,2,1:T(2,128)S(1)}, f32[2,1,1,8,8,128]{5,0,4,3,2,1:T(2,128)S(1)}, u32[]{:S(2)}, u32[]{:S(2)}) collective-permute-start(f32[2,1,1,8,8,128]{5,0,4,3,2,1:T(2,128)S(1)} %maximum_bitcast_fusion.9), channel_id=1, source_target_pairs={{0,4},{4,8},{8,12},{12,16},{16,20},{20,24},{24,28},{1,5},{5,9},{9,... | collective-permute-start | bytes 196616 | tf_op jit(solution)/shard_map/ppermute | solution.py:16
  8.3 0.9 fusion.94
  10.0 1.2 fusion.20
  11.3 1.3 collective-permute-start.1
  13.3 4.3 %collective-permute-done.1 = f32[2,1,1,8,8,128]{5,0,4,3,2,1:T(2,128)S(1)} collective-permute-done((f32[2,1,1,8,8,128]{5,0,4,3,2,1:T(2,128)S(1)}, f32[2,1,1,8,8,128]{5,0,4,3,2,1:T(2,128)S(1)}, u32[]{:S(2)}, u32[]{:S(2)}) %collective-permute-start.1) | collective-permute-done | bytes 65568 | tf_op jit(solution)/shard_map/ppermute | solution.py:19
  17.6 1.9 %collective-permute-start.2 = (f32[2,1,1,8,8,128]{5,3,0,4,2,1:T(8,128)S(1)}, f32[2,1,1,8,8,128]{5,3,0,4,2,1:T(8,128)S(1)}, u32[]{:S(2)}, u32[]{:S(2)}) collective-permute-start(f32[2,1,1,8,8,128]{5,3,0,4,2,1:T(8,128)S(1)} %maximum_bitcast_fusion.7), channel_id=1, source_target_pairs={{0,1},{1,2},{2,3},{4,5},{5,6},{6,7},{8,9},{9,10},{10,11},{12,13},{... | collective-permute-start | bytes 196616 | tf_op jit(solution)/shard_map/ppermute | solution.py:16
  19.5 3.6 %collective-permute-done.2 = f32[2,1,1,8,8,128]{5,3,0,4,2,1:T(8,128)S(1)} collective-permute-done((f32[2,1,1,8,8,128]{5,3,0,4,2,1:T(8,128)S(1)}, f32[2,1,1,8,8,128]{5,3,0,4,2,1:T(8,128)S(1)}, u32[]{:S(2)}, u32[]{:S(2)}) %collective-permute-start.2) | collective-permute-done | bytes 65568 | tf_op jit(solution)/shard_map/ppermute | solution.py:16
  23.2 1.9 %collective-permute-start.3 = (f32[2,1,1,8,8,128]{5,3,0,4,2,1:T(8,128)S(1)}, f32[2,1,1,8,8,128]{5,3,0,4,2,1:T(8,128)S(1)}, u32[]{:S(2)}, u32[]{:S(2)}) collective-permute-start(f32[2,1,1,8,8,128]{5,3,0,4,2,1:T(8,128)S(1)} %get-tuple-element.44), channel_id=1, source_target_pairs={{1,0},{2,1},{3,2},{5,4},{6,5},{7,6},{9,8},{10,9},{11,10},{13,12},{... | collective-permute-start | bytes 196616 | tf_op jit(solution)/shard_map/ppermute | solution.py:19
  25.5 1.5 %collective-permute-done.3 = f32[2,1,1,8,8,128]{5,3,0,4,2,1:T(8,128)S(1)} collective-permute-done((f32[2,1,1,8,8,128]{5,3,0,4,2,1:T(8,128)S(1)}, f32[2,1,1,8,8,128]{5,3,0,4,2,1:T(8,128)S(1)}, u32[]{:S(2)}, u32[]{:S(2)}) %collective-permute-start.3) | collective-permute-done | bytes 65568 | tf_op jit(solution)/shard_map/ppermute | solution.py:19
  28.8 0.9 fusion.30
  29.8 4.3 %collective-permute-start.4 = (f32[1,1,1,8,8,128]{5,4,3,2,1,0:T(8,128)S(1)}, f32[1,1,1,8,8,128]{5,4,3,2,1,0:T(8,128)S(1)}, u32[]{:S(2)}, u32[]{:S(2)}) collective-permute-start(f32[1,1,1,8,8,128]{5,4,3,2,1,0:T(8,128)S(1)} %bitcast.484), channel_id=1, source_target_pairs={{0,4},{4,8},{8,12},{12,16},{16,20},{20,24},{24,28},{1,5},{5,9},{9,... | collective-permute-start | bytes 98312 | tf_op jit(solution)/shard_map/ppermute | solution.py:16
  34.1 1.3 collective-permute-start.5
  35.7 4.2 %collective-permute-done.5 = f32[1,1,1,8,8,128]{5,4,3,2,1,0:T(8,128)S(1)} collective-permute-done((f32[1,1,1,8,8,128]{5,4,3,2,1,0:T(8,128)S(1)}, f32[1,1,1,8,8,128]{5,4,3,2,1,0:T(8,128)S(1)}, u32[]{:S(2)}, u32[]{:S(2)}) %collective-permute-start.5) | collective-permute-done | bytes 32800 | tf_op jit(solution)/shard_map/ppermute | solution.py:19
  39.9 1.9 %collective-permute-start.6 = (f32[1,1,1,8,8,128]{5,3,4,2,1,0:T(8,128)S(1)}, f32[1,1,1,8,8,128]{5,3,4,2,1,0:T(8,128)S(1)}, u32[]{:S(2)}, u32[]{:S(2)}) collective-permute-start(f32[1,1,1,8,8,128]{5,3,4,2,1,0:T(8,128)S(1)} %maximum_bitcast_fusion.19), channel_id=1, source_target_pairs={{0,1},{1,2},{2,3},{4,5},{5,6},{6,7},{8,9},{9,10},{10,11},{12,13},{... | collective-permute-start | bytes 98312 | tf_op jit(solution)/shard_map/ppermute | solution.py:16
  41.9 1.9 %fusion = f32[768,256]{1,0:T(8,128)S(1)} fusion(bf16[256,4096]{1,0:T(8,128)(2,1)S(1)} %get-tuple-element.85, bf16[256,4096]{1,0:T(8,128)(2,1)S(1)} %get-tuple-element.86, bf16[256,4096]{1,0:T(8,128)(2,1)S(1)} %get-tuple-element.84, s32[4096]{0:T(1024)S(1)} %add_select_fusion), kind=kOutput, calls=%fused_computation | convolution fusion | flops 1630535680 | bytes 7094272 | tf_op jit(solution)/shard_map/dot_general | solution.py:167
  43.8 1.4 collective-permute-done.6
  45.2 2.3 %collective-permute-start.7 = (f32[1,1,1,8,8,128]{5,3,4,2,1,0:T(8,128)S(1)}, f32[1,1,1,8,8,128]{5,3,4,2,1,0:T(8,128)S(1)}, u32[]{:S(2)}, u32[]{:S(2)}) collective-permute-start(f32[1,1,1,8,8,128]{5,3,4,2,1,0:T(8,128)S(1)} %get-tuple-element.40), channel_id=1, source_target_pairs={{1,0},{2,1},{3,2},{5,4},{6,5},{7,6},{9,8},{10,9},{11,10},{13,12},{... | collective-permute-start | bytes 98312 | tf_op jit(solution)/shard_map/ppermute | solution.py:19
  47.7 1.4 collective-permute-done.7
  51.0 4.1 %collective-permute-start.8 = (f32[1,1,1,8,8,128]{5,4,3,2,1,0:T(8,128)S(1)}, f32[1,1,1,8,8,128]{5,4,3,2,1,0:T(8,128)S(1)}, u32[]{:S(2)}, u32[]{:S(2)}) collective-permute-start(f32[1,1,1,8,8,128]{5,4,3,2,1,0:T(8,128)S(1)} %get-tuple-element.70), channel_id=1, source_target_pairs={{0,4},{4,8},{8,12},{12,16},{16,20},{20,24},{24,28},{1,5},{5,9},{9,... | collective-permute-start | bytes 98312 | tf_op jit(solution)/shard_map/ppermute | solution.py:16
  55.1 1.3 collective-permute-start.9
  56.7 4.2 %collective-permute-done.9 = f32[1,1,1,8,8,128]{5,4,3,2,1,0:T(8,128)S(1)} collective-permute-done((f32[1,1,1,8,8,128]{5,4,3,2,1,0:T(8,128)S(1)}, f32[1,1,1,8,8,128]{5,4,3,2,1,0:T(8,128)S(1)}, u32[]{:S(2)}, u32[]{:S(2)}) %collective-permute-start.9) | collective-permute-done | bytes 32800 | tf_op jit(solution)/shard_map/ppermute | solution.py:19
  60.9 1.9 %collective-permute-start.10 = (f32[1,1,1,8,8,128]{5,4,3,2,1,0:T(8,128)S(1)}, f32[1,1,1,8,8,128]{5,4,3,2,1,0:T(8,128)S(1)}, u32[]{:S(2)}, u32[]{:S(2)}) collective-permute-start(f32[1,1,1,8,8,128]{5,4,3,2,1,0:T(8,128)S(1)} %maximum_bitcast_fusion.17), channel_id=1, source_target_pairs={{0,1},{1,2},{2,3},{4,5},{5,6},{6,7},{8,9},{9,10},{10,11},{12,13},{... | collective-permute-start | bytes 98312 | tf_op jit(solution)/shard_map/ppermute | solution.py:16
  62.9 3.2 %collective-permute-done.10 = f32[1,1,1,8,8,128]{5,4,3,2,1,0:T(8,128)S(1)} collective-permute-done((f32[1,1,1,8,8,128]{5,4,3,2,1,0:T(8,128)S(1)}, f32[1,1,1,8,8,128]{5,4,3,2,1,0:T(8,128)S(1)}, u32[]{:S(2)}, u32[]{:S(2)}) %collective-permute-start.10) | collective-permute-done | bytes 32800 | tf_op jit(solution)/shard_map/ppermute | solution.py:16
  66.2 2.1 %collective-permute-start.11 = (f32[1,1,1,8,8,128]{5,4,3,2,1,0:T(8,128)S(1)}, f32[1,1,1,8,8,128]{5,4,3,2,1,0:T(8,128)S(1)}, u32[]{:S(2)}, u32[]{:S(2)}) collective-permute-start(f32[1,1,1,8,8,128]{5,4,3,2,1,0:T(8,128)S(1)} %get-tuple-element.38), channel_id=1, source_target_pairs={{1,0},{2,1},{3,2},{5,4},{6,5},{7,6},{9,8},{10,9},{11,10},{13,12},{... | collective-permute-start | bytes 98312 | tf_op jit(solution)/shard_map/ppermute | solution.py:19
  68.4 1.3 collective-permute-done.11
  71.8 3.6 %collective-permute-start.12 = (f32[1,1,1,8,8,128]{5,4,3,2,1,0:T(8,128)S(1)}, f32[1,1,1,8,8,128]{5,4,3,2,1,0:T(8,128)S(1)}, u32[]{:S(2)}, u32[]{:S(2)}) collective-permute-start(f32[1,1,1,8,8,128]{5,4,3,2,1,0:T(8,128)S(1)} %get-tuple-element.64), channel_id=1, source_target_pairs={{0,4},{4,8},{8,12},{12,16},{16,20},{20,24},{24,28},{1,5},{5,9},{9,... | collective-permute-start | bytes 98312 | tf_op jit(solution)/shard_map/ppermute | solution.py:16
  75.4 1.3 collective-permute-start.13
  77.0 4.2 %collective-permute-done.13 = f32[1,1,1,8,8,128]{5,4,3,2,1,0:T(8,128)S(1)} collective-permute-done((f32[1,1,1,8,8,128]{5,4,3,2,1,0:T(8,128)S(1)}, f32[1,1,1,8,8,128]{5,4,3,2,1,0:T(8,128)S(1)}, u32[]{:S(2)}, u32[]{:S(2)}) %collective-permute-start.13) | collective-permute-done | bytes 32800 | tf_op jit(solution)/shard_map/ppermute | solution.py:19
  81.2 1.9 %collective-permute-start.14 = (f32[1,1,1,8,8,128]{5,4,3,2,1,0:T(8,128)S(1)}, f32[1,1,1,8,8,128]{5,4,3,2,1,0:T(8,128)S(1)}, u32[]{:S(2)}, u32[]{:S(2)}) collective-permute-start(f32[1,1,1,8,8,128]{5,4,3,2,1,0:T(8,128)S(1)} %maximum_bitcast_fusion.15), channel_id=1, source_target_pairs={{0,1},{1,2},{2,3},{4,5},{5,6},{6,7},{8,9},{9,10},{10,11},{12,13},{... | collective-permute-start | bytes 98312 | tf_op jit(solution)/shard_map/ppermute | solution.py:16
  83.2 1.9 %fusion.15 = f32[768,4096]{1,0:T(8,128)S(1)} fusion(s32[4096]{0:T(1024)S(1)} %bitcast.478, bf16[256,256]{1,0:T(8,128)(2,1)S(1)} %get-tuple-element.58, bf16[256,256]{1,0:T(8,128)(2,1)S(1)} %get-tuple-element.59, bf16[256,256]{1,0:T(8,128)(2,1)S(1)} %get-tuple-element.57), kind=kOutput, calls=%fused_computation.19 | convolution fusion | flops 1612840960 | bytes 12992512 | tf_op jit(solution)/shard_map/dot_general | solution.py:153
  85.1 1.4 %collective-permute-done.14 = f32[1,1,1,8,8,128]{5,4,3,2,1,0:T(8,128)S(1)} collective-permute-done((f32[1,1,1,8,8,128]{5,4,3,2,1,0:T(8,128)S(1)}, f32[1,1,1,8,8,128]{5,4,3,2,1,0:T(8,128)S(1)}, u32[]{:S(2)}, u32[]{:S(2)}) %collective-permute-start.14) | collective-permute-done | bytes 32800 | tf_op jit(solution)/shard_map/ppermute | solution.py:16
  86.5 2.2 %collective-permute-start.15 = (f32[1,1,1,8,8,128]{5,4,3,2,1,0:T(8,128)S(1)}, f32[1,1,1,8,8,128]{5,4,3,2,1,0:T(8,128)S(1)}, u32[]{:S(2)}, u32[]{:S(2)}) collective-permute-start(f32[1,1,1,8,8,128]{5,4,3,2,1,0:T(8,128)S(1)} %get-tuple-element.34), channel_id=1, source_target_pairs={{1,0},{2,1},{3,2},{5,4},{6,5},{7,6},{9,8},{10,9},{11,10},{13,12},{... | collective-permute-start | bytes 98312 | tf_op jit(solution)/shard_map/ppermute | solution.py:19
  88.7 1.4 fusion.9
  92.2 1.3 fusion.14
  93.5 0.9 fusion.7
  94.4 0.9 fusion.17
  95.3 1.4 %fusion.10 = f32[512,256]{1,0:T(8,128)S(1)} fusion(bf16[256,4096]{1,0:T(8,128)(2,1)S(1)} %get-tuple-element.83, bf16[256,4096]{1,0:T(8,128)(2,1)S(1)} %get-tuple-element.82, s32[4096]{0:T(1024)S(1)} %add_select_fusion), kind=kOutput, calls=%fused_computation.13 | convolution fusion | flops 1083179008 | bytes 4734976 | tf_op jit(solution)/shard_map/dot_general | solution.py:167
  96.9 1.2 copy.203
  98.1 5.1 %all-to-all-start = ((f32[32,2,2048]{2,1,0:T(2,128)}), f32[32,2,2048]{2,1,0:T(2,128)S(1)}, u32[]{:S(2)}, u32[]{:S(2)}) async-start(f32[32,2,2048]{2,1,0:T(2,128)} %bitcast.117), calls=%async_computation | async-start | bytes 1048576 | tf_op jit(solution)/shard_map/all_to_all | solution.py:182
  104.1 3.4 %collective-permute-start.16 = (f32[1,1,1,8,8,128]{5,4,3,2,1,0:T(8,128)S(1)}, f32[1,1,1,8,8,128]{5,4,3,2,1,0:T(8,128)S(1)}, u32[]{:S(2)}, u32[]{:S(2)}) collective-permute-start(f32[1,1,1,8,8,128]{5,4,3,2,1,0:T(8,128)S(1)} %get-tuple-element.55), channel_id=1, source_target_pairs={{0,4},{4,8},{8,12},{12,16},{16,20},{20,24},{24,28},{1,5},{5,9},{9,... | collective-permute-start | bytes 98312 | tf_op jit(solution)/shard_map/ppermute | solution.py:16
  107.5 1.3 collective-permute-start.17
  109.5 3.9 %collective-permute-done.17 = f32[1,1,1,8,8,128]{5,4,3,2,1,0:T(8,128)S(1)} collective-permute-done((f32[1,1,1,8,8,128]{5,4,3,2,1,0:T(8,128)S(1)}, f32[1,1,1,8,8,128]{5,4,3,2,1,0:T(8,128)S(1)}, u32[]{:S(2)}, u32[]{:S(2)}) %collective-permute-start.17) | collective-permute-done | bytes 32800 | tf_op jit(solution)/shard_map/ppermute | solution.py:19
  113.4 1.9 %collective-permute-start.18 = (f32[1,1,1,8,8,128]{5,3,4,2,1,0:T(8,128)S(1)}, f32[1,1,1,8,8,128]{5,3,4,2,1,0:T(8,128)S(1)}, u32[]{:S(2)}, u32[]{:S(2)}) collective-permute-start(f32[1,1,1,8,8,128]{5,3,4,2,1,0:T(8,128)S(1)} %get-tuple-element.50), channel_id=1, source_target_pairs={{0,1},{1,2},{2,3},{4,5},{5,6},{6,7},{8,9},{9,10},{10,11},{12,13},{... | collective-permute-start | bytes 98312 | tf_op jit(solution)/shard_map/ppermute | solution.py:16
  115.3 3.6 %collective-permute-start.19 = (f32[1,1,1,8,8,128]{5,3,4,2,1,0:T(8,128)S(1)}, f32[1,1,1,8,8,128]{5,3,4,2,1,0:T(8,128)S(1)}, u32[]{:S(2)}, u32[]{:S(2)}) collective-permute-start(f32[1,1,1,8,8,128]{5,3,4,2,1,0:T(8,128)S(1)} %get-tuple-element.49), channel_id=1, source_target_pairs={{1,0},{2,1},{3,2},{5,4},{6,5},{7,6},{9,8},{10,9},{11,10},{13,12},{... | collective-permute-start | bytes 98312 | tf_op jit(solution)/shard_map/ppermute | solution.py:19
  119.1 1.5 %collective-permute-done.19 = f32[1,1,1,8,8,128]{5,3,4,2,1,0:T(8,128)S(1)} collective-permute-done((f32[1,1,1,8,8,128]{5,3,4,2,1,0:T(8,128)S(1)}, f32[1,1,1,8,8,128]{5,3,4,2,1,0:T(8,128)S(1)}, u32[]{:S(2)}, u32[]{:S(2)}) %collective-permute-start.19) | collective-permute-done | bytes 32800 | tf_op jit(solution)/shard_map/ppermute | solution.py:19
  121.6 8.0 %all-to-all-start.1 = ((f32[8,2,2048]{2,1,0:T(2,128)}), f32[8,2,2048]{2,1,0:T(2,128)S(1)}, u32[]{:S(2)}, u32[]{:S(2)}) async-start(f32[8,2,2048]{2,1,0:T(2,128)} %broadcast_in_dim.213), calls=%async_computation.1 | async-start | bytes 262144 | tf_op jit(solution)/shard_map/all_to_all | solution.py:189
  130.4 6.6 %all-to-all-done.1 = f32[8,2,2048]{2,1,0:T(2,128)S(1)} async-done(((f32[8,2,2048]{2,1,0:T(2,128)}), f32[8,2,2048]{2,1,0:T(2,128)S(1)}, u32[]{:S(2)}, u32[]{:S(2)}) %all-to-all-start.1) | async-done | bytes 131104 | tf_op jit(solution)/shard_map/all_to_all | solution.py:189
  (134 shorter events, 18.2 us)
Async XLA Ops:
  0.6 10.6 %copy-start = (f32[1,1,8,8,8,128]{5,4,3,2,1,0:T(8,128)S(1)}, f32[1,1,8,8,8,128]{5,4,3,2,1,0:T(8,128)}, u32[]{:S(2)}) copy-start(f32[1,1,8,8,8,128]{5,4,3,2,1,0:T(8,128)} %param.36) | copy-start | bytes 786436
  4.9 6.3 %collective-permute-start = (f32[2,1,1,8,8,128]{5,0,4,3,2,1:T(2,128)S(1)}, f32[2,1,1,8,8,128]{5,0,4,3,2,1:T(2,128)S(1)}, u32[]{:S(2)}, u32[]{:S(2)}) collective-permute-start(f32[2,1,1,8,8,128]{5,0,4,3,2,1:T(2,128)S(1)} %maximum_bitcast_fusion.9), channel_id=1, source_target_pairs={{0,4},{4,8},{8,12},{12,16},{16,20},{20,24},{24,28},{1,5},{5,9},{9,... | collective-permute-start | bytes 196616 | tf_op jit(solution)/shard_map/ppermute | solution.py:16
  10.0 9.5 %copy-start.4 = (s32[1,4096,1]{1,2,0:T(1,128)S(1)}, s32[1,4096,1]{1,2,0:T(1,128)}, u32[]{:S(2)}) copy-start(s32[1,4096,1]{1,2,0:T(1,128)} %param.39) | copy-start | bytes 49156
  11.3 6.2 %collective-permute-start.1 = (f32[2,1,1,8,8,128]{5,0,4,3,2,1:T(2,128)S(1)}, f32[2,1,1,8,8,128]{5,0,4,3,2,1:T(2,128)S(1)}, u32[]{:S(2)}, u32[]{:S(2)}) collective-permute-start(f32[2,1,1,8,8,128]{5,0,4,3,2,1:T(2,128)S(1)} %get-tuple-element.46), channel_id=1, source_target_pairs={{4,0},{8,4},{12,8},{16,12},{20,16},{24,20},{28,24},{5,1},{9,5},{13... | collective-permute-start | bytes 196616 | tf_op jit(solution)/shard_map/ppermute | solution.py:19
  17.6 5.6 %collective-permute-start.2 = (f32[2,1,1,8,8,128]{5,3,0,4,2,1:T(8,128)S(1)}, f32[2,1,1,8,8,128]{5,3,0,4,2,1:T(8,128)S(1)}, u32[]{:S(2)}, u32[]{:S(2)}) collective-permute-start(f32[2,1,1,8,8,128]{5,3,0,4,2,1:T(8,128)S(1)} %maximum_bitcast_fusion.7), channel_id=1, source_target_pairs={{0,1},{1,2},{2,3},{4,5},{5,6},{6,7},{8,9},{9,10},{10,11},{12,13},{... | collective-permute-start | bytes 196616 | tf_op jit(solution)/shard_map/ppermute | solution.py:16
  23.2 4.7 %copy-start.1 = (f32[8,8,1,1]{1,0,3,2:T(8,128)S(1)}, f32[8,8,1,1]{1,0,3,2:T(8,128)}, u32[]{:S(2)}) copy-start(f32[8,8,1,1]{1,0,3,2:T(8,128)} %constant.130) | copy-start | bytes 772
  23.2 3.8 %collective-permute-start.3 = (f32[2,1,1,8,8,128]{5,3,0,4,2,1:T(8,128)S(1)}, f32[2,1,1,8,8,128]{5,3,0,4,2,1:T(8,128)S(1)}, u32[]{:S(2)}, u32[]{:S(2)}) collective-permute-start(f32[2,1,1,8,8,128]{5,3,0,4,2,1:T(8,128)S(1)} %get-tuple-element.44), channel_id=1, source_target_pairs={{1,0},{2,1},{3,2},{5,4},{6,5},{7,6},{9,8},{10,9},{11,10},{13,12},{... | collective-permute-start | bytes 196616 | tf_op jit(solution)/shard_map/ppermute | solution.py:19
  25.3 3.4 %copy-start.6 = (f32[8]{0:T(128)S(1)}, f32[8]{0:T(128)}, u32[]{:S(2)}) copy-start(f32[8]{0:T(128)} %constant.125) | copy-start | bytes 100
  27.2 8.2 %copy-start.2 = (s32[1,4096]{1,0:T(1,128)S(1)}, s32[1,4096]{1,0:T(1,128)}, u32[]{:S(2)}) copy-start(s32[1,4096]{1,0:T(1,128)} %param.40) | copy-start | bytes 49156
  29.8 5.9 %collective-permute-start.4 = (f32[1,1,1,8,8,128]{5,4,3,2,1,0:T(8,128)S(1)}, f32[1,1,1,8,8,128]{5,4,3,2,1,0:T(8,128)S(1)}, u32[]{:S(2)}, u32[]{:S(2)}) collective-permute-start(f32[1,1,1,8,8,128]{5,4,3,2,1,0:T(8,128)S(1)} %bitcast.484), channel_id=1, source_target_pairs={{0,4},{4,8},{8,12},{12,16},{16,20},{20,24},{24,28},{1,5},{5,9},{9,... | collective-permute-start | bytes 98312 | tf_op jit(solution)/shard_map/ppermute | solution.py:16
  34.1 5.8 %collective-permute-start.5 = (f32[1,1,1,8,8,128]{5,4,3,2,1,0:T(8,128)S(1)}, f32[1,1,1,8,8,128]{5,4,3,2,1,0:T(8,128)S(1)}, u32[]{:S(2)}, u32[]{:S(2)}) collective-permute-start(f32[1,1,1,8,8,128]{5,4,3,2,1,0:T(8,128)S(1)} %bitcast.486), channel_id=1, source_target_pairs={{4,0},{8,4},{12,8},{16,12},{20,16},{24,20},{28,24},{5,1},{9,5},{13... | collective-permute-start | bytes 98312 | tf_op jit(solution)/shard_map/ppermute | solution.py:19
  39.9 5.2 %collective-permute-start.6 = (f32[1,1,1,8,8,128]{5,3,4,2,1,0:T(8,128)S(1)}, f32[1,1,1,8,8,128]{5,3,4,2,1,0:T(8,128)S(1)}, u32[]{:S(2)}, u32[]{:S(2)}) collective-permute-start(f32[1,1,1,8,8,128]{5,3,4,2,1,0:T(8,128)S(1)} %maximum_bitcast_fusion.19), channel_id=1, source_target_pairs={{0,1},{1,2},{2,3},{4,5},{5,6},{6,7},{8,9},{9,10},{10,11},{12,13},{... | collective-permute-start | bytes 98312 | tf_op jit(solution)/shard_map/ppermute | solution.py:16
  45.2 17.7 %copy-start.3 = (s32[1,4096]{1,0:T(1,128)S(1)}, s32[1,4096]{1,0:T(1,128)}, u32[]{:S(2)}) copy-start(s32[1,4096]{1,0:T(1,128)} %param.38) | copy-start | bytes 49156
  45.2 3.9 %collective-permute-start.7 = (f32[1,1,1,8,8,128]{5,3,4,2,1,0:T(8,128)S(1)}, f32[1,1,1,8,8,128]{5,3,4,2,1,0:T(8,128)S(1)}, u32[]{:S(2)}, u32[]{:S(2)}) collective-permute-start(f32[1,1,1,8,8,128]{5,3,4,2,1,0:T(8,128)S(1)} %get-tuple-element.40), channel_id=1, source_target_pairs={{1,0},{2,1},{3,2},{5,4},{6,5},{7,6},{9,8},{10,9},{11,10},{13,12},{... | collective-permute-start | bytes 98312 | tf_op jit(solution)/shard_map/ppermute | solution.py:19
  51.0 5.7 %collective-permute-start.8 = (f32[1,1,1,8,8,128]{5,4,3,2,1,0:T(8,128)S(1)}, f32[1,1,1,8,8,128]{5,4,3,2,1,0:T(8,128)S(1)}, u32[]{:S(2)}, u32[]{:S(2)}) collective-permute-start(f32[1,1,1,8,8,128]{5,4,3,2,1,0:T(8,128)S(1)} %get-tuple-element.70), channel_id=1, source_target_pairs={{0,4},{4,8},{8,12},{12,16},{16,20},{20,24},{24,28},{1,5},{5,9},{9,... | collective-permute-start | bytes 98312 | tf_op jit(solution)/shard_map/ppermute | solution.py:16
  55.1 5.8 %collective-permute-start.9 = (f32[1,1,1,8,8,128]{5,4,3,2,1,0:T(8,128)S(1)}, f32[1,1,1,8,8,128]{5,4,3,2,1,0:T(8,128)S(1)}, u32[]{:S(2)}, u32[]{:S(2)}) collective-permute-start(f32[1,1,1,8,8,128]{5,4,3,2,1,0:T(8,128)S(1)} %get-tuple-element.71), channel_id=1, source_target_pairs={{4,0},{8,4},{12,8},{16,12},{20,16},{24,20},{28,24},{5,1},{9,5},{13... | collective-permute-start | bytes 98312 | tf_op jit(solution)/shard_map/ppermute | solution.py:19
  60.9 5.2 %collective-permute-start.10 = (f32[1,1,1,8,8,128]{5,4,3,2,1,0:T(8,128)S(1)}, f32[1,1,1,8,8,128]{5,4,3,2,1,0:T(8,128)S(1)}, u32[]{:S(2)}, u32[]{:S(2)}) collective-permute-start(f32[1,1,1,8,8,128]{5,4,3,2,1,0:T(8,128)S(1)} %maximum_bitcast_fusion.17), channel_id=1, source_target_pairs={{0,1},{1,2},{2,3},{4,5},{5,6},{6,7},{8,9},{9,10},{10,11},{12,13},{... | collective-permute-start | bytes 98312 | tf_op jit(solution)/shard_map/ppermute | solution.py:16
  66.2 3.5 %collective-permute-start.11 = (f32[1,1,1,8,8,128]{5,4,3,2,1,0:T(8,128)S(1)}, f32[1,1,1,8,8,128]{5,4,3,2,1,0:T(8,128)S(1)}, u32[]{:S(2)}, u32[]{:S(2)}) collective-permute-start(f32[1,1,1,8,8,128]{5,4,3,2,1,0:T(8,128)S(1)} %get-tuple-element.38), channel_id=1, source_target_pairs={{1,0},{2,1},{3,2},{5,4},{6,5},{7,6},{9,8},{10,9},{11,10},{13,12},{... | collective-permute-start | bytes 98312 | tf_op jit(solution)/shard_map/ppermute | solution.py:19
  71.8 5.2 %collective-permute-start.12 = (f32[1,1,1,8,8,128]{5,4,3,2,1,0:T(8,128)S(1)}, f32[1,1,1,8,8,128]{5,4,3,2,1,0:T(8,128)S(1)}, u32[]{:S(2)}, u32[]{:S(2)}) collective-permute-start(f32[1,1,1,8,8,128]{5,4,3,2,1,0:T(8,128)S(1)} %get-tuple-element.64), channel_id=1, source_target_pairs={{0,4},{4,8},{8,12},{12,16},{16,20},{20,24},{24,28},{1,5},{5,9},{9,... | collective-permute-start | bytes 98312 | tf_op jit(solution)/shard_map/ppermute | solution.py:16
  75.4 5.8 %collective-permute-start.13 = (f32[1,1,1,8,8,128]{5,4,3,2,1,0:T(8,128)S(1)}, f32[1,1,1,8,8,128]{5,4,3,2,1,0:T(8,128)S(1)}, u32[]{:S(2)}, u32[]{:S(2)}) collective-permute-start(f32[1,1,1,8,8,128]{5,4,3,2,1,0:T(8,128)S(1)} %get-tuple-element.65), channel_id=1, source_target_pairs={{4,0},{8,4},{12,8},{16,12},{20,16},{24,20},{28,24},{5,1},{9,5},{13... | collective-permute-start | bytes 98312 | tf_op jit(solution)/shard_map/ppermute | solution.py:19
  81.2 5.2 %collective-permute-start.14 = (f32[1,1,1,8,8,128]{5,4,3,2,1,0:T(8,128)S(1)}, f32[1,1,1,8,8,128]{5,4,3,2,1,0:T(8,128)S(1)}, u32[]{:S(2)}, u32[]{:S(2)}) collective-permute-start(f32[1,1,1,8,8,128]{5,4,3,2,1,0:T(8,128)S(1)} %maximum_bitcast_fusion.15), channel_id=1, source_target_pairs={{0,1},{1,2},{2,3},{4,5},{5,6},{6,7},{8,9},{9,10},{10,11},{12,13},{... | collective-permute-start | bytes 98312 | tf_op jit(solution)/shard_map/ppermute | solution.py:16
  86.5 3.8 %collective-permute-start.15 = (f32[1,1,1,8,8,128]{5,4,3,2,1,0:T(8,128)S(1)}, f32[1,1,1,8,8,128]{5,4,3,2,1,0:T(8,128)S(1)}, u32[]{:S(2)}, u32[]{:S(2)}) collective-permute-start(f32[1,1,1,8,8,128]{5,4,3,2,1,0:T(8,128)S(1)} %get-tuple-element.34), channel_id=1, source_target_pairs={{1,0},{2,1},{3,2},{5,4},{6,5},{7,6},{9,8},{10,9},{11,10},{13,12},{... | collective-permute-start | bytes 98312 | tf_op jit(solution)/shard_map/ppermute | solution.py:19
  93.5 0.9 copy-start.5
  98.1 22.5 %all-to-all-start = ((f32[32,2,2048]{2,1,0:T(2,128)}), f32[32,2,2048]{2,1,0:T(2,128)S(1)}, u32[]{:S(2)}, u32[]{:S(2)}) async-start(f32[32,2,2048]{2,1,0:T(2,128)} %bitcast.117), calls=%async_computation | async-start | bytes 1048576 | tf_op jit(solution)/shard_map/all_to_all | solution.py:182
  104.1 5.4 %collective-permute-start.16 = (f32[1,1,1,8,8,128]{5,4,3,2,1,0:T(8,128)S(1)}, f32[1,1,1,8,8,128]{5,4,3,2,1,0:T(8,128)S(1)}, u32[]{:S(2)}, u32[]{:S(2)}) collective-permute-start(f32[1,1,1,8,8,128]{5,4,3,2,1,0:T(8,128)S(1)} %get-tuple-element.55), channel_id=1, source_target_pairs={{0,4},{4,8},{8,12},{12,16},{16,20},{20,24},{24,28},{1,5},{5,9},{9,... | collective-permute-start | bytes 98312 | tf_op jit(solution)/shard_map/ppermute | solution.py:16
  107.5 5.9 %collective-permute-start.17 = (f32[1,1,1,8,8,128]{5,4,3,2,1,0:T(8,128)S(1)}, f32[1,1,1,8,8,128]{5,4,3,2,1,0:T(8,128)S(1)}, u32[]{:S(2)}, u32[]{:S(2)}) collective-permute-start(f32[1,1,1,8,8,128]{5,4,3,2,1,0:T(8,128)S(1)} %get-tuple-element.56), channel_id=1, source_target_pairs={{4,0},{8,4},{12,8},{16,12},{20,16},{24,20},{28,24},{5,1},{9,5},{13... | collective-permute-start | bytes 98312 | tf_op jit(solution)/shard_map/ppermute | solution.py:19
  113.4 5.7 %collective-permute-start.18 = (f32[1,1,1,8,8,128]{5,3,4,2,1,0:T(8,128)S(1)}, f32[1,1,1,8,8,128]{5,3,4,2,1,0:T(8,128)S(1)}, u32[]{:S(2)}, u32[]{:S(2)}) collective-permute-start(f32[1,1,1,8,8,128]{5,3,4,2,1,0:T(8,128)S(1)} %get-tuple-element.50), channel_id=1, source_target_pairs={{0,1},{1,2},{2,3},{4,5},{5,6},{6,7},{8,9},{9,10},{10,11},{12,13},{... | collective-permute-start | bytes 98312 | tf_op jit(solution)/shard_map/ppermute | solution.py:16
  115.3 5.2 %collective-permute-start.19 = (f32[1,1,1,8,8,128]{5,3,4,2,1,0:T(8,128)S(1)}, f32[1,1,1,8,8,128]{5,3,4,2,1,0:T(8,128)S(1)}, u32[]{:S(2)}, u32[]{:S(2)}) collective-permute-start(f32[1,1,1,8,8,128]{5,3,4,2,1,0:T(8,128)S(1)} %get-tuple-element.49), channel_id=1, source_target_pairs={{1,0},{2,1},{3,2},{5,4},{6,5},{7,6},{9,8},{10,9},{11,10},{13,12},{... | collective-permute-start | bytes 98312 | tf_op jit(solution)/shard_map/ppermute | solution.py:19
  121.6 15.3 %all-to-all-start.1 = ((f32[8,2,2048]{2,1,0:T(2,128)}), f32[8,2,2048]{2,1,0:T(2,128)S(1)}, u32[]{:S(2)}, u32[]{:S(2)}) async-start(f32[8,2,2048]{2,1,0:T(2,128)} %broadcast_in_dim.213), calls=%async_computation.1 | async-start | bytes 262144 | tf_op jit(solution)/shard_map/all_to_all | solution.py:189

commit v14 on v12

--- a/solution.py
+++ b/solution.py
@@ -159,7 +159,7 @@
 
 
 def segment_sum(values, ids, bins, lanes, count=3):
-    rows = bins // lanes
+    rows = -(-bins // lanes)
     hit_row_t = lax.broadcasted_iota(jnp.int32, (rows, 1), 0) == (ids // lanes)[None, :]
     lhs = jnp.concatenate(
         [jnp.where(hit_row_t, part[None, :], jnp.bfloat16(0)) for part in split_parts(values, count)], axis=0
@@ -168,18 +168,24 @@
     total = sums[:rows]
     for n in range(1, count):
         total = total + sums[n * rows : (n + 1) * rows]
-    return total.reshape(-1)
+    return total.reshape(-1)[:bins]
+
+
+def chunk_ids(ids, strips, strip_size):
+    n_ex = lax.axis_size("ex")
+    piece = -(-strip_size // n_ex)
+    strip, offset = ids // strip_size, ids % strip_size
+    return ((offset // piece) * strips + strip) * piece + offset % piece, n_ex * strips * piece
 
 
 def strip_reduce(partial, strips, strip_size):
     n_ex = lax.axis_size("ex")
     piece = -(-strip_size // n_ex)
-    chunks = partial.reshape(2, strips, strip_size)
-    if piece * n_ex != strip_size:
-        chunks = jnp.pad(chunks, ((0, 0), (0, 0), (0, piece * n_ex - strip_size)))
-    chunks = chunks.reshape(2, strips, n_ex, piece).transpose(2, 1, 0, 3)
-    chunks = chunks.reshape(n_ex * strips, 2, piece)
-    return lax.all_to_all(chunks, ("ex", "ey"), 0, 0, tiled=True).sum(0)
+    chunks = partial.reshape(2, n_ex * strips, piece)
+    if piece % 128:
+        chunks = chunks.transpose(1, 0, 2)
+        return lax.all_to_all(chunks, ("ex", "ey"), 0, 0, tiled=True).sum(0)
+    return lax.all_to_all(chunks, ("ex", "ey"), 1, 1, tiled=True).sum(1)
 
 
 def strip_gather(mine, strip_size):
@@ -206,8 +212,9 @@
     picks = fac_point[0]
     areas = fac_area[0]
     strips = lax.axis_size("ey")
-    global_ids = fac_strip[0, :, 0] * SHELL_STRIP + fac_shell[0]
-    denom = segment_sum(areas, global_ids, strips * SHELL_STRIP, 256)
+    global_ids, bins = chunk_ids(fac_strip[0, :, 0] * SHELL_STRIP + fac_shell[0], strips, SHELL_STRIP)
+    lanes = 128 * int(np.ceil(np.sqrt(bins) / 128))
+    denom = segment_sum(areas, global_ids, bins, lanes)
     for step in range(SWEEPS):
         pressure = pressure + update
         if step + 2 == SWEEPS:
@@ -215,7 +222,7 @@
         applied = element_apply(update, metric, weights, stiff)
         if step + 1 == SWEEPS:
             samples = early + gather_flat(update.reshape(-1), picks, 256, 2)
-            numer = segment_sum(areas * samples, global_ids, strips * SHELL_STRIP, 256, 2)
+            numer = segment_sum(areas * samples, global_ids, bins, lanes, 2)
             partial = jnp.stack([numer, denom])
             assembled, mine = assemble(applied[None], strip_reduce(partial, strips, SHELL_STRIP))
         else:

time: 139 us -> 139 us (level)
  other arithmetic: 14.5 us -> 16 us
where the time goes in v14:
time: 139 us; the launch traced here: 138 us
  starting transfers between devices  53.7 us (39%)
  waiting for transfers between devices  50.5 us (36%)
  other arithmetic  16 us (12%)
  matrix products  12 us (9%)
  local copies, waits for them, and re-layouts  4.28 us (3%)
  between operations  1.57 us (1%)
    ppermute x10, starting transfers between devices, padded_2(): lax.ppermute(lax.slice_in_dim(block, block.shape[dim] - width, None, axis...  28.5 us
    ppermute x10, waiting for transfers between devices, padded_2(): lax.ppermute(lax.slice_in_dim(block, 0, width, axis=dim), axis, backward)  25.8 us
    ppermute x10, starting transfers between devices, padded_2(): lax.ppermute(lax.slice_in_dim(block, 0, width, axis=dim), axis, backward)  16.9 us
    ppermute x10, waiting for transfers between devices, padded_2(): lax.ppermute(lax.slice_in_dim(block, block.shape[dim] - width, None, axis...  13.8 us
    all_to_all x1, waiting for transfers between devices, strip_gather(): whole = lax.all_to_all(spread_out, 'ex', 0, 0, tiled=True)  6.78 us
    all_to_all x1, starting transfers between devices, strip_reduce(): return lax.all_to_all(chunks, ('ex', 'ey'), 1, 1, tiled=True).sum(1)  4.83 us
    all_to_all x1, waiting for transfers between devices, strip_reduce(): return lax.all_to_all(chunks, ('ex', 'ey'), 1, 1, tiled=True).sum(1)  4.09 us
    all_to_all x1, starting transfers between devices, strip_gather(): whole = lax.all_to_all(spread_out, 'ex', 0, 0, tiled=True)  3.45 us
  transfers between devices with their start and end apart: 22, of which 20 were waited for; matrix products, arithmetic and copies ran while one was open for 9% of the time, Pallas kernels for 0%

profile of v14, /device:TPU:2, one launch (start us, length us, event | category | flops | bytes accessed | tf_op | source)
XLA Modules:
  0.0 138.2 jit_solution(3523959770182121492)
XLA Ops:
  2.9 1.2 fusion.90
  4.9 3.4 %collective-permute-start = (f32[2,1,1,8,8,128]{5,0,4,3,2,1:T(2,128)S(1)}, f32[2,1,1,8,8,128]{5,0,4,3,2,1:T(2,128)S(1)}, u32[]{:S(2)}, u32[]{:S(2)}) collective-permute-start(f32[2,1,1,8,8,128]{5,0,4,3,2,1:T(2,128)S(1)} %maximum_bitcast_fusion.8), channel_id=1, source_target_pairs={{0,4},{4,8},{8,12},{12,16},{16,20},{20,24},{24,28},{1,5},{5,9},{9,... | collective-permute-start | bytes 196616 | tf_op jit(solution)/shard_map/ppermute | solution.py:16
  9.2 1.1 and_select_fusion.2
  10.3 1.2 fusion.20
  11.6 1.3 collective-permute-start.1
  13.5 4.3 %collective-permute-done.1 = f32[2,1,1,8,8,128]{5,0,4,3,2,1:T(2,128)S(1)} collective-permute-done((f32[2,1,1,8,8,128]{5,0,4,3,2,1:T(2,128)S(1)}, f32[2,1,1,8,8,128]{5,0,4,3,2,1:T(2,128)S(1)}, u32[]{:S(2)}, u32[]{:S(2)}) %collective-permute-start.1) | collective-permute-done | bytes 65568 | tf_op jit(solution)/shard_map/ppermute | solution.py:19
  17.8 1.9 %collective-permute-start.2 = (f32[2,1,1,8,8,128]{5,3,0,4,2,1:T(8,128)S(1)}, f32[2,1,1,8,8,128]{5,3,0,4,2,1:T(8,128)S(1)}, u32[]{:S(2)}, u32[]{:S(2)}) collective-permute-start(f32[2,1,1,8,8,128]{5,3,0,4,2,1:T(8,128)S(1)} %maximum_bitcast_fusion.6), channel_id=1, source_target_pairs={{0,1},{1,2},{2,3},{4,5},{5,6},{6,7},{8,9},{9,10},{10,11},{12,13},{... | collective-permute-start | bytes 196616 | tf_op jit(solution)/shard_map/ppermute | solution.py:16
  19.8 3.6 %collective-permute-done.2 = f32[2,1,1,8,8,128]{5,3,0,4,2,1:T(8,128)S(1)} collective-permute-done((f32[2,1,1,8,8,128]{5,3,0,4,2,1:T(8,128)S(1)}, f32[2,1,1,8,8,128]{5,3,0,4,2,1:T(8,128)S(1)}, u32[]{:S(2)}, u32[]{:S(2)}) %collective-permute-start.2) | collective-permute-done | bytes 65568 | tf_op jit(solution)/shard_map/ppermute | solution.py:16
  23.5 1.9 %collective-permute-start.3 = (f32[2,1,1,8,8,128]{5,3,0,4,2,1:T(8,128)S(1)}, f32[2,1,1,8,8,128]{5,3,0,4,2,1:T(8,128)S(1)}, u32[]{:S(2)}, u32[]{:S(2)}) collective-permute-start(f32[2,1,1,8,8,128]{5,3,0,4,2,1:T(8,128)S(1)} %get-tuple-element.43), channel_id=1, source_target_pairs={{1,0},{2,1},{3,2},{5,4},{6,5},{7,6},{9,8},{10,9},{11,10},{13,12},{... | collective-permute-start | bytes 196616 | tf_op jit(solution)/shard_map/ppermute | solution.py:19
  25.8 1.5 %collective-permute-done.3 = f32[2,1,1,8,8,128]{5,3,0,4,2,1:T(8,128)S(1)} collective-permute-done((f32[2,1,1,8,8,128]{5,3,0,4,2,1:T(8,128)S(1)}, f32[2,1,1,8,8,128]{5,3,0,4,2,1:T(8,128)S(1)}, u32[]{:S(2)}, u32[]{:S(2)}) %collective-permute-start.3) | collective-permute-done | bytes 65568 | tf_op jit(solution)/shard_map/ppermute | solution.py:19
  29.0 0.9 fusion.30
  30.0 4.3 %collective-permute-start.4 = (f32[1,1,1,8,8,128]{5,4,3,2,1,0:T(8,128)S(1)}, f32[1,1,1,8,8,128]{5,4,3,2,1,0:T(8,128)S(1)}, u32[]{:S(2)}, u32[]{:S(2)}) collective-permute-start(f32[1,1,1,8,8,128]{5,4,3,2,1,0:T(8,128)S(1)} %bitcast.487), channel_id=1, source_target_pairs={{0,4},{4,8},{8,12},{12,16},{16,20},{20,24},{24,28},{1,5},{5,9},{9,... | collective-permute-start | bytes 98312 | tf_op jit(solution)/shard_map/ppermute | solution.py:16
  34.3 1.3 collective-permute-start.5
  35.9 4.2 %collective-permute-done.5 = f32[1,1,1,8,8,128]{5,4,3,2,1,0:T(8,128)S(1)} collective-permute-done((f32[1,1,1,8,8,128]{5,4,3,2,1,0:T(8,128)S(1)}, f32[1,1,1,8,8,128]{5,4,3,2,1,0:T(8,128)S(1)}, u32[]{:S(2)}, u32[]{:S(2)}) %collective-permute-start.5) | collective-permute-done | bytes 32800 | tf_op jit(solution)/shard_map/ppermute | solution.py:19
  40.2 1.9 %collective-permute-start.6 = (f32[1,1,1,8,8,128]{5,3,4,2,1,0:T(8,128)S(1)}, f32[1,1,1,8,8,128]{5,3,4,2,1,0:T(8,128)S(1)}, u32[]{:S(2)}, u32[]{:S(2)}) collective-permute-start(f32[1,1,1,8,8,128]{5,3,4,2,1,0:T(8,128)S(1)} %maximum_bitcast_fusion.18), channel_id=1, source_target_pairs={{0,1},{1,2},{2,3},{4,5},{5,6},{6,7},{8,9},{9,10},{10,11},{12,13},{... | collective-permute-start | bytes 98312 | tf_op jit(solution)/shard_map/ppermute | solution.py:16
  42.1 1.9 %fusion = f32[768,256]{1,0:T(8,128)S(1)} fusion(bf16[256,4096]{1,0:T(8,128)(2,1)S(1)} %get-tuple-element.80, bf16[256,4096]{1,0:T(8,128)(2,1)S(1)} %get-tuple-element.81, bf16[256,4096]{1,0:T(8,128)(2,1)S(1)} %get-tuple-element.79, s32[4096]{0:T(1024)S(1)} %add_select_fusion), kind=kOutput, calls=%fused_computation | convolution fusion | flops 1630535680 | bytes 7094272 | tf_op jit(solution)/shard_map/dot_general | solution.py:167
  44.0 1.4 collective-permute-done.6
  45.4 2.3 %collective-permute-start.7 = (f32[1,1,1,8,8,128]{5,3,4,2,1,0:T(8,128)S(1)}, f32[1,1,1,8,8,128]{5,3,4,2,1,0:T(8,128)S(1)}, u32[]{:S(2)}, u32[]{:S(2)}) collective-permute-start(f32[1,1,1,8,8,128]{5,3,4,2,1,0:T(8,128)S(1)} %get-tuple-element.39), channel_id=1, source_target_pairs={{1,0},{2,1},{3,2},{5,4},{6,5},{7,6},{9,8},{10,9},{11,10},{13,12},{... | collective-permute-start | bytes 98312 | tf_op jit(solution)/shard_map/ppermute | solution.py:19
  47.9 1.4 collective-permute-done.7
  51.2 3.9 %collective-permute-start.8 = (f32[1,1,1,8,8,128]{5,4,3,2,1,0:T(8,128)S(1)}, f32[1,1,1,8,8,128]{5,4,3,2,1,0:T(8,128)S(1)}, u32[]{:S(2)}, u32[]{:S(2)}) collective-permute-start(f32[1,1,1,8,8,128]{5,4,3,2,1,0:T(8,128)S(1)} %get-tuple-element.67), channel_id=1, source_target_pairs={{0,4},{4,8},{8,12},{12,16},{16,20},{20,24},{24,28},{1,5},{5,9},{9,... | collective-permute-start | bytes 98312 | tf_op jit(solution)/shard_map/ppermute | solution.py:16
  55.1 1.3 collective-permute-start.9
  56.7 4.2 %collective-permute-done.9 = f32[1,1,1,8,8,128]{5,4,3,2,1,0:T(8,128)S(1)} collective-permute-done((f32[1,1,1,8,8,128]{5,4,3,2,1,0:T(8,128)S(1)}, f32[1,1,1,8,8,128]{5,4,3,2,1,0:T(8,128)S(1)}, u32[]{:S(2)}, u32[]{:S(2)}) %collective-permute-start.9) | collective-permute-done | bytes 32800 | tf_op jit(solution)/shard_map/ppermute | solution.py:19
  60.9 1.9 %collective-permute-start.10 = (f32[1,1,1,8,8,128]{5,4,3,2,1,0:T(8,128)S(1)}, f32[1,1,1,8,8,128]{5,4,3,2,1,0:T(8,128)S(1)}, u32[]{:S(2)}, u32[]{:S(2)}) collective-permute-start(f32[1,1,1,8,8,128]{5,4,3,2,1,0:T(8,128)S(1)} %maximum_bitcast_fusion.16), channel_id=1, source_target_pairs={{0,1},{1,2},{2,3},{4,5},{5,6},{6,7},{8,9},{9,10},{10,11},{12,13},{... | collective-permute-start | bytes 98312 | tf_op jit(solution)/shard_map/ppermute | solution.py:16
  62.9 3.2 %collective-permute-done.10 = f32[1,1,1,8,8,128]{5,4,3,2,1,0:T(8,128)S(1)} collective-permute-done((f32[1,1,1,8,8,128]{5,4,3,2,1,0:T(8,128)S(1)}, f32[1,1,1,8,8,128]{5,4,3,2,1,0:T(8,128)S(1)}, u32[]{:S(2)}, u32[]{:S(2)}) %collective-permute-start.10) | collective-permute-done | bytes 32800 | tf_op jit(solution)/shard_map/ppermute | solution.py:16
  66.2 2.1 %collective-permute-start.11 = (f32[1,1,1,8,8,128]{5,4,3,2,1,0:T(8,128)S(1)}, f32[1,1,1,8,8,128]{5,4,3,2,1,0:T(8,128)S(1)}, u32[]{:S(2)}, u32[]{:S(2)}) collective-permute-start(f32[1,1,1,8,8,128]{5,4,3,2,1,0:T(8,128)S(1)} %get-tuple-element.37), channel_id=1, source_target_pairs={{1,0},{2,1},{3,2},{5,4},{6,5},{7,6},{9,8},{10,9},{11,10},{13,12},{... | collective-permute-start | bytes 98312 | tf_op jit(solution)/shard_map/ppermute | solution.py:19
  68.4 1.3 collective-permute-done.11
  71.8 3.9 %collective-permute-start.12 = (f32[1,1,1,8,8,128]{5,4,3,2,1,0:T(8,128)S(1)}, f32[1,1,1,8,8,128]{5,4,3,2,1,0:T(8,128)S(1)}, u32[]{:S(2)}, u32[]{:S(2)}) collective-permute-start(f32[1,1,1,8,8,128]{5,4,3,2,1,0:T(8,128)S(1)} %get-tuple-element.61), channel_id=1, source_target_pairs={{0,4},{4,8},{8,12},{12,16},{16,20},{20,24},{24,28},{1,5},{5,9},{9,... | collective-permute-start | bytes 98312 | tf_op jit(solution)/shard_map/ppermute | solution.py:16
  75.7 1.3 collective-permute-start.13
  77.2 4.2 %collective-permute-done.13 = f32[1,1,1,8,8,128]{5,4,3,2,1,0:T(8,128)S(1)} collective-permute-done((f32[1,1,1,8,8,128]{5,4,3,2,1,0:T(8,128)S(1)}, f32[1,1,1,8,8,128]{5,4,3,2,1,0:T(8,128)S(1)}, u32[]{:S(2)}, u32[]{:S(2)}) %collective-permute-start.13) | collective-permute-done | bytes 32800 | tf_op jit(solution)/shard_map/ppermute | solution.py:19
  81.5 1.9 %collective-permute-start.14 = (f32[1,1,1,8,8,128]{5,4,3,2,1,0:T(8,128)S(1)}, f32[1,1,1,8,8,128]{5,4,3,2,1,0:T(8,128)S(1)}, u32[]{:S(2)}, u32[]{:S(2)}) collective-permute-start(f32[1,1,1,8,8,128]{5,4,3,2,1,0:T(8,128)S(1)} %maximum_bitcast_fusion.14), channel_id=1, source_target_pairs={{0,1},{1,2},{2,3},{4,5},{5,6},{6,7},{8,9},{9,10},{10,11},{12,13},{... | collective-permute-start | bytes 98312 | tf_op jit(solution)/shard_map/ppermute | solution.py:16
  83.4 1.9 %fusion.15 = f32[768,4096]{1,0:T(8,128)S(1)} fusion(s32[4096]{0:T(1024)S(1)} %bitcast.481, bf16[256,256]{1,0:T(8,128)(2,1)S(1)} %get-tuple-element.55, bf16[256,256]{1,0:T(8,128)(2,1)S(1)} %get-tuple-element.56, bf16[256,256]{1,0:T(8,128)(2,1)S(1)} %get-tuple-element.54), kind=kOutput, calls=%fused_computation.19 | convolution fusion | flops 1612840960 | bytes 12992512 | tf_op jit(solution)/shard_map/dot_general | solution.py:153
  85.3 1.4 %collective-permute-done.14 = f32[1,1,1,8,8,128]{5,4,3,2,1,0:T(8,128)S(1)} collective-permute-done((f32[1,1,1,8,8,128]{5,4,3,2,1,0:T(8,128)S(1)}, f32[1,1,1,8,8,128]{5,4,3,2,1,0:T(8,128)S(1)}, u32[]{:S(2)}, u32[]{:S(2)}) %collective-permute-start.14) | collective-permute-done | bytes 32800 | tf_op jit(solution)/shard_map/ppermute | solution.py:16
  86.7 2.2 %collective-permute-start.15 = (f32[1,1,1,8,8,128]{5,4,3,2,1,0:T(8,128)S(1)}, f32[1,1,1,8,8,128]{5,4,3,2,1,0:T(8,128)S(1)}, u32[]{:S(2)}, u32[]{:S(2)}) collective-permute-start(f32[1,1,1,8,8,128]{5,4,3,2,1,0:T(8,128)S(1)} %get-tuple-element.33), channel_id=1, source_target_pairs={{1,0},{2,1},{3,2},{5,4},{6,5},{7,6},{9,8},{10,9},{11,10},{13,12},{... | collective-permute-start | bytes 98312 | tf_op jit(solution)/shard_map/ppermute | solution.py:19
  89.0 1.4 fusion.9
  92.0 1.3 fusion.14
  93.4 0.9 fusion.7
  95.2 1.4 %fusion.10 = f32[512,256]{1,0:T(8,128)S(1)} fusion(bf16[256,4096]{1,0:T(8,128)(2,1)S(1)} %get-tuple-element.78, bf16[256,4096]{1,0:T(8,128)(2,1)S(1)} %get-tuple-element.77, s32[4096]{0:T(1024)S(1)} %add_select_fusion), kind=kOutput, calls=%fused_computation.13 | convolution fusion | flops 1083179008 | bytes 4734976 | tf_op jit(solution)/shard_map/dot_general | solution.py:167
  97.0 1.3 pad_maximum_fusion.1
  98.2 4.8 %all-to-all-start = ((f32[2,32,2048]{2,0,1:T(2,128)}), f32[2,32,2048]{2,0,1:T(2,128)S(1)}, u32[]{:S(2)}, u32[]{:S(2)}) async-start(f32[2,32,2048]{2,0,1:T(2,128)} %pad_maximum_fusion.1), calls=%async_computation | async-start | bytes 1048576 | tf_op jit(solution)/shard_map/all_to_all | solution.py:188
  104.4 3.4 %collective-permute-start.16 = (f32[1,1,1,8,8,128]{5,4,3,2,1,0:T(8,128)S(1)}, f32[1,1,1,8,8,128]{5,4,3,2,1,0:T(8,128)S(1)}, u32[]{:S(2)}, u32[]{:S(2)}) collective-permute-start(f32[1,1,1,8,8,128]{5,4,3,2,1,0:T(8,128)S(1)} %get-tuple-element.52), channel_id=1, source_target_pairs={{0,4},{4,8},{8,12},{12,16},{16,20},{20,24},{24,28},{1,5},{5,9},{9,... | collective-permute-start | bytes 98312 | tf_op jit(solution)/shard_map/ppermute | solution.py:16
  107.8 1.3 collective-permute-start.17
  109.5 4.5 %collective-permute-done.17 = f32[1,1,1,8,8,128]{5,4,3,2,1,0:T(8,128)S(1)} collective-permute-done((f32[1,1,1,8,8,128]{5,4,3,2,1,0:T(8,128)S(1)}, f32[1,1,1,8,8,128]{5,4,3,2,1,0:T(8,128)S(1)}, u32[]{:S(2)}, u32[]{:S(2)}) %collective-permute-start.17) | collective-permute-done | bytes 32800 | tf_op jit(solution)/shard_map/ppermute | solution.py:19
  114.0 4.1 %all-to-all-done = f32[2,32,2048]{2,0,1:T(2,128)S(1)} async-done(((f32[2,32,2048]{2,0,1:T(2,128)}), f32[2,32,2048]{2,0,1:T(2,128)S(1)}, u32[]{:S(2)}, u32[]{:S(2)}) %all-to-all-start) | async-done | bytes 524320 | tf_op jit(solution)/shard_map/all_to_all | solution.py:188
  118.3 2.0 %collective-permute-start.18 = (f32[1,1,1,8,8,128]{5,3,4,2,1,0:T(8,128)S(1)}, f32[1,1,1,8,8,128]{5,3,4,2,1,0:T(8,128)S(1)}, u32[]{:S(2)}, u32[]{:S(2)}) collective-permute-start(f32[1,1,1,8,8,128]{5,3,4,2,1,0:T(8,128)S(1)} %maximum_bitcast_fusion.12), channel_id=1, source_target_pairs={{0,1},{1,2},{2,3},{4,5},{5,6},{6,7},{8,9},{9,10},{10,11},{12,13},{... | collective-permute-start | bytes 98312 | tf_op jit(solution)/shard_map/ppermute | solution.py:16
  120.3 3.3 %collective-permute-done.18 = f32[1,1,1,8,8,128]{5,3,4,2,1,0:T(8,128)S(1)} collective-permute-done((f32[1,1,1,8,8,128]{5,3,4,2,1,0:T(8,128)S(1)}, f32[1,1,1,8,8,128]{5,3,4,2,1,0:T(8,128)S(1)}, u32[]{:S(2)}, u32[]{:S(2)}) %collective-permute-start.18) | collective-permute-done | bytes 32800 | tf_op jit(solution)/shard_map/ppermute | solution.py:16
  123.6 1.9 %collective-permute-start.19 = (f32[1,1,1,8,8,128]{5,3,4,2,1,0:T(8,128)S(1)}, f32[1,1,1,8,8,128]{5,3,4,2,1,0:T(8,128)S(1)}, u32[]{:S(2)}, u32[]{:S(2)}) collective-permute-start(f32[1,1,1,8,8,128]{5,3,4,2,1,0:T(8,128)S(1)} %get-tuple-element.27), channel_id=1, source_target_pairs={{1,0},{2,1},{3,2},{5,4},{6,5},{7,6},{9,8},{10,9},{11,10},{13,12},{... | collective-permute-start | bytes 98312 | tf_op jit(solution)/shard_map/ppermute | solution.py:19
  126.2 3.4 %all-to-all-start.1 = ((f32[8,2,2048]{2,1,0:T(2,128)}), f32[8,2,2048]{2,1,0:T(2,128)S(1)}, u32[]{:S(2)}, u32[]{:S(2)}) async-start(f32[8,2,2048]{2,1,0:T(2,128)} %broadcast_in_dim.213), calls=%async_computation.1 | async-start | bytes 262144 | tf_op jit(solution)/shard_map/all_to_all | solution.py:195
  130.7 6.8 %all-to-all-done.1 = f32[8,2,2048]{2,1,0:T(2,128)S(1)} async-done(((f32[8,2,2048]{2,1,0:T(2,128)}), f32[8,2,2048]{2,1,0:T(2,128)S(1)}, u32[]{:S(2)}, u32[]{:S(2)}) %all-to-all-start.1) | async-done | bytes 131104 | tf_op jit(solution)/shard_map/all_to_all | solution.py:195
  (133 shorter events, 19.1 us)
Async XLA Ops:
  0.6 10.9 %copy-start = (f32[1,1,8,8,8,128]{5,4,3,2,1,0:T(8,128)S(1)}, f32[1,1,8,8,8,128]{5,4,3,2,1,0:T(8,128)}, u32[]{:S(2)}) copy-start(f32[1,1,8,8,8,128]{5,4,3,2,1,0:T(8,128)} %param.36) | copy-start | bytes 786436
  4.9 6.6 %collective-permute-start = (f32[2,1,1,8,8,128]{5,0,4,3,2,1:T(2,128)S(1)}, f32[2,1,1,8,8,128]{5,0,4,3,2,1:T(2,128)S(1)}, u32[]{:S(2)}, u32[]{:S(2)}) collective-permute-start(f32[2,1,1,8,8,128]{5,0,4,3,2,1:T(2,128)S(1)} %maximum_bitcast_fusion.8), channel_id=1, source_target_pairs={{0,4},{4,8},{8,12},{12,16},{16,20},{20,24},{24,28},{1,5},{5,9},{9,... | collective-permute-start | bytes 196616 | tf_op jit(solution)/shard_map/ppermute | solution.py:16
  10.2 9.5 %copy-start.4 = (s32[1,4096,1]{1,2,0:T(1,128)S(1)}, s32[1,4096,1]{1,2,0:T(1,128)}, u32[]{:S(2)}) copy-start(s32[1,4096,1]{1,2,0:T(1,128)} %param.39) | copy-start | bytes 49156
  11.6 6.2 %collective-permute-start.1 = (f32[2,1,1,8,8,128]{5,0,4,3,2,1:T(2,128)S(1)}, f32[2,1,1,8,8,128]{5,0,4,3,2,1:T(2,128)S(1)}, u32[]{:S(2)}, u32[]{:S(2)}) collective-permute-start(f32[2,1,1,8,8,128]{5,0,4,3,2,1:T(2,128)S(1)} %get-tuple-element.45), channel_id=1, source_target_pairs={{4,0},{8,4},{12,8},{16,12},{20,16},{24,20},{28,24},{5,1},{9,5},{13... | collective-permute-start | bytes 196616 | tf_op jit(solution)/shard_map/ppermute | solution.py:19
  17.8 5.6 %collective-permute-start.2 = (f32[2,1,1,8,8,128]{5,3,0,4,2,1:T(8,128)S(1)}, f32[2,1,1,8,8,128]{5,3,0,4,2,1:T(8,128)S(1)}, u32[]{:S(2)}, u32[]{:S(2)}) collective-permute-start(f32[2,1,1,8,8,128]{5,3,0,4,2,1:T(8,128)S(1)} %maximum_bitcast_fusion.6), channel_id=1, source_target_pairs={{0,1},{1,2},{2,3},{4,5},{5,6},{6,7},{8,9},{9,10},{10,11},{12,13},{... | collective-permute-start | bytes 196616 | tf_op jit(solution)/shard_map/ppermute | solution.py:16
  23.4 4.7 %copy-start.1 = (f32[8,8,1,1]{1,0,3,2:T(8,128)S(1)}, f32[8,8,1,1]{1,0,3,2:T(8,128)}, u32[]{:S(2)}) copy-start(f32[8,8,1,1]{1,0,3,2:T(8,128)} %constant.176) | copy-start | bytes 772
  23.5 3.8 %collective-permute-start.3 = (f32[2,1,1,8,8,128]{5,3,0,4,2,1:T(8,128)S(1)}, f32[2,1,1,8,8,128]{5,3,0,4,2,1:T(8,128)S(1)}, u32[]{:S(2)}, u32[]{:S(2)}) collective-permute-start(f32[2,1,1,8,8,128]{5,3,0,4,2,1:T(8,128)S(1)} %get-tuple-element.43), channel_id=1, source_target_pairs={{1,0},{2,1},{3,2},{5,4},{6,5},{7,6},{9,8},{10,9},{11,10},{13,12},{... | collective-permute-start | bytes 196616 | tf_op jit(solution)/shard_map/ppermute | solution.py:19
  25.5 3.4 %copy-start.6 = (f32[8]{0:T(128)S(1)}, f32[8]{0:T(128)}, u32[]{:S(2)}) copy-start(f32[8]{0:T(128)} %constant.171) | copy-start | bytes 100
  27.4 8.2 %copy-start.2 = (s32[1,4096]{1,0:T(1,128)S(1)}, s32[1,4096]{1,0:T(1,128)}, u32[]{:S(2)}) copy-start(s32[1,4096]{1,0:T(1,128)} %param.40) | copy-start | bytes 49156
  30.0 5.9 %collective-permute-start.4 = (f32[1,1,1,8,8,128]{5,4,3,2,1,0:T(8,128)S(1)}, f32[1,1,1,8,8,128]{5,4,3,2,1,0:T(8,128)S(1)}, u32[]{:S(2)}, u32[]{:S(2)}) collective-permute-start(f32[1,1,1,8,8,128]{5,4,3,2,1,0:T(8,128)S(1)} %bitcast.487), channel_id=1, source_target_pairs={{0,4},{4,8},{8,12},{12,16},{16,20},{20,24},{24,28},{1,5},{5,9},{9,... | collective-permute-start | bytes 98312 | tf_op jit(solution)/shard_map/ppermute | solution.py:16
  34.3 5.8 %collective-permute-start.5 = (f32[1,1,1,8,8,128]{5,4,3,2,1,0:T(8,128)S(1)}, f32[1,1,1,8,8,128]{5,4,3,2,1,0:T(8,128)S(1)}, u32[]{:S(2)}, u32[]{:S(2)}) collective-permute-start(f32[1,1,1,8,8,128]{5,4,3,2,1,0:T(8,128)S(1)} %bitcast.489), channel_id=1, source_target_pairs={{4,0},{8,4},{12,8},{16,12},{20,16},{24,20},{28,24},{5,1},{9,5},{13... | collective-permute-start | bytes 98312 | tf_op jit(solution)/shard_map/ppermute | solution.py:19
  40.2 5.2 %collective-permute-start.6 = (f32[1,1,1,8,8,128]{5,3,4,2,1,0:T(8,128)S(1)}, f32[1,1,1,8,8,128]{5,3,4,2,1,0:T(8,128)S(1)}, u32[]{:S(2)}, u32[]{:S(2)}) collective-permute-start(f32[1,1,1,8,8,128]{5,3,4,2,1,0:T(8,128)S(1)} %maximum_bitcast_fusion.18), channel_id=1, source_target_pairs={{0,1},{1,2},{2,3},{4,5},{5,6},{6,7},{8,9},{9,10},{10,11},{12,13},{... | collective-permute-start | bytes 98312 | tf_op jit(solution)/shard_map/ppermute | solution.py:16
  45.4 17.4 %copy-start.3 = (s32[1,4096]{1,0:T(1,128)S(1)}, s32[1,4096]{1,0:T(1,128)}, u32[]{:S(2)}) copy-start(s32[1,4096]{1,0:T(1,128)} %param.38) | copy-start | bytes 49156
  45.4 3.9 %collective-permute-start.7 = (f32[1,1,1,8,8,128]{5,3,4,2,1,0:T(8,128)S(1)}, f32[1,1,1,8,8,128]{5,3,4,2,1,0:T(8,128)S(1)}, u32[]{:S(2)}, u32[]{:S(2)}) collective-permute-start(f32[1,1,1,8,8,128]{5,3,4,2,1,0:T(8,128)S(1)} %get-tuple-element.39), channel_id=1, source_target_pairs={{1,0},{2,1},{3,2},{5,4},{6,5},{7,6},{9,8},{10,9},{11,10},{13,12},{... | collective-permute-start | bytes 98312 | tf_op jit(solution)/shard_map/ppermute | solution.py:19
  51.2 5.5 %collective-permute-start.8 = (f32[1,1,1,8,8,128]{5,4,3,2,1,0:T(8,128)S(1)}, f32[1,1,1,8,8,128]{5,4,3,2,1,0:T(8,128)S(1)}, u32[]{:S(2)}, u32[]{:S(2)}) collective-permute-start(f32[1,1,1,8,8,128]{5,4,3,2,1,0:T(8,128)S(1)} %get-tuple-element.67), channel_id=1, source_target_pairs={{0,4},{4,8},{8,12},{12,16},{16,20},{20,24},{24,28},{1,5},{5,9},{9,... | collective-permute-start | bytes 98312 | tf_op jit(solution)/shard_map/ppermute | solution.py:16
  55.1 5.8 %collective-permute-start.9 = (f32[1,1,1,8,8,128]{5,4,3,2,1,0:T(8,128)S(1)}, f32[1,1,1,8,8,128]{5,4,3,2,1,0:T(8,128)S(1)}, u32[]{:S(2)}, u32[]{:S(2)}) collective-permute-start(f32[1,1,1,8,8,128]{5,4,3,2,1,0:T(8,128)S(1)} %get-tuple-element.68), channel_id=1, source_target_pairs={{4,0},{8,4},{12,8},{16,12},{20,16},{24,20},{28,24},{5,1},{9,5},{13... | collective-permute-start | bytes 98312 | tf_op jit(solution)/shard_map/ppermute | solution.py:19
  60.9 5.2 %collective-permute-start.10 = (f32[1,1,1,8,8,128]{5,4,3,2,1,0:T(8,128)S(1)}, f32[1,1,1,8,8,128]{5,4,3,2,1,0:T(8,128)S(1)}, u32[]{:S(2)}, u32[]{:S(2)}) collective-permute-start(f32[1,1,1,8,8,128]{5,4,3,2,1,0:T(8,128)S(1)} %maximum_bitcast_fusion.16), channel_id=1, source_target_pairs={{0,1},{1,2},{2,3},{4,5},{5,6},{6,7},{8,9},{9,10},{10,11},{12,13},{... | collective-permute-start | bytes 98312 | tf_op jit(solution)/shard_map/ppermute | solution.py:16
  66.2 3.5 %collective-permute-start.11 = (f32[1,1,1,8,8,128]{5,4,3,2,1,0:T(8,128)S(1)}, f32[1,1,1,8,8,128]{5,4,3,2,1,0:T(8,128)S(1)}, u32[]{:S(2)}, u32[]{:S(2)}) collective-permute-start(f32[1,1,1,8,8,128]{5,4,3,2,1,0:T(8,128)S(1)} %get-tuple-element.37), channel_id=1, source_target_pairs={{1,0},{2,1},{3,2},{5,4},{6,5},{7,6},{9,8},{10,9},{11,10},{13,12},{... | collective-permute-start | bytes 98312 | tf_op jit(solution)/shard_map/ppermute | solution.py:19
  71.8 5.5 %collective-permute-start.12 = (f32[1,1,1,8,8,128]{5,4,3,2,1,0:T(8,128)S(1)}, f32[1,1,1,8,8,128]{5,4,3,2,1,0:T(8,128)S(1)}, u32[]{:S(2)}, u32[]{:S(2)}) collective-permute-start(f32[1,1,1,8,8,128]{5,4,3,2,1,0:T(8,128)S(1)} %get-tuple-element.61), channel_id=1, source_target_pairs={{0,4},{4,8},{8,12},{12,16},{16,20},{20,24},{24,28},{1,5},{5,9},{9,... | collective-permute-start | bytes 98312 | tf_op jit(solution)/shard_map/ppermute | solution.py:16
  75.7 5.8 %collective-permute-start.13 = (f32[1,1,1,8,8,128]{5,4,3,2,1,0:T(8,128)S(1)}, f32[1,1,1,8,8,128]{5,4,3,2,1,0:T(8,128)S(1)}, u32[]{:S(2)}, u32[]{:S(2)}) collective-permute-start(f32[1,1,1,8,8,128]{5,4,3,2,1,0:T(8,128)S(1)} %get-tuple-element.62), channel_id=1, source_target_pairs={{4,0},{8,4},{12,8},{16,12},{20,16},{24,20},{28,24},{5,1},{9,5},{13... | collective-permute-start | bytes 98312 | tf_op jit(solution)/shard_map/ppermute | solution.py:19
  81.5 5.2 %collective-permute-start.14 = (f32[1,1,1,8,8,128]{5,4,3,2,1,0:T(8,128)S(1)}, f32[1,1,1,8,8,128]{5,4,3,2,1,0:T(8,128)S(1)}, u32[]{:S(2)}, u32[]{:S(2)}) collective-permute-start(f32[1,1,1,8,8,128]{5,4,3,2,1,0:T(8,128)S(1)} %maximum_bitcast_fusion.14), channel_id=1, source_target_pairs={{0,1},{1,2},{2,3},{4,5},{5,6},{6,7},{8,9},{9,10},{10,11},{12,13},{... | collective-permute-start | bytes 98312 | tf_op jit(solution)/shard_map/ppermute | solution.py:16
  86.7 3.8 %collective-permute-start.15 = (f32[1,1,1,8,8,128]{5,4,3,2,1,0:T(8,128)S(1)}, f32[1,1,1,8,8,128]{5,4,3,2,1,0:T(8,128)S(1)}, u32[]{:S(2)}, u32[]{:S(2)}) collective-permute-start(f32[1,1,1,8,8,128]{5,4,3,2,1,0:T(8,128)S(1)} %get-tuple-element.33), channel_id=1, source_target_pairs={{1,0},{2,1},{3,2},{5,4},{6,5},{7,6},{9,8},{10,9},{11,10},{13,12},{... | collective-permute-start | bytes 98312 | tf_op jit(solution)/shard_map/ppermute | solution.py:19
  93.4 0.9 copy-start.5
  98.2 19.9 %all-to-all-start = ((f32[2,32,2048]{2,0,1:T(2,128)}), f32[2,32,2048]{2,0,1:T(2,128)S(1)}, u32[]{:S(2)}, u32[]{:S(2)}) async-start(f32[2,32,2048]{2,0,1:T(2,128)} %pad_maximum_fusion.1), calls=%async_computation | async-start | bytes 1048576 | tf_op jit(solution)/shard_map/all_to_all | solution.py:188
  104.4 5.1 %collective-permute-start.16 = (f32[1,1,1,8,8,128]{5,4,3,2,1,0:T(8,128)S(1)}, f32[1,1,1,8,8,128]{5,4,3,2,1,0:T(8,128)S(1)}, u32[]{:S(2)}, u32[]{:S(2)}) collective-permute-start(f32[1,1,1,8,8,128]{5,4,3,2,1,0:T(8,128)S(1)} %get-tuple-element.52), channel_id=1, source_target_pairs={{0,4},{4,8},{8,12},{12,16},{16,20},{20,24},{24,28},{1,5},{5,9},{9,... | collective-permute-start | bytes 98312 | tf_op jit(solution)/shard_map/ppermute | solution.py:16
  107.8 6.2 %collective-permute-start.17 = (f32[1,1,1,8,8,128]{5,4,3,2,1,0:T(8,128)S(1)}, f32[1,1,1,8,8,128]{5,4,3,2,1,0:T(8,128)S(1)}, u32[]{:S(2)}, u32[]{:S(2)}) collective-permute-start(f32[1,1,1,8,8,128]{5,4,3,2,1,0:T(8,128)S(1)} %get-tuple-element.53), channel_id=1, source_target_pairs={{4,0},{8,4},{12,8},{16,12},{20,16},{24,20},{28,24},{5,1},{9,5},{13... | collective-permute-start | bytes 98312 | tf_op jit(solution)/shard_map/ppermute | solution.py:19
  118.3 5.2 %collective-permute-start.18 = (f32[1,1,1,8,8,128]{5,3,4,2,1,0:T(8,128)S(1)}, f32[1,1,1,8,8,128]{5,3,4,2,1,0:T(8,128)S(1)}, u32[]{:S(2)}, u32[]{:S(2)}) collective-permute-start(f32[1,1,1,8,8,128]{5,3,4,2,1,0:T(8,128)S(1)} %maximum_bitcast_fusion.12), channel_id=1, source_target_pairs={{0,1},{1,2},{2,3},{4,5},{5,6},{6,7},{8,9},{9,10},{10,11},{12,13},{... | collective-permute-start | bytes 98312 | tf_op jit(solution)/shard_map/ppermute | solution.py:16
  123.6 6.1 %collective-permute-start.19 = (f32[1,1,1,8,8,128]{5,3,4,2,1,0:T(8,128)S(1)}, f32[1,1,1,8,8,128]{5,3,4,2,1,0:T(8,128)S(1)}, u32[]{:S(2)}, u32[]{:S(2)}) collective-permute-start(f32[1,1,1,8,8,128]{5,3,4,2,1,0:T(8,128)S(1)} %get-tuple-element.27), channel_id=1, source_target_pairs={{1,0},{2,1},{3,2},{5,4},{6,5},{7,6},{9,8},{10,9},{11,10},{13,12},{... | collective-permute-start | bytes 98312 | tf_op jit(solution)/shard_map/ppermute | solution.py:19
  126.2 11.2 %all-to-all-start.1 = ((f32[8,2,2048]{2,1,0:T(2,128)}), f32[8,2,2048]{2,1,0:T(2,128)S(1)}, u32[]{:S(2)}, u32[]{:S(2)}) async-start(f32[8,2,2048]{2,1,0:T(2,128)} %broadcast_in_dim.213), calls=%async_computation.1 | async-start | bytes 262144 | tf_op jit(solution)/shard_map/all_to_all | solution.py:195

commit v15 on v12

--- a/solution.py
+++ b/solution.py
@@ -72,6 +72,27 @@
     )
 
 
+def x_faces_apply(values_in, metric, weights, stiff):
+    top = lax.Precision.HIGHEST
+    last = values_in.shape[2] - 1
+    weight_j = weights[None, None, :, None, None]
+    weight_k = weights[None, None, None, :, None]
+    out = []
+    for edge in (0, last):
+        plane = values_in[:, :, edge]
+        along_x = jnp.einsum("m,abmjkc->abjkc", stiff[edge], values_in, precision=top)
+        along_y = jnp.einsum("jm,abmkc->abjkc", stiff, plane, precision=top)
+        along_z = jnp.einsum("km,abjmc->abjkc", stiff, plane, precision=top)
+        weight_i = weights[edge]
+        out.append(
+            metric[0][:, :, None, None, :] * weight_j * weight_k * along_x
+            + metric[1][:, :, None, None, :] * weight_i * weight_k * along_y
+            + metric[2][:, :, None, None, :] * weight_i * weight_j * along_z
+            + metric[3][:, :, None, None, :] * weight_i * weight_j * weight_k * plane
+        )
+    return out
+
+
 def local_diagonal(metric, weights, stiff):
     stiff_diag = np.diagonal(stiff)
     weight_i = weights[None, None, :, None, None, None]
@@ -114,8 +135,8 @@
     )
 
 
-def assemble(values_in, ride=None):
-    lower, upper = faces(values_in, 3)
+def assemble(values_in, ride=None, x_faces=None):
+    lower, upper = faces(values_in, 3) if x_faces is None else x_faces
     rim_faces = jnp.concatenate([lower, upper], 1)
     padded = padded_2(rim_faces, (("ex", 1),), 1)
     if ride is not None:
@@ -213,13 +234,14 @@
         if step + 2 == SWEEPS:
             early = gather_flat(pressure.reshape(-1), picks, 256)
         applied = element_apply(update, metric, weights, stiff)
+        x_faces = [face[None] for face in x_faces_apply(update, metric, weights, stiff)]
         if step + 1 == SWEEPS:
             samples = early + gather_flat(update.reshape(-1), picks, 256, 2)
             numer = segment_sum(areas * samples, global_ids, strips * SHELL_STRIP, 256, 2)
             partial = jnp.stack([numer, denom])
-            assembled, mine = assemble(applied[None], strip_reduce(partial, strips, SHELL_STRIP))
+            assembled, mine = assemble(applied[None], strip_reduce(partial, strips, SHELL_STRIP), x_faces)
         else:
-            assembled, _ = assemble(applied[None])
+            assembled, _ = assemble(applied[None], None, x_faces)
         assembled = assembled[0]
         if step + 2 == SWEEPS:
             assembled, early = lax.optimization_barrier((assembled, early))

time: 139 us -> 143 us (1.029)
  waiting for transfers between devices: 50.5 us -> 39.7 us
  matrix products: 12 us -> 19.2 us
  starting transfers between devices: 54 us -> 58 us
  other arithmetic: 14.5 us -> 17.1 us
    ppermute x10, waiting for transfers between devices: 13.9 us -> 6.66 us  [padded_2(): lax.ppermute(lax.slice_in_dim(block, block.shape[dim] - width, None, axis...]
    dot_general x0 -> x24, matrix products: none -> 6.63 us  [the longest x8 4.01 us: x_faces_apply(): jnp.einsum('m,abmjkc->abjkc', stiff[edge], values_in, precision=top)]
    ppermute x10, starting transfers between devices: 16.9 us -> 21.5 us  [padded_2(): lax.ppermute(lax.slice_in_dim(block, 0, width, axis=dim), axis, backward)]
    ppermute x10, waiting for transfers between devices: 25.8 us -> 21.6 us  [padded_2(): lax.ppermute(lax.slice_in_dim(block, 0, width, axis=dim), axis, backward)]
  transfers between devices with their start and end apart: 22 -> 22, of which waited for: 20 -> 12; matrix products, arithmetic and copies ran while one was open for 9% -> 14% of each run, Pallas kernels for 0% -> 0%
where the time goes in v15:
time: 143 us; the launch traced here: 142 us
  starting transfers between devices  58 us (41%)
  waiting for transfers between devices  39.7 us (28%)
  matrix products  19.2 us (13%)
  other arithmetic  17.1 us (12%)
  local copies, waits for them, and re-layouts  5.88 us (4%)
  between operations  1.85 us (1%)
    ppermute x10, starting transfers between devices, padded_2(): lax.ppermute(lax.slice_in_dim(block, block.shape[dim] - width, None, axis...  28.7 us
    ppermute x10, waiting for transfers between devices, padded_2(): lax.ppermute(lax.slice_in_dim(block, 0, width, axis=dim), axis, backward)  21.6 us
    ppermute x10, starting transfers between devices, padded_2(): lax.ppermute(lax.slice_in_dim(block, 0, width, axis=dim), axis, backward)  21.5 us
    ppermute x10, waiting for transfers between devices, padded_2(): lax.ppermute(lax.slice_in_dim(block, block.shape[dim] - width, None, axis...  6.66 us
    all_to_all x1, waiting for transfers between devices, strip_gather(): whole = lax.all_to_all(spread_out, 'ex', 0, 0, tiled=True)  6.22 us
    all_to_all x1, waiting for transfers between devices, strip_reduce(): return lax.all_to_all(chunks, ('ex', 'ey'), 0, 0, tiled=True).sum(0)  5.17 us
    all_to_all x1, starting transfers between devices, strip_reduce(): return lax.all_to_all(chunks, ('ex', 'ey'), 0, 0, tiled=True).sum(0)  4.34 us
    dot_general x8, matrix products, x_faces_apply(): jnp.einsum('m,abmjkc->abjkc', stiff[edge], values_in, precision=top)  4.01 us
  transfers between devices with their start and end apart: 22, of which 12 were waited for; matrix products, arithmetic and copies ran while one was open for 14% of the time, Pallas kernels for 0%

profile of v15, /device:TPU:2, one launch (start us, length us, event | category | flops | bytes accessed | tf_op | source)
XLA Modules:
  0.0 141.8 jit_solution(1486424812919884343)
XLA Ops:
  3.6 1.2 fusion.129
  4.8 0.8 maximum_bitcast_fusion.9
  5.6 3.4 %collective-permute-start = (f32[2,1,1,8,8,128]{5,0,4,3,2,1:T(2,128)S(1)}, f32[2,1,1,8,8,128]{5,0,4,3,2,1:T(2,128)S(1)}, u32[]{:S(2)}, u32[]{:S(2)}) collective-permute-start(f32[2,1,1,8,8,128]{5,0,4,3,2,1:T(2,128)S(1)} %maximum_bitcast_fusion.9), channel_id=1, source_target_pairs={{0,4},{4,8},{8,12},{12,16},{16,20},{20,24},{24,28},{1,5},{5,9},{9,... | collective-permute-start | bytes 196616 | tf_op jit(solution)/shard_map/ppermute | solution.py:16
  9.0 0.9 fusion.177
  10.6 0.8 and_select_fusion.2
  12.9 1.2 fusion.20
  14.2 1.9 %fusion = f32[768,256]{1,0:T(8,128)S(1)} fusion(bf16[256,4096]{1,0:T(8,128)(2,1)S(1)} %get-tuple-element.82, bf16[256,4096]{1,0:T(8,128)(2,1)S(1)} %get-tuple-element.83, bf16[256,4096]{1,0:T(8,128)(2,1)S(1)} %get-tuple-element.81, s32[4096]{0:T(1024)S(1)} %add_select_fusion), kind=kOutput, calls=%fused_computation | convolution fusion | flops 1630535680 | bytes 7094272 | tf_op jit(solution)/shard_map/dot_general | solution.py:188
  16.2 1.3 collective-permute-start.1
  18.1 4.3 %collective-permute-done.1 = f32[2,1,1,8,8,128]{5,0,4,3,2,1:T(2,128)S(1)} collective-permute-done((f32[2,1,1,8,8,128]{5,0,4,3,2,1:T(2,128)S(1)}, f32[2,1,1,8,8,128]{5,0,4,3,2,1:T(2,128)S(1)}, u32[]{:S(2)}, u32[]{:S(2)}) %collective-permute-start.1) | collective-permute-done | bytes 65568 | tf_op jit(solution)/shard_map/ppermute | solution.py:19
  22.5 1.9 %collective-permute-start.2 = (f32[2,1,1,8,8,128]{5,3,0,4,2,1:T(8,128)S(1)}, f32[2,1,1,8,8,128]{5,3,0,4,2,1:T(8,128)S(1)}, u32[]{:S(2)}, u32[]{:S(2)}) collective-permute-start(f32[2,1,1,8,8,128]{5,3,0,4,2,1:T(8,128)S(1)} %maximum_bitcast_fusion.7), channel_id=1, source_target_pairs={{0,1},{1,2},{2,3},{4,5},{5,6},{6,7},{8,9},{9,10},{10,11},{12,13},{... | collective-permute-start | bytes 196616 | tf_op jit(solution)/shard_map/ppermute | solution.py:16
  24.5 3.6 %collective-permute-done.2 = f32[2,1,1,8,8,128]{5,3,0,4,2,1:T(8,128)S(1)} collective-permute-done((f32[2,1,1,8,8,128]{5,3,0,4,2,1:T(8,128)S(1)}, f32[2,1,1,8,8,128]{5,3,0,4,2,1:T(8,128)S(1)}, u32[]{:S(2)}, u32[]{:S(2)}) %collective-permute-start.2) | collective-permute-done | bytes 65568 | tf_op jit(solution)/shard_map/ppermute | solution.py:16
  28.1 2.1 %collective-permute-start.3 = (f32[2,1,1,8,8,128]{5,3,0,4,2,1:T(8,128)S(1)}, f32[2,1,1,8,8,128]{5,3,0,4,2,1:T(8,128)S(1)}, u32[]{:S(2)}, u32[]{:S(2)}) collective-permute-start(f32[2,1,1,8,8,128]{5,3,0,4,2,1:T(8,128)S(1)} %get-tuple-element.41), channel_id=1, source_target_pairs={{1,0},{2,1},{3,2},{5,4},{6,5},{7,6},{9,8},{10,9},{11,10},{13,12},{... | collective-permute-start | bytes 196616 | tf_op jit(solution)/shard_map/ppermute | solution.py:19
  30.6 1.5 %collective-permute-done.3 = f32[2,1,1,8,8,128]{5,3,0,4,2,1:T(8,128)S(1)} collective-permute-done((f32[2,1,1,8,8,128]{5,3,0,4,2,1:T(8,128)S(1)}, f32[2,1,1,8,8,128]{5,3,0,4,2,1:T(8,128)S(1)}, u32[]{:S(2)}, u32[]{:S(2)}) %collective-permute-start.3) | collective-permute-done | bytes 65568 | tf_op jit(solution)/shard_map/ppermute | solution.py:19
  34.9 4.3 %collective-permute-start.4 = (f32[1,1,1,8,8,128]{5,3,4,2,1,0:T(8,128)S(1)}, f32[1,1,1,8,8,128]{5,3,4,2,1,0:T(8,128)S(1)}, u32[]{:S(2)}, u32[]{:S(2)}) collective-permute-start(f32[1,1,1,8,8,128]{5,3,4,2,1,0:T(8,128)S(1)} %fusion.54), channel_id=1, source_target_pairs={{0,4},{4,8},{8,12},{12,16},{16,20},{20,24},{24,28},{1,5},{5,9},{9,... | collective-permute-start | bytes 98312 | tf_op jit(solution)/shard_map/ppermute | solution.py:16
  39.2 0.9 fusion.30
  40.3 1.3 collective-permute-start.5
  41.7 4.4 %collective-permute-done.5 = f32[1,1,1,8,8,128]{5,3,4,2,1,0:T(8,128)S(1)} collective-permute-done((f32[1,1,1,8,8,128]{5,3,4,2,1,0:T(8,128)S(1)}, f32[1,1,1,8,8,128]{5,3,4,2,1,0:T(8,128)S(1)}, u32[]{:S(2)}, u32[]{:S(2)}) %collective-permute-start.5) | collective-permute-done | bytes 32800 | tf_op jit(solution)/shard_map/ppermute | solution.py:19
  46.2 1.9 %collective-permute-start.6 = (f32[1,1,1,8,8,128]{5,3,4,2,1,0:T(8,128)S(1)}, f32[1,1,1,8,8,128]{5,3,4,2,1,0:T(8,128)S(1)}, u32[]{:S(2)}, u32[]{:S(2)}) collective-permute-start(f32[1,1,1,8,8,128]{5,3,4,2,1,0:T(8,128)S(1)} %maximum_bitcast_fusion.13), channel_id=1, source_target_pairs={{0,1},{1,2},{2,3},{4,5},{5,6},{6,7},{8,9},{9,10},{10,11},{12,13},{... | collective-permute-start | bytes 98312 | tf_op jit(solution)/shard_map/ppermute | solution.py:16
  48.4 3.1 %collective-permute-done.6 = f32[1,1,1,8,8,128]{5,3,4,2,1,0:T(8,128)S(1)} collective-permute-done((f32[1,1,1,8,8,128]{5,3,4,2,1,0:T(8,128)S(1)}, f32[1,1,1,8,8,128]{5,3,4,2,1,0:T(8,128)S(1)}, u32[]{:S(2)}, u32[]{:S(2)}) %collective-permute-start.6) | collective-permute-done | bytes 32800 | tf_op jit(solution)/shard_map/ppermute | solution.py:16
  51.5 1.9 %collective-permute-start.7 = (f32[1,1,1,8,8,128]{5,3,4,2,1,0:T(8,128)S(1)}, f32[1,1,1,8,8,128]{5,3,4,2,1,0:T(8,128)S(1)}, u32[]{:S(2)}, u32[]{:S(2)}) collective-permute-start(f32[1,1,1,8,8,128]{5,3,4,2,1,0:T(8,128)S(1)} %get-tuple-element.37), channel_id=1, source_target_pairs={{1,0},{2,1},{3,2},{5,4},{6,5},{7,6},{9,8},{10,9},{11,10},{13,12},{... | collective-permute-start | bytes 98312 | tf_op jit(solution)/shard_map/ppermute | solution.py:19
  53.6 1.4 collective-permute-done.7
  57.6 3.6 %collective-permute-start.8 = (f32[1,1,1,8,8,128]{5,3,4,2,1,0:T(8,128)S(1)}, f32[1,1,1,8,8,128]{5,3,4,2,1,0:T(8,128)S(1)}, u32[]{:S(2)}, u32[]{:S(2)}) collective-permute-start(f32[1,1,1,8,8,128]{5,3,4,2,1,0:T(8,128)S(1)} %fusion.66), channel_id=1, source_target_pairs={{0,4},{4,8},{8,12},{12,16},{16,20},{20,24},{24,28},{1,5},{5,9},{9,... | collective-permute-start | bytes 98312 | tf_op jit(solution)/shard_map/ppermute | solution.py:16
  62.5 1.3 collective-permute-start.9
  63.8 4.5 %collective-permute-done.9 = f32[1,1,1,8,8,128]{5,3,4,2,1,0:T(8,128)S(1)} collective-permute-done((f32[1,1,1,8,8,128]{5,3,4,2,1,0:T(8,128)S(1)}, f32[1,1,1,8,8,128]{5,3,4,2,1,0:T(8,128)S(1)}, u32[]{:S(2)}, u32[]{:S(2)}) %collective-permute-start.9) | collective-permute-done | bytes 32800 | tf_op jit(solution)/shard_map/ppermute | solution.py:19
  68.4 1.9 %collective-permute-start.10 = (f32[1,1,1,8,8,128]{5,4,3,2,1,0:T(8,128)S(1)}, f32[1,1,1,8,8,128]{5,4,3,2,1,0:T(8,128)S(1)}, u32[]{:S(2)}, u32[]{:S(2)}) collective-permute-start(f32[1,1,1,8,8,128]{5,4,3,2,1,0:T(8,128)S(1)} %bitcast.842), channel_id=1, source_target_pairs={{0,1},{1,2},{2,3},{4,5},{5,6},{6,7},{8,9},{9,10},{10,11},{12,13},{... | collective-permute-start | bytes 98312 | tf_op jit(solution)/shard_map/ppermute | solution.py:16
  70.3 3.6 %collective-permute-start.11 = (f32[1,1,1,8,8,128]{5,4,3,2,1,0:T(8,128)S(1)}, f32[1,1,1,8,8,128]{5,4,3,2,1,0:T(8,128)S(1)}, u32[]{:S(2)}, u32[]{:S(2)}) collective-permute-start(f32[1,1,1,8,8,128]{5,4,3,2,1,0:T(8,128)S(1)} %bitcast.846), channel_id=1, source_target_pairs={{1,0},{2,1},{3,2},{5,4},{6,5},{7,6},{9,8},{10,9},{11,10},{13,12},{... | collective-permute-start | bytes 98312 | tf_op jit(solution)/shard_map/ppermute | solution.py:19
  74.1 1.4 collective-permute-done.11
  78.4 4.3 %collective-permute-start.12 = (f32[1,1,1,8,8,128]{5,3,4,2,1,0:T(8,128)S(1)}, f32[1,1,1,8,8,128]{5,3,4,2,1,0:T(8,128)S(1)}, u32[]{:S(2)}, u32[]{:S(2)}) collective-permute-start(f32[1,1,1,8,8,128]{5,3,4,2,1,0:T(8,128)S(1)} %fusion.78), channel_id=1, source_target_pairs={{0,4},{4,8},{8,12},{12,16},{16,20},{20,24},{24,28},{1,5},{5,9},{9,... | collective-permute-start | bytes 98312 | tf_op jit(solution)/shard_map/ppermute | solution.py:16
  82.9 1.3 collective-permute-start.13
  85.0 1.9 %fusion.15 = f32[768,4096]{1,0:T(8,128)S(1)} fusion(s32[4096]{0:T(1024)S(1)} %bitcast.836, bf16[256,256]{1,0:T(8,128)(2,1)S(1)} %get-tuple-element.55, bf16[256,256]{1,0:T(8,128)(2,1)S(1)} %get-tuple-element.56, bf16[256,256]{1,0:T(8,128)(2,1)S(1)} %get-tuple-element.54), kind=kOutput, calls=%fused_computation.19 | convolution fusion | flops 1612840960 | bytes 12992512 | tf_op jit(solution)/shard_map/dot_general | solution.py:174
  87.2 1.5 %collective-permute-done.13 = f32[1,1,1,8,8,128]{5,3,4,2,1,0:T(8,128)S(1)} collective-permute-done((f32[1,1,1,8,8,128]{5,3,4,2,1,0:T(8,128)S(1)}, f32[1,1,1,8,8,128]{5,3,4,2,1,0:T(8,128)S(1)}, u32[]{:S(2)}, u32[]{:S(2)}) %collective-permute-start.13) | collective-permute-done | bytes 32800 | tf_op jit(solution)/shard_map/ppermute | solution.py:19
  88.8 1.9 %collective-permute-start.14 = (f32[1,1,1,8,8,128]{5,4,3,2,1,0:T(8,128)S(1)}, f32[1,1,1,8,8,128]{5,4,3,2,1,0:T(8,128)S(1)}, u32[]{:S(2)}, u32[]{:S(2)}) collective-permute-start(f32[1,1,1,8,8,128]{5,4,3,2,1,0:T(8,128)S(1)} %bitcast.844), channel_id=1, source_target_pairs={{0,1},{1,2},{2,3},{4,5},{5,6},{6,7},{8,9},{9,10},{10,11},{12,13},{... | collective-permute-start | bytes 98312 | tf_op jit(solution)/shard_map/ppermute | solution.py:16
  90.7 3.9 %collective-permute-start.15 = (f32[1,1,1,8,8,128]{5,4,3,2,1,0:T(8,128)S(1)}, f32[1,1,1,8,8,128]{5,4,3,2,1,0:T(8,128)S(1)}, u32[]{:S(2)}, u32[]{:S(2)}) collective-permute-start(f32[1,1,1,8,8,128]{5,4,3,2,1,0:T(8,128)S(1)} %bitcast.848), channel_id=1, source_target_pairs={{1,0},{2,1},{3,2},{5,4},{6,5},{7,6},{9,8},{10,9},{11,10},{13,12},{... | collective-permute-start | bytes 98312 | tf_op jit(solution)/shard_map/ppermute | solution.py:19
  94.6 1.4 fusion.9
  97.7 1.3 fusion.14
  99.0 0.9 fusion.7
  100.0 0.9 fusion.17
  100.8 1.4 %fusion.10 = f32[512,256]{1,0:T(8,128)S(1)} fusion(bf16[256,4096]{1,0:T(8,128)(2,1)S(1)} %get-tuple-element.80, bf16[256,4096]{1,0:T(8,128)(2,1)S(1)} %get-tuple-element.79, s32[4096]{0:T(1024)S(1)} %add_select_fusion), kind=kOutput, calls=%fused_computation.13 | convolution fusion | flops 1083179008 | bytes 4734976 | tf_op jit(solution)/shard_map/dot_general | solution.py:188
  102.4 1.2 copy.287
  103.6 4.3 %all-to-all-start = ((f32[32,2,2048]{2,1,0:T(2,128)}), f32[32,2,2048]{2,1,0:T(2,128)S(1)}, u32[]{:S(2)}, u32[]{:S(2)}) async-start(f32[32,2,2048]{2,1,0:T(2,128)} %bitcast.186), calls=%async_computation | async-start | bytes 1048576 | tf_op jit(solution)/shard_map/all_to_all | solution.py:203
  108.3 3.4 %collective-permute-start.16 = (f32[1,1,1,8,8,128]{5,3,4,2,1,0:T(8,128)S(1)}, f32[1,1,1,8,8,128]{5,3,4,2,1,0:T(8,128)S(1)}, u32[]{:S(2)}, u32[]{:S(2)}) collective-permute-start(f32[1,1,1,8,8,128]{5,3,4,2,1,0:T(8,128)S(1)} %fusion.90), channel_id=1, source_target_pairs={{0,4},{4,8},{8,12},{12,16},{16,20},{20,24},{24,28},{1,5},{5,9},{9,... | collective-permute-start | bytes 98312 | tf_op jit(solution)/shard_map/ppermute | solution.py:16
  112.0 1.3 collective-permute-start.17
  115.2 2.7 %collective-permute-done.17 = f32[1,1,1,8,8,128]{5,3,4,2,1,0:T(8,128)S(1)} collective-permute-done((f32[1,1,1,8,8,128]{5,3,4,2,1,0:T(8,128)S(1)}, f32[1,1,1,8,8,128]{5,3,4,2,1,0:T(8,128)S(1)}, u32[]{:S(2)}, u32[]{:S(2)}) %collective-permute-start.17) | collective-permute-done | bytes 32800 | tf_op jit(solution)/shard_map/ppermute | solution.py:19
  117.8 5.2 %all-to-all-done = f32[32,2,2048]{2,1,0:T(2,128)S(1)} async-done(((f32[32,2,2048]{2,1,0:T(2,128)}), f32[32,2,2048]{2,1,0:T(2,128)S(1)}, u32[]{:S(2)}, u32[]{:S(2)}) %all-to-all-start) | async-done | bytes 524320 | tf_op jit(solution)/shard_map/all_to_all | solution.py:203
  123.2 2.0 %collective-permute-start.18 = (f32[1,1,1,8,8,128]{5,4,3,2,1,0:T(8,128)S(1)}, f32[1,1,1,8,8,128]{5,4,3,2,1,0:T(8,128)S(1)}, u32[]{:S(2)}, u32[]{:S(2)}) collective-permute-start(f32[1,1,1,8,8,128]{5,4,3,2,1,0:T(8,128)S(1)} %bitcast.838), channel_id=1, source_target_pairs={{0,1},{1,2},{2,3},{4,5},{5,6},{6,7},{8,9},{9,10},{10,11},{12,13},{... | collective-permute-start | bytes 98312 | tf_op jit(solution)/shard_map/ppermute | solution.py:16
  125.2 3.6 %collective-permute-start.19 = (f32[1,1,1,8,8,128]{5,4,3,2,1,0:T(8,128)S(1)}, f32[1,1,1,8,8,128]{5,4,3,2,1,0:T(8,128)S(1)}, u32[]{:S(2)}, u32[]{:S(2)}) collective-permute-start(f32[1,1,1,8,8,128]{5,4,3,2,1,0:T(8,128)S(1)} %bitcast.840), channel_id=1, source_target_pairs={{1,0},{2,1},{3,2},{5,4},{6,5},{7,6},{9,8},{10,9},{11,10},{13,12},{... | collective-permute-start | bytes 98312 | tf_op jit(solution)/shard_map/ppermute | solution.py:19
  130.3 3.4 %all-to-all-start.1 = ((f32[8,2,2048]{2,1,0:T(2,128)}), f32[8,2,2048]{2,1,0:T(2,128)S(1)}, u32[]{:S(2)}, u32[]{:S(2)}) async-start(f32[8,2,2048]{2,1,0:T(2,128)} %broadcast_in_dim.245), calls=%async_computation.1 | async-start | bytes 262144 | tf_op jit(solution)/shard_map/all_to_all | solution.py:210
  134.8 6.2 %all-to-all-done.1 = f32[8,2,2048]{2,1,0:T(2,128)S(1)} async-done(((f32[8,2,2048]{2,1,0:T(2,128)}), f32[8,2,2048]{2,1,0:T(2,128)S(1)}, u32[]{:S(2)}, u32[]{:S(2)}) %all-to-all-start.1) | async-done | bytes 131104 | tf_op jit(solution)/shard_map/all_to_all | solution.py:210
  (168 shorter events, 25.6 us)
Async XLA Ops:
  5.6 10.5 %collective-permute-start = (f32[2,1,1,8,8,128]{5,0,4,3,2,1:T(2,128)S(1)}, f32[2,1,1,8,8,128]{5,0,4,3,2,1:T(2,128)S(1)}, u32[]{:S(2)}, u32[]{:S(2)}) collective-permute-start(f32[2,1,1,8,8,128]{5,0,4,3,2,1:T(2,128)S(1)} %maximum_bitcast_fusion.9), channel_id=1, source_target_pairs={{0,4},{4,8},{8,12},{12,16},{16,20},{20,24},{24,28},{1,5},{5,9},{9,... | collective-permute-start | bytes 196616 | tf_op jit(solution)/shard_map/ppermute | solution.py:16
  14.2 2.0 %copy-start = (f32[1,1,8,8,8,128]{5,4,3,2,1,0:T(8,128)S(1)}, f32[1,1,8,8,8,128]{5,4,3,2,1,0:T(8,128)}, u32[]{:S(2)}) copy-start(f32[1,1,8,8,8,128]{5,4,3,2,1,0:T(8,128)} %param.68) | copy-start | bytes 786436
  16.2 6.2 %collective-permute-start.1 = (f32[2,1,1,8,8,128]{5,0,4,3,2,1:T(2,128)S(1)}, f32[2,1,1,8,8,128]{5,0,4,3,2,1:T(2,128)S(1)}, u32[]{:S(2)}, u32[]{:S(2)}) collective-permute-start(f32[2,1,1,8,8,128]{5,0,4,3,2,1:T(2,128)S(1)} %get-tuple-element.43), channel_id=1, source_target_pairs={{4,0},{8,4},{12,8},{16,12},{20,16},{24,20},{28,24},{5,1},{9,5},{13... | collective-permute-start | bytes 196616 | tf_op jit(solution)/shard_map/ppermute | solution.py:19
  22.5 5.6 %collective-permute-start.2 = (f32[2,1,1,8,8,128]{5,3,0,4,2,1:T(8,128)S(1)}, f32[2,1,1,8,8,128]{5,3,0,4,2,1:T(8,128)S(1)}, u32[]{:S(2)}, u32[]{:S(2)}) collective-permute-start(f32[2,1,1,8,8,128]{5,3,0,4,2,1:T(8,128)S(1)} %maximum_bitcast_fusion.7), channel_id=1, source_target_pairs={{0,1},{1,2},{2,3},{4,5},{5,6},{6,7},{8,9},{9,10},{10,11},{12,13},{... | collective-permute-start | bytes 196616 | tf_op jit(solution)/shard_map/ppermute | solution.py:16
  24.5 8.1 %copy-start.2 = (f32[8,8,1,1]{1,0,3,2:T(8,128)S(1)}, f32[8,8,1,1]{1,0,3,2:T(8,128)}, u32[]{:S(2)}) copy-start(f32[8,8,1,1]{1,0,3,2:T(8,128)} %constant.149) | copy-start | bytes 772
  28.1 5.2 %copy-start.6 = (f32[8,1,1,1]{0,1,3,2:T(1,128)S(1)}, f32[8,1,1,1]{0,1,3,2:T(1,128)}, u32[]{:S(2)}) copy-start(f32[8,1,1,1]{0,1,3,2:T(1,128)} %constant.146) | copy-start | bytes 100
  28.1 5.8 %copy-start.1 = (f32[8,8,1]{1,0,2:T(8,128)S(1)}, f32[8,8,1]{1,0,2:T(8,128)}, u32[]{:S(2)}) copy-start(f32[8,8,1]{1,0,2:T(8,128)} %constant.147) | copy-start | bytes 772
  28.1 6.1 %copy-start.7 = (f32[8,1,1,1]{0,1,3,2:T(1,128)S(1)}, f32[8,1,1,1]{0,1,3,2:T(1,128)}, u32[]{:S(2)}) copy-start(f32[8,1,1,1]{0,1,3,2:T(1,128)} %constant.148) | copy-start | bytes 100
  28.1 6.6 %copy-start.3 = (f32[8]{0:T(128)S(1)}, f32[8]{0:T(128)}, u32[]{:S(2)}) copy-start(f32[8]{0:T(128)} %constant.139) | copy-start | bytes 100
  28.1 3.9 %collective-permute-start.3 = (f32[2,1,1,8,8,128]{5,3,0,4,2,1:T(8,128)S(1)}, f32[2,1,1,8,8,128]{5,3,0,4,2,1:T(8,128)S(1)}, u32[]{:S(2)}, u32[]{:S(2)}) collective-permute-start(f32[2,1,1,8,8,128]{5,3,0,4,2,1:T(8,128)S(1)} %get-tuple-element.41), channel_id=1, source_target_pairs={{1,0},{2,1},{3,2},{5,4},{6,5},{7,6},{9,8},{10,9},{11,10},{13,12},{... | collective-permute-start | bytes 196616 | tf_op jit(solution)/shard_map/ppermute | solution.py:19
  34.9 6.8 %collective-permute-start.4 = (f32[1,1,1,8,8,128]{5,3,4,2,1,0:T(8,128)S(1)}, f32[1,1,1,8,8,128]{5,3,4,2,1,0:T(8,128)S(1)}, u32[]{:S(2)}, u32[]{:S(2)}) collective-permute-start(f32[1,1,1,8,8,128]{5,3,4,2,1,0:T(8,128)S(1)} %fusion.54), channel_id=1, source_target_pairs={{0,4},{4,8},{8,12},{12,16},{16,20},{20,24},{24,28},{1,5},{5,9},{9,... | collective-permute-start | bytes 98312 | tf_op jit(solution)/shard_map/ppermute | solution.py:16
  40.3 5.8 %collective-permute-start.5 = (f32[1,1,1,8,8,128]{5,3,4,2,1,0:T(8,128)S(1)}, f32[1,1,1,8,8,128]{5,3,4,2,1,0:T(8,128)S(1)}, u32[]{:S(2)}, u32[]{:S(2)}) collective-permute-start(f32[1,1,1,8,8,128]{5,3,4,2,1,0:T(8,128)S(1)} %fusion.48), channel_id=1, source_target_pairs={{4,0},{8,4},{12,8},{16,12},{20,16},{24,20},{28,24},{5,1},{9,5},{13... | collective-permute-start | bytes 98312 | tf_op jit(solution)/shard_map/ppermute | solution.py:19
  46.2 5.2 %collective-permute-start.6 = (f32[1,1,1,8,8,128]{5,3,4,2,1,0:T(8,128)S(1)}, f32[1,1,1,8,8,128]{5,3,4,2,1,0:T(8,128)S(1)}, u32[]{:S(2)}, u32[]{:S(2)}) collective-permute-start(f32[1,1,1,8,8,128]{5,3,4,2,1,0:T(8,128)S(1)} %maximum_bitcast_fusion.13), channel_id=1, source_target_pairs={{0,1},{1,2},{2,3},{4,5},{5,6},{6,7},{8,9},{9,10},{10,11},{12,13},{... | collective-permute-start | bytes 98312 | tf_op jit(solution)/shard_map/ppermute | solution.py:16
  51.5 3.5 %collective-permute-start.7 = (f32[1,1,1,8,8,128]{5,3,4,2,1,0:T(8,128)S(1)}, f32[1,1,1,8,8,128]{5,3,4,2,1,0:T(8,128)S(1)}, u32[]{:S(2)}, u32[]{:S(2)}) collective-permute-start(f32[1,1,1,8,8,128]{5,3,4,2,1,0:T(8,128)S(1)} %get-tuple-element.37), channel_id=1, source_target_pairs={{1,0},{2,1},{3,2},{5,4},{6,5},{7,6},{9,8},{10,9},{11,10},{13,12},{... | collective-permute-start | bytes 98312 | tf_op jit(solution)/shard_map/ppermute | solution.py:19
  53.5 20.5 %copy-start.4 = (s32[1,4096]{1,0:T(1,128)S(1)}, s32[1,4096]{1,0:T(1,128)}, u32[]{:S(2)}) copy-start(s32[1,4096]{1,0:T(1,128)} %param.70) | copy-start | bytes 49156
  57.6 6.2 %collective-permute-start.8 = (f32[1,1,1,8,8,128]{5,3,4,2,1,0:T(8,128)S(1)}, f32[1,1,1,8,8,128]{5,3,4,2,1,0:T(8,128)S(1)}, u32[]{:S(2)}, u32[]{:S(2)}) collective-permute-start(f32[1,1,1,8,8,128]{5,3,4,2,1,0:T(8,128)S(1)} %fusion.66), channel_id=1, source_target_pairs={{0,4},{4,8},{8,12},{12,16},{16,20},{20,24},{24,28},{1,5},{5,9},{9,... | collective-permute-start | bytes 98312 | tf_op jit(solution)/shard_map/ppermute | solution.py:16
  62.5 5.8 %collective-permute-start.9 = (f32[1,1,1,8,8,128]{5,3,4,2,1,0:T(8,128)S(1)}, f32[1,1,1,8,8,128]{5,3,4,2,1,0:T(8,128)S(1)}, u32[]{:S(2)}, u32[]{:S(2)}) collective-permute-start(f32[1,1,1,8,8,128]{5,3,4,2,1,0:T(8,128)S(1)} %fusion.60), channel_id=1, source_target_pairs={{4,0},{8,4},{12,8},{16,12},{20,16},{24,20},{28,24},{5,1},{9,5},{13... | collective-permute-start | bytes 98312 | tf_op jit(solution)/shard_map/ppermute | solution.py:19
  68.4 5.7 %collective-permute-start.10 = (f32[1,1,1,8,8,128]{5,4,3,2,1,0:T(8,128)S(1)}, f32[1,1,1,8,8,128]{5,4,3,2,1,0:T(8,128)S(1)}, u32[]{:S(2)}, u32[]{:S(2)}) collective-permute-start(f32[1,1,1,8,8,128]{5,4,3,2,1,0:T(8,128)S(1)} %bitcast.842), channel_id=1, source_target_pairs={{0,1},{1,2},{2,3},{4,5},{5,6},{6,7},{8,9},{9,10},{10,11},{12,13},{... | collective-permute-start | bytes 98312 | tf_op jit(solution)/shard_map/ppermute | solution.py:16
  70.3 5.2 %collective-permute-start.11 = (f32[1,1,1,8,8,128]{5,4,3,2,1,0:T(8,128)S(1)}, f32[1,1,1,8,8,128]{5,4,3,2,1,0:T(8,128)S(1)}, u32[]{:S(2)}, u32[]{:S(2)}) collective-permute-start(f32[1,1,1,8,8,128]{5,4,3,2,1,0:T(8,128)S(1)} %bitcast.846), channel_id=1, source_target_pairs={{1,0},{2,1},{3,2},{5,4},{6,5},{7,6},{9,8},{10,9},{11,10},{13,12},{... | collective-permute-start | bytes 98312 | tf_op jit(solution)/shard_map/ppermute | solution.py:19
  78.4 8.8 %collective-permute-start.12 = (f32[1,1,1,8,8,128]{5,3,4,2,1,0:T(8,128)S(1)}, f32[1,1,1,8,8,128]{5,3,4,2,1,0:T(8,128)S(1)}, u32[]{:S(2)}, u32[]{:S(2)}) collective-permute-start(f32[1,1,1,8,8,128]{5,3,4,2,1,0:T(8,128)S(1)} %fusion.78), channel_id=1, source_target_pairs={{0,4},{4,8},{8,12},{12,16},{16,20},{20,24},{24,28},{1,5},{5,9},{9,... | collective-permute-start | bytes 98312 | tf_op jit(solution)/shard_map/ppermute | solution.py:16
  82.9 5.8 %collective-permute-start.13 = (f32[1,1,1,8,8,128]{5,3,4,2,1,0:T(8,128)S(1)}, f32[1,1,1,8,8,128]{5,3,4,2,1,0:T(8,128)S(1)}, u32[]{:S(2)}, u32[]{:S(2)}) collective-permute-start(f32[1,1,1,8,8,128]{5,3,4,2,1,0:T(8,128)S(1)} %fusion.72), channel_id=1, source_target_pairs={{4,0},{8,4},{12,8},{16,12},{20,16},{24,20},{28,24},{5,1},{9,5},{13... | collective-permute-start | bytes 98312 | tf_op jit(solution)/shard_map/ppermute | solution.py:19
  88.8 7.2 %collective-permute-start.14 = (f32[1,1,1,8,8,128]{5,4,3,2,1,0:T(8,128)S(1)}, f32[1,1,1,8,8,128]{5,4,3,2,1,0:T(8,128)S(1)}, u32[]{:S(2)}, u32[]{:S(2)}) collective-permute-start(f32[1,1,1,8,8,128]{5,4,3,2,1,0:T(8,128)S(1)} %bitcast.844), channel_id=1, source_target_pairs={{0,1},{1,2},{2,3},{4,5},{5,6},{6,7},{8,9},{9,10},{10,11},{12,13},{... | collective-permute-start | bytes 98312 | tf_op jit(solution)/shard_map/ppermute | solution.py:16
  90.7 5.3 %collective-permute-start.15 = (f32[1,1,1,8,8,128]{5,4,3,2,1,0:T(8,128)S(1)}, f32[1,1,1,8,8,128]{5,4,3,2,1,0:T(8,128)S(1)}, u32[]{:S(2)}, u32[]{:S(2)}) collective-permute-start(f32[1,1,1,8,8,128]{5,4,3,2,1,0:T(8,128)S(1)} %bitcast.848), channel_id=1, source_target_pairs={{1,0},{2,1},{3,2},{5,4},{6,5},{7,6},{9,8},{10,9},{11,10},{13,12},{... | collective-permute-start | bytes 98312 | tf_op jit(solution)/shard_map/ppermute | solution.py:19
  99.0 0.9 copy-start.5
  103.6 19.4 %all-to-all-start = ((f32[32,2,2048]{2,1,0:T(2,128)}), f32[32,2,2048]{2,1,0:T(2,128)S(1)}, u32[]{:S(2)}, u32[]{:S(2)}) async-start(f32[32,2,2048]{2,1,0:T(2,128)} %bitcast.186), calls=%async_computation | async-start | bytes 1048576 | tf_op jit(solution)/shard_map/all_to_all | solution.py:203
  108.3 6.9 %collective-permute-start.16 = (f32[1,1,1,8,8,128]{5,3,4,2,1,0:T(8,128)S(1)}, f32[1,1,1,8,8,128]{5,3,4,2,1,0:T(8,128)S(1)}, u32[]{:S(2)}, u32[]{:S(2)}) collective-permute-start(f32[1,1,1,8,8,128]{5,3,4,2,1,0:T(8,128)S(1)} %fusion.90), channel_id=1, source_target_pairs={{0,4},{4,8},{8,12},{12,16},{16,20},{20,24},{24,28},{1,5},{5,9},{9,... | collective-permute-start | bytes 98312 | tf_op jit(solution)/shard_map/ppermute | solution.py:16
  112.0 5.8 %collective-permute-start.17 = (f32[1,1,1,8,8,128]{5,3,4,2,1,0:T(8,128)S(1)}, f32[1,1,1,8,8,128]{5,3,4,2,1,0:T(8,128)S(1)}, u32[]{:S(2)}, u32[]{:S(2)}) collective-permute-start(f32[1,1,1,8,8,128]{5,3,4,2,1,0:T(8,128)S(1)} %fusion.84), channel_id=1, source_target_pairs={{4,0},{8,4},{12,8},{16,12},{20,16},{24,20},{28,24},{5,1},{9,5},{13... | collective-permute-start | bytes 98312 | tf_op jit(solution)/shard_map/ppermute | solution.py:19
  123.2 10.5 %collective-permute-start.18 = (f32[1,1,1,8,8,128]{5,4,3,2,1,0:T(8,128)S(1)}, f32[1,1,1,8,8,128]{5,4,3,2,1,0:T(8,128)S(1)}, u32[]{:S(2)}, u32[]{:S(2)}) collective-permute-start(f32[1,1,1,8,8,128]{5,4,3,2,1,0:T(8,128)S(1)} %bitcast.838), channel_id=1, source_target_pairs={{0,1},{1,2},{2,3},{4,5},{5,6},{6,7},{8,9},{9,10},{10,11},{12,13},{... | collective-permute-start | bytes 98312 | tf_op jit(solution)/shard_map/ppermute | solution.py:16
  125.2 8.5 %collective-permute-start.19 = (f32[1,1,1,8,8,128]{5,4,3,2,1,0:T(8,128)S(1)}, f32[1,1,1,8,8,128]{5,4,3,2,1,0:T(8,128)S(1)}, u32[]{:S(2)}, u32[]{:S(2)}) collective-permute-start(f32[1,1,1,8,8,128]{5,4,3,2,1,0:T(8,128)S(1)} %bitcast.840), channel_id=1, source_target_pairs={{1,0},{2,1},{3,2},{5,4},{6,5},{7,6},{9,8},{10,9},{11,10},{13,12},{... | collective-permute-start | bytes 98312 | tf_op jit(solution)/shard_map/ppermute | solution.py:19
  130.3 10.8 %all-to-all-start.1 = ((f32[8,2,2048]{2,1,0:T(2,128)}), f32[8,2,2048]{2,1,0:T(2,128)S(1)}, u32[]{:S(2)}, u32[]{:S(2)}) async-start(f32[8,2,2048]{2,1,0:T(2,128)} %broadcast_in_dim.245), calls=%async_computation.1 | async-start | bytes 262144 | tf_op jit(solution)/shard_map/all_to_all | solution.py:210

commit v16 on v12

--- a/solution.py
+++ b/solution.py
@@ -185,9 +185,9 @@
 def strip_gather(mine, strip_size):
     n_ex = lax.axis_size("ex")
     count, piece = mine.shape
-    spread_out = jnp.broadcast_to(mine[None], (n_ex, 2, piece))
-    whole = lax.all_to_all(spread_out, "ex", 0, 0, tiled=True)
-    return whole.transpose(1, 0, 2).reshape(2, n_ex * piece)[:, :strip_size]
+    spread_out = jnp.broadcast_to(mine[:, None], (2, n_ex, piece))
+    whole = lax.all_to_all(spread_out, "ex", 1, 1, tiled=True)
+    return whole.reshape(2, n_ex * piece)[:, :strip_size]
 
 
 def on_device(source, metric, fac_point, fac_strip, fac_shell, fac_area):

time: 139 us -> 139 us (level)
  no operation moved by 1% of the time
where the time goes in v16:
time: 139 us; the launch traced here: 138 us
  starting transfers between devices  54 us (39%)
  waiting for transfers between devices  50.5 us (36%)
  other arithmetic  14.5 us (10%)
  matrix products  12 us (9%)
  local copies, waits for them, and re-layouts  5.3 us (4%)
  between operations  1.61 us (1%)
    ppermute x10, starting transfers between devices, padded_2(): lax.ppermute(lax.slice_in_dim(block, block.shape[dim] - width, None, axis...  28.5 us
    ppermute x10, waiting for transfers between devices, padded_2(): lax.ppermute(lax.slice_in_dim(block, 0, width, axis=dim), axis, backward)  25.8 us
    ppermute x10, starting transfers between devices, padded_2(): lax.ppermute(lax.slice_in_dim(block, 0, width, axis=dim), axis, backward)  16.9 us
    ppermute x10, waiting for transfers between devices, padded_2(): lax.ppermute(lax.slice_in_dim(block, block.shape[dim] - width, None, axis...  13.9 us
    all_to_all x1, waiting for transfers between devices, strip_gather(): whole = lax.all_to_all(spread_out, 'ex', 1, 1, tiled=True)  6.78 us
    all_to_all x1, starting transfers between devices, strip_reduce(): return lax.all_to_all(chunks, ('ex', 'ey'), 0, 0, tiled=True).sum(0)  5.08 us
    all_to_all x1, waiting for transfers between devices, strip_reduce(): return lax.all_to_all(chunks, ('ex', 'ey'), 0, 0, tiled=True).sum(0)  4.09 us
    all_to_all x1, starting transfers between devices, strip_gather(): whole = lax.all_to_all(spread_out, 'ex', 1, 1, tiled=True)  3.45 us
  transfers between devices with their start and end apart: 22, of which 20 were waited for; matrix products, arithmetic and copies ran while one was open for 9% of the time, Pallas kernels for 0%

profile of v16, /device:TPU:2, one launch (start us, length us, event | category | flops | bytes accessed | tf_op | source)
XLA Modules:
  0.0 137.9 jit_solution(625179949913847734)
XLA Ops:
  2.9 1.2 fusion.90
  4.9 3.4 %collective-permute-start = (f32[2,1,1,8,8,128]{5,0,4,3,2,1:T(2,128)S(1)}, f32[2,1,1,8,8,128]{5,0,4,3,2,1:T(2,128)S(1)}, u32[]{:S(2)}, u32[]{:S(2)}) collective-permute-start(f32[2,1,1,8,8,128]{5,0,4,3,2,1:T(2,128)S(1)} %maximum_bitcast_fusion.9), channel_id=1, source_target_pairs={{0,4},{4,8},{8,12},{12,16},{16,20},{20,24},{24,28},{1,5},{5,9},{9,... | collective-permute-start | bytes 196616 | tf_op jit(solution)/shard_map/ppermute | solution.py:16
  10.0 1.2 fusion.20
  11.3 1.3 collective-permute-start.1
  13.3 4.3 %collective-permute-done.1 = f32[2,1,1,8,8,128]{5,0,4,3,2,1:T(2,128)S(1)} collective-permute-done((f32[2,1,1,8,8,128]{5,0,4,3,2,1:T(2,128)S(1)}, f32[2,1,1,8,8,128]{5,0,4,3,2,1:T(2,128)S(1)}, u32[]{:S(2)}, u32[]{:S(2)}) %collective-permute-start.1) | collective-permute-done | bytes 65568 | tf_op jit(solution)/shard_map/ppermute | solution.py:19
  17.6 1.9 %collective-permute-start.2 = (f32[2,1,1,8,8,128]{5,3,0,4,2,1:T(8,128)S(1)}, f32[2,1,1,8,8,128]{5,3,0,4,2,1:T(8,128)S(1)}, u32[]{:S(2)}, u32[]{:S(2)}) collective-permute-start(f32[2,1,1,8,8,128]{5,3,0,4,2,1:T(8,128)S(1)} %maximum_bitcast_fusion.7), channel_id=1, source_target_pairs={{0,1},{1,2},{2,3},{4,5},{5,6},{6,7},{8,9},{9,10},{10,11},{12,13},{... | collective-permute-start | bytes 196616 | tf_op jit(solution)/shard_map/ppermute | solution.py:16
  19.5 3.6 %collective-permute-done.2 = f32[2,1,1,8,8,128]{5,3,0,4,2,1:T(8,128)S(1)} collective-permute-done((f32[2,1,1,8,8,128]{5,3,0,4,2,1:T(8,128)S(1)}, f32[2,1,1,8,8,128]{5,3,0,4,2,1:T(8,128)S(1)}, u32[]{:S(2)}, u32[]{:S(2)}) %collective-permute-start.2) | collective-permute-done | bytes 65568 | tf_op jit(solution)/shard_map/ppermute | solution.py:16
  23.2 1.9 %collective-permute-start.3 = (f32[2,1,1,8,8,128]{5,3,0,4,2,1:T(8,128)S(1)}, f32[2,1,1,8,8,128]{5,3,0,4,2,1:T(8,128)S(1)}, u32[]{:S(2)}, u32[]{:S(2)}) collective-permute-start(f32[2,1,1,8,8,128]{5,3,0,4,2,1:T(8,128)S(1)} %get-tuple-element.49), channel_id=1, source_target_pairs={{1,0},{2,1},{3,2},{5,4},{6,5},{7,6},{9,8},{10,9},{11,10},{13,12},{... | collective-permute-start | bytes 196616 | tf_op jit(solution)/shard_map/ppermute | solution.py:19
  25.5 1.5 %collective-permute-done.3 = f32[2,1,1,8,8,128]{5,3,0,4,2,1:T(8,128)S(1)} collective-permute-done((f32[2,1,1,8,8,128]{5,3,0,4,2,1:T(8,128)S(1)}, f32[2,1,1,8,8,128]{5,3,0,4,2,1:T(8,128)S(1)}, u32[]{:S(2)}, u32[]{:S(2)}) %collective-permute-start.3) | collective-permute-done | bytes 65568 | tf_op jit(solution)/shard_map/ppermute | solution.py:19
  28.8 0.9 fusion.30
  29.8 4.3 %collective-permute-start.4 = (f32[1,1,1,8,8,128]{5,4,3,2,1,0:T(8,128)S(1)}, f32[1,1,1,8,8,128]{5,4,3,2,1,0:T(8,128)S(1)}, u32[]{:S(2)}, u32[]{:S(2)}) collective-permute-start(f32[1,1,1,8,8,128]{5,4,3,2,1,0:T(8,128)S(1)} %bitcast.485), channel_id=1, source_target_pairs={{0,4},{4,8},{8,12},{12,16},{16,20},{20,24},{24,28},{1,5},{5,9},{9,... | collective-permute-start | bytes 98312 | tf_op jit(solution)/shard_map/ppermute | solution.py:16
  34.1 1.3 collective-permute-start.5
  35.7 4.2 %collective-permute-done.5 = f32[1,1,1,8,8,128]{5,4,3,2,1,0:T(8,128)S(1)} collective-permute-done((f32[1,1,1,8,8,128]{5,4,3,2,1,0:T(8,128)S(1)}, f32[1,1,1,8,8,128]{5,4,3,2,1,0:T(8,128)S(1)}, u32[]{:S(2)}, u32[]{:S(2)}) %collective-permute-start.5) | collective-permute-done | bytes 32800 | tf_op jit(solution)/shard_map/ppermute | solution.py:19
  39.9 1.9 %collective-permute-start.6 = (f32[1,1,1,8,8,128]{5,3,4,2,1,0:T(8,128)S(1)}, f32[1,1,1,8,8,128]{5,3,4,2,1,0:T(8,128)S(1)}, u32[]{:S(2)}, u32[]{:S(2)}) collective-permute-start(f32[1,1,1,8,8,128]{5,3,4,2,1,0:T(8,128)S(1)} %maximum_bitcast_fusion.19), channel_id=1, source_target_pairs={{0,1},{1,2},{2,3},{4,5},{5,6},{6,7},{8,9},{9,10},{10,11},{12,13},{... | collective-permute-start | bytes 98312 | tf_op jit(solution)/shard_map/ppermute | solution.py:16
  41.9 1.9 %fusion = f32[768,256]{1,0:T(8,128)S(1)} fusion(bf16[256,4096]{1,0:T(8,128)(2,1)S(1)} %get-tuple-element.86, bf16[256,4096]{1,0:T(8,128)(2,1)S(1)} %get-tuple-element.87, bf16[256,4096]{1,0:T(8,128)(2,1)S(1)} %get-tuple-element.85, s32[4096]{0:T(1024)S(1)} %add_select_fusion), kind=kOutput, calls=%fused_computation | convolution fusion | flops 1630535680 | bytes 7094272 | tf_op jit(solution)/shard_map/dot_general | solution.py:167
  43.8 1.4 collective-permute-done.6
  45.2 2.3 %collective-permute-start.7 = (f32[1,1,1,8,8,128]{5,3,4,2,1,0:T(8,128)S(1)}, f32[1,1,1,8,8,128]{5,3,4,2,1,0:T(8,128)S(1)}, u32[]{:S(2)}, u32[]{:S(2)}) collective-permute-start(f32[1,1,1,8,8,128]{5,3,4,2,1,0:T(8,128)S(1)} %get-tuple-element.45), channel_id=1, source_target_pairs={{1,0},{2,1},{3,2},{5,4},{6,5},{7,6},{9,8},{10,9},{11,10},{13,12},{... | collective-permute-start | bytes 98312 | tf_op jit(solution)/shard_map/ppermute | solution.py:19
  47.7 1.4 collective-permute-done.7
  51.0 4.1 %collective-permute-start.8 = (f32[1,1,1,8,8,128]{5,4,3,2,1,0:T(8,128)S(1)}, f32[1,1,1,8,8,128]{5,4,3,2,1,0:T(8,128)S(1)}, u32[]{:S(2)}, u32[]{:S(2)}) collective-permute-start(f32[1,1,1,8,8,128]{5,4,3,2,1,0:T(8,128)S(1)} %get-tuple-element.73), channel_id=1, source_target_pairs={{0,4},{4,8},{8,12},{12,16},{16,20},{20,24},{24,28},{1,5},{5,9},{9,... | collective-permute-start | bytes 98312 | tf_op jit(solution)/shard_map/ppermute | solution.py:16
  55.1 1.3 collective-permute-start.9
  56.7 4.2 %collective-permute-done.9 = f32[1,1,1,8,8,128]{5,4,3,2,1,0:T(8,128)S(1)} collective-permute-done((f32[1,1,1,8,8,128]{5,4,3,2,1,0:T(8,128)S(1)}, f32[1,1,1,8,8,128]{5,4,3,2,1,0:T(8,128)S(1)}, u32[]{:S(2)}, u32[]{:S(2)}) %collective-permute-start.9) | collective-permute-done | bytes 32800 | tf_op jit(solution)/shard_map/ppermute | solution.py:19
  60.9 1.9 %collective-permute-start.10 = (f32[1,1,1,8,8,128]{5,4,3,2,1,0:T(8,128)S(1)}, f32[1,1,1,8,8,128]{5,4,3,2,1,0:T(8,128)S(1)}, u32[]{:S(2)}, u32[]{:S(2)}) collective-permute-start(f32[1,1,1,8,8,128]{5,4,3,2,1,0:T(8,128)S(1)} %maximum_bitcast_fusion.17), channel_id=1, source_target_pairs={{0,1},{1,2},{2,3},{4,5},{5,6},{6,7},{8,9},{9,10},{10,11},{12,13},{... | collective-permute-start | bytes 98312 | tf_op jit(solution)/shard_map/ppermute | solution.py:16
  62.9 3.2 %collective-permute-done.10 = f32[1,1,1,8,8,128]{5,4,3,2,1,0:T(8,128)S(1)} collective-permute-done((f32[1,1,1,8,8,128]{5,4,3,2,1,0:T(8,128)S(1)}, f32[1,1,1,8,8,128]{5,4,3,2,1,0:T(8,128)S(1)}, u32[]{:S(2)}, u32[]{:S(2)}) %collective-permute-start.10) | collective-permute-done | bytes 32800 | tf_op jit(solution)/shard_map/ppermute | solution.py:16
  66.2 2.1 %collective-permute-start.11 = (f32[1,1,1,8,8,128]{5,4,3,2,1,0:T(8,128)S(1)}, f32[1,1,1,8,8,128]{5,4,3,2,1,0:T(8,128)S(1)}, u32[]{:S(2)}, u32[]{:S(2)}) collective-permute-start(f32[1,1,1,8,8,128]{5,4,3,2,1,0:T(8,128)S(1)} %get-tuple-element.43), channel_id=1, source_target_pairs={{1,0},{2,1},{3,2},{5,4},{6,5},{7,6},{9,8},{10,9},{11,10},{13,12},{... | collective-permute-start | bytes 98312 | tf_op jit(solution)/shard_map/ppermute | solution.py:19
  68.4 1.3 collective-permute-done.11
  71.8 3.6 %collective-permute-start.12 = (f32[1,1,1,8,8,128]{5,4,3,2,1,0:T(8,128)S(1)}, f32[1,1,1,8,8,128]{5,4,3,2,1,0:T(8,128)S(1)}, u32[]{:S(2)}, u32[]{:S(2)}) collective-permute-start(f32[1,1,1,8,8,128]{5,4,3,2,1,0:T(8,128)S(1)} %get-tuple-element.67), channel_id=1, source_target_pairs={{0,4},{4,8},{8,12},{12,16},{16,20},{20,24},{24,28},{1,5},{5,9},{9,... | collective-permute-start | bytes 98312 | tf_op jit(solution)/shard_map/ppermute | solution.py:16
  75.4 1.3 collective-permute-start.13
  77.0 4.2 %collective-permute-done.13 = f32[1,1,1,8,8,128]{5,4,3,2,1,0:T(8,128)S(1)} collective-permute-done((f32[1,1,1,8,8,128]{5,4,3,2,1,0:T(8,128)S(1)}, f32[1,1,1,8,8,128]{5,4,3,2,1,0:T(8,128)S(1)}, u32[]{:S(2)}, u32[]{:S(2)}) %collective-permute-start.13) | collective-permute-done | bytes 32800 | tf_op jit(solution)/shard_map/ppermute | solution.py:19
  81.2 1.9 %collective-permute-start.14 = (f32[1,1,1,8,8,128]{5,4,3,2,1,0:T(8,128)S(1)}, f32[1,1,1,8,8,128]{5,4,3,2,1,0:T(8,128)S(1)}, u32[]{:S(2)}, u32[]{:S(2)}) collective-permute-start(f32[1,1,1,8,8,128]{5,4,3,2,1,0:T(8,128)S(1)} %maximum_bitcast_fusion.15), channel_id=1, source_target_pairs={{0,1},{1,2},{2,3},{4,5},{5,6},{6,7},{8,9},{9,10},{10,11},{12,13},{... | collective-permute-start | bytes 98312 | tf_op jit(solution)/shard_map/ppermute | solution.py:16
  83.2 1.9 %fusion.15 = f32[768,4096]{1,0:T(8,128)S(1)} fusion(s32[4096]{0:T(1024)S(1)} %bitcast.479, bf16[256,256]{1,0:T(8,128)(2,1)S(1)} %get-tuple-element.61, bf16[256,256]{1,0:T(8,128)(2,1)S(1)} %get-tuple-element.62, bf16[256,256]{1,0:T(8,128)(2,1)S(1)} %get-tuple-element.60), kind=kOutput, calls=%fused_computation.19 | convolution fusion | flops 1612840960 | bytes 12992512 | tf_op jit(solution)/shard_map/dot_general | solution.py:153
  85.1 1.4 %collective-permute-done.14 = f32[1,1,1,8,8,128]{5,4,3,2,1,0:T(8,128)S(1)} collective-permute-done((f32[1,1,1,8,8,128]{5,4,3,2,1,0:T(8,128)S(1)}, f32[1,1,1,8,8,128]{5,4,3,2,1,0:T(8,128)S(1)}, u32[]{:S(2)}, u32[]{:S(2)}) %collective-permute-start.14) | collective-permute-done | bytes 32800 | tf_op jit(solution)/shard_map/ppermute | solution.py:16
  86.5 2.2 %collective-permute-start.15 = (f32[1,1,1,8,8,128]{5,4,3,2,1,0:T(8,128)S(1)}, f32[1,1,1,8,8,128]{5,4,3,2,1,0:T(8,128)S(1)}, u32[]{:S(2)}, u32[]{:S(2)}) collective-permute-start(f32[1,1,1,8,8,128]{5,4,3,2,1,0:T(8,128)S(1)} %get-tuple-element.39), channel_id=1, source_target_pairs={{1,0},{2,1},{3,2},{5,4},{6,5},{7,6},{9,8},{10,9},{11,10},{13,12},{... | collective-permute-start | bytes 98312 | tf_op jit(solution)/shard_map/ppermute | solution.py:19
  88.7 1.4 fusion.9
  91.8 1.3 fusion.14
  93.1 0.9 fusion.7
  94.1 0.9 fusion.17
  94.9 1.4 %fusion.10 = f32[512,256]{1,0:T(8,128)S(1)} fusion(bf16[256,4096]{1,0:T(8,128)(2,1)S(1)} %get-tuple-element.84, bf16[256,4096]{1,0:T(8,128)(2,1)S(1)} %get-tuple-element.83, s32[4096]{0:T(1024)S(1)} %add_select_fusion), kind=kOutput, calls=%fused_computation.13 | convolution fusion | flops 1083179008 | bytes 4734976 | tf_op jit(solution)/shard_map/dot_general | solution.py:167
  96.5 1.2 copy.258
  97.7 5.1 %all-to-all-start = ((f32[32,2,2048]{2,1,0:T(2,128)}), f32[32,2,2048]{2,1,0:T(2,128)S(1)}, u32[]{:S(2)}, u32[]{:S(2)}) async-start(f32[32,2,2048]{2,1,0:T(2,128)} %bitcast.112), calls=%async_computation | async-start | bytes 1048576 | tf_op jit(solution)/shard_map/all_to_all | solution.py:182
  104.1 3.4 %collective-permute-start.16 = (f32[1,1,1,8,8,128]{5,4,3,2,1,0:T(8,128)S(1)}, f32[1,1,1,8,8,128]{5,4,3,2,1,0:T(8,128)S(1)}, u32[]{:S(2)}, u32[]{:S(2)}) collective-permute-start(f32[1,1,1,8,8,128]{5,4,3,2,1,0:T(8,128)S(1)} %get-tuple-element.58), channel_id=1, source_target_pairs={{0,4},{4,8},{8,12},{12,16},{16,20},{20,24},{24,28},{1,5},{5,9},{9,... | collective-permute-start | bytes 98312 | tf_op jit(solution)/shard_map/ppermute | solution.py:16
  107.5 1.3 collective-permute-start.17
  109.2 4.5 %collective-permute-done.17 = f32[1,1,1,8,8,128]{5,4,3,2,1,0:T(8,128)S(1)} collective-permute-done((f32[1,1,1,8,8,128]{5,4,3,2,1,0:T(8,128)S(1)}, f32[1,1,1,8,8,128]{5,4,3,2,1,0:T(8,128)S(1)}, u32[]{:S(2)}, u32[]{:S(2)}) %collective-permute-start.17) | collective-permute-done | bytes 32800 | tf_op jit(solution)/shard_map/ppermute | solution.py:19
  113.8 4.1 %all-to-all-done = f32[32,2,2048]{2,1,0:T(2,128)S(1)} async-done(((f32[32,2,2048]{2,1,0:T(2,128)}), f32[32,2,2048]{2,1,0:T(2,128)S(1)}, u32[]{:S(2)}, u32[]{:S(2)}) %all-to-all-start) | async-done | bytes 524320 | tf_op jit(solution)/shard_map/all_to_all | solution.py:182
  118.0 2.0 %collective-permute-start.18 = (f32[1,1,1,8,8,128]{5,3,4,2,1,0:T(8,128)S(1)}, f32[1,1,1,8,8,128]{5,3,4,2,1,0:T(8,128)S(1)}, u32[]{:S(2)}, u32[]{:S(2)}) collective-permute-start(f32[1,1,1,8,8,128]{5,3,4,2,1,0:T(8,128)S(1)} %maximum_bitcast_fusion.13), channel_id=1, source_target_pairs={{0,1},{1,2},{2,3},{4,5},{5,6},{6,7},{8,9},{9,10},{10,11},{12,13},{... | collective-permute-start | bytes 98312 | tf_op jit(solution)/shard_map/ppermute | solution.py:16
  120.0 3.3 %collective-permute-done.18 = f32[1,1,1,8,8,128]{5,3,4,2,1,0:T(8,128)S(1)} collective-permute-done((f32[1,1,1,8,8,128]{5,3,4,2,1,0:T(8,128)S(1)}, f32[1,1,1,8,8,128]{5,3,4,2,1,0:T(8,128)S(1)}, u32[]{:S(2)}, u32[]{:S(2)}) %collective-permute-start.18) | collective-permute-done | bytes 32800 | tf_op jit(solution)/shard_map/ppermute | solution.py:16
  123.3 1.9 %collective-permute-start.19 = (f32[1,1,1,8,8,128]{5,3,4,2,1,0:T(8,128)S(1)}, f32[1,1,1,8,8,128]{5,3,4,2,1,0:T(8,128)S(1)}, u32[]{:S(2)}, u32[]{:S(2)}) collective-permute-start(f32[1,1,1,8,8,128]{5,3,4,2,1,0:T(8,128)S(1)} %get-tuple-element.33), channel_id=1, source_target_pairs={{1,0},{2,1},{3,2},{5,4},{6,5},{7,6},{9,8},{10,9},{11,10},{13,12},{... | collective-permute-start | bytes 98312 | tf_op jit(solution)/shard_map/ppermute | solution.py:19
  126.0 3.4 %all-to-all-start.1 = ((f32[2,8,2048]{2,0,1:T(2,128)}), f32[2,8,2048]{2,0,1:T(2,128)S(1)}, u32[]{:S(2)}, u32[]{:S(2)}) async-start(f32[2,8,2048]{2,0,1:T(2,128)} %broadcast_in_dim.213), calls=%async_computation.1 | async-start | bytes 262144 | tf_op jit(solution)/shard_map/all_to_all | solution.py:189
  130.4 6.8 %all-to-all-done.1 = f32[2,8,2048]{2,0,1:T(2,128)S(1)} async-done(((f32[2,8,2048]{2,0,1:T(2,128)}), f32[2,8,2048]{2,0,1:T(2,128)S(1)}, u32[]{:S(2)}, u32[]{:S(2)}) %all-to-all-start.1) | async-done | bytes 131104 | tf_op jit(solution)/shard_map/all_to_all | solution.py:189
  (135 shorter events, 18.8 us)
Async XLA Ops:
  0.6 10.6 %copy-start = (f32[1,1,8,8,8,128]{5,4,3,2,1,0:T(8,128)S(1)}, f32[1,1,8,8,8,128]{5,4,3,2,1,0:T(8,128)}, u32[]{:S(2)}) copy-start(f32[1,1,8,8,8,128]{5,4,3,2,1,0:T(8,128)} %param.36) | copy-start | bytes 786436
  4.9 6.3 %collective-permute-start = (f32[2,1,1,8,8,128]{5,0,4,3,2,1:T(2,128)S(1)}, f32[2,1,1,8,8,128]{5,0,4,3,2,1:T(2,128)S(1)}, u32[]{:S(2)}, u32[]{:S(2)}) collective-permute-start(f32[2,1,1,8,8,128]{5,0,4,3,2,1:T(2,128)S(1)} %maximum_bitcast_fusion.9), channel_id=1, source_target_pairs={{0,4},{4,8},{8,12},{12,16},{16,20},{20,24},{24,28},{1,5},{5,9},{9,... | collective-permute-start | bytes 196616 | tf_op jit(solution)/shard_map/ppermute | solution.py:16
  10.0 9.5 %copy-start.4 = (s32[1,4096,1]{1,2,0:T(1,128)S(1)}, s32[1,4096,1]{1,2,0:T(1,128)}, u32[]{:S(2)}) copy-start(s32[1,4096,1]{1,2,0:T(1,128)} %param.39) | copy-start | bytes 49156
  11.3 6.2 %collective-permute-start.1 = (f32[2,1,1,8,8,128]{5,0,4,3,2,1:T(2,128)S(1)}, f32[2,1,1,8,8,128]{5,0,4,3,2,1:T(2,128)S(1)}, u32[]{:S(2)}, u32[]{:S(2)}) collective-permute-start(f32[2,1,1,8,8,128]{5,0,4,3,2,1:T(2,128)S(1)} %get-tuple-element.51), channel_id=1, source_target_pairs={{4,0},{8,4},{12,8},{16,12},{20,16},{24,20},{28,24},{5,1},{9,5},{13... | collective-permute-start | bytes 196616 | tf_op jit(solution)/shard_map/ppermute | solution.py:19
  17.6 5.6 %collective-permute-start.2 = (f32[2,1,1,8,8,128]{5,3,0,4,2,1:T(8,128)S(1)}, f32[2,1,1,8,8,128]{5,3,0,4,2,1:T(8,128)S(1)}, u32[]{:S(2)}, u32[]{:S(2)}) collective-permute-start(f32[2,1,1,8,8,128]{5,3,0,4,2,1:T(8,128)S(1)} %maximum_bitcast_fusion.7), channel_id=1, source_target_pairs={{0,1},{1,2},{2,3},{4,5},{5,6},{6,7},{8,9},{9,10},{10,11},{12,13},{... | collective-permute-start | bytes 196616 | tf_op jit(solution)/shard_map/ppermute | solution.py:16
  23.2 4.7 %copy-start.1 = (f32[8,8,1,1]{1,0,3,2:T(8,128)S(1)}, f32[8,8,1,1]{1,0,3,2:T(8,128)}, u32[]{:S(2)}) copy-start(f32[8,8,1,1]{1,0,3,2:T(8,128)} %constant.130) | copy-start | bytes 772
  23.2 3.8 %collective-permute-start.3 = (f32[2,1,1,8,8,128]{5,3,0,4,2,1:T(8,128)S(1)}, f32[2,1,1,8,8,128]{5,3,0,4,2,1:T(8,128)S(1)}, u32[]{:S(2)}, u32[]{:S(2)}) collective-permute-start(f32[2,1,1,8,8,128]{5,3,0,4,2,1:T(8,128)S(1)} %get-tuple-element.49), channel_id=1, source_target_pairs={{1,0},{2,1},{3,2},{5,4},{6,5},{7,6},{9,8},{10,9},{11,10},{13,12},{... | collective-permute-start | bytes 196616 | tf_op jit(solution)/shard_map/ppermute | solution.py:19
  25.3 3.4 %copy-start.6 = (f32[8]{0:T(128)S(1)}, f32[8]{0:T(128)}, u32[]{:S(2)}) copy-start(f32[8]{0:T(128)} %constant.125) | copy-start | bytes 100
  27.2 8.2 %copy-start.2 = (s32[1,4096]{1,0:T(1,128)S(1)}, s32[1,4096]{1,0:T(1,128)}, u32[]{:S(2)}) copy-start(s32[1,4096]{1,0:T(1,128)} %param.40) | copy-start | bytes 49156
  29.8 5.9 %collective-permute-start.4 = (f32[1,1,1,8,8,128]{5,4,3,2,1,0:T(8,128)S(1)}, f32[1,1,1,8,8,128]{5,4,3,2,1,0:T(8,128)S(1)}, u32[]{:S(2)}, u32[]{:S(2)}) collective-permute-start(f32[1,1,1,8,8,128]{5,4,3,2,1,0:T(8,128)S(1)} %bitcast.485), channel_id=1, source_target_pairs={{0,4},{4,8},{8,12},{12,16},{16,20},{20,24},{24,28},{1,5},{5,9},{9,... | collective-permute-start | bytes 98312 | tf_op jit(solution)/shard_map/ppermute | solution.py:16
  34.1 5.8 %collective-permute-start.5 = (f32[1,1,1,8,8,128]{5,4,3,2,1,0:T(8,128)S(1)}, f32[1,1,1,8,8,128]{5,4,3,2,1,0:T(8,128)S(1)}, u32[]{:S(2)}, u32[]{:S(2)}) collective-permute-start(f32[1,1,1,8,8,128]{5,4,3,2,1,0:T(8,128)S(1)} %bitcast.487), channel_id=1, source_target_pairs={{4,0},{8,4},{12,8},{16,12},{20,16},{24,20},{28,24},{5,1},{9,5},{13... | collective-permute-start | bytes 98312 | tf_op jit(solution)/shard_map/ppermute | solution.py:19
  39.9 5.2 %collective-permute-start.6 = (f32[1,1,1,8,8,128]{5,3,4,2,1,0:T(8,128)S(1)}, f32[1,1,1,8,8,128]{5,3,4,2,1,0:T(8,128)S(1)}, u32[]{:S(2)}, u32[]{:S(2)}) collective-permute-start(f32[1,1,1,8,8,128]{5,3,4,2,1,0:T(8,128)S(1)} %maximum_bitcast_fusion.19), channel_id=1, source_target_pairs={{0,1},{1,2},{2,3},{4,5},{5,6},{6,7},{8,9},{9,10},{10,11},{12,13},{... | collective-permute-start | bytes 98312 | tf_op jit(solution)/shard_map/ppermute | solution.py:16
  45.2 17.7 %copy-start.3 = (s32[1,4096]{1,0:T(1,128)S(1)}, s32[1,4096]{1,0:T(1,128)}, u32[]{:S(2)}) copy-start(s32[1,4096]{1,0:T(1,128)} %param.38) | copy-start | bytes 49156
  45.2 3.9 %collective-permute-start.7 = (f32[1,1,1,8,8,128]{5,3,4,2,1,0:T(8,128)S(1)}, f32[1,1,1,8,8,128]{5,3,4,2,1,0:T(8,128)S(1)}, u32[]{:S(2)}, u32[]{:S(2)}) collective-permute-start(f32[1,1,1,8,8,128]{5,3,4,2,1,0:T(8,128)S(1)} %get-tuple-element.45), channel_id=1, source_target_pairs={{1,0},{2,1},{3,2},{5,4},{6,5},{7,6},{9,8},{10,9},{11,10},{13,12},{... | collective-permute-start | bytes 98312 | tf_op jit(solution)/shard_map/ppermute | solution.py:19
  51.0 5.7 %collective-permute-start.8 = (f32[1,1,1,8,8,128]{5,4,3,2,1,0:T(8,128)S(1)}, f32[1,1,1,8,8,128]{5,4,3,2,1,0:T(8,128)S(1)}, u32[]{:S(2)}, u32[]{:S(2)}) collective-permute-start(f32[1,1,1,8,8,128]{5,4,3,2,1,0:T(8,128)S(1)} %get-tuple-element.73), channel_id=1, source_target_pairs={{0,4},{4,8},{8,12},{12,16},{16,20},{20,24},{24,28},{1,5},{5,9},{9,... | collective-permute-start | bytes 98312 | tf_op jit(solution)/shard_map/ppermute | solution.py:16
  55.1 5.8 %collective-permute-start.9 = (f32[1,1,1,8,8,128]{5,4,3,2,1,0:T(8,128)S(1)}, f32[1,1,1,8,8,128]{5,4,3,2,1,0:T(8,128)S(1)}, u32[]{:S(2)}, u32[]{:S(2)}) collective-permute-start(f32[1,1,1,8,8,128]{5,4,3,2,1,0:T(8,128)S(1)} %get-tuple-element.74), channel_id=1, source_target_pairs={{4,0},{8,4},{12,8},{16,12},{20,16},{24,20},{28,24},{5,1},{9,5},{13... | collective-permute-start | bytes 98312 | tf_op jit(solution)/shard_map/ppermute | solution.py:19
  60.9 5.2 %collective-permute-start.10 = (f32[1,1,1,8,8,128]{5,4,3,2,1,0:T(8,128)S(1)}, f32[1,1,1,8,8,128]{5,4,3,2,1,0:T(8,128)S(1)}, u32[]{:S(2)}, u32[]{:S(2)}) collective-permute-start(f32[1,1,1,8,8,128]{5,4,3,2,1,0:T(8,128)S(1)} %maximum_bitcast_fusion.17), channel_id=1, source_target_pairs={{0,1},{1,2},{2,3},{4,5},{5,6},{6,7},{8,9},{9,10},{10,11},{12,13},{... | collective-permute-start | bytes 98312 | tf_op jit(solution)/shard_map/ppermute | solution.py:16
  66.2 3.5 %collective-permute-start.11 = (f32[1,1,1,8,8,128]{5,4,3,2,1,0:T(8,128)S(1)}, f32[1,1,1,8,8,128]{5,4,3,2,1,0:T(8,128)S(1)}, u32[]{:S(2)}, u32[]{:S(2)}) collective-permute-start(f32[1,1,1,8,8,128]{5,4,3,2,1,0:T(8,128)S(1)} %get-tuple-element.43), channel_id=1, source_target_pairs={{1,0},{2,1},{3,2},{5,4},{6,5},{7,6},{9,8},{10,9},{11,10},{13,12},{... | collective-permute-start | bytes 98312 | tf_op jit(solution)/shard_map/ppermute | solution.py:19
  71.8 5.2 %collective-permute-start.12 = (f32[1,1,1,8,8,128]{5,4,3,2,1,0:T(8,128)S(1)}, f32[1,1,1,8,8,128]{5,4,3,2,1,0:T(8,128)S(1)}, u32[]{:S(2)}, u32[]{:S(2)}) collective-permute-start(f32[1,1,1,8,8,128]{5,4,3,2,1,0:T(8,128)S(1)} %get-tuple-element.67), channel_id=1, source_target_pairs={{0,4},{4,8},{8,12},{12,16},{16,20},{20,24},{24,28},{1,5},{5,9},{9,... | collective-permute-start | bytes 98312 | tf_op jit(solution)/shard_map/ppermute | solution.py:16
  75.4 5.8 %collective-permute-start.13 = (f32[1,1,1,8,8,128]{5,4,3,2,1,0:T(8,128)S(1)}, f32[1,1,1,8,8,128]{5,4,3,2,1,0:T(8,128)S(1)}, u32[]{:S(2)}, u32[]{:S(2)}) collective-permute-start(f32[1,1,1,8,8,128]{5,4,3,2,1,0:T(8,128)S(1)} %get-tuple-element.68), channel_id=1, source_target_pairs={{4,0},{8,4},{12,8},{16,12},{20,16},{24,20},{28,24},{5,1},{9,5},{13... | collective-permute-start | bytes 98312 | tf_op jit(solution)/shard_map/ppermute | solution.py:19
  81.2 5.2 %collective-permute-start.14 = (f32[1,1,1,8,8,128]{5,4,3,2,1,0:T(8,128)S(1)}, f32[1,1,1,8,8,128]{5,4,3,2,1,0:T(8,128)S(1)}, u32[]{:S(2)}, u32[]{:S(2)}) collective-permute-start(f32[1,1,1,8,8,128]{5,4,3,2,1,0:T(8,128)S(1)} %maximum_bitcast_fusion.15), channel_id=1, source_target_pairs={{0,1},{1,2},{2,3},{4,5},{5,6},{6,7},{8,9},{9,10},{10,11},{12,13},{... | collective-permute-start | bytes 98312 | tf_op jit(solution)/shard_map/ppermute | solution.py:16
  86.5 3.8 %collective-permute-start.15 = (f32[1,1,1,8,8,128]{5,4,3,2,1,0:T(8,128)S(1)}, f32[1,1,1,8,8,128]{5,4,3,2,1,0:T(8,128)S(1)}, u32[]{:S(2)}, u32[]{:S(2)}) collective-permute-start(f32[1,1,1,8,8,128]{5,4,3,2,1,0:T(8,128)S(1)} %get-tuple-element.39), channel_id=1, source_target_pairs={{1,0},{2,1},{3,2},{5,4},{6,5},{7,6},{9,8},{10,9},{11,10},{13,12},{... | collective-permute-start | bytes 98312 | tf_op jit(solution)/shard_map/ppermute | solution.py:19
  93.1 0.9 copy-start.5
  97.7 20.1 %all-to-all-start = ((f32[32,2,2048]{2,1,0:T(2,128)}), f32[32,2,2048]{2,1,0:T(2,128)S(1)}, u32[]{:S(2)}, u32[]{:S(2)}) async-start(f32[32,2,2048]{2,1,0:T(2,128)} %bitcast.112), calls=%async_computation | async-start | bytes 1048576 | tf_op jit(solution)/shard_map/all_to_all | solution.py:182
  104.1 5.1 %collective-permute-start.16 = (f32[1,1,1,8,8,128]{5,4,3,2,1,0:T(8,128)S(1)}, f32[1,1,1,8,8,128]{5,4,3,2,1,0:T(8,128)S(1)}, u32[]{:S(2)}, u32[]{:S(2)}) collective-permute-start(f32[1,1,1,8,8,128]{5,4,3,2,1,0:T(8,128)S(1)} %get-tuple-element.58), channel_id=1, source_target_pairs={{0,4},{4,8},{8,12},{12,16},{16,20},{20,24},{24,28},{1,5},{5,9},{9,... | collective-permute-start | bytes 98312 | tf_op jit(solution)/shard_map/ppermute | solution.py:16
  107.5 6.2 %collective-permute-start.17 = (f32[1,1,1,8,8,128]{5,4,3,2,1,0:T(8,128)S(1)}, f32[1,1,1,8,8,128]{5,4,3,2,1,0:T(8,128)S(1)}, u32[]{:S(2)}, u32[]{:S(2)}) collective-permute-start(f32[1,1,1,8,8,128]{5,4,3,2,1,0:T(8,128)S(1)} %get-tuple-element.59), channel_id=1, source_target_pairs={{4,0},{8,4},{12,8},{16,12},{20,16},{24,20},{28,24},{5,1},{9,5},{13... | collective-permute-start | bytes 98312 | tf_op jit(solution)/shard_map/ppermute | solution.py:19
  118.0 5.2 %collective-permute-start.18 = (f32[1,1,1,8,8,128]{5,3,4,2,1,0:T(8,128)S(1)}, f32[1,1,1,8,8,128]{5,3,4,2,1,0:T(8,128)S(1)}, u32[]{:S(2)}, u32[]{:S(2)}) collective-permute-start(f32[1,1,1,8,8,128]{5,3,4,2,1,0:T(8,128)S(1)} %maximum_bitcast_fusion.13), channel_id=1, source_target_pairs={{0,1},{1,2},{2,3},{4,5},{5,6},{6,7},{8,9},{9,10},{10,11},{12,13},{... | collective-permute-start | bytes 98312 | tf_op jit(solution)/shard_map/ppermute | solution.py:16
  123.3 6.1 %collective-permute-start.19 = (f32[1,1,1,8,8,128]{5,3,4,2,1,0:T(8,128)S(1)}, f32[1,1,1,8,8,128]{5,3,4,2,1,0:T(8,128)S(1)}, u32[]{:S(2)}, u32[]{:S(2)}) collective-permute-start(f32[1,1,1,8,8,128]{5,3,4,2,1,0:T(8,128)S(1)} %get-tuple-element.33), channel_id=1, source_target_pairs={{1,0},{2,1},{3,2},{5,4},{6,5},{7,6},{9,8},{10,9},{11,10},{13,12},{... | collective-permute-start | bytes 98312 | tf_op jit(solution)/shard_map/ppermute | solution.py:19
  126.0 11.2 %all-to-all-start.1 = ((f32[2,8,2048]{2,0,1:T(2,128)}), f32[2,8,2048]{2,0,1:T(2,128)S(1)}, u32[]{:S(2)}, u32[]{:S(2)}) async-start(f32[2,8,2048]{2,0,1:T(2,128)} %broadcast_in_dim.213), calls=%async_computation.1 | async-start | bytes 262144 | tf_op jit(solution)/shard_map/all_to_all | solution.py:189

commit v17 on v12

--- a/solution.py
+++ b/solution.py
@@ -114,7 +114,7 @@
     )
 
 
-def assemble(values_in, ride=None):
+def assemble(values_in, ride=None, then=None):
     lower, upper = faces(values_in, 3)
     rim_faces = jnp.concatenate([lower, upper], 1)
     padded = padded_2(rim_faces, (("ex", 1),), 1)
@@ -123,6 +123,9 @@
     values_in = combine(values_in, 3, 1, lower, upper, padded[:, :1], padded[:, 3:])
     lower, upper = faces(values_in, 4)
     rim_faces = jnp.concatenate([lower, upper], 2)
+    if then is not None:
+        ride = then(ride)
+        rim_faces, ride = lax.optimization_barrier((rim_faces, ride))
     padded = padded_2(rim_faces, (("ey", 2),), 1)
     values_in = combine(values_in, 4, 2, lower, upper, padded[:, :, :1], padded[:, :, 3:])
     lower, upper = faces(values_in, 5)
@@ -182,10 +185,12 @@
     return lax.all_to_all(chunks, ("ex", "ey"), 0, 0, tiled=True).sum(0)
 
 
-def strip_gather(mine, strip_size):
-    n_ex = lax.axis_size("ex")
-    count, piece = mine.shape
-    spread_out = jnp.broadcast_to(mine[None], (n_ex, 2, piece))
+def strip_spread(mine):
+    return jnp.broadcast_to(mine[None], (lax.axis_size("ex"),) + mine.shape)
+
+
+def strip_gather(spread_out, strip_size):
+    n_ex, count, piece = spread_out.shape
     whole = lax.all_to_all(spread_out, "ex", 0, 0, tiled=True)
     return whole.transpose(1, 0, 2).reshape(2, n_ex * piece)[:, :strip_size]
 
@@ -217,7 +222,7 @@
             samples = early + gather_flat(update.reshape(-1), picks, 256, 2)
             numer = segment_sum(areas * samples, global_ids, strips * SHELL_STRIP, 256, 2)
             partial = jnp.stack([numer, denom])
-            assembled, mine = assemble(applied[None], strip_reduce(partial, strips, SHELL_STRIP))
+            assembled, mine = assemble(applied[None], strip_reduce(partial, strips, SHELL_STRIP), strip_spread)
         else:
             assembled, _ = assemble(applied[None])
         assembled = assembled[0]

time: 139 us -> 137 us (0.986)
  waiting for transfers between devices: 50.5 us -> 46.8 us
  starting transfers between devices: 54 us -> 55.7 us
    ppermute x10, waiting for transfers between devices: 13.9 us -> 10.6 us  [padded_2(): lax.ppermute(lax.slice_in_dim(block, block.shape[dim] - width, None, axis...]
    ppermute x10, starting transfers between devices: 16.9 us -> 18.6 us  [padded_2(): lax.ppermute(lax.slice_in_dim(block, 0, width, axis=dim), axis, backward)]
  transfers between devices with their start and end apart: 22 -> 22, of which waited for: 20 -> 19; matrix products, arithmetic and copies ran while one was open for 9% -> 9% of each run, Pallas kernels for 0% -> 0%
where the time goes in v17:
time: 137 us; the launch traced here: 136 us
  starting transfers between devices  55.7 us (41%)
  waiting for transfers between devices  46.8 us (34%)
  other arithmetic  14.5 us (11%)
  matrix products  12 us (9%)
  local copies, waits for them, and re-layouts  5.33 us (4%)
  between operations  1.63 us (1%)
    ppermute x10, starting transfers between devices, padded_2(): lax.ppermute(lax.slice_in_dim(block, block.shape[dim] - width, None, axis...  28.5 us
    ppermute x10, waiting for transfers between devices, padded_2(): lax.ppermute(lax.slice_in_dim(block, 0, width, axis=dim), axis, backward)  25.8 us
    ppermute x10, starting transfers between devices, padded_2(): lax.ppermute(lax.slice_in_dim(block, 0, width, axis=dim), axis, backward)  18.6 us
    ppermute x10, waiting for transfers between devices, padded_2(): lax.ppermute(lax.slice_in_dim(block, block.shape[dim] - width, None, axis...  10.6 us
    all_to_all x1, waiting for transfers between devices, strip_gather(): whole = lax.all_to_all(spread_out, 'ex', 0, 0, tiled=True)  6.31 us
    all_to_all x1, starting transfers between devices, strip_reduce(): return lax.all_to_all(chunks, ('ex', 'ey'), 0, 0, tiled=True).sum(0)  5.08 us
    all_to_all x1, waiting for transfers between devices, strip_reduce(): return lax.all_to_all(chunks, ('ex', 'ey'), 0, 0, tiled=True).sum(0)  4.09 us
    all_to_all x1, starting transfers between devices, strip_gather(): whole = lax.all_to_all(spread_out, 'ex', 0, 0, tiled=True)  3.46 us
  transfers between devices with their start and end apart: 22, of which 19 were waited for; matrix products, arithmetic and copies ran while one was open for 9% of the time, Pallas kernels for 0%

profile of v17, /device:TPU:2, one launch (start us, length us, event | category | flops | bytes accessed | tf_op | source)
XLA Modules:
  0.0 135.9 jit_solution(9135722904755714070)
XLA Ops:
  2.9 1.2 fusion.90
  4.9 3.4 %collective-permute-start = (f32[2,1,1,8,8,128]{5,0,4,3,2,1:T(2,128)S(1)}, f32[2,1,1,8,8,128]{5,0,4,3,2,1:T(2,128)S(1)}, u32[]{:S(2)}, u32[]{:S(2)}) collective-permute-start(f32[2,1,1,8,8,128]{5,0,4,3,2,1:T(2,128)S(1)} %maximum_bitcast_fusion.9), channel_id=1, source_target_pairs={{0,4},{4,8},{8,12},{12,16},{16,20},{20,24},{24,28},{1,5},{5,9},{9,... | collective-permute-start | bytes 196616 | tf_op jit(solution)/shard_map/ppermute | solution.py:16
  8.3 0.9 fusion.94
  10.0 1.2 fusion.20
  11.3 1.3 collective-permute-start.1
  13.3 4.3 %collective-permute-done.1 = f32[2,1,1,8,8,128]{5,0,4,3,2,1:T(2,128)S(1)} collective-permute-done((f32[2,1,1,8,8,128]{5,0,4,3,2,1:T(2,128)S(1)}, f32[2,1,1,8,8,128]{5,0,4,3,2,1:T(2,128)S(1)}, u32[]{:S(2)}, u32[]{:S(2)}) %collective-permute-start.1) | collective-permute-done | bytes 65568 | tf_op jit(solution)/shard_map/ppermute | solution.py:19
  17.6 1.9 %collective-permute-start.2 = (f32[2,1,1,8,8,128]{5,3,0,4,2,1:T(8,128)S(1)}, f32[2,1,1,8,8,128]{5,3,0,4,2,1:T(8,128)S(1)}, u32[]{:S(2)}, u32[]{:S(2)}) collective-permute-start(f32[2,1,1,8,8,128]{5,3,0,4,2,1:T(8,128)S(1)} %maximum_bitcast_fusion.7), channel_id=1, source_target_pairs={{0,1},{1,2},{2,3},{4,5},{5,6},{6,7},{8,9},{9,10},{10,11},{12,13},{... | collective-permute-start | bytes 196616 | tf_op jit(solution)/shard_map/ppermute | solution.py:16
  19.5 3.6 %collective-permute-done.2 = f32[2,1,1,8,8,128]{5,3,0,4,2,1:T(8,128)S(1)} collective-permute-done((f32[2,1,1,8,8,128]{5,3,0,4,2,1:T(8,128)S(1)}, f32[2,1,1,8,8,128]{5,3,0,4,2,1:T(8,128)S(1)}, u32[]{:S(2)}, u32[]{:S(2)}) %collective-permute-start.2) | collective-permute-done | bytes 65568 | tf_op jit(solution)/shard_map/ppermute | solution.py:16
  23.2 1.9 %collective-permute-start.3 = (f32[2,1,1,8,8,128]{5,3,0,4,2,1:T(8,128)S(1)}, f32[2,1,1,8,8,128]{5,3,0,4,2,1:T(8,128)S(1)}, u32[]{:S(2)}, u32[]{:S(2)}) collective-permute-start(f32[2,1,1,8,8,128]{5,3,0,4,2,1:T(8,128)S(1)} %get-tuple-element.48), channel_id=1, source_target_pairs={{1,0},{2,1},{3,2},{5,4},{6,5},{7,6},{9,8},{10,9},{11,10},{13,12},{... | collective-permute-start | bytes 196616 | tf_op jit(solution)/shard_map/ppermute | solution.py:19
  25.5 1.5 %collective-permute-done.3 = f32[2,1,1,8,8,128]{5,3,0,4,2,1:T(8,128)S(1)} collective-permute-done((f32[2,1,1,8,8,128]{5,3,0,4,2,1:T(8,128)S(1)}, f32[2,1,1,8,8,128]{5,3,0,4,2,1:T(8,128)S(1)}, u32[]{:S(2)}, u32[]{:S(2)}) %collective-permute-start.3) | collective-permute-done | bytes 65568 | tf_op jit(solution)/shard_map/ppermute | solution.py:19
  28.8 0.9 fusion.30
  29.8 4.3 %collective-permute-start.4 = (f32[1,1,1,8,8,128]{5,4,3,2,1,0:T(8,128)S(1)}, f32[1,1,1,8,8,128]{5,4,3,2,1,0:T(8,128)S(1)}, u32[]{:S(2)}, u32[]{:S(2)}) collective-permute-start(f32[1,1,1,8,8,128]{5,4,3,2,1,0:T(8,128)S(1)} %bitcast.484), channel_id=1, source_target_pairs={{0,4},{4,8},{8,12},{12,16},{16,20},{20,24},{24,28},{1,5},{5,9},{9,... | collective-permute-start | bytes 98312 | tf_op jit(solution)/shard_map/ppermute | solution.py:16
  34.1 1.3 collective-permute-start.5
  35.7 4.2 %collective-permute-done.5 = f32[1,1,1,8,8,128]{5,4,3,2,1,0:T(8,128)S(1)} collective-permute-done((f32[1,1,1,8,8,128]{5,4,3,2,1,0:T(8,128)S(1)}, f32[1,1,1,8,8,128]{5,4,3,2,1,0:T(8,128)S(1)}, u32[]{:S(2)}, u32[]{:S(2)}) %collective-permute-start.5) | collective-permute-done | bytes 32800 | tf_op jit(solution)/shard_map/ppermute | solution.py:19
  39.9 1.9 %collective-permute-start.6 = (f32[1,1,1,8,8,128]{5,3,4,2,1,0:T(8,128)S(1)}, f32[1,1,1,8,8,128]{5,3,4,2,1,0:T(8,128)S(1)}, u32[]{:S(2)}, u32[]{:S(2)}) collective-permute-start(f32[1,1,1,8,8,128]{5,3,4,2,1,0:T(8,128)S(1)} %maximum_bitcast_fusion.19), channel_id=1, source_target_pairs={{0,1},{1,2},{2,3},{4,5},{5,6},{6,7},{8,9},{9,10},{10,11},{12,13},{... | collective-permute-start | bytes 98312 | tf_op jit(solution)/shard_map/ppermute | solution.py:16
  41.9 1.9 %fusion = f32[768,256]{1,0:T(8,128)S(1)} fusion(bf16[256,4096]{1,0:T(8,128)(2,1)S(1)} %get-tuple-element.89, bf16[256,4096]{1,0:T(8,128)(2,1)S(1)} %get-tuple-element.90, bf16[256,4096]{1,0:T(8,128)(2,1)S(1)} %get-tuple-element.88, s32[4096]{0:T(1024)S(1)} %add_select_fusion), kind=kOutput, calls=%fused_computation | convolution fusion | flops 1630535680 | bytes 7094272 | tf_op jit(solution)/shard_map/dot_general | solution.py:170
  43.8 1.4 %collective-permute-done.6 = f32[1,1,1,8,8,128]{5,3,4,2,1,0:T(8,128)S(1)} collective-permute-done((f32[1,1,1,8,8,128]{5,3,4,2,1,0:T(8,128)S(1)}, f32[1,1,1,8,8,128]{5,3,4,2,1,0:T(8,128)S(1)}, u32[]{:S(2)}, u32[]{:S(2)}) %collective-permute-start.6) | collective-permute-done | bytes 32800 | tf_op jit(solution)/shard_map/ppermute | solution.py:16
  45.2 2.3 %collective-permute-start.7 = (f32[1,1,1,8,8,128]{5,3,4,2,1,0:T(8,128)S(1)}, f32[1,1,1,8,8,128]{5,3,4,2,1,0:T(8,128)S(1)}, u32[]{:S(2)}, u32[]{:S(2)}) collective-permute-start(f32[1,1,1,8,8,128]{5,3,4,2,1,0:T(8,128)S(1)} %get-tuple-element.44), channel_id=1, source_target_pairs={{1,0},{2,1},{3,2},{5,4},{6,5},{7,6},{9,8},{10,9},{11,10},{13,12},{... | collective-permute-start | bytes 98312 | tf_op jit(solution)/shard_map/ppermute | solution.py:19
  47.7 1.4 %collective-permute-done.7 = f32[1,1,1,8,8,128]{5,3,4,2,1,0:T(8,128)S(1)} collective-permute-done((f32[1,1,1,8,8,128]{5,3,4,2,1,0:T(8,128)S(1)}, f32[1,1,1,8,8,128]{5,3,4,2,1,0:T(8,128)S(1)}, u32[]{:S(2)}, u32[]{:S(2)}) %collective-permute-start.7) | collective-permute-done | bytes 32800 | tf_op jit(solution)/shard_map/ppermute | solution.py:19
  51.0 4.1 %collective-permute-start.8 = (f32[1,1,1,8,8,128]{5,4,3,2,1,0:T(8,128)S(1)}, f32[1,1,1,8,8,128]{5,4,3,2,1,0:T(8,128)S(1)}, u32[]{:S(2)}, u32[]{:S(2)}) collective-permute-start(f32[1,1,1,8,8,128]{5,4,3,2,1,0:T(8,128)S(1)} %get-tuple-element.74), channel_id=1, source_target_pairs={{0,4},{4,8},{8,12},{12,16},{16,20},{20,24},{24,28},{1,5},{5,9},{9,... | collective-permute-start | bytes 98312 | tf_op jit(solution)/shard_map/ppermute | solution.py:16
  55.1 1.3 collective-permute-start.9
  56.7 4.2 %collective-permute-done.9 = f32[1,1,1,8,8,128]{5,4,3,2,1,0:T(8,128)S(1)} collective-permute-done((f32[1,1,1,8,8,128]{5,4,3,2,1,0:T(8,128)S(1)}, f32[1,1,1,8,8,128]{5,4,3,2,1,0:T(8,128)S(1)}, u32[]{:S(2)}, u32[]{:S(2)}) %collective-permute-start.9) | collective-permute-done | bytes 32800 | tf_op jit(solution)/shard_map/ppermute | solution.py:19
  60.9 1.9 %collective-permute-start.10 = (f32[1,1,1,8,8,128]{5,4,3,2,1,0:T(8,128)S(1)}, f32[1,1,1,8,8,128]{5,4,3,2,1,0:T(8,128)S(1)}, u32[]{:S(2)}, u32[]{:S(2)}) collective-permute-start(f32[1,1,1,8,8,128]{5,4,3,2,1,0:T(8,128)S(1)} %maximum_bitcast_fusion.17), channel_id=1, source_target_pairs={{0,1},{1,2},{2,3},{4,5},{5,6},{6,7},{8,9},{9,10},{10,11},{12,13},{... | collective-permute-start | bytes 98312 | tf_op jit(solution)/shard_map/ppermute | solution.py:16
  62.9 3.2 %collective-permute-done.10 = f32[1,1,1,8,8,128]{5,4,3,2,1,0:T(8,128)S(1)} collective-permute-done((f32[1,1,1,8,8,128]{5,4,3,2,1,0:T(8,128)S(1)}, f32[1,1,1,8,8,128]{5,4,3,2,1,0:T(8,128)S(1)}, u32[]{:S(2)}, u32[]{:S(2)}) %collective-permute-start.10) | collective-permute-done | bytes 32800 | tf_op jit(solution)/shard_map/ppermute | solution.py:16
  66.2 2.1 %collective-permute-start.11 = (f32[1,1,1,8,8,128]{5,4,3,2,1,0:T(8,128)S(1)}, f32[1,1,1,8,8,128]{5,4,3,2,1,0:T(8,128)S(1)}, u32[]{:S(2)}, u32[]{:S(2)}) collective-permute-start(f32[1,1,1,8,8,128]{5,4,3,2,1,0:T(8,128)S(1)} %get-tuple-element.42), channel_id=1, source_target_pairs={{1,0},{2,1},{3,2},{5,4},{6,5},{7,6},{9,8},{10,9},{11,10},{13,12},{... | collective-permute-start | bytes 98312 | tf_op jit(solution)/shard_map/ppermute | solution.py:19
  68.4 1.3 collective-permute-done.11
  71.8 3.6 %collective-permute-start.12 = (f32[1,1,1,8,8,128]{5,4,3,2,1,0:T(8,128)S(1)}, f32[1,1,1,8,8,128]{5,4,3,2,1,0:T(8,128)S(1)}, u32[]{:S(2)}, u32[]{:S(2)}) collective-permute-start(f32[1,1,1,8,8,128]{5,4,3,2,1,0:T(8,128)S(1)} %get-tuple-element.68), channel_id=1, source_target_pairs={{0,4},{4,8},{8,12},{12,16},{16,20},{20,24},{24,28},{1,5},{5,9},{9,... | collective-permute-start | bytes 98312 | tf_op jit(solution)/shard_map/ppermute | solution.py:16
  75.4 1.3 collective-permute-start.13
  77.0 4.2 %collective-permute-done.13 = f32[1,1,1,8,8,128]{5,4,3,2,1,0:T(8,128)S(1)} collective-permute-done((f32[1,1,1,8,8,128]{5,4,3,2,1,0:T(8,128)S(1)}, f32[1,1,1,8,8,128]{5,4,3,2,1,0:T(8,128)S(1)}, u32[]{:S(2)}, u32[]{:S(2)}) %collective-permute-start.13) | collective-permute-done | bytes 32800 | tf_op jit(solution)/shard_map/ppermute | solution.py:19
  81.2 1.9 %collective-permute-start.14 = (f32[1,1,1,8,8,128]{5,4,3,2,1,0:T(8,128)S(1)}, f32[1,1,1,8,8,128]{5,4,3,2,1,0:T(8,128)S(1)}, u32[]{:S(2)}, u32[]{:S(2)}) collective-permute-start(f32[1,1,1,8,8,128]{5,4,3,2,1,0:T(8,128)S(1)} %maximum_bitcast_fusion.15), channel_id=1, source_target_pairs={{0,1},{1,2},{2,3},{4,5},{5,6},{6,7},{8,9},{9,10},{10,11},{12,13},{... | collective-permute-start | bytes 98312 | tf_op jit(solution)/shard_map/ppermute | solution.py:16
  83.2 1.9 %fusion.15 = f32[768,4096]{1,0:T(8,128)S(1)} fusion(s32[4096]{0:T(1024)S(1)} %bitcast.478, bf16[256,256]{1,0:T(8,128)(2,1)S(1)} %get-tuple-element.62, bf16[256,256]{1,0:T(8,128)(2,1)S(1)} %get-tuple-element.63, bf16[256,256]{1,0:T(8,128)(2,1)S(1)} %get-tuple-element.61), kind=kOutput, calls=%fused_computation.19 | convolution fusion | flops 1612840960 | bytes 12992512 | tf_op jit(solution)/shard_map/dot_general | solution.py:156
  85.1 1.4 %collective-permute-done.14 = f32[1,1,1,8,8,128]{5,4,3,2,1,0:T(8,128)S(1)} collective-permute-done((f32[1,1,1,8,8,128]{5,4,3,2,1,0:T(8,128)S(1)}, f32[1,1,1,8,8,128]{5,4,3,2,1,0:T(8,128)S(1)}, u32[]{:S(2)}, u32[]{:S(2)}) %collective-permute-start.14) | collective-permute-done | bytes 32800 | tf_op jit(solution)/shard_map/ppermute | solution.py:16
  86.5 2.2 %collective-permute-start.15 = (f32[1,1,1,8,8,128]{5,4,3,2,1,0:T(8,128)S(1)}, f32[1,1,1,8,8,128]{5,4,3,2,1,0:T(8,128)S(1)}, u32[]{:S(2)}, u32[]{:S(2)}) collective-permute-start(f32[1,1,1,8,8,128]{5,4,3,2,1,0:T(8,128)S(1)} %get-tuple-element.38), channel_id=1, source_target_pairs={{1,0},{2,1},{3,2},{5,4},{6,5},{7,6},{9,8},{10,9},{11,10},{13,12},{... | collective-permute-start | bytes 98312 | tf_op jit(solution)/shard_map/ppermute | solution.py:19
  88.7 1.4 fusion.9
  91.8 1.3 fusion.14
  93.1 0.9 fusion.7
  94.1 0.9 fusion.17
  94.9 1.4 %fusion.10 = f32[512,256]{1,0:T(8,128)S(1)} fusion(bf16[256,4096]{1,0:T(8,128)(2,1)S(1)} %get-tuple-element.87, bf16[256,4096]{1,0:T(8,128)(2,1)S(1)} %get-tuple-element.86, s32[4096]{0:T(1024)S(1)} %add_select_fusion), kind=kOutput, calls=%fused_computation.13 | convolution fusion | flops 1083179008 | bytes 4734976 | tf_op jit(solution)/shard_map/dot_general | solution.py:170
  96.5 1.2 copy.201
  97.7 5.1 %all-to-all-start = ((f32[32,2,2048]{2,1,0:T(2,128)}), f32[32,2,2048]{2,1,0:T(2,128)S(1)}, u32[]{:S(2)}, u32[]{:S(2)}) async-start(f32[32,2,2048]{2,1,0:T(2,128)} %bitcast.112), calls=%async_computation | async-start | bytes 1048576 | tf_op jit(solution)/shard_map/all_to_all | solution.py:185
  104.1 3.4 %collective-permute-start.16 = (f32[1,1,1,8,8,128]{5,4,3,2,1,0:T(8,128)S(1)}, f32[1,1,1,8,8,128]{5,4,3,2,1,0:T(8,128)S(1)}, u32[]{:S(2)}, u32[]{:S(2)}) collective-permute-start(f32[1,1,1,8,8,128]{5,4,3,2,1,0:T(8,128)S(1)} %get-tuple-element.59), channel_id=1, source_target_pairs={{0,4},{4,8},{8,12},{12,16},{16,20},{20,24},{24,28},{1,5},{5,9},{9,... | collective-permute-start | bytes 98312 | tf_op jit(solution)/shard_map/ppermute | solution.py:16
  107.5 1.3 collective-permute-start.17
  109.2 4.5 %collective-permute-done.17 = f32[1,1,1,8,8,128]{5,4,3,2,1,0:T(8,128)S(1)} collective-permute-done((f32[1,1,1,8,8,128]{5,4,3,2,1,0:T(8,128)S(1)}, f32[1,1,1,8,8,128]{5,4,3,2,1,0:T(8,128)S(1)}, u32[]{:S(2)}, u32[]{:S(2)}) %collective-permute-start.17) | collective-permute-done | bytes 32800 | tf_op jit(solution)/shard_map/ppermute | solution.py:19
  113.8 4.1 %all-to-all-done = f32[32,2,2048]{2,1,0:T(2,128)S(1)} async-done(((f32[32,2,2048]{2,1,0:T(2,128)}), f32[32,2,2048]{2,1,0:T(2,128)S(1)}, u32[]{:S(2)}, u32[]{:S(2)}) %all-to-all-start) | async-done | bytes 524320 | tf_op jit(solution)/shard_map/all_to_all | solution.py:185
  118.8 1.9 %collective-permute-start.18 = (f32[1,1,1,8,8,128]{5,3,4,2,1,0:T(8,128)S(1)}, f32[1,1,1,8,8,128]{5,3,4,2,1,0:T(8,128)S(1)}, u32[]{:S(2)}, u32[]{:S(2)}) collective-permute-start(f32[1,1,1,8,8,128]{5,3,4,2,1,0:T(8,128)S(1)} %get-tuple-element.82), channel_id=1, source_target_pairs={{0,1},{1,2},{2,3},{4,5},{5,6},{6,7},{8,9},{9,10},{10,11},{12,13},{... | collective-permute-start | bytes 98312 | tf_op jit(solution)/shard_map/ppermute | solution.py:16
  120.8 3.6 %collective-permute-start.19 = (f32[1,1,1,8,8,128]{5,3,4,2,1,0:T(8,128)S(1)}, f32[1,1,1,8,8,128]{5,3,4,2,1,0:T(8,128)S(1)}, u32[]{:S(2)}, u32[]{:S(2)}) collective-permute-start(f32[1,1,1,8,8,128]{5,3,4,2,1,0:T(8,128)S(1)} %get-tuple-element.83), channel_id=1, source_target_pairs={{1,0},{2,1},{3,2},{5,4},{6,5},{7,6},{9,8},{10,9},{11,10},{13,12},{... | collective-permute-start | bytes 98312 | tf_op jit(solution)/shard_map/ppermute | solution.py:19
  124.4 3.5 %all-to-all-start.1 = ((f32[8,2,2048]{2,1,0:T(2,128)}), f32[8,2,2048]{2,1,0:T(2,128)S(1)}, u32[]{:S(2)}, u32[]{:S(2)}) async-start(f32[8,2,2048]{2,1,0:T(2,128)} %broadcast_in_dim.209), calls=%async_computation.1 | async-start | bytes 262144 | tf_op jit(solution)/shard_map/all_to_all | solution.py:194
  128.9 6.3 %all-to-all-done.1 = f32[8,2,2048]{2,1,0:T(2,128)S(1)} async-done(((f32[8,2,2048]{2,1,0:T(2,128)}), f32[8,2,2048]{2,1,0:T(2,128)S(1)}, u32[]{:S(2)}, u32[]{:S(2)}) %all-to-all-start.1) | async-done | bytes 131104 | tf_op jit(solution)/shard_map/all_to_all | solution.py:194
  (137 shorter events, 18.0 us)
Async XLA Ops:
  0.6 10.6 %copy-start = (f32[1,1,8,8,8,128]{5,4,3,2,1,0:T(8,128)S(1)}, f32[1,1,8,8,8,128]{5,4,3,2,1,0:T(8,128)}, u32[]{:S(2)}) copy-start(f32[1,1,8,8,8,128]{5,4,3,2,1,0:T(8,128)} %param.36) | copy-start | bytes 786436
  4.9 6.3 %collective-permute-start = (f32[2,1,1,8,8,128]{5,0,4,3,2,1:T(2,128)S(1)}, f32[2,1,1,8,8,128]{5,0,4,3,2,1:T(2,128)S(1)}, u32[]{:S(2)}, u32[]{:S(2)}) collective-permute-start(f32[2,1,1,8,8,128]{5,0,4,3,2,1:T(2,128)S(1)} %maximum_bitcast_fusion.9), channel_id=1, source_target_pairs={{0,4},{4,8},{8,12},{12,16},{16,20},{20,24},{24,28},{1,5},{5,9},{9,... | collective-permute-start | bytes 196616 | tf_op jit(solution)/shard_map/ppermute | solution.py:16
  10.0 9.5 %copy-start.4 = (s32[1,4096,1]{1,2,0:T(1,128)S(1)}, s32[1,4096,1]{1,2,0:T(1,128)}, u32[]{:S(2)}) copy-start(s32[1,4096,1]{1,2,0:T(1,128)} %param.39) | copy-start | bytes 49156
  11.3 6.2 %collective-permute-start.1 = (f32[2,1,1,8,8,128]{5,0,4,3,2,1:T(2,128)S(1)}, f32[2,1,1,8,8,128]{5,0,4,3,2,1:T(2,128)S(1)}, u32[]{:S(2)}, u32[]{:S(2)}) collective-permute-start(f32[2,1,1,8,8,128]{5,0,4,3,2,1:T(2,128)S(1)} %get-tuple-element.50), channel_id=1, source_target_pairs={{4,0},{8,4},{12,8},{16,12},{20,16},{24,20},{28,24},{5,1},{9,5},{13... | collective-permute-start | bytes 196616 | tf_op jit(solution)/shard_map/ppermute | solution.py:19
  17.6 5.6 %collective-permute-start.2 = (f32[2,1,1,8,8,128]{5,3,0,4,2,1:T(8,128)S(1)}, f32[2,1,1,8,8,128]{5,3,0,4,2,1:T(8,128)S(1)}, u32[]{:S(2)}, u32[]{:S(2)}) collective-permute-start(f32[2,1,1,8,8,128]{5,3,0,4,2,1:T(8,128)S(1)} %maximum_bitcast_fusion.7), channel_id=1, source_target_pairs={{0,1},{1,2},{2,3},{4,5},{5,6},{6,7},{8,9},{9,10},{10,11},{12,13},{... | collective-permute-start | bytes 196616 | tf_op jit(solution)/shard_map/ppermute | solution.py:16
  23.2 4.7 %copy-start.1 = (f32[8,8,1,1]{1,0,3,2:T(8,128)S(1)}, f32[8,8,1,1]{1,0,3,2:T(8,128)}, u32[]{:S(2)}) copy-start(f32[8,8,1,1]{1,0,3,2:T(8,128)} %constant.130) | copy-start | bytes 772
  23.2 3.8 %collective-permute-start.3 = (f32[2,1,1,8,8,128]{5,3,0,4,2,1:T(8,128)S(1)}, f32[2,1,1,8,8,128]{5,3,0,4,2,1:T(8,128)S(1)}, u32[]{:S(2)}, u32[]{:S(2)}) collective-permute-start(f32[2,1,1,8,8,128]{5,3,0,4,2,1:T(8,128)S(1)} %get-tuple-element.48), channel_id=1, source_target_pairs={{1,0},{2,1},{3,2},{5,4},{6,5},{7,6},{9,8},{10,9},{11,10},{13,12},{... | collective-permute-start | bytes 196616 | tf_op jit(solution)/shard_map/ppermute | solution.py:19
  25.3 3.4 %copy-start.6 = (f32[8]{0:T(128)S(1)}, f32[8]{0:T(128)}, u32[]{:S(2)}) copy-start(f32[8]{0:T(128)} %constant.125) | copy-start | bytes 100
  27.2 8.2 %copy-start.2 = (s32[1,4096]{1,0:T(1,128)S(1)}, s32[1,4096]{1,0:T(1,128)}, u32[]{:S(2)}) copy-start(s32[1,4096]{1,0:T(1,128)} %param.40) | copy-start | bytes 49156
  29.8 5.9 %collective-permute-start.4 = (f32[1,1,1,8,8,128]{5,4,3,2,1,0:T(8,128)S(1)}, f32[1,1,1,8,8,128]{5,4,3,2,1,0:T(8,128)S(1)}, u32[]{:S(2)}, u32[]{:S(2)}) collective-permute-start(f32[1,1,1,8,8,128]{5,4,3,2,1,0:T(8,128)S(1)} %bitcast.484), channel_id=1, source_target_pairs={{0,4},{4,8},{8,12},{12,16},{16,20},{20,24},{24,28},{1,5},{5,9},{9,... | collective-permute-start | bytes 98312 | tf_op jit(solution)/shard_map/ppermute | solution.py:16
  34.1 5.8 %collective-permute-start.5 = (f32[1,1,1,8,8,128]{5,4,3,2,1,0:T(8,128)S(1)}, f32[1,1,1,8,8,128]{5,4,3,2,1,0:T(8,128)S(1)}, u32[]{:S(2)}, u32[]{:S(2)}) collective-permute-start(f32[1,1,1,8,8,128]{5,4,3,2,1,0:T(8,128)S(1)} %bitcast.486), channel_id=1, source_target_pairs={{4,0},{8,4},{12,8},{16,12},{20,16},{24,20},{28,24},{5,1},{9,5},{13... | collective-permute-start | bytes 98312 | tf_op jit(solution)/shard_map/ppermute | solution.py:19
  39.9 5.2 %collective-permute-start.6 = (f32[1,1,1,8,8,128]{5,3,4,2,1,0:T(8,128)S(1)}, f32[1,1,1,8,8,128]{5,3,4,2,1,0:T(8,128)S(1)}, u32[]{:S(2)}, u32[]{:S(2)}) collective-permute-start(f32[1,1,1,8,8,128]{5,3,4,2,1,0:T(8,128)S(1)} %maximum_bitcast_fusion.19), channel_id=1, source_target_pairs={{0,1},{1,2},{2,3},{4,5},{5,6},{6,7},{8,9},{9,10},{10,11},{12,13},{... | collective-permute-start | bytes 98312 | tf_op jit(solution)/shard_map/ppermute | solution.py:16
  45.2 17.7 %copy-start.3 = (s32[1,4096]{1,0:T(1,128)S(1)}, s32[1,4096]{1,0:T(1,128)}, u32[]{:S(2)}) copy-start(s32[1,4096]{1,0:T(1,128)} %param.38) | copy-start | bytes 49156
  45.2 3.9 %collective-permute-start.7 = (f32[1,1,1,8,8,128]{5,3,4,2,1,0:T(8,128)S(1)}, f32[1,1,1,8,8,128]{5,3,4,2,1,0:T(8,128)S(1)}, u32[]{:S(2)}, u32[]{:S(2)}) collective-permute-start(f32[1,1,1,8,8,128]{5,3,4,2,1,0:T(8,128)S(1)} %get-tuple-element.44), channel_id=1, source_target_pairs={{1,0},{2,1},{3,2},{5,4},{6,5},{7,6},{9,8},{10,9},{11,10},{13,12},{... | collective-permute-start | bytes 98312 | tf_op jit(solution)/shard_map/ppermute | solution.py:19
  51.0 5.7 %collective-permute-start.8 = (f32[1,1,1,8,8,128]{5,4,3,2,1,0:T(8,128)S(1)}, f32[1,1,1,8,8,128]{5,4,3,2,1,0:T(8,128)S(1)}, u32[]{:S(2)}, u32[]{:S(2)}) collective-permute-start(f32[1,1,1,8,8,128]{5,4,3,2,1,0:T(8,128)S(1)} %get-tuple-element.74), channel_id=1, source_target_pairs={{0,4},{4,8},{8,12},{12,16},{16,20},{20,24},{24,28},{1,5},{5,9},{9,... | collective-permute-start | bytes 98312 | tf_op jit(solution)/shard_map/ppermute | solution.py:16
  55.1 5.8 %collective-permute-start.9 = (f32[1,1,1,8,8,128]{5,4,3,2,1,0:T(8,128)S(1)}, f32[1,1,1,8,8,128]{5,4,3,2,1,0:T(8,128)S(1)}, u32[]{:S(2)}, u32[]{:S(2)}) collective-permute-start(f32[1,1,1,8,8,128]{5,4,3,2,1,0:T(8,128)S(1)} %get-tuple-element.75), channel_id=1, source_target_pairs={{4,0},{8,4},{12,8},{16,12},{20,16},{24,20},{28,24},{5,1},{9,5},{13... | collective-permute-start | bytes 98312 | tf_op jit(solution)/shard_map/ppermute | solution.py:19
  60.9 5.2 %collective-permute-start.10 = (f32[1,1,1,8,8,128]{5,4,3,2,1,0:T(8,128)S(1)}, f32[1,1,1,8,8,128]{5,4,3,2,1,0:T(8,128)S(1)}, u32[]{:S(2)}, u32[]{:S(2)}) collective-permute-start(f32[1,1,1,8,8,128]{5,4,3,2,1,0:T(8,128)S(1)} %maximum_bitcast_fusion.17), channel_id=1, source_target_pairs={{0,1},{1,2},{2,3},{4,5},{5,6},{6,7},{8,9},{9,10},{10,11},{12,13},{... | collective-permute-start | bytes 98312 | tf_op jit(solution)/shard_map/ppermute | solution.py:16
  66.2 3.5 %collective-permute-start.11 = (f32[1,1,1,8,8,128]{5,4,3,2,1,0:T(8,128)S(1)}, f32[1,1,1,8,8,128]{5,4,3,2,1,0:T(8,128)S(1)}, u32[]{:S(2)}, u32[]{:S(2)}) collective-permute-start(f32[1,1,1,8,8,128]{5,4,3,2,1,0:T(8,128)S(1)} %get-tuple-element.42), channel_id=1, source_target_pairs={{1,0},{2,1},{3,2},{5,4},{6,5},{7,6},{9,8},{10,9},{11,10},{13,12},{... | collective-permute-start | bytes 98312 | tf_op jit(solution)/shard_map/ppermute | solution.py:19
  71.8 5.2 %collective-permute-start.12 = (f32[1,1,1,8,8,128]{5,4,3,2,1,0:T(8,128)S(1)}, f32[1,1,1,8,8,128]{5,4,3,2,1,0:T(8,128)S(1)}, u32[]{:S(2)}, u32[]{:S(2)}) collective-permute-start(f32[1,1,1,8,8,128]{5,4,3,2,1,0:T(8,128)S(1)} %get-tuple-element.68), channel_id=1, source_target_pairs={{0,4},{4,8},{8,12},{12,16},{16,20},{20,24},{24,28},{1,5},{5,9},{9,... | collective-permute-start | bytes 98312 | tf_op jit(solution)/shard_map/ppermute | solution.py:16
  75.4 5.8 %collective-permute-start.13 = (f32[1,1,1,8,8,128]{5,4,3,2,1,0:T(8,128)S(1)}, f32[1,1,1,8,8,128]{5,4,3,2,1,0:T(8,128)S(1)}, u32[]{:S(2)}, u32[]{:S(2)}) collective-permute-start(f32[1,1,1,8,8,128]{5,4,3,2,1,0:T(8,128)S(1)} %get-tuple-element.69), channel_id=1, source_target_pairs={{4,0},{8,4},{12,8},{16,12},{20,16},{24,20},{28,24},{5,1},{9,5},{13... | collective-permute-start | bytes 98312 | tf_op jit(solution)/shard_map/ppermute | solution.py:19
  81.2 5.2 %collective-permute-start.14 = (f32[1,1,1,8,8,128]{5,4,3,2,1,0:T(8,128)S(1)}, f32[1,1,1,8,8,128]{5,4,3,2,1,0:T(8,128)S(1)}, u32[]{:S(2)}, u32[]{:S(2)}) collective-permute-start(f32[1,1,1,8,8,128]{5,4,3,2,1,0:T(8,128)S(1)} %maximum_bitcast_fusion.15), channel_id=1, source_target_pairs={{0,1},{1,2},{2,3},{4,5},{5,6},{6,7},{8,9},{9,10},{10,11},{12,13},{... | collective-permute-start | bytes 98312 | tf_op jit(solution)/shard_map/ppermute | solution.py:16
  86.5 3.8 %collective-permute-start.15 = (f32[1,1,1,8,8,128]{5,4,3,2,1,0:T(8,128)S(1)}, f32[1,1,1,8,8,128]{5,4,3,2,1,0:T(8,128)S(1)}, u32[]{:S(2)}, u32[]{:S(2)}) collective-permute-start(f32[1,1,1,8,8,128]{5,4,3,2,1,0:T(8,128)S(1)} %get-tuple-element.38), channel_id=1, source_target_pairs={{1,0},{2,1},{3,2},{5,4},{6,5},{7,6},{9,8},{10,9},{11,10},{13,12},{... | collective-permute-start | bytes 98312 | tf_op jit(solution)/shard_map/ppermute | solution.py:19
  93.1 0.9 copy-start.5
  97.7 20.1 %all-to-all-start = ((f32[32,2,2048]{2,1,0:T(2,128)}), f32[32,2,2048]{2,1,0:T(2,128)S(1)}, u32[]{:S(2)}, u32[]{:S(2)}) async-start(f32[32,2,2048]{2,1,0:T(2,128)} %bitcast.112), calls=%async_computation | async-start | bytes 1048576 | tf_op jit(solution)/shard_map/all_to_all | solution.py:185
  104.1 5.1 %collective-permute-start.16 = (f32[1,1,1,8,8,128]{5,4,3,2,1,0:T(8,128)S(1)}, f32[1,1,1,8,8,128]{5,4,3,2,1,0:T(8,128)S(1)}, u32[]{:S(2)}, u32[]{:S(2)}) collective-permute-start(f32[1,1,1,8,8,128]{5,4,3,2,1,0:T(8,128)S(1)} %get-tuple-element.59), channel_id=1, source_target_pairs={{0,4},{4,8},{8,12},{12,16},{16,20},{20,24},{24,28},{1,5},{5,9},{9,... | collective-permute-start | bytes 98312 | tf_op jit(solution)/shard_map/ppermute | solution.py:16
  107.5 6.2 %collective-permute-start.17 = (f32[1,1,1,8,8,128]{5,4,3,2,1,0:T(8,128)S(1)}, f32[1,1,1,8,8,128]{5,4,3,2,1,0:T(8,128)S(1)}, u32[]{:S(2)}, u32[]{:S(2)}) collective-permute-start(f32[1,1,1,8,8,128]{5,4,3,2,1,0:T(8,128)S(1)} %get-tuple-element.60), channel_id=1, source_target_pairs={{4,0},{8,4},{12,8},{16,12},{20,16},{24,20},{28,24},{5,1},{9,5},{13... | collective-permute-start | bytes 98312 | tf_op jit(solution)/shard_map/ppermute | solution.py:19
  118.8 9.1 %collective-permute-start.18 = (f32[1,1,1,8,8,128]{5,3,4,2,1,0:T(8,128)S(1)}, f32[1,1,1,8,8,128]{5,3,4,2,1,0:T(8,128)S(1)}, u32[]{:S(2)}, u32[]{:S(2)}) collective-permute-start(f32[1,1,1,8,8,128]{5,3,4,2,1,0:T(8,128)S(1)} %get-tuple-element.82), channel_id=1, source_target_pairs={{0,1},{1,2},{2,3},{4,5},{5,6},{6,7},{8,9},{9,10},{10,11},{12,13},{... | collective-permute-start | bytes 98312 | tf_op jit(solution)/shard_map/ppermute | solution.py:16
  120.8 7.1 %collective-permute-start.19 = (f32[1,1,1,8,8,128]{5,3,4,2,1,0:T(8,128)S(1)}, f32[1,1,1,8,8,128]{5,3,4,2,1,0:T(8,128)S(1)}, u32[]{:S(2)}, u32[]{:S(2)}) collective-permute-start(f32[1,1,1,8,8,128]{5,3,4,2,1,0:T(8,128)S(1)} %get-tuple-element.83), channel_id=1, source_target_pairs={{1,0},{2,1},{3,2},{5,4},{6,5},{7,6},{9,8},{10,9},{11,10},{13,12},{... | collective-permute-start | bytes 98312 | tf_op jit(solution)/shard_map/ppermute | solution.py:19
  124.4 10.8 %all-to-all-start.1 = ((f32[8,2,2048]{2,1,0:T(2,128)}), f32[8,2,2048]{2,1,0:T(2,128)S(1)}, u32[]{:S(2)}, u32[]{:S(2)}) async-start(f32[8,2,2048]{2,1,0:T(2,128)} %broadcast_in_dim.209), calls=%async_computation.1 | async-start | bytes 262144 | tf_op jit(solution)/shard_map/all_to_all | solution.py:194

commit v18 on v17

--- a/solution.py
+++ b/solution.py
@@ -192,7 +192,8 @@
 def strip_gather(spread_out, strip_size):
     n_ex, count, piece = spread_out.shape
     whole = lax.all_to_all(spread_out, "ex", 0, 0, tiled=True)
-    return whole.transpose(1, 0, 2).reshape(2, n_ex * piece)[:, :strip_size]
+    load = whole[:, 0] / jnp.maximum(whole[:, 1], 1.0)
+    return load.reshape(n_ex * piece)[:strip_size]
 
 
 def on_device(source, metric, fac_point, fac_strip, fac_shell, fac_area):
@@ -235,8 +236,7 @@
             rho_new = 1.0 / (2.0 * sigma - rho_now)
             update = rho_new * rho_now * update + 2.0 * rho_new / delta * pinv * resid
             rho_now = rho_new
-    total = strip_gather(mine, SHELL_STRIP)
-    shell_load = total[0] / jnp.maximum(total[1], 1.0)
+    shell_load = strip_gather(mine, SHELL_STRIP)
     return (pressure, resid, shell_load)
 
 

time: 137 us -> 137 us (level)
  no operation moved by 1% of the time
where the time goes in v18:
time: 137 us; the launch traced here: 136 us
  starting transfers between devices  55.7 us (41%)
  waiting for transfers between devices  46.8 us (34%)
  other arithmetic  14.5 us (11%)
  matrix products  12 us (9%)
  local copies, waits for them, and re-layouts  5.33 us (4%)
  between operations  1.63 us (1%)
    ppermute x10, starting transfers between devices, padded_2(): lax.ppermute(lax.slice_in_dim(block, block.shape[dim] - width, None, axis...  28.5 us
    ppermute x10, waiting for transfers between devices, padded_2(): lax.ppermute(lax.slice_in_dim(block, 0, width, axis=dim), axis, backward)  25.8 us
    ppermute x10, starting transfers between devices, padded_2(): lax.ppermute(lax.slice_in_dim(block, 0, width, axis=dim), axis, backward)  18.6 us
    ppermute x10, waiting for transfers between devices, padded_2(): lax.ppermute(lax.slice_in_dim(block, block.shape[dim] - width, None, axis...  10.6 us
    all_to_all x1, waiting for transfers between devices, strip_gather(): whole = lax.all_to_all(spread_out, 'ex', 0, 0, tiled=True)  6.31 us
    all_to_all x1, starting transfers between devices, strip_reduce(): return lax.all_to_all(chunks, ('ex', 'ey'), 0, 0, tiled=True).sum(0)  5.08 us
    all_to_all x1, waiting for transfers between devices, strip_reduce(): return lax.all_to_all(chunks, ('ex', 'ey'), 0, 0, tiled=True).sum(0)  4.09 us
    all_to_all x1, starting transfers between devices, strip_gather(): whole = lax.all_to_all(spread_out, 'ex', 0, 0, tiled=True)  3.46 us
  transfers between devices with their start and end apart: 22, of which 19 were waited for; matrix products, arithmetic and copies ran while one was open for 9% of the time, Pallas kernels for 0%

profile of v18, /device:TPU:2, one launch (start us, length us, event | category | flops | bytes accessed | tf_op | source)
XLA Modules:
  0.0 135.9 jit_solution(18299219947576272566)
XLA Ops:
  2.9 1.2 fusion.90
  4.9 3.4 %collective-permute-start = (f32[2,1,1,8,8,128]{5,0,4,3,2,1:T(2,128)S(1)}, f32[2,1,1,8,8,128]{5,0,4,3,2,1:T(2,128)S(1)}, u32[]{:S(2)}, u32[]{:S(2)}) collective-permute-start(f32[2,1,1,8,8,128]{5,0,4,3,2,1:T(2,128)S(1)} %maximum_bitcast_fusion.9), channel_id=1, source_target_pairs={{0,4},{4,8},{8,12},{12,16},{16,20},{20,24},{24,28},{1,5},{5,9},{9,... | collective-permute-start | bytes 196616 | tf_op jit(solution)/shard_map/ppermute | solution.py:16
  8.3 0.9 fusion.94
  10.0 1.2 fusion.20
  11.3 1.3 collective-permute-start.1
  13.3 4.3 %collective-permute-done.1 = f32[2,1,1,8,8,128]{5,0,4,3,2,1:T(2,128)S(1)} collective-permute-done((f32[2,1,1,8,8,128]{5,0,4,3,2,1:T(2,128)S(1)}, f32[2,1,1,8,8,128]{5,0,4,3,2,1:T(2,128)S(1)}, u32[]{:S(2)}, u32[]{:S(2)}) %collective-permute-start.1) | collective-permute-done | bytes 65568 | tf_op jit(solution)/shard_map/ppermute | solution.py:19
  17.6 1.9 %collective-permute-start.2 = (f32[2,1,1,8,8,128]{5,3,0,4,2,1:T(8,128)S(1)}, f32[2,1,1,8,8,128]{5,3,0,4,2,1:T(8,128)S(1)}, u32[]{:S(2)}, u32[]{:S(2)}) collective-permute-start(f32[2,1,1,8,8,128]{5,3,0,4,2,1:T(8,128)S(1)} %maximum_bitcast_fusion.7), channel_id=1, source_target_pairs={{0,1},{1,2},{2,3},{4,5},{5,6},{6,7},{8,9},{9,10},{10,11},{12,13},{... | collective-permute-start | bytes 196616 | tf_op jit(solution)/shard_map/ppermute | solution.py:16
  19.5 3.6 %collective-permute-done.2 = f32[2,1,1,8,8,128]{5,3,0,4,2,1:T(8,128)S(1)} collective-permute-done((f32[2,1,1,8,8,128]{5,3,0,4,2,1:T(8,128)S(1)}, f32[2,1,1,8,8,128]{5,3,0,4,2,1:T(8,128)S(1)}, u32[]{:S(2)}, u32[]{:S(2)}) %collective-permute-start.2) | collective-permute-done | bytes 65568 | tf_op jit(solution)/shard_map/ppermute | solution.py:16
  23.2 1.9 %collective-permute-start.3 = (f32[2,1,1,8,8,128]{5,3,0,4,2,1:T(8,128)S(1)}, f32[2,1,1,8,8,128]{5,3,0,4,2,1:T(8,128)S(1)}, u32[]{:S(2)}, u32[]{:S(2)}) collective-permute-start(f32[2,1,1,8,8,128]{5,3,0,4,2,1:T(8,128)S(1)} %get-tuple-element.48), channel_id=1, source_target_pairs={{1,0},{2,1},{3,2},{5,4},{6,5},{7,6},{9,8},{10,9},{11,10},{13,12},{... | collective-permute-start | bytes 196616 | tf_op jit(solution)/shard_map/ppermute | solution.py:19
  25.5 1.5 %collective-permute-done.3 = f32[2,1,1,8,8,128]{5,3,0,4,2,1:T(8,128)S(1)} collective-permute-done((f32[2,1,1,8,8,128]{5,3,0,4,2,1:T(8,128)S(1)}, f32[2,1,1,8,8,128]{5,3,0,4,2,1:T(8,128)S(1)}, u32[]{:S(2)}, u32[]{:S(2)}) %collective-permute-start.3) | collective-permute-done | bytes 65568 | tf_op jit(solution)/shard_map/ppermute | solution.py:19
  28.8 0.9 fusion.30
  29.8 4.3 %collective-permute-start.4 = (f32[1,1,1,8,8,128]{5,4,3,2,1,0:T(8,128)S(1)}, f32[1,1,1,8,8,128]{5,4,3,2,1,0:T(8,128)S(1)}, u32[]{:S(2)}, u32[]{:S(2)}) collective-permute-start(f32[1,1,1,8,8,128]{5,4,3,2,1,0:T(8,128)S(1)} %bitcast.482), channel_id=1, source_target_pairs={{0,4},{4,8},{8,12},{12,16},{16,20},{20,24},{24,28},{1,5},{5,9},{9,... | collective-permute-start | bytes 98312 | tf_op jit(solution)/shard_map/ppermute | solution.py:16
  34.1 1.3 collective-permute-start.5
  35.7 4.2 %collective-permute-done.5 = f32[1,1,1,8,8,128]{5,4,3,2,1,0:T(8,128)S(1)} collective-permute-done((f32[1,1,1,8,8,128]{5,4,3,2,1,0:T(8,128)S(1)}, f32[1,1,1,8,8,128]{5,4,3,2,1,0:T(8,128)S(1)}, u32[]{:S(2)}, u32[]{:S(2)}) %collective-permute-start.5) | collective-permute-done | bytes 32800 | tf_op jit(solution)/shard_map/ppermute | solution.py:19
  39.9 1.9 %collective-permute-start.6 = (f32[1,1,1,8,8,128]{5,3,4,2,1,0:T(8,128)S(1)}, f32[1,1,1,8,8,128]{5,3,4,2,1,0:T(8,128)S(1)}, u32[]{:S(2)}, u32[]{:S(2)}) collective-permute-start(f32[1,1,1,8,8,128]{5,3,4,2,1,0:T(8,128)S(1)} %maximum_bitcast_fusion.19), channel_id=1, source_target_pairs={{0,1},{1,2},{2,3},{4,5},{5,6},{6,7},{8,9},{9,10},{10,11},{12,13},{... | collective-permute-start | bytes 98312 | tf_op jit(solution)/shard_map/ppermute | solution.py:16
  41.9 1.9 %fusion = f32[768,256]{1,0:T(8,128)S(1)} fusion(bf16[256,4096]{1,0:T(8,128)(2,1)S(1)} %get-tuple-element.89, bf16[256,4096]{1,0:T(8,128)(2,1)S(1)} %get-tuple-element.90, bf16[256,4096]{1,0:T(8,128)(2,1)S(1)} %get-tuple-element.88, s32[4096]{0:T(1024)S(1)} %add_select_fusion), kind=kOutput, calls=%fused_computation | convolution fusion | flops 1630535680 | bytes 7094272 | tf_op jit(solution)/shard_map/dot_general | solution.py:170
  43.8 1.4 %collective-permute-done.6 = f32[1,1,1,8,8,128]{5,3,4,2,1,0:T(8,128)S(1)} collective-permute-done((f32[1,1,1,8,8,128]{5,3,4,2,1,0:T(8,128)S(1)}, f32[1,1,1,8,8,128]{5,3,4,2,1,0:T(8,128)S(1)}, u32[]{:S(2)}, u32[]{:S(2)}) %collective-permute-start.6) | collective-permute-done | bytes 32800 | tf_op jit(solution)/shard_map/ppermute | solution.py:16
  45.2 2.3 %collective-permute-start.7 = (f32[1,1,1,8,8,128]{5,3,4,2,1,0:T(8,128)S(1)}, f32[1,1,1,8,8,128]{5,3,4,2,1,0:T(8,128)S(1)}, u32[]{:S(2)}, u32[]{:S(2)}) collective-permute-start(f32[1,1,1,8,8,128]{5,3,4,2,1,0:T(8,128)S(1)} %get-tuple-element.44), channel_id=1, source_target_pairs={{1,0},{2,1},{3,2},{5,4},{6,5},{7,6},{9,8},{10,9},{11,10},{13,12},{... | collective-permute-start | bytes 98312 | tf_op jit(solution)/shard_map/ppermute | solution.py:19
  47.7 1.4 %collective-permute-done.7 = f32[1,1,1,8,8,128]{5,3,4,2,1,0:T(8,128)S(1)} collective-permute-done((f32[1,1,1,8,8,128]{5,3,4,2,1,0:T(8,128)S(1)}, f32[1,1,1,8,8,128]{5,3,4,2,1,0:T(8,128)S(1)}, u32[]{:S(2)}, u32[]{:S(2)}) %collective-permute-start.7) | collective-permute-done | bytes 32800 | tf_op jit(solution)/shard_map/ppermute | solution.py:19
  51.0 4.1 %collective-permute-start.8 = (f32[1,1,1,8,8,128]{5,4,3,2,1,0:T(8,128)S(1)}, f32[1,1,1,8,8,128]{5,4,3,2,1,0:T(8,128)S(1)}, u32[]{:S(2)}, u32[]{:S(2)}) collective-permute-start(f32[1,1,1,8,8,128]{5,4,3,2,1,0:T(8,128)S(1)} %get-tuple-element.74), channel_id=1, source_target_pairs={{0,4},{4,8},{8,12},{12,16},{16,20},{20,24},{24,28},{1,5},{5,9},{9,... | collective-permute-start | bytes 98312 | tf_op jit(solution)/shard_map/ppermute | solution.py:16
  55.1 1.3 collective-permute-start.9
  56.7 4.2 %collective-permute-done.9 = f32[1,1,1,8,8,128]{5,4,3,2,1,0:T(8,128)S(1)} collective-permute-done((f32[1,1,1,8,8,128]{5,4,3,2,1,0:T(8,128)S(1)}, f32[1,1,1,8,8,128]{5,4,3,2,1,0:T(8,128)S(1)}, u32[]{:S(2)}, u32[]{:S(2)}) %collective-permute-start.9) | collective-permute-done | bytes 32800 | tf_op jit(solution)/shard_map/ppermute | solution.py:19
  60.9 1.9 %collective-permute-start.10 = (f32[1,1,1,8,8,128]{5,4,3,2,1,0:T(8,128)S(1)}, f32[1,1,1,8,8,128]{5,4,3,2,1,0:T(8,128)S(1)}, u32[]{:S(2)}, u32[]{:S(2)}) collective-permute-start(f32[1,1,1,8,8,128]{5,4,3,2,1,0:T(8,128)S(1)} %maximum_bitcast_fusion.17), channel_id=1, source_target_pairs={{0,1},{1,2},{2,3},{4,5},{5,6},{6,7},{8,9},{9,10},{10,11},{12,13},{... | collective-permute-start | bytes 98312 | tf_op jit(solution)/shard_map/ppermute | solution.py:16
  62.9 3.2 %collective-permute-done.10 = f32[1,1,1,8,8,128]{5,4,3,2,1,0:T(8,128)S(1)} collective-permute-done((f32[1,1,1,8,8,128]{5,4,3,2,1,0:T(8,128)S(1)}, f32[1,1,1,8,8,128]{5,4,3,2,1,0:T(8,128)S(1)}, u32[]{:S(2)}, u32[]{:S(2)}) %collective-permute-start.10) | collective-permute-done | bytes 32800 | tf_op jit(solution)/shard_map/ppermute | solution.py:16
  66.2 2.1 %collective-permute-start.11 = (f32[1,1,1,8,8,128]{5,4,3,2,1,0:T(8,128)S(1)}, f32[1,1,1,8,8,128]{5,4,3,2,1,0:T(8,128)S(1)}, u32[]{:S(2)}, u32[]{:S(2)}) collective-permute-start(f32[1,1,1,8,8,128]{5,4,3,2,1,0:T(8,128)S(1)} %get-tuple-element.42), channel_id=1, source_target_pairs={{1,0},{2,1},{3,2},{5,4},{6,5},{7,6},{9,8},{10,9},{11,10},{13,12},{... | collective-permute-start | bytes 98312 | tf_op jit(solution)/shard_map/ppermute | solution.py:19
  68.4 1.3 collective-permute-done.11
  71.8 3.6 %collective-permute-start.12 = (f32[1,1,1,8,8,128]{5,4,3,2,1,0:T(8,128)S(1)}, f32[1,1,1,8,8,128]{5,4,3,2,1,0:T(8,128)S(1)}, u32[]{:S(2)}, u32[]{:S(2)}) collective-permute-start(f32[1,1,1,8,8,128]{5,4,3,2,1,0:T(8,128)S(1)} %get-tuple-element.68), channel_id=1, source_target_pairs={{0,4},{4,8},{8,12},{12,16},{16,20},{20,24},{24,28},{1,5},{5,9},{9,... | collective-permute-start | bytes 98312 | tf_op jit(solution)/shard_map/ppermute | solution.py:16
  75.4 1.3 collective-permute-start.13
  77.0 4.2 %collective-permute-done.13 = f32[1,1,1,8,8,128]{5,4,3,2,1,0:T(8,128)S(1)} collective-permute-done((f32[1,1,1,8,8,128]{5,4,3,2,1,0:T(8,128)S(1)}, f32[1,1,1,8,8,128]{5,4,3,2,1,0:T(8,128)S(1)}, u32[]{:S(2)}, u32[]{:S(2)}) %collective-permute-start.13) | collective-permute-done | bytes 32800 | tf_op jit(solution)/shard_map/ppermute | solution.py:19
  81.2 1.9 %collective-permute-start.14 = (f32[1,1,1,8,8,128]{5,4,3,2,1,0:T(8,128)S(1)}, f32[1,1,1,8,8,128]{5,4,3,2,1,0:T(8,128)S(1)}, u32[]{:S(2)}, u32[]{:S(2)}) collective-permute-start(f32[1,1,1,8,8,128]{5,4,3,2,1,0:T(8,128)S(1)} %maximum_bitcast_fusion.15), channel_id=1, source_target_pairs={{0,1},{1,2},{2,3},{4,5},{5,6},{6,7},{8,9},{9,10},{10,11},{12,13},{... | collective-permute-start | bytes 98312 | tf_op jit(solution)/shard_map/ppermute | solution.py:16
  83.2 1.9 %fusion.15 = f32[768,4096]{1,0:T(8,128)S(1)} fusion(s32[4096]{0:T(1024)S(1)} %bitcast.476, bf16[256,256]{1,0:T(8,128)(2,1)S(1)} %get-tuple-element.62, bf16[256,256]{1,0:T(8,128)(2,1)S(1)} %get-tuple-element.63, bf16[256,256]{1,0:T(8,128)(2,1)S(1)} %get-tuple-element.61), kind=kOutput, calls=%fused_computation.19 | convolution fusion | flops 1612840960 | bytes 12992512 | tf_op jit(solution)/shard_map/dot_general | solution.py:156
  85.1 1.4 %collective-permute-done.14 = f32[1,1,1,8,8,128]{5,4,3,2,1,0:T(8,128)S(1)} collective-permute-done((f32[1,1,1,8,8,128]{5,4,3,2,1,0:T(8,128)S(1)}, f32[1,1,1,8,8,128]{5,4,3,2,1,0:T(8,128)S(1)}, u32[]{:S(2)}, u32[]{:S(2)}) %collective-permute-start.14) | collective-permute-done | bytes 32800 | tf_op jit(solution)/shard_map/ppermute | solution.py:16
  86.5 2.2 %collective-permute-start.15 = (f32[1,1,1,8,8,128]{5,4,3,2,1,0:T(8,128)S(1)}, f32[1,1,1,8,8,128]{5,4,3,2,1,0:T(8,128)S(1)}, u32[]{:S(2)}, u32[]{:S(2)}) collective-permute-start(f32[1,1,1,8,8,128]{5,4,3,2,1,0:T(8,128)S(1)} %get-tuple-element.38), channel_id=1, source_target_pairs={{1,0},{2,1},{3,2},{5,4},{6,5},{7,6},{9,8},{10,9},{11,10},{13,12},{... | collective-permute-start | bytes 98312 | tf_op jit(solution)/shard_map/ppermute | solution.py:19
  88.7 1.4 fusion.9
  91.8 1.3 fusion.14
  93.1 0.9 fusion.7
  94.1 0.9 fusion.17
  94.9 1.4 %fusion.10 = f32[512,256]{1,0:T(8,128)S(1)} fusion(bf16[256,4096]{1,0:T(8,128)(2,1)S(1)} %get-tuple-element.87, bf16[256,4096]{1,0:T(8,128)(2,1)S(1)} %get-tuple-element.86, s32[4096]{0:T(1024)S(1)} %add_select_fusion), kind=kOutput, calls=%fused_computation.13 | convolution fusion | flops 1083179008 | bytes 4734976 | tf_op jit(solution)/shard_map/dot_general | solution.py:170
  96.5 1.2 copy.201
  97.7 5.1 %all-to-all-start = ((f32[32,2,2048]{2,1,0:T(2,128)}), f32[32,2,2048]{2,1,0:T(2,128)S(1)}, u32[]{:S(2)}, u32[]{:S(2)}) async-start(f32[32,2,2048]{2,1,0:T(2,128)} %bitcast.112), calls=%async_computation | async-start | bytes 1048576 | tf_op jit(solution)/shard_map/all_to_all | solution.py:185
  104.1 3.4 %collective-permute-start.16 = (f32[1,1,1,8,8,128]{5,4,3,2,1,0:T(8,128)S(1)}, f32[1,1,1,8,8,128]{5,4,3,2,1,0:T(8,128)S(1)}, u32[]{:S(2)}, u32[]{:S(2)}) collective-permute-start(f32[1,1,1,8,8,128]{5,4,3,2,1,0:T(8,128)S(1)} %get-tuple-element.59), channel_id=1, source_target_pairs={{0,4},{4,8},{8,12},{12,16},{16,20},{20,24},{24,28},{1,5},{5,9},{9,... | collective-permute-start | bytes 98312 | tf_op jit(solution)/shard_map/ppermute | solution.py:16
  107.5 1.3 collective-permute-start.17
  109.2 4.5 %collective-permute-done.17 = f32[1,1,1,8,8,128]{5,4,3,2,1,0:T(8,128)S(1)} collective-permute-done((f32[1,1,1,8,8,128]{5,4,3,2,1,0:T(8,128)S(1)}, f32[1,1,1,8,8,128]{5,4,3,2,1,0:T(8,128)S(1)}, u32[]{:S(2)}, u32[]{:S(2)}) %collective-permute-start.17) | collective-permute-done | bytes 32800 | tf_op jit(solution)/shard_map/ppermute | solution.py:19
  113.8 4.1 %all-to-all-done = f32[32,2,2048]{2,1,0:T(2,128)S(1)} async-done(((f32[32,2,2048]{2,1,0:T(2,128)}), f32[32,2,2048]{2,1,0:T(2,128)S(1)}, u32[]{:S(2)}, u32[]{:S(2)}) %all-to-all-start) | async-done | bytes 524320 | tf_op jit(solution)/shard_map/all_to_all | solution.py:185
  118.8 1.9 %collective-permute-start.18 = (f32[1,1,1,8,8,128]{5,3,4,2,1,0:T(8,128)S(1)}, f32[1,1,1,8,8,128]{5,3,4,2,1,0:T(8,128)S(1)}, u32[]{:S(2)}, u32[]{:S(2)}) collective-permute-start(f32[1,1,1,8,8,128]{5,3,4,2,1,0:T(8,128)S(1)} %get-tuple-element.82), channel_id=1, source_target_pairs={{0,1},{1,2},{2,3},{4,5},{5,6},{6,7},{8,9},{9,10},{10,11},{12,13},{... | collective-permute-start | bytes 98312 | tf_op jit(solution)/shard_map/ppermute | solution.py:16
  120.8 3.6 %collective-permute-start.19 = (f32[1,1,1,8,8,128]{5,3,4,2,1,0:T(8,128)S(1)}, f32[1,1,1,8,8,128]{5,3,4,2,1,0:T(8,128)S(1)}, u32[]{:S(2)}, u32[]{:S(2)}) collective-permute-start(f32[1,1,1,8,8,128]{5,3,4,2,1,0:T(8,128)S(1)} %get-tuple-element.83), channel_id=1, source_target_pairs={{1,0},{2,1},{3,2},{5,4},{6,5},{7,6},{9,8},{10,9},{11,10},{13,12},{... | collective-permute-start | bytes 98312 | tf_op jit(solution)/shard_map/ppermute | solution.py:19
  124.4 3.5 %all-to-all-start.1 = ((f32[8,2,2048]{2,1,0:T(2,128)}), f32[8,2,2048]{2,1,0:T(2,128)S(1)}, u32[]{:S(2)}, u32[]{:S(2)}) async-start(f32[8,2,2048]{2,1,0:T(2,128)} %broadcast_in_dim.209), calls=%async_computation.1 | async-start | bytes 262144 | tf_op jit(solution)/shard_map/all_to_all | solution.py:194
  128.9 6.3 %all-to-all-done.1 = f32[8,2,2048]{2,1,0:T(2,128)S(1)} async-done(((f32[8,2,2048]{2,1,0:T(2,128)}), f32[8,2,2048]{2,1,0:T(2,128)S(1)}, u32[]{:S(2)}, u32[]{:S(2)}) %all-to-all-start.1) | async-done | bytes 131104 | tf_op jit(solution)/shard_map/all_to_all | solution.py:194
  (137 shorter events, 18.0 us)
Async XLA Ops:
  0.6 10.6 %copy-start = (f32[1,1,8,8,8,128]{5,4,3,2,1,0:T(8,128)S(1)}, f32[1,1,8,8,8,128]{5,4,3,2,1,0:T(8,128)}, u32[]{:S(2)}) copy-start(f32[1,1,8,8,8,128]{5,4,3,2,1,0:T(8,128)} %param.36) | copy-start | bytes 786436
  4.9 6.3 %collective-permute-start = (f32[2,1,1,8,8,128]{5,0,4,3,2,1:T(2,128)S(1)}, f32[2,1,1,8,8,128]{5,0,4,3,2,1:T(2,128)S(1)}, u32[]{:S(2)}, u32[]{:S(2)}) collective-permute-start(f32[2,1,1,8,8,128]{5,0,4,3,2,1:T(2,128)S(1)} %maximum_bitcast_fusion.9), channel_id=1, source_target_pairs={{0,4},{4,8},{8,12},{12,16},{16,20},{20,24},{24,28},{1,5},{5,9},{9,... | collective-permute-start | bytes 196616 | tf_op jit(solution)/shard_map/ppermute | solution.py:16
  10.0 9.5 %copy-start.4 = (s32[1,4096,1]{1,2,0:T(1,128)S(1)}, s32[1,4096,1]{1,2,0:T(1,128)}, u32[]{:S(2)}) copy-start(s32[1,4096,1]{1,2,0:T(1,128)} %param.39) | copy-start | bytes 49156
  11.3 6.2 %collective-permute-start.1 = (f32[2,1,1,8,8,128]{5,0,4,3,2,1:T(2,128)S(1)}, f32[2,1,1,8,8,128]{5,0,4,3,2,1:T(2,128)S(1)}, u32[]{:S(2)}, u32[]{:S(2)}) collective-permute-start(f32[2,1,1,8,8,128]{5,0,4,3,2,1:T(2,128)S(1)} %get-tuple-element.50), channel_id=1, source_target_pairs={{4,0},{8,4},{12,8},{16,12},{20,16},{24,20},{28,24},{5,1},{9,5},{13... | collective-permute-start | bytes 196616 | tf_op jit(solution)/shard_map/ppermute | solution.py:19
  17.6 5.6 %collective-permute-start.2 = (f32[2,1,1,8,8,128]{5,3,0,4,2,1:T(8,128)S(1)}, f32[2,1,1,8,8,128]{5,3,0,4,2,1:T(8,128)S(1)}, u32[]{:S(2)}, u32[]{:S(2)}) collective-permute-start(f32[2,1,1,8,8,128]{5,3,0,4,2,1:T(8,128)S(1)} %maximum_bitcast_fusion.7), channel_id=1, source_target_pairs={{0,1},{1,2},{2,3},{4,5},{5,6},{6,7},{8,9},{9,10},{10,11},{12,13},{... | collective-permute-start | bytes 196616 | tf_op jit(solution)/shard_map/ppermute | solution.py:16
  23.2 4.7 %copy-start.1 = (f32[8,8,1,1]{1,0,3,2:T(8,128)S(1)}, f32[8,8,1,1]{1,0,3,2:T(8,128)}, u32[]{:S(2)}) copy-start(f32[8,8,1,1]{1,0,3,2:T(8,128)} %constant.130) | copy-start | bytes 772
  23.2 3.8 %collective-permute-start.3 = (f32[2,1,1,8,8,128]{5,3,0,4,2,1:T(8,128)S(1)}, f32[2,1,1,8,8,128]{5,3,0,4,2,1:T(8,128)S(1)}, u32[]{:S(2)}, u32[]{:S(2)}) collective-permute-start(f32[2,1,1,8,8,128]{5,3,0,4,2,1:T(8,128)S(1)} %get-tuple-element.48), channel_id=1, source_target_pairs={{1,0},{2,1},{3,2},{5,4},{6,5},{7,6},{9,8},{10,9},{11,10},{13,12},{... | collective-permute-start | bytes 196616 | tf_op jit(solution)/shard_map/ppermute | solution.py:19
  25.3 3.4 %copy-start.6 = (f32[8]{0:T(128)S(1)}, f32[8]{0:T(128)}, u32[]{:S(2)}) copy-start(f32[8]{0:T(128)} %constant.125) | copy-start | bytes 100
  27.2 8.2 %copy-start.2 = (s32[1,4096]{1,0:T(1,128)S(1)}, s32[1,4096]{1,0:T(1,128)}, u32[]{:S(2)}) copy-start(s32[1,4096]{1,0:T(1,128)} %param.40) | copy-start | bytes 49156
  29.8 5.9 %collective-permute-start.4 = (f32[1,1,1,8,8,128]{5,4,3,2,1,0:T(8,128)S(1)}, f32[1,1,1,8,8,128]{5,4,3,2,1,0:T(8,128)S(1)}, u32[]{:S(2)}, u32[]{:S(2)}) collective-permute-start(f32[1,1,1,8,8,128]{5,4,3,2,1,0:T(8,128)S(1)} %bitcast.482), channel_id=1, source_target_pairs={{0,4},{4,8},{8,12},{12,16},{16,20},{20,24},{24,28},{1,5},{5,9},{9,... | collective-permute-start | bytes 98312 | tf_op jit(solution)/shard_map/ppermute | solution.py:16
  34.1 5.8 %collective-permute-start.5 = (f32[1,1,1,8,8,128]{5,4,3,2,1,0:T(8,128)S(1)}, f32[1,1,1,8,8,128]{5,4,3,2,1,0:T(8,128)S(1)}, u32[]{:S(2)}, u32[]{:S(2)}) collective-permute-start(f32[1,1,1,8,8,128]{5,4,3,2,1,0:T(8,128)S(1)} %bitcast.484), channel_id=1, source_target_pairs={{4,0},{8,4},{12,8},{16,12},{20,16},{24,20},{28,24},{5,1},{9,5},{13... | collective-permute-start | bytes 98312 | tf_op jit(solution)/shard_map/ppermute | solution.py:19
  39.9 5.2 %collective-permute-start.6 = (f32[1,1,1,8,8,128]{5,3,4,2,1,0:T(8,128)S(1)}, f32[1,1,1,8,8,128]{5,3,4,2,1,0:T(8,128)S(1)}, u32[]{:S(2)}, u32[]{:S(2)}) collective-permute-start(f32[1,1,1,8,8,128]{5,3,4,2,1,0:T(8,128)S(1)} %maximum_bitcast_fusion.19), channel_id=1, source_target_pairs={{0,1},{1,2},{2,3},{4,5},{5,6},{6,7},{8,9},{9,10},{10,11},{12,13},{... | collective-permute-start | bytes 98312 | tf_op jit(solution)/shard_map/ppermute | solution.py:16
  45.2 17.7 %copy-start.3 = (s32[1,4096]{1,0:T(1,128)S(1)}, s32[1,4096]{1,0:T(1,128)}, u32[]{:S(2)}) copy-start(s32[1,4096]{1,0:T(1,128)} %param.38) | copy-start | bytes 49156
  45.2 3.9 %collective-permute-start.7 = (f32[1,1,1,8,8,128]{5,3,4,2,1,0:T(8,128)S(1)}, f32[1,1,1,8,8,128]{5,3,4,2,1,0:T(8,128)S(1)}, u32[]{:S(2)}, u32[]{:S(2)}) collective-permute-start(f32[1,1,1,8,8,128]{5,3,4,2,1,0:T(8,128)S(1)} %get-tuple-element.44), channel_id=1, source_target_pairs={{1,0},{2,1},{3,2},{5,4},{6,5},{7,6},{9,8},{10,9},{11,10},{13,12},{... | collective-permute-start | bytes 98312 | tf_op jit(solution)/shard_map/ppermute | solution.py:19
  51.0 5.7 %collective-permute-start.8 = (f32[1,1,1,8,8,128]{5,4,3,2,1,0:T(8,128)S(1)}, f32[1,1,1,8,8,128]{5,4,3,2,1,0:T(8,128)S(1)}, u32[]{:S(2)}, u32[]{:S(2)}) collective-permute-start(f32[1,1,1,8,8,128]{5,4,3,2,1,0:T(8,128)S(1)} %get-tuple-element.74), channel_id=1, source_target_pairs={{0,4},{4,8},{8,12},{12,16},{16,20},{20,24},{24,28},{1,5},{5,9},{9,... | collective-permute-start | bytes 98312 | tf_op jit(solution)/shard_map/ppermute | solution.py:16
  55.1 5.8 %collective-permute-start.9 = (f32[1,1,1,8,8,128]{5,4,3,2,1,0:T(8,128)S(1)}, f32[1,1,1,8,8,128]{5,4,3,2,1,0:T(8,128)S(1)}, u32[]{:S(2)}, u32[]{:S(2)}) collective-permute-start(f32[1,1,1,8,8,128]{5,4,3,2,1,0:T(8,128)S(1)} %get-tuple-element.75), channel_id=1, source_target_pairs={{4,0},{8,4},{12,8},{16,12},{20,16},{24,20},{28,24},{5,1},{9,5},{13... | collective-permute-start | bytes 98312 | tf_op jit(solution)/shard_map/ppermute | solution.py:19
  60.9 5.2 %collective-permute-start.10 = (f32[1,1,1,8,8,128]{5,4,3,2,1,0:T(8,128)S(1)}, f32[1,1,1,8,8,128]{5,4,3,2,1,0:T(8,128)S(1)}, u32[]{:S(2)}, u32[]{:S(2)}) collective-permute-start(f32[1,1,1,8,8,128]{5,4,3,2,1,0:T(8,128)S(1)} %maximum_bitcast_fusion.17), channel_id=1, source_target_pairs={{0,1},{1,2},{2,3},{4,5},{5,6},{6,7},{8,9},{9,10},{10,11},{12,13},{... | collective-permute-start | bytes 98312 | tf_op jit(solution)/shard_map/ppermute | solution.py:16
  66.2 3.5 %collective-permute-start.11 = (f32[1,1,1,8,8,128]{5,4,3,2,1,0:T(8,128)S(1)}, f32[1,1,1,8,8,128]{5,4,3,2,1,0:T(8,128)S(1)}, u32[]{:S(2)}, u32[]{:S(2)}) collective-permute-start(f32[1,1,1,8,8,128]{5,4,3,2,1,0:T(8,128)S(1)} %get-tuple-element.42), channel_id=1, source_target_pairs={{1,0},{2,1},{3,2},{5,4},{6,5},{7,6},{9,8},{10,9},{11,10},{13,12},{... | collective-permute-start | bytes 98312 | tf_op jit(solution)/shard_map/ppermute | solution.py:19
  71.8 5.2 %collective-permute-start.12 = (f32[1,1,1,8,8,128]{5,4,3,2,1,0:T(8,128)S(1)}, f32[1,1,1,8,8,128]{5,4,3,2,1,0:T(8,128)S(1)}, u32[]{:S(2)}, u32[]{:S(2)}) collective-permute-start(f32[1,1,1,8,8,128]{5,4,3,2,1,0:T(8,128)S(1)} %get-tuple-element.68), channel_id=1, source_target_pairs={{0,4},{4,8},{8,12},{12,16},{16,20},{20,24},{24,28},{1,5},{5,9},{9,... | collective-permute-start | bytes 98312 | tf_op jit(solution)/shard_map/ppermute | solution.py:16
  75.4 5.8 %collective-permute-start.13 = (f32[1,1,1,8,8,128]{5,4,3,2,1,0:T(8,128)S(1)}, f32[1,1,1,8,8,128]{5,4,3,2,1,0:T(8,128)S(1)}, u32[]{:S(2)}, u32[]{:S(2)}) collective-permute-start(f32[1,1,1,8,8,128]{5,4,3,2,1,0:T(8,128)S(1)} %get-tuple-element.69), channel_id=1, source_target_pairs={{4,0},{8,4},{12,8},{16,12},{20,16},{24,20},{28,24},{5,1},{9,5},{13... | collective-permute-start | bytes 98312 | tf_op jit(solution)/shard_map/ppermute | solution.py:19
  81.2 5.2 %collective-permute-start.14 = (f32[1,1,1,8,8,128]{5,4,3,2,1,0:T(8,128)S(1)}, f32[1,1,1,8,8,128]{5,4,3,2,1,0:T(8,128)S(1)}, u32[]{:S(2)}, u32[]{:S(2)}) collective-permute-start(f32[1,1,1,8,8,128]{5,4,3,2,1,0:T(8,128)S(1)} %maximum_bitcast_fusion.15), channel_id=1, source_target_pairs={{0,1},{1,2},{2,3},{4,5},{5,6},{6,7},{8,9},{9,10},{10,11},{12,13},{... | collective-permute-start | bytes 98312 | tf_op jit(solution)/shard_map/ppermute | solution.py:16
  86.5 3.8 %collective-permute-start.15 = (f32[1,1,1,8,8,128]{5,4,3,2,1,0:T(8,128)S(1)}, f32[1,1,1,8,8,128]{5,4,3,2,1,0:T(8,128)S(1)}, u32[]{:S(2)}, u32[]{:S(2)}) collective-permute-start(f32[1,1,1,8,8,128]{5,4,3,2,1,0:T(8,128)S(1)} %get-tuple-element.38), channel_id=1, source_target_pairs={{1,0},{2,1},{3,2},{5,4},{6,5},{7,6},{9,8},{10,9},{11,10},{13,12},{... | collective-permute-start | bytes 98312 | tf_op jit(solution)/shard_map/ppermute | solution.py:19
  93.1 0.9 copy-start.5
  97.7 20.1 %all-to-all-start = ((f32[32,2,2048]{2,1,0:T(2,128)}), f32[32,2,2048]{2,1,0:T(2,128)S(1)}, u32[]{:S(2)}, u32[]{:S(2)}) async-start(f32[32,2,2048]{2,1,0:T(2,128)} %bitcast.112), calls=%async_computation | async-start | bytes 1048576 | tf_op jit(solution)/shard_map/all_to_all | solution.py:185
  104.1 5.1 %collective-permute-start.16 = (f32[1,1,1,8,8,128]{5,4,3,2,1,0:T(8,128)S(1)}, f32[1,1,1,8,8,128]{5,4,3,2,1,0:T(8,128)S(1)}, u32[]{:S(2)}, u32[]{:S(2)}) collective-permute-start(f32[1,1,1,8,8,128]{5,4,3,2,1,0:T(8,128)S(1)} %get-tuple-element.59), channel_id=1, source_target_pairs={{0,4},{4,8},{8,12},{12,16},{16,20},{20,24},{24,28},{1,5},{5,9},{9,... | collective-permute-start | bytes 98312 | tf_op jit(solution)/shard_map/ppermute | solution.py:16
  107.5 6.2 %collective-permute-start.17 = (f32[1,1,1,8,8,128]{5,4,3,2,1,0:T(8,128)S(1)}, f32[1,1,1,8,8,128]{5,4,3,2,1,0:T(8,128)S(1)}, u32[]{:S(2)}, u32[]{:S(2)}) collective-permute-start(f32[1,1,1,8,8,128]{5,4,3,2,1,0:T(8,128)S(1)} %get-tuple-element.60), channel_id=1, source_target_pairs={{4,0},{8,4},{12,8},{16,12},{20,16},{24,20},{28,24},{5,1},{9,5},{13... | collective-permute-start | bytes 98312 | tf_op jit(solution)/shard_map/ppermute | solution.py:19
  118.8 9.1 %collective-permute-start.18 = (f32[1,1,1,8,8,128]{5,3,4,2,1,0:T(8,128)S(1)}, f32[1,1,1,8,8,128]{5,3,4,2,1,0:T(8,128)S(1)}, u32[]{:S(2)}, u32[]{:S(2)}) collective-permute-start(f32[1,1,1,8,8,128]{5,3,4,2,1,0:T(8,128)S(1)} %get-tuple-element.82), channel_id=1, source_target_pairs={{0,1},{1,2},{2,3},{4,5},{5,6},{6,7},{8,9},{9,10},{10,11},{12,13},{... | collective-permute-start | bytes 98312 | tf_op jit(solution)/shard_map/ppermute | solution.py:16
  120.8 7.1 %collective-permute-start.19 = (f32[1,1,1,8,8,128]{5,3,4,2,1,0:T(8,128)S(1)}, f32[1,1,1,8,8,128]{5,3,4,2,1,0:T(8,128)S(1)}, u32[]{:S(2)}, u32[]{:S(2)}) collective-permute-start(f32[1,1,1,8,8,128]{5,3,4,2,1,0:T(8,128)S(1)} %get-tuple-element.83), channel_id=1, source_target_pairs={{1,0},{2,1},{3,2},{5,4},{6,5},{7,6},{9,8},{10,9},{11,10},{13,12},{... | collective-permute-start | bytes 98312 | tf_op jit(solution)/shard_map/ppermute | solution.py:19
  124.4 10.8 %all-to-all-start.1 = ((f32[8,2,2048]{2,1,0:T(2,128)}), f32[8,2,2048]{2,1,0:T(2,128)S(1)}, u32[]{:S(2)}, u32[]{:S(2)}) async-start(f32[8,2,2048]{2,1,0:T(2,128)} %broadcast_in_dim.209), calls=%async_computation.1 | async-start | bytes 262144 | tf_op jit(solution)/shard_map/all_to_all | solution.py:194

commit v19 on v18

--- a/solution.py
+++ b/solution.py
@@ -229,7 +229,7 @@
         assembled = assembled[0]
         if step + 2 == SWEEPS:
             assembled, early = lax.optimization_barrier((assembled, early))
-        if step == 0:
+        if step == 1:
             assembled, denom = lax.optimization_barrier((assembled, denom))
         resid = resid - assembled
         if step + 1 < SWEEPS:

time: 137 us -> 139 us (1.015)
  other arithmetic: 14.5 us -> 17.1 us
  waiting for transfers between devices: 46.8 us -> 45.2 us
where the time goes in v19:
time: 139 us; the launch traced here: 138 us
  starting transfers between devices  56.2 us (40%)
  waiting for transfers between devices  45.2 us (33%)
  other arithmetic  17.1 us (12%)
  matrix products  12 us (9%)
  local copies, waits for them, and re-layouts  5.35 us (4%)
  between operations  1.59 us (1%)
    ppermute x10, starting transfers between devices, padded_2(): lax.ppermute(lax.slice_in_dim(block, block.shape[dim] - width, None, axis...  28.9 us
    ppermute x10, waiting for transfers between devices, padded_2(): lax.ppermute(lax.slice_in_dim(block, 0, width, axis=dim), axis, backward)  25.5 us
    ppermute x10, starting transfers between devices, padded_2(): lax.ppermute(lax.slice_in_dim(block, 0, width, axis=dim), axis, backward)  18.6 us
    ppermute x10, waiting for transfers between devices, padded_2(): lax.ppermute(lax.slice_in_dim(block, block.shape[dim] - width, None, axis...  9.33 us
    all_to_all x1, waiting for transfers between devices, strip_gather(): whole = lax.all_to_all(spread_out, 'ex', 0, 0, tiled=True)  6.31 us
    all_to_all x1, starting transfers between devices, strip_reduce(): return lax.all_to_all(chunks, ('ex', 'ey'), 0, 0, tiled=True).sum(0)  5.3 us
    all_to_all x1, waiting for transfers between devices, strip_reduce(): return lax.all_to_all(chunks, ('ex', 'ey'), 0, 0, tiled=True).sum(0)  4.09 us
    all_to_all x1, starting transfers between devices, strip_gather(): whole = lax.all_to_all(spread_out, 'ex', 0, 0, tiled=True)  3.46 us
  transfers between devices with their start and end apart: 22, of which 19 were waited for; matrix products, arithmetic and copies ran while one was open for 9% of the time, Pallas kernels for 0%

profile of v19, /device:TPU:2, one launch (start us, length us, event | category | flops | bytes accessed | tf_op | source)
XLA Modules:
  0.0 137.5 jit_solution(15712963783911882111)
XLA Ops:
  2.8 1.2 fusion.87
  4.8 3.4 %collective-permute-start = (f32[2,1,1,8,8,128]{5,0,4,3,2,1:T(2,128)S(1)}, f32[2,1,1,8,8,128]{5,0,4,3,2,1:T(2,128)S(1)}, u32[]{:S(2)}, u32[]{:S(2)}) collective-permute-start(f32[2,1,1,8,8,128]{5,0,4,3,2,1:T(2,128)S(1)} %maximum_bitcast_fusion.8), channel_id=1, source_target_pairs={{0,4},{4,8},{8,12},{12,16},{16,20},{20,24},{24,28},{1,5},{5,9},{9,... | collective-permute-start | bytes 196616 | tf_op jit(solution)/shard_map/ppermute | solution.py:16
  9.1 1.3 pad_maximum_fusion.5
  11.5 1.3 collective-permute-start.1
  13.6 4.0 %collective-permute-done.1 = f32[2,1,1,8,8,128]{5,0,4,3,2,1:T(2,128)S(1)} collective-permute-done((f32[2,1,1,8,8,128]{5,0,4,3,2,1:T(2,128)S(1)}, f32[2,1,1,8,8,128]{5,0,4,3,2,1:T(2,128)S(1)}, u32[]{:S(2)}, u32[]{:S(2)}) %collective-permute-start.1) | collective-permute-done | bytes 65568 | tf_op jit(solution)/shard_map/ppermute | solution.py:19
  17.7 1.9 %collective-permute-start.2 = (f32[2,1,1,8,8,128]{5,3,0,4,2,1:T(8,128)S(1)}, f32[2,1,1,8,8,128]{5,3,0,4,2,1:T(8,128)S(1)}, u32[]{:S(2)}, u32[]{:S(2)}) collective-permute-start(f32[2,1,1,8,8,128]{5,3,0,4,2,1:T(8,128)S(1)} %maximum_bitcast_fusion.6), channel_id=1, source_target_pairs={{0,1},{1,2},{2,3},{4,5},{5,6},{6,7},{8,9},{9,10},{10,11},{12,13},{... | collective-permute-start | bytes 196616 | tf_op jit(solution)/shard_map/ppermute | solution.py:16
  19.7 1.2 fusion.20
  20.9 2.4 %collective-permute-done.2 = f32[2,1,1,8,8,128]{5,3,0,4,2,1:T(8,128)S(1)} collective-permute-done((f32[2,1,1,8,8,128]{5,3,0,4,2,1:T(8,128)S(1)}, f32[2,1,1,8,8,128]{5,3,0,4,2,1:T(8,128)S(1)}, u32[]{:S(2)}, u32[]{:S(2)}) %collective-permute-start.2) | collective-permute-done | bytes 65568 | tf_op jit(solution)/shard_map/ppermute | solution.py:16
  23.4 1.9 %collective-permute-start.3 = (f32[2,1,1,8,8,128]{5,3,0,4,2,1:T(8,128)S(1)}, f32[2,1,1,8,8,128]{5,3,0,4,2,1:T(8,128)S(1)}, u32[]{:S(2)}, u32[]{:S(2)}) collective-permute-start(f32[2,1,1,8,8,128]{5,3,0,4,2,1:T(8,128)S(1)} %get-tuple-element.54), channel_id=1, source_target_pairs={{1,0},{2,1},{3,2},{5,4},{6,5},{7,6},{9,8},{10,9},{11,10},{13,12},{... | collective-permute-start | bytes 196616 | tf_op jit(solution)/shard_map/ppermute | solution.py:19
  25.7 1.5 %collective-permute-done.3 = f32[2,1,1,8,8,128]{5,3,0,4,2,1:T(8,128)S(1)} collective-permute-done((f32[2,1,1,8,8,128]{5,3,0,4,2,1:T(8,128)S(1)}, f32[2,1,1,8,8,128]{5,3,0,4,2,1:T(8,128)S(1)}, u32[]{:S(2)}, u32[]{:S(2)}) %collective-permute-start.3) | collective-permute-done | bytes 65568 | tf_op jit(solution)/shard_map/ppermute | solution.py:19
  29.0 0.9 fusion.30
  30.0 4.7 %collective-permute-start.4 = (f32[1,1,1,8,8,128]{5,4,3,2,1,0:T(8,128)S(1)}, f32[1,1,1,8,8,128]{5,4,3,2,1,0:T(8,128)S(1)}, u32[]{:S(2)}, u32[]{:S(2)}) collective-permute-start(f32[1,1,1,8,8,128]{5,4,3,2,1,0:T(8,128)S(1)} %bitcast.463), channel_id=1, source_target_pairs={{0,4},{4,8},{8,12},{12,16},{16,20},{20,24},{24,28},{1,5},{5,9},{9,... | collective-permute-start | bytes 98312 | tf_op jit(solution)/shard_map/ppermute | solution.py:16
  34.6 1.3 collective-permute-start.5
  36.2 4.2 %collective-permute-done.5 = f32[1,1,1,8,8,128]{5,4,3,2,1,0:T(8,128)S(1)} collective-permute-done((f32[1,1,1,8,8,128]{5,4,3,2,1,0:T(8,128)S(1)}, f32[1,1,1,8,8,128]{5,4,3,2,1,0:T(8,128)S(1)}, u32[]{:S(2)}, u32[]{:S(2)}) %collective-permute-start.5) | collective-permute-done | bytes 32800 | tf_op jit(solution)/shard_map/ppermute | solution.py:19
  40.5 1.9 %collective-permute-start.6 = (f32[1,1,1,8,8,128]{5,3,4,2,1,0:T(8,128)S(1)}, f32[1,1,1,8,8,128]{5,3,4,2,1,0:T(8,128)S(1)}, u32[]{:S(2)}, u32[]{:S(2)}) collective-permute-start(f32[1,1,1,8,8,128]{5,3,4,2,1,0:T(8,128)S(1)} %maximum_bitcast_fusion.18), channel_id=1, source_target_pairs={{0,1},{1,2},{2,3},{4,5},{5,6},{6,7},{8,9},{9,10},{10,11},{12,13},{... | collective-permute-start | bytes 98312 | tf_op jit(solution)/shard_map/ppermute | solution.py:16
  42.5 3.2 %collective-permute-done.6 = f32[1,1,1,8,8,128]{5,3,4,2,1,0:T(8,128)S(1)} collective-permute-done((f32[1,1,1,8,8,128]{5,3,4,2,1,0:T(8,128)S(1)}, f32[1,1,1,8,8,128]{5,3,4,2,1,0:T(8,128)S(1)}, u32[]{:S(2)}, u32[]{:S(2)}) %collective-permute-start.6) | collective-permute-done | bytes 32800 | tf_op jit(solution)/shard_map/ppermute | solution.py:16
  45.7 1.9 %collective-permute-start.7 = (f32[1,1,1,8,8,128]{5,3,4,2,1,0:T(8,128)S(1)}, f32[1,1,1,8,8,128]{5,3,4,2,1,0:T(8,128)S(1)}, u32[]{:S(2)}, u32[]{:S(2)}) collective-permute-start(f32[1,1,1,8,8,128]{5,3,4,2,1,0:T(8,128)S(1)} %get-tuple-element.48), channel_id=1, source_target_pairs={{1,0},{2,1},{3,2},{5,4},{6,5},{7,6},{9,8},{10,9},{11,10},{13,12},{... | collective-permute-start | bytes 98312 | tf_op jit(solution)/shard_map/ppermute | solution.py:19
  47.7 1.5 %collective-permute-done.7 = f32[1,1,1,8,8,128]{5,3,4,2,1,0:T(8,128)S(1)} collective-permute-done((f32[1,1,1,8,8,128]{5,3,4,2,1,0:T(8,128)S(1)}, f32[1,1,1,8,8,128]{5,3,4,2,1,0:T(8,128)S(1)}, u32[]{:S(2)}, u32[]{:S(2)}) %collective-permute-start.7) | collective-permute-done | bytes 32800 | tf_op jit(solution)/shard_map/ppermute | solution.py:19
  52.0 4.3 %collective-permute-start.8 = (f32[1,1,1,8,8,128]{5,4,3,2,1,0:T(8,128)S(1)}, f32[1,1,1,8,8,128]{5,4,3,2,1,0:T(8,128)S(1)}, u32[]{:S(2)}, u32[]{:S(2)}) collective-permute-start(f32[1,1,1,8,8,128]{5,4,3,2,1,0:T(8,128)S(1)} %bitcast.465), channel_id=1, source_target_pairs={{0,4},{4,8},{8,12},{12,16},{16,20},{20,24},{24,28},{1,5},{5,9},{9,... | collective-permute-start | bytes 98312 | tf_op jit(solution)/shard_map/ppermute | solution.py:16
  56.3 1.3 collective-permute-start.9
  57.9 4.2 %collective-permute-done.9 = f32[1,1,1,8,8,128]{5,4,3,2,1,0:T(8,128)S(1)} collective-permute-done((f32[1,1,1,8,8,128]{5,4,3,2,1,0:T(8,128)S(1)}, f32[1,1,1,8,8,128]{5,4,3,2,1,0:T(8,128)S(1)}, u32[]{:S(2)}, u32[]{:S(2)}) %collective-permute-start.9) | collective-permute-done | bytes 32800 | tf_op jit(solution)/shard_map/ppermute | solution.py:19
  62.2 1.9 %collective-permute-start.10 = (f32[1,1,1,8,8,128]{5,3,4,2,1,0:T(8,128)S(1)}, f32[1,1,1,8,8,128]{5,3,4,2,1,0:T(8,128)S(1)}, u32[]{:S(2)}, u32[]{:S(2)}) collective-permute-start(f32[1,1,1,8,8,128]{5,3,4,2,1,0:T(8,128)S(1)} %maximum_bitcast_fusion.16), channel_id=1, source_target_pairs={{0,1},{1,2},{2,3},{4,5},{5,6},{6,7},{8,9},{9,10},{10,11},{12,13},{... | collective-permute-start | bytes 98312 | tf_op jit(solution)/shard_map/ppermute | solution.py:16
  64.1 1.9 %fusion = f32[768,256]{1,0:T(8,128)S(1)} fusion(bf16[256,4096]{1,0:T(8,128)(2,1)S(1)} %get-tuple-element.97, bf16[256,4096]{1,0:T(8,128)(2,1)S(1)} %get-tuple-element.98, bf16[256,4096]{1,0:T(8,128)(2,1)S(1)} %get-tuple-element.96, s32[4096]{0:T(1024)S(1)} %add_select_fusion), kind=kOutput, calls=%fused_computation | convolution fusion | flops 1630535680 | bytes 7094272 | tf_op jit(solution)/shard_map/dot_general | solution.py:170
  66.0 1.4 collective-permute-done.10
  67.4 2.5 %collective-permute-start.11 = (f32[1,1,1,8,8,128]{5,3,4,2,1,0:T(8,128)S(1)}, f32[1,1,1,8,8,128]{5,3,4,2,1,0:T(8,128)S(1)}, u32[]{:S(2)}, u32[]{:S(2)}) collective-permute-start(f32[1,1,1,8,8,128]{5,3,4,2,1,0:T(8,128)S(1)} %get-tuple-element.42), channel_id=1, source_target_pairs={{1,0},{2,1},{3,2},{5,4},{6,5},{7,6},{9,8},{10,9},{11,10},{13,12},{... | collective-permute-start | bytes 98312 | tf_op jit(solution)/shard_map/ppermute | solution.py:19
  70.2 1.1 collective-permute-done.11
  73.3 3.4 %collective-permute-start.12 = (f32[1,1,1,8,8,128]{5,4,3,2,1,0:T(8,128)S(1)}, f32[1,1,1,8,8,128]{5,4,3,2,1,0:T(8,128)S(1)}, u32[]{:S(2)}, u32[]{:S(2)}) collective-permute-start(f32[1,1,1,8,8,128]{5,4,3,2,1,0:T(8,128)S(1)} %get-tuple-element.74), channel_id=1, source_target_pairs={{0,4},{4,8},{8,12},{12,16},{16,20},{20,24},{24,28},{1,5},{5,9},{9,... | collective-permute-start | bytes 98312 | tf_op jit(solution)/shard_map/ppermute | solution.py:16
  76.8 1.3 collective-permute-start.13
  78.3 4.2 %collective-permute-done.13 = f32[1,1,1,8,8,128]{5,4,3,2,1,0:T(8,128)S(1)} collective-permute-done((f32[1,1,1,8,8,128]{5,4,3,2,1,0:T(8,128)S(1)}, f32[1,1,1,8,8,128]{5,4,3,2,1,0:T(8,128)S(1)}, u32[]{:S(2)}, u32[]{:S(2)}) %collective-permute-start.13) | collective-permute-done | bytes 32800 | tf_op jit(solution)/shard_map/ppermute | solution.py:19
  82.6 1.9 %collective-permute-start.14 = (f32[1,1,1,8,8,128]{5,4,3,2,1,0:T(8,128)S(1)}, f32[1,1,1,8,8,128]{5,4,3,2,1,0:T(8,128)S(1)}, u32[]{:S(2)}, u32[]{:S(2)}) collective-permute-start(f32[1,1,1,8,8,128]{5,4,3,2,1,0:T(8,128)S(1)} %maximum_bitcast_fusion.14), channel_id=1, source_target_pairs={{0,1},{1,2},{2,3},{4,5},{5,6},{6,7},{8,9},{9,10},{10,11},{12,13},{... | collective-permute-start | bytes 98312 | tf_op jit(solution)/shard_map/ppermute | solution.py:16
  84.5 1.9 %fusion.15 = f32[768,4096]{1,0:T(8,128)S(1)} fusion(s32[4096]{0:T(1024)S(1)} %bitcast.459, bf16[256,256]{1,0:T(8,128)(2,1)S(1)} %get-tuple-element.68, bf16[256,256]{1,0:T(8,128)(2,1)S(1)} %get-tuple-element.69, bf16[256,256]{1,0:T(8,128)(2,1)S(1)} %get-tuple-element.67), kind=kOutput, calls=%fused_computation.19 | convolution fusion | flops 1612840960 | bytes 12992512 | tf_op jit(solution)/shard_map/dot_general | solution.py:156
  86.4 1.4 %collective-permute-done.14 = f32[1,1,1,8,8,128]{5,4,3,2,1,0:T(8,128)S(1)} collective-permute-done((f32[1,1,1,8,8,128]{5,4,3,2,1,0:T(8,128)S(1)}, f32[1,1,1,8,8,128]{5,4,3,2,1,0:T(8,128)S(1)}, u32[]{:S(2)}, u32[]{:S(2)}) %collective-permute-start.14) | collective-permute-done | bytes 32800 | tf_op jit(solution)/shard_map/ppermute | solution.py:16
  87.8 2.2 %collective-permute-start.15 = (f32[1,1,1,8,8,128]{5,4,3,2,1,0:T(8,128)S(1)}, f32[1,1,1,8,8,128]{5,4,3,2,1,0:T(8,128)S(1)}, u32[]{:S(2)}, u32[]{:S(2)}) collective-permute-start(f32[1,1,1,8,8,128]{5,4,3,2,1,0:T(8,128)S(1)} %get-tuple-element.38), channel_id=1, source_target_pairs={{1,0},{2,1},{3,2},{5,4},{6,5},{7,6},{9,8},{10,9},{11,10},{13,12},{... | collective-permute-start | bytes 98312 | tf_op jit(solution)/shard_map/ppermute | solution.py:19
  90.1 1.4 fusion.9
  93.1 1.3 fusion.14
  94.5 0.9 fusion.7
  95.4 0.9 fusion.17
  96.3 1.4 %fusion.10 = f32[512,256]{1,0:T(8,128)S(1)} fusion(bf16[256,4096]{1,0:T(8,128)(2,1)S(1)} %get-tuple-element.95, bf16[256,4096]{1,0:T(8,128)(2,1)S(1)} %get-tuple-element.94, s32[4096]{0:T(1024)S(1)} %add_select_fusion), kind=kOutput, calls=%fused_computation.13 | convolution fusion | flops 1083179008 | bytes 4734976 | tf_op jit(solution)/shard_map/dot_general | solution.py:170
  97.9 1.2 copy.221
  99.1 5.3 %all-to-all-start = ((f32[32,2,2048]{2,1,0:T(2,128)}), f32[32,2,2048]{2,1,0:T(2,128)S(1)}, u32[]{:S(2)}, u32[]{:S(2)}) async-start(f32[32,2,2048]{2,1,0:T(2,128)} %bitcast.115), calls=%async_computation | async-start | bytes 1048576 | tf_op jit(solution)/shard_map/all_to_all | solution.py:185
  105.7 3.4 %collective-permute-start.16 = (f32[1,1,1,8,8,128]{5,4,3,2,1,0:T(8,128)S(1)}, f32[1,1,1,8,8,128]{5,4,3,2,1,0:T(8,128)S(1)}, u32[]{:S(2)}, u32[]{:S(2)}) collective-permute-start(f32[1,1,1,8,8,128]{5,4,3,2,1,0:T(8,128)S(1)} %get-tuple-element.65), channel_id=1, source_target_pairs={{0,4},{4,8},{8,12},{12,16},{16,20},{20,24},{24,28},{1,5},{5,9},{9,... | collective-permute-start | bytes 98312 | tf_op jit(solution)/shard_map/ppermute | solution.py:16
  109.1 1.3 collective-permute-start.17
  110.8 4.5 %collective-permute-done.17 = f32[1,1,1,8,8,128]{5,4,3,2,1,0:T(8,128)S(1)} collective-permute-done((f32[1,1,1,8,8,128]{5,4,3,2,1,0:T(8,128)S(1)}, f32[1,1,1,8,8,128]{5,4,3,2,1,0:T(8,128)S(1)}, u32[]{:S(2)}, u32[]{:S(2)}) %collective-permute-start.17) | collective-permute-done | bytes 32800 | tf_op jit(solution)/shard_map/ppermute | solution.py:19
  115.3 4.1 %all-to-all-done = f32[32,2,2048]{2,1,0:T(2,128)S(1)} async-done(((f32[32,2,2048]{2,1,0:T(2,128)}), f32[32,2,2048]{2,1,0:T(2,128)S(1)}, u32[]{:S(2)}, u32[]{:S(2)}) %all-to-all-start) | async-done | bytes 524320 | tf_op jit(solution)/shard_map/all_to_all | solution.py:185
  120.4 1.9 %collective-permute-start.18 = (f32[1,1,1,8,8,128]{5,3,4,2,1,0:T(8,128)S(1)}, f32[1,1,1,8,8,128]{5,3,4,2,1,0:T(8,128)S(1)}, u32[]{:S(2)}, u32[]{:S(2)}) collective-permute-start(f32[1,1,1,8,8,128]{5,3,4,2,1,0:T(8,128)S(1)} %get-tuple-element.88), channel_id=1, source_target_pairs={{0,1},{1,2},{2,3},{4,5},{5,6},{6,7},{8,9},{9,10},{10,11},{12,13},{... | collective-permute-start | bytes 98312 | tf_op jit(solution)/shard_map/ppermute | solution.py:16
  122.4 3.6 %collective-permute-start.19 = (f32[1,1,1,8,8,128]{5,3,4,2,1,0:T(8,128)S(1)}, f32[1,1,1,8,8,128]{5,3,4,2,1,0:T(8,128)S(1)}, u32[]{:S(2)}, u32[]{:S(2)}) collective-permute-start(f32[1,1,1,8,8,128]{5,3,4,2,1,0:T(8,128)S(1)} %get-tuple-element.89), channel_id=1, source_target_pairs={{1,0},{2,1},{3,2},{5,4},{6,5},{7,6},{9,8},{10,9},{11,10},{13,12},{... | collective-permute-start | bytes 98312 | tf_op jit(solution)/shard_map/ppermute | solution.py:19
  126.0 3.5 %all-to-all-start.1 = ((f32[8,2,2048]{2,1,0:T(2,128)}), f32[8,2,2048]{2,1,0:T(2,128)S(1)}, u32[]{:S(2)}, u32[]{:S(2)}) async-start(f32[8,2,2048]{2,1,0:T(2,128)} %broadcast_in_dim.209), calls=%async_computation.1 | async-start | bytes 262144 | tf_op jit(solution)/shard_map/all_to_all | solution.py:194
  130.5 6.3 %all-to-all-done.1 = f32[8,2,2048]{2,1,0:T(2,128)S(1)} async-done(((f32[8,2,2048]{2,1,0:T(2,128)}), f32[8,2,2048]{2,1,0:T(2,128)S(1)}, u32[]{:S(2)}, u32[]{:S(2)}) %all-to-all-start.1) | async-done | bytes 131104 | tf_op jit(solution)/shard_map/all_to_all | solution.py:194
  (136 shorter events, 20.1 us)
Async XLA Ops:
  4.8 5.8 %collective-permute-start = (f32[2,1,1,8,8,128]{5,0,4,3,2,1:T(2,128)S(1)}, f32[2,1,1,8,8,128]{5,0,4,3,2,1:T(2,128)S(1)}, u32[]{:S(2)}, u32[]{:S(2)}) collective-permute-start(f32[2,1,1,8,8,128]{5,0,4,3,2,1:T(2,128)S(1)} %maximum_bitcast_fusion.8), channel_id=1, source_target_pairs={{0,4},{4,8},{8,12},{12,16},{16,20},{20,24},{24,28},{1,5},{5,9},{9,... | collective-permute-start | bytes 196616 | tf_op jit(solution)/shard_map/ppermute | solution.py:16
  11.5 6.2 %collective-permute-start.1 = (f32[2,1,1,8,8,128]{5,0,4,3,2,1:T(2,128)S(1)}, f32[2,1,1,8,8,128]{5,0,4,3,2,1:T(2,128)S(1)}, u32[]{:S(2)}, u32[]{:S(2)}) collective-permute-start(f32[2,1,1,8,8,128]{5,0,4,3,2,1:T(2,128)S(1)} %get-tuple-element.56), channel_id=1, source_target_pairs={{4,0},{8,4},{12,8},{16,12},{20,16},{24,20},{28,24},{5,1},{9,5},{13... | collective-permute-start | bytes 196616 | tf_op jit(solution)/shard_map/ppermute | solution.py:19
  17.7 5.6 %collective-permute-start.2 = (f32[2,1,1,8,8,128]{5,3,0,4,2,1:T(8,128)S(1)}, f32[2,1,1,8,8,128]{5,3,0,4,2,1:T(8,128)S(1)}, u32[]{:S(2)}, u32[]{:S(2)}) collective-permute-start(f32[2,1,1,8,8,128]{5,3,0,4,2,1:T(8,128)S(1)} %maximum_bitcast_fusion.6), channel_id=1, source_target_pairs={{0,1},{1,2},{2,3},{4,5},{5,6},{6,7},{8,9},{9,10},{10,11},{12,13},{... | collective-permute-start | bytes 196616 | tf_op jit(solution)/shard_map/ppermute | solution.py:16
  23.3 4.7 %copy-start.5 = (f32[8]{0:T(128)S(1)}, f32[8]{0:T(128)}, u32[]{:S(2)}) copy-start(f32[8]{0:T(128)} %constant.125) | copy-start | bytes 100
  23.4 3.8 %collective-permute-start.3 = (f32[2,1,1,8,8,128]{5,3,0,4,2,1:T(8,128)S(1)}, f32[2,1,1,8,8,128]{5,3,0,4,2,1:T(8,128)S(1)}, u32[]{:S(2)}, u32[]{:S(2)}) collective-permute-start(f32[2,1,1,8,8,128]{5,3,0,4,2,1:T(8,128)S(1)} %get-tuple-element.54), channel_id=1, source_target_pairs={{1,0},{2,1},{3,2},{5,4},{6,5},{7,6},{9,8},{10,9},{11,10},{13,12},{... | collective-permute-start | bytes 196616 | tf_op jit(solution)/shard_map/ppermute | solution.py:19
  25.4 2.8 %copy-start = (f32[8,8,1,1]{1,0,3,2:T(8,128)S(1)}, f32[8,8,1,1]{1,0,3,2:T(8,128)}, u32[]{:S(2)}) copy-start(f32[8,8,1,1]{1,0,3,2:T(8,128)} %constant.130) | copy-start | bytes 772
  27.4 8.6 %copy-start.1 = (s32[1,4096]{1,0:T(1,128)S(1)}, s32[1,4096]{1,0:T(1,128)}, u32[]{:S(2)}) copy-start(s32[1,4096]{1,0:T(1,128)} %param.38) | copy-start | bytes 49156
  27.8 19.9 %copy-start.3 = (s32[1,4096,1]{1,2,0:T(1,128)S(1)}, s32[1,4096,1]{1,2,0:T(1,128)}, u32[]{:S(2)}) copy-start(s32[1,4096,1]{1,2,0:T(1,128)} %param.39) | copy-start | bytes 49156
  30.0 6.3 %collective-permute-start.4 = (f32[1,1,1,8,8,128]{5,4,3,2,1,0:T(8,128)S(1)}, f32[1,1,1,8,8,128]{5,4,3,2,1,0:T(8,128)S(1)}, u32[]{:S(2)}, u32[]{:S(2)}) collective-permute-start(f32[1,1,1,8,8,128]{5,4,3,2,1,0:T(8,128)S(1)} %bitcast.463), channel_id=1, source_target_pairs={{0,4},{4,8},{8,12},{12,16},{16,20},{20,24},{24,28},{1,5},{5,9},{9,... | collective-permute-start | bytes 98312 | tf_op jit(solution)/shard_map/ppermute | solution.py:16
  34.6 5.8 %collective-permute-start.5 = (f32[1,1,1,8,8,128]{5,4,3,2,1,0:T(8,128)S(1)}, f32[1,1,1,8,8,128]{5,4,3,2,1,0:T(8,128)S(1)}, u32[]{:S(2)}, u32[]{:S(2)}) collective-permute-start(f32[1,1,1,8,8,128]{5,4,3,2,1,0:T(8,128)S(1)} %bitcast.467), channel_id=1, source_target_pairs={{4,0},{8,4},{12,8},{16,12},{20,16},{24,20},{28,24},{5,1},{9,5},{13... | collective-permute-start | bytes 98312 | tf_op jit(solution)/shard_map/ppermute | solution.py:19
  40.5 17.2 %copy-start.2 = (s32[1,4096]{1,0:T(1,128)S(1)}, s32[1,4096]{1,0:T(1,128)}, u32[]{:S(2)}) copy-start(s32[1,4096]{1,0:T(1,128)} %param.40) | copy-start | bytes 49156
  40.5 5.2 %collective-permute-start.6 = (f32[1,1,1,8,8,128]{5,3,4,2,1,0:T(8,128)S(1)}, f32[1,1,1,8,8,128]{5,3,4,2,1,0:T(8,128)S(1)}, u32[]{:S(2)}, u32[]{:S(2)}) collective-permute-start(f32[1,1,1,8,8,128]{5,3,4,2,1,0:T(8,128)S(1)} %maximum_bitcast_fusion.18), channel_id=1, source_target_pairs={{0,1},{1,2},{2,3},{4,5},{5,6},{6,7},{8,9},{9,10},{10,11},{12,13},{... | collective-permute-start | bytes 98312 | tf_op jit(solution)/shard_map/ppermute | solution.py:16
  45.7 3.5 %collective-permute-start.7 = (f32[1,1,1,8,8,128]{5,3,4,2,1,0:T(8,128)S(1)}, f32[1,1,1,8,8,128]{5,3,4,2,1,0:T(8,128)S(1)}, u32[]{:S(2)}, u32[]{:S(2)}) collective-permute-start(f32[1,1,1,8,8,128]{5,3,4,2,1,0:T(8,128)S(1)} %get-tuple-element.48), channel_id=1, source_target_pairs={{1,0},{2,1},{3,2},{5,4},{6,5},{7,6},{9,8},{10,9},{11,10},{13,12},{... | collective-permute-start | bytes 98312 | tf_op jit(solution)/shard_map/ppermute | solution.py:19
  52.0 5.9 %collective-permute-start.8 = (f32[1,1,1,8,8,128]{5,4,3,2,1,0:T(8,128)S(1)}, f32[1,1,1,8,8,128]{5,4,3,2,1,0:T(8,128)S(1)}, u32[]{:S(2)}, u32[]{:S(2)}) collective-permute-start(f32[1,1,1,8,8,128]{5,4,3,2,1,0:T(8,128)S(1)} %bitcast.465), channel_id=1, source_target_pairs={{0,4},{4,8},{8,12},{12,16},{16,20},{20,24},{24,28},{1,5},{5,9},{9,... | collective-permute-start | bytes 98312 | tf_op jit(solution)/shard_map/ppermute | solution.py:16
  56.3 5.8 %collective-permute-start.9 = (f32[1,1,1,8,8,128]{5,4,3,2,1,0:T(8,128)S(1)}, f32[1,1,1,8,8,128]{5,4,3,2,1,0:T(8,128)S(1)}, u32[]{:S(2)}, u32[]{:S(2)}) collective-permute-start(f32[1,1,1,8,8,128]{5,4,3,2,1,0:T(8,128)S(1)} %bitcast.469), channel_id=1, source_target_pairs={{4,0},{8,4},{12,8},{16,12},{20,16},{24,20},{28,24},{5,1},{9,5},{13... | collective-permute-start | bytes 98312 | tf_op jit(solution)/shard_map/ppermute | solution.py:19
  62.2 5.2 %collective-permute-start.10 = (f32[1,1,1,8,8,128]{5,3,4,2,1,0:T(8,128)S(1)}, f32[1,1,1,8,8,128]{5,3,4,2,1,0:T(8,128)S(1)}, u32[]{:S(2)}, u32[]{:S(2)}) collective-permute-start(f32[1,1,1,8,8,128]{5,3,4,2,1,0:T(8,128)S(1)} %maximum_bitcast_fusion.16), channel_id=1, source_target_pairs={{0,1},{1,2},{2,3},{4,5},{5,6},{6,7},{8,9},{9,10},{10,11},{12,13},{... | collective-permute-start | bytes 98312 | tf_op jit(solution)/shard_map/ppermute | solution.py:16
  67.4 3.9 %collective-permute-start.11 = (f32[1,1,1,8,8,128]{5,3,4,2,1,0:T(8,128)S(1)}, f32[1,1,1,8,8,128]{5,3,4,2,1,0:T(8,128)S(1)}, u32[]{:S(2)}, u32[]{:S(2)}) collective-permute-start(f32[1,1,1,8,8,128]{5,3,4,2,1,0:T(8,128)S(1)} %get-tuple-element.42), channel_id=1, source_target_pairs={{1,0},{2,1},{3,2},{5,4},{6,5},{7,6},{9,8},{10,9},{11,10},{13,12},{... | collective-permute-start | bytes 98312 | tf_op jit(solution)/shard_map/ppermute | solution.py:19
  73.3 5.0 %collective-permute-start.12 = (f32[1,1,1,8,8,128]{5,4,3,2,1,0:T(8,128)S(1)}, f32[1,1,1,8,8,128]{5,4,3,2,1,0:T(8,128)S(1)}, u32[]{:S(2)}, u32[]{:S(2)}) collective-permute-start(f32[1,1,1,8,8,128]{5,4,3,2,1,0:T(8,128)S(1)} %get-tuple-element.74), channel_id=1, source_target_pairs={{0,4},{4,8},{8,12},{12,16},{16,20},{20,24},{24,28},{1,5},{5,9},{9,... | collective-permute-start | bytes 98312 | tf_op jit(solution)/shard_map/ppermute | solution.py:16
  76.8 5.8 %collective-permute-start.13 = (f32[1,1,1,8,8,128]{5,4,3,2,1,0:T(8,128)S(1)}, f32[1,1,1,8,8,128]{5,4,3,2,1,0:T(8,128)S(1)}, u32[]{:S(2)}, u32[]{:S(2)}) collective-permute-start(f32[1,1,1,8,8,128]{5,4,3,2,1,0:T(8,128)S(1)} %get-tuple-element.75), channel_id=1, source_target_pairs={{4,0},{8,4},{12,8},{16,12},{20,16},{24,20},{28,24},{5,1},{9,5},{13... | collective-permute-start | bytes 98312 | tf_op jit(solution)/shard_map/ppermute | solution.py:19
  82.6 5.2 %collective-permute-start.14 = (f32[1,1,1,8,8,128]{5,4,3,2,1,0:T(8,128)S(1)}, f32[1,1,1,8,8,128]{5,4,3,2,1,0:T(8,128)S(1)}, u32[]{:S(2)}, u32[]{:S(2)}) collective-permute-start(f32[1,1,1,8,8,128]{5,4,3,2,1,0:T(8,128)S(1)} %maximum_bitcast_fusion.14), channel_id=1, source_target_pairs={{0,1},{1,2},{2,3},{4,5},{5,6},{6,7},{8,9},{9,10},{10,11},{12,13},{... | collective-permute-start | bytes 98312 | tf_op jit(solution)/shard_map/ppermute | solution.py:16
  87.8 3.8 %collective-permute-start.15 = (f32[1,1,1,8,8,128]{5,4,3,2,1,0:T(8,128)S(1)}, f32[1,1,1,8,8,128]{5,4,3,2,1,0:T(8,128)S(1)}, u32[]{:S(2)}, u32[]{:S(2)}) collective-permute-start(f32[1,1,1,8,8,128]{5,4,3,2,1,0:T(8,128)S(1)} %get-tuple-element.38), channel_id=1, source_target_pairs={{1,0},{2,1},{3,2},{5,4},{6,5},{7,6},{9,8},{10,9},{11,10},{13,12},{... | collective-permute-start | bytes 98312 | tf_op jit(solution)/shard_map/ppermute | solution.py:19
  94.5 0.9 copy-start.4
  99.1 20.3 %all-to-all-start = ((f32[32,2,2048]{2,1,0:T(2,128)}), f32[32,2,2048]{2,1,0:T(2,128)S(1)}, u32[]{:S(2)}, u32[]{:S(2)}) async-start(f32[32,2,2048]{2,1,0:T(2,128)} %bitcast.115), calls=%async_computation | async-start | bytes 1048576 | tf_op jit(solution)/shard_map/all_to_all | solution.py:185
  105.7 5.1 %collective-permute-start.16 = (f32[1,1,1,8,8,128]{5,4,3,2,1,0:T(8,128)S(1)}, f32[1,1,1,8,8,128]{5,4,3,2,1,0:T(8,128)S(1)}, u32[]{:S(2)}, u32[]{:S(2)}) collective-permute-start(f32[1,1,1,8,8,128]{5,4,3,2,1,0:T(8,128)S(1)} %get-tuple-element.65), channel_id=1, source_target_pairs={{0,4},{4,8},{8,12},{12,16},{16,20},{20,24},{24,28},{1,5},{5,9},{9,... | collective-permute-start | bytes 98312 | tf_op jit(solution)/shard_map/ppermute | solution.py:16
  109.1 6.2 %collective-permute-start.17 = (f32[1,1,1,8,8,128]{5,4,3,2,1,0:T(8,128)S(1)}, f32[1,1,1,8,8,128]{5,4,3,2,1,0:T(8,128)S(1)}, u32[]{:S(2)}, u32[]{:S(2)}) collective-permute-start(f32[1,1,1,8,8,128]{5,4,3,2,1,0:T(8,128)S(1)} %get-tuple-element.66), channel_id=1, source_target_pairs={{4,0},{8,4},{12,8},{16,12},{20,16},{24,20},{28,24},{5,1},{9,5},{13... | collective-permute-start | bytes 98312 | tf_op jit(solution)/shard_map/ppermute | solution.py:19
  120.4 9.1 %collective-permute-start.18 = (f32[1,1,1,8,8,128]{5,3,4,2,1,0:T(8,128)S(1)}, f32[1,1,1,8,8,128]{5,3,4,2,1,0:T(8,128)S(1)}, u32[]{:S(2)}, u32[]{:S(2)}) collective-permute-start(f32[1,1,1,8,8,128]{5,3,4,2,1,0:T(8,128)S(1)} %get-tuple-element.88), channel_id=1, source_target_pairs={{0,1},{1,2},{2,3},{4,5},{5,6},{6,7},{8,9},{9,10},{10,11},{12,13},{... | collective-permute-start | bytes 98312 | tf_op jit(solution)/shard_map/ppermute | solution.py:16
  122.4 7.1 %collective-permute-start.19 = (f32[1,1,1,8,8,128]{5,3,4,2,1,0:T(8,128)S(1)}, f32[1,1,1,8,8,128]{5,3,4,2,1,0:T(8,128)S(1)}, u32[]{:S(2)}, u32[]{:S(2)}) collective-permute-start(f32[1,1,1,8,8,128]{5,3,4,2,1,0:T(8,128)S(1)} %get-tuple-element.89), channel_id=1, source_target_pairs={{1,0},{2,1},{3,2},{5,4},{6,5},{7,6},{9,8},{10,9},{11,10},{13,12},{... | collective-permute-start | bytes 98312 | tf_op jit(solution)/shard_map/ppermute | solution.py:19
  126.0 10.8 %all-to-all-start.1 = ((f32[8,2,2048]{2,1,0:T(2,128)}), f32[8,2,2048]{2,1,0:T(2,128)S(1)}, u32[]{:S(2)}, u32[]{:S(2)}) async-start(f32[8,2,2048]{2,1,0:T(2,128)} %broadcast_in_dim.209), calls=%async_computation.1 | async-start | bytes 262144 | tf_op jit(solution)/shard_map/all_to_all | solution.py:194

commit v20 on v18

--- a/solution.py
+++ b/solution.py
@@ -114,8 +114,8 @@
     )
 
 
-def assemble(values_in, ride=None, then=None):
-    lower, upper = faces(values_in, 3)
+def assemble(values_in, ride=None, then=None, x_faces=None):
+    lower, upper = faces(values_in, 3) if x_faces is None else x_faces
     rim_faces = jnp.concatenate([lower, upper], 1)
     padded = padded_2(rim_faces, (("ex", 1),), 1)
     if ride is not None:
@@ -203,7 +203,10 @@
     delta = (high - low) / 2.0
     sigma = theta / delta
     rho_now = 1.0 / sigma
-    both, _ = assemble(jnp.stack([source, local_diagonal(metric, weights, stiff)]))
+    diagonal = local_diagonal(metric, weights, stiff)
+    last = source.shape[2] - 1
+    rims = [jnp.stack([source[:, :, edge], diagonal[:, :, edge]]) for edge in (0, last)]
+    both, _ = assemble(jnp.stack([source, diagonal]), x_faces=rims)
     rhs = both[0]
     pinv = 1.0 / both[1]
     pressure = jnp.zeros_like(source)

time: 137 us -> 135 us (0.985)
  waiting for transfers between devices: 46.8 us -> 43.6 us
  starting transfers between devices: 55.7 us -> 57.3 us
  other arithmetic: 14.5 us -> 13 us
    ppermute x10, waiting for transfers between devices: 10.6 us -> 6.99 us  [padded_2(): lax.ppermute(lax.slice_in_dim(block, block.shape[dim] - width, None, axis...]
    ppermute x10, starting transfers between devices: 18.6 us -> 20.2 us  [padded_2(): lax.ppermute(lax.slice_in_dim(block, 0, width, axis=dim), axis, backward)]
  transfers between devices with their start and end apart: 22 -> 22, of which waited for: 19 -> 18; matrix products, arithmetic and copies ran while one was open for 9% -> 9% of each run, Pallas kernels for 0% -> 0%
where the time goes in v20:
time: 135 us; the launch traced here: 134 us
  starting transfers between devices  57.3 us (42%)
  waiting for transfers between devices  43.6 us (32%)
  other arithmetic  13 us (10%)
  matrix products  12 us (9%)
  local copies, waits for them, and re-layouts  6.25 us (5%)
  between operations  1.69 us (1%)
    ppermute x10, starting transfers between devices, padded_2(): lax.ppermute(lax.slice_in_dim(block, block.shape[dim] - width, None, axis...  28.7 us
    ppermute x10, waiting for transfers between devices, padded_2(): lax.ppermute(lax.slice_in_dim(block, 0, width, axis=dim), axis, backward)  26.2 us
    ppermute x10, starting transfers between devices, padded_2(): lax.ppermute(lax.slice_in_dim(block, 0, width, axis=dim), axis, backward)  20.2 us
    ppermute x10, waiting for transfers between devices, padded_2(): lax.ppermute(lax.slice_in_dim(block, block.shape[dim] - width, None, axis...  6.99 us
    all_to_all x1, waiting for transfers between devices, strip_gather(): whole = lax.all_to_all(spread_out, 'ex', 0, 0, tiled=True)  6.31 us
    all_to_all x1, starting transfers between devices, strip_reduce(): return lax.all_to_all(chunks, ('ex', 'ey'), 0, 0, tiled=True).sum(0)  5.02 us
    all_to_all x1, waiting for transfers between devices, strip_reduce(): return lax.all_to_all(chunks, ('ex', 'ey'), 0, 0, tiled=True).sum(0)  4.09 us
    all_to_all x1, starting transfers between devices, strip_gather(): whole = lax.all_to_all(spread_out, 'ex', 0, 0, tiled=True)  3.46 us
  transfers between devices with their start and end apart: 22, of which 18 were waited for; matrix products, arithmetic and copies ran while one was open for 9% of the time, Pallas kernels for 0%

profile of v20, /device:TPU:2, one launch (start us, length us, event | category | flops | bytes accessed | tf_op | source)
XLA Modules:
  0.0 133.9 jit_solution(15629941768326690129)
XLA Ops:
  4.5 3.4 %collective-permute-start = (f32[2,1,1,8,8,128]{5,4,3,2,1,0:T(8,128)S(1)}, f32[2,1,1,8,8,128]{5,4,3,2,1,0:T(8,128)S(1)}, u32[]{:S(2)}, u32[]{:S(2)}) collective-permute-start(f32[2,1,1,8,8,128]{5,4,3,2,1,0:T(8,128)S(1)} %pad_maximum_fusion.9), channel_id=1, source_target_pairs={{0,4},{4,8},{8,12},{12,16},{16,20},{20,24},{24,28},{1,5},{5,9},{9,... | collective-permute-start | bytes 196616 | tf_op jit(solution)/shard_map/ppermute | solution.py:16
  8.0 0.9 fusion.97
  8.8 0.8 and_select_fusion.2
  9.6 1.2 fusion.20
  10.9 1.3 collective-permute-start.1
  12.6 4.5 %collective-permute-done.1 = f32[2,1,1,8,8,128]{5,4,3,2,1,0:T(8,128)S(1)} collective-permute-done((f32[2,1,1,8,8,128]{5,4,3,2,1,0:T(8,128)S(1)}, f32[2,1,1,8,8,128]{5,4,3,2,1,0:T(8,128)S(1)}, u32[]{:S(2)}, u32[]{:S(2)}) %collective-permute-start.1) | collective-permute-done | bytes 65568 | tf_op jit(solution)/shard_map/ppermute | solution.py:19
  17.4 1.9 %collective-permute-start.2 = (f32[2,1,1,8,8,128]{5,3,0,4,2,1:T(8,128)S(1)}, f32[2,1,1,8,8,128]{5,3,0,4,2,1:T(8,128)S(1)}, u32[]{:S(2)}, u32[]{:S(2)}) collective-permute-start(f32[2,1,1,8,8,128]{5,3,0,4,2,1:T(8,128)S(1)} %get-tuple-element.51), channel_id=1, source_target_pairs={{0,1},{1,2},{2,3},{4,5},{5,6},{6,7},{8,9},{9,10},{10,11},{12,13},{... | collective-permute-start | bytes 196616 | tf_op jit(solution)/shard_map/ppermute | solution.py:16
  19.3 3.6 %collective-permute-start.3 = (f32[2,1,1,8,8,128]{5,3,0,4,2,1:T(8,128)S(1)}, f32[2,1,1,8,8,128]{5,3,0,4,2,1:T(8,128)S(1)}, u32[]{:S(2)}, u32[]{:S(2)}) collective-permute-start(f32[2,1,1,8,8,128]{5,3,0,4,2,1:T(8,128)S(1)} %get-tuple-element.52), channel_id=1, source_target_pairs={{1,0},{2,1},{3,2},{5,4},{6,5},{7,6},{9,8},{10,9},{11,10},{13,12},{... | collective-permute-start | bytes 196616 | tf_op jit(solution)/shard_map/ppermute | solution.py:19
  23.3 1.6 %collective-permute-done.3 = f32[2,1,1,8,8,128]{5,3,0,4,2,1:T(8,128)S(1)} collective-permute-done((f32[2,1,1,8,8,128]{5,3,0,4,2,1:T(8,128)S(1)}, f32[2,1,1,8,8,128]{5,3,0,4,2,1:T(8,128)S(1)}, u32[]{:S(2)}, u32[]{:S(2)}) %collective-permute-start.3) | collective-permute-done | bytes 65568 | tf_op jit(solution)/shard_map/ppermute | solution.py:19
  26.6 0.9 fusion.30
  27.6 4.3 %collective-permute-start.4 = (f32[1,1,1,8,8,128]{5,4,3,2,1,0:T(8,128)S(1)}, f32[1,1,1,8,8,128]{5,4,3,2,1,0:T(8,128)S(1)}, u32[]{:S(2)}, u32[]{:S(2)}) collective-permute-start(f32[1,1,1,8,8,128]{5,4,3,2,1,0:T(8,128)S(1)} %bitcast.474), channel_id=1, source_target_pairs={{0,4},{4,8},{8,12},{12,16},{16,20},{20,24},{24,28},{1,5},{5,9},{9,... | collective-permute-start | bytes 98312 | tf_op jit(solution)/shard_map/ppermute | solution.py:16
  31.9 1.3 collective-permute-start.5
  33.5 4.2 %collective-permute-done.5 = f32[1,1,1,8,8,128]{5,4,3,2,1,0:T(8,128)S(1)} collective-permute-done((f32[1,1,1,8,8,128]{5,4,3,2,1,0:T(8,128)S(1)}, f32[1,1,1,8,8,128]{5,4,3,2,1,0:T(8,128)S(1)}, u32[]{:S(2)}, u32[]{:S(2)}) %collective-permute-start.5) | collective-permute-done | bytes 32800 | tf_op jit(solution)/shard_map/ppermute | solution.py:19
  37.7 1.9 %collective-permute-start.6 = (f32[1,1,1,8,8,128]{5,3,4,2,1,0:T(8,128)S(1)}, f32[1,1,1,8,8,128]{5,3,4,2,1,0:T(8,128)S(1)}, u32[]{:S(2)}, u32[]{:S(2)}) collective-permute-start(f32[1,1,1,8,8,128]{5,3,4,2,1,0:T(8,128)S(1)} %maximum_bitcast_fusion.15), channel_id=1, source_target_pairs={{0,1},{1,2},{2,3},{4,5},{5,6},{6,7},{8,9},{9,10},{10,11},{12,13},{... | collective-permute-start | bytes 98312 | tf_op jit(solution)/shard_map/ppermute | solution.py:16
  39.7 1.9 %fusion = f32[768,256]{1,0:T(8,128)S(1)} fusion(bf16[256,4096]{1,0:T(8,128)(2,1)S(1)} %get-tuple-element.95, bf16[256,4096]{1,0:T(8,128)(2,1)S(1)} %get-tuple-element.96, bf16[256,4096]{1,0:T(8,128)(2,1)S(1)} %get-tuple-element.94, s32[4096]{0:T(1024)S(1)} %add_select_fusion), kind=kOutput, calls=%fused_computation | convolution fusion | flops 1630535680 | bytes 7094272 | tf_op jit(solution)/shard_map/dot_general | solution.py:170
  41.6 1.4 %collective-permute-done.6 = f32[1,1,1,8,8,128]{5,3,4,2,1,0:T(8,128)S(1)} collective-permute-done((f32[1,1,1,8,8,128]{5,3,4,2,1,0:T(8,128)S(1)}, f32[1,1,1,8,8,128]{5,3,4,2,1,0:T(8,128)S(1)}, u32[]{:S(2)}, u32[]{:S(2)}) %collective-permute-start.6) | collective-permute-done | bytes 32800 | tf_op jit(solution)/shard_map/ppermute | solution.py:16
  43.0 2.3 %collective-permute-start.7 = (f32[1,1,1,8,8,128]{5,3,4,2,1,0:T(8,128)S(1)}, f32[1,1,1,8,8,128]{5,3,4,2,1,0:T(8,128)S(1)}, u32[]{:S(2)}, u32[]{:S(2)}) collective-permute-start(f32[1,1,1,8,8,128]{5,3,4,2,1,0:T(8,128)S(1)} %get-tuple-element.44), channel_id=1, source_target_pairs={{1,0},{2,1},{3,2},{5,4},{6,5},{7,6},{9,8},{10,9},{11,10},{13,12},{... | collective-permute-start | bytes 98312 | tf_op jit(solution)/shard_map/ppermute | solution.py:19
  45.5 1.4 %collective-permute-done.7 = f32[1,1,1,8,8,128]{5,3,4,2,1,0:T(8,128)S(1)} collective-permute-done((f32[1,1,1,8,8,128]{5,3,4,2,1,0:T(8,128)S(1)}, f32[1,1,1,8,8,128]{5,3,4,2,1,0:T(8,128)S(1)}, u32[]{:S(2)}, u32[]{:S(2)}) %collective-permute-start.7) | collective-permute-done | bytes 32800 | tf_op jit(solution)/shard_map/ppermute | solution.py:19
  48.8 4.1 %collective-permute-start.8 = (f32[1,1,1,8,8,128]{5,4,3,2,1,0:T(8,128)S(1)}, f32[1,1,1,8,8,128]{5,4,3,2,1,0:T(8,128)S(1)}, u32[]{:S(2)}, u32[]{:S(2)}) collective-permute-start(f32[1,1,1,8,8,128]{5,4,3,2,1,0:T(8,128)S(1)} %get-tuple-element.74), channel_id=1, source_target_pairs={{0,4},{4,8},{8,12},{12,16},{16,20},{20,24},{24,28},{1,5},{5,9},{9,... | collective-permute-start | bytes 98312 | tf_op jit(solution)/shard_map/ppermute | solution.py:16
  52.9 1.3 collective-permute-start.9
  54.4 4.2 %collective-permute-done.9 = f32[1,1,1,8,8,128]{5,4,3,2,1,0:T(8,128)S(1)} collective-permute-done((f32[1,1,1,8,8,128]{5,4,3,2,1,0:T(8,128)S(1)}, f32[1,1,1,8,8,128]{5,4,3,2,1,0:T(8,128)S(1)}, u32[]{:S(2)}, u32[]{:S(2)}) %collective-permute-start.9) | collective-permute-done | bytes 32800 | tf_op jit(solution)/shard_map/ppermute | solution.py:19
  58.7 1.9 %collective-permute-start.10 = (f32[1,1,1,8,8,128]{5,4,3,2,1,0:T(8,128)S(1)}, f32[1,1,1,8,8,128]{5,4,3,2,1,0:T(8,128)S(1)}, u32[]{:S(2)}, u32[]{:S(2)}) collective-permute-start(f32[1,1,1,8,8,128]{5,4,3,2,1,0:T(8,128)S(1)} %maximum_bitcast_fusion.13), channel_id=1, source_target_pairs={{0,1},{1,2},{2,3},{4,5},{5,6},{6,7},{8,9},{9,10},{10,11},{12,13},{... | collective-permute-start | bytes 98312 | tf_op jit(solution)/shard_map/ppermute | solution.py:16
  60.7 3.2 %collective-permute-done.10 = f32[1,1,1,8,8,128]{5,4,3,2,1,0:T(8,128)S(1)} collective-permute-done((f32[1,1,1,8,8,128]{5,4,3,2,1,0:T(8,128)S(1)}, f32[1,1,1,8,8,128]{5,4,3,2,1,0:T(8,128)S(1)}, u32[]{:S(2)}, u32[]{:S(2)}) %collective-permute-start.10) | collective-permute-done | bytes 32800 | tf_op jit(solution)/shard_map/ppermute | solution.py:16
  63.9 1.9 %collective-permute-start.11 = (f32[1,1,1,8,8,128]{5,4,3,2,1,0:T(8,128)S(1)}, f32[1,1,1,8,8,128]{5,4,3,2,1,0:T(8,128)S(1)}, u32[]{:S(2)}, u32[]{:S(2)}) collective-permute-start(f32[1,1,1,8,8,128]{5,4,3,2,1,0:T(8,128)S(1)} %get-tuple-element.42), channel_id=1, source_target_pairs={{1,0},{2,1},{3,2},{5,4},{6,5},{7,6},{9,8},{10,9},{11,10},{13,12},{... | collective-permute-start | bytes 98312 | tf_op jit(solution)/shard_map/ppermute | solution.py:19
  66.0 1.5 %collective-permute-done.11 = f32[1,1,1,8,8,128]{5,4,3,2,1,0:T(8,128)S(1)} collective-permute-done((f32[1,1,1,8,8,128]{5,4,3,2,1,0:T(8,128)S(1)}, f32[1,1,1,8,8,128]{5,4,3,2,1,0:T(8,128)S(1)}, u32[]{:S(2)}, u32[]{:S(2)}) %collective-permute-start.11) | collective-permute-done | bytes 32800 | tf_op jit(solution)/shard_map/ppermute | solution.py:19
  69.5 3.7 %collective-permute-start.12 = (f32[1,1,1,8,8,128]{5,4,3,2,1,0:T(8,128)S(1)}, f32[1,1,1,8,8,128]{5,4,3,2,1,0:T(8,128)S(1)}, u32[]{:S(2)}, u32[]{:S(2)}) collective-permute-start(f32[1,1,1,8,8,128]{5,4,3,2,1,0:T(8,128)S(1)} %get-tuple-element.68), channel_id=1, source_target_pairs={{0,4},{4,8},{8,12},{12,16},{16,20},{20,24},{24,28},{1,5},{5,9},{9,... | collective-permute-start | bytes 98312 | tf_op jit(solution)/shard_map/ppermute | solution.py:16
  73.2 1.3 collective-permute-start.13
  74.8 4.2 %collective-permute-done.13 = f32[1,1,1,8,8,128]{5,4,3,2,1,0:T(8,128)S(1)} collective-permute-done((f32[1,1,1,8,8,128]{5,4,3,2,1,0:T(8,128)S(1)}, f32[1,1,1,8,8,128]{5,4,3,2,1,0:T(8,128)S(1)}, u32[]{:S(2)}, u32[]{:S(2)}) %collective-permute-start.13) | collective-permute-done | bytes 32800 | tf_op jit(solution)/shard_map/ppermute | solution.py:19
  79.1 2.1 %collective-permute-start.14 = (f32[1,1,1,8,8,128]{5,4,3,2,1,0:T(8,128)S(1)}, f32[1,1,1,8,8,128]{5,4,3,2,1,0:T(8,128)S(1)}, u32[]{:S(2)}, u32[]{:S(2)}) collective-permute-start(f32[1,1,1,8,8,128]{5,4,3,2,1,0:T(8,128)S(1)} %maximum_bitcast_fusion.11), channel_id=1, source_target_pairs={{0,1},{1,2},{2,3},{4,5},{5,6},{6,7},{8,9},{9,10},{10,11},{12,13},{... | collective-permute-start | bytes 98312 | tf_op jit(solution)/shard_map/ppermute | solution.py:16
  81.2 1.9 %fusion.15 = f32[768,4096]{1,0:T(8,128)S(1)} fusion(s32[4096]{0:T(1024)S(1)} %bitcast.468, bf16[256,256]{1,0:T(8,128)(2,1)S(1)} %get-tuple-element.62, bf16[256,256]{1,0:T(8,128)(2,1)S(1)} %get-tuple-element.63, bf16[256,256]{1,0:T(8,128)(2,1)S(1)} %get-tuple-element.61), kind=kOutput, calls=%fused_computation.19 | convolution fusion | flops 1612840960 | bytes 12992512 | tf_op jit(solution)/shard_map/dot_general | solution.py:156
  83.0 1.4 %collective-permute-done.14 = f32[1,1,1,8,8,128]{5,4,3,2,1,0:T(8,128)S(1)} collective-permute-done((f32[1,1,1,8,8,128]{5,4,3,2,1,0:T(8,128)S(1)}, f32[1,1,1,8,8,128]{5,4,3,2,1,0:T(8,128)S(1)}, u32[]{:S(2)}, u32[]{:S(2)}) %collective-permute-start.14) | collective-permute-done | bytes 32800 | tf_op jit(solution)/shard_map/ppermute | solution.py:16
  84.5 2.2 %collective-permute-start.15 = (f32[1,1,1,8,8,128]{5,4,3,2,1,0:T(8,128)S(1)}, f32[1,1,1,8,8,128]{5,4,3,2,1,0:T(8,128)S(1)}, u32[]{:S(2)}, u32[]{:S(2)}) collective-permute-start(f32[1,1,1,8,8,128]{5,4,3,2,1,0:T(8,128)S(1)} %get-tuple-element.38), channel_id=1, source_target_pairs={{1,0},{2,1},{3,2},{5,4},{6,5},{7,6},{9,8},{10,9},{11,10},{13,12},{... | collective-permute-start | bytes 98312 | tf_op jit(solution)/shard_map/ppermute | solution.py:19
  86.7 1.4 %fusion.9 = f32[4096]{0:T(1024)S(1)} fusion(f32[768,4096]{1,0:T(8,128)S(1)} %fusion.15, s32[4096]{0:T(1024)S(1)} %bitcast.466), kind=kLoop, calls=%fused_computation.11 | loop fusion | flops 5238784 | bytes 12615680 | tf_op jit(solution)/shard_map/reduce_sum | solution.py:161
  88.8 0.8 fusion.114
  89.8 1.3 %fusion.14 = f32[512,4096]{1,0:T(8,128)S(1)} fusion(s32[4096]{0:T(1024)S(1)} %bitcast.469, bf16[256,256]{1,0:T(8,128)(2,1)S(1)} %get-tuple-element.58, bf16[256,256]{1,0:T(8,128)(2,1)S(1)} %get-tuple-element.57), kind=kOutput, calls=%fused_computation.18 | convolution fusion | flops 1075314688 | bytes 8667136 | tf_op jit(solution)/shard_map/dot_general | solution.py:156
  91.1 0.9 fusion.7
  92.1 0.9 fusion.17
  92.9 1.4 %fusion.10 = f32[512,256]{1,0:T(8,128)S(1)} fusion(bf16[256,4096]{1,0:T(8,128)(2,1)S(1)} %get-tuple-element.93, bf16[256,4096]{1,0:T(8,128)(2,1)S(1)} %get-tuple-element.92, s32[4096]{0:T(1024)S(1)} %add_select_fusion), kind=kOutput, calls=%fused_computation.13 | convolution fusion | flops 1083179008 | bytes 4734976 | tf_op jit(solution)/shard_map/dot_general | solution.py:170
  94.5 1.2 copy.213
  95.7 5.0 %all-to-all-start = ((f32[32,2,2048]{2,1,0:T(2,128)}), f32[32,2,2048]{2,1,0:T(2,128)S(1)}, u32[]{:S(2)}, u32[]{:S(2)}) async-start(f32[32,2,2048]{2,1,0:T(2,128)} %bitcast.109), calls=%async_computation | async-start | bytes 1048576 | tf_op jit(solution)/shard_map/all_to_all | solution.py:185
  102.1 3.4 %collective-permute-start.16 = (f32[1,1,1,8,8,128]{5,4,3,2,1,0:T(8,128)S(1)}, f32[1,1,1,8,8,128]{5,4,3,2,1,0:T(8,128)S(1)}, u32[]{:S(2)}, u32[]{:S(2)}) collective-permute-start(f32[1,1,1,8,8,128]{5,4,3,2,1,0:T(8,128)S(1)} %get-tuple-element.59), channel_id=1, source_target_pairs={{0,4},{4,8},{8,12},{12,16},{16,20},{20,24},{24,28},{1,5},{5,9},{9,... | collective-permute-start | bytes 98312 | tf_op jit(solution)/shard_map/ppermute | solution.py:16
  105.5 1.3 collective-permute-start.17
  107.2 4.5 %collective-permute-done.17 = f32[1,1,1,8,8,128]{5,4,3,2,1,0:T(8,128)S(1)} collective-permute-done((f32[1,1,1,8,8,128]{5,4,3,2,1,0:T(8,128)S(1)}, f32[1,1,1,8,8,128]{5,4,3,2,1,0:T(8,128)S(1)}, u32[]{:S(2)}, u32[]{:S(2)}) %collective-permute-start.17) | collective-permute-done | bytes 32800 | tf_op jit(solution)/shard_map/ppermute | solution.py:19
  111.7 4.1 %all-to-all-done = f32[32,2,2048]{2,1,0:T(2,128)S(1)} async-done(((f32[32,2,2048]{2,1,0:T(2,128)}), f32[32,2,2048]{2,1,0:T(2,128)S(1)}, u32[]{:S(2)}, u32[]{:S(2)}) %all-to-all-start) | async-done | bytes 524320 | tf_op jit(solution)/shard_map/all_to_all | solution.py:185
  116.7 1.9 %collective-permute-start.18 = (f32[1,1,1,8,8,128]{5,3,4,2,1,0:T(8,128)S(1)}, f32[1,1,1,8,8,128]{5,3,4,2,1,0:T(8,128)S(1)}, u32[]{:S(2)}, u32[]{:S(2)}) collective-permute-start(f32[1,1,1,8,8,128]{5,3,4,2,1,0:T(8,128)S(1)} %get-tuple-element.86), channel_id=1, source_target_pairs={{0,1},{1,2},{2,3},{4,5},{5,6},{6,7},{8,9},{9,10},{10,11},{12,13},{... | collective-permute-start | bytes 98312 | tf_op jit(solution)/shard_map/ppermute | solution.py:16
  118.7 3.6 %collective-permute-start.19 = (f32[1,1,1,8,8,128]{5,3,4,2,1,0:T(8,128)S(1)}, f32[1,1,1,8,8,128]{5,3,4,2,1,0:T(8,128)S(1)}, u32[]{:S(2)}, u32[]{:S(2)}) collective-permute-start(f32[1,1,1,8,8,128]{5,3,4,2,1,0:T(8,128)S(1)} %get-tuple-element.87), channel_id=1, source_target_pairs={{1,0},{2,1},{3,2},{5,4},{6,5},{7,6},{9,8},{10,9},{11,10},{13,12},{... | collective-permute-start | bytes 98312 | tf_op jit(solution)/shard_map/ppermute | solution.py:19
  122.4 3.5 %all-to-all-start.1 = ((f32[8,2,2048]{2,1,0:T(2,128)}), f32[8,2,2048]{2,1,0:T(2,128)S(1)}, u32[]{:S(2)}, u32[]{:S(2)}) async-start(f32[8,2,2048]{2,1,0:T(2,128)} %broadcast_in_dim.209), calls=%async_computation.1 | async-start | bytes 262144 | tf_op jit(solution)/shard_map/all_to_all | solution.py:194
  126.9 6.3 %all-to-all-done.1 = f32[8,2,2048]{2,1,0:T(2,128)S(1)} async-done(((f32[8,2,2048]{2,1,0:T(2,128)}), f32[8,2,2048]{2,1,0:T(2,128)S(1)}, u32[]{:S(2)}, u32[]{:S(2)}) %all-to-all-start.1) | async-done | bytes 131104 | tf_op jit(solution)/shard_map/all_to_all | solution.py:194
  (145 shorter events, 16.9 us)
Async XLA Ops:
  0.6 11.6 %copy-start.7 = (f32[8]{0:T(128)S(1)}, f32[8]{0:T(128)}, u32[]{:S(2)}) copy-start(f32[8]{0:T(128)} %constant.124) | copy-start | bytes 100
  0.6 11.6 %copy-start.6 = (f32[8]{0:T(128)S(1)}, f32[8]{0:T(128)}, u32[]{:S(2)}) copy-start(f32[8]{0:T(128)} %constant.125) | copy-start | bytes 100
  0.7 11.7 %copy-start.1 = (f32[1,1,8,8,8,128]{5,4,3,2,1,0:T(8,128)S(1)}, f32[1,1,8,8,8,128]{5,4,3,2,1,0:T(8,128)}, u32[]{:S(2)}) copy-start(f32[1,1,8,8,8,128]{5,4,3,2,1,0:T(8,128)} %param.36) | copy-start | bytes 786436
  4.5 6.4 %collective-permute-start = (f32[2,1,1,8,8,128]{5,4,3,2,1,0:T(8,128)S(1)}, f32[2,1,1,8,8,128]{5,4,3,2,1,0:T(8,128)S(1)}, u32[]{:S(2)}, u32[]{:S(2)}) collective-permute-start(f32[2,1,1,8,8,128]{5,4,3,2,1,0:T(8,128)S(1)} %pad_maximum_fusion.9), channel_id=1, source_target_pairs={{0,4},{4,8},{8,12},{12,16},{16,20},{20,24},{24,28},{1,5},{5,9},{9,... | collective-permute-start | bytes 196616 | tf_op jit(solution)/shard_map/ppermute | solution.py:16
  9.6 13.3 %copy-start.4 = (s32[1,4096,1]{1,2,0:T(1,128)S(1)}, s32[1,4096,1]{1,2,0:T(1,128)}, u32[]{:S(2)}) copy-start(s32[1,4096,1]{1,2,0:T(1,128)} %param.39) | copy-start | bytes 49156
  10.9 6.2 %collective-permute-start.1 = (f32[2,1,1,8,8,128]{5,4,3,2,1,0:T(8,128)S(1)}, f32[2,1,1,8,8,128]{5,4,3,2,1,0:T(8,128)S(1)}, u32[]{:S(2)}, u32[]{:S(2)}) collective-permute-start(f32[2,1,1,8,8,128]{5,4,3,2,1,0:T(8,128)S(1)} %get-tuple-element.89), channel_id=1, source_target_pairs={{4,0},{8,4},{12,8},{16,12},{20,16},{24,20},{28,24},{5,1},{9,5},{13... | collective-permute-start | bytes 196616 | tf_op jit(solution)/shard_map/ppermute | solution.py:19
  17.3 8.4 %copy-start = (f32[8,8,1,1]{1,0,3,2:T(8,128)S(1)}, f32[8,8,1,1]{1,0,3,2:T(8,128)}, u32[]{:S(2)}) copy-start(f32[8,8,1,1]{1,0,3,2:T(8,128)} %constant.130) | copy-start | bytes 772
  17.4 5.9 %collective-permute-start.2 = (f32[2,1,1,8,8,128]{5,3,0,4,2,1:T(8,128)S(1)}, f32[2,1,1,8,8,128]{5,3,0,4,2,1:T(8,128)S(1)}, u32[]{:S(2)}, u32[]{:S(2)}) collective-permute-start(f32[2,1,1,8,8,128]{5,3,0,4,2,1:T(8,128)S(1)} %get-tuple-element.51), channel_id=1, source_target_pairs={{0,1},{1,2},{2,3},{4,5},{5,6},{6,7},{8,9},{9,10},{10,11},{12,13},{... | collective-permute-start | bytes 196616 | tf_op jit(solution)/shard_map/ppermute | solution.py:16
  19.3 5.5 %collective-permute-start.3 = (f32[2,1,1,8,8,128]{5,3,0,4,2,1:T(8,128)S(1)}, f32[2,1,1,8,8,128]{5,3,0,4,2,1:T(8,128)S(1)}, u32[]{:S(2)}, u32[]{:S(2)}) collective-permute-start(f32[2,1,1,8,8,128]{5,3,0,4,2,1:T(8,128)S(1)} %get-tuple-element.52), channel_id=1, source_target_pairs={{1,0},{2,1},{3,2},{5,4},{6,5},{7,6},{9,8},{10,9},{11,10},{13,12},{... | collective-permute-start | bytes 196616 | tf_op jit(solution)/shard_map/ppermute | solution.py:19
  25.0 8.2 %copy-start.2 = (s32[1,4096]{1,0:T(1,128)S(1)}, s32[1,4096]{1,0:T(1,128)}, u32[]{:S(2)}) copy-start(s32[1,4096]{1,0:T(1,128)} %param.40) | copy-start | bytes 49156
  27.6 5.9 %collective-permute-start.4 = (f32[1,1,1,8,8,128]{5,4,3,2,1,0:T(8,128)S(1)}, f32[1,1,1,8,8,128]{5,4,3,2,1,0:T(8,128)S(1)}, u32[]{:S(2)}, u32[]{:S(2)}) collective-permute-start(f32[1,1,1,8,8,128]{5,4,3,2,1,0:T(8,128)S(1)} %bitcast.474), channel_id=1, source_target_pairs={{0,4},{4,8},{8,12},{12,16},{16,20},{20,24},{24,28},{1,5},{5,9},{9,... | collective-permute-start | bytes 98312 | tf_op jit(solution)/shard_map/ppermute | solution.py:16
  31.9 5.8 %collective-permute-start.5 = (f32[1,1,1,8,8,128]{5,4,3,2,1,0:T(8,128)S(1)}, f32[1,1,1,8,8,128]{5,4,3,2,1,0:T(8,128)S(1)}, u32[]{:S(2)}, u32[]{:S(2)}) collective-permute-start(f32[1,1,1,8,8,128]{5,4,3,2,1,0:T(8,128)S(1)} %bitcast.476), channel_id=1, source_target_pairs={{4,0},{8,4},{12,8},{16,12},{20,16},{24,20},{28,24},{5,1},{9,5},{13... | collective-permute-start | bytes 98312 | tf_op jit(solution)/shard_map/ppermute | solution.py:19
  37.7 5.2 %collective-permute-start.6 = (f32[1,1,1,8,8,128]{5,3,4,2,1,0:T(8,128)S(1)}, f32[1,1,1,8,8,128]{5,3,4,2,1,0:T(8,128)S(1)}, u32[]{:S(2)}, u32[]{:S(2)}) collective-permute-start(f32[1,1,1,8,8,128]{5,3,4,2,1,0:T(8,128)S(1)} %maximum_bitcast_fusion.15), channel_id=1, source_target_pairs={{0,1},{1,2},{2,3},{4,5},{5,6},{6,7},{8,9},{9,10},{10,11},{12,13},{... | collective-permute-start | bytes 98312 | tf_op jit(solution)/shard_map/ppermute | solution.py:16
  43.0 17.6 %copy-start.3 = (s32[1,4096]{1,0:T(1,128)S(1)}, s32[1,4096]{1,0:T(1,128)}, u32[]{:S(2)}) copy-start(s32[1,4096]{1,0:T(1,128)} %param.38) | copy-start | bytes 49156
  43.0 3.9 %collective-permute-start.7 = (f32[1,1,1,8,8,128]{5,3,4,2,1,0:T(8,128)S(1)}, f32[1,1,1,8,8,128]{5,3,4,2,1,0:T(8,128)S(1)}, u32[]{:S(2)}, u32[]{:S(2)}) collective-permute-start(f32[1,1,1,8,8,128]{5,3,4,2,1,0:T(8,128)S(1)} %get-tuple-element.44), channel_id=1, source_target_pairs={{1,0},{2,1},{3,2},{5,4},{6,5},{7,6},{9,8},{10,9},{11,10},{13,12},{... | collective-permute-start | bytes 98312 | tf_op jit(solution)/shard_map/ppermute | solution.py:19
  48.8 5.7 %collective-permute-start.8 = (f32[1,1,1,8,8,128]{5,4,3,2,1,0:T(8,128)S(1)}, f32[1,1,1,8,8,128]{5,4,3,2,1,0:T(8,128)S(1)}, u32[]{:S(2)}, u32[]{:S(2)}) collective-permute-start(f32[1,1,1,8,8,128]{5,4,3,2,1,0:T(8,128)S(1)} %get-tuple-element.74), channel_id=1, source_target_pairs={{0,4},{4,8},{8,12},{12,16},{16,20},{20,24},{24,28},{1,5},{5,9},{9,... | collective-permute-start | bytes 98312 | tf_op jit(solution)/shard_map/ppermute | solution.py:16
  52.9 5.8 %collective-permute-start.9 = (f32[1,1,1,8,8,128]{5,4,3,2,1,0:T(8,128)S(1)}, f32[1,1,1,8,8,128]{5,4,3,2,1,0:T(8,128)S(1)}, u32[]{:S(2)}, u32[]{:S(2)}) collective-permute-start(f32[1,1,1,8,8,128]{5,4,3,2,1,0:T(8,128)S(1)} %get-tuple-element.75), channel_id=1, source_target_pairs={{4,0},{8,4},{12,8},{16,12},{20,16},{24,20},{28,24},{5,1},{9,5},{13... | collective-permute-start | bytes 98312 | tf_op jit(solution)/shard_map/ppermute | solution.py:19
  58.7 5.2 %collective-permute-start.10 = (f32[1,1,1,8,8,128]{5,4,3,2,1,0:T(8,128)S(1)}, f32[1,1,1,8,8,128]{5,4,3,2,1,0:T(8,128)S(1)}, u32[]{:S(2)}, u32[]{:S(2)}) collective-permute-start(f32[1,1,1,8,8,128]{5,4,3,2,1,0:T(8,128)S(1)} %maximum_bitcast_fusion.13), channel_id=1, source_target_pairs={{0,1},{1,2},{2,3},{4,5},{5,6},{6,7},{8,9},{9,10},{10,11},{12,13},{... | collective-permute-start | bytes 98312 | tf_op jit(solution)/shard_map/ppermute | solution.py:16
  63.9 3.5 %collective-permute-start.11 = (f32[1,1,1,8,8,128]{5,4,3,2,1,0:T(8,128)S(1)}, f32[1,1,1,8,8,128]{5,4,3,2,1,0:T(8,128)S(1)}, u32[]{:S(2)}, u32[]{:S(2)}) collective-permute-start(f32[1,1,1,8,8,128]{5,4,3,2,1,0:T(8,128)S(1)} %get-tuple-element.42), channel_id=1, source_target_pairs={{1,0},{2,1},{3,2},{5,4},{6,5},{7,6},{9,8},{10,9},{11,10},{13,12},{... | collective-permute-start | bytes 98312 | tf_op jit(solution)/shard_map/ppermute | solution.py:19
  69.5 5.3 %collective-permute-start.12 = (f32[1,1,1,8,8,128]{5,4,3,2,1,0:T(8,128)S(1)}, f32[1,1,1,8,8,128]{5,4,3,2,1,0:T(8,128)S(1)}, u32[]{:S(2)}, u32[]{:S(2)}) collective-permute-start(f32[1,1,1,8,8,128]{5,4,3,2,1,0:T(8,128)S(1)} %get-tuple-element.68), channel_id=1, source_target_pairs={{0,4},{4,8},{8,12},{12,16},{16,20},{20,24},{24,28},{1,5},{5,9},{9,... | collective-permute-start | bytes 98312 | tf_op jit(solution)/shard_map/ppermute | solution.py:16
  73.2 5.8 %collective-permute-start.13 = (f32[1,1,1,8,8,128]{5,4,3,2,1,0:T(8,128)S(1)}, f32[1,1,1,8,8,128]{5,4,3,2,1,0:T(8,128)S(1)}, u32[]{:S(2)}, u32[]{:S(2)}) collective-permute-start(f32[1,1,1,8,8,128]{5,4,3,2,1,0:T(8,128)S(1)} %get-tuple-element.69), channel_id=1, source_target_pairs={{4,0},{8,4},{12,8},{16,12},{20,16},{24,20},{28,24},{5,1},{9,5},{13... | collective-permute-start | bytes 98312 | tf_op jit(solution)/shard_map/ppermute | solution.py:19
  79.1 5.4 %collective-permute-start.14 = (f32[1,1,1,8,8,128]{5,4,3,2,1,0:T(8,128)S(1)}, f32[1,1,1,8,8,128]{5,4,3,2,1,0:T(8,128)S(1)}, u32[]{:S(2)}, u32[]{:S(2)}) collective-permute-start(f32[1,1,1,8,8,128]{5,4,3,2,1,0:T(8,128)S(1)} %maximum_bitcast_fusion.11), channel_id=1, source_target_pairs={{0,1},{1,2},{2,3},{4,5},{5,6},{6,7},{8,9},{9,10},{10,11},{12,13},{... | collective-permute-start | bytes 98312 | tf_op jit(solution)/shard_map/ppermute | solution.py:16
  84.5 3.8 %collective-permute-start.15 = (f32[1,1,1,8,8,128]{5,4,3,2,1,0:T(8,128)S(1)}, f32[1,1,1,8,8,128]{5,4,3,2,1,0:T(8,128)S(1)}, u32[]{:S(2)}, u32[]{:S(2)}) collective-permute-start(f32[1,1,1,8,8,128]{5,4,3,2,1,0:T(8,128)S(1)} %get-tuple-element.38), channel_id=1, source_target_pairs={{1,0},{2,1},{3,2},{5,4},{6,5},{7,6},{9,8},{10,9},{11,10},{13,12},{... | collective-permute-start | bytes 98312 | tf_op jit(solution)/shard_map/ppermute | solution.py:19
  91.1 0.9 copy-start.5
  95.7 20.1 %all-to-all-start = ((f32[32,2,2048]{2,1,0:T(2,128)}), f32[32,2,2048]{2,1,0:T(2,128)S(1)}, u32[]{:S(2)}, u32[]{:S(2)}) async-start(f32[32,2,2048]{2,1,0:T(2,128)} %bitcast.109), calls=%async_computation | async-start | bytes 1048576 | tf_op jit(solution)/shard_map/all_to_all | solution.py:185
  102.1 5.1 %collective-permute-start.16 = (f32[1,1,1,8,8,128]{5,4,3,2,1,0:T(8,128)S(1)}, f32[1,1,1,8,8,128]{5,4,3,2,1,0:T(8,128)S(1)}, u32[]{:S(2)}, u32[]{:S(2)}) collective-permute-start(f32[1,1,1,8,8,128]{5,4,3,2,1,0:T(8,128)S(1)} %get-tuple-element.59), channel_id=1, source_target_pairs={{0,4},{4,8},{8,12},{12,16},{16,20},{20,24},{24,28},{1,5},{5,9},{9,... | collective-permute-start | bytes 98312 | tf_op jit(solution)/shard_map/ppermute | solution.py:16
  105.5 6.2 %collective-permute-start.17 = (f32[1,1,1,8,8,128]{5,4,3,2,1,0:T(8,128)S(1)}, f32[1,1,1,8,8,128]{5,4,3,2,1,0:T(8,128)S(1)}, u32[]{:S(2)}, u32[]{:S(2)}) collective-permute-start(f32[1,1,1,8,8,128]{5,4,3,2,1,0:T(8,128)S(1)} %get-tuple-element.60), channel_id=1, source_target_pairs={{4,0},{8,4},{12,8},{16,12},{20,16},{24,20},{28,24},{5,1},{9,5},{13... | collective-permute-start | bytes 98312 | tf_op jit(solution)/shard_map/ppermute | solution.py:19
  116.7 9.1 %collective-permute-start.18 = (f32[1,1,1,8,8,128]{5,3,4,2,1,0:T(8,128)S(1)}, f32[1,1,1,8,8,128]{5,3,4,2,1,0:T(8,128)S(1)}, u32[]{:S(2)}, u32[]{:S(2)}) collective-permute-start(f32[1,1,1,8,8,128]{5,3,4,2,1,0:T(8,128)S(1)} %get-tuple-element.86), channel_id=1, source_target_pairs={{0,1},{1,2},{2,3},{4,5},{5,6},{6,7},{8,9},{9,10},{10,11},{12,13},{... | collective-permute-start | bytes 98312 | tf_op jit(solution)/shard_map/ppermute | solution.py:16
  118.7 7.1 %collective-permute-start.19 = (f32[1,1,1,8,8,128]{5,3,4,2,1,0:T(8,128)S(1)}, f32[1,1,1,8,8,128]{5,3,4,2,1,0:T(8,128)S(1)}, u32[]{:S(2)}, u32[]{:S(2)}) collective-permute-start(f32[1,1,1,8,8,128]{5,3,4,2,1,0:T(8,128)S(1)} %get-tuple-element.87), channel_id=1, source_target_pairs={{1,0},{2,1},{3,2},{5,4},{6,5},{7,6},{9,8},{10,9},{11,10},{13,12},{... | collective-permute-start | bytes 98312 | tf_op jit(solution)/shard_map/ppermute | solution.py:19
  122.4 10.8 %all-to-all-start.1 = ((f32[8,2,2048]{2,1,0:T(2,128)}), f32[8,2,2048]{2,1,0:T(2,128)S(1)}, u32[]{:S(2)}, u32[]{:S(2)}) async-start(f32[8,2,2048]{2,1,0:T(2,128)} %broadcast_in_dim.209), calls=%async_computation.1 | async-start | bytes 262144 | tf_op jit(solution)/shard_map/all_to_all | solution.py:194

commit v21 on v20

--- a/solution.py
+++ b/solution.py
@@ -206,16 +206,17 @@
     diagonal = local_diagonal(metric, weights, stiff)
     last = source.shape[2] - 1
     rims = [jnp.stack([source[:, :, edge], diagonal[:, :, edge]]) for edge in (0, last)]
-    both, _ = assemble(jnp.stack([source, diagonal]), x_faces=rims)
+    shell_inputs = (fac_area[0], fac_strip[0, :, 0], fac_shell[0])
+    both, shell_inputs = assemble(jnp.stack([source, diagonal]), shell_inputs, x_faces=rims)
     rhs = both[0]
     pinv = 1.0 / both[1]
     pressure = jnp.zeros_like(source)
     resid = rhs
     update = pinv * resid / theta
     picks = fac_point[0]
-    areas = fac_area[0]
+    areas, strip_of, shell_of = shell_inputs
     strips = lax.axis_size("ey")
-    global_ids = fac_strip[0, :, 0] * SHELL_STRIP + fac_shell[0]
+    global_ids = strip_of * SHELL_STRIP + shell_of
     denom = segment_sum(areas, global_ids, strips * SHELL_STRIP, 256)
     for step in range(SWEEPS):
         pressure = pressure + update

time: 135 us -> 131 us (0.970)
  waiting for transfers between devices: 43.6 us -> 40.6 us
    ppermute x10, waiting for transfers between devices: 26.2 us -> 23.6 us  [padded_2(): lax.ppermute(lax.slice_in_dim(block, 0, width, axis=dim), axis, backward)]
  transfers between devices with their start and end apart: 22 -> 22, of which waited for: 18 -> 17; matrix products, arithmetic and copies ran while one was open for 9% -> 9% of each run, Pallas kernels for 0% -> 0%
where the time goes in v21:
time: 131 us; the launch traced here: 130 us
  starting transfers between devices  56.9 us (43%)
  waiting for transfers between devices  40.6 us (31%)
  other arithmetic  12 us (9%)
  matrix products  12 us (9%)
  local copies, waits for them, and re-layouts  7.15 us (5%)
  between operations  1.68 us (1%)
    ppermute x10, starting transfers between devices, padded_2(): lax.ppermute(lax.slice_in_dim(block, block.shape[dim] - width, None, axis...  28.7 us
    ppermute x10, waiting for transfers between devices, padded_2(): lax.ppermute(lax.slice_in_dim(block, 0, width, axis=dim), axis, backward)  23.6 us
    ppermute x10, starting transfers between devices, padded_2(): lax.ppermute(lax.slice_in_dim(block, 0, width, axis=dim), axis, backward)  20.3 us
    ppermute x10, waiting for transfers between devices, padded_2(): lax.ppermute(lax.slice_in_dim(block, block.shape[dim] - width, None, axis...  6.59 us
    all_to_all x1, waiting for transfers between devices, strip_gather(): whole = lax.all_to_all(spread_out, 'ex', 0, 0, tiled=True)  6.31 us
    all_to_all x1, starting transfers between devices, strip_reduce(): return lax.all_to_all(chunks, ('ex', 'ey'), 0, 0, tiled=True).sum(0)  4.39 us
    all_to_all x1, waiting for transfers between devices, strip_reduce(): return lax.all_to_all(chunks, ('ex', 'ey'), 0, 0, tiled=True).sum(0)  4.09 us
    all_to_all x1, starting transfers between devices, strip_gather(): whole = lax.all_to_all(spread_out, 'ex', 0, 0, tiled=True)  3.46 us
  transfers between devices with their start and end apart: 22, of which 17 were waited for; matrix products, arithmetic and copies ran while one was open for 9% of the time, Pallas kernels for 0%

profile of v21, /device:TPU:2, one launch (start us, length us, event | category | flops | bytes accessed | tf_op | source)
XLA Modules:
  0.0 130.3 jit_solution(12877475591851440869)
XLA Ops:
  2.9 0.8 multiply_add_fusion
  4.5 3.4 %collective-permute-start = (f32[2,1,1,8,8,128]{5,4,3,2,1,0:T(8,128)S(1)}, f32[2,1,1,8,8,128]{5,4,3,2,1,0:T(8,128)S(1)}, u32[]{:S(2)}, u32[]{:S(2)}) collective-permute-start(f32[2,1,1,8,8,128]{5,4,3,2,1,0:T(8,128)S(1)} %pad_maximum_fusion.10), channel_id=1, source_target_pairs={{0,4},{4,8},{8,12},{12,16},{16,20},{20,24},{24,28},{1,5},{5,9},{9,... | collective-permute-start | bytes 196616 | tf_op jit(solution)/shard_map/ppermute | solution.py:16
  7.9 1.3 collective-permute-start.1
  10.1 1.1 copy.281
  11.2 2.9 %collective-permute-done.1 = f32[2,1,1,8,8,128]{5,4,3,2,1,0:T(8,128)S(1)} collective-permute-done((f32[2,1,1,8,8,128]{5,4,3,2,1,0:T(8,128)S(1)}, f32[2,1,1,8,8,128]{5,4,3,2,1,0:T(8,128)S(1)}, u32[]{:S(2)}, u32[]{:S(2)}) %collective-permute-start.1) | collective-permute-done | bytes 65568 | tf_op jit(solution)/shard_map/ppermute | solution.py:19
  14.5 1.9 %collective-permute-start.2 = (f32[2,1,1,8,8,128]{5,3,0,4,2,1:T(8,128)S(1)}, f32[2,1,1,8,8,128]{5,3,0,4,2,1:T(8,128)S(1)}, u32[]{:S(2)}, u32[]{:S(2)}) collective-permute-start(f32[2,1,1,8,8,128]{5,3,0,4,2,1:T(8,128)S(1)} %get-tuple-element.56), channel_id=1, source_target_pairs={{0,1},{1,2},{2,3},{4,5},{5,6},{6,7},{8,9},{9,10},{10,11},{12,13},{... | collective-permute-start | bytes 196616 | tf_op jit(solution)/shard_map/ppermute | solution.py:16
  16.4 3.6 %collective-permute-start.3 = (f32[2,1,1,8,8,128]{5,3,0,4,2,1:T(8,128)S(1)}, f32[2,1,1,8,8,128]{5,3,0,4,2,1:T(8,128)S(1)}, u32[]{:S(2)}, u32[]{:S(2)}) collective-permute-start(f32[2,1,1,8,8,128]{5,3,0,4,2,1:T(8,128)S(1)} %get-tuple-element.57), channel_id=1, source_target_pairs={{1,0},{2,1},{3,2},{5,4},{6,5},{7,6},{9,8},{10,9},{11,10},{13,12},{... | collective-permute-start | bytes 196616 | tf_op jit(solution)/shard_map/ppermute | solution.py:19
  20.4 1.5 %collective-permute-done.3 = f32[2,1,1,8,8,128]{5,3,0,4,2,1:T(8,128)S(1)} collective-permute-done((f32[2,1,1,8,8,128]{5,3,0,4,2,1:T(8,128)S(1)}, f32[2,1,1,8,8,128]{5,3,0,4,2,1:T(8,128)S(1)}, u32[]{:S(2)}, u32[]{:S(2)}) %collective-permute-start.3) | collective-permute-done | bytes 65568 | tf_op jit(solution)/shard_map/ppermute | solution.py:19
  23.7 0.9 fusion.30
  24.7 4.3 %collective-permute-start.4 = (f32[1,1,1,8,8,128]{5,4,3,2,1,0:T(8,128)S(1)}, f32[1,1,1,8,8,128]{5,4,3,2,1,0:T(8,128)S(1)}, u32[]{:S(2)}, u32[]{:S(2)}) collective-permute-start(f32[1,1,1,8,8,128]{5,4,3,2,1,0:T(8,128)S(1)} %bitcast.467), channel_id=1, source_target_pairs={{0,4},{4,8},{8,12},{12,16},{16,20},{20,24},{24,28},{1,5},{5,9},{9,... | collective-permute-start | bytes 98312 | tf_op jit(solution)/shard_map/ppermute | solution.py:16
  29.0 1.3 collective-permute-start.5
  30.3 1.2 fusion.20
  31.6 3.2 %collective-permute-done.5 = f32[1,1,1,8,8,128]{5,4,3,2,1,0:T(8,128)S(1)} collective-permute-done((f32[1,1,1,8,8,128]{5,4,3,2,1,0:T(8,128)S(1)}, f32[1,1,1,8,8,128]{5,4,3,2,1,0:T(8,128)S(1)}, u32[]{:S(2)}, u32[]{:S(2)}) %collective-permute-start.5) | collective-permute-done | bytes 32800 | tf_op jit(solution)/shard_map/ppermute | solution.py:19
  34.8 1.9 %collective-permute-start.6 = (f32[1,1,1,8,8,128]{5,3,4,2,1,0:T(8,128)S(1)}, f32[1,1,1,8,8,128]{5,3,4,2,1,0:T(8,128)S(1)}, u32[]{:S(2)}, u32[]{:S(2)}) collective-permute-start(f32[1,1,1,8,8,128]{5,3,4,2,1,0:T(8,128)S(1)} %maximum_bitcast_fusion.15), channel_id=1, source_target_pairs={{0,1},{1,2},{2,3},{4,5},{5,6},{6,7},{8,9},{9,10},{10,11},{12,13},{... | collective-permute-start | bytes 98312 | tf_op jit(solution)/shard_map/ppermute | solution.py:16
  36.8 1.9 %fusion = f32[768,256]{1,0:T(8,128)S(1)} fusion(bf16[256,4096]{1,0:T(8,128)(2,1)S(1)} %get-tuple-element.102, bf16[256,4096]{1,0:T(8,128)(2,1)S(1)} %get-tuple-element.103, bf16[256,4096]{1,0:T(8,128)(2,1)S(1)} %get-tuple-element.101, s32[4096]{0:T(1024)S(1)} %get-tuple-element.97), kind=kOutput, calls=%fused_computation | convolution fusion | flops 1630535680 | bytes 7094272 | tf_op jit(solution)/shard_map/dot_general | solution.py:170
  38.7 1.4 %collective-permute-done.6 = f32[1,1,1,8,8,128]{5,3,4,2,1,0:T(8,128)S(1)} collective-permute-done((f32[1,1,1,8,8,128]{5,3,4,2,1,0:T(8,128)S(1)}, f32[1,1,1,8,8,128]{5,3,4,2,1,0:T(8,128)S(1)}, u32[]{:S(2)}, u32[]{:S(2)}) %collective-permute-start.6) | collective-permute-done | bytes 32800 | tf_op jit(solution)/shard_map/ppermute | solution.py:16
  40.1 2.3 %collective-permute-start.7 = (f32[1,1,1,8,8,128]{5,3,4,2,1,0:T(8,128)S(1)}, f32[1,1,1,8,8,128]{5,3,4,2,1,0:T(8,128)S(1)}, u32[]{:S(2)}, u32[]{:S(2)}) collective-permute-start(f32[1,1,1,8,8,128]{5,3,4,2,1,0:T(8,128)S(1)} %get-tuple-element.49), channel_id=1, source_target_pairs={{1,0},{2,1},{3,2},{5,4},{6,5},{7,6},{9,8},{10,9},{11,10},{13,12},{... | collective-permute-start | bytes 98312 | tf_op jit(solution)/shard_map/ppermute | solution.py:19
  42.6 1.4 %collective-permute-done.7 = f32[1,1,1,8,8,128]{5,3,4,2,1,0:T(8,128)S(1)} collective-permute-done((f32[1,1,1,8,8,128]{5,3,4,2,1,0:T(8,128)S(1)}, f32[1,1,1,8,8,128]{5,3,4,2,1,0:T(8,128)S(1)}, u32[]{:S(2)}, u32[]{:S(2)}) %collective-permute-start.7) | collective-permute-done | bytes 32800 | tf_op jit(solution)/shard_map/ppermute | solution.py:19
  45.9 3.4 %collective-permute-start.8 = (f32[1,1,1,8,8,128]{5,4,3,2,1,0:T(8,128)S(1)}, f32[1,1,1,8,8,128]{5,4,3,2,1,0:T(8,128)S(1)}, u32[]{:S(2)}, u32[]{:S(2)}) collective-permute-start(f32[1,1,1,8,8,128]{5,4,3,2,1,0:T(8,128)S(1)} %get-tuple-element.79), channel_id=1, source_target_pairs={{0,4},{4,8},{8,12},{12,16},{16,20},{20,24},{24,28},{1,5},{5,9},{9,... | collective-permute-start | bytes 98312 | tf_op jit(solution)/shard_map/ppermute | solution.py:16
  49.3 1.3 collective-permute-start.9
  50.9 4.2 %collective-permute-done.9 = f32[1,1,1,8,8,128]{5,4,3,2,1,0:T(8,128)S(1)} collective-permute-done((f32[1,1,1,8,8,128]{5,4,3,2,1,0:T(8,128)S(1)}, f32[1,1,1,8,8,128]{5,4,3,2,1,0:T(8,128)S(1)}, u32[]{:S(2)}, u32[]{:S(2)}) %collective-permute-start.9) | collective-permute-done | bytes 32800 | tf_op jit(solution)/shard_map/ppermute | solution.py:19
  55.1 1.9 %collective-permute-start.10 = (f32[1,1,1,8,8,128]{5,4,3,2,1,0:T(8,128)S(1)}, f32[1,1,1,8,8,128]{5,4,3,2,1,0:T(8,128)S(1)}, u32[]{:S(2)}, u32[]{:S(2)}) collective-permute-start(f32[1,1,1,8,8,128]{5,4,3,2,1,0:T(8,128)S(1)} %maximum_bitcast_fusion.13), channel_id=1, source_target_pairs={{0,1},{1,2},{2,3},{4,5},{5,6},{6,7},{8,9},{9,10},{10,11},{12,13},{... | collective-permute-start | bytes 98312 | tf_op jit(solution)/shard_map/ppermute | solution.py:16
  57.1 3.2 %collective-permute-done.10 = f32[1,1,1,8,8,128]{5,4,3,2,1,0:T(8,128)S(1)} collective-permute-done((f32[1,1,1,8,8,128]{5,4,3,2,1,0:T(8,128)S(1)}, f32[1,1,1,8,8,128]{5,4,3,2,1,0:T(8,128)S(1)}, u32[]{:S(2)}, u32[]{:S(2)}) %collective-permute-start.10) | collective-permute-done | bytes 32800 | tf_op jit(solution)/shard_map/ppermute | solution.py:16
  60.4 1.9 %collective-permute-start.11 = (f32[1,1,1,8,8,128]{5,4,3,2,1,0:T(8,128)S(1)}, f32[1,1,1,8,8,128]{5,4,3,2,1,0:T(8,128)S(1)}, u32[]{:S(2)}, u32[]{:S(2)}) collective-permute-start(f32[1,1,1,8,8,128]{5,4,3,2,1,0:T(8,128)S(1)} %get-tuple-element.47), channel_id=1, source_target_pairs={{1,0},{2,1},{3,2},{5,4},{6,5},{7,6},{9,8},{10,9},{11,10},{13,12},{... | collective-permute-start | bytes 98312 | tf_op jit(solution)/shard_map/ppermute | solution.py:19
  62.4 1.5 %collective-permute-done.11 = f32[1,1,1,8,8,128]{5,4,3,2,1,0:T(8,128)S(1)} collective-permute-done((f32[1,1,1,8,8,128]{5,4,3,2,1,0:T(8,128)S(1)}, f32[1,1,1,8,8,128]{5,4,3,2,1,0:T(8,128)S(1)}, u32[]{:S(2)}, u32[]{:S(2)}) %collective-permute-start.11) | collective-permute-done | bytes 32800 | tf_op jit(solution)/shard_map/ppermute | solution.py:19
  66.0 4.3 %collective-permute-start.12 = (f32[1,1,1,8,8,128]{5,4,3,2,1,0:T(8,128)S(1)}, f32[1,1,1,8,8,128]{5,4,3,2,1,0:T(8,128)S(1)}, u32[]{:S(2)}, u32[]{:S(2)}) collective-permute-start(f32[1,1,1,8,8,128]{5,4,3,2,1,0:T(8,128)S(1)} %get-tuple-element.73), channel_id=1, source_target_pairs={{0,4},{4,8},{8,12},{12,16},{16,20},{20,24},{24,28},{1,5},{5,9},{9,... | collective-permute-start | bytes 98312 | tf_op jit(solution)/shard_map/ppermute | solution.py:16
  70.3 1.3 collective-permute-start.13
  71.9 4.2 %collective-permute-done.13 = f32[1,1,1,8,8,128]{5,4,3,2,1,0:T(8,128)S(1)} collective-permute-done((f32[1,1,1,8,8,128]{5,4,3,2,1,0:T(8,128)S(1)}, f32[1,1,1,8,8,128]{5,4,3,2,1,0:T(8,128)S(1)}, u32[]{:S(2)}, u32[]{:S(2)}) %collective-permute-start.13) | collective-permute-done | bytes 32800 | tf_op jit(solution)/shard_map/ppermute | solution.py:19
  76.1 2.1 %collective-permute-start.14 = (f32[1,1,1,8,8,128]{5,4,3,2,1,0:T(8,128)S(1)}, f32[1,1,1,8,8,128]{5,4,3,2,1,0:T(8,128)S(1)}, u32[]{:S(2)}, u32[]{:S(2)}) collective-permute-start(f32[1,1,1,8,8,128]{5,4,3,2,1,0:T(8,128)S(1)} %maximum_bitcast_fusion.11), channel_id=1, source_target_pairs={{0,1},{1,2},{2,3},{4,5},{5,6},{6,7},{8,9},{9,10},{10,11},{12,13},{... | collective-permute-start | bytes 98312 | tf_op jit(solution)/shard_map/ppermute | solution.py:16
  78.3 1.9 %fusion.15 = f32[768,4096]{1,0:T(8,128)S(1)} fusion(s32[4096]{0:T(1024)S(1)} %bitcast.461, bf16[256,256]{1,0:T(8,128)(2,1)S(1)} %get-tuple-element.67, bf16[256,256]{1,0:T(8,128)(2,1)S(1)} %get-tuple-element.68, bf16[256,256]{1,0:T(8,128)(2,1)S(1)} %get-tuple-element.66), kind=kOutput, calls=%fused_computation.19 | convolution fusion | flops 1612840960 | bytes 12992512 | tf_op jit(solution)/shard_map/dot_general | solution.py:156
  80.1 1.2 collective-permute-done.14
  81.4 2.4 %collective-permute-start.15 = (f32[1,1,1,8,8,128]{5,4,3,2,1,0:T(8,128)S(1)}, f32[1,1,1,8,8,128]{5,4,3,2,1,0:T(8,128)S(1)}, u32[]{:S(2)}, u32[]{:S(2)}) collective-permute-start(f32[1,1,1,8,8,128]{5,4,3,2,1,0:T(8,128)S(1)} %get-tuple-element.43), channel_id=1, source_target_pairs={{1,0},{2,1},{3,2},{5,4},{6,5},{7,6},{9,8},{10,9},{11,10},{13,12},{... | collective-permute-start | bytes 98312 | tf_op jit(solution)/shard_map/ppermute | solution.py:19
  83.8 1.4 %fusion.9 = f32[4096]{0:T(1024)S(1)} fusion(f32[768,4096]{1,0:T(8,128)S(1)} %fusion.15, s32[4096]{0:T(1024)S(1)} %bitcast.459), kind=kLoop, calls=%fused_computation.11 | loop fusion | flops 5238784 | bytes 12615680 | tf_op jit(solution)/shard_map/reduce_sum | solution.py:161
  85.9 0.8 fusion.112
  86.9 1.3 %fusion.14 = f32[512,4096]{1,0:T(8,128)S(1)} fusion(s32[4096]{0:T(1024)S(1)} %bitcast.462, bf16[256,256]{1,0:T(8,128)(2,1)S(1)} %get-tuple-element.63, bf16[256,256]{1,0:T(8,128)(2,1)S(1)} %get-tuple-element.62), kind=kOutput, calls=%fused_computation.18 | convolution fusion | flops 1075314688 | bytes 8667136 | tf_op jit(solution)/shard_map/dot_general | solution.py:156
  88.2 0.9 fusion.7
  89.1 0.9 fusion.17
  90.0 1.4 %fusion.10 = f32[512,256]{1,0:T(8,128)S(1)} fusion(bf16[256,4096]{1,0:T(8,128)(2,1)S(1)} %get-tuple-element.100, bf16[256,4096]{1,0:T(8,128)(2,1)S(1)} %get-tuple-element.99, s32[4096]{0:T(1024)S(1)} %get-tuple-element.97), kind=kOutput, calls=%fused_computation.13 | convolution fusion | flops 1083179008 | bytes 4734976 | tf_op jit(solution)/shard_map/dot_general | solution.py:170
  91.6 1.2 copy.213
  92.8 4.4 %all-to-all-start = ((f32[32,2,2048]{2,1,0:T(2,128)}), f32[32,2,2048]{2,1,0:T(2,128)S(1)}, u32[]{:S(2)}, u32[]{:S(2)}) async-start(f32[32,2,2048]{2,1,0:T(2,128)} %bitcast.107), calls=%async_computation | async-start | bytes 1048576 | tf_op jit(solution)/shard_map/all_to_all | solution.py:185
  98.5 3.4 %collective-permute-start.16 = (f32[1,1,1,8,8,128]{5,4,3,2,1,0:T(8,128)S(1)}, f32[1,1,1,8,8,128]{5,4,3,2,1,0:T(8,128)S(1)}, u32[]{:S(2)}, u32[]{:S(2)}) collective-permute-start(f32[1,1,1,8,8,128]{5,4,3,2,1,0:T(8,128)S(1)} %get-tuple-element.64), channel_id=1, source_target_pairs={{0,4},{4,8},{8,12},{12,16},{16,20},{20,24},{24,28},{1,5},{5,9},{9,... | collective-permute-start | bytes 98312 | tf_op jit(solution)/shard_map/ppermute | solution.py:16
  101.9 1.3 collective-permute-start.17
  103.6 4.5 %collective-permute-done.17 = f32[1,1,1,8,8,128]{5,4,3,2,1,0:T(8,128)S(1)} collective-permute-done((f32[1,1,1,8,8,128]{5,4,3,2,1,0:T(8,128)S(1)}, f32[1,1,1,8,8,128]{5,4,3,2,1,0:T(8,128)S(1)}, u32[]{:S(2)}, u32[]{:S(2)}) %collective-permute-start.17) | collective-permute-done | bytes 32800 | tf_op jit(solution)/shard_map/ppermute | solution.py:19
  108.1 4.1 %all-to-all-done = f32[32,2,2048]{2,1,0:T(2,128)S(1)} async-done(((f32[32,2,2048]{2,1,0:T(2,128)}), f32[32,2,2048]{2,1,0:T(2,128)S(1)}, u32[]{:S(2)}, u32[]{:S(2)}) %all-to-all-start) | async-done | bytes 524320 | tf_op jit(solution)/shard_map/all_to_all | solution.py:185
  113.2 1.9 %collective-permute-start.18 = (f32[1,1,1,8,8,128]{5,3,4,2,1,0:T(8,128)S(1)}, f32[1,1,1,8,8,128]{5,3,4,2,1,0:T(8,128)S(1)}, u32[]{:S(2)}, u32[]{:S(2)}) collective-permute-start(f32[1,1,1,8,8,128]{5,3,4,2,1,0:T(8,128)S(1)} %get-tuple-element.93), channel_id=1, source_target_pairs={{0,1},{1,2},{2,3},{4,5},{5,6},{6,7},{8,9},{9,10},{10,11},{12,13},{... | collective-permute-start | bytes 98312 | tf_op jit(solution)/shard_map/ppermute | solution.py:16
  115.2 3.6 %collective-permute-start.19 = (f32[1,1,1,8,8,128]{5,3,4,2,1,0:T(8,128)S(1)}, f32[1,1,1,8,8,128]{5,3,4,2,1,0:T(8,128)S(1)}, u32[]{:S(2)}, u32[]{:S(2)}) collective-permute-start(f32[1,1,1,8,8,128]{5,3,4,2,1,0:T(8,128)S(1)} %get-tuple-element.94), channel_id=1, source_target_pairs={{1,0},{2,1},{3,2},{5,4},{6,5},{7,6},{9,8},{10,9},{11,10},{13,12},{... | collective-permute-start | bytes 98312 | tf_op jit(solution)/shard_map/ppermute | solution.py:19
  118.8 3.5 %all-to-all-start.1 = ((f32[8,2,2048]{2,1,0:T(2,128)}), f32[8,2,2048]{2,1,0:T(2,128)S(1)}, u32[]{:S(2)}, u32[]{:S(2)}) async-start(f32[8,2,2048]{2,1,0:T(2,128)} %broadcast_in_dim.200), calls=%async_computation.1 | async-start | bytes 262144 | tf_op jit(solution)/shard_map/all_to_all | solution.py:194
  123.3 6.3 %all-to-all-done.1 = f32[8,2,2048]{2,1,0:T(2,128)S(1)} async-done(((f32[8,2,2048]{2,1,0:T(2,128)}), f32[8,2,2048]{2,1,0:T(2,128)S(1)}, u32[]{:S(2)}, u32[]{:S(2)}) %all-to-all-start.1) | async-done | bytes 131104 | tf_op jit(solution)/shard_map/all_to_all | solution.py:194
  (140 shorter events, 16.4 us)
Async XLA Ops:
  0.6 19.5 %copy-start.2 = (f32[1,4096]{1,0:T(1,128)S(1)}, f32[1,4096]{1,0:T(1,128)}, u32[]{:S(2)}) copy-start(f32[1,4096]{1,0:T(1,128)} %param.41) | copy-start | bytes 49156
  0.6 19.4 %copy-start.5 = (s32[1,4096,1]{1,2,0:T(1,128)S(1)}, s32[1,4096,1]{1,2,0:T(1,128)}, u32[]{:S(2)}) copy-start(s32[1,4096,1]{1,2,0:T(1,128)} %param.39) | copy-start | bytes 49156
  0.7 19.4 %copy-start.4 = (s32[1,4096]{1,0:T(1,128)S(1)}, s32[1,4096]{1,0:T(1,128)}, u32[]{:S(2)}) copy-start(s32[1,4096]{1,0:T(1,128)} %param.40) | copy-start | bytes 49156
  4.5 6.7 %collective-permute-start = (f32[2,1,1,8,8,128]{5,4,3,2,1,0:T(8,128)S(1)}, f32[2,1,1,8,8,128]{5,4,3,2,1,0:T(8,128)S(1)}, u32[]{:S(2)}, u32[]{:S(2)}) collective-permute-start(f32[2,1,1,8,8,128]{5,4,3,2,1,0:T(8,128)S(1)} %pad_maximum_fusion.10), channel_id=1, source_target_pairs={{0,4},{4,8},{8,12},{12,16},{16,20},{20,24},{24,28},{1,5},{5,9},{9,... | collective-permute-start | bytes 196616 | tf_op jit(solution)/shard_map/ppermute | solution.py:16
  7.9 6.2 %collective-permute-start.1 = (f32[2,1,1,8,8,128]{5,4,3,2,1,0:T(8,128)S(1)}, f32[2,1,1,8,8,128]{5,4,3,2,1,0:T(8,128)S(1)}, u32[]{:S(2)}, u32[]{:S(2)}) collective-permute-start(f32[2,1,1,8,8,128]{5,4,3,2,1,0:T(8,128)S(1)} %pad_maximum_fusion.9), channel_id=1, source_target_pairs={{4,0},{8,4},{12,8},{16,12},{20,16},{24,20},{28,24},{5,1},{9,5},{13... | collective-permute-start | bytes 196616 | tf_op jit(solution)/shard_map/ppermute | solution.py:19
  14.5 8.3 %copy-start = (f32[8,8,1,1]{1,0,3,2:T(8,128)S(1)}, f32[8,8,1,1]{1,0,3,2:T(8,128)}, u32[]{:S(2)}) copy-start(f32[8,8,1,1]{1,0,3,2:T(8,128)} %constant.130) | copy-start | bytes 772
  14.5 6.0 %collective-permute-start.2 = (f32[2,1,1,8,8,128]{5,3,0,4,2,1:T(8,128)S(1)}, f32[2,1,1,8,8,128]{5,3,0,4,2,1:T(8,128)S(1)}, u32[]{:S(2)}, u32[]{:S(2)}) collective-permute-start(f32[2,1,1,8,8,128]{5,3,0,4,2,1:T(8,128)S(1)} %get-tuple-element.56), channel_id=1, source_target_pairs={{0,1},{1,2},{2,3},{4,5},{5,6},{6,7},{8,9},{9,10},{10,11},{12,13},{... | collective-permute-start | bytes 196616 | tf_op jit(solution)/shard_map/ppermute | solution.py:16
  16.4 5.5 %collective-permute-start.3 = (f32[2,1,1,8,8,128]{5,3,0,4,2,1:T(8,128)S(1)}, f32[2,1,1,8,8,128]{5,3,0,4,2,1:T(8,128)S(1)}, u32[]{:S(2)}, u32[]{:S(2)}) collective-permute-start(f32[2,1,1,8,8,128]{5,3,0,4,2,1:T(8,128)S(1)} %get-tuple-element.57), channel_id=1, source_target_pairs={{1,0},{2,1},{3,2},{5,4},{6,5},{7,6},{9,8},{10,9},{11,10},{13,12},{... | collective-permute-start | bytes 196616 | tf_op jit(solution)/shard_map/ppermute | solution.py:19
  20.2 3.4 %copy-start.3 = (f32[8]{0:T(128)S(1)}, f32[8]{0:T(128)}, u32[]{:S(2)}) copy-start(f32[8]{0:T(128)} %constant.125) | copy-start | bytes 100
  24.7 6.9 %collective-permute-start.4 = (f32[1,1,1,8,8,128]{5,4,3,2,1,0:T(8,128)S(1)}, f32[1,1,1,8,8,128]{5,4,3,2,1,0:T(8,128)S(1)}, u32[]{:S(2)}, u32[]{:S(2)}) collective-permute-start(f32[1,1,1,8,8,128]{5,4,3,2,1,0:T(8,128)S(1)} %bitcast.467), channel_id=1, source_target_pairs={{0,4},{4,8},{8,12},{12,16},{16,20},{20,24},{24,28},{1,5},{5,9},{9,... | collective-permute-start | bytes 98312 | tf_op jit(solution)/shard_map/ppermute | solution.py:16
  29.0 5.8 %collective-permute-start.5 = (f32[1,1,1,8,8,128]{5,4,3,2,1,0:T(8,128)S(1)}, f32[1,1,1,8,8,128]{5,4,3,2,1,0:T(8,128)S(1)}, u32[]{:S(2)}, u32[]{:S(2)}) collective-permute-start(f32[1,1,1,8,8,128]{5,4,3,2,1,0:T(8,128)S(1)} %bitcast.469), channel_id=1, source_target_pairs={{4,0},{8,4},{12,8},{16,12},{20,16},{24,20},{28,24},{5,1},{9,5},{13... | collective-permute-start | bytes 98312 | tf_op jit(solution)/shard_map/ppermute | solution.py:19
  34.8 5.2 %collective-permute-start.6 = (f32[1,1,1,8,8,128]{5,3,4,2,1,0:T(8,128)S(1)}, f32[1,1,1,8,8,128]{5,3,4,2,1,0:T(8,128)S(1)}, u32[]{:S(2)}, u32[]{:S(2)}) collective-permute-start(f32[1,1,1,8,8,128]{5,3,4,2,1,0:T(8,128)S(1)} %maximum_bitcast_fusion.15), channel_id=1, source_target_pairs={{0,1},{1,2},{2,3},{4,5},{5,6},{6,7},{8,9},{9,10},{10,11},{12,13},{... | collective-permute-start | bytes 98312 | tf_op jit(solution)/shard_map/ppermute | solution.py:16
  40.1 17.0 %copy-start.1 = (s32[1,4096]{1,0:T(1,128)S(1)}, s32[1,4096]{1,0:T(1,128)}, u32[]{:S(2)}) copy-start(s32[1,4096]{1,0:T(1,128)} %param.38) | copy-start | bytes 49156
  40.1 3.9 %collective-permute-start.7 = (f32[1,1,1,8,8,128]{5,3,4,2,1,0:T(8,128)S(1)}, f32[1,1,1,8,8,128]{5,3,4,2,1,0:T(8,128)S(1)}, u32[]{:S(2)}, u32[]{:S(2)}) collective-permute-start(f32[1,1,1,8,8,128]{5,3,4,2,1,0:T(8,128)S(1)} %get-tuple-element.49), channel_id=1, source_target_pairs={{1,0},{2,1},{3,2},{5,4},{6,5},{7,6},{9,8},{10,9},{11,10},{13,12},{... | collective-permute-start | bytes 98312 | tf_op jit(solution)/shard_map/ppermute | solution.py:19
  45.9 5.0 %collective-permute-start.8 = (f32[1,1,1,8,8,128]{5,4,3,2,1,0:T(8,128)S(1)}, f32[1,1,1,8,8,128]{5,4,3,2,1,0:T(8,128)S(1)}, u32[]{:S(2)}, u32[]{:S(2)}) collective-permute-start(f32[1,1,1,8,8,128]{5,4,3,2,1,0:T(8,128)S(1)} %get-tuple-element.79), channel_id=1, source_target_pairs={{0,4},{4,8},{8,12},{12,16},{16,20},{20,24},{24,28},{1,5},{5,9},{9,... | collective-permute-start | bytes 98312 | tf_op jit(solution)/shard_map/ppermute | solution.py:16
  49.3 5.8 %collective-permute-start.9 = (f32[1,1,1,8,8,128]{5,4,3,2,1,0:T(8,128)S(1)}, f32[1,1,1,8,8,128]{5,4,3,2,1,0:T(8,128)S(1)}, u32[]{:S(2)}, u32[]{:S(2)}) collective-permute-start(f32[1,1,1,8,8,128]{5,4,3,2,1,0:T(8,128)S(1)} %get-tuple-element.80), channel_id=1, source_target_pairs={{4,0},{8,4},{12,8},{16,12},{20,16},{24,20},{28,24},{5,1},{9,5},{13... | collective-permute-start | bytes 98312 | tf_op jit(solution)/shard_map/ppermute | solution.py:19
  55.1 5.2 %collective-permute-start.10 = (f32[1,1,1,8,8,128]{5,4,3,2,1,0:T(8,128)S(1)}, f32[1,1,1,8,8,128]{5,4,3,2,1,0:T(8,128)S(1)}, u32[]{:S(2)}, u32[]{:S(2)}) collective-permute-start(f32[1,1,1,8,8,128]{5,4,3,2,1,0:T(8,128)S(1)} %maximum_bitcast_fusion.13), channel_id=1, source_target_pairs={{0,1},{1,2},{2,3},{4,5},{5,6},{6,7},{8,9},{9,10},{10,11},{12,13},{... | collective-permute-start | bytes 98312 | tf_op jit(solution)/shard_map/ppermute | solution.py:16
  60.4 3.5 %collective-permute-start.11 = (f32[1,1,1,8,8,128]{5,4,3,2,1,0:T(8,128)S(1)}, f32[1,1,1,8,8,128]{5,4,3,2,1,0:T(8,128)S(1)}, u32[]{:S(2)}, u32[]{:S(2)}) collective-permute-start(f32[1,1,1,8,8,128]{5,4,3,2,1,0:T(8,128)S(1)} %get-tuple-element.47), channel_id=1, source_target_pairs={{1,0},{2,1},{3,2},{5,4},{6,5},{7,6},{9,8},{10,9},{11,10},{13,12},{... | collective-permute-start | bytes 98312 | tf_op jit(solution)/shard_map/ppermute | solution.py:19
  66.0 5.9 %collective-permute-start.12 = (f32[1,1,1,8,8,128]{5,4,3,2,1,0:T(8,128)S(1)}, f32[1,1,1,8,8,128]{5,4,3,2,1,0:T(8,128)S(1)}, u32[]{:S(2)}, u32[]{:S(2)}) collective-permute-start(f32[1,1,1,8,8,128]{5,4,3,2,1,0:T(8,128)S(1)} %get-tuple-element.73), channel_id=1, source_target_pairs={{0,4},{4,8},{8,12},{12,16},{16,20},{20,24},{24,28},{1,5},{5,9},{9,... | collective-permute-start | bytes 98312 | tf_op jit(solution)/shard_map/ppermute | solution.py:16
  70.3 5.8 %collective-permute-start.13 = (f32[1,1,1,8,8,128]{5,4,3,2,1,0:T(8,128)S(1)}, f32[1,1,1,8,8,128]{5,4,3,2,1,0:T(8,128)S(1)}, u32[]{:S(2)}, u32[]{:S(2)}) collective-permute-start(f32[1,1,1,8,8,128]{5,4,3,2,1,0:T(8,128)S(1)} %get-tuple-element.74), channel_id=1, source_target_pairs={{4,0},{8,4},{12,8},{16,12},{20,16},{24,20},{28,24},{5,1},{9,5},{13... | collective-permute-start | bytes 98312 | tf_op jit(solution)/shard_map/ppermute | solution.py:19
  76.1 5.2 %collective-permute-start.14 = (f32[1,1,1,8,8,128]{5,4,3,2,1,0:T(8,128)S(1)}, f32[1,1,1,8,8,128]{5,4,3,2,1,0:T(8,128)S(1)}, u32[]{:S(2)}, u32[]{:S(2)}) collective-permute-start(f32[1,1,1,8,8,128]{5,4,3,2,1,0:T(8,128)S(1)} %maximum_bitcast_fusion.11), channel_id=1, source_target_pairs={{0,1},{1,2},{2,3},{4,5},{5,6},{6,7},{8,9},{9,10},{10,11},{12,13},{... | collective-permute-start | bytes 98312 | tf_op jit(solution)/shard_map/ppermute | solution.py:16
  81.4 4.0 %collective-permute-start.15 = (f32[1,1,1,8,8,128]{5,4,3,2,1,0:T(8,128)S(1)}, f32[1,1,1,8,8,128]{5,4,3,2,1,0:T(8,128)S(1)}, u32[]{:S(2)}, u32[]{:S(2)}) collective-permute-start(f32[1,1,1,8,8,128]{5,4,3,2,1,0:T(8,128)S(1)} %get-tuple-element.43), channel_id=1, source_target_pairs={{1,0},{2,1},{3,2},{5,4},{6,5},{7,6},{9,8},{10,9},{11,10},{13,12},{... | collective-permute-start | bytes 98312 | tf_op jit(solution)/shard_map/ppermute | solution.py:19
  92.8 19.4 %all-to-all-start = ((f32[32,2,2048]{2,1,0:T(2,128)}), f32[32,2,2048]{2,1,0:T(2,128)S(1)}, u32[]{:S(2)}, u32[]{:S(2)}) async-start(f32[32,2,2048]{2,1,0:T(2,128)} %bitcast.107), calls=%async_computation | async-start | bytes 1048576 | tf_op jit(solution)/shard_map/all_to_all | solution.py:185
  98.5 5.1 %collective-permute-start.16 = (f32[1,1,1,8,8,128]{5,4,3,2,1,0:T(8,128)S(1)}, f32[1,1,1,8,8,128]{5,4,3,2,1,0:T(8,128)S(1)}, u32[]{:S(2)}, u32[]{:S(2)}) collective-permute-start(f32[1,1,1,8,8,128]{5,4,3,2,1,0:T(8,128)S(1)} %get-tuple-element.64), channel_id=1, source_target_pairs={{0,4},{4,8},{8,12},{12,16},{16,20},{20,24},{24,28},{1,5},{5,9},{9,... | collective-permute-start | bytes 98312 | tf_op jit(solution)/shard_map/ppermute | solution.py:16
  101.9 6.2 %collective-permute-start.17 = (f32[1,1,1,8,8,128]{5,4,3,2,1,0:T(8,128)S(1)}, f32[1,1,1,8,8,128]{5,4,3,2,1,0:T(8,128)S(1)}, u32[]{:S(2)}, u32[]{:S(2)}) collective-permute-start(f32[1,1,1,8,8,128]{5,4,3,2,1,0:T(8,128)S(1)} %get-tuple-element.65), channel_id=1, source_target_pairs={{4,0},{8,4},{12,8},{16,12},{20,16},{24,20},{28,24},{5,1},{9,5},{13... | collective-permute-start | bytes 98312 | tf_op jit(solution)/shard_map/ppermute | solution.py:19
  113.2 9.1 %collective-permute-start.18 = (f32[1,1,1,8,8,128]{5,3,4,2,1,0:T(8,128)S(1)}, f32[1,1,1,8,8,128]{5,3,4,2,1,0:T(8,128)S(1)}, u32[]{:S(2)}, u32[]{:S(2)}) collective-permute-start(f32[1,1,1,8,8,128]{5,3,4,2,1,0:T(8,128)S(1)} %get-tuple-element.93), channel_id=1, source_target_pairs={{0,1},{1,2},{2,3},{4,5},{5,6},{6,7},{8,9},{9,10},{10,11},{12,13},{... | collective-permute-start | bytes 98312 | tf_op jit(solution)/shard_map/ppermute | solution.py:16
  115.2 7.1 %collective-permute-start.19 = (f32[1,1,1,8,8,128]{5,3,4,2,1,0:T(8,128)S(1)}, f32[1,1,1,8,8,128]{5,3,4,2,1,0:T(8,128)S(1)}, u32[]{:S(2)}, u32[]{:S(2)}) collective-permute-start(f32[1,1,1,8,8,128]{5,3,4,2,1,0:T(8,128)S(1)} %get-tuple-element.94), channel_id=1, source_target_pairs={{1,0},{2,1},{3,2},{5,4},{6,5},{7,6},{9,8},{10,9},{11,10},{13,12},{... | collective-permute-start | bytes 98312 | tf_op jit(solution)/shard_map/ppermute | solution.py:19
  118.8 10.8 %all-to-all-start.1 = ((f32[8,2,2048]{2,1,0:T(2,128)}), f32[8,2,2048]{2,1,0:T(2,128)S(1)}, u32[]{:S(2)}, u32[]{:S(2)}) async-start(f32[8,2,2048]{2,1,0:T(2,128)} %broadcast_in_dim.200), calls=%async_computation.1 | async-start | bytes 262144 | tf_op jit(solution)/shard_map/all_to_all | solution.py:194

commit v22 on v21

--- a/solution.py
+++ b/solution.py
@@ -208,16 +208,17 @@
     rims = [jnp.stack([source[:, :, edge], diagonal[:, :, edge]]) for edge in (0, last)]
     shell_inputs = (fac_area[0], fac_strip[0, :, 0], fac_shell[0])
     both, shell_inputs = assemble(jnp.stack([source, diagonal]), shell_inputs, x_faces=rims)
+    picks = fac_point[0]
+    areas, strip_of, shell_of = shell_inputs
+    strips = lax.axis_size("ey")
+    global_ids = strip_of * SHELL_STRIP + shell_of
+    denom = segment_sum(areas, global_ids, strips * SHELL_STRIP, 256)
+    both, denom = lax.optimization_barrier((both, denom))
     rhs = both[0]
     pinv = 1.0 / both[1]
     pressure = jnp.zeros_like(source)
     resid = rhs
     update = pinv * resid / theta
-    picks = fac_point[0]
-    areas, strip_of, shell_of = shell_inputs
-    strips = lax.axis_size("ey")
-    global_ids = strip_of * SHELL_STRIP + shell_of
-    denom = segment_sum(areas, global_ids, strips * SHELL_STRIP, 256)
     for step in range(SWEEPS):
         pressure = pressure + update
         if step + 2 == SWEEPS:
@@ -233,8 +234,6 @@
         assembled = assembled[0]
         if step + 2 == SWEEPS:
             assembled, early = lax.optimization_barrier((assembled, early))
-        if step == 0:
-            assembled, denom = lax.optimization_barrier((assembled, denom))
         resid = resid - assembled
         if step + 1 < SWEEPS:
             rho_new = 1.0 / (2.0 * sigma - rho_now)

time: 131 us -> 135 us (1.031)
  other arithmetic: 12 us -> 14.4 us
  waiting for transfers between devices: 40.6 us -> 42.5 us
    ppermute x10, waiting for transfers between devices: 6.59 us -> 8.91 us  [padded_2(): lax.ppermute(lax.slice_in_dim(block, block.shape[dim] - width, None, axis...]
where the time goes in v22:
time: 135 us; the launch traced here: 134 us
  starting transfers between devices  56.5 us (42%)
  waiting for transfers between devices  42.5 us (31%)
  other arithmetic  14.4 us (11%)
  matrix products  11.9 us (9%)
  local copies, waits for them, and re-layouts  6.95 us (5%)
  between operations  1.6 us (1%)
    ppermute x10, starting transfers between devices, padded_2(): lax.ppermute(lax.slice_in_dim(block, block.shape[dim] - width, None, axis...  28.7 us
    ppermute x10, waiting for transfers between devices, padded_2(): lax.ppermute(lax.slice_in_dim(block, 0, width, axis=dim), axis, backward)  23.3 us
    ppermute x10, starting transfers between devices, padded_2(): lax.ppermute(lax.slice_in_dim(block, 0, width, axis=dim), axis, backward)  20 us
    ppermute x10, waiting for transfers between devices, padded_2(): lax.ppermute(lax.slice_in_dim(block, block.shape[dim] - width, None, axis...  8.91 us
    all_to_all x1, waiting for transfers between devices, strip_gather(): whole = lax.all_to_all(spread_out, 'ex', 0, 0, tiled=True)  6.2 us
    all_to_all x1, starting transfers between devices, strip_reduce(): return lax.all_to_all(chunks, ('ex', 'ey'), 0, 0, tiled=True).sum(0)  4.39 us
    all_to_all x1, waiting for transfers between devices, strip_reduce(): return lax.all_to_all(chunks, ('ex', 'ey'), 0, 0, tiled=True).sum(0)  4.09 us
    all_to_all x1, starting transfers between devices, strip_gather(): whole = lax.all_to_all(spread_out, 'ex', 0, 0, tiled=True)  3.46 us
  transfers between devices with their start and end apart: 22, of which 17 were waited for; matrix products, arithmetic and copies ran while one was open for 9% of the time, Pallas kernels for 0%

profile of v22, /device:TPU:2, one launch (start us, length us, event | category | flops | bytes accessed | tf_op | source)
XLA Modules:
  0.0 133.8 jit_solution(10545817952769512537)
XLA Ops:
  4.4 1.2 fusion.91
  6.4 3.4 %collective-permute-start = (f32[2,1,1,8,8,128]{5,0,4,3,2,1:T(2,128)S(1)}, f32[2,1,1,8,8,128]{5,0,4,3,2,1:T(2,128)S(1)}, u32[]{:S(2)}, u32[]{:S(2)}) collective-permute-start(f32[2,1,1,8,8,128]{5,0,4,3,2,1:T(2,128)S(1)} %pad_maximum_fusion.6), channel_id=1, source_target_pairs={{0,4},{4,8},{8,12},{12,16},{16,20},{20,24},{24,28},{1,5},{5,9},{9,... | collective-permute-start | bytes 196616 | tf_op jit(solution)/shard_map/ppermute | solution.py:16
  9.9 1.3 collective-permute-start.1
  11.2 0.8 fusion.90
  12.0 1.1 copy.307
  13.2 2.9 %collective-permute-done.1 = f32[2,1,1,8,8,128]{5,0,4,3,2,1:T(2,128)S(1)} collective-permute-done((f32[2,1,1,8,8,128]{5,0,4,3,2,1:T(2,128)S(1)}, f32[2,1,1,8,8,128]{5,0,4,3,2,1:T(2,128)S(1)}, u32[]{:S(2)}, u32[]{:S(2)}) %collective-permute-start.1) | collective-permute-done | bytes 65568 | tf_op jit(solution)/shard_map/ppermute | solution.py:19
  17.3 1.9 %collective-permute-start.2 = (f32[2,1,1,8,8,128]{5,3,0,4,2,1:T(8,128)S(1)}, f32[2,1,1,8,8,128]{5,3,0,4,2,1:T(8,128)S(1)}, u32[]{:S(2)}, u32[]{:S(2)}) collective-permute-start(f32[2,1,1,8,8,128]{5,3,0,4,2,1:T(8,128)S(1)} %get-tuple-element.52), channel_id=1, source_target_pairs={{0,1},{1,2},{2,3},{4,5},{5,6},{6,7},{8,9},{9,10},{10,11},{12,13},{... | collective-permute-start | bytes 196616 | tf_op jit(solution)/shard_map/ppermute | solution.py:16
  19.2 3.6 %collective-permute-start.3 = (f32[2,1,1,8,8,128]{5,3,0,4,2,1:T(8,128)S(1)}, f32[2,1,1,8,8,128]{5,3,0,4,2,1:T(8,128)S(1)}, u32[]{:S(2)}, u32[]{:S(2)}) collective-permute-start(f32[2,1,1,8,8,128]{5,3,0,4,2,1:T(8,128)S(1)} %get-tuple-element.53), channel_id=1, source_target_pairs={{1,0},{2,1},{3,2},{5,4},{6,5},{7,6},{9,8},{10,9},{11,10},{13,12},{... | collective-permute-start | bytes 196616 | tf_op jit(solution)/shard_map/ppermute | solution.py:19
  22.9 1.2 fusion.20
  24.1 1.9 %fusion = f32[768,256]{1,0:T(8,128)S(1)} fusion(bf16[256,4096]{1,0:T(8,128)(2,1)S(1)} %get-tuple-element.100, bf16[256,4096]{1,0:T(8,128)(2,1)S(1)} %get-tuple-element.101, bf16[256,4096]{1,0:T(8,128)(2,1)S(1)} %get-tuple-element.99, s32[4096]{0:T(1024)S(1)} %get-tuple-element.95), kind=kOutput, calls=%fused_computation | convolution fusion | flops 1630535680 | bytes 7094272 | tf_op jit(solution)/shard_map/dot_general | solution.py:170
  28.9 4.3 %collective-permute-start.4 = (f32[1,1,1,8,8,128]{5,4,3,2,1,0:T(8,128)S(1)}, f32[1,1,1,8,8,128]{5,4,3,2,1,0:T(8,128)S(1)}, u32[]{:S(2)}, u32[]{:S(2)}) collective-permute-start(f32[1,1,1,8,8,128]{5,4,3,2,1,0:T(8,128)S(1)} %get-tuple-element.83), channel_id=1, source_target_pairs={{0,4},{4,8},{8,12},{12,16},{16,20},{20,24},{24,28},{1,5},{5,9},{9,... | collective-permute-start | bytes 98312 | tf_op jit(solution)/shard_map/ppermute | solution.py:16
  33.2 1.3 collective-permute-start.5
  34.8 4.2 %collective-permute-done.5 = f32[1,1,1,8,8,128]{5,4,3,2,1,0:T(8,128)S(1)} collective-permute-done((f32[1,1,1,8,8,128]{5,4,3,2,1,0:T(8,128)S(1)}, f32[1,1,1,8,8,128]{5,4,3,2,1,0:T(8,128)S(1)}, u32[]{:S(2)}, u32[]{:S(2)}) %collective-permute-start.5) | collective-permute-done | bytes 32800 | tf_op jit(solution)/shard_map/ppermute | solution.py:19
  39.0 1.9 %collective-permute-start.6 = (f32[1,1,1,8,8,128]{5,4,3,2,1,0:T(8,128)S(1)}, f32[1,1,1,8,8,128]{5,4,3,2,1,0:T(8,128)S(1)}, u32[]{:S(2)}, u32[]{:S(2)}) collective-permute-start(f32[1,1,1,8,8,128]{5,4,3,2,1,0:T(8,128)S(1)} %maximum_bitcast_fusion.11), channel_id=1, source_target_pairs={{0,1},{1,2},{2,3},{4,5},{5,6},{6,7},{8,9},{9,10},{10,11},{12,13},{... | collective-permute-start | bytes 98312 | tf_op jit(solution)/shard_map/ppermute | solution.py:16
  41.0 3.3 %collective-permute-done.6 = f32[1,1,1,8,8,128]{5,4,3,2,1,0:T(8,128)S(1)} collective-permute-done((f32[1,1,1,8,8,128]{5,4,3,2,1,0:T(8,128)S(1)}, f32[1,1,1,8,8,128]{5,4,3,2,1,0:T(8,128)S(1)}, u32[]{:S(2)}, u32[]{:S(2)}) %collective-permute-start.6) | collective-permute-done | bytes 32800 | tf_op jit(solution)/shard_map/ppermute | solution.py:16
  44.3 1.9 %collective-permute-start.7 = (f32[1,1,1,8,8,128]{5,4,3,2,1,0:T(8,128)S(1)}, f32[1,1,1,8,8,128]{5,4,3,2,1,0:T(8,128)S(1)}, u32[]{:S(2)}, u32[]{:S(2)}) collective-permute-start(f32[1,1,1,8,8,128]{5,4,3,2,1,0:T(8,128)S(1)} %get-tuple-element.47), channel_id=1, source_target_pairs={{1,0},{2,1},{3,2},{5,4},{6,5},{7,6},{9,8},{10,9},{11,10},{13,12},{... | collective-permute-start | bytes 98312 | tf_op jit(solution)/shard_map/ppermute | solution.py:19
  46.2 1.6 %collective-permute-done.7 = f32[1,1,1,8,8,128]{5,4,3,2,1,0:T(8,128)S(1)} collective-permute-done((f32[1,1,1,8,8,128]{5,4,3,2,1,0:T(8,128)S(1)}, f32[1,1,1,8,8,128]{5,4,3,2,1,0:T(8,128)S(1)}, u32[]{:S(2)}, u32[]{:S(2)}) %collective-permute-start.7) | collective-permute-done | bytes 32800 | tf_op jit(solution)/shard_map/ppermute | solution.py:19
  49.6 3.4 %collective-permute-start.8 = (f32[1,1,1,8,8,128]{5,4,3,2,1,0:T(8,128)S(1)}, f32[1,1,1,8,8,128]{5,4,3,2,1,0:T(8,128)S(1)}, u32[]{:S(2)}, u32[]{:S(2)}) collective-permute-start(f32[1,1,1,8,8,128]{5,4,3,2,1,0:T(8,128)S(1)} %get-tuple-element.77), channel_id=1, source_target_pairs={{0,4},{4,8},{8,12},{12,16},{16,20},{20,24},{24,28},{1,5},{5,9},{9,... | collective-permute-start | bytes 98312 | tf_op jit(solution)/shard_map/ppermute | solution.py:16
  53.0 1.3 collective-permute-start.9
  54.6 4.2 %collective-permute-done.9 = f32[1,1,1,8,8,128]{5,4,3,2,1,0:T(8,128)S(1)} collective-permute-done((f32[1,1,1,8,8,128]{5,4,3,2,1,0:T(8,128)S(1)}, f32[1,1,1,8,8,128]{5,4,3,2,1,0:T(8,128)S(1)}, u32[]{:S(2)}, u32[]{:S(2)}) %collective-permute-start.9) | collective-permute-done | bytes 32800 | tf_op jit(solution)/shard_map/ppermute | solution.py:19
  58.8 1.9 %collective-permute-start.10 = (f32[1,1,1,8,8,128]{5,4,3,2,1,0:T(8,128)S(1)}, f32[1,1,1,8,8,128]{5,4,3,2,1,0:T(8,128)S(1)}, u32[]{:S(2)}, u32[]{:S(2)}) collective-permute-start(f32[1,1,1,8,8,128]{5,4,3,2,1,0:T(8,128)S(1)} %maximum_bitcast_fusion.9), channel_id=1, source_target_pairs={{0,1},{1,2},{2,3},{4,5},{5,6},{6,7},{8,9},{9,10},{10,11},{12,13},{... | collective-permute-start | bytes 98312 | tf_op jit(solution)/shard_map/ppermute | solution.py:16
  60.8 3.2 %collective-permute-done.10 = f32[1,1,1,8,8,128]{5,4,3,2,1,0:T(8,128)S(1)} collective-permute-done((f32[1,1,1,8,8,128]{5,4,3,2,1,0:T(8,128)S(1)}, f32[1,1,1,8,8,128]{5,4,3,2,1,0:T(8,128)S(1)}, u32[]{:S(2)}, u32[]{:S(2)}) %collective-permute-start.10) | collective-permute-done | bytes 32800 | tf_op jit(solution)/shard_map/ppermute | solution.py:16
  64.1 1.9 %collective-permute-start.11 = (f32[1,1,1,8,8,128]{5,4,3,2,1,0:T(8,128)S(1)}, f32[1,1,1,8,8,128]{5,4,3,2,1,0:T(8,128)S(1)}, u32[]{:S(2)}, u32[]{:S(2)}) collective-permute-start(f32[1,1,1,8,8,128]{5,4,3,2,1,0:T(8,128)S(1)} %get-tuple-element.45), channel_id=1, source_target_pairs={{1,0},{2,1},{3,2},{5,4},{6,5},{7,6},{9,8},{10,9},{11,10},{13,12},{... | collective-permute-start | bytes 98312 | tf_op jit(solution)/shard_map/ppermute | solution.py:19
  66.1 1.5 %collective-permute-done.11 = f32[1,1,1,8,8,128]{5,4,3,2,1,0:T(8,128)S(1)} collective-permute-done((f32[1,1,1,8,8,128]{5,4,3,2,1,0:T(8,128)S(1)}, f32[1,1,1,8,8,128]{5,4,3,2,1,0:T(8,128)S(1)}, u32[]{:S(2)}, u32[]{:S(2)}) %collective-permute-start.11) | collective-permute-done | bytes 32800 | tf_op jit(solution)/shard_map/ppermute | solution.py:19
  69.7 4.3 %collective-permute-start.12 = (f32[1,1,1,8,8,128]{5,4,3,2,1,0:T(8,128)S(1)}, f32[1,1,1,8,8,128]{5,4,3,2,1,0:T(8,128)S(1)}, u32[]{:S(2)}, u32[]{:S(2)}) collective-permute-start(f32[1,1,1,8,8,128]{5,4,3,2,1,0:T(8,128)S(1)} %get-tuple-element.71), channel_id=1, source_target_pairs={{0,4},{4,8},{8,12},{12,16},{16,20},{20,24},{24,28},{1,5},{5,9},{9,... | collective-permute-start | bytes 98312 | tf_op jit(solution)/shard_map/ppermute | solution.py:16
  74.0 1.3 collective-permute-start.13
  75.6 4.2 %collective-permute-done.13 = f32[1,1,1,8,8,128]{5,4,3,2,1,0:T(8,128)S(1)} collective-permute-done((f32[1,1,1,8,8,128]{5,4,3,2,1,0:T(8,128)S(1)}, f32[1,1,1,8,8,128]{5,4,3,2,1,0:T(8,128)S(1)}, u32[]{:S(2)}, u32[]{:S(2)}) %collective-permute-start.13) | collective-permute-done | bytes 32800 | tf_op jit(solution)/shard_map/ppermute | solution.py:19
  79.8 2.1 %collective-permute-start.14 = (f32[1,1,1,8,8,128]{5,4,3,2,1,0:T(8,128)S(1)}, f32[1,1,1,8,8,128]{5,4,3,2,1,0:T(8,128)S(1)}, u32[]{:S(2)}, u32[]{:S(2)}) collective-permute-start(f32[1,1,1,8,8,128]{5,4,3,2,1,0:T(8,128)S(1)} %maximum_bitcast_fusion.7), channel_id=1, source_target_pairs={{0,1},{1,2},{2,3},{4,5},{5,6},{6,7},{8,9},{9,10},{10,11},{12,13},{... | collective-permute-start | bytes 98312 | tf_op jit(solution)/shard_map/ppermute | solution.py:16
  82.0 1.9 %fusion.15 = f32[768,4096]{1,0:T(8,128)S(1)} fusion(s32[4096]{0:T(1024)S(1)} %bitcast.485, bf16[256,256]{1,0:T(8,128)(2,1)S(1)} %get-tuple-element.65, bf16[256,256]{1,0:T(8,128)(2,1)S(1)} %get-tuple-element.66, bf16[256,256]{1,0:T(8,128)(2,1)S(1)} %get-tuple-element.64), kind=kOutput, calls=%fused_computation.19 | convolution fusion | flops 1612840960 | bytes 12992512 | tf_op jit(solution)/shard_map/dot_general | solution.py:156
  83.8 1.2 collective-permute-done.14
  85.1 2.4 %collective-permute-start.15 = (f32[1,1,1,8,8,128]{5,4,3,2,1,0:T(8,128)S(1)}, f32[1,1,1,8,8,128]{5,4,3,2,1,0:T(8,128)S(1)}, u32[]{:S(2)}, u32[]{:S(2)}) collective-permute-start(f32[1,1,1,8,8,128]{5,4,3,2,1,0:T(8,128)S(1)} %get-tuple-element.43), channel_id=1, source_target_pairs={{1,0},{2,1},{3,2},{5,4},{6,5},{7,6},{9,8},{10,9},{11,10},{13,12},{... | collective-permute-start | bytes 98312 | tf_op jit(solution)/shard_map/ppermute | solution.py:19
  87.5 1.4 %fusion.9 = f32[4096]{0:T(1024)S(1)} fusion(f32[768,4096]{1,0:T(8,128)S(1)} %fusion.15, s32[4096]{0:T(1024)S(1)} %bitcast.483), kind=kLoop, calls=%fused_computation.11 | loop fusion | flops 5238784 | bytes 12615680 | tf_op jit(solution)/shard_map/reduce_sum | solution.py:161
  89.5 0.9 fusion.73
  90.5 1.3 %fusion.14 = f32[512,4096]{1,0:T(8,128)S(1)} fusion(s32[4096]{0:T(1024)S(1)} %bitcast.486, bf16[256,256]{1,0:T(8,128)(2,1)S(1)} %get-tuple-element.61, bf16[256,256]{1,0:T(8,128)(2,1)S(1)} %get-tuple-element.60), kind=kOutput, calls=%fused_computation.18 | convolution fusion | flops 1075314688 | bytes 8667136 | tf_op jit(solution)/shard_map/dot_general | solution.py:156
  91.8 0.9 fusion.7
  92.8 0.9 fusion.17
  93.6 1.4 %fusion.10 = f32[512,256]{1,0:T(8,128)S(1)} fusion(bf16[256,4096]{1,0:T(8,128)(2,1)S(1)} %get-tuple-element.98, bf16[256,4096]{1,0:T(8,128)(2,1)S(1)} %get-tuple-element.97, s32[4096]{0:T(1024)S(1)} %get-tuple-element.95), kind=kOutput, calls=%fused_computation.13 | convolution fusion | flops 1083179008 | bytes 4734976 | tf_op jit(solution)/shard_map/dot_general | solution.py:170
  95.2 1.2 copy.257
  96.4 4.4 %all-to-all-start = ((f32[32,2,2048]{2,1,0:T(2,128)}), f32[32,2,2048]{2,1,0:T(2,128)S(1)}, u32[]{:S(2)}, u32[]{:S(2)}) async-start(f32[32,2,2048]{2,1,0:T(2,128)} %bitcast.113), calls=%async_computation | async-start | bytes 1048576 | tf_op jit(solution)/shard_map/all_to_all | solution.py:185
  102.1 3.4 %collective-permute-start.16 = (f32[1,1,1,8,8,128]{5,4,3,2,1,0:T(8,128)S(1)}, f32[1,1,1,8,8,128]{5,4,3,2,1,0:T(8,128)S(1)}, u32[]{:S(2)}, u32[]{:S(2)}) collective-permute-start(f32[1,1,1,8,8,128]{5,4,3,2,1,0:T(8,128)S(1)} %get-tuple-element.62), channel_id=1, source_target_pairs={{0,4},{4,8},{8,12},{12,16},{16,20},{20,24},{24,28},{1,5},{5,9},{9,... | collective-permute-start | bytes 98312 | tf_op jit(solution)/shard_map/ppermute | solution.py:16
  105.5 1.3 collective-permute-start.17
  107.2 4.5 %collective-permute-done.17 = f32[1,1,1,8,8,128]{5,4,3,2,1,0:T(8,128)S(1)} collective-permute-done((f32[1,1,1,8,8,128]{5,4,3,2,1,0:T(8,128)S(1)}, f32[1,1,1,8,8,128]{5,4,3,2,1,0:T(8,128)S(1)}, u32[]{:S(2)}, u32[]{:S(2)}) %collective-permute-start.17) | collective-permute-done | bytes 32800 | tf_op jit(solution)/shard_map/ppermute | solution.py:19
  111.8 4.1 %all-to-all-done = f32[32,2,2048]{2,1,0:T(2,128)S(1)} async-done(((f32[32,2,2048]{2,1,0:T(2,128)}), f32[32,2,2048]{2,1,0:T(2,128)S(1)}, u32[]{:S(2)}, u32[]{:S(2)}) %all-to-all-start) | async-done | bytes 524320 | tf_op jit(solution)/shard_map/all_to_all | solution.py:185
  116.8 1.9 %collective-permute-start.18 = (f32[1,1,1,8,8,128]{5,4,3,2,1,0:T(8,128)S(1)}, f32[1,1,1,8,8,128]{5,4,3,2,1,0:T(8,128)S(1)}, u32[]{:S(2)}, u32[]{:S(2)}) collective-permute-start(f32[1,1,1,8,8,128]{5,4,3,2,1,0:T(8,128)S(1)} %get-tuple-element.91), channel_id=1, source_target_pairs={{0,1},{1,2},{2,3},{4,5},{5,6},{6,7},{8,9},{9,10},{10,11},{12,13},{... | collective-permute-start | bytes 98312 | tf_op jit(solution)/shard_map/ppermute | solution.py:16
  118.7 3.6 %collective-permute-start.19 = (f32[1,1,1,8,8,128]{5,4,3,2,1,0:T(8,128)S(1)}, f32[1,1,1,8,8,128]{5,4,3,2,1,0:T(8,128)S(1)}, u32[]{:S(2)}, u32[]{:S(2)}) collective-permute-start(f32[1,1,1,8,8,128]{5,4,3,2,1,0:T(8,128)S(1)} %get-tuple-element.92), channel_id=1, source_target_pairs={{1,0},{2,1},{3,2},{5,4},{6,5},{7,6},{9,8},{10,9},{11,10},{13,12},{... | collective-permute-start | bytes 98312 | tf_op jit(solution)/shard_map/ppermute | solution.py:19
  122.3 3.5 %all-to-all-start.1 = ((f32[8,2,2048]{2,1,0:T(2,128)}), f32[8,2,2048]{2,1,0:T(2,128)S(1)}, u32[]{:S(2)}, u32[]{:S(2)}) async-start(f32[8,2,2048]{2,1,0:T(2,128)} %broadcast_in_dim.200), calls=%async_computation.1 | async-start | bytes 262144 | tf_op jit(solution)/shard_map/all_to_all | solution.py:194
  126.1 0.8 fusion.69
  126.9 6.2 %all-to-all-done.1 = f32[8,2,2048]{2,1,0:T(2,128)S(1)} async-done(((f32[8,2,2048]{2,1,0:T(2,128)}), f32[8,2,2048]{2,1,0:T(2,128)S(1)}, u32[]{:S(2)}, u32[]{:S(2)}) %all-to-all-start.1) | async-done | bytes 131104 | tf_op jit(solution)/shard_map/all_to_all | solution.py:194
  (134 shorter events, 17.7 us)
Async XLA Ops:
  0.6 22.2 %copy-start.4 = (s32[1,4096]{1,0:T(1,128)S(1)}, s32[1,4096]{1,0:T(1,128)}, u32[]{:S(2)}) copy-start(s32[1,4096]{1,0:T(1,128)} %param.40) | copy-start | bytes 49156
  0.6 22.2 %copy-start.5 = (s32[1,4096,1]{1,2,0:T(1,128)S(1)}, s32[1,4096,1]{1,2,0:T(1,128)}, u32[]{:S(2)}) copy-start(s32[1,4096,1]{1,2,0:T(1,128)} %param.39) | copy-start | bytes 49156
  6.4 6.8 %collective-permute-start = (f32[2,1,1,8,8,128]{5,0,4,3,2,1:T(2,128)S(1)}, f32[2,1,1,8,8,128]{5,0,4,3,2,1:T(2,128)S(1)}, u32[]{:S(2)}, u32[]{:S(2)}) collective-permute-start(f32[2,1,1,8,8,128]{5,0,4,3,2,1:T(2,128)S(1)} %pad_maximum_fusion.6), channel_id=1, source_target_pairs={{0,4},{4,8},{8,12},{12,16},{16,20},{20,24},{24,28},{1,5},{5,9},{9,... | collective-permute-start | bytes 196616 | tf_op jit(solution)/shard_map/ppermute | solution.py:16
  9.9 6.2 %collective-permute-start.1 = (f32[2,1,1,8,8,128]{5,0,4,3,2,1:T(2,128)S(1)}, f32[2,1,1,8,8,128]{5,0,4,3,2,1:T(2,128)S(1)}, u32[]{:S(2)}, u32[]{:S(2)}) collective-permute-start(f32[2,1,1,8,8,128]{5,0,4,3,2,1:T(2,128)S(1)} %pad_maximum_fusion.5), channel_id=1, source_target_pairs={{4,0},{8,4},{12,8},{16,12},{20,16},{24,20},{28,24},{5,1},{9,5},{13... | collective-permute-start | bytes 196616 | tf_op jit(solution)/shard_map/ppermute | solution.py:19
  17.3 9.3 %collective-permute-start.2 = (f32[2,1,1,8,8,128]{5,3,0,4,2,1:T(8,128)S(1)}, f32[2,1,1,8,8,128]{5,3,0,4,2,1:T(8,128)S(1)}, u32[]{:S(2)}, u32[]{:S(2)}) collective-permute-start(f32[2,1,1,8,8,128]{5,3,0,4,2,1:T(8,128)S(1)} %get-tuple-element.52), channel_id=1, source_target_pairs={{0,1},{1,2},{2,3},{4,5},{5,6},{6,7},{8,9},{9,10},{10,11},{12,13},{... | collective-permute-start | bytes 196616 | tf_op jit(solution)/shard_map/ppermute | solution.py:16
  19.2 7.4 %collective-permute-start.3 = (f32[2,1,1,8,8,128]{5,3,0,4,2,1:T(8,128)S(1)}, f32[2,1,1,8,8,128]{5,3,0,4,2,1:T(8,128)S(1)}, u32[]{:S(2)}, u32[]{:S(2)}) collective-permute-start(f32[2,1,1,8,8,128]{5,3,0,4,2,1:T(8,128)S(1)} %get-tuple-element.53), channel_id=1, source_target_pairs={{1,0},{2,1},{3,2},{5,4},{6,5},{7,6},{9,8},{10,9},{11,10},{13,12},{... | collective-permute-start | bytes 196616 | tf_op jit(solution)/shard_map/ppermute | solution.py:19
  26.1 1.3 %copy-start = (f32[8,8,1,1]{1,0,3,2:T(8,128)S(1)}, f32[8,8,1,1]{1,0,3,2:T(8,128)}, u32[]{:S(2)}) copy-start(f32[8,8,1,1]{1,0,3,2:T(8,128)} %constant.130) | copy-start | bytes 772
  26.3 2.1 %copy-start.3 = (f32[8]{0:T(128)S(1)}, f32[8]{0:T(128)}, u32[]{:S(2)}) copy-start(f32[8]{0:T(128)} %constant.125) | copy-start | bytes 100
  28.8 31.9 %copy-start.1 = (s32[1,4096]{1,0:T(1,128)S(1)}, s32[1,4096]{1,0:T(1,128)}, u32[]{:S(2)}) copy-start(s32[1,4096]{1,0:T(1,128)} %param.38) | copy-start | bytes 49156
  28.9 5.9 %collective-permute-start.4 = (f32[1,1,1,8,8,128]{5,4,3,2,1,0:T(8,128)S(1)}, f32[1,1,1,8,8,128]{5,4,3,2,1,0:T(8,128)S(1)}, u32[]{:S(2)}, u32[]{:S(2)}) collective-permute-start(f32[1,1,1,8,8,128]{5,4,3,2,1,0:T(8,128)S(1)} %get-tuple-element.83), channel_id=1, source_target_pairs={{0,4},{4,8},{8,12},{12,16},{16,20},{20,24},{24,28},{1,5},{5,9},{9,... | collective-permute-start | bytes 98312 | tf_op jit(solution)/shard_map/ppermute | solution.py:16
  33.2 5.8 %collective-permute-start.5 = (f32[1,1,1,8,8,128]{5,4,3,2,1,0:T(8,128)S(1)}, f32[1,1,1,8,8,128]{5,4,3,2,1,0:T(8,128)S(1)}, u32[]{:S(2)}, u32[]{:S(2)}) collective-permute-start(f32[1,1,1,8,8,128]{5,4,3,2,1,0:T(8,128)S(1)} %get-tuple-element.84), channel_id=1, source_target_pairs={{4,0},{8,4},{12,8},{16,12},{20,16},{24,20},{28,24},{5,1},{9,5},{13... | collective-permute-start | bytes 98312 | tf_op jit(solution)/shard_map/ppermute | solution.py:19
  39.0 5.2 %collective-permute-start.6 = (f32[1,1,1,8,8,128]{5,4,3,2,1,0:T(8,128)S(1)}, f32[1,1,1,8,8,128]{5,4,3,2,1,0:T(8,128)S(1)}, u32[]{:S(2)}, u32[]{:S(2)}) collective-permute-start(f32[1,1,1,8,8,128]{5,4,3,2,1,0:T(8,128)S(1)} %maximum_bitcast_fusion.11), channel_id=1, source_target_pairs={{0,1},{1,2},{2,3},{4,5},{5,6},{6,7},{8,9},{9,10},{10,11},{12,13},{... | collective-permute-start | bytes 98312 | tf_op jit(solution)/shard_map/ppermute | solution.py:16
  44.3 3.5 %collective-permute-start.7 = (f32[1,1,1,8,8,128]{5,4,3,2,1,0:T(8,128)S(1)}, f32[1,1,1,8,8,128]{5,4,3,2,1,0:T(8,128)S(1)}, u32[]{:S(2)}, u32[]{:S(2)}) collective-permute-start(f32[1,1,1,8,8,128]{5,4,3,2,1,0:T(8,128)S(1)} %get-tuple-element.47), channel_id=1, source_target_pairs={{1,0},{2,1},{3,2},{5,4},{6,5},{7,6},{9,8},{10,9},{11,10},{13,12},{... | collective-permute-start | bytes 98312 | tf_op jit(solution)/shard_map/ppermute | solution.py:19
  49.6 5.0 %collective-permute-start.8 = (f32[1,1,1,8,8,128]{5,4,3,2,1,0:T(8,128)S(1)}, f32[1,1,1,8,8,128]{5,4,3,2,1,0:T(8,128)S(1)}, u32[]{:S(2)}, u32[]{:S(2)}) collective-permute-start(f32[1,1,1,8,8,128]{5,4,3,2,1,0:T(8,128)S(1)} %get-tuple-element.77), channel_id=1, source_target_pairs={{0,4},{4,8},{8,12},{12,16},{16,20},{20,24},{24,28},{1,5},{5,9},{9,... | collective-permute-start | bytes 98312 | tf_op jit(solution)/shard_map/ppermute | solution.py:16
  53.0 5.8 %collective-permute-start.9 = (f32[1,1,1,8,8,128]{5,4,3,2,1,0:T(8,128)S(1)}, f32[1,1,1,8,8,128]{5,4,3,2,1,0:T(8,128)S(1)}, u32[]{:S(2)}, u32[]{:S(2)}) collective-permute-start(f32[1,1,1,8,8,128]{5,4,3,2,1,0:T(8,128)S(1)} %get-tuple-element.78), channel_id=1, source_target_pairs={{4,0},{8,4},{12,8},{16,12},{20,16},{24,20},{28,24},{5,1},{9,5},{13... | collective-permute-start | bytes 98312 | tf_op jit(solution)/shard_map/ppermute | solution.py:19
  58.8 5.2 %collective-permute-start.10 = (f32[1,1,1,8,8,128]{5,4,3,2,1,0:T(8,128)S(1)}, f32[1,1,1,8,8,128]{5,4,3,2,1,0:T(8,128)S(1)}, u32[]{:S(2)}, u32[]{:S(2)}) collective-permute-start(f32[1,1,1,8,8,128]{5,4,3,2,1,0:T(8,128)S(1)} %maximum_bitcast_fusion.9), channel_id=1, source_target_pairs={{0,1},{1,2},{2,3},{4,5},{5,6},{6,7},{8,9},{9,10},{10,11},{12,13},{... | collective-permute-start | bytes 98312 | tf_op jit(solution)/shard_map/ppermute | solution.py:16
  64.1 3.5 %collective-permute-start.11 = (f32[1,1,1,8,8,128]{5,4,3,2,1,0:T(8,128)S(1)}, f32[1,1,1,8,8,128]{5,4,3,2,1,0:T(8,128)S(1)}, u32[]{:S(2)}, u32[]{:S(2)}) collective-permute-start(f32[1,1,1,8,8,128]{5,4,3,2,1,0:T(8,128)S(1)} %get-tuple-element.45), channel_id=1, source_target_pairs={{1,0},{2,1},{3,2},{5,4},{6,5},{7,6},{9,8},{10,9},{11,10},{13,12},{... | collective-permute-start | bytes 98312 | tf_op jit(solution)/shard_map/ppermute | solution.py:19
  69.7 5.9 %collective-permute-start.12 = (f32[1,1,1,8,8,128]{5,4,3,2,1,0:T(8,128)S(1)}, f32[1,1,1,8,8,128]{5,4,3,2,1,0:T(8,128)S(1)}, u32[]{:S(2)}, u32[]{:S(2)}) collective-permute-start(f32[1,1,1,8,8,128]{5,4,3,2,1,0:T(8,128)S(1)} %get-tuple-element.71), channel_id=1, source_target_pairs={{0,4},{4,8},{8,12},{12,16},{16,20},{20,24},{24,28},{1,5},{5,9},{9,... | collective-permute-start | bytes 98312 | tf_op jit(solution)/shard_map/ppermute | solution.py:16
  74.0 5.8 %collective-permute-start.13 = (f32[1,1,1,8,8,128]{5,4,3,2,1,0:T(8,128)S(1)}, f32[1,1,1,8,8,128]{5,4,3,2,1,0:T(8,128)S(1)}, u32[]{:S(2)}, u32[]{:S(2)}) collective-permute-start(f32[1,1,1,8,8,128]{5,4,3,2,1,0:T(8,128)S(1)} %get-tuple-element.72), channel_id=1, source_target_pairs={{4,0},{8,4},{12,8},{16,12},{20,16},{24,20},{28,24},{5,1},{9,5},{13... | collective-permute-start | bytes 98312 | tf_op jit(solution)/shard_map/ppermute | solution.py:19
  79.8 5.2 %collective-permute-start.14 = (f32[1,1,1,8,8,128]{5,4,3,2,1,0:T(8,128)S(1)}, f32[1,1,1,8,8,128]{5,4,3,2,1,0:T(8,128)S(1)}, u32[]{:S(2)}, u32[]{:S(2)}) collective-permute-start(f32[1,1,1,8,8,128]{5,4,3,2,1,0:T(8,128)S(1)} %maximum_bitcast_fusion.7), channel_id=1, source_target_pairs={{0,1},{1,2},{2,3},{4,5},{5,6},{6,7},{8,9},{9,10},{10,11},{12,13},{... | collective-permute-start | bytes 98312 | tf_op jit(solution)/shard_map/ppermute | solution.py:16
  85.1 4.0 %collective-permute-start.15 = (f32[1,1,1,8,8,128]{5,4,3,2,1,0:T(8,128)S(1)}, f32[1,1,1,8,8,128]{5,4,3,2,1,0:T(8,128)S(1)}, u32[]{:S(2)}, u32[]{:S(2)}) collective-permute-start(f32[1,1,1,8,8,128]{5,4,3,2,1,0:T(8,128)S(1)} %get-tuple-element.43), channel_id=1, source_target_pairs={{1,0},{2,1},{3,2},{5,4},{6,5},{7,6},{9,8},{10,9},{11,10},{13,12},{... | collective-permute-start | bytes 98312 | tf_op jit(solution)/shard_map/ppermute | solution.py:19
  91.8 0.9 copy-start.2
  96.4 19.4 %all-to-all-start = ((f32[32,2,2048]{2,1,0:T(2,128)}), f32[32,2,2048]{2,1,0:T(2,128)S(1)}, u32[]{:S(2)}, u32[]{:S(2)}) async-start(f32[32,2,2048]{2,1,0:T(2,128)} %bitcast.113), calls=%async_computation | async-start | bytes 1048576 | tf_op jit(solution)/shard_map/all_to_all | solution.py:185
  102.1 5.1 %collective-permute-start.16 = (f32[1,1,1,8,8,128]{5,4,3,2,1,0:T(8,128)S(1)}, f32[1,1,1,8,8,128]{5,4,3,2,1,0:T(8,128)S(1)}, u32[]{:S(2)}, u32[]{:S(2)}) collective-permute-start(f32[1,1,1,8,8,128]{5,4,3,2,1,0:T(8,128)S(1)} %get-tuple-element.62), channel_id=1, source_target_pairs={{0,4},{4,8},{8,12},{12,16},{16,20},{20,24},{24,28},{1,5},{5,9},{9,... | collective-permute-start | bytes 98312 | tf_op jit(solution)/shard_map/ppermute | solution.py:16
  105.5 6.2 %collective-permute-start.17 = (f32[1,1,1,8,8,128]{5,4,3,2,1,0:T(8,128)S(1)}, f32[1,1,1,8,8,128]{5,4,3,2,1,0:T(8,128)S(1)}, u32[]{:S(2)}, u32[]{:S(2)}) collective-permute-start(f32[1,1,1,8,8,128]{5,4,3,2,1,0:T(8,128)S(1)} %get-tuple-element.63), channel_id=1, source_target_pairs={{4,0},{8,4},{12,8},{16,12},{20,16},{24,20},{28,24},{5,1},{9,5},{13... | collective-permute-start | bytes 98312 | tf_op jit(solution)/shard_map/ppermute | solution.py:19
  116.8 9.0 %collective-permute-start.18 = (f32[1,1,1,8,8,128]{5,4,3,2,1,0:T(8,128)S(1)}, f32[1,1,1,8,8,128]{5,4,3,2,1,0:T(8,128)S(1)}, u32[]{:S(2)}, u32[]{:S(2)}) collective-permute-start(f32[1,1,1,8,8,128]{5,4,3,2,1,0:T(8,128)S(1)} %get-tuple-element.91), channel_id=1, source_target_pairs={{0,1},{1,2},{2,3},{4,5},{5,6},{6,7},{8,9},{9,10},{10,11},{12,13},{... | collective-permute-start | bytes 98312 | tf_op jit(solution)/shard_map/ppermute | solution.py:16
  118.7 7.1 %collective-permute-start.19 = (f32[1,1,1,8,8,128]{5,4,3,2,1,0:T(8,128)S(1)}, f32[1,1,1,8,8,128]{5,4,3,2,1,0:T(8,128)S(1)}, u32[]{:S(2)}, u32[]{:S(2)}) collective-permute-start(f32[1,1,1,8,8,128]{5,4,3,2,1,0:T(8,128)S(1)} %get-tuple-element.92), channel_id=1, source_target_pairs={{1,0},{2,1},{3,2},{5,4},{6,5},{7,6},{9,8},{10,9},{11,10},{13,12},{... | collective-permute-start | bytes 98312 | tf_op jit(solution)/shard_map/ppermute | solution.py:19
  122.3 10.8 %all-to-all-start.1 = ((f32[8,2,2048]{2,1,0:T(2,128)}), f32[8,2,2048]{2,1,0:T(2,128)S(1)}, u32[]{:S(2)}, u32[]{:S(2)}) async-start(f32[8,2,2048]{2,1,0:T(2,128)} %broadcast_in_dim.200), calls=%async_computation.1 | async-start | bytes 262144 | tf_op jit(solution)/shard_map/all_to_all | solution.py:194

commit v23 on v21

--- a/solution.py
+++ b/solution.py
@@ -229,10 +229,11 @@
             partial = jnp.stack([numer, denom])
             assembled, mine = assemble(applied[None], strip_reduce(partial, strips, SHELL_STRIP), strip_spread)
         else:
-            assembled, _ = assemble(applied[None])
+            if step + 2 == SWEEPS:
+                assembled, early = assemble(applied[None], early)
+            else:
+                assembled, _ = assemble(applied[None])
         assembled = assembled[0]
-        if step + 2 == SWEEPS:
-            assembled, early = lax.optimization_barrier((assembled, early))
         if step == 0:
             assembled, denom = lax.optimization_barrier((assembled, denom))
         resid = resid - assembled

time: 131 us -> 131 us (level)
    ppermute x10, waiting for transfers between devices: 6.59 us -> 8.46 us  [padded_2(): lax.ppermute(lax.slice_in_dim(block, block.shape[dim] - width, None, axis...]
    ppermute x10, waiting for transfers between devices: 23.6 us -> 21.8 us  [padded_2(): lax.ppermute(lax.slice_in_dim(block, 0, width, axis=dim), axis, backward)]
  transfers between devices with their start and end apart: 22 -> 22, of which waited for: 17 -> 16; matrix products, arithmetic and copies ran while one was open for 9% -> 9% of each run, Pallas kernels for 0% -> 0%
where the time goes in v23:
time: 131 us; the launch traced here: 130 us
  starting transfers between devices  56.5 us (43%)
  waiting for transfers between devices  40.7 us (31%)
  other arithmetic  12 us (9%)
  matrix products  12 us (9%)
  local copies, waits for them, and re-layouts  7.15 us (5%)
  between operations  1.68 us (1%)
    ppermute x10, starting transfers between devices, padded_2(): lax.ppermute(lax.slice_in_dim(block, block.shape[dim] - width, None, axis...  28.5 us
    ppermute x10, waiting for transfers between devices, padded_2(): lax.ppermute(lax.slice_in_dim(block, 0, width, axis=dim), axis, backward)  21.8 us
    ppermute x10, starting transfers between devices, padded_2(): lax.ppermute(lax.slice_in_dim(block, 0, width, axis=dim), axis, backward)  20 us
    ppermute x10, waiting for transfers between devices, padded_2(): lax.ppermute(lax.slice_in_dim(block, block.shape[dim] - width, None, axis...  8.46 us
    all_to_all x1, waiting for transfers between devices, strip_gather(): whole = lax.all_to_all(spread_out, 'ex', 0, 0, tiled=True)  6.31 us
    all_to_all x1, starting transfers between devices, strip_reduce(): return lax.all_to_all(chunks, ('ex', 'ey'), 0, 0, tiled=True).sum(0)  4.53 us
    all_to_all x1, waiting for transfers between devices, strip_reduce(): return lax.all_to_all(chunks, ('ex', 'ey'), 0, 0, tiled=True).sum(0)  4.09 us
    all_to_all x1, starting transfers between devices, strip_gather(): whole = lax.all_to_all(spread_out, 'ex', 0, 0, tiled=True)  3.46 us
  transfers between devices with their start and end apart: 22, of which 16 were waited for; matrix products, arithmetic and copies ran while one was open for 9% of the time, Pallas kernels for 0%

profile of v23, /device:TPU:2, one launch (start us, length us, event | category | flops | bytes accessed | tf_op | source)
XLA Modules:
  0.0 130.1 jit_solution(13488169554836720979)
XLA Ops:
  4.5 3.4 %collective-permute-start = (f32[2,1,1,8,8,128]{5,4,3,2,1,0:T(8,128)S(1)}, f32[2,1,1,8,8,128]{5,4,3,2,1,0:T(8,128)S(1)}, u32[]{:S(2)}, u32[]{:S(2)}) collective-permute-start(f32[2,1,1,8,8,128]{5,4,3,2,1,0:T(8,128)S(1)} %pad_maximum_fusion.11), channel_id=1, source_target_pairs={{0,4},{4,8},{8,12},{12,16},{16,20},{20,24},{24,28},{1,5},{5,9},{9,... | collective-permute-start | bytes 196616 | tf_op jit(solution)/shard_map/ppermute | solution.py:16
  7.9 1.3 collective-permute-start.1
  10.1 1.1 copy.281
  11.2 2.9 %collective-permute-done.1 = f32[2,1,1,8,8,128]{5,4,3,2,1,0:T(8,128)S(1)} collective-permute-done((f32[2,1,1,8,8,128]{5,4,3,2,1,0:T(8,128)S(1)}, f32[2,1,1,8,8,128]{5,4,3,2,1,0:T(8,128)S(1)}, u32[]{:S(2)}, u32[]{:S(2)}) %collective-permute-start.1) | collective-permute-done | bytes 65568 | tf_op jit(solution)/shard_map/ppermute | solution.py:19
  14.5 1.9 %collective-permute-start.2 = (f32[2,1,1,8,8,128]{5,3,0,4,2,1:T(8,128)S(1)}, f32[2,1,1,8,8,128]{5,3,0,4,2,1:T(8,128)S(1)}, u32[]{:S(2)}, u32[]{:S(2)}) collective-permute-start(f32[2,1,1,8,8,128]{5,3,0,4,2,1:T(8,128)S(1)} %get-tuple-element.56), channel_id=1, source_target_pairs={{0,1},{1,2},{2,3},{4,5},{5,6},{6,7},{8,9},{9,10},{10,11},{12,13},{... | collective-permute-start | bytes 196616 | tf_op jit(solution)/shard_map/ppermute | solution.py:16
  16.4 3.6 %collective-permute-start.3 = (f32[2,1,1,8,8,128]{5,3,0,4,2,1:T(8,128)S(1)}, f32[2,1,1,8,8,128]{5,3,0,4,2,1:T(8,128)S(1)}, u32[]{:S(2)}, u32[]{:S(2)}) collective-permute-start(f32[2,1,1,8,8,128]{5,3,0,4,2,1:T(8,128)S(1)} %get-tuple-element.57), channel_id=1, source_target_pairs={{1,0},{2,1},{3,2},{5,4},{6,5},{7,6},{9,8},{10,9},{11,10},{13,12},{... | collective-permute-start | bytes 196616 | tf_op jit(solution)/shard_map/ppermute | solution.py:19
  20.4 1.5 %collective-permute-done.3 = f32[2,1,1,8,8,128]{5,3,0,4,2,1:T(8,128)S(1)} collective-permute-done((f32[2,1,1,8,8,128]{5,3,0,4,2,1:T(8,128)S(1)}, f32[2,1,1,8,8,128]{5,3,0,4,2,1:T(8,128)S(1)}, u32[]{:S(2)}, u32[]{:S(2)}) %collective-permute-start.3) | collective-permute-done | bytes 65568 | tf_op jit(solution)/shard_map/ppermute | solution.py:19
  23.7 0.9 fusion.30
  24.7 4.3 %collective-permute-start.4 = (f32[1,1,1,8,8,128]{5,4,3,2,1,0:T(8,128)S(1)}, f32[1,1,1,8,8,128]{5,4,3,2,1,0:T(8,128)S(1)}, u32[]{:S(2)}, u32[]{:S(2)}) collective-permute-start(f32[1,1,1,8,8,128]{5,4,3,2,1,0:T(8,128)S(1)} %bitcast.467), channel_id=1, source_target_pairs={{0,4},{4,8},{8,12},{12,16},{16,20},{20,24},{24,28},{1,5},{5,9},{9,... | collective-permute-start | bytes 98312 | tf_op jit(solution)/shard_map/ppermute | solution.py:16
  29.0 1.3 collective-permute-start.5
  30.3 1.2 fusion.20
  31.6 3.2 %collective-permute-done.5 = f32[1,1,1,8,8,128]{5,4,3,2,1,0:T(8,128)S(1)} collective-permute-done((f32[1,1,1,8,8,128]{5,4,3,2,1,0:T(8,128)S(1)}, f32[1,1,1,8,8,128]{5,4,3,2,1,0:T(8,128)S(1)}, u32[]{:S(2)}, u32[]{:S(2)}) %collective-permute-start.5) | collective-permute-done | bytes 32800 | tf_op jit(solution)/shard_map/ppermute | solution.py:19
  34.8 1.9 %collective-permute-start.6 = (f32[1,1,1,8,8,128]{5,3,4,2,1,0:T(8,128)S(1)}, f32[1,1,1,8,8,128]{5,3,4,2,1,0:T(8,128)S(1)}, u32[]{:S(2)}, u32[]{:S(2)}) collective-permute-start(f32[1,1,1,8,8,128]{5,3,4,2,1,0:T(8,128)S(1)} %maximum_bitcast_fusion.15), channel_id=1, source_target_pairs={{0,1},{1,2},{2,3},{4,5},{5,6},{6,7},{8,9},{9,10},{10,11},{12,13},{... | collective-permute-start | bytes 98312 | tf_op jit(solution)/shard_map/ppermute | solution.py:16
  36.8 1.9 %fusion = f32[768,256]{1,0:T(8,128)S(1)} fusion(bf16[256,4096]{1,0:T(8,128)(2,1)S(1)} %get-tuple-element.102, bf16[256,4096]{1,0:T(8,128)(2,1)S(1)} %get-tuple-element.103, bf16[256,4096]{1,0:T(8,128)(2,1)S(1)} %get-tuple-element.101, s32[4096]{0:T(1024)S(1)} %get-tuple-element.97), kind=kOutput, calls=%fused_computation | convolution fusion | flops 1630535680 | bytes 7094272 | tf_op jit(solution)/shard_map/dot_general | solution.py:170
  38.7 1.4 %collective-permute-done.6 = f32[1,1,1,8,8,128]{5,3,4,2,1,0:T(8,128)S(1)} collective-permute-done((f32[1,1,1,8,8,128]{5,3,4,2,1,0:T(8,128)S(1)}, f32[1,1,1,8,8,128]{5,3,4,2,1,0:T(8,128)S(1)}, u32[]{:S(2)}, u32[]{:S(2)}) %collective-permute-start.6) | collective-permute-done | bytes 32800 | tf_op jit(solution)/shard_map/ppermute | solution.py:16
  40.1 2.3 %collective-permute-start.7 = (f32[1,1,1,8,8,128]{5,3,4,2,1,0:T(8,128)S(1)}, f32[1,1,1,8,8,128]{5,3,4,2,1,0:T(8,128)S(1)}, u32[]{:S(2)}, u32[]{:S(2)}) collective-permute-start(f32[1,1,1,8,8,128]{5,3,4,2,1,0:T(8,128)S(1)} %get-tuple-element.49), channel_id=1, source_target_pairs={{1,0},{2,1},{3,2},{5,4},{6,5},{7,6},{9,8},{10,9},{11,10},{13,12},{... | collective-permute-start | bytes 98312 | tf_op jit(solution)/shard_map/ppermute | solution.py:19
  42.6 1.4 %collective-permute-done.7 = f32[1,1,1,8,8,128]{5,3,4,2,1,0:T(8,128)S(1)} collective-permute-done((f32[1,1,1,8,8,128]{5,3,4,2,1,0:T(8,128)S(1)}, f32[1,1,1,8,8,128]{5,3,4,2,1,0:T(8,128)S(1)}, u32[]{:S(2)}, u32[]{:S(2)}) %collective-permute-start.7) | collective-permute-done | bytes 32800 | tf_op jit(solution)/shard_map/ppermute | solution.py:19
  45.9 3.4 %collective-permute-start.8 = (f32[1,1,1,8,8,128]{5,4,3,2,1,0:T(8,128)S(1)}, f32[1,1,1,8,8,128]{5,4,3,2,1,0:T(8,128)S(1)}, u32[]{:S(2)}, u32[]{:S(2)}) collective-permute-start(f32[1,1,1,8,8,128]{5,4,3,2,1,0:T(8,128)S(1)} %get-tuple-element.79), channel_id=1, source_target_pairs={{0,4},{4,8},{8,12},{12,16},{16,20},{20,24},{24,28},{1,5},{5,9},{9,... | collective-permute-start | bytes 98312 | tf_op jit(solution)/shard_map/ppermute | solution.py:16
  49.3 1.3 collective-permute-start.9
  50.9 4.2 %collective-permute-done.9 = f32[1,1,1,8,8,128]{5,4,3,2,1,0:T(8,128)S(1)} collective-permute-done((f32[1,1,1,8,8,128]{5,4,3,2,1,0:T(8,128)S(1)}, f32[1,1,1,8,8,128]{5,4,3,2,1,0:T(8,128)S(1)}, u32[]{:S(2)}, u32[]{:S(2)}) %collective-permute-start.9) | collective-permute-done | bytes 32800 | tf_op jit(solution)/shard_map/ppermute | solution.py:19
  55.2 1.9 %collective-permute-start.10 = (f32[1,1,1,8,8,128]{5,4,3,2,1,0:T(8,128)S(1)}, f32[1,1,1,8,8,128]{5,4,3,2,1,0:T(8,128)S(1)}, u32[]{:S(2)}, u32[]{:S(2)}) collective-permute-start(f32[1,1,1,8,8,128]{5,4,3,2,1,0:T(8,128)S(1)} %maximum_bitcast_fusion.13), channel_id=1, source_target_pairs={{0,1},{1,2},{2,3},{4,5},{5,6},{6,7},{8,9},{9,10},{10,11},{12,13},{... | collective-permute-start | bytes 98312 | tf_op jit(solution)/shard_map/ppermute | solution.py:16
  57.2 3.2 %collective-permute-done.10 = f32[1,1,1,8,8,128]{5,4,3,2,1,0:T(8,128)S(1)} collective-permute-done((f32[1,1,1,8,8,128]{5,4,3,2,1,0:T(8,128)S(1)}, f32[1,1,1,8,8,128]{5,4,3,2,1,0:T(8,128)S(1)}, u32[]{:S(2)}, u32[]{:S(2)}) %collective-permute-start.10) | collective-permute-done | bytes 32800 | tf_op jit(solution)/shard_map/ppermute | solution.py:16
  60.4 1.9 %collective-permute-start.11 = (f32[1,1,1,8,8,128]{5,4,3,2,1,0:T(8,128)S(1)}, f32[1,1,1,8,8,128]{5,4,3,2,1,0:T(8,128)S(1)}, u32[]{:S(2)}, u32[]{:S(2)}) collective-permute-start(f32[1,1,1,8,8,128]{5,4,3,2,1,0:T(8,128)S(1)} %get-tuple-element.47), channel_id=1, source_target_pairs={{1,0},{2,1},{3,2},{5,4},{6,5},{7,6},{9,8},{10,9},{11,10},{13,12},{... | collective-permute-start | bytes 98312 | tf_op jit(solution)/shard_map/ppermute | solution.py:19
  62.4 1.5 %collective-permute-done.11 = f32[1,1,1,8,8,128]{5,4,3,2,1,0:T(8,128)S(1)} collective-permute-done((f32[1,1,1,8,8,128]{5,4,3,2,1,0:T(8,128)S(1)}, f32[1,1,1,8,8,128]{5,4,3,2,1,0:T(8,128)S(1)}, u32[]{:S(2)}, u32[]{:S(2)}) %collective-permute-start.11) | collective-permute-done | bytes 32800 | tf_op jit(solution)/shard_map/ppermute | solution.py:19
  66.1 4.3 %collective-permute-start.12 = (f32[1,1,1,8,8,128]{5,4,3,2,1,0:T(8,128)S(1)}, f32[1,1,1,8,8,128]{5,4,3,2,1,0:T(8,128)S(1)}, u32[]{:S(2)}, u32[]{:S(2)}) collective-permute-start(f32[1,1,1,8,8,128]{5,4,3,2,1,0:T(8,128)S(1)} %get-tuple-element.73), channel_id=1, source_target_pairs={{0,4},{4,8},{8,12},{12,16},{16,20},{20,24},{24,28},{1,5},{5,9},{9,... | collective-permute-start | bytes 98312 | tf_op jit(solution)/shard_map/ppermute | solution.py:16
  70.4 1.5 %collective-permute-start.13 = (f32[1,1,1,8,8,128]{5,4,3,2,1,0:T(8,128)S(1)}, f32[1,1,1,8,8,128]{5,4,3,2,1,0:T(8,128)S(1)}, u32[]{:S(2)}, u32[]{:S(2)}) collective-permute-start(f32[1,1,1,8,8,128]{5,4,3,2,1,0:T(8,128)S(1)} %get-tuple-element.74), channel_id=1, source_target_pairs={{4,0},{8,4},{12,8},{16,12},{20,16},{24,20},{28,24},{5,1},{9,5},{13... | collective-permute-start | bytes 98312 | tf_op jit(solution)/shard_map/ppermute | solution.py:19
  71.9 1.9 %fusion.15 = f32[768,4096]{1,0:T(8,128)S(1)} fusion(s32[4096]{0:T(1024)S(1)} %bitcast.461, bf16[256,256]{1,0:T(8,128)(2,1)S(1)} %get-tuple-element.71, bf16[256,256]{1,0:T(8,128)(2,1)S(1)} %get-tuple-element.72, bf16[256,256]{1,0:T(8,128)(2,1)S(1)} %get-tuple-element.70), kind=kOutput, calls=%fused_computation.19 | convolution fusion | flops 1612840960 | bytes 12992512 | tf_op jit(solution)/shard_map/dot_general | solution.py:156
  73.8 1.4 %fusion.9 = f32[4096]{0:T(1024)S(1)} fusion(f32[768,4096]{1,0:T(8,128)S(1)} %fusion.15, s32[4096]{0:T(1024)S(1)} %bitcast.459), kind=kLoop, calls=%fused_computation.11 | loop fusion | flops 5238784 | bytes 12615680 | tf_op jit(solution)/shard_map/reduce_sum | solution.py:161
  75.2 1.1 collective-permute-done.13
  76.3 1.9 %collective-permute-start.14 = (f32[1,1,1,8,8,128]{5,4,3,2,1,0:T(8,128)S(1)}, f32[1,1,1,8,8,128]{5,4,3,2,1,0:T(8,128)S(1)}, u32[]{:S(2)}, u32[]{:S(2)}) collective-permute-start(f32[1,1,1,8,8,128]{5,4,3,2,1,0:T(8,128)S(1)} %maximum_bitcast_fusion.11), channel_id=1, source_target_pairs={{0,1},{1,2},{2,3},{4,5},{5,6},{6,7},{8,9},{9,10},{10,11},{12,13},{... | collective-permute-start | bytes 98312 | tf_op jit(solution)/shard_map/ppermute | solution.py:16
  78.2 3.3 %collective-permute-done.14 = f32[1,1,1,8,8,128]{5,4,3,2,1,0:T(8,128)S(1)} collective-permute-done((f32[1,1,1,8,8,128]{5,4,3,2,1,0:T(8,128)S(1)}, f32[1,1,1,8,8,128]{5,4,3,2,1,0:T(8,128)S(1)}, u32[]{:S(2)}, u32[]{:S(2)}) %collective-permute-start.14) | collective-permute-done | bytes 32800 | tf_op jit(solution)/shard_map/ppermute | solution.py:16
  81.5 1.9 %collective-permute-start.15 = (f32[1,1,1,8,8,128]{5,4,3,2,1,0:T(8,128)S(1)}, f32[1,1,1,8,8,128]{5,4,3,2,1,0:T(8,128)S(1)}, u32[]{:S(2)}, u32[]{:S(2)}) collective-permute-start(f32[1,1,1,8,8,128]{5,4,3,2,1,0:T(8,128)S(1)} %get-tuple-element.41), channel_id=1, source_target_pairs={{1,0},{2,1},{3,2},{5,4},{6,5},{7,6},{9,8},{10,9},{11,10},{13,12},{... | collective-permute-start | bytes 98312 | tf_op jit(solution)/shard_map/ppermute | solution.py:19
  83.5 1.5 %collective-permute-done.15 = f32[1,1,1,8,8,128]{5,4,3,2,1,0:T(8,128)S(1)} collective-permute-done((f32[1,1,1,8,8,128]{5,4,3,2,1,0:T(8,128)S(1)}, f32[1,1,1,8,8,128]{5,4,3,2,1,0:T(8,128)S(1)}, u32[]{:S(2)}, u32[]{:S(2)}) %collective-permute-start.15) | collective-permute-done | bytes 32800 | tf_op jit(solution)/shard_map/ppermute | solution.py:19
  85.6 0.8 fusion.112
  86.5 1.3 %fusion.14 = f32[512,4096]{1,0:T(8,128)S(1)} fusion(s32[4096]{0:T(1024)S(1)} %bitcast.462, bf16[256,256]{1,0:T(8,128)(2,1)S(1)} %get-tuple-element.65, bf16[256,256]{1,0:T(8,128)(2,1)S(1)} %get-tuple-element.64), kind=kOutput, calls=%fused_computation.18 | convolution fusion | flops 1075314688 | bytes 8667136 | tf_op jit(solution)/shard_map/dot_general | solution.py:156
  87.8 0.9 fusion.7
  88.7 0.9 fusion.17
  89.6 1.4 %fusion.10 = f32[512,256]{1,0:T(8,128)S(1)} fusion(bf16[256,4096]{1,0:T(8,128)(2,1)S(1)} %get-tuple-element.100, bf16[256,4096]{1,0:T(8,128)(2,1)S(1)} %get-tuple-element.99, s32[4096]{0:T(1024)S(1)} %get-tuple-element.97), kind=kOutput, calls=%fused_computation.13 | convolution fusion | flops 1083179008 | bytes 4734976 | tf_op jit(solution)/shard_map/dot_general | solution.py:170
  91.2 1.2 copy.213
  92.4 4.5 %all-to-all-start = ((f32[32,2,2048]{2,1,0:T(2,128)}), f32[32,2,2048]{2,1,0:T(2,128)S(1)}, u32[]{:S(2)}, u32[]{:S(2)}) async-start(f32[32,2,2048]{2,1,0:T(2,128)} %bitcast.107), calls=%async_computation | async-start | bytes 1048576 | tf_op jit(solution)/shard_map/all_to_all | solution.py:185
  98.3 3.4 %collective-permute-start.16 = (f32[1,1,1,8,8,128]{5,4,3,2,1,0:T(8,128)S(1)}, f32[1,1,1,8,8,128]{5,4,3,2,1,0:T(8,128)S(1)}, u32[]{:S(2)}, u32[]{:S(2)}) collective-permute-start(f32[1,1,1,8,8,128]{5,4,3,2,1,0:T(8,128)S(1)} %get-tuple-element.66), channel_id=1, source_target_pairs={{0,4},{4,8},{8,12},{12,16},{16,20},{20,24},{24,28},{1,5},{5,9},{9,... | collective-permute-start | bytes 98312 | tf_op jit(solution)/shard_map/ppermute | solution.py:16
  101.6 1.3 collective-permute-start.17
  103.4 4.5 %collective-permute-done.17 = f32[1,1,1,8,8,128]{5,4,3,2,1,0:T(8,128)S(1)} collective-permute-done((f32[1,1,1,8,8,128]{5,4,3,2,1,0:T(8,128)S(1)}, f32[1,1,1,8,8,128]{5,4,3,2,1,0:T(8,128)S(1)}, u32[]{:S(2)}, u32[]{:S(2)}) %collective-permute-start.17) | collective-permute-done | bytes 32800 | tf_op jit(solution)/shard_map/ppermute | solution.py:19
  107.9 4.1 %all-to-all-done = f32[32,2,2048]{2,1,0:T(2,128)S(1)} async-done(((f32[32,2,2048]{2,1,0:T(2,128)}), f32[32,2,2048]{2,1,0:T(2,128)S(1)}, u32[]{:S(2)}, u32[]{:S(2)}) %all-to-all-start) | async-done | bytes 524320 | tf_op jit(solution)/shard_map/all_to_all | solution.py:185
  112.9 1.9 %collective-permute-start.18 = (f32[1,1,1,8,8,128]{5,3,4,2,1,0:T(8,128)S(1)}, f32[1,1,1,8,8,128]{5,3,4,2,1,0:T(8,128)S(1)}, u32[]{:S(2)}, u32[]{:S(2)}) collective-permute-start(f32[1,1,1,8,8,128]{5,3,4,2,1,0:T(8,128)S(1)} %get-tuple-element.93), channel_id=1, source_target_pairs={{0,1},{1,2},{2,3},{4,5},{5,6},{6,7},{8,9},{9,10},{10,11},{12,13},{... | collective-permute-start | bytes 98312 | tf_op jit(solution)/shard_map/ppermute | solution.py:16
  114.9 3.6 %collective-permute-start.19 = (f32[1,1,1,8,8,128]{5,3,4,2,1,0:T(8,128)S(1)}, f32[1,1,1,8,8,128]{5,3,4,2,1,0:T(8,128)S(1)}, u32[]{:S(2)}, u32[]{:S(2)}) collective-permute-start(f32[1,1,1,8,8,128]{5,3,4,2,1,0:T(8,128)S(1)} %get-tuple-element.94), channel_id=1, source_target_pairs={{1,0},{2,1},{3,2},{5,4},{6,5},{7,6},{9,8},{10,9},{11,10},{13,12},{... | collective-permute-start | bytes 98312 | tf_op jit(solution)/shard_map/ppermute | solution.py:19
  118.6 3.5 %all-to-all-start.1 = ((f32[8,2,2048]{2,1,0:T(2,128)}), f32[8,2,2048]{2,1,0:T(2,128)S(1)}, u32[]{:S(2)}, u32[]{:S(2)}) async-start(f32[8,2,2048]{2,1,0:T(2,128)} %broadcast_in_dim.200), calls=%async_computation.1 | async-start | bytes 262144 | tf_op jit(solution)/shard_map/all_to_all | solution.py:194
  123.0 6.3 %all-to-all-done.1 = f32[8,2,2048]{2,1,0:T(2,128)S(1)} async-done(((f32[8,2,2048]{2,1,0:T(2,128)}), f32[8,2,2048]{2,1,0:T(2,128)S(1)}, u32[]{:S(2)}, u32[]{:S(2)}) %all-to-all-start.1) | async-done | bytes 131104 | tf_op jit(solution)/shard_map/all_to_all | solution.py:194
  (141 shorter events, 16.8 us)
Async XLA Ops:
  0.6 19.5 %copy-start.2 = (f32[1,4096]{1,0:T(1,128)S(1)}, f32[1,4096]{1,0:T(1,128)}, u32[]{:S(2)}) copy-start(f32[1,4096]{1,0:T(1,128)} %param.41) | copy-start | bytes 49156
  0.6 19.4 %copy-start.5 = (s32[1,4096,1]{1,2,0:T(1,128)S(1)}, s32[1,4096,1]{1,2,0:T(1,128)}, u32[]{:S(2)}) copy-start(s32[1,4096,1]{1,2,0:T(1,128)} %param.39) | copy-start | bytes 49156
  0.7 19.4 %copy-start.4 = (s32[1,4096]{1,0:T(1,128)S(1)}, s32[1,4096]{1,0:T(1,128)}, u32[]{:S(2)}) copy-start(s32[1,4096]{1,0:T(1,128)} %param.40) | copy-start | bytes 49156
  4.5 6.7 %collective-permute-start = (f32[2,1,1,8,8,128]{5,4,3,2,1,0:T(8,128)S(1)}, f32[2,1,1,8,8,128]{5,4,3,2,1,0:T(8,128)S(1)}, u32[]{:S(2)}, u32[]{:S(2)}) collective-permute-start(f32[2,1,1,8,8,128]{5,4,3,2,1,0:T(8,128)S(1)} %pad_maximum_fusion.11), channel_id=1, source_target_pairs={{0,4},{4,8},{8,12},{12,16},{16,20},{20,24},{24,28},{1,5},{5,9},{9,... | collective-permute-start | bytes 196616 | tf_op jit(solution)/shard_map/ppermute | solution.py:16
  7.9 6.2 %collective-permute-start.1 = (f32[2,1,1,8,8,128]{5,4,3,2,1,0:T(8,128)S(1)}, f32[2,1,1,8,8,128]{5,4,3,2,1,0:T(8,128)S(1)}, u32[]{:S(2)}, u32[]{:S(2)}) collective-permute-start(f32[2,1,1,8,8,128]{5,4,3,2,1,0:T(8,128)S(1)} %pad_maximum_fusion.10), channel_id=1, source_target_pairs={{4,0},{8,4},{12,8},{16,12},{20,16},{24,20},{28,24},{5,1},{9,5},{13... | collective-permute-start | bytes 196616 | tf_op jit(solution)/shard_map/ppermute | solution.py:19
  14.5 8.3 %copy-start = (f32[8,8,1,1]{1,0,3,2:T(8,128)S(1)}, f32[8,8,1,1]{1,0,3,2:T(8,128)}, u32[]{:S(2)}) copy-start(f32[8,8,1,1]{1,0,3,2:T(8,128)} %constant.130) | copy-start | bytes 772
  14.5 6.0 %collective-permute-start.2 = (f32[2,1,1,8,8,128]{5,3,0,4,2,1:T(8,128)S(1)}, f32[2,1,1,8,8,128]{5,3,0,4,2,1:T(8,128)S(1)}, u32[]{:S(2)}, u32[]{:S(2)}) collective-permute-start(f32[2,1,1,8,8,128]{5,3,0,4,2,1:T(8,128)S(1)} %get-tuple-element.56), channel_id=1, source_target_pairs={{0,1},{1,2},{2,3},{4,5},{5,6},{6,7},{8,9},{9,10},{10,11},{12,13},{... | collective-permute-start | bytes 196616 | tf_op jit(solution)/shard_map/ppermute | solution.py:16
  16.4 5.5 %collective-permute-start.3 = (f32[2,1,1,8,8,128]{5,3,0,4,2,1:T(8,128)S(1)}, f32[2,1,1,8,8,128]{5,3,0,4,2,1:T(8,128)S(1)}, u32[]{:S(2)}, u32[]{:S(2)}) collective-permute-start(f32[2,1,1,8,8,128]{5,3,0,4,2,1:T(8,128)S(1)} %get-tuple-element.57), channel_id=1, source_target_pairs={{1,0},{2,1},{3,2},{5,4},{6,5},{7,6},{9,8},{10,9},{11,10},{13,12},{... | collective-permute-start | bytes 196616 | tf_op jit(solution)/shard_map/ppermute | solution.py:19
  20.2 3.4 %copy-start.3 = (f32[8]{0:T(128)S(1)}, f32[8]{0:T(128)}, u32[]{:S(2)}) copy-start(f32[8]{0:T(128)} %constant.125) | copy-start | bytes 100
  24.7 6.9 %collective-permute-start.4 = (f32[1,1,1,8,8,128]{5,4,3,2,1,0:T(8,128)S(1)}, f32[1,1,1,8,8,128]{5,4,3,2,1,0:T(8,128)S(1)}, u32[]{:S(2)}, u32[]{:S(2)}) collective-permute-start(f32[1,1,1,8,8,128]{5,4,3,2,1,0:T(8,128)S(1)} %bitcast.467), channel_id=1, source_target_pairs={{0,4},{4,8},{8,12},{12,16},{16,20},{20,24},{24,28},{1,5},{5,9},{9,... | collective-permute-start | bytes 98312 | tf_op jit(solution)/shard_map/ppermute | solution.py:16
  29.0 5.8 %collective-permute-start.5 = (f32[1,1,1,8,8,128]{5,4,3,2,1,0:T(8,128)S(1)}, f32[1,1,1,8,8,128]{5,4,3,2,1,0:T(8,128)S(1)}, u32[]{:S(2)}, u32[]{:S(2)}) collective-permute-start(f32[1,1,1,8,8,128]{5,4,3,2,1,0:T(8,128)S(1)} %bitcast.469), channel_id=1, source_target_pairs={{4,0},{8,4},{12,8},{16,12},{20,16},{24,20},{28,24},{5,1},{9,5},{13... | collective-permute-start | bytes 98312 | tf_op jit(solution)/shard_map/ppermute | solution.py:19
  34.8 5.2 %collective-permute-start.6 = (f32[1,1,1,8,8,128]{5,3,4,2,1,0:T(8,128)S(1)}, f32[1,1,1,8,8,128]{5,3,4,2,1,0:T(8,128)S(1)}, u32[]{:S(2)}, u32[]{:S(2)}) collective-permute-start(f32[1,1,1,8,8,128]{5,3,4,2,1,0:T(8,128)S(1)} %maximum_bitcast_fusion.15), channel_id=1, source_target_pairs={{0,1},{1,2},{2,3},{4,5},{5,6},{6,7},{8,9},{9,10},{10,11},{12,13},{... | collective-permute-start | bytes 98312 | tf_op jit(solution)/shard_map/ppermute | solution.py:16
  40.1 17.0 %copy-start.1 = (s32[1,4096]{1,0:T(1,128)S(1)}, s32[1,4096]{1,0:T(1,128)}, u32[]{:S(2)}) copy-start(s32[1,4096]{1,0:T(1,128)} %param.38) | copy-start | bytes 49156
  40.1 3.9 %collective-permute-start.7 = (f32[1,1,1,8,8,128]{5,3,4,2,1,0:T(8,128)S(1)}, f32[1,1,1,8,8,128]{5,3,4,2,1,0:T(8,128)S(1)}, u32[]{:S(2)}, u32[]{:S(2)}) collective-permute-start(f32[1,1,1,8,8,128]{5,3,4,2,1,0:T(8,128)S(1)} %get-tuple-element.49), channel_id=1, source_target_pairs={{1,0},{2,1},{3,2},{5,4},{6,5},{7,6},{9,8},{10,9},{11,10},{13,12},{... | collective-permute-start | bytes 98312 | tf_op jit(solution)/shard_map/ppermute | solution.py:19
  45.9 5.0 %collective-permute-start.8 = (f32[1,1,1,8,8,128]{5,4,3,2,1,0:T(8,128)S(1)}, f32[1,1,1,8,8,128]{5,4,3,2,1,0:T(8,128)S(1)}, u32[]{:S(2)}, u32[]{:S(2)}) collective-permute-start(f32[1,1,1,8,8,128]{5,4,3,2,1,0:T(8,128)S(1)} %get-tuple-element.79), channel_id=1, source_target_pairs={{0,4},{4,8},{8,12},{12,16},{16,20},{20,24},{24,28},{1,5},{5,9},{9,... | collective-permute-start | bytes 98312 | tf_op jit(solution)/shard_map/ppermute | solution.py:16
  49.3 5.8 %collective-permute-start.9 = (f32[1,1,1,8,8,128]{5,4,3,2,1,0:T(8,128)S(1)}, f32[1,1,1,8,8,128]{5,4,3,2,1,0:T(8,128)S(1)}, u32[]{:S(2)}, u32[]{:S(2)}) collective-permute-start(f32[1,1,1,8,8,128]{5,4,3,2,1,0:T(8,128)S(1)} %get-tuple-element.80), channel_id=1, source_target_pairs={{4,0},{8,4},{12,8},{16,12},{20,16},{24,20},{28,24},{5,1},{9,5},{13... | collective-permute-start | bytes 98312 | tf_op jit(solution)/shard_map/ppermute | solution.py:19
  55.2 5.2 %collective-permute-start.10 = (f32[1,1,1,8,8,128]{5,4,3,2,1,0:T(8,128)S(1)}, f32[1,1,1,8,8,128]{5,4,3,2,1,0:T(8,128)S(1)}, u32[]{:S(2)}, u32[]{:S(2)}) collective-permute-start(f32[1,1,1,8,8,128]{5,4,3,2,1,0:T(8,128)S(1)} %maximum_bitcast_fusion.13), channel_id=1, source_target_pairs={{0,1},{1,2},{2,3},{4,5},{5,6},{6,7},{8,9},{9,10},{10,11},{12,13},{... | collective-permute-start | bytes 98312 | tf_op jit(solution)/shard_map/ppermute | solution.py:16
  60.4 3.5 %collective-permute-start.11 = (f32[1,1,1,8,8,128]{5,4,3,2,1,0:T(8,128)S(1)}, f32[1,1,1,8,8,128]{5,4,3,2,1,0:T(8,128)S(1)}, u32[]{:S(2)}, u32[]{:S(2)}) collective-permute-start(f32[1,1,1,8,8,128]{5,4,3,2,1,0:T(8,128)S(1)} %get-tuple-element.47), channel_id=1, source_target_pairs={{1,0},{2,1},{3,2},{5,4},{6,5},{7,6},{9,8},{10,9},{11,10},{13,12},{... | collective-permute-start | bytes 98312 | tf_op jit(solution)/shard_map/ppermute | solution.py:19
  66.1 9.1 %collective-permute-start.12 = (f32[1,1,1,8,8,128]{5,4,3,2,1,0:T(8,128)S(1)}, f32[1,1,1,8,8,128]{5,4,3,2,1,0:T(8,128)S(1)}, u32[]{:S(2)}, u32[]{:S(2)}) collective-permute-start(f32[1,1,1,8,8,128]{5,4,3,2,1,0:T(8,128)S(1)} %get-tuple-element.73), channel_id=1, source_target_pairs={{0,4},{4,8},{8,12},{12,16},{16,20},{20,24},{24,28},{1,5},{5,9},{9,... | collective-permute-start | bytes 98312 | tf_op jit(solution)/shard_map/ppermute | solution.py:16
  70.4 5.8 %collective-permute-start.13 = (f32[1,1,1,8,8,128]{5,4,3,2,1,0:T(8,128)S(1)}, f32[1,1,1,8,8,128]{5,4,3,2,1,0:T(8,128)S(1)}, u32[]{:S(2)}, u32[]{:S(2)}) collective-permute-start(f32[1,1,1,8,8,128]{5,4,3,2,1,0:T(8,128)S(1)} %get-tuple-element.74), channel_id=1, source_target_pairs={{4,0},{8,4},{12,8},{16,12},{20,16},{24,20},{28,24},{5,1},{9,5},{13... | collective-permute-start | bytes 98312 | tf_op jit(solution)/shard_map/ppermute | solution.py:19
  76.3 5.2 %collective-permute-start.14 = (f32[1,1,1,8,8,128]{5,4,3,2,1,0:T(8,128)S(1)}, f32[1,1,1,8,8,128]{5,4,3,2,1,0:T(8,128)S(1)}, u32[]{:S(2)}, u32[]{:S(2)}) collective-permute-start(f32[1,1,1,8,8,128]{5,4,3,2,1,0:T(8,128)S(1)} %maximum_bitcast_fusion.11), channel_id=1, source_target_pairs={{0,1},{1,2},{2,3},{4,5},{5,6},{6,7},{8,9},{9,10},{10,11},{12,13},{... | collective-permute-start | bytes 98312 | tf_op jit(solution)/shard_map/ppermute | solution.py:16
  81.5 3.5 %collective-permute-start.15 = (f32[1,1,1,8,8,128]{5,4,3,2,1,0:T(8,128)S(1)}, f32[1,1,1,8,8,128]{5,4,3,2,1,0:T(8,128)S(1)}, u32[]{:S(2)}, u32[]{:S(2)}) collective-permute-start(f32[1,1,1,8,8,128]{5,4,3,2,1,0:T(8,128)S(1)} %get-tuple-element.41), channel_id=1, source_target_pairs={{1,0},{2,1},{3,2},{5,4},{6,5},{7,6},{9,8},{10,9},{11,10},{13,12},{... | collective-permute-start | bytes 98312 | tf_op jit(solution)/shard_map/ppermute | solution.py:19
  92.4 19.6 %all-to-all-start = ((f32[32,2,2048]{2,1,0:T(2,128)}), f32[32,2,2048]{2,1,0:T(2,128)S(1)}, u32[]{:S(2)}, u32[]{:S(2)}) async-start(f32[32,2,2048]{2,1,0:T(2,128)} %bitcast.107), calls=%async_computation | async-start | bytes 1048576 | tf_op jit(solution)/shard_map/all_to_all | solution.py:185
  98.3 5.1 %collective-permute-start.16 = (f32[1,1,1,8,8,128]{5,4,3,2,1,0:T(8,128)S(1)}, f32[1,1,1,8,8,128]{5,4,3,2,1,0:T(8,128)S(1)}, u32[]{:S(2)}, u32[]{:S(2)}) collective-permute-start(f32[1,1,1,8,8,128]{5,4,3,2,1,0:T(8,128)S(1)} %get-tuple-element.66), channel_id=1, source_target_pairs={{0,4},{4,8},{8,12},{12,16},{16,20},{20,24},{24,28},{1,5},{5,9},{9,... | collective-permute-start | bytes 98312 | tf_op jit(solution)/shard_map/ppermute | solution.py:16
  101.6 6.2 %collective-permute-start.17 = (f32[1,1,1,8,8,128]{5,4,3,2,1,0:T(8,128)S(1)}, f32[1,1,1,8,8,128]{5,4,3,2,1,0:T(8,128)S(1)}, u32[]{:S(2)}, u32[]{:S(2)}) collective-permute-start(f32[1,1,1,8,8,128]{5,4,3,2,1,0:T(8,128)S(1)} %get-tuple-element.67), channel_id=1, source_target_pairs={{4,0},{8,4},{12,8},{16,12},{20,16},{24,20},{28,24},{5,1},{9,5},{13... | collective-permute-start | bytes 98312 | tf_op jit(solution)/shard_map/ppermute | solution.py:19
  112.9 9.1 %collective-permute-start.18 = (f32[1,1,1,8,8,128]{5,3,4,2,1,0:T(8,128)S(1)}, f32[1,1,1,8,8,128]{5,3,4,2,1,0:T(8,128)S(1)}, u32[]{:S(2)}, u32[]{:S(2)}) collective-permute-start(f32[1,1,1,8,8,128]{5,3,4,2,1,0:T(8,128)S(1)} %get-tuple-element.93), channel_id=1, source_target_pairs={{0,1},{1,2},{2,3},{4,5},{5,6},{6,7},{8,9},{9,10},{10,11},{12,13},{... | collective-permute-start | bytes 98312 | tf_op jit(solution)/shard_map/ppermute | solution.py:16
  114.9 7.1 %collective-permute-start.19 = (f32[1,1,1,8,8,128]{5,3,4,2,1,0:T(8,128)S(1)}, f32[1,1,1,8,8,128]{5,3,4,2,1,0:T(8,128)S(1)}, u32[]{:S(2)}, u32[]{:S(2)}) collective-permute-start(f32[1,1,1,8,8,128]{5,3,4,2,1,0:T(8,128)S(1)} %get-tuple-element.94), channel_id=1, source_target_pairs={{1,0},{2,1},{3,2},{5,4},{6,5},{7,6},{9,8},{10,9},{11,10},{13,12},{... | collective-permute-start | bytes 98312 | tf_op jit(solution)/shard_map/ppermute | solution.py:19
  118.6 10.8 %all-to-all-start.1 = ((f32[8,2,2048]{2,1,0:T(2,128)}), f32[8,2,2048]{2,1,0:T(2,128)S(1)}, u32[]{:S(2)}, u32[]{:S(2)}) async-start(f32[8,2,2048]{2,1,0:T(2,128)} %broadcast_in_dim.200), calls=%async_computation.1 | async-start | bytes 262144 | tf_op jit(solution)/shard_map/all_to_all | solution.py:194

commit v24 on v23

--- a/solution.py
+++ b/solution.py
@@ -231,11 +231,11 @@
         else:
             if step + 2 == SWEEPS:
                 assembled, early = assemble(applied[None], early)
+            elif step == 0:
+                assembled, denom = assemble(applied[None], denom)
             else:
                 assembled, _ = assemble(applied[None])
         assembled = assembled[0]
-        if step == 0:
-            assembled, denom = lax.optimization_barrier((assembled, denom))
         resid = resid - assembled
         if step + 1 < SWEEPS:
             rho_new = 1.0 / (2.0 * sigma - rho_now)

time: 131 us -> 134 us (1.023)
  other arithmetic: 12 us -> 14.5 us
  waiting for transfers between devices: 40.7 us -> 42.2 us
    ppermute x10, waiting for transfers between devices: 8.46 us -> 10.7 us  [padded_2(): lax.ppermute(lax.slice_in_dim(block, block.shape[dim] - width, None, axis...]
  transfers between devices with their start and end apart: 22 -> 22, of which waited for: 16 -> 15; matrix products, arithmetic and copies ran while one was open for 9% -> 9% of each run, Pallas kernels for 0% -> 0%
where the time goes in v24:
time: 134 us; the launch traced here: 133 us
  starting transfers between devices  56.1 us (42%)
  waiting for transfers between devices  42.2 us (31%)
  other arithmetic  14.5 us (11%)
  matrix products  11.9 us (9%)
  local copies, waits for them, and re-layouts  6.95 us (5%)
  between operations  1.65 us (1%)
    ppermute x10, starting transfers between devices, padded_2(): lax.ppermute(lax.slice_in_dim(block, block.shape[dim] - width, None, axis...  28.5 us
    ppermute x10, waiting for transfers between devices, padded_2(): lax.ppermute(lax.slice_in_dim(block, 0, width, axis=dim), axis, backward)  21.3 us
    ppermute x10, starting transfers between devices, padded_2(): lax.ppermute(lax.slice_in_dim(block, 0, width, axis=dim), axis, backward)  19.6 us
    ppermute x10, waiting for transfers between devices, padded_2(): lax.ppermute(lax.slice_in_dim(block, block.shape[dim] - width, None, axis...  10.7 us
    all_to_all x1, waiting for transfers between devices, strip_gather(): whole = lax.all_to_all(spread_out, 'ex', 0, 0, tiled=True)  6.13 us
    all_to_all x1, starting transfers between devices, strip_reduce(): return lax.all_to_all(chunks, ('ex', 'ey'), 0, 0, tiled=True).sum(0)  4.52 us
    all_to_all x1, waiting for transfers between devices, strip_reduce(): return lax.all_to_all(chunks, ('ex', 'ey'), 0, 0, tiled=True).sum(0)  4.06 us
    all_to_all x1, starting transfers between devices, strip_gather(): whole = lax.all_to_all(spread_out, 'ex', 0, 0, tiled=True)  3.46 us
  transfers between devices with their start and end apart: 22, of which 15 were waited for; matrix products, arithmetic and copies ran while one was open for 9% of the time, Pallas kernels for 0%

profile of v24, /device:TPU:2, one launch (start us, length us, event | category | flops | bytes accessed | tf_op | source)
XLA Modules:
  0.0 133.3 jit_solution(9684725727861735802)
XLA Ops:
  4.4 1.2 fusion.89
  6.4 3.4 %collective-permute-start = (f32[2,1,1,8,8,128]{5,0,4,3,2,1:T(2,128)S(1)}, f32[2,1,1,8,8,128]{5,0,4,3,2,1:T(2,128)S(1)}, u32[]{:S(2)}, u32[]{:S(2)}) collective-permute-start(f32[2,1,1,8,8,128]{5,0,4,3,2,1:T(2,128)S(1)} %pad_maximum_fusion.8), channel_id=1, source_target_pairs={{0,4},{4,8},{8,12},{12,16},{16,20},{20,24},{24,28},{1,5},{5,9},{9,... | collective-permute-start | bytes 196616 | tf_op jit(solution)/shard_map/ppermute | solution.py:16
  9.9 1.3 collective-permute-start.1
  12.0 1.1 copy.307
  13.2 2.9 %collective-permute-done.1 = f32[2,1,1,8,8,128]{5,0,4,3,2,1:T(2,128)S(1)} collective-permute-done((f32[2,1,1,8,8,128]{5,0,4,3,2,1:T(2,128)S(1)}, f32[2,1,1,8,8,128]{5,0,4,3,2,1:T(2,128)S(1)}, u32[]{:S(2)}, u32[]{:S(2)}) %collective-permute-start.1) | collective-permute-done | bytes 65568 | tf_op jit(solution)/shard_map/ppermute | solution.py:19
  17.3 1.9 %collective-permute-start.2 = (f32[2,1,1,8,8,128]{5,3,0,4,2,1:T(8,128)S(1)}, f32[2,1,1,8,8,128]{5,3,0,4,2,1:T(8,128)S(1)}, u32[]{:S(2)}, u32[]{:S(2)}) collective-permute-start(f32[2,1,1,8,8,128]{5,3,0,4,2,1:T(8,128)S(1)} %get-tuple-element.53), channel_id=1, source_target_pairs={{0,1},{1,2},{2,3},{4,5},{5,6},{6,7},{8,9},{9,10},{10,11},{12,13},{... | collective-permute-start | bytes 196616 | tf_op jit(solution)/shard_map/ppermute | solution.py:16
  19.2 3.6 %collective-permute-start.3 = (f32[2,1,1,8,8,128]{5,3,0,4,2,1:T(8,128)S(1)}, f32[2,1,1,8,8,128]{5,3,0,4,2,1:T(8,128)S(1)}, u32[]{:S(2)}, u32[]{:S(2)}) collective-permute-start(f32[2,1,1,8,8,128]{5,3,0,4,2,1:T(8,128)S(1)} %get-tuple-element.54), channel_id=1, source_target_pairs={{1,0},{2,1},{3,2},{5,4},{6,5},{7,6},{9,8},{10,9},{11,10},{13,12},{... | collective-permute-start | bytes 196616 | tf_op jit(solution)/shard_map/ppermute | solution.py:19
  22.9 1.2 fusion.20
  24.1 1.9 %fusion = f32[768,256]{1,0:T(8,128)S(1)} fusion(bf16[256,4096]{1,0:T(8,128)(2,1)S(1)} %get-tuple-element.101, bf16[256,4096]{1,0:T(8,128)(2,1)S(1)} %get-tuple-element.102, bf16[256,4096]{1,0:T(8,128)(2,1)S(1)} %get-tuple-element.100, s32[4096]{0:T(1024)S(1)} %get-tuple-element.96), kind=kOutput, calls=%fused_computation | convolution fusion | flops 1630535680 | bytes 7094272 | tf_op jit(solution)/shard_map/dot_general | solution.py:170
  28.7 4.3 %collective-permute-start.4 = (f32[1,1,1,8,8,128]{5,4,3,2,1,0:T(8,128)S(1)}, f32[1,1,1,8,8,128]{5,4,3,2,1,0:T(8,128)S(1)}, u32[]{:S(2)}, u32[]{:S(2)}) collective-permute-start(f32[1,1,1,8,8,128]{5,4,3,2,1,0:T(8,128)S(1)} %get-tuple-element.84), channel_id=1, source_target_pairs={{0,4},{4,8},{8,12},{12,16},{16,20},{20,24},{24,28},{1,5},{5,9},{9,... | collective-permute-start | bytes 98312 | tf_op jit(solution)/shard_map/ppermute | solution.py:16
  33.0 1.3 collective-permute-start.5
  34.6 4.2 %collective-permute-done.5 = f32[1,1,1,8,8,128]{5,4,3,2,1,0:T(8,128)S(1)} collective-permute-done((f32[1,1,1,8,8,128]{5,4,3,2,1,0:T(8,128)S(1)}, f32[1,1,1,8,8,128]{5,4,3,2,1,0:T(8,128)S(1)}, u32[]{:S(2)}, u32[]{:S(2)}) %collective-permute-start.5) | collective-permute-done | bytes 32800 | tf_op jit(solution)/shard_map/ppermute | solution.py:19
  38.8 1.9 %collective-permute-start.6 = (f32[1,1,1,8,8,128]{5,4,3,2,1,0:T(8,128)S(1)}, f32[1,1,1,8,8,128]{5,4,3,2,1,0:T(8,128)S(1)}, u32[]{:S(2)}, u32[]{:S(2)}) collective-permute-start(f32[1,1,1,8,8,128]{5,4,3,2,1,0:T(8,128)S(1)} %maximum_bitcast_fusion.9), channel_id=1, source_target_pairs={{0,1},{1,2},{2,3},{4,5},{5,6},{6,7},{8,9},{9,10},{10,11},{12,13},{... | collective-permute-start | bytes 98312 | tf_op jit(solution)/shard_map/ppermute | solution.py:16
  40.8 3.3 %collective-permute-done.6 = f32[1,1,1,8,8,128]{5,4,3,2,1,0:T(8,128)S(1)} collective-permute-done((f32[1,1,1,8,8,128]{5,4,3,2,1,0:T(8,128)S(1)}, f32[1,1,1,8,8,128]{5,4,3,2,1,0:T(8,128)S(1)}, u32[]{:S(2)}, u32[]{:S(2)}) %collective-permute-start.6) | collective-permute-done | bytes 32800 | tf_op jit(solution)/shard_map/ppermute | solution.py:16
  44.1 1.9 %collective-permute-start.7 = (f32[1,1,1,8,8,128]{5,4,3,2,1,0:T(8,128)S(1)}, f32[1,1,1,8,8,128]{5,4,3,2,1,0:T(8,128)S(1)}, u32[]{:S(2)}, u32[]{:S(2)}) collective-permute-start(f32[1,1,1,8,8,128]{5,4,3,2,1,0:T(8,128)S(1)} %get-tuple-element.48), channel_id=1, source_target_pairs={{1,0},{2,1},{3,2},{5,4},{6,5},{7,6},{9,8},{10,9},{11,10},{13,12},{... | collective-permute-start | bytes 98312 | tf_op jit(solution)/shard_map/ppermute | solution.py:19
  46.0 1.6 %collective-permute-done.7 = f32[1,1,1,8,8,128]{5,4,3,2,1,0:T(8,128)S(1)} collective-permute-done((f32[1,1,1,8,8,128]{5,4,3,2,1,0:T(8,128)S(1)}, f32[1,1,1,8,8,128]{5,4,3,2,1,0:T(8,128)S(1)}, u32[]{:S(2)}, u32[]{:S(2)}) %collective-permute-start.7) | collective-permute-done | bytes 32800 | tf_op jit(solution)/shard_map/ppermute | solution.py:19
  49.4 3.4 %collective-permute-start.8 = (f32[1,1,1,8,8,128]{5,4,3,2,1,0:T(8,128)S(1)}, f32[1,1,1,8,8,128]{5,4,3,2,1,0:T(8,128)S(1)}, u32[]{:S(2)}, u32[]{:S(2)}) collective-permute-start(f32[1,1,1,8,8,128]{5,4,3,2,1,0:T(8,128)S(1)} %get-tuple-element.80), channel_id=1, source_target_pairs={{0,4},{4,8},{8,12},{12,16},{16,20},{20,24},{24,28},{1,5},{5,9},{9,... | collective-permute-start | bytes 98312 | tf_op jit(solution)/shard_map/ppermute | solution.py:16
  52.8 1.3 collective-permute-start.9
  54.4 4.2 %collective-permute-done.9 = f32[1,1,1,8,8,128]{5,4,3,2,1,0:T(8,128)S(1)} collective-permute-done((f32[1,1,1,8,8,128]{5,4,3,2,1,0:T(8,128)S(1)}, f32[1,1,1,8,8,128]{5,4,3,2,1,0:T(8,128)S(1)}, u32[]{:S(2)}, u32[]{:S(2)}) %collective-permute-start.9) | collective-permute-done | bytes 32800 | tf_op jit(solution)/shard_map/ppermute | solution.py:19
  58.6 1.9 %collective-permute-start.10 = (f32[1,1,1,8,8,128]{5,4,3,2,1,0:T(8,128)S(1)}, f32[1,1,1,8,8,128]{5,4,3,2,1,0:T(8,128)S(1)}, u32[]{:S(2)}, u32[]{:S(2)}) collective-permute-start(f32[1,1,1,8,8,128]{5,4,3,2,1,0:T(8,128)S(1)} %maximum_bitcast_fusion.7), channel_id=1, source_target_pairs={{0,1},{1,2},{2,3},{4,5},{5,6},{6,7},{8,9},{9,10},{10,11},{12,13},{... | collective-permute-start | bytes 98312 | tf_op jit(solution)/shard_map/ppermute | solution.py:16
  60.6 3.2 %collective-permute-done.10 = f32[1,1,1,8,8,128]{5,4,3,2,1,0:T(8,128)S(1)} collective-permute-done((f32[1,1,1,8,8,128]{5,4,3,2,1,0:T(8,128)S(1)}, f32[1,1,1,8,8,128]{5,4,3,2,1,0:T(8,128)S(1)}, u32[]{:S(2)}, u32[]{:S(2)}) %collective-permute-start.10) | collective-permute-done | bytes 32800 | tf_op jit(solution)/shard_map/ppermute | solution.py:16
  63.9 1.9 %collective-permute-start.11 = (f32[1,1,1,8,8,128]{5,4,3,2,1,0:T(8,128)S(1)}, f32[1,1,1,8,8,128]{5,4,3,2,1,0:T(8,128)S(1)}, u32[]{:S(2)}, u32[]{:S(2)}) collective-permute-start(f32[1,1,1,8,8,128]{5,4,3,2,1,0:T(8,128)S(1)} %get-tuple-element.46), channel_id=1, source_target_pairs={{1,0},{2,1},{3,2},{5,4},{6,5},{7,6},{9,8},{10,9},{11,10},{13,12},{... | collective-permute-start | bytes 98312 | tf_op jit(solution)/shard_map/ppermute | solution.py:19
  65.9 1.5 %collective-permute-done.11 = f32[1,1,1,8,8,128]{5,4,3,2,1,0:T(8,128)S(1)} collective-permute-done((f32[1,1,1,8,8,128]{5,4,3,2,1,0:T(8,128)S(1)}, f32[1,1,1,8,8,128]{5,4,3,2,1,0:T(8,128)S(1)}, u32[]{:S(2)}, u32[]{:S(2)}) %collective-permute-start.11) | collective-permute-done | bytes 32800 | tf_op jit(solution)/shard_map/ppermute | solution.py:19
  69.5 4.3 %collective-permute-start.12 = (f32[1,1,1,8,8,128]{5,4,3,2,1,0:T(8,128)S(1)}, f32[1,1,1,8,8,128]{5,4,3,2,1,0:T(8,128)S(1)}, u32[]{:S(2)}, u32[]{:S(2)}) collective-permute-start(f32[1,1,1,8,8,128]{5,4,3,2,1,0:T(8,128)S(1)} %get-tuple-element.74), channel_id=1, source_target_pairs={{0,4},{4,8},{8,12},{12,16},{16,20},{20,24},{24,28},{1,5},{5,9},{9,... | collective-permute-start | bytes 98312 | tf_op jit(solution)/shard_map/ppermute | solution.py:16
  73.8 1.5 %collective-permute-start.13 = (f32[1,1,1,8,8,128]{5,4,3,2,1,0:T(8,128)S(1)}, f32[1,1,1,8,8,128]{5,4,3,2,1,0:T(8,128)S(1)}, u32[]{:S(2)}, u32[]{:S(2)}) collective-permute-start(f32[1,1,1,8,8,128]{5,4,3,2,1,0:T(8,128)S(1)} %get-tuple-element.75), channel_id=1, source_target_pairs={{4,0},{8,4},{12,8},{16,12},{20,16},{24,20},{28,24},{5,1},{9,5},{13... | collective-permute-start | bytes 98312 | tf_op jit(solution)/shard_map/ppermute | solution.py:19
  75.3 1.9 %fusion.15 = f32[768,4096]{1,0:T(8,128)S(1)} fusion(s32[4096]{0:T(1024)S(1)} %bitcast.476, bf16[256,256]{1,0:T(8,128)(2,1)S(1)} %get-tuple-element.72, bf16[256,256]{1,0:T(8,128)(2,1)S(1)} %get-tuple-element.73, bf16[256,256]{1,0:T(8,128)(2,1)S(1)} %get-tuple-element.71), kind=kOutput, calls=%fused_computation.19 | convolution fusion | flops 1612840960 | bytes 12992512 | tf_op jit(solution)/shard_map/dot_general | solution.py:156
  77.2 1.4 %fusion.9 = f32[4096]{0:T(1024)S(1)} fusion(f32[768,4096]{1,0:T(8,128)S(1)} %fusion.15, s32[4096]{0:T(1024)S(1)} %bitcast.474), kind=kLoop, calls=%fused_computation.11 | loop fusion | flops 5238784 | bytes 12615680 | tf_op jit(solution)/shard_map/reduce_sum | solution.py:161
  78.6 1.1 collective-permute-done.13
  79.7 1.9 %collective-permute-start.14 = (f32[1,1,1,8,8,128]{5,4,3,2,1,0:T(8,128)S(1)}, f32[1,1,1,8,8,128]{5,4,3,2,1,0:T(8,128)S(1)}, u32[]{:S(2)}, u32[]{:S(2)}) collective-permute-start(f32[1,1,1,8,8,128]{5,4,3,2,1,0:T(8,128)S(1)} %maximum_bitcast_fusion.5), channel_id=1, source_target_pairs={{0,1},{1,2},{2,3},{4,5},{5,6},{6,7},{8,9},{9,10},{10,11},{12,13},{... | collective-permute-start | bytes 98312 | tf_op jit(solution)/shard_map/ppermute | solution.py:16
  81.6 3.3 %collective-permute-done.14 = f32[1,1,1,8,8,128]{5,4,3,2,1,0:T(8,128)S(1)} collective-permute-done((f32[1,1,1,8,8,128]{5,4,3,2,1,0:T(8,128)S(1)}, f32[1,1,1,8,8,128]{5,4,3,2,1,0:T(8,128)S(1)}, u32[]{:S(2)}, u32[]{:S(2)}) %collective-permute-start.14) | collective-permute-done | bytes 32800 | tf_op jit(solution)/shard_map/ppermute | solution.py:16
  84.9 1.9 %collective-permute-start.15 = (f32[1,1,1,8,8,128]{5,4,3,2,1,0:T(8,128)S(1)}, f32[1,1,1,8,8,128]{5,4,3,2,1,0:T(8,128)S(1)}, u32[]{:S(2)}, u32[]{:S(2)}) collective-permute-start(f32[1,1,1,8,8,128]{5,4,3,2,1,0:T(8,128)S(1)} %get-tuple-element.39), channel_id=1, source_target_pairs={{1,0},{2,1},{3,2},{5,4},{6,5},{7,6},{9,8},{10,9},{11,10},{13,12},{... | collective-permute-start | bytes 98312 | tf_op jit(solution)/shard_map/ppermute | solution.py:19
  86.9 1.5 %collective-permute-done.15 = f32[1,1,1,8,8,128]{5,4,3,2,1,0:T(8,128)S(1)} collective-permute-done((f32[1,1,1,8,8,128]{5,4,3,2,1,0:T(8,128)S(1)}, f32[1,1,1,8,8,128]{5,4,3,2,1,0:T(8,128)S(1)}, u32[]{:S(2)}, u32[]{:S(2)}) %collective-permute-start.15) | collective-permute-done | bytes 32800 | tf_op jit(solution)/shard_map/ppermute | solution.py:19
  89.0 1.3 %fusion.14 = f32[512,4096]{1,0:T(8,128)S(1)} fusion(s32[4096]{0:T(1024)S(1)} %bitcast.477, bf16[256,256]{1,0:T(8,128)(2,1)S(1)} %get-tuple-element.66, bf16[256,256]{1,0:T(8,128)(2,1)S(1)} %get-tuple-element.65), kind=kOutput, calls=%fused_computation.18 | convolution fusion | flops 1075314688 | bytes 8667136 | tf_op jit(solution)/shard_map/dot_general | solution.py:156
  90.3 0.9 fusion.7
  91.3 0.9 fusion.17
  92.1 1.4 %fusion.10 = f32[512,256]{1,0:T(8,128)S(1)} fusion(bf16[256,4096]{1,0:T(8,128)(2,1)S(1)} %get-tuple-element.99, bf16[256,4096]{1,0:T(8,128)(2,1)S(1)} %get-tuple-element.98, s32[4096]{0:T(1024)S(1)} %get-tuple-element.96), kind=kOutput, calls=%fused_computation.13 | convolution fusion | flops 1083179008 | bytes 4734976 | tf_op jit(solution)/shard_map/dot_general | solution.py:170
  93.7 1.2 copy.257
  94.9 4.5 %all-to-all-start = ((f32[32,2,2048]{2,1,0:T(2,128)}), f32[32,2,2048]{2,1,0:T(2,128)S(1)}, u32[]{:S(2)}, u32[]{:S(2)}) async-start(f32[32,2,2048]{2,1,0:T(2,128)} %bitcast.111), calls=%async_computation | async-start | bytes 1048576 | tf_op jit(solution)/shard_map/all_to_all | solution.py:185
  100.9 3.4 %collective-permute-start.16 = (f32[1,1,1,8,8,128]{5,4,3,2,1,0:T(8,128)S(1)}, f32[1,1,1,8,8,128]{5,4,3,2,1,0:T(8,128)S(1)}, u32[]{:S(2)}, u32[]{:S(2)}) collective-permute-start(f32[1,1,1,8,8,128]{5,4,3,2,1,0:T(8,128)S(1)} %get-tuple-element.67), channel_id=1, source_target_pairs={{0,4},{4,8},{8,12},{12,16},{16,20},{20,24},{24,28},{1,5},{5,9},{9,... | collective-permute-start | bytes 98312 | tf_op jit(solution)/shard_map/ppermute | solution.py:16
  104.3 1.3 collective-permute-start.17
  106.1 4.3 %collective-permute-done.17 = f32[1,1,1,8,8,128]{5,4,3,2,1,0:T(8,128)S(1)} collective-permute-done((f32[1,1,1,8,8,128]{5,4,3,2,1,0:T(8,128)S(1)}, f32[1,1,1,8,8,128]{5,4,3,2,1,0:T(8,128)S(1)}, u32[]{:S(2)}, u32[]{:S(2)}) %collective-permute-start.17) | collective-permute-done | bytes 32800 | tf_op jit(solution)/shard_map/ppermute | solution.py:19
  110.4 4.1 %all-to-all-done = f32[32,2,2048]{2,1,0:T(2,128)S(1)} async-done(((f32[32,2,2048]{2,1,0:T(2,128)}), f32[32,2,2048]{2,1,0:T(2,128)S(1)}, u32[]{:S(2)}, u32[]{:S(2)}) %all-to-all-start) | async-done | bytes 524320 | tf_op jit(solution)/shard_map/all_to_all | solution.py:185
  115.4 1.9 %collective-permute-start.18 = (f32[1,1,1,8,8,128]{5,4,3,2,1,0:T(8,128)S(1)}, f32[1,1,1,8,8,128]{5,4,3,2,1,0:T(8,128)S(1)}, u32[]{:S(2)}, u32[]{:S(2)}) collective-permute-start(f32[1,1,1,8,8,128]{5,4,3,2,1,0:T(8,128)S(1)} %get-tuple-element.92), channel_id=1, source_target_pairs={{0,1},{1,2},{2,3},{4,5},{5,6},{6,7},{8,9},{9,10},{10,11},{12,13},{... | collective-permute-start | bytes 98312 | tf_op jit(solution)/shard_map/ppermute | solution.py:16
  117.4 0.8 fusion.71
  118.2 3.6 %collective-permute-start.19 = (f32[1,1,1,8,8,128]{5,4,3,2,1,0:T(8,128)S(1)}, f32[1,1,1,8,8,128]{5,4,3,2,1,0:T(8,128)S(1)}, u32[]{:S(2)}, u32[]{:S(2)}) collective-permute-start(f32[1,1,1,8,8,128]{5,4,3,2,1,0:T(8,128)S(1)} %get-tuple-element.93), channel_id=1, source_target_pairs={{1,0},{2,1},{3,2},{5,4},{6,5},{7,6},{9,8},{10,9},{11,10},{13,12},{... | collective-permute-start | bytes 98312 | tf_op jit(solution)/shard_map/ppermute | solution.py:19
  121.8 3.5 %all-to-all-start.1 = ((f32[8,2,2048]{2,1,0:T(2,128)}), f32[8,2,2048]{2,1,0:T(2,128)S(1)}, u32[]{:S(2)}, u32[]{:S(2)}) async-start(f32[8,2,2048]{2,1,0:T(2,128)} %broadcast_in_dim.200), calls=%async_computation.1 | async-start | bytes 262144 | tf_op jit(solution)/shard_map/all_to_all | solution.py:194
  125.6 0.9 fusion.69
  126.5 6.1 %all-to-all-done.1 = f32[8,2,2048]{2,1,0:T(2,128)S(1)} async-done(((f32[8,2,2048]{2,1,0:T(2,128)}), f32[8,2,2048]{2,1,0:T(2,128)S(1)}, u32[]{:S(2)}, u32[]{:S(2)}) %all-to-all-start.1) | async-done | bytes 131104 | tf_op jit(solution)/shard_map/all_to_all | solution.py:194
  (137 shorter events, 18.1 us)
Async XLA Ops:
  0.6 22.2 %copy-start.4 = (s32[1,4096]{1,0:T(1,128)S(1)}, s32[1,4096]{1,0:T(1,128)}, u32[]{:S(2)}) copy-start(s32[1,4096]{1,0:T(1,128)} %param.40) | copy-start | bytes 49156
  0.6 22.2 %copy-start.5 = (s32[1,4096,1]{1,2,0:T(1,128)S(1)}, s32[1,4096,1]{1,2,0:T(1,128)}, u32[]{:S(2)}) copy-start(s32[1,4096,1]{1,2,0:T(1,128)} %param.39) | copy-start | bytes 49156
  6.4 6.8 %collective-permute-start = (f32[2,1,1,8,8,128]{5,0,4,3,2,1:T(2,128)S(1)}, f32[2,1,1,8,8,128]{5,0,4,3,2,1:T(2,128)S(1)}, u32[]{:S(2)}, u32[]{:S(2)}) collective-permute-start(f32[2,1,1,8,8,128]{5,0,4,3,2,1:T(2,128)S(1)} %pad_maximum_fusion.8), channel_id=1, source_target_pairs={{0,4},{4,8},{8,12},{12,16},{16,20},{20,24},{24,28},{1,5},{5,9},{9,... | collective-permute-start | bytes 196616 | tf_op jit(solution)/shard_map/ppermute | solution.py:16
  9.9 6.2 %collective-permute-start.1 = (f32[2,1,1,8,8,128]{5,0,4,3,2,1:T(2,128)S(1)}, f32[2,1,1,8,8,128]{5,0,4,3,2,1:T(2,128)S(1)}, u32[]{:S(2)}, u32[]{:S(2)}) collective-permute-start(f32[2,1,1,8,8,128]{5,0,4,3,2,1:T(2,128)S(1)} %pad_maximum_fusion.7), channel_id=1, source_target_pairs={{4,0},{8,4},{12,8},{16,12},{20,16},{24,20},{28,24},{5,1},{9,5},{13... | collective-permute-start | bytes 196616 | tf_op jit(solution)/shard_map/ppermute | solution.py:19
  17.3 9.1 %collective-permute-start.2 = (f32[2,1,1,8,8,128]{5,3,0,4,2,1:T(8,128)S(1)}, f32[2,1,1,8,8,128]{5,3,0,4,2,1:T(8,128)S(1)}, u32[]{:S(2)}, u32[]{:S(2)}) collective-permute-start(f32[2,1,1,8,8,128]{5,3,0,4,2,1:T(8,128)S(1)} %get-tuple-element.53), channel_id=1, source_target_pairs={{0,1},{1,2},{2,3},{4,5},{5,6},{6,7},{8,9},{9,10},{10,11},{12,13},{... | collective-permute-start | bytes 196616 | tf_op jit(solution)/shard_map/ppermute | solution.py:16
  19.2 7.2 %collective-permute-start.3 = (f32[2,1,1,8,8,128]{5,3,0,4,2,1:T(8,128)S(1)}, f32[2,1,1,8,8,128]{5,3,0,4,2,1:T(8,128)S(1)}, u32[]{:S(2)}, u32[]{:S(2)}) collective-permute-start(f32[2,1,1,8,8,128]{5,3,0,4,2,1:T(8,128)S(1)} %get-tuple-element.54), channel_id=1, source_target_pairs={{1,0},{2,1},{3,2},{5,4},{6,5},{7,6},{9,8},{10,9},{11,10},{13,12},{... | collective-permute-start | bytes 196616 | tf_op jit(solution)/shard_map/ppermute | solution.py:19
  26.1 1.2 copy-start
  26.1 2.1 %copy-start.3 = (f32[8]{0:T(128)S(1)}, f32[8]{0:T(128)}, u32[]{:S(2)}) copy-start(f32[8]{0:T(128)} %constant.125) | copy-start | bytes 100
  28.7 5.9 %collective-permute-start.4 = (f32[1,1,1,8,8,128]{5,4,3,2,1,0:T(8,128)S(1)}, f32[1,1,1,8,8,128]{5,4,3,2,1,0:T(8,128)S(1)}, u32[]{:S(2)}, u32[]{:S(2)}) collective-permute-start(f32[1,1,1,8,8,128]{5,4,3,2,1,0:T(8,128)S(1)} %get-tuple-element.84), channel_id=1, source_target_pairs={{0,4},{4,8},{8,12},{12,16},{16,20},{20,24},{24,28},{1,5},{5,9},{9,... | collective-permute-start | bytes 98312 | tf_op jit(solution)/shard_map/ppermute | solution.py:16
  33.0 5.8 %collective-permute-start.5 = (f32[1,1,1,8,8,128]{5,4,3,2,1,0:T(8,128)S(1)}, f32[1,1,1,8,8,128]{5,4,3,2,1,0:T(8,128)S(1)}, u32[]{:S(2)}, u32[]{:S(2)}) collective-permute-start(f32[1,1,1,8,8,128]{5,4,3,2,1,0:T(8,128)S(1)} %get-tuple-element.85), channel_id=1, source_target_pairs={{4,0},{8,4},{12,8},{16,12},{20,16},{24,20},{28,24},{5,1},{9,5},{13... | collective-permute-start | bytes 98312 | tf_op jit(solution)/shard_map/ppermute | solution.py:19
  34.3 26.2 %copy-start.1 = (s32[1,4096]{1,0:T(1,128)S(1)}, s32[1,4096]{1,0:T(1,128)}, u32[]{:S(2)}) copy-start(s32[1,4096]{1,0:T(1,128)} %param.38) | copy-start | bytes 49156
  38.8 5.2 %collective-permute-start.6 = (f32[1,1,1,8,8,128]{5,4,3,2,1,0:T(8,128)S(1)}, f32[1,1,1,8,8,128]{5,4,3,2,1,0:T(8,128)S(1)}, u32[]{:S(2)}, u32[]{:S(2)}) collective-permute-start(f32[1,1,1,8,8,128]{5,4,3,2,1,0:T(8,128)S(1)} %maximum_bitcast_fusion.9), channel_id=1, source_target_pairs={{0,1},{1,2},{2,3},{4,5},{5,6},{6,7},{8,9},{9,10},{10,11},{12,13},{... | collective-permute-start | bytes 98312 | tf_op jit(solution)/shard_map/ppermute | solution.py:16
  44.1 3.5 %collective-permute-start.7 = (f32[1,1,1,8,8,128]{5,4,3,2,1,0:T(8,128)S(1)}, f32[1,1,1,8,8,128]{5,4,3,2,1,0:T(8,128)S(1)}, u32[]{:S(2)}, u32[]{:S(2)}) collective-permute-start(f32[1,1,1,8,8,128]{5,4,3,2,1,0:T(8,128)S(1)} %get-tuple-element.48), channel_id=1, source_target_pairs={{1,0},{2,1},{3,2},{5,4},{6,5},{7,6},{9,8},{10,9},{11,10},{13,12},{... | collective-permute-start | bytes 98312 | tf_op jit(solution)/shard_map/ppermute | solution.py:19
  49.4 5.0 %collective-permute-start.8 = (f32[1,1,1,8,8,128]{5,4,3,2,1,0:T(8,128)S(1)}, f32[1,1,1,8,8,128]{5,4,3,2,1,0:T(8,128)S(1)}, u32[]{:S(2)}, u32[]{:S(2)}) collective-permute-start(f32[1,1,1,8,8,128]{5,4,3,2,1,0:T(8,128)S(1)} %get-tuple-element.80), channel_id=1, source_target_pairs={{0,4},{4,8},{8,12},{12,16},{16,20},{20,24},{24,28},{1,5},{5,9},{9,... | collective-permute-start | bytes 98312 | tf_op jit(solution)/shard_map/ppermute | solution.py:16
  52.8 5.8 %collective-permute-start.9 = (f32[1,1,1,8,8,128]{5,4,3,2,1,0:T(8,128)S(1)}, f32[1,1,1,8,8,128]{5,4,3,2,1,0:T(8,128)S(1)}, u32[]{:S(2)}, u32[]{:S(2)}) collective-permute-start(f32[1,1,1,8,8,128]{5,4,3,2,1,0:T(8,128)S(1)} %get-tuple-element.81), channel_id=1, source_target_pairs={{4,0},{8,4},{12,8},{16,12},{20,16},{24,20},{28,24},{5,1},{9,5},{13... | collective-permute-start | bytes 98312 | tf_op jit(solution)/shard_map/ppermute | solution.py:19
  58.6 5.2 %collective-permute-start.10 = (f32[1,1,1,8,8,128]{5,4,3,2,1,0:T(8,128)S(1)}, f32[1,1,1,8,8,128]{5,4,3,2,1,0:T(8,128)S(1)}, u32[]{:S(2)}, u32[]{:S(2)}) collective-permute-start(f32[1,1,1,8,8,128]{5,4,3,2,1,0:T(8,128)S(1)} %maximum_bitcast_fusion.7), channel_id=1, source_target_pairs={{0,1},{1,2},{2,3},{4,5},{5,6},{6,7},{8,9},{9,10},{10,11},{12,13},{... | collective-permute-start | bytes 98312 | tf_op jit(solution)/shard_map/ppermute | solution.py:16
  63.9 3.5 %collective-permute-start.11 = (f32[1,1,1,8,8,128]{5,4,3,2,1,0:T(8,128)S(1)}, f32[1,1,1,8,8,128]{5,4,3,2,1,0:T(8,128)S(1)}, u32[]{:S(2)}, u32[]{:S(2)}) collective-permute-start(f32[1,1,1,8,8,128]{5,4,3,2,1,0:T(8,128)S(1)} %get-tuple-element.46), channel_id=1, source_target_pairs={{1,0},{2,1},{3,2},{5,4},{6,5},{7,6},{9,8},{10,9},{11,10},{13,12},{... | collective-permute-start | bytes 98312 | tf_op jit(solution)/shard_map/ppermute | solution.py:19
  69.5 9.1 %collective-permute-start.12 = (f32[1,1,1,8,8,128]{5,4,3,2,1,0:T(8,128)S(1)}, f32[1,1,1,8,8,128]{5,4,3,2,1,0:T(8,128)S(1)}, u32[]{:S(2)}, u32[]{:S(2)}) collective-permute-start(f32[1,1,1,8,8,128]{5,4,3,2,1,0:T(8,128)S(1)} %get-tuple-element.74), channel_id=1, source_target_pairs={{0,4},{4,8},{8,12},{12,16},{16,20},{20,24},{24,28},{1,5},{5,9},{9,... | collective-permute-start | bytes 98312 | tf_op jit(solution)/shard_map/ppermute | solution.py:16
  73.8 5.8 %collective-permute-start.13 = (f32[1,1,1,8,8,128]{5,4,3,2,1,0:T(8,128)S(1)}, f32[1,1,1,8,8,128]{5,4,3,2,1,0:T(8,128)S(1)}, u32[]{:S(2)}, u32[]{:S(2)}) collective-permute-start(f32[1,1,1,8,8,128]{5,4,3,2,1,0:T(8,128)S(1)} %get-tuple-element.75), channel_id=1, source_target_pairs={{4,0},{8,4},{12,8},{16,12},{20,16},{24,20},{28,24},{5,1},{9,5},{13... | collective-permute-start | bytes 98312 | tf_op jit(solution)/shard_map/ppermute | solution.py:19
  79.7 5.2 %collective-permute-start.14 = (f32[1,1,1,8,8,128]{5,4,3,2,1,0:T(8,128)S(1)}, f32[1,1,1,8,8,128]{5,4,3,2,1,0:T(8,128)S(1)}, u32[]{:S(2)}, u32[]{:S(2)}) collective-permute-start(f32[1,1,1,8,8,128]{5,4,3,2,1,0:T(8,128)S(1)} %maximum_bitcast_fusion.5), channel_id=1, source_target_pairs={{0,1},{1,2},{2,3},{4,5},{5,6},{6,7},{8,9},{9,10},{10,11},{12,13},{... | collective-permute-start | bytes 98312 | tf_op jit(solution)/shard_map/ppermute | solution.py:16
  84.9 3.5 %collective-permute-start.15 = (f32[1,1,1,8,8,128]{5,4,3,2,1,0:T(8,128)S(1)}, f32[1,1,1,8,8,128]{5,4,3,2,1,0:T(8,128)S(1)}, u32[]{:S(2)}, u32[]{:S(2)}) collective-permute-start(f32[1,1,1,8,8,128]{5,4,3,2,1,0:T(8,128)S(1)} %get-tuple-element.39), channel_id=1, source_target_pairs={{1,0},{2,1},{3,2},{5,4},{6,5},{7,6},{9,8},{10,9},{11,10},{13,12},{... | collective-permute-start | bytes 98312 | tf_op jit(solution)/shard_map/ppermute | solution.py:19
  90.3 0.9 copy-start.2
  94.9 19.6 %all-to-all-start = ((f32[32,2,2048]{2,1,0:T(2,128)}), f32[32,2,2048]{2,1,0:T(2,128)S(1)}, u32[]{:S(2)}, u32[]{:S(2)}) async-start(f32[32,2,2048]{2,1,0:T(2,128)} %bitcast.111), calls=%async_computation | async-start | bytes 1048576 | tf_op jit(solution)/shard_map/all_to_all | solution.py:185
  100.9 5.2 %collective-permute-start.16 = (f32[1,1,1,8,8,128]{5,4,3,2,1,0:T(8,128)S(1)}, f32[1,1,1,8,8,128]{5,4,3,2,1,0:T(8,128)S(1)}, u32[]{:S(2)}, u32[]{:S(2)}) collective-permute-start(f32[1,1,1,8,8,128]{5,4,3,2,1,0:T(8,128)S(1)} %get-tuple-element.67), channel_id=1, source_target_pairs={{0,4},{4,8},{8,12},{12,16},{16,20},{20,24},{24,28},{1,5},{5,9},{9,... | collective-permute-start | bytes 98312 | tf_op jit(solution)/shard_map/ppermute | solution.py:16
  104.3 6.2 %collective-permute-start.17 = (f32[1,1,1,8,8,128]{5,4,3,2,1,0:T(8,128)S(1)}, f32[1,1,1,8,8,128]{5,4,3,2,1,0:T(8,128)S(1)}, u32[]{:S(2)}, u32[]{:S(2)}) collective-permute-start(f32[1,1,1,8,8,128]{5,4,3,2,1,0:T(8,128)S(1)} %get-tuple-element.68), channel_id=1, source_target_pairs={{4,0},{8,4},{12,8},{16,12},{20,16},{24,20},{28,24},{5,1},{9,5},{13... | collective-permute-start | bytes 98312 | tf_op jit(solution)/shard_map/ppermute | solution.py:19
  115.4 9.8 %collective-permute-start.18 = (f32[1,1,1,8,8,128]{5,4,3,2,1,0:T(8,128)S(1)}, f32[1,1,1,8,8,128]{5,4,3,2,1,0:T(8,128)S(1)}, u32[]{:S(2)}, u32[]{:S(2)}) collective-permute-start(f32[1,1,1,8,8,128]{5,4,3,2,1,0:T(8,128)S(1)} %get-tuple-element.92), channel_id=1, source_target_pairs={{0,1},{1,2},{2,3},{4,5},{5,6},{6,7},{8,9},{9,10},{10,11},{12,13},{... | collective-permute-start | bytes 98312 | tf_op jit(solution)/shard_map/ppermute | solution.py:16
  118.2 7.1 %collective-permute-start.19 = (f32[1,1,1,8,8,128]{5,4,3,2,1,0:T(8,128)S(1)}, f32[1,1,1,8,8,128]{5,4,3,2,1,0:T(8,128)S(1)}, u32[]{:S(2)}, u32[]{:S(2)}) collective-permute-start(f32[1,1,1,8,8,128]{5,4,3,2,1,0:T(8,128)S(1)} %get-tuple-element.93), channel_id=1, source_target_pairs={{1,0},{2,1},{3,2},{5,4},{6,5},{7,6},{9,8},{10,9},{11,10},{13,12},{... | collective-permute-start | bytes 98312 | tf_op jit(solution)/shard_map/ppermute | solution.py:19
  121.8 10.8 %all-to-all-start.1 = ((f32[8,2,2048]{2,1,0:T(2,128)}), f32[8,2,2048]{2,1,0:T(2,128)S(1)}, u32[]{:S(2)}, u32[]{:S(2)}) async-start(f32[8,2,2048]{2,1,0:T(2,128)} %broadcast_in_dim.200), calls=%async_computation.1 | async-start | bytes 262144 | tf_op jit(solution)/shard_map/all_to_all | solution.py:194

commit v25 on v23

--- a/solution.py
+++ b/solution.py
@@ -217,11 +217,11 @@
     areas, strip_of, shell_of = shell_inputs
     strips = lax.axis_size("ey")
     global_ids = strip_of * SHELL_STRIP + shell_of
-    denom = segment_sum(areas, global_ids, strips * SHELL_STRIP, 256)
+    denom = segment_sum(areas, global_ids, strips * SHELL_STRIP, 256, 2)
     for step in range(SWEEPS):
         pressure = pressure + update
         if step + 2 == SWEEPS:
-            early = gather_flat(pressure.reshape(-1), picks, 256)
+            early = gather_flat(pressure.reshape(-1), picks, 256, 2)
         applied = element_apply(update, metric, weights, stiff)
         if step + 1 == SWEEPS:
             samples = early + gather_flat(update.reshape(-1), picks, 256, 2)

time: 131 us -> 131 us (level)
  waiting for transfers between devices: 40.7 us -> 42.5 us
    ppermute x10, waiting for transfers between devices: 21.8 us -> 23.2 us  [padded_2(): lax.ppermute(lax.slice_in_dim(block, 0, width, axis=dim), axis, backward)]
  transfers between devices with their start and end apart: 22 -> 22, of which waited for: 16 -> 16; matrix products, arithmetic and copies ran while one was open for 9% -> 7% of each run, Pallas kernels for 0% -> 0%
where the time goes in v25:
time: 131 us; the launch traced here: 130 us
  starting transfers between devices  56 us (43%)
  waiting for transfers between devices  42.5 us (32%)
  other arithmetic  11.2 us (9%)
  matrix products  11 us (8%)
  local copies, waits for them, and re-layouts  7.15 us (5%)
  between operations  1.68 us (1%)
    ppermute x10, starting transfers between devices, padded_2(): lax.ppermute(lax.slice_in_dim(block, block.shape[dim] - width, None, axis...  28.5 us
    ppermute x10, waiting for transfers between devices, padded_2(): lax.ppermute(lax.slice_in_dim(block, 0, width, axis=dim), axis, backward)  23.2 us
    ppermute x10, starting transfers between devices, padded_2(): lax.ppermute(lax.slice_in_dim(block, 0, width, axis=dim), axis, backward)  19.7 us
    ppermute x10, waiting for transfers between devices, padded_2(): lax.ppermute(lax.slice_in_dim(block, block.shape[dim] - width, None, axis...  8.96 us
    all_to_all x1, waiting for transfers between devices, strip_gather(): whole = lax.all_to_all(spread_out, 'ex', 0, 0, tiled=True)  6.31 us
    all_to_all x1, starting transfers between devices, strip_reduce(): return lax.all_to_all(chunks, ('ex', 'ey'), 0, 0, tiled=True).sum(0)  4.38 us
    all_to_all x1, waiting for transfers between devices, strip_reduce(): return lax.all_to_all(chunks, ('ex', 'ey'), 0, 0, tiled=True).sum(0)  4.09 us
    all_to_all x1, starting transfers between devices, strip_gather(): whole = lax.all_to_all(spread_out, 'ex', 0, 0, tiled=True)  3.46 us
  transfers between devices with their start and end apart: 22, of which 16 were waited for; matrix products, arithmetic and copies ran while one was open for 7% of the time, Pallas kernels for 0%

profile of v25, /device:TPU:2, one launch (start us, length us, event | category | flops | bytes accessed | tf_op | source)
XLA Modules:
  0.0 129.5 jit_solution(2251277609806530398)
XLA Ops:
  4.5 3.4 %collective-permute-start = (f32[2,1,1,8,8,128]{5,4,3,2,1,0:T(8,128)S(1)}, f32[2,1,1,8,8,128]{5,4,3,2,1,0:T(8,128)S(1)}, u32[]{:S(2)}, u32[]{:S(2)}) collective-permute-start(f32[2,1,1,8,8,128]{5,4,3,2,1,0:T(8,128)S(1)} %pad_maximum_fusion.11), channel_id=1, source_target_pairs={{0,4},{4,8},{8,12},{12,16},{16,20},{20,24},{24,28},{1,5},{5,9},{9,... | collective-permute-start | bytes 196616 | tf_op jit(solution)/shard_map/ppermute | solution.py:16
  7.9 1.3 collective-permute-start.1
  10.1 1.1 copy.281
  11.2 2.9 %collective-permute-done.1 = f32[2,1,1,8,8,128]{5,4,3,2,1,0:T(8,128)S(1)} collective-permute-done((f32[2,1,1,8,8,128]{5,4,3,2,1,0:T(8,128)S(1)}, f32[2,1,1,8,8,128]{5,4,3,2,1,0:T(8,128)S(1)}, u32[]{:S(2)}, u32[]{:S(2)}) %collective-permute-start.1) | collective-permute-done | bytes 65568 | tf_op jit(solution)/shard_map/ppermute | solution.py:19
  14.5 1.9 %collective-permute-start.2 = (f32[2,1,1,8,8,128]{5,3,0,4,2,1:T(8,128)S(1)}, f32[2,1,1,8,8,128]{5,3,0,4,2,1:T(8,128)S(1)}, u32[]{:S(2)}, u32[]{:S(2)}) collective-permute-start(f32[2,1,1,8,8,128]{5,3,0,4,2,1:T(8,128)S(1)} %get-tuple-element.56), channel_id=1, source_target_pairs={{0,1},{1,2},{2,3},{4,5},{5,6},{6,7},{8,9},{9,10},{10,11},{12,13},{... | collective-permute-start | bytes 196616 | tf_op jit(solution)/shard_map/ppermute | solution.py:16
  16.4 3.6 %collective-permute-start.3 = (f32[2,1,1,8,8,128]{5,3,0,4,2,1:T(8,128)S(1)}, f32[2,1,1,8,8,128]{5,3,0,4,2,1:T(8,128)S(1)}, u32[]{:S(2)}, u32[]{:S(2)}) collective-permute-start(f32[2,1,1,8,8,128]{5,3,0,4,2,1:T(8,128)S(1)} %get-tuple-element.57), channel_id=1, source_target_pairs={{1,0},{2,1},{3,2},{5,4},{6,5},{7,6},{9,8},{10,9},{11,10},{13,12},{... | collective-permute-start | bytes 196616 | tf_op jit(solution)/shard_map/ppermute | solution.py:19
  20.4 1.5 %collective-permute-done.3 = f32[2,1,1,8,8,128]{5,3,0,4,2,1:T(8,128)S(1)} collective-permute-done((f32[2,1,1,8,8,128]{5,3,0,4,2,1:T(8,128)S(1)}, f32[2,1,1,8,8,128]{5,3,0,4,2,1:T(8,128)S(1)}, u32[]{:S(2)}, u32[]{:S(2)}) %collective-permute-start.3) | collective-permute-done | bytes 65568 | tf_op jit(solution)/shard_map/ppermute | solution.py:19
  23.7 0.9 fusion.27
  24.7 4.3 %collective-permute-start.4 = (f32[1,1,1,8,8,128]{5,4,3,2,1,0:T(8,128)S(1)}, f32[1,1,1,8,8,128]{5,4,3,2,1,0:T(8,128)S(1)}, u32[]{:S(2)}, u32[]{:S(2)}) collective-permute-start(f32[1,1,1,8,8,128]{5,4,3,2,1,0:T(8,128)S(1)} %bitcast.467), channel_id=1, source_target_pairs={{0,4},{4,8},{8,12},{12,16},{16,20},{20,24},{24,28},{1,5},{5,9},{9,... | collective-permute-start | bytes 98312 | tf_op jit(solution)/shard_map/ppermute | solution.py:16
  29.0 1.3 collective-permute-start.5
  30.3 0.9 fusion.17
  31.2 3.6 %collective-permute-done.5 = f32[1,1,1,8,8,128]{5,4,3,2,1,0:T(8,128)S(1)} collective-permute-done((f32[1,1,1,8,8,128]{5,4,3,2,1,0:T(8,128)S(1)}, f32[1,1,1,8,8,128]{5,4,3,2,1,0:T(8,128)S(1)}, u32[]{:S(2)}, u32[]{:S(2)}) %collective-permute-start.5) | collective-permute-done | bytes 32800 | tf_op jit(solution)/shard_map/ppermute | solution.py:19
  34.8 1.9 %collective-permute-start.6 = (f32[1,1,1,8,8,128]{5,3,4,2,1,0:T(8,128)S(1)}, f32[1,1,1,8,8,128]{5,3,4,2,1,0:T(8,128)S(1)}, u32[]{:S(2)}, u32[]{:S(2)}) collective-permute-start(f32[1,1,1,8,8,128]{5,3,4,2,1,0:T(8,128)S(1)} %maximum_bitcast_fusion.15), channel_id=1, source_target_pairs={{0,1},{1,2},{2,3},{4,5},{5,6},{6,7},{8,9},{9,10},{10,11},{12,13},{... | collective-permute-start | bytes 98312 | tf_op jit(solution)/shard_map/ppermute | solution.py:16
  36.8 1.4 %fusion.4 = f32[512,256]{1,0:T(8,128)S(1)} fusion(bf16[256,4096]{1,0:T(8,128)(2,1)S(1)} %get-tuple-element.101, bf16[256,4096]{1,0:T(8,128)(2,1)S(1)} %get-tuple-element.100, s32[4096]{0:T(1024)S(1)} %get-tuple-element.96), kind=kOutput, calls=%fused_computation.6 | convolution fusion | flops 1083179008 | bytes 4734976 | tf_op jit(solution)/shard_map/dot_general | solution.py:170
  38.2 1.9 %collective-permute-done.6 = f32[1,1,1,8,8,128]{5,3,4,2,1,0:T(8,128)S(1)} collective-permute-done((f32[1,1,1,8,8,128]{5,3,4,2,1,0:T(8,128)S(1)}, f32[1,1,1,8,8,128]{5,3,4,2,1,0:T(8,128)S(1)}, u32[]{:S(2)}, u32[]{:S(2)}) %collective-permute-start.6) | collective-permute-done | bytes 32800 | tf_op jit(solution)/shard_map/ppermute | solution.py:16
  40.1 1.9 %collective-permute-start.7 = (f32[1,1,1,8,8,128]{5,3,4,2,1,0:T(8,128)S(1)}, f32[1,1,1,8,8,128]{5,3,4,2,1,0:T(8,128)S(1)}, u32[]{:S(2)}, u32[]{:S(2)}) collective-permute-start(f32[1,1,1,8,8,128]{5,3,4,2,1,0:T(8,128)S(1)} %get-tuple-element.49), channel_id=1, source_target_pairs={{1,0},{2,1},{3,2},{5,4},{6,5},{7,6},{9,8},{10,9},{11,10},{13,12},{... | collective-permute-start | bytes 98312 | tf_op jit(solution)/shard_map/ppermute | solution.py:19
  42.2 1.4 %collective-permute-done.7 = f32[1,1,1,8,8,128]{5,3,4,2,1,0:T(8,128)S(1)} collective-permute-done((f32[1,1,1,8,8,128]{5,3,4,2,1,0:T(8,128)S(1)}, f32[1,1,1,8,8,128]{5,3,4,2,1,0:T(8,128)S(1)}, u32[]{:S(2)}, u32[]{:S(2)}) %collective-permute-start.7) | collective-permute-done | bytes 32800 | tf_op jit(solution)/shard_map/ppermute | solution.py:19
  45.5 3.4 %collective-permute-start.8 = (f32[1,1,1,8,8,128]{5,4,3,2,1,0:T(8,128)S(1)}, f32[1,1,1,8,8,128]{5,4,3,2,1,0:T(8,128)S(1)}, u32[]{:S(2)}, u32[]{:S(2)}) collective-permute-start(f32[1,1,1,8,8,128]{5,4,3,2,1,0:T(8,128)S(1)} %get-tuple-element.78), channel_id=1, source_target_pairs={{0,4},{4,8},{8,12},{12,16},{16,20},{20,24},{24,28},{1,5},{5,9},{9,... | collective-permute-start | bytes 98312 | tf_op jit(solution)/shard_map/ppermute | solution.py:16
  49.0 1.3 collective-permute-start.9
  50.5 4.2 %collective-permute-done.9 = f32[1,1,1,8,8,128]{5,4,3,2,1,0:T(8,128)S(1)} collective-permute-done((f32[1,1,1,8,8,128]{5,4,3,2,1,0:T(8,128)S(1)}, f32[1,1,1,8,8,128]{5,4,3,2,1,0:T(8,128)S(1)}, u32[]{:S(2)}, u32[]{:S(2)}) %collective-permute-start.9) | collective-permute-done | bytes 32800 | tf_op jit(solution)/shard_map/ppermute | solution.py:19
  54.8 1.9 %collective-permute-start.10 = (f32[1,1,1,8,8,128]{5,4,3,2,1,0:T(8,128)S(1)}, f32[1,1,1,8,8,128]{5,4,3,2,1,0:T(8,128)S(1)}, u32[]{:S(2)}, u32[]{:S(2)}) collective-permute-start(f32[1,1,1,8,8,128]{5,4,3,2,1,0:T(8,128)S(1)} %maximum_bitcast_fusion.13), channel_id=1, source_target_pairs={{0,1},{1,2},{2,3},{4,5},{5,6},{6,7},{8,9},{9,10},{10,11},{12,13},{... | collective-permute-start | bytes 98312 | tf_op jit(solution)/shard_map/ppermute | solution.py:16
  56.8 3.2 %collective-permute-done.10 = f32[1,1,1,8,8,128]{5,4,3,2,1,0:T(8,128)S(1)} collective-permute-done((f32[1,1,1,8,8,128]{5,4,3,2,1,0:T(8,128)S(1)}, f32[1,1,1,8,8,128]{5,4,3,2,1,0:T(8,128)S(1)}, u32[]{:S(2)}, u32[]{:S(2)}) %collective-permute-start.10) | collective-permute-done | bytes 32800 | tf_op jit(solution)/shard_map/ppermute | solution.py:16
  60.0 1.9 %collective-permute-start.11 = (f32[1,1,1,8,8,128]{5,4,3,2,1,0:T(8,128)S(1)}, f32[1,1,1,8,8,128]{5,4,3,2,1,0:T(8,128)S(1)}, u32[]{:S(2)}, u32[]{:S(2)}) collective-permute-start(f32[1,1,1,8,8,128]{5,4,3,2,1,0:T(8,128)S(1)} %get-tuple-element.47), channel_id=1, source_target_pairs={{1,0},{2,1},{3,2},{5,4},{6,5},{7,6},{9,8},{10,9},{11,10},{13,12},{... | collective-permute-start | bytes 98312 | tf_op jit(solution)/shard_map/ppermute | solution.py:19
  62.0 1.5 %collective-permute-done.11 = f32[1,1,1,8,8,128]{5,4,3,2,1,0:T(8,128)S(1)} collective-permute-done((f32[1,1,1,8,8,128]{5,4,3,2,1,0:T(8,128)S(1)}, f32[1,1,1,8,8,128]{5,4,3,2,1,0:T(8,128)S(1)}, u32[]{:S(2)}, u32[]{:S(2)}) %collective-permute-start.11) | collective-permute-done | bytes 32800 | tf_op jit(solution)/shard_map/ppermute | solution.py:19
  65.7 4.3 %collective-permute-start.12 = (f32[1,1,1,8,8,128]{5,4,3,2,1,0:T(8,128)S(1)}, f32[1,1,1,8,8,128]{5,4,3,2,1,0:T(8,128)S(1)}, u32[]{:S(2)}, u32[]{:S(2)}) collective-permute-start(f32[1,1,1,8,8,128]{5,4,3,2,1,0:T(8,128)S(1)} %get-tuple-element.72), channel_id=1, source_target_pairs={{0,4},{4,8},{8,12},{12,16},{16,20},{20,24},{24,28},{1,5},{5,9},{9,... | collective-permute-start | bytes 98312 | tf_op jit(solution)/shard_map/ppermute | solution.py:16
  70.0 1.5 %collective-permute-start.13 = (f32[1,1,1,8,8,128]{5,4,3,2,1,0:T(8,128)S(1)}, f32[1,1,1,8,8,128]{5,4,3,2,1,0:T(8,128)S(1)}, u32[]{:S(2)}, u32[]{:S(2)}) collective-permute-start(f32[1,1,1,8,8,128]{5,4,3,2,1,0:T(8,128)S(1)} %get-tuple-element.73), channel_id=1, source_target_pairs={{4,0},{8,4},{12,8},{16,12},{20,16},{24,20},{28,24},{5,1},{9,5},{13... | collective-permute-start | bytes 98312 | tf_op jit(solution)/shard_map/ppermute | solution.py:19
  71.5 1.3 %fusion.13 = f32[512,4096]{1,0:T(8,128)S(1)} fusion(s32[4096]{0:T(1024)S(1)} %bitcast.461, bf16[256,256]{1,0:T(8,128)(2,1)S(1)} %get-tuple-element.71, bf16[256,256]{1,0:T(8,128)(2,1)S(1)} %get-tuple-element.70), kind=kOutput, calls=%fused_computation.16 | convolution fusion | flops 1075314688 | bytes 8667136 | tf_op jit(solution)/shard_map/dot_general | solution.py:156
  72.8 0.9 fusion.3
  73.8 2.0 %collective-permute-done.13 = f32[1,1,1,8,8,128]{5,4,3,2,1,0:T(8,128)S(1)} collective-permute-done((f32[1,1,1,8,8,128]{5,4,3,2,1,0:T(8,128)S(1)}, f32[1,1,1,8,8,128]{5,4,3,2,1,0:T(8,128)S(1)}, u32[]{:S(2)}, u32[]{:S(2)}) %collective-permute-start.13) | collective-permute-done | bytes 32800 | tf_op jit(solution)/shard_map/ppermute | solution.py:19
  75.9 1.9 %collective-permute-start.14 = (f32[1,1,1,8,8,128]{5,4,3,2,1,0:T(8,128)S(1)}, f32[1,1,1,8,8,128]{5,4,3,2,1,0:T(8,128)S(1)}, u32[]{:S(2)}, u32[]{:S(2)}) collective-permute-start(f32[1,1,1,8,8,128]{5,4,3,2,1,0:T(8,128)S(1)} %maximum_bitcast_fusion.11), channel_id=1, source_target_pairs={{0,1},{1,2},{2,3},{4,5},{5,6},{6,7},{8,9},{9,10},{10,11},{12,13},{... | collective-permute-start | bytes 98312 | tf_op jit(solution)/shard_map/ppermute | solution.py:16
  77.8 3.3 %collective-permute-done.14 = f32[1,1,1,8,8,128]{5,4,3,2,1,0:T(8,128)S(1)} collective-permute-done((f32[1,1,1,8,8,128]{5,4,3,2,1,0:T(8,128)S(1)}, f32[1,1,1,8,8,128]{5,4,3,2,1,0:T(8,128)S(1)}, u32[]{:S(2)}, u32[]{:S(2)}) %collective-permute-start.14) | collective-permute-done | bytes 32800 | tf_op jit(solution)/shard_map/ppermute | solution.py:16
  81.1 1.9 %collective-permute-start.15 = (f32[1,1,1,8,8,128]{5,4,3,2,1,0:T(8,128)S(1)}, f32[1,1,1,8,8,128]{5,4,3,2,1,0:T(8,128)S(1)}, u32[]{:S(2)}, u32[]{:S(2)}) collective-permute-start(f32[1,1,1,8,8,128]{5,4,3,2,1,0:T(8,128)S(1)} %get-tuple-element.41), channel_id=1, source_target_pairs={{1,0},{2,1},{3,2},{5,4},{6,5},{7,6},{9,8},{10,9},{11,10},{13,12},{... | collective-permute-start | bytes 98312 | tf_op jit(solution)/shard_map/ppermute | solution.py:19
  83.1 1.5 %collective-permute-done.15 = f32[1,1,1,8,8,128]{5,4,3,2,1,0:T(8,128)S(1)} collective-permute-done((f32[1,1,1,8,8,128]{5,4,3,2,1,0:T(8,128)S(1)}, f32[1,1,1,8,8,128]{5,4,3,2,1,0:T(8,128)S(1)}, u32[]{:S(2)}, u32[]{:S(2)}) %collective-permute-start.15) | collective-permute-done | bytes 32800 | tf_op jit(solution)/shard_map/ppermute | solution.py:19
  85.2 0.8 fusion.107
  86.1 1.3 %fusion.12 = f32[512,4096]{1,0:T(8,128)S(1)} fusion(s32[4096]{0:T(1024)S(1)} %bitcast.462, bf16[256,256]{1,0:T(8,128)(2,1)S(1)} %get-tuple-element.65, bf16[256,256]{1,0:T(8,128)(2,1)S(1)} %get-tuple-element.64), kind=kOutput, calls=%fused_computation.15 | convolution fusion | flops 1075314688 | bytes 8667136 | tf_op jit(solution)/shard_map/dot_general | solution.py:156
  87.4 0.9 fusion.1
  88.4 0.9 fusion.15
  89.2 1.4 %fusion.8 = f32[512,256]{1,0:T(8,128)S(1)} fusion(bf16[256,4096]{1,0:T(8,128)(2,1)S(1)} %get-tuple-element.99, bf16[256,4096]{1,0:T(8,128)(2,1)S(1)} %get-tuple-element.98, s32[4096]{0:T(1024)S(1)} %get-tuple-element.96), kind=kOutput, calls=%fused_computation.10 | convolution fusion | flops 1083179008 | bytes 4734976 | tf_op jit(solution)/shard_map/dot_general | solution.py:170
  90.8 1.2 copy.213
  92.0 4.4 %all-to-all-start = ((f32[32,2,2048]{2,1,0:T(2,128)}), f32[32,2,2048]{2,1,0:T(2,128)S(1)}, u32[]{:S(2)}, u32[]{:S(2)}) async-start(f32[32,2,2048]{2,1,0:T(2,128)} %bitcast.107), calls=%async_computation | async-start | bytes 1048576 | tf_op jit(solution)/shard_map/all_to_all | solution.py:185
  97.7 3.4 %collective-permute-start.16 = (f32[1,1,1,8,8,128]{5,4,3,2,1,0:T(8,128)S(1)}, f32[1,1,1,8,8,128]{5,4,3,2,1,0:T(8,128)S(1)}, u32[]{:S(2)}, u32[]{:S(2)}) collective-permute-start(f32[1,1,1,8,8,128]{5,4,3,2,1,0:T(8,128)S(1)} %get-tuple-element.66), channel_id=1, source_target_pairs={{0,4},{4,8},{8,12},{12,16},{16,20},{20,24},{24,28},{1,5},{5,9},{9,... | collective-permute-start | bytes 98312 | tf_op jit(solution)/shard_map/ppermute | solution.py:16
  101.1 1.3 collective-permute-start.17
  102.8 4.5 %collective-permute-done.17 = f32[1,1,1,8,8,128]{5,4,3,2,1,0:T(8,128)S(1)} collective-permute-done((f32[1,1,1,8,8,128]{5,4,3,2,1,0:T(8,128)S(1)}, f32[1,1,1,8,8,128]{5,4,3,2,1,0:T(8,128)S(1)}, u32[]{:S(2)}, u32[]{:S(2)}) %collective-permute-start.17) | collective-permute-done | bytes 32800 | tf_op jit(solution)/shard_map/ppermute | solution.py:19
  107.4 4.1 %all-to-all-done = f32[32,2,2048]{2,1,0:T(2,128)S(1)} async-done(((f32[32,2,2048]{2,1,0:T(2,128)}), f32[32,2,2048]{2,1,0:T(2,128)S(1)}, u32[]{:S(2)}, u32[]{:S(2)}) %all-to-all-start) | async-done | bytes 524320 | tf_op jit(solution)/shard_map/all_to_all | solution.py:185
  112.4 1.9 %collective-permute-start.18 = (f32[1,1,1,8,8,128]{5,3,4,2,1,0:T(8,128)S(1)}, f32[1,1,1,8,8,128]{5,3,4,2,1,0:T(8,128)S(1)}, u32[]{:S(2)}, u32[]{:S(2)}) collective-permute-start(f32[1,1,1,8,8,128]{5,3,4,2,1,0:T(8,128)S(1)} %get-tuple-element.92), channel_id=1, source_target_pairs={{0,1},{1,2},{2,3},{4,5},{5,6},{6,7},{8,9},{9,10},{10,11},{12,13},{... | collective-permute-start | bytes 98312 | tf_op jit(solution)/shard_map/ppermute | solution.py:16
  114.4 3.6 %collective-permute-start.19 = (f32[1,1,1,8,8,128]{5,3,4,2,1,0:T(8,128)S(1)}, f32[1,1,1,8,8,128]{5,3,4,2,1,0:T(8,128)S(1)}, u32[]{:S(2)}, u32[]{:S(2)}) collective-permute-start(f32[1,1,1,8,8,128]{5,3,4,2,1,0:T(8,128)S(1)} %get-tuple-element.93), channel_id=1, source_target_pairs={{1,0},{2,1},{3,2},{5,4},{6,5},{7,6},{9,8},{10,9},{11,10},{13,12},{... | collective-permute-start | bytes 98312 | tf_op jit(solution)/shard_map/ppermute | solution.py:19
  118.0 3.5 %all-to-all-start.1 = ((f32[8,2,2048]{2,1,0:T(2,128)}), f32[8,2,2048]{2,1,0:T(2,128)S(1)}, u32[]{:S(2)}, u32[]{:S(2)}) async-start(f32[8,2,2048]{2,1,0:T(2,128)} %broadcast_in_dim.192), calls=%async_computation.1 | async-start | bytes 262144 | tf_op jit(solution)/shard_map/all_to_all | solution.py:194
  122.5 6.3 %all-to-all-done.1 = f32[8,2,2048]{2,1,0:T(2,128)S(1)} async-done(((f32[8,2,2048]{2,1,0:T(2,128)}), f32[8,2,2048]{2,1,0:T(2,128)S(1)}, u32[]{:S(2)}, u32[]{:S(2)}) %all-to-all-start.1) | async-done | bytes 131104 | tf_op jit(solution)/shard_map/all_to_all | solution.py:194
  (141 shorter events, 16.8 us)
Async XLA Ops:
  0.6 19.5 %copy-start.2 = (f32[1,4096]{1,0:T(1,128)S(1)}, f32[1,4096]{1,0:T(1,128)}, u32[]{:S(2)}) copy-start(f32[1,4096]{1,0:T(1,128)} %param.41) | copy-start | bytes 49156
  0.6 19.4 %copy-start.5 = (s32[1,4096,1]{1,2,0:T(1,128)S(1)}, s32[1,4096,1]{1,2,0:T(1,128)}, u32[]{:S(2)}) copy-start(s32[1,4096,1]{1,2,0:T(1,128)} %param.39) | copy-start | bytes 49156
  0.7 19.4 %copy-start.4 = (s32[1,4096]{1,0:T(1,128)S(1)}, s32[1,4096]{1,0:T(1,128)}, u32[]{:S(2)}) copy-start(s32[1,4096]{1,0:T(1,128)} %param.40) | copy-start | bytes 49156
  4.5 6.7 %collective-permute-start = (f32[2,1,1,8,8,128]{5,4,3,2,1,0:T(8,128)S(1)}, f32[2,1,1,8,8,128]{5,4,3,2,1,0:T(8,128)S(1)}, u32[]{:S(2)}, u32[]{:S(2)}) collective-permute-start(f32[2,1,1,8,8,128]{5,4,3,2,1,0:T(8,128)S(1)} %pad_maximum_fusion.11), channel_id=1, source_target_pairs={{0,4},{4,8},{8,12},{12,16},{16,20},{20,24},{24,28},{1,5},{5,9},{9,... | collective-permute-start | bytes 196616 | tf_op jit(solution)/shard_map/ppermute | solution.py:16
  7.9 6.2 %collective-permute-start.1 = (f32[2,1,1,8,8,128]{5,4,3,2,1,0:T(8,128)S(1)}, f32[2,1,1,8,8,128]{5,4,3,2,1,0:T(8,128)S(1)}, u32[]{:S(2)}, u32[]{:S(2)}) collective-permute-start(f32[2,1,1,8,8,128]{5,4,3,2,1,0:T(8,128)S(1)} %pad_maximum_fusion.10), channel_id=1, source_target_pairs={{4,0},{8,4},{12,8},{16,12},{20,16},{24,20},{28,24},{5,1},{9,5},{13... | collective-permute-start | bytes 196616 | tf_op jit(solution)/shard_map/ppermute | solution.py:19
  14.5 8.3 %copy-start = (f32[8,8,1,1]{1,0,3,2:T(8,128)S(1)}, f32[8,8,1,1]{1,0,3,2:T(8,128)}, u32[]{:S(2)}) copy-start(f32[8,8,1,1]{1,0,3,2:T(8,128)} %constant.130) | copy-start | bytes 772
  14.5 5.9 %collective-permute-start.2 = (f32[2,1,1,8,8,128]{5,3,0,4,2,1:T(8,128)S(1)}, f32[2,1,1,8,8,128]{5,3,0,4,2,1:T(8,128)S(1)}, u32[]{:S(2)}, u32[]{:S(2)}) collective-permute-start(f32[2,1,1,8,8,128]{5,3,0,4,2,1:T(8,128)S(1)} %get-tuple-element.56), channel_id=1, source_target_pairs={{0,1},{1,2},{2,3},{4,5},{5,6},{6,7},{8,9},{9,10},{10,11},{12,13},{... | collective-permute-start | bytes 196616 | tf_op jit(solution)/shard_map/ppermute | solution.py:16
  16.4 5.5 %collective-permute-start.3 = (f32[2,1,1,8,8,128]{5,3,0,4,2,1:T(8,128)S(1)}, f32[2,1,1,8,8,128]{5,3,0,4,2,1:T(8,128)S(1)}, u32[]{:S(2)}, u32[]{:S(2)}) collective-permute-start(f32[2,1,1,8,8,128]{5,3,0,4,2,1:T(8,128)S(1)} %get-tuple-element.57), channel_id=1, source_target_pairs={{1,0},{2,1},{3,2},{5,4},{6,5},{7,6},{9,8},{10,9},{11,10},{13,12},{... | collective-permute-start | bytes 196616 | tf_op jit(solution)/shard_map/ppermute | solution.py:19
  20.2 3.4 %copy-start.3 = (f32[8]{0:T(128)S(1)}, f32[8]{0:T(128)}, u32[]{:S(2)}) copy-start(f32[8]{0:T(128)} %constant.125) | copy-start | bytes 100
  24.7 6.5 %collective-permute-start.4 = (f32[1,1,1,8,8,128]{5,4,3,2,1,0:T(8,128)S(1)}, f32[1,1,1,8,8,128]{5,4,3,2,1,0:T(8,128)S(1)}, u32[]{:S(2)}, u32[]{:S(2)}) collective-permute-start(f32[1,1,1,8,8,128]{5,4,3,2,1,0:T(8,128)S(1)} %bitcast.467), channel_id=1, source_target_pairs={{0,4},{4,8},{8,12},{12,16},{16,20},{20,24},{24,28},{1,5},{5,9},{9,... | collective-permute-start | bytes 98312 | tf_op jit(solution)/shard_map/ppermute | solution.py:16
  29.0 5.8 %collective-permute-start.5 = (f32[1,1,1,8,8,128]{5,4,3,2,1,0:T(8,128)S(1)}, f32[1,1,1,8,8,128]{5,4,3,2,1,0:T(8,128)S(1)}, u32[]{:S(2)}, u32[]{:S(2)}) collective-permute-start(f32[1,1,1,8,8,128]{5,4,3,2,1,0:T(8,128)S(1)} %bitcast.469), channel_id=1, source_target_pairs={{4,0},{8,4},{12,8},{16,12},{20,16},{24,20},{28,24},{5,1},{9,5},{13... | collective-permute-start | bytes 98312 | tf_op jit(solution)/shard_map/ppermute | solution.py:19
  34.8 5.2 %collective-permute-start.6 = (f32[1,1,1,8,8,128]{5,3,4,2,1,0:T(8,128)S(1)}, f32[1,1,1,8,8,128]{5,3,4,2,1,0:T(8,128)S(1)}, u32[]{:S(2)}, u32[]{:S(2)}) collective-permute-start(f32[1,1,1,8,8,128]{5,3,4,2,1,0:T(8,128)S(1)} %maximum_bitcast_fusion.15), channel_id=1, source_target_pairs={{0,1},{1,2},{2,3},{4,5},{5,6},{6,7},{8,9},{9,10},{10,11},{12,13},{... | collective-permute-start | bytes 98312 | tf_op jit(solution)/shard_map/ppermute | solution.py:16
  40.1 16.6 %copy-start.1 = (s32[1,4096]{1,0:T(1,128)S(1)}, s32[1,4096]{1,0:T(1,128)}, u32[]{:S(2)}) copy-start(s32[1,4096]{1,0:T(1,128)} %param.38) | copy-start | bytes 49156
  40.1 3.5 %collective-permute-start.7 = (f32[1,1,1,8,8,128]{5,3,4,2,1,0:T(8,128)S(1)}, f32[1,1,1,8,8,128]{5,3,4,2,1,0:T(8,128)S(1)}, u32[]{:S(2)}, u32[]{:S(2)}) collective-permute-start(f32[1,1,1,8,8,128]{5,3,4,2,1,0:T(8,128)S(1)} %get-tuple-element.49), channel_id=1, source_target_pairs={{1,0},{2,1},{3,2},{5,4},{6,5},{7,6},{9,8},{10,9},{11,10},{13,12},{... | collective-permute-start | bytes 98312 | tf_op jit(solution)/shard_map/ppermute | solution.py:19
  45.5 5.0 %collective-permute-start.8 = (f32[1,1,1,8,8,128]{5,4,3,2,1,0:T(8,128)S(1)}, f32[1,1,1,8,8,128]{5,4,3,2,1,0:T(8,128)S(1)}, u32[]{:S(2)}, u32[]{:S(2)}) collective-permute-start(f32[1,1,1,8,8,128]{5,4,3,2,1,0:T(8,128)S(1)} %get-tuple-element.78), channel_id=1, source_target_pairs={{0,4},{4,8},{8,12},{12,16},{16,20},{20,24},{24,28},{1,5},{5,9},{9,... | collective-permute-start | bytes 98312 | tf_op jit(solution)/shard_map/ppermute | solution.py:16
  49.0 5.8 %collective-permute-start.9 = (f32[1,1,1,8,8,128]{5,4,3,2,1,0:T(8,128)S(1)}, f32[1,1,1,8,8,128]{5,4,3,2,1,0:T(8,128)S(1)}, u32[]{:S(2)}, u32[]{:S(2)}) collective-permute-start(f32[1,1,1,8,8,128]{5,4,3,2,1,0:T(8,128)S(1)} %get-tuple-element.79), channel_id=1, source_target_pairs={{4,0},{8,4},{12,8},{16,12},{20,16},{24,20},{28,24},{5,1},{9,5},{13... | collective-permute-start | bytes 98312 | tf_op jit(solution)/shard_map/ppermute | solution.py:19
  54.8 5.2 %collective-permute-start.10 = (f32[1,1,1,8,8,128]{5,4,3,2,1,0:T(8,128)S(1)}, f32[1,1,1,8,8,128]{5,4,3,2,1,0:T(8,128)S(1)}, u32[]{:S(2)}, u32[]{:S(2)}) collective-permute-start(f32[1,1,1,8,8,128]{5,4,3,2,1,0:T(8,128)S(1)} %maximum_bitcast_fusion.13), channel_id=1, source_target_pairs={{0,1},{1,2},{2,3},{4,5},{5,6},{6,7},{8,9},{9,10},{10,11},{12,13},{... | collective-permute-start | bytes 98312 | tf_op jit(solution)/shard_map/ppermute | solution.py:16
  60.0 3.5 %collective-permute-start.11 = (f32[1,1,1,8,8,128]{5,4,3,2,1,0:T(8,128)S(1)}, f32[1,1,1,8,8,128]{5,4,3,2,1,0:T(8,128)S(1)}, u32[]{:S(2)}, u32[]{:S(2)}) collective-permute-start(f32[1,1,1,8,8,128]{5,4,3,2,1,0:T(8,128)S(1)} %get-tuple-element.47), channel_id=1, source_target_pairs={{1,0},{2,1},{3,2},{5,4},{6,5},{7,6},{9,8},{10,9},{11,10},{13,12},{... | collective-permute-start | bytes 98312 | tf_op jit(solution)/shard_map/ppermute | solution.py:19
  65.7 8.1 %collective-permute-start.12 = (f32[1,1,1,8,8,128]{5,4,3,2,1,0:T(8,128)S(1)}, f32[1,1,1,8,8,128]{5,4,3,2,1,0:T(8,128)S(1)}, u32[]{:S(2)}, u32[]{:S(2)}) collective-permute-start(f32[1,1,1,8,8,128]{5,4,3,2,1,0:T(8,128)S(1)} %get-tuple-element.72), channel_id=1, source_target_pairs={{0,4},{4,8},{8,12},{12,16},{16,20},{20,24},{24,28},{1,5},{5,9},{9,... | collective-permute-start | bytes 98312 | tf_op jit(solution)/shard_map/ppermute | solution.py:16
  70.0 5.8 %collective-permute-start.13 = (f32[1,1,1,8,8,128]{5,4,3,2,1,0:T(8,128)S(1)}, f32[1,1,1,8,8,128]{5,4,3,2,1,0:T(8,128)S(1)}, u32[]{:S(2)}, u32[]{:S(2)}) collective-permute-start(f32[1,1,1,8,8,128]{5,4,3,2,1,0:T(8,128)S(1)} %get-tuple-element.73), channel_id=1, source_target_pairs={{4,0},{8,4},{12,8},{16,12},{20,16},{24,20},{28,24},{5,1},{9,5},{13... | collective-permute-start | bytes 98312 | tf_op jit(solution)/shard_map/ppermute | solution.py:19
  75.9 5.2 %collective-permute-start.14 = (f32[1,1,1,8,8,128]{5,4,3,2,1,0:T(8,128)S(1)}, f32[1,1,1,8,8,128]{5,4,3,2,1,0:T(8,128)S(1)}, u32[]{:S(2)}, u32[]{:S(2)}) collective-permute-start(f32[1,1,1,8,8,128]{5,4,3,2,1,0:T(8,128)S(1)} %maximum_bitcast_fusion.11), channel_id=1, source_target_pairs={{0,1},{1,2},{2,3},{4,5},{5,6},{6,7},{8,9},{9,10},{10,11},{12,13},{... | collective-permute-start | bytes 98312 | tf_op jit(solution)/shard_map/ppermute | solution.py:16
  81.1 3.5 %collective-permute-start.15 = (f32[1,1,1,8,8,128]{5,4,3,2,1,0:T(8,128)S(1)}, f32[1,1,1,8,8,128]{5,4,3,2,1,0:T(8,128)S(1)}, u32[]{:S(2)}, u32[]{:S(2)}) collective-permute-start(f32[1,1,1,8,8,128]{5,4,3,2,1,0:T(8,128)S(1)} %get-tuple-element.41), channel_id=1, source_target_pairs={{1,0},{2,1},{3,2},{5,4},{6,5},{7,6},{9,8},{10,9},{11,10},{13,12},{... | collective-permute-start | bytes 98312 | tf_op jit(solution)/shard_map/ppermute | solution.py:19
  92.0 19.4 %all-to-all-start = ((f32[32,2,2048]{2,1,0:T(2,128)}), f32[32,2,2048]{2,1,0:T(2,128)S(1)}, u32[]{:S(2)}, u32[]{:S(2)}) async-start(f32[32,2,2048]{2,1,0:T(2,128)} %bitcast.107), calls=%async_computation | async-start | bytes 1048576 | tf_op jit(solution)/shard_map/all_to_all | solution.py:185
  97.7 5.1 %collective-permute-start.16 = (f32[1,1,1,8,8,128]{5,4,3,2,1,0:T(8,128)S(1)}, f32[1,1,1,8,8,128]{5,4,3,2,1,0:T(8,128)S(1)}, u32[]{:S(2)}, u32[]{:S(2)}) collective-permute-start(f32[1,1,1,8,8,128]{5,4,3,2,1,0:T(8,128)S(1)} %get-tuple-element.66), channel_id=1, source_target_pairs={{0,4},{4,8},{8,12},{12,16},{16,20},{20,24},{24,28},{1,5},{5,9},{9,... | collective-permute-start | bytes 98312 | tf_op jit(solution)/shard_map/ppermute | solution.py:16
  101.1 6.2 %collective-permute-start.17 = (f32[1,1,1,8,8,128]{5,4,3,2,1,0:T(8,128)S(1)}, f32[1,1,1,8,8,128]{5,4,3,2,1,0:T(8,128)S(1)}, u32[]{:S(2)}, u32[]{:S(2)}) collective-permute-start(f32[1,1,1,8,8,128]{5,4,3,2,1,0:T(8,128)S(1)} %get-tuple-element.67), channel_id=1, source_target_pairs={{4,0},{8,4},{12,8},{16,12},{20,16},{24,20},{28,24},{5,1},{9,5},{13... | collective-permute-start | bytes 98312 | tf_op jit(solution)/shard_map/ppermute | solution.py:19
  112.4 9.1 %collective-permute-start.18 = (f32[1,1,1,8,8,128]{5,3,4,2,1,0:T(8,128)S(1)}, f32[1,1,1,8,8,128]{5,3,4,2,1,0:T(8,128)S(1)}, u32[]{:S(2)}, u32[]{:S(2)}) collective-permute-start(f32[1,1,1,8,8,128]{5,3,4,2,1,0:T(8,128)S(1)} %get-tuple-element.92), channel_id=1, source_target_pairs={{0,1},{1,2},{2,3},{4,5},{5,6},{6,7},{8,9},{9,10},{10,11},{12,13},{... | collective-permute-start | bytes 98312 | tf_op jit(solution)/shard_map/ppermute | solution.py:16
  114.4 7.1 %collective-permute-start.19 = (f32[1,1,1,8,8,128]{5,3,4,2,1,0:T(8,128)S(1)}, f32[1,1,1,8,8,128]{5,3,4,2,1,0:T(8,128)S(1)}, u32[]{:S(2)}, u32[]{:S(2)}) collective-permute-start(f32[1,1,1,8,8,128]{5,3,4,2,1,0:T(8,128)S(1)} %get-tuple-element.93), channel_id=1, source_target_pairs={{1,0},{2,1},{3,2},{5,4},{6,5},{7,6},{9,8},{10,9},{11,10},{13,12},{... | collective-permute-start | bytes 98312 | tf_op jit(solution)/shard_map/ppermute | solution.py:19
  118.0 10.8 %all-to-all-start.1 = ((f32[8,2,2048]{2,1,0:T(2,128)}), f32[8,2,2048]{2,1,0:T(2,128)S(1)}, u32[]{:S(2)}, u32[]{:S(2)}) async-start(f32[8,2,2048]{2,1,0:T(2,128)} %broadcast_in_dim.192), calls=%async_computation.1 | async-start | bytes 262144 | tf_op jit(solution)/shard_map/all_to_all | solution.py:194
